TPU v7x, 32 devices: a whole 2x2x4 slice. The times are simulated.
32 devices in a mesh: gx: 4 (over y, x), gy: 8 (over z, core).
Axes of the slice: x: 2, y: 2, z: 4, core: 2. Of those that a mesh axis runs over, the one named last changes fastest.
Arguments:
- start_field: float32 [64, 64, 512], P('gx', 'gy'), may hold values from -6 to 6
- right_side: float32 [64, 64, 512], P('gx', 'gy'), may hold values from -12 to 12
- accumulation: float32 [64, 64, 512], P('gx', 'gy'), may hold values from 0.05 to 1
- trans_x: float32 [64, 64, 512], P('gx', 'gy'), may hold values from 0.1 to 10
- trans_y: float32 [64, 64, 512], P('gx', 'gy'), may hold values from 0.1 to 10
- trans_z: float32 [64, 64, 512], P('gx', 'gy'), may hold values from 0.1 to 10
Outputs:
- ortho_basis: float32 [5, 64, 64, 512], P(None, 'gx', 'gy')
- upper_factor: float32 [5, 5], replicated
- residual_scale: float32 [], replicated
All inputs are finite; a program needn't handle non-finite values.
Results may differ from a plain program's by a relative error of at most 0.0003.
Values sent between devices are 32-bit elements; how exact they have to be, the bound alone decides.
No kernel may reach another device: no remote copies, remote signals or barrier semaphores. Data moves between devices by JAX's collectives and lax.ppermute only.
A program may use at most 64 MiB of HBM per device.

v0:
```python
import jax
import jax.numpy as jnp
from jax import lax
from jax.sharding import PartitionSpec as P

STEPS = 4


EPS = 1e-06


def padded(block, sides, width):
    for axis, dim in sides:
        count = lax.axis_size(axis)
        forward = [(i, i + 1) for i in range(count - 1)]
        backward = [(target, source) for source, target in forward]
        low = lax.ppermute(
            lax.slice_in_dim(block, block.shape[dim] - width, None, axis=dim), axis, forward
        )
        high = lax.ppermute(lax.slice_in_dim(block, 0, width, axis=dim), axis, backward)
        block = jnp.concatenate([low, block, high], axis=dim)
    return block


def from_behind(value, axis, by):
    peers = lax.axis_size(axis)
    pairs = [(i, i + by) for i in range(peers) if 0 <= i + by < peers]
    return lax.ppermute(value, axis, pairs)


def neighbours(field, coef):
    acc_c, t_x, t_y, t_z = coef
    lx = field.shape[0] - 2
    ly = field.shape[1] - 2
    ox = (t_x.shape[0] - lx) // 2
    oy = (t_x.shape[1] - ly) // 2

    def piece(a, dx, dy):
        return a[ox + dx : ox + dx + lx, oy + dy : oy + dy + ly]

    centre = field[1:-1, 1:-1]
    zero_plane = jnp.zeros_like(centre[..., :1])
    tz_low = piece(t_z, 0, 0)
    tz_high = jnp.concatenate([tz_low[..., 1:], zero_plane], axis=-1)
    z_low = jnp.concatenate([zero_plane, centre[..., :-1]], axis=-1)
    z_high = jnp.concatenate([centre[..., 1:], zero_plane], axis=-1)
    tx_low = piece(t_x, 0, 0)
    tx_high = piece(t_x, 1, 0)
    ty_low = piece(t_y, 0, 0)
    ty_high = piece(t_y, 0, 1)
    total = tx_low * field[:-2, 1:-1] + tx_high * field[2:, 1:-1]
    total = total + ty_low * field[1:-1, :-2] + ty_high * field[1:-1, 2:]
    total = total + tz_low * z_low + tz_high * z_high
    diagonal = piece(acc_c, 0, 0) + tx_low + tx_high + ty_low + ty_high + tz_low + tz_high
    return (total, diagonal)


def upper_inverse(upper):
    size = upper.shape[0]
    columns = []
    for col in range(size):
        values = [None] * size
        for row in reversed(range(size)):
            value = jnp.float32(1.0 if row == col else 0.0)
            for inner in range(row + 1, size):
                value = value - upper[row, inner] * values[inner]
            values[row] = value / upper[row, row]
        columns.append(jnp.stack(values))
    return jnp.stack(columns, axis=1)


def pad_plain(a):
    return jnp.pad(a, ((1, 1), (1, 1), (0, 0)))


def field_widen(field):
    return padded(field, (("gx", 0), ("gy", 1)), 1)


def local(start_field, right_side, accumulation, trans_x, trans_y, trans_z):
    size_x, size_y, size_z = start_field.shape
    cells = size_x * size_y * size_z * lax.axis_size("gx") * lax.axis_size("gy")
    plane_x = from_behind(trans_x[:1], "gx", -1)
    plane_y = from_behind(trans_y[:, :1], "gy", -1)
    rim_x = jnp.pad(jnp.concatenate([trans_x, plane_x], axis=0), ((1, 0), (1, 1), (0, 0)))
    rim_y = jnp.pad(jnp.concatenate([trans_y, plane_y], axis=1), ((1, 1), (1, 0), (0, 0)))
    coef = (pad_plain(accumulation), rim_x, rim_y, pad_plain(trans_z))
    total, diagonal = neighbours(field_widen(start_field), coef)
    residual0 = right_side - (diagonal * start_field - total)
    squares = lax.psum(jnp.sum(residual0 * residual0), ("gx", "gy"))
    scale = jnp.sqrt(squares / cells + EPS)
    vector = residual0 / scale
    basis = [residual0 / scale]
    for step in range(STEPS):
        total, diagonal = neighbours(field_widen(vector), coef)
        vector = 2.0 * total / diagonal
        basis.append(vector)
    block = jnp.stack(basis)
    local_gram = jnp.einsum("axyz,bxyz->ab", block, block, precision=lax.Precision.HIGHEST)
    gram = lax.psum(local_gram, ("gx", "gy")) / cells
    upper = jnp.linalg.cholesky(gram).T
    inverse = upper_inverse(upper)
    ortho = jnp.einsum("jk,jxyz->kxyz", inverse, block, precision=lax.Precision.HIGHEST)
    return (ortho, upper, scale)


def solution(mesh):
    in_specs = (
        P("gx", "gy", None),
        P("gx", "gy", None),
        P("gx", "gy", None),
        P("gx", "gy", None),
        P("gx", "gy", None),
        P("gx", "gy", None),
    )
    out_specs = (P(None, "gx", "gy", None), P(), P())
    return jax.shard_map(local, mesh=mesh, in_specs=in_specs, out_specs=out_specs, check_vma=False)
```

profile of v0, /device:TPU:0, one launch (start us, length us, event | category | flops | bytes accessed | tf_op | source)
XLA Modules:
  0.0 220.1 jit_solution(5682292001169341076)
XLA Ops:
  0.7 0.8 fusion.73
  1.5 4.8 %collective-permute-start.2 = (f32[1,8,512]{2,1,0:T(8,128)S(1)}, f32[1,8,512]{2,1,0:T(8,128)S(1)}, u32[]{:S(2)}, u32[]{:S(2)}) collective-permute-start(f32[1,8,512]{2,1,0:T(8,128)S(1)} %get-tuple-element.35), channel_id=1, source_target_pairs={{0,8},{8,16},{16,24},{1,9},{9,17},{17,25},{2,10},{10,18},{18,26},{... | collective-permute-start | bytes 49160 | tf_op jit(solution)/shard_map/ppermute | solution.py:17
  6.4 0.7 slice.332
  7.1 1.3 collective-permute-start
  8.4 1.3 collective-permute-start.3
  9.7 1.0 slice.334
  10.7 1.3 collective-permute-start.1
  12.0 1.0 constant_dynamic-update-slice_fusion.1
  13.0 1.7 collective-permute-done.3
  14.7 1.4 collective-permute-start.4
  16.1 1.3 collective-permute-start.5
  17.4 1.2 fusion.74
  18.6 0.1 slice.336
  18.7 2.2 %collective-permute-done.5 = f32[18,1,512]{2,1,0:T(1,128)S(1)} collective-permute-done((f32[18,1,512]{2,1,0:T(1,128)S(1)}, f32[18,1,512]{2,1,0:T(1,128)S(1)}, u32[]{:S(2)}, u32[]{:S(2)}) %collective-permute-start.5) | collective-permute-done | bytes 36896 | tf_op jit(solution)/shard_map/ppermute | solution.py:20
  21.0 1.0 multiply_reduce_fusion
  21.9 44.0 %psum.14 = f32[]{:T(128)} all-reduce(f32[]{:T(128)} %get-tuple-element.6), channel_id=1, replica_groups=mesh['gx'=4,'gy'=8] {'gx','gy'}, use_global_device_ids=true, to_apply=%region_1.2 | all-reduce | flops 1 | bytes 8 | tf_op jit(solution)/shard_map/psum | solution.py:90
  66.7 4.2 %collective-permute-start.6 = (f32[1,8,512]{2,1,0:T(8,128)S(1)}, f32[1,8,512]{2,1,0:T(8,128)S(1)}, u32[]{:S(2)}, u32[]{:S(2)}) collective-permute-start(f32[1,8,512]{2,1,0:T(8,128)S(1)} %get-tuple-element.32), channel_id=1, source_target_pairs={{0,8},{8,16},{16,24},{1,9},{9,17},{17,25},{2,10},{10,18},{18,26},{... | collective-permute-start | bytes 49160 | tf_op jit(solution)/shard_map/ppermute | solution.py:17
  70.9 1.3 collective-permute-start.7
  72.2 0.1 collective-permute-done.6
  72.3 4.2 %collective-permute-done.7 = f32[1,8,512]{2,1,0:T(8,128)S(1)} collective-permute-done((f32[1,8,512]{2,1,0:T(8,128)S(1)}, f32[1,8,512]{2,1,0:T(8,128)S(1)}, u32[]{:S(2)}, u32[]{:S(2)}) %collective-permute-start.7) | collective-permute-done | bytes 16416 | tf_op jit(solution)/shard_map/ppermute | solution.py:20
  76.6 1.3 collective-permute-start.8
  77.9 1.3 collective-permute-start.9
  79.2 0.1 fusion.71
  79.3 3.2 %collective-permute-done.9 = f32[18,1,512]{2,1,0:T(1,128)S(1)} collective-permute-done((f32[18,1,512]{2,1,0:T(1,128)S(1)}, f32[18,1,512]{2,1,0:T(1,128)S(1)}, u32[]{:S(2)}, u32[]{:S(2)}) %collective-permute-start.9) | collective-permute-done | bytes 36896 | tf_op jit(solution)/shard_map/ppermute | solution.py:20
  82.6 0.3 fusion.38
  82.9 4.5 %collective-permute-start.10 = (f32[1,8,512]{2,1,0:T(8,128)S(1)}, f32[1,8,512]{2,1,0:T(8,128)S(1)}, u32[]{:S(2)}, u32[]{:S(2)}) collective-permute-start(f32[1,8,512]{2,1,0:T(8,128)S(1)} %get-tuple-element.28), channel_id=1, source_target_pairs={{0,8},{8,16},{16,24},{1,9},{9,17},{17,25},{2,10},{10,18},{18,26},{... | collective-permute-start | bytes 49160 | tf_op jit(solution)/shard_map/ppermute | solution.py:17
  87.4 1.3 collective-permute-start.11
  88.8 4.2 %collective-permute-done.11 = f32[1,8,512]{2,1,0:T(8,128)S(1)} collective-permute-done((f32[1,8,512]{2,1,0:T(8,128)S(1)}, f32[1,8,512]{2,1,0:T(8,128)S(1)}, u32[]{:S(2)}, u32[]{:S(2)}) %collective-permute-start.11) | collective-permute-done | bytes 16416 | tf_op jit(solution)/shard_map/ppermute | solution.py:20
  93.1 3.1 %collective-permute-start.12 = (f32[18,1,512]{2,1,0:T(1,128)S(1)}, f32[18,1,512]{2,1,0:T(1,128)S(1)}, u32[]{:S(2)}, u32[]{:S(2)}) collective-permute-start(f32[18,1,512]{2,1,0:T(1,128)S(1)} %get-tuple-element.12), channel_id=1, source_target_pairs={{0,1},{1,2},{2,3},{3,4},{4,5},{5,6},{6,7},{8,9},{9,10},{10,11},{11... | collective-permute-start | bytes 110600 | tf_op jit(solution)/shard_map/ppermute | solution.py:17
  96.2 1.3 collective-permute-start.13
  97.5 0.1 fusion.69
  97.7 2.6 %collective-permute-done.13 = f32[18,1,512]{2,1,0:T(1,128)S(1)} collective-permute-done((f32[18,1,512]{2,1,0:T(1,128)S(1)}, f32[18,1,512]{2,1,0:T(1,128)S(1)}, u32[]{:S(2)}, u32[]{:S(2)}) %collective-permute-start.13) | collective-permute-done | bytes 36896 | tf_op jit(solution)/shard_map/ppermute | solution.py:20
  100.3 0.3 fusion.27
  100.6 2.8 %collective-permute-start.14 = (f32[1,8,512]{2,1,0:T(8,128)S(1)}, f32[1,8,512]{2,1,0:T(8,128)S(1)}, u32[]{:S(2)}, u32[]{:S(2)}) collective-permute-start(f32[1,8,512]{2,1,0:T(8,128)S(1)} %get-tuple-element.24), channel_id=1, source_target_pairs={{0,8},{8,16},{16,24},{1,9},{9,17},{17,25},{2,10},{10,18},{18,26},{... | collective-permute-start | bytes 49160 | tf_op jit(solution)/shard_map/ppermute | solution.py:17
  103.5 1.3 collective-permute-start.15
  104.9 4.2 %collective-permute-done.15 = f32[1,8,512]{2,1,0:T(8,128)S(1)} collective-permute-done((f32[1,8,512]{2,1,0:T(8,128)S(1)}, f32[1,8,512]{2,1,0:T(8,128)S(1)}, u32[]{:S(2)}, u32[]{:S(2)}) %collective-permute-start.15) | collective-permute-done | bytes 16416 | tf_op jit(solution)/shard_map/ppermute | solution.py:20
  109.1 3.1 %collective-permute-start.16 = (f32[18,1,512]{2,1,0:T(1,128)S(1)}, f32[18,1,512]{2,1,0:T(1,128)S(1)}, u32[]{:S(2)}, u32[]{:S(2)}) collective-permute-start(f32[18,1,512]{2,1,0:T(1,128)S(1)} %get-tuple-element.10), channel_id=1, source_target_pairs={{0,1},{1,2},{2,3},{3,4},{4,5},{5,6},{6,7},{8,9},{9,10},{10,11},{11... | collective-permute-start | bytes 110600 | tf_op jit(solution)/shard_map/ppermute | solution.py:17
  112.3 1.3 collective-permute-start.17
  113.6 0.1 fusion.67
  113.7 2.6 %collective-permute-done.17 = f32[18,1,512]{2,1,0:T(1,128)S(1)} collective-permute-done((f32[18,1,512]{2,1,0:T(1,128)S(1)}, f32[18,1,512]{2,1,0:T(1,128)S(1)}, u32[]{:S(2)}, u32[]{:S(2)}) %collective-permute-start.17) | collective-permute-done | bytes 36896 | tf_op jit(solution)/shard_map/ppermute | solution.py:20
  116.3 0.3 fusion.16
  116.7 2.8 %collective-permute-start.18 = (f32[1,8,512]{2,1,0:T(8,128)S(1)}, f32[1,8,512]{2,1,0:T(8,128)S(1)}, u32[]{:S(2)}, u32[]{:S(2)}) collective-permute-start(f32[1,8,512]{2,1,0:T(8,128)S(1)} %get-tuple-element.20), channel_id=1, source_target_pairs={{0,8},{8,16},{16,24},{1,9},{9,17},{17,25},{2,10},{10,18},{18,26},{... | collective-permute-start | bytes 49160 | tf_op jit(solution)/shard_map/ppermute | solution.py:17
  119.5 1.3 collective-permute-start.19
  120.9 0.3 copy.9
  121.1 0.3 copy.10
  121.4 0.3 copy.11
  121.7 3.5 %collective-permute-done.19 = f32[1,8,512]{2,1,0:T(8,128)S(1)} collective-permute-done((f32[1,8,512]{2,1,0:T(8,128)S(1)}, f32[1,8,512]{2,1,0:T(8,128)S(1)}, u32[]{:S(2)}, u32[]{:S(2)}) %collective-permute-start.19) | collective-permute-done | bytes 16416 | tf_op jit(solution)/shard_map/ppermute | solution.py:20
  125.2 3.1 %collective-permute-start.20 = (f32[18,1,512]{2,1,0:T(1,128)S(1)}, f32[18,1,512]{2,1,0:T(1,128)S(1)}, u32[]{:S(2)}, u32[]{:S(2)}) collective-permute-start(f32[18,1,512]{2,1,0:T(1,128)S(1)} %get-tuple-element.8), channel_id=1, source_target_pairs={{0,1},{1,2},{2,3},{3,4},{4,5},{5,6},{6,7},{8,9},{9,10},{10,11},{11... | collective-permute-start | bytes 110600 | tf_op jit(solution)/shard_map/ppermute | solution.py:17
  128.4 1.3 collective-permute-start.21
  129.7 0.1 fusion.65
  129.8 0.3 copy.12
  130.1 2.3 %collective-permute-done.21 = f32[18,1,512]{2,1,0:T(1,128)S(1)} collective-permute-done((f32[18,1,512]{2,1,0:T(1,128)S(1)}, f32[18,1,512]{2,1,0:T(1,128)S(1)}, u32[]{:S(2)}, u32[]{:S(2)}) %collective-permute-start.21) | collective-permute-done | bytes 36896 | tf_op jit(solution)/shard_map/ppermute | solution.py:20
  132.4 0.4 fusion.5
  132.8 0.2 stack.118
  132.9 2.1 stack.119
  135.0 4.6 %convolution_bitcast_fusion = f32[5,5]{0,1:T(8,128)S(1)} fusion(f32[5,16,8,512]{3,0,2,1:T(8,128)S(1)} %stack.119), kind=kOutput, calls=%fused_computation | convolution fusion | flops 19660800 | bytes 1310820 | tf_op jit(solution)/shard_map/axyz,bxyz->ab/dot_general | solution.py:99
  139.6 40.9 %psum.15 = f32[5,5]{0,1:T(8,128)S(1)} all-reduce(f32[5,5]{0,1:T(8,128)S(1)} %convolution_bitcast_fusion), channel_id=1, replica_groups=mesh['gx'=4,'gy'=8] {'gx','gy'}, use_global_device_ids=true, to_apply=%region_2.3 | all-reduce | flops 25 | bytes 200 | tf_op jit(solution)/shard_map/psum | solution.py:100
  180.6 0.4 cholesky.18
  181.0 0.6 compare_reduce_fusion
  181.7 0.6 select_bitcast_fusion
  182.4 0.7 copy.16
  183.0 0.7 fusion.75
  215.3 1.8 fusion.60
  217.1 1.8 copy.15
  (46 shorter events, 1.2 us)
Async XLA Ops:
  0.6 20.3 %copy-start.4 = (f32[16,8,512]{2,1,0:T(8,128)S(1)}, f32[16,8,512]{2,1,0:T(8,128)}, u32[]{:S(2)}) copy-start(f32[16,8,512]{2,1,0:T(8,128)} %param.6) | copy-start | bytes 786436
  0.6 20.3 %copy-start.2 = (f32[16,8,512]{2,1,0:T(8,128)S(1)}, f32[16,8,512]{2,1,0:T(8,128)}, u32[]{:S(2)}) copy-start(f32[16,8,512]{2,1,0:T(8,128)} %param.9) | copy-start | bytes 786436
  0.7 20.3 %copy-start.1 = (f32[16,8,512]{2,1,0:T(8,128)S(1)}, f32[16,8,512]{2,1,0:T(8,128)}, u32[]{:S(2)}) copy-start(f32[16,8,512]{2,1,0:T(8,128)} %param.10) | copy-start | bytes 786436
  0.7 17.9 %copy-start = (f32[16,8,512]{2,1,0:T(8,128)S(1)}, f32[16,8,512]{2,1,0:T(8,128)}, u32[]{:S(2)}) copy-start(f32[16,8,512]{2,1,0:T(8,128)} %param.11) | copy-start | bytes 786436
  0.7 20.3 %copy-start.3 = (f32[16,8,512]{2,1,0:T(8,128)S(1)}, f32[16,8,512]{2,1,0:T(8,128)}, u32[]{:S(2)}) copy-start(f32[16,8,512]{2,1,0:T(8,128)} %param.8) | copy-start | bytes 786436
  0.7 20.3 %copy-start.5 = (f32[16,8,512]{2,1,0:T(8,128)S(1)}, f32[16,8,512]{2,1,0:T(8,128)}, u32[]{:S(2)}) copy-start(f32[16,8,512]{2,1,0:T(8,128)} %param.7) | copy-start | bytes 786436
  1.5 10.4 %collective-permute-start.2 = (f32[1,8,512]{2,1,0:T(8,128)S(1)}, f32[1,8,512]{2,1,0:T(8,128)S(1)}, u32[]{:S(2)}, u32[]{:S(2)}) collective-permute-start(f32[1,8,512]{2,1,0:T(8,128)S(1)} %get-tuple-element.35), channel_id=1, source_target_pairs={{0,8},{8,16},{16,24},{1,9},{9,17},{17,25},{2,10},{10,18},{18,26},{... | collective-permute-start | bytes 49160 | tf_op jit(solution)/shard_map/ppermute | solution.py:17
  7.1 11.6 %collective-permute-start = (f32[1,8,512]{2,1,0:T(8,128)S(1)}, f32[1,8,512]{2,1,0:T(8,128)S(1)}, u32[]{:S(2)}, u32[]{:S(2)}) collective-permute-start(f32[1,8,512]{2,1,0:T(8,128)S(1)} %slice.332), channel_id=1, source_target_pairs={{8,0},{16,8},{24,16},{9,1},{17,9},{25,17},{10,2},{18,10},{26,18},{... | collective-permute-start | bytes 49160 | tf_op jit(solution)/shard_map/ppermute | solution.py:28
  8.4 6.3 %collective-permute-start.3 = (f32[1,8,512]{2,1,0:T(8,128)S(1)}, f32[1,8,512]{2,1,0:T(8,128)S(1)}, u32[]{:S(2)}, u32[]{:S(2)}) collective-permute-start(f32[1,8,512]{2,1,0:T(8,128)S(1)} %get-tuple-element.34), channel_id=1, source_target_pairs={{8,0},{16,8},{24,16},{9,1},{17,9},{25,17},{10,2},{18,10},{26,18},{... | collective-permute-start | bytes 49160 | tf_op jit(solution)/shard_map/ppermute | solution.py:20
  10.7 8.0 %collective-permute-start.1 = (f32[16,1,512]{2,1,0:T(1,128)S(1)}, f32[16,1,512]{2,1,0:T(1,128)S(1)}, u32[]{:S(2)}, u32[]{:S(2)}) collective-permute-start(f32[16,1,512]{2,1,0:T(1,128)S(1)} %slice.334), channel_id=1, source_target_pairs={{1,0},{2,1},{3,2},{4,3},{5,4},{6,5},{7,6},{9,8},{10,9},{11,10},{12... | collective-permute-start | bytes 98312 | tf_op jit(solution)/shard_map/ppermute | solution.py:28
  14.7 4.0 %collective-permute-start.4 = (f32[18,1,512]{2,1,0:T(1,128)S(1)}, f32[18,1,512]{2,1,0:T(1,128)S(1)}, u32[]{:S(2)}, u32[]{:S(2)}) collective-permute-start(f32[18,1,512]{2,1,0:T(1,128)S(1)} %get-tuple-element.16), channel_id=1, source_target_pairs={{0,1},{1,2},{2,3},{3,4},{4,5},{5,6},{6,7},{8,9},{9,10},{10,11},{11... | collective-permute-start | bytes 110600 | tf_op jit(solution)/shard_map/ppermute | solution.py:17
  16.1 4.8 %collective-permute-start.5 = (f32[18,1,512]{2,1,0:T(1,128)S(1)}, f32[18,1,512]{2,1,0:T(1,128)S(1)}, u32[]{:S(2)}, u32[]{:S(2)}) collective-permute-start(f32[18,1,512]{2,1,0:T(1,128)S(1)} %get-tuple-element.17), channel_id=1, source_target_pairs={{1,0},{2,1},{3,2},{4,3},{5,4},{6,5},{7,6},{9,8},{10,9},{11,10},{12... | collective-permute-start | bytes 110600 | tf_op jit(solution)/shard_map/ppermute | solution.py:20
  66.7 5.6 %collective-permute-start.6 = (f32[1,8,512]{2,1,0:T(8,128)S(1)}, f32[1,8,512]{2,1,0:T(8,128)S(1)}, u32[]{:S(2)}, u32[]{:S(2)}) collective-permute-start(f32[1,8,512]{2,1,0:T(8,128)S(1)} %get-tuple-element.32), channel_id=1, source_target_pairs={{0,8},{8,16},{16,24},{1,9},{9,17},{17,25},{2,10},{10,18},{18,26},{... | collective-permute-start | bytes 49160 | tf_op jit(solution)/shard_map/ppermute | solution.py:17
  70.9 5.6 %collective-permute-start.7 = (f32[1,8,512]{2,1,0:T(8,128)S(1)}, f32[1,8,512]{2,1,0:T(8,128)S(1)}, u32[]{:S(2)}, u32[]{:S(2)}) collective-permute-start(f32[1,8,512]{2,1,0:T(8,128)S(1)} %get-tuple-element.33), channel_id=1, source_target_pairs={{8,0},{16,8},{24,16},{9,1},{17,9},{25,17},{10,2},{18,10},{26,18},{... | collective-permute-start | bytes 49160 | tf_op jit(solution)/shard_map/ppermute | solution.py:20
  76.6 2.7 %collective-permute-start.8 = (f32[18,1,512]{2,1,0:T(1,128)S(1)}, f32[18,1,512]{2,1,0:T(1,128)S(1)}, u32[]{:S(2)}, u32[]{:S(2)}) collective-permute-start(f32[18,1,512]{2,1,0:T(1,128)S(1)} %get-tuple-element.14), channel_id=1, source_target_pairs={{0,1},{1,2},{2,3},{3,4},{4,5},{5,6},{6,7},{8,9},{9,10},{10,11},{11... | collective-permute-start | bytes 110600 | tf_op jit(solution)/shard_map/ppermute | solution.py:17
  77.9 4.7 %collective-permute-start.9 = (f32[18,1,512]{2,1,0:T(1,128)S(1)}, f32[18,1,512]{2,1,0:T(1,128)S(1)}, u32[]{:S(2)}, u32[]{:S(2)}) collective-permute-start(f32[18,1,512]{2,1,0:T(1,128)S(1)} %get-tuple-element.15), channel_id=1, source_target_pairs={{1,0},{2,1},{3,2},{4,3},{5,4},{6,5},{7,6},{9,8},{10,9},{11,10},{12... | collective-permute-start | bytes 110600 | tf_op jit(solution)/shard_map/ppermute | solution.py:20
  82.9 5.9 %collective-permute-start.10 = (f32[1,8,512]{2,1,0:T(8,128)S(1)}, f32[1,8,512]{2,1,0:T(8,128)S(1)}, u32[]{:S(2)}, u32[]{:S(2)}) collective-permute-start(f32[1,8,512]{2,1,0:T(8,128)S(1)} %get-tuple-element.28), channel_id=1, source_target_pairs={{0,8},{8,16},{16,24},{1,9},{9,17},{17,25},{2,10},{10,18},{18,26},{... | collective-permute-start | bytes 49160 | tf_op jit(solution)/shard_map/ppermute | solution.py:17
  87.4 5.6 %collective-permute-start.11 = (f32[1,8,512]{2,1,0:T(8,128)S(1)}, f32[1,8,512]{2,1,0:T(8,128)S(1)}, u32[]{:S(2)}, u32[]{:S(2)}) collective-permute-start(f32[1,8,512]{2,1,0:T(8,128)S(1)} %get-tuple-element.29), channel_id=1, source_target_pairs={{8,0},{16,8},{24,16},{9,1},{17,9},{25,17},{10,2},{18,10},{26,18},{... | collective-permute-start | bytes 49160 | tf_op jit(solution)/shard_map/ppermute | solution.py:20
  93.1 4.6 %collective-permute-start.12 = (f32[18,1,512]{2,1,0:T(1,128)S(1)}, f32[18,1,512]{2,1,0:T(1,128)S(1)}, u32[]{:S(2)}, u32[]{:S(2)}) collective-permute-start(f32[18,1,512]{2,1,0:T(1,128)S(1)} %get-tuple-element.12), channel_id=1, source_target_pairs={{0,1},{1,2},{2,3},{3,4},{4,5},{5,6},{6,7},{8,9},{9,10},{10,11},{11... | collective-permute-start | bytes 110600 | tf_op jit(solution)/shard_map/ppermute | solution.py:17
  96.2 4.0 %collective-permute-start.13 = (f32[18,1,512]{2,1,0:T(1,128)S(1)}, f32[18,1,512]{2,1,0:T(1,128)S(1)}, u32[]{:S(2)}, u32[]{:S(2)}) collective-permute-start(f32[18,1,512]{2,1,0:T(1,128)S(1)} %get-tuple-element.13), channel_id=1, source_target_pairs={{1,0},{2,1},{3,2},{4,3},{5,4},{6,5},{7,6},{9,8},{10,9},{11,10},{12... | collective-permute-start | bytes 110600 | tf_op jit(solution)/shard_map/ppermute | solution.py:20
  100.6 4.3 %collective-permute-start.14 = (f32[1,8,512]{2,1,0:T(8,128)S(1)}, f32[1,8,512]{2,1,0:T(8,128)S(1)}, u32[]{:S(2)}, u32[]{:S(2)}) collective-permute-start(f32[1,8,512]{2,1,0:T(8,128)S(1)} %get-tuple-element.24), channel_id=1, source_target_pairs={{0,8},{8,16},{16,24},{1,9},{9,17},{17,25},{2,10},{10,18},{18,26},{... | collective-permute-start | bytes 49160 | tf_op jit(solution)/shard_map/ppermute | solution.py:17
  103.5 5.6 %collective-permute-start.15 = (f32[1,8,512]{2,1,0:T(8,128)S(1)}, f32[1,8,512]{2,1,0:T(8,128)S(1)}, u32[]{:S(2)}, u32[]{:S(2)}) collective-permute-start(f32[1,8,512]{2,1,0:T(8,128)S(1)} %get-tuple-element.25), channel_id=1, source_target_pairs={{8,0},{16,8},{24,16},{9,1},{17,9},{25,17},{10,2},{18,10},{26,18},{... | collective-permute-start | bytes 49160 | tf_op jit(solution)/shard_map/ppermute | solution.py:20
  109.1 4.6 %collective-permute-start.16 = (f32[18,1,512]{2,1,0:T(1,128)S(1)}, f32[18,1,512]{2,1,0:T(1,128)S(1)}, u32[]{:S(2)}, u32[]{:S(2)}) collective-permute-start(f32[18,1,512]{2,1,0:T(1,128)S(1)} %get-tuple-element.10), channel_id=1, source_target_pairs={{0,1},{1,2},{2,3},{3,4},{4,5},{5,6},{6,7},{8,9},{9,10},{10,11},{11... | collective-permute-start | bytes 110600 | tf_op jit(solution)/shard_map/ppermute | solution.py:17
  112.3 4.0 %collective-permute-start.17 = (f32[18,1,512]{2,1,0:T(1,128)S(1)}, f32[18,1,512]{2,1,0:T(1,128)S(1)}, u32[]{:S(2)}, u32[]{:S(2)}) collective-permute-start(f32[18,1,512]{2,1,0:T(1,128)S(1)} %get-tuple-element.11), channel_id=1, source_target_pairs={{1,0},{2,1},{3,2},{4,3},{5,4},{6,5},{7,6},{9,8},{10,9},{11,10},{12... | collective-permute-start | bytes 110600 | tf_op jit(solution)/shard_map/ppermute | solution.py:20
  116.7 5.0 %collective-permute-start.18 = (f32[1,8,512]{2,1,0:T(8,128)S(1)}, f32[1,8,512]{2,1,0:T(8,128)S(1)}, u32[]{:S(2)}, u32[]{:S(2)}) collective-permute-start(f32[1,8,512]{2,1,0:T(8,128)S(1)} %get-tuple-element.20), channel_id=1, source_target_pairs={{0,8},{8,16},{16,24},{1,9},{9,17},{17,25},{2,10},{10,18},{18,26},{... | collective-permute-start | bytes 49160 | tf_op jit(solution)/shard_map/ppermute | solution.py:17
  119.5 5.6 %collective-permute-start.19 = (f32[1,8,512]{2,1,0:T(8,128)S(1)}, f32[1,8,512]{2,1,0:T(8,128)S(1)}, u32[]{:S(2)}, u32[]{:S(2)}) collective-permute-start(f32[1,8,512]{2,1,0:T(8,128)S(1)} %get-tuple-element.21), channel_id=1, source_target_pairs={{8,0},{16,8},{24,16},{9,1},{17,9},{25,17},{10,2},{18,10},{26,18},{... | collective-permute-start | bytes 49160 | tf_op jit(solution)/shard_map/ppermute | solution.py:20
  125.2 4.9 %collective-permute-start.20 = (f32[18,1,512]{2,1,0:T(1,128)S(1)}, f32[18,1,512]{2,1,0:T(1,128)S(1)}, u32[]{:S(2)}, u32[]{:S(2)}) collective-permute-start(f32[18,1,512]{2,1,0:T(1,128)S(1)} %get-tuple-element.8), channel_id=1, source_target_pairs={{0,1},{1,2},{2,3},{3,4},{4,5},{5,6},{6,7},{8,9},{9,10},{10,11},{11... | collective-permute-start | bytes 110600 | tf_op jit(solution)/shard_map/ppermute | solution.py:17
  128.4 4.0 %collective-permute-start.21 = (f32[18,1,512]{2,1,0:T(1,128)S(1)}, f32[18,1,512]{2,1,0:T(1,128)S(1)}, u32[]{:S(2)}, u32[]{:S(2)}) collective-permute-start(f32[18,1,512]{2,1,0:T(1,128)S(1)} %get-tuple-element.9), channel_id=1, source_target_pairs={{1,0},{2,1},{3,2},{4,3},{5,4},{6,5},{7,6},{9,8},{10,9},{11,10},{12... | collective-permute-start | bytes 110600 | tf_op jit(solution)/shard_map/ppermute | solution.py:20
where the time goes:
time: 222 us; the launch traced here: 220 us
  blocking collectives  84.9 us (38%)
  starting transfers between devices  46.7 us (21%)
  between operations  34.1 us (15%)
  waiting for transfers between devices  31.1 us (14%)
  local copies, waits for them, and re-layouts  12.5 us (6%)
  matrix products  6.41 us (3%)
  other arithmetic  4.38 us (2%)
    psum x1, blocking collectives, local(): squares = lax.psum(jnp.sum(residual0 * residual0), ('gx', 'gy'))  44 us
    psum x1, blocking collectives, local(): gram = lax.psum(local_gram, ('gx', 'gy')) / cells  40.9 us
    ppermute x10, starting transfers between devices, padded(): lax.ppermute(lax.slice_in_dim(block, block.shape[dim] - width, None, axis...  31.2 us
    ppermute x10, waiting for transfers between devices, padded(): lax.ppermute(lax.slice_in_dim(block, 0, width, axis=dim), axis, backward)  30.7 us
    ppermute x10, starting transfers between devices, padded(): lax.ppermute(lax.slice_in_dim(block, 0, width, axis=dim), axis, backward)  12.9 us
    dot_general x1, matrix products, local(): jnp.einsum('axyz,bxyz->ab', block, block, precision=lax.Precision.HIGHEST)  4.56 us
  transfers between devices with their start and end apart: 22, of which 13 were waited for; matrix products, arithmetic and copies ran while one was open for 3% of the time, Pallas kernels for 0%

commit v1 on v0

v1 whole, which is shorter than its diff:
```python
import jax
import jax.numpy as jnp
from jax import lax
from jax.sharding import PartitionSpec as P

STEPS = 4


EPS = 1e-06


def shift_pairs(axis, by):
    peers = lax.axis_size(axis)
    return [(i, i + by) for i in range(peers) if 0 <= i + by < peers]


def exchange(to_low_x, to_high_x, to_low_y, to_high_y):
    from_high_x = lax.ppermute(to_low_x, "gx", shift_pairs("gx", -1))
    from_low_x = lax.ppermute(to_high_x, "gx", shift_pairs("gx", 1))
    from_high_y = lax.ppermute(to_low_y, "gy", shift_pairs("gy", -1))
    from_low_y = lax.ppermute(to_high_y, "gy", shift_pairs("gy", 1))
    return from_low_x, from_high_x, from_low_y, from_high_y


def neighbour_sum(u, halo, coef):
    lo_x, hi_x, lo_y, hi_y = halo
    tx_lo, tx_hi, ty_lo, ty_hi, tz_lo, tz_hi = coef
    zero_plane = jnp.zeros_like(u[..., :1])
    u_xm = jnp.concatenate([lo_x, u[:-1]], axis=0)
    u_xp = jnp.concatenate([u[1:], hi_x], axis=0)
    u_ym = jnp.concatenate([lo_y, u[:, :-1]], axis=1)
    u_yp = jnp.concatenate([u[:, 1:], hi_y], axis=1)
    u_zm = jnp.concatenate([zero_plane, u[..., :-1]], axis=-1)
    u_zp = jnp.concatenate([u[..., 1:], zero_plane], axis=-1)
    total = tx_lo * u_xm + tx_hi * u_xp
    total = total + ty_lo * u_ym + ty_hi * u_yp
    total = total + tz_lo * u_zm + tz_hi * u_zp
    return total


def field_halo(u):
    return exchange(u[:1], u[-1:], u[:, :1], u[:, -1:])


def all_sum(x):
    for axis in ("gy", "gx"):
        n = lax.axis_size(axis)
        if n & (n - 1):
            x = lax.psum(x, axis)
            continue
        step = 1
        while step < n:
            x = x + lax.ppermute(x, axis, [(i, i ^ step) for i in range(n)])
            step *= 2
    return x


def cholesky_upper(gram):
    size = gram.shape[0]
    rows = []
    for row in range(size):
        cur = gram[row]
        for prev in range(row):
            cur = cur - rows[prev][row] * rows[prev]
        pivot = jnp.sqrt(cur[row])
        mask = jnp.arange(size) >= row
        rows.append(jnp.where(mask, cur / pivot, 0.0))
    return jnp.stack(rows)


def upper_inverse(upper):
    size = upper.shape[0]
    eye = jnp.eye(size, dtype=upper.dtype)
    rows = [None] * size
    for row in reversed(range(size)):
        value = eye[row]
        for inner in range(row + 1, size):
            value = value - upper[row, inner] * rows[inner]
        rows[row] = value / upper[row, row]
    return jnp.stack(rows)


def local(start_field, right_side, accumulation, trans_x, trans_y, trans_z):
    size_x, size_y, size_z = start_field.shape
    cells = size_x * size_y * size_z * lax.axis_size("gx") * lax.axis_size("gy")

    lo_x, hi_both_x, lo_y, hi_both_y = exchange(
        jnp.concatenate([start_field[:1], trans_x[:1]], axis=0),
        start_field[-1:],
        jnp.concatenate([start_field[:, :1], trans_y[:, :1]], axis=1),
        start_field[:, -1:],
    )
    hi_x, plane_x = hi_both_x[:1], hi_both_x[1:]
    hi_y, plane_y = hi_both_y[:, :1], hi_both_y[:, 1:]

    zero_plane = jnp.zeros_like(trans_z[..., :1])
    tx_lo = trans_x
    tx_hi = jnp.concatenate([trans_x[1:], plane_x], axis=0)
    ty_lo = trans_y
    ty_hi = jnp.concatenate([trans_y[:, 1:], plane_y], axis=1)
    tz_lo = trans_z
    tz_hi = jnp.concatenate([trans_z[..., 1:], zero_plane], axis=-1)
    coef = (tx_lo, tx_hi, ty_lo, ty_hi, tz_lo, tz_hi)
    diagonal = accumulation + tx_lo + tx_hi + ty_lo + ty_hi + tz_lo + tz_hi

    total = neighbour_sum(start_field, (lo_x, hi_x, lo_y, hi_y), coef)
    residual0 = right_side - (diagonal * start_field - total)

    vector = residual0
    basis = [vector]
    for step in range(STEPS):
        total = neighbour_sum(vector, field_halo(vector), coef)
        vector = 2.0 * total / diagonal
        basis.append(vector)
    block = jnp.stack(basis)
    local_gram = jnp.einsum("axyz,bxyz->ab", block, block, precision=lax.Precision.HIGHEST)
    squares = jnp.sum(residual0 * residual0)
    stats = jnp.concatenate([squares[None], local_gram.reshape(-1)])
    stats = all_sum(stats)
    scale = jnp.sqrt(stats[0] / cells + EPS)
    gram = stats[1:].reshape(local_gram.shape) / cells / (scale * scale)
    upper = cholesky_upper(gram)
    inverse = upper_inverse(upper) / scale
    ortho = jnp.einsum("jk,jxyz->kxyz", inverse, block, precision=lax.Precision.HIGHEST)
    return (ortho, upper, scale)


def solution(mesh):
    in_specs = (
        P("gx", "gy", None),
        P("gx", "gy", None),
        P("gx", "gy", None),
        P("gx", "gy", None),
        P("gx", "gy", None),
        P("gx", "gy", None),
    )
    out_specs = (P(None, "gx", "gy", None), P(), P())
    return jax.shard_map(local, mesh=mesh, in_specs=in_specs, out_specs=out_specs, check_vma=False)
```

time: 222 us -> 147 us (0.66)
  blocking collectives: 84.9 us -> 0 us
  between operations: 34.1 us -> 5.95 us
  starting transfers between devices: 46.7 us -> 71.8 us
  other arithmetic: 4.38 us -> 29.4 us
  waiting for transfers between devices: 31.1 us -> 11 us
  local copies, waits for them, and re-layouts: 12.5 us -> 21.2 us
    psum x2 -> x0, blocking collectives: 84.9 us -> none  [the longest x1 44 us: local(): squares = lax.psum(jnp.sum(residual0 * residual0), ('gx', 'gy'))]
    ppermute x22 -> x25, starting transfers between devices: 46.7 us -> 71.8 us  [the longest x5 25.5 us: exchange(): from_low_x = lax.ppermute(to_high_x, 'gx', shift_pairs('gx', 1))]
    ppermute x22 -> x25, waiting for transfers between devices: 31.1 us -> 11 us  [the longest x5 8.34 us: all_sum(): x = x + lax.ppermute(x, axis, [(i, i ^ step) for i in range(n)])]
    div x3 -> x4, other arithmetic: 0.04 us -> 12.1 us  [the longest x2 12 us: upper_inverse(): rows[row] = value / upper[row, row]]
    slice x15 -> x48, local copies, waits for them, and re-layouts: 5.11 us -> 14.9 us  [the longest x5 2.98 us: cholesky_upper(): pivot = jnp.sqrt(cur[row])]
    select_n x0 -> x4, other arithmetic: none -> 6.26 us  [cholesky_upper(): rows.append(jnp.where(mask, cur / pivot, 0.0))]
    sub x0 -> x3, other arithmetic: none -> 3.93 us  [cholesky_upper(): cur = cur - rows[prev][row] * rows[prev]]
    mul x0 -> x1, other arithmetic: none -> 2.64 us  [cholesky_upper(): cur = cur - rows[prev][row] * rows[prev]]
  transfers between devices with their start and end apart: 22 -> 25, of which waited for: 13 -> 10; matrix products, arithmetic and copies ran while one was open for 3% -> 5% of each run, Pallas kernels for 0% -> 0%
where the time goes in v1:
time: 147 us; the launch traced here: 146 us
  starting transfers between devices  71.8 us (49%)
  other arithmetic  29.4 us (20%)
  local copies, waits for them, and re-layouts  21.2 us (14%)
  waiting for transfers between devices  11 us (7%)
  matrix products  6.39 us (4%)
  between operations  5.95 us (4%)
    ppermute x5, starting transfers between devices, exchange(): from_low_x = lax.ppermute(to_high_x, 'gx', shift_pairs('gx', 1))  25.5 us
    ppermute x5, starting transfers between devices, exchange(): from_low_y = lax.ppermute(to_high_y, 'gy', shift_pairs('gy', 1))  21.6 us
    div x2, other arithmetic, upper_inverse(): rows[row] = value / upper[row, row]  12 us
    ppermute x5, starting transfers between devices, all_sum(): x = x + lax.ppermute(x, axis, [(i, i ^ step) for i in range(n)])  11.8 us
    ppermute x5, waiting for transfers between devices, all_sum(): x = x + lax.ppermute(x, axis, [(i, i ^ step) for i in range(n)])  8.34 us
    ppermute x5, starting transfers between devices, exchange(): from_high_y = lax.ppermute(to_low_y, 'gy', shift_pairs('gy', -1))  6.46 us
    ppermute x5, starting transfers between devices, exchange(): from_high_x = lax.ppermute(to_low_x, 'gx', shift_pairs('gx', -1))  6.45 us
    select_n x4, other arithmetic, cholesky_upper(): rows.append(jnp.where(mask, cur / pivot, 0.0))  6.26 us
  transfers between devices with their start and end apart: 25, of which 10 were waited for; matrix products, arithmetic and copies ran while one was open for 5% of the time, Pallas kernels for 0%

profile of v1, /device:TPU:0, one launch (start us, length us, event | category | flops | bytes accessed | tf_op | source)
XLA Modules:
  0.0 145.7 jit_solution(9374992882529838649)
XLA Ops:
  0.7 0.8 fusion.61
  1.5 4.8 %collective-permute-start.2 = (f32[1,8,512]{2,1,0:T(8,128)S(1)}, f32[1,8,512]{2,1,0:T(8,128)S(1)}, u32[]{:S(2)}, u32[]{:S(2)}) collective-permute-start(f32[1,8,512]{2,1,0:T(8,128)S(1)} %get-tuple-element.63), channel_id=1, source_target_pairs={{0,8},{8,16},{16,24},{1,9},{9,17},{17,25},{2,10},{10,18},{18,26},{... | collective-permute-start | bytes 49160 | tf_op jit(solution)/shard_map/ppermute | solution.py:19
  6.3 0.7 slice.317
  7.0 1.3 collective-permute-start
  8.3 1.1 fusion.63
  9.4 1.5 %collective-permute-start.3 = (f32[16,1,512]{2,1,0:T(1,128)S(1)}, f32[16,1,512]{2,1,0:T(1,128)S(1)}, u32[]{:S(2)}, u32[]{:S(2)}) collective-permute-start(f32[16,1,512]{2,1,0:T(1,128)S(1)} %get-tuple-element.67), channel_id=1, source_target_pairs={{0,1},{1,2},{2,3},{3,4},{4,5},{5,6},{6,7},{8,9},{9,10},{10,11},{11... | collective-permute-start | bytes 98312 | tf_op jit(solution)/shard_map/ppermute | solution.py:21
  10.9 1.0 slice.321
  11.9 1.3 collective-permute-start.1
  13.2 1.1 fusion.64
  14.3 1.2 fusion.65
  15.9 0.9 collective-permute-done.1
  16.8 1.1 multiply_reduce_fusion
  18.2 1.3 collective-permute-start.5
  19.5 5.2 %collective-permute-start.4 = (f32[1,8,512]{2,1,0:T(8,128)S(1)}, f32[1,8,512]{2,1,0:T(8,128)S(1)}, u32[]{:S(2)}, u32[]{:S(2)}) collective-permute-start(f32[1,8,512]{2,1,0:T(8,128)S(1)} %get-tuple-element.62), channel_id=1, source_target_pairs={{0,8},{8,16},{16,24},{1,9},{9,17},{17,25},{2,10},{10,18},{18,26},{... | collective-permute-start | bytes 49160 | tf_op jit(solution)/shard_map/ppermute | solution.py:19
  24.7 1.3 collective-permute-start.7
  26.0 5.2 %collective-permute-start.6 = (f32[16,1,512]{2,1,0:T(1,128)S(1)}, f32[16,1,512]{2,1,0:T(1,128)S(1)}, u32[]{:S(2)}, u32[]{:S(2)}) collective-permute-start(f32[16,1,512]{2,1,0:T(1,128)S(1)} %get-tuple-element.58), channel_id=1, source_target_pairs={{0,1},{1,2},{2,3},{3,4},{4,5},{5,6},{6,7},{8,9},{9,10},{10,11},{11... | collective-permute-start | bytes 98312 | tf_op jit(solution)/shard_map/ppermute | solution.py:21
  32.7 1.3 collective-permute-start.9
  34.0 5.2 %collective-permute-start.8 = (f32[1,8,512]{2,1,0:T(8,128)S(1)}, f32[1,8,512]{2,1,0:T(8,128)S(1)}, u32[]{:S(2)}, u32[]{:S(2)}) collective-permute-start(f32[1,8,512]{2,1,0:T(8,128)S(1)} %get-tuple-element.52), channel_id=1, source_target_pairs={{0,8},{8,16},{16,24},{1,9},{9,17},{17,25},{2,10},{10,18},{18,26},{... | collective-permute-start | bytes 49160 | tf_op jit(solution)/shard_map/ppermute | solution.py:19
  39.2 1.3 collective-permute-start.11
  40.5 4.2 %collective-permute-start.10 = (f32[16,1,512]{2,1,0:T(1,128)S(1)}, f32[16,1,512]{2,1,0:T(1,128)S(1)}, u32[]{:S(2)}, u32[]{:S(2)}) collective-permute-start(f32[16,1,512]{2,1,0:T(1,128)S(1)} %get-tuple-element.48), channel_id=1, source_target_pairs={{0,1},{1,2},{2,3},{3,4},{4,5},{5,6},{6,7},{8,9},{9,10},{10,11},{11... | collective-permute-start | bytes 98312 | tf_op jit(solution)/shard_map/ppermute | solution.py:21
  46.2 1.3 collective-permute-start.13
  47.5 5.2 %collective-permute-start.12 = (f32[1,8,512]{2,1,0:T(8,128)S(1)}, f32[1,8,512]{2,1,0:T(8,128)S(1)}, u32[]{:S(2)}, u32[]{:S(2)}) collective-permute-start(f32[1,8,512]{2,1,0:T(8,128)S(1)} %get-tuple-element.42), channel_id=1, source_target_pairs={{0,8},{8,16},{16,24},{1,9},{9,17},{17,25},{2,10},{10,18},{18,26},{... | collective-permute-start | bytes 49160 | tf_op jit(solution)/shard_map/ppermute | solution.py:19
  52.7 1.3 collective-permute-start.15
  54.0 5.3 %collective-permute-start.14 = (f32[16,1,512]{2,1,0:T(1,128)S(1)}, f32[16,1,512]{2,1,0:T(1,128)S(1)}, u32[]{:S(2)}, u32[]{:S(2)}) collective-permute-start(f32[16,1,512]{2,1,0:T(1,128)S(1)} %get-tuple-element.38), channel_id=1, source_target_pairs={{0,1},{1,2},{2,3},{3,4},{4,5},{5,6},{6,7},{8,9},{9,10},{10,11},{11... | collective-permute-start | bytes 98312 | tf_op jit(solution)/shard_map/ppermute | solution.py:21
  60.8 1.3 collective-permute-start.17
  62.1 5.2 %collective-permute-start.16 = (f32[1,8,512]{2,1,0:T(8,128)S(1)}, f32[1,8,512]{2,1,0:T(8,128)S(1)}, u32[]{:S(2)}, u32[]{:S(2)}) collective-permute-start(f32[1,8,512]{2,1,0:T(8,128)S(1)} %get-tuple-element.32), channel_id=1, source_target_pairs={{0,8},{8,16},{16,24},{1,9},{9,17},{17,25},{2,10},{10,18},{18,26},{... | collective-permute-start | bytes 49160 | tf_op jit(solution)/shard_map/ppermute | solution.py:19
  67.3 1.3 collective-permute-start.19
  68.6 5.5 %collective-permute-start.18 = (f32[16,1,512]{2,1,0:T(1,128)S(1)}, f32[16,1,512]{2,1,0:T(1,128)S(1)}, u32[]{:S(2)}, u32[]{:S(2)}) collective-permute-start(f32[16,1,512]{2,1,0:T(1,128)S(1)} %get-tuple-element.28), channel_id=1, source_target_pairs={{0,1},{1,2},{2,3},{3,4},{4,5},{5,6},{6,7},{8,9},{9,10},{10,11},{11... | collective-permute-start | bytes 98312 | tf_op jit(solution)/shard_map/ppermute | solution.py:21
  75.4 2.1 %stack.39 = f32[5,16,8,512]{3,0,2,1:T(8,128)S(1)} concatenate(f32[1,16,8,512]{3,0,2,1:T(1,128)S(1)} %copy.24, f32[1,16,8,512]{3,0,2,1:T(1,128)S(1)} %copy.25, f32[1,16,8,512]{3,0,2,1:T(1,128)S(1)} %copy.26, f32[1,16,8,512]{3,0,2,1:T(1,128)S(1)} %copy.27, f32[1,16,8,512]{3,0,2,1:T(1,128)S(1)} %stack.38), dimensions={0} | concatenate | bytes 2621440 | tf_op jit(solution)/shard_map/stack | solution.py:115
  77.4 4.5 %convolution_bitcast_fusion = f32[5,5]{1,0:T(8,128)S(1)} fusion(f32[5,16,8,512]{3,0,2,1:T(8,128)S(1)} %stack.39), kind=kOutput, calls=%fused_computation | convolution fusion | flops 19660800 | bytes 1310820 | tf_op jit(solution)/shard_map/axyz,bxyz->ab/dot_general | solution.py:116
  82.1 0.7 pad_maximum_fusion.4
  82.8 2.8 %collective-permute-start.20 = (f32[26]{0:T(128)S(1)}, f32[26]{0:T(128)S(1)}, u32[]{:S(2)}, u32[]{:S(2)}) collective-permute-start(f32[26]{0:T(128)S(1)} %pad_maximum_fusion.4), channel_id=1, source_target_pairs={{0,1},{1,0},{2,3},{3,2},{4,5},{5,4},{6,7},{7,6},{8,9},{9,8},{10,11... | collective-permute-start | bytes 320 | tf_op jit(solution)/shard_map/ppermute | solution.py:53
  85.6 0.8 collective-permute-done.20
  86.4 0.7 fusion.77
  87.1 2.5 %collective-permute-start.21 = (f32[26]{0:T(128)S(1)}, f32[26]{0:T(128)S(1)}, u32[]{:S(2)}, u32[]{:S(2)}) collective-permute-start(f32[26]{0:T(128)S(1)} %fusion.77), channel_id=1, source_target_pairs={{0,2},{1,3},{2,0},{3,1},{4,6},{5,7},{6,4},{7,5},{8,10},{9,11},{10,... | collective-permute-start | bytes 320 | tf_op jit(solution)/shard_map/ppermute | solution.py:53
  89.6 1.5 %collective-permute-done.21 = f32[26]{0:T(128)S(1)} collective-permute-done((f32[26]{0:T(128)S(1)}, f32[26]{0:T(128)S(1)}, u32[]{:S(2)}, u32[]{:S(2)}) %collective-permute-start.21) | collective-permute-done | bytes 136 | tf_op jit(solution)/shard_map/ppermute | solution.py:53
  91.1 3.0 %collective-permute-start.22 = (f32[26]{0:T(128)S(1)}, f32[26]{0:T(128)S(1)}, u32[]{:S(2)}, u32[]{:S(2)}) collective-permute-start(f32[26]{0:T(128)S(1)} %add.166), channel_id=1, source_target_pairs={{0,4},{1,5},{2,6},{3,7},{4,0},{5,1},{6,2},{7,3},{8,12},{9,13},{10,... | collective-permute-start | bytes 320 | tf_op jit(solution)/shard_map/ppermute | solution.py:53
  94.2 1.5 %collective-permute-done.22 = f32[26]{0:T(128)S(1)} collective-permute-done((f32[26]{0:T(128)S(1)}, f32[26]{0:T(128)S(1)}, u32[]{:S(2)}, u32[]{:S(2)}) %collective-permute-start.22) | collective-permute-done | bytes 136 | tf_op jit(solution)/shard_map/ppermute | solution.py:53
  95.7 2.9 %collective-permute-start.23 = (f32[26]{0:T(128)S(1)}, f32[26]{0:T(128)S(1)}, u32[]{:S(2)}, u32[]{:S(2)}) collective-permute-start(f32[26]{0:T(128)S(1)} %add.167), channel_id=1, source_target_pairs={{0,8},{8,0},{16,24},{24,16},{1,9},{9,1},{17,25},{25,17},{2,10},{10... | collective-permute-start | bytes 320 | tf_op jit(solution)/shard_map/ppermute | solution.py:53
  98.6 1.5 %collective-permute-done.23 = f32[26]{0:T(128)S(1)} collective-permute-done((f32[26]{0:T(128)S(1)}, f32[26]{0:T(128)S(1)}, u32[]{:S(2)}, u32[]{:S(2)}) %collective-permute-start.23) | collective-permute-done | bytes 136 | tf_op jit(solution)/shard_map/ppermute | solution.py:53
  100.1 0.6 collective-permute-start.24
  100.7 3.0 %collective-permute-done.24 = f32[26]{0:T(128)S(1)} collective-permute-done((f32[26]{0:T(128)S(1)}, f32[26]{0:T(128)S(1)}, u32[]{:S(2)}, u32[]{:S(2)}) %collective-permute-start.24) | collective-permute-done | bytes 136 | tf_op jit(solution)/shard_map/ppermute | solution.py:53
  103.9 0.5 slice.377
  105.1 0.7 fusion.71
  105.9 2.6 %multiply_reduce_fusion.1 = (f32[5]{0:T(128)S(1)}, f32[5]{0:T(128)S(1)}, f32[5]{0:T(128)S(1)}, f32[5]{0:T(128)S(1)}) fusion(f32[1,5]{0,1:T(8,128)S(1)} %copy.28, f32[]{:T(128)} %bitcast.26, f32[]{:T(128)} %bitcast.10, f32[]{:T(128)} %bitcast.15, f32[]{:T(128)} %bitcast.20), kind=kLoop, calls=%fused_computation.80 | loop fusion | flops 20 | bytes 116 | tf_op jit(solution)/shard_map/mul | solution.py:64
  108.6 0.6 slice.382
  109.9 0.7 fusion.72
  110.6 0.7 multiply_subtract_fusion.2
  111.3 0.7 slice.389
  112.7 0.6 fusion.73
  113.3 1.3 multiply_subtract_fusion.1
  114.6 0.6 slice.397
  115.8 0.7 slice.405
  116.4 1.9 %multiply_subtract_fusion = f32[5]{0:T(128)S(1)} fusion(f32[5]{0:T(128)S(1)} %get-tuple-element.9, f32[25]{0:T(128)S(1)} %multiply_divide_fusion, f32[]{:T(128)} %bitcast.29, f32[]{:T(128)} %bitcast.28, f32[]{:T(128)} %bitcast.27, f32[5]{0:T(128)S(1)} %multiply_subtract_fusion.1, f32[]{:T(128)} %bitcast.23, f32[5]{0:T(128)S(1)} %multiply_subtract_fusion.2, ...), kind=kLoop, calls=%fused_computation.89 | loop fusion | flops 80 | bytes 144 | tf_op jit(solution)/shard_map/sub | solution.py:64
  118.4 0.6 slice.406
  120.0 6.2 %divide_select_fusion = (f32[1,5]{0,1:T(8,128)S(1)}, f32[1,5]{0,1:T(8,128)S(1)}, f32[1,5]{0,1:T(8,128)S(1)}, f32[1,5]{0,1:T(8,128)S(1)}) fusion(f32[1,5]{0,1:T(8,128)S(1)} %copy.35, f32[1,5]{0,1:T(8,128)S(1)} %copy.28, f32[]{:T(128)} %bitcast.30, f32[]{:T(128)} %bitcast.29, f32[]{:T(128)} %bitcast.28, f32[]{:T(128)} %bitcast.27, f32[]{:T(128)} %bitcast.26, ...), kind=kLoop, calls=%fused_computation.69 | loop fusion | flops 160 | bytes 236 | tf_op jit(solution)/shard_map/jit(_where)/select_n | solution.py:67
  126.3 0.6 slice.407
  126.8 0.6 fusion.68
  127.5 0.6 fusion.70
  128.1 0.7 copy.38
  128.8 6.3 %subtract_divide_fusion.1 = (f32[1,5]{0,1:T(8,128)S(1)}, f32[1,5]{0,1:T(8,128)S(1)}, f32[1,5]{0,1:T(8,128)S(1)}, f32[1,5]{0,1:T(8,128)S(1)}) fusion(f32[5,5]{0,1:T(8,128)S(1)} %fusion.38, f32[]{:T(128)} %bitcast.37, f32[]{:T(128)} %bitcast.36, f32[]{:T(128)} %bitcast.35, f32[]{:T(128)} %bitcast.13, f32[]{:T(128)} %bitcast.34, f32[]{:T(128)} %bitcast.33, ...), kind=kLoop, calls=%fused_computation.66 | loop fusion | flops 80 | bytes 200 | tf_op jit(solution)/shard_map/div | solution.py:79
  135.1 5.7 %subtract_divide_fusion = f32[1,5]{0,1:T(8,128)S(1)} fusion(f32[1,5]{0,1:T(8,128)S(1)} %get-tuple-element.16, f32[1,5]{0,1:T(8,128)S(1)} %get-tuple-element.15, f32[1,5]{0,1:T(8,128)S(1)} %get-tuple-element.14, f32[5,5]{0,1:T(8,128)S(1)} %fusion.38, f32[]{:T(128)} %bitcast.38, f32[]{:T(128)} %bitcast.26, f32[]{:T(128)} %bitcast.20, f32[]{:T(128)} %bitcast.15, ...), kind=kLoop, calls=%fused_computation.65 | loop fusion | flops 80 | bytes 156 | tf_op jit(solution)/shard_map/div | solution.py:79
  140.9 1.8 %fusion.35 = f32[5,16,8,512]{3,0,2,1:T(8,128)S(1)} fusion(f32[5,16,8,512]{3,0,2,1:T(8,128)S(1)} %stack.39, f32[5,5]{0,1:T(8,128)S(1)} %stack.40, f32[]{:T(128)} %bitcast.7), kind=kOutput, calls=%fused_computation.62 | convolution fusion | flops 19660824 | bytes 2621544 | tf_op jit(solution)/shard_map/jk,jxyz->kxyz/dot_general | solution.py:124
  142.7 1.8 %copy.37 = f32[5,16,8,512]{3,2,1,0:T(8,128)} copy(f32[5,16,8,512]{3,0,2,1:T(8,128)S(1)} %fusion.35) | data formatting | bytes 2621440
  (88 shorter events, 7.2 us)
Async XLA Ops:
  0.6 14.9 %copy-start = (f32[16,8,512]{2,1,0:T(8,128)S(1)}, f32[16,8,512]{2,1,0:T(8,128)}, u32[]{:S(2)}) copy-start(f32[16,8,512]{2,1,0:T(8,128)} %param.6) | copy-start | bytes 786436
  0.6 15.0 %copy-start.3 = (f32[16,8,512]{2,1,0:T(8,128)S(1)}, f32[16,8,512]{2,1,0:T(8,128)}, u32[]{:S(2)}) copy-start(f32[16,8,512]{2,1,0:T(8,128)} %param.9) | copy-start | bytes 786436
  0.7 15.0 %copy-start.1 = (f32[16,8,512]{2,1,0:T(8,128)S(1)}, f32[16,8,512]{2,1,0:T(8,128)}, u32[]{:S(2)}) copy-start(f32[16,8,512]{2,1,0:T(8,128)} %param.10) | copy-start | bytes 786436
  1.5 15.3 %collective-permute-start.2 = (f32[1,8,512]{2,1,0:T(8,128)S(1)}, f32[1,8,512]{2,1,0:T(8,128)S(1)}, u32[]{:S(2)}, u32[]{:S(2)}) collective-permute-start(f32[1,8,512]{2,1,0:T(8,128)S(1)} %get-tuple-element.63), channel_id=1, source_target_pairs={{0,8},{8,16},{16,24},{1,9},{9,17},{17,25},{2,10},{10,18},{18,26},{... | collective-permute-start | bytes 49160 | tf_op jit(solution)/shard_map/ppermute | solution.py:19
  7.0 8.8 %collective-permute-start = (f32[2,8,512]{2,1,0:T(8,128)S(1)}, f32[2,8,512]{2,1,0:T(8,128)S(1)}, u32[]{:S(2)}, u32[]{:S(2)}) collective-permute-start(f32[2,8,512]{2,1,0:T(8,128)S(1)} %pad_maximum_fusion.3), channel_id=1, source_target_pairs={{8,0},{16,8},{24,16},{9,1},{17,9},{25,17},{10,2},{18,10},{26,18},{... | collective-permute-start | bytes 98312 | tf_op jit(solution)/shard_map/ppermute | solution.py:18
  9.4 7.4 %collective-permute-start.3 = (f32[16,1,512]{2,1,0:T(1,128)S(1)}, f32[16,1,512]{2,1,0:T(1,128)S(1)}, u32[]{:S(2)}, u32[]{:S(2)}) collective-permute-start(f32[16,1,512]{2,1,0:T(1,128)S(1)} %get-tuple-element.67), channel_id=1, source_target_pairs={{0,1},{1,2},{2,3},{3,4},{4,5},{5,6},{6,7},{8,9},{9,10},{10,11},{11... | collective-permute-start | bytes 98312 | tf_op jit(solution)/shard_map/ppermute | solution.py:21
  11.9 3.8 %copy-start.2 = (f32[16,8,512]{2,1,0:T(8,128)S(1)}, f32[16,8,512]{2,1,0:T(8,128)}, u32[]{:S(2)}) copy-start(f32[16,8,512]{2,1,0:T(8,128)} %param.11) | copy-start | bytes 786436
  11.9 4.8 %collective-permute-start.1 = (f32[16,2,512]{2,1,0:T(2,128)S(1)}, f32[16,2,512]{2,1,0:T(2,128)S(1)}, u32[]{:S(2)}, u32[]{:S(2)}) collective-permute-start(f32[16,2,512]{2,1,0:T(2,128)S(1)} %pad_maximum_fusion.2), channel_id=1, source_target_pairs={{1,0},{2,1},{3,2},{4,3},{5,4},{6,5},{7,6},{9,8},{10,9},{11,10},{12... | collective-permute-start | bytes 196616 | tf_op jit(solution)/shard_map/ppermute | solution.py:20
  14.3 2.5 %copy-start.4 = (f32[16,8,512]{2,1,0:T(8,128)S(1)}, f32[16,8,512]{2,1,0:T(8,128)}, u32[]{:S(2)}) copy-start(f32[16,8,512]{2,1,0:T(8,128)} %param.8) | copy-start | bytes 786436
  14.3 2.5 %copy-start.5 = (f32[16,8,512]{2,1,0:T(8,128)S(1)}, f32[16,8,512]{2,1,0:T(8,128)}, u32[]{:S(2)}) copy-start(f32[16,8,512]{2,1,0:T(8,128)} %param.7) | copy-start | bytes 786436
  18.2 13.3 %collective-permute-start.5 = (f32[1,8,512]{2,1,0:T(8,128)S(1)}, f32[1,8,512]{2,1,0:T(8,128)S(1)}, u32[]{:S(2)}, u32[]{:S(2)}) collective-permute-start(f32[1,8,512]{2,1,0:T(8,128)S(1)} %get-tuple-element.61), channel_id=1, source_target_pairs={{8,0},{16,8},{24,16},{9,1},{17,9},{25,17},{10,2},{18,10},{26,18},{... | collective-permute-start | bytes 49160 | tf_op jit(solution)/shard_map/ppermute | solution.py:18
  19.5 12.0 %collective-permute-start.4 = (f32[1,8,512]{2,1,0:T(8,128)S(1)}, f32[1,8,512]{2,1,0:T(8,128)S(1)}, u32[]{:S(2)}, u32[]{:S(2)}) collective-permute-start(f32[1,8,512]{2,1,0:T(8,128)S(1)} %get-tuple-element.62), channel_id=1, source_target_pairs={{0,8},{8,16},{16,24},{1,9},{9,17},{17,25},{2,10},{10,18},{18,26},{... | collective-permute-start | bytes 49160 | tf_op jit(solution)/shard_map/ppermute | solution.py:19
  24.7 6.9 %collective-permute-start.7 = (f32[16,1,512]{2,1,0:T(1,128)S(1)}, f32[16,1,512]{2,1,0:T(1,128)S(1)}, u32[]{:S(2)}, u32[]{:S(2)}) collective-permute-start(f32[16,1,512]{2,1,0:T(1,128)S(1)} %get-tuple-element.57), channel_id=1, source_target_pairs={{1,0},{2,1},{3,2},{4,3},{5,4},{6,5},{7,6},{9,8},{10,9},{11,10},{12... | collective-permute-start | bytes 98312 | tf_op jit(solution)/shard_map/ppermute | solution.py:20
  26.0 6.0 %collective-permute-start.6 = (f32[16,1,512]{2,1,0:T(1,128)S(1)}, f32[16,1,512]{2,1,0:T(1,128)S(1)}, u32[]{:S(2)}, u32[]{:S(2)}) collective-permute-start(f32[16,1,512]{2,1,0:T(1,128)S(1)} %get-tuple-element.58), channel_id=1, source_target_pairs={{0,1},{1,2},{2,3},{3,4},{4,5},{5,6},{6,7},{8,9},{9,10},{10,11},{11... | collective-permute-start | bytes 98312 | tf_op jit(solution)/shard_map/ppermute | solution.py:21
  32.7 12.3 %collective-permute-start.9 = (f32[1,8,512]{2,1,0:T(8,128)S(1)}, f32[1,8,512]{2,1,0:T(8,128)S(1)}, u32[]{:S(2)}, u32[]{:S(2)}) collective-permute-start(f32[1,8,512]{2,1,0:T(8,128)S(1)} %get-tuple-element.51), channel_id=1, source_target_pairs={{8,0},{16,8},{24,16},{9,1},{17,9},{25,17},{10,2},{18,10},{26,18},{... | collective-permute-start | bytes 49160 | tf_op jit(solution)/shard_map/ppermute | solution.py:18
  34.0 11.0 %collective-permute-start.8 = (f32[1,8,512]{2,1,0:T(8,128)S(1)}, f32[1,8,512]{2,1,0:T(8,128)S(1)}, u32[]{:S(2)}, u32[]{:S(2)}) collective-permute-start(f32[1,8,512]{2,1,0:T(8,128)S(1)} %get-tuple-element.52), channel_id=1, source_target_pairs={{0,8},{8,16},{16,24},{1,9},{9,17},{17,25},{2,10},{10,18},{18,26},{... | collective-permute-start | bytes 49160 | tf_op jit(solution)/shard_map/ppermute | solution.py:19
  39.2 5.8 %collective-permute-start.11 = (f32[16,1,512]{2,1,0:T(1,128)S(1)}, f32[16,1,512]{2,1,0:T(1,128)S(1)}, u32[]{:S(2)}, u32[]{:S(2)}) collective-permute-start(f32[16,1,512]{2,1,0:T(1,128)S(1)} %get-tuple-element.47), channel_id=1, source_target_pairs={{1,0},{2,1},{3,2},{4,3},{5,4},{6,5},{7,6},{9,8},{10,9},{11,10},{12... | collective-permute-start | bytes 98312 | tf_op jit(solution)/shard_map/ppermute | solution.py:20
  40.5 5.0 %collective-permute-start.10 = (f32[16,1,512]{2,1,0:T(1,128)S(1)}, f32[16,1,512]{2,1,0:T(1,128)S(1)}, u32[]{:S(2)}, u32[]{:S(2)}) collective-permute-start(f32[16,1,512]{2,1,0:T(1,128)S(1)} %get-tuple-element.48), channel_id=1, source_target_pairs={{0,1},{1,2},{2,3},{3,4},{4,5},{5,6},{6,7},{8,9},{9,10},{10,11},{11... | collective-permute-start | bytes 98312 | tf_op jit(solution)/shard_map/ppermute | solution.py:21
  46.2 13.4 %collective-permute-start.13 = (f32[1,8,512]{2,1,0:T(8,128)S(1)}, f32[1,8,512]{2,1,0:T(8,128)S(1)}, u32[]{:S(2)}, u32[]{:S(2)}) collective-permute-start(f32[1,8,512]{2,1,0:T(8,128)S(1)} %get-tuple-element.41), channel_id=1, source_target_pairs={{8,0},{16,8},{24,16},{9,1},{17,9},{25,17},{10,2},{18,10},{26,18},{... | collective-permute-start | bytes 49160 | tf_op jit(solution)/shard_map/ppermute | solution.py:18
  47.5 12.1 %collective-permute-start.12 = (f32[1,8,512]{2,1,0:T(8,128)S(1)}, f32[1,8,512]{2,1,0:T(8,128)S(1)}, u32[]{:S(2)}, u32[]{:S(2)}) collective-permute-start(f32[1,8,512]{2,1,0:T(8,128)S(1)} %get-tuple-element.42), channel_id=1, source_target_pairs={{0,8},{8,16},{16,24},{1,9},{9,17},{17,25},{2,10},{10,18},{18,26},{... | collective-permute-start | bytes 49160 | tf_op jit(solution)/shard_map/ppermute | solution.py:19
  52.7 7.0 %collective-permute-start.15 = (f32[16,1,512]{2,1,0:T(1,128)S(1)}, f32[16,1,512]{2,1,0:T(1,128)S(1)}, u32[]{:S(2)}, u32[]{:S(2)}) collective-permute-start(f32[16,1,512]{2,1,0:T(1,128)S(1)} %get-tuple-element.37), channel_id=1, source_target_pairs={{1,0},{2,1},{3,2},{4,3},{5,4},{6,5},{7,6},{9,8},{10,9},{11,10},{12... | collective-permute-start | bytes 98312 | tf_op jit(solution)/shard_map/ppermute | solution.py:20
  54.0 6.1 %collective-permute-start.14 = (f32[16,1,512]{2,1,0:T(1,128)S(1)}, f32[16,1,512]{2,1,0:T(1,128)S(1)}, u32[]{:S(2)}, u32[]{:S(2)}) collective-permute-start(f32[16,1,512]{2,1,0:T(1,128)S(1)} %get-tuple-element.38), channel_id=1, source_target_pairs={{0,1},{1,2},{2,3},{3,4},{4,5},{5,6},{6,7},{8,9},{9,10},{10,11},{11... | collective-permute-start | bytes 98312 | tf_op jit(solution)/shard_map/ppermute | solution.py:21
  60.8 13.6 %collective-permute-start.17 = (f32[1,8,512]{2,1,0:T(8,128)S(1)}, f32[1,8,512]{2,1,0:T(8,128)S(1)}, u32[]{:S(2)}, u32[]{:S(2)}) collective-permute-start(f32[1,8,512]{2,1,0:T(8,128)S(1)} %get-tuple-element.31), channel_id=1, source_target_pairs={{8,0},{16,8},{24,16},{9,1},{17,9},{25,17},{10,2},{18,10},{26,18},{... | collective-permute-start | bytes 49160 | tf_op jit(solution)/shard_map/ppermute | solution.py:18
  62.1 12.3 %collective-permute-start.16 = (f32[1,8,512]{2,1,0:T(8,128)S(1)}, f32[1,8,512]{2,1,0:T(8,128)S(1)}, u32[]{:S(2)}, u32[]{:S(2)}) collective-permute-start(f32[1,8,512]{2,1,0:T(8,128)S(1)} %get-tuple-element.32), channel_id=1, source_target_pairs={{0,8},{8,16},{16,24},{1,9},{9,17},{17,25},{2,10},{10,18},{18,26},{... | collective-permute-start | bytes 49160 | tf_op jit(solution)/shard_map/ppermute | solution.py:19
  67.3 7.1 %collective-permute-start.19 = (f32[16,1,512]{2,1,0:T(1,128)S(1)}, f32[16,1,512]{2,1,0:T(1,128)S(1)}, u32[]{:S(2)}, u32[]{:S(2)}) collective-permute-start(f32[16,1,512]{2,1,0:T(1,128)S(1)} %get-tuple-element.27), channel_id=1, source_target_pairs={{1,0},{2,1},{3,2},{4,3},{5,4},{6,5},{7,6},{9,8},{10,9},{11,10},{12... | collective-permute-start | bytes 98312 | tf_op jit(solution)/shard_map/ppermute | solution.py:20
  68.6 6.1 %collective-permute-start.18 = (f32[16,1,512]{2,1,0:T(1,128)S(1)}, f32[16,1,512]{2,1,0:T(1,128)S(1)}, u32[]{:S(2)}, u32[]{:S(2)}) collective-permute-start(f32[16,1,512]{2,1,0:T(1,128)S(1)} %get-tuple-element.28), channel_id=1, source_target_pairs={{0,1},{1,2},{2,3},{3,4},{4,5},{5,6},{6,7},{8,9},{9,10},{10,11},{11... | collective-permute-start | bytes 98312 | tf_op jit(solution)/shard_map/ppermute | solution.py:21
  82.8 3.6 %collective-permute-start.20 = (f32[26]{0:T(128)S(1)}, f32[26]{0:T(128)S(1)}, u32[]{:S(2)}, u32[]{:S(2)}) collective-permute-start(f32[26]{0:T(128)S(1)} %pad_maximum_fusion.4), channel_id=1, source_target_pairs={{0,1},{1,0},{2,3},{3,2},{4,5},{5,4},{6,7},{7,6},{8,9},{9,8},{10,11... | collective-permute-start | bytes 320 | tf_op jit(solution)/shard_map/ppermute | solution.py:53
  87.1 4.0 %collective-permute-start.21 = (f32[26]{0:T(128)S(1)}, f32[26]{0:T(128)S(1)}, u32[]{:S(2)}, u32[]{:S(2)}) collective-permute-start(f32[26]{0:T(128)S(1)} %fusion.77), channel_id=1, source_target_pairs={{0,2},{1,3},{2,0},{3,1},{4,6},{5,7},{6,4},{7,5},{8,10},{9,11},{10,... | collective-permute-start | bytes 320 | tf_op jit(solution)/shard_map/ppermute | solution.py:53
  91.1 4.6 %collective-permute-start.22 = (f32[26]{0:T(128)S(1)}, f32[26]{0:T(128)S(1)}, u32[]{:S(2)}, u32[]{:S(2)}) collective-permute-start(f32[26]{0:T(128)S(1)} %add.166), channel_id=1, source_target_pairs={{0,4},{1,5},{2,6},{3,7},{4,0},{5,1},{6,2},{7,3},{8,12},{9,13},{10,... | collective-permute-start | bytes 320 | tf_op jit(solution)/shard_map/ppermute | solution.py:53
  95.7 4.4 %collective-permute-start.23 = (f32[26]{0:T(128)S(1)}, f32[26]{0:T(128)S(1)}, u32[]{:S(2)}, u32[]{:S(2)}) collective-permute-start(f32[26]{0:T(128)S(1)} %add.167), channel_id=1, source_target_pairs={{0,8},{8,0},{16,24},{24,16},{1,9},{9,1},{17,25},{25,17},{2,10},{10... | collective-permute-start | bytes 320 | tf_op jit(solution)/shard_map/ppermute | solution.py:53
  100.1 3.5 %collective-permute-start.24 = (f32[26]{0:T(128)S(1)}, f32[26]{0:T(128)S(1)}, u32[]{:S(2)}, u32[]{:S(2)}) collective-permute-start(f32[26]{0:T(128)S(1)} %add.168), channel_id=1, source_target_pairs={{0,16},{8,24},{16,0},{24,8},{1,17},{9,25},{17,1},{25,9},{2,18},{10... | collective-permute-start | bytes 320 | tf_op jit(solution)/shard_map/ppermute | solution.py:53

commit v2 on v1

--- a/solution.py
+++ b/solution.py
@@ -2,6 +2,8 @@
 import jax.numpy as jnp
 from jax import lax
 from jax.sharding import PartitionSpec as P
+from jax.experimental import pallas as pl
+from jax.experimental.pallas import tpu as pltpu
 
 STEPS = 4
 
@@ -55,29 +57,74 @@
     return x
 
 
-def cholesky_upper(gram):
-    size = gram.shape[0]
-    rows = []
+def finish_kernel(cells, size, stats_ref, basis_ref, ortho_ref, upper_ref, scale_ref):
+    tile = (8, 128)
+
+    def held(i):
+        return jnp.full(tile, stats_ref[i], jnp.float32)
+
+    scale = jnp.sqrt(held(0) / cells + EPS)
+    square = scale * scale
+    gram = [[held(1 + a * size + b) / cells / square for b in range(size)] for a in range(size)]
+    upper = [[None] * size for _ in range(size)]
     for row in range(size):
-        cur = gram[row]
+        value = gram[row][row]
         for prev in range(row):
-            cur = cur - rows[prev][row] * rows[prev]
-        pivot = jnp.sqrt(cur[row])
-        mask = jnp.arange(size) >= row
-        rows.append(jnp.where(mask, cur / pivot, 0.0))
-    return jnp.stack(rows)
+            value = value - upper[prev][row] * upper[prev][row]
+        pivot = jnp.sqrt(value)
+        upper[row][row] = pivot
+        for col in range(row + 1, size):
+            value = gram[row][col]
+            for prev in range(row):
+                value = value - upper[prev][row] * upper[prev][col]
+            upper[row][col] = value / pivot
+    inverse = [[None] * size for _ in range(size)]
+    for col in range(size):
+        for row in reversed(range(col + 1)):
+            value = jnp.full(tile, 1.0 if row == col else 0.0, jnp.float32)
+            for inner in range(row + 1, col + 1):
+                value = value - upper[row][inner] * inverse[inner][col]
+            inverse[row][col] = value / upper[row][row]
+    rows = lax.broadcasted_iota(jnp.int32, tile, 0)
+    cols = lax.broadcasted_iota(jnp.int32, tile, 1)
+    packed = jnp.zeros(tile, jnp.float32)
+    for row in range(size):
+        for col in range(row, size):
+            packed = jnp.where((rows == row) & (cols == col), upper[row][col], packed)
+    upper_ref[...] = packed
+    scale_ref[...] = scale
+    lanes = basis_ref.shape[-1] // tile[1]
+    weight = [
+        [jnp.tile(inverse[j][k] / scale, (1, lanes)) if j <= k else None for k in range(size)]
+        for j in range(size)
+    ]
+
+    def plane(i, carry):
+        parts = [basis_ref[j, i] for j in range(size)]
+        for k in range(size):
+            acc = parts[0] * weight[0][k]
+            for j in range(1, k + 1):
+                acc = acc + parts[j] * weight[j][k]
+            ortho_ref[k, i] = acc
+        return carry
+
+    lax.fori_loop(0, basis_ref.shape[1], plane, 0)
 
 
-def upper_inverse(upper):
-    size = upper.shape[0]
-    eye = jnp.eye(size, dtype=upper.dtype)
-    rows = [None] * size
-    for row in reversed(range(size)):
-        value = eye[row]
-        for inner in range(row + 1, size):
-            value = value - upper[row, inner] * rows[inner]
-        rows[row] = value / upper[row, row]
-    return jnp.stack(rows)
+def finish(stats, block, cells):
+    size = block.shape[0]
+    vmem = pl.BlockSpec(memory_space=pltpu.VMEM)
+    ortho, upper, scale = pl.pallas_call(
+        lambda *refs: finish_kernel(float(cells), size, *refs),
+        out_shape=(
+            jax.ShapeDtypeStruct(block.shape, jnp.float32),
+            jax.ShapeDtypeStruct((8, 128), jnp.float32),
+            jax.ShapeDtypeStruct((8, 128), jnp.float32),
+        ),
+        in_specs=[pl.BlockSpec(memory_space=pltpu.SMEM), vmem],
+        out_specs=(vmem, vmem, vmem),
+    )(stats, block)
+    return ortho, upper[:size, :size], scale[0, 0]
 
 
 def local(start_field, right_side, accumulation, trans_x, trans_y, trans_z):
@@ -117,11 +164,7 @@
     squares = jnp.sum(residual0 * residual0)
     stats = jnp.concatenate([squares[None], local_gram.reshape(-1)])
     stats = all_sum(stats)
-    scale = jnp.sqrt(stats[0] / cells + EPS)
-    gram = stats[1:].reshape(local_gram.shape) / cells / (scale * scale)
-    upper = cholesky_upper(gram)
-    inverse = upper_inverse(upper) / scale
-    ortho = jnp.einsum("jk,jxyz->kxyz", inverse, block, precision=lax.Precision.HIGHEST)
+    ortho, upper, scale = finish(stats, block, cells)
     return (ortho, upper, scale)
 
 

time: 147 us -> 109 us (0.74)
  other arithmetic: 29.4 us -> 4.88 us
  local copies, waits for them, and re-layouts: 21.2 us -> 8.21 us
  waiting for transfers between devices: 11 us -> 16 us
  between operations: 5.95 us -> 1.23 us
  Pallas kernels: 0 us -> 2.8 us
  starting transfers between devices: 71.8 us -> 70.2 us
  matrix products: 6.39 us -> 4.84 us
    div x8 -> x0, other arithmetic: 13.8 us -> none  [the longest x2 12 us: upper_inverse(): rows[row] = value / upper[row, row]]
    ppermute x5, waiting for transfers between devices: 0.87 us -> 8.26 us  [exchange(): from_high_y = lax.ppermute(to_low_y, 'gy', shift_pairs('gy', -1))]
    slice x24 -> x1, local copies, waits for them, and re-layouts: 8.07 us -> 1.19 us  [finish(): return (ortho, upper[:size, :size], scale[0, 0])]
    select_n x4 -> x0, other arithmetic: 6.26 us -> none  [cholesky_upper(): rows.append(jnp.where(mask, cur / pivot, 0.0))]
    sub x3 -> x0, other arithmetic: 3.93 us -> none  [cholesky_upper(): cur = cur - rows[prev][row] * rows[prev]]
    another operation x8 -> x0, local copies, waits for them, and re-layouts: 3.5 us -> none  [the longest x6 3.34 us: local(): block = jnp.stack(basis)]
    ppermute x5, starting transfers between devices: 21.6 us -> 18.4 us  [exchange(): from_low_y = lax.ppermute(to_high_y, 'gy', shift_pairs('gy', 1))]
    pallas_call x0 -> x1, Pallas kernels: none -> 2.8 us  [finish(): pl.pallas_call(lambda *refs: finish_kernel(float(cells), size, *refs), ou...]
  transfers between devices with their start and end apart: 25 -> 25, of which waited for: 10 -> 10; matrix products, arithmetic and copies ran while one was open for 5% -> 4% of each run, Pallas kernels for 0% -> 0%
where the time goes in v2:
time: 109 us; the launch traced here: 108 us
  starting transfers between devices  70.2 us (64%)
  waiting for transfers between devices  16 us (15%)
  local copies, waits for them, and re-layouts  8.21 us (8%)
  other arithmetic  4.88 us (4%)
  matrix products  4.84 us (4%)
  Pallas kernels  2.8 us (3%)
  between operations  1.23 us (1%)
    ppermute x5, starting transfers between devices, exchange(): from_low_x = lax.ppermute(to_high_x, 'gx', shift_pairs('gx', 1))  25.2 us
    ppermute x5, starting transfers between devices, exchange(): from_low_y = lax.ppermute(to_high_y, 'gy', shift_pairs('gy', 1))  18.4 us
    ppermute x5, starting transfers between devices, all_sum(): x = x + lax.ppermute(x, axis, [(i, i ^ step) for i in range(n)])  13.6 us
    ppermute x5, waiting for transfers between devices, exchange(): from_high_y = lax.ppermute(to_low_y, 'gy', shift_pairs('gy', -1))  8.26 us
    ppermute x5, waiting for transfers between devices, all_sum(): x = x + lax.ppermute(x, axis, [(i, i ^ step) for i in range(n)])  7.67 us
    ppermute x5, starting transfers between devices, exchange(): from_high_y = lax.ppermute(to_low_y, 'gy', shift_pairs('gy', -1))  6.59 us
    ppermute x5, starting transfers between devices, exchange(): from_high_x = lax.ppermute(to_low_x, 'gx', shift_pairs('gx', -1))  6.45 us
    dot_general x1, matrix products, local(): jnp.einsum('axyz,bxyz->ab', block, block, precision=lax.Precision.HIGHEST)  4.84 us
  transfers between devices with their start and end apart: 25, of which 10 were waited for; matrix products, arithmetic and copies ran while one was open for 4% of the time, Pallas kernels for 0%

profile of v2, /device:TPU:0, one launch (start us, length us, event | category | flops | bytes accessed | tf_op | source)
XLA Modules:
  0.0 108.2 jit_solution(9084693059427508145)
XLA Ops:
  0.6 0.8 fusion.64
  1.4 4.8 %collective-permute-start.2 = (f32[1,8,512]{2,1,0:T(8,128)S(1)}, f32[1,8,512]{2,1,0:T(8,128)S(1)}, u32[]{:S(2)}, u32[]{:S(2)}) collective-permute-start(f32[1,8,512]{2,1,0:T(8,128)S(1)} %get-tuple-element.57), channel_id=1, source_target_pairs={{0,8},{8,16},{16,24},{1,9},{9,17},{17,25},{2,10},{10,18},{18,26},{... | collective-permute-start | bytes 49160 | tf_op jit(solution)/shard_map/ppermute | solution.py:21
  6.3 0.7 slice.185
  7.0 1.3 %collective-permute-start = (f32[2,8,512]{2,1,0:T(8,128)S(1)}, f32[2,8,512]{2,1,0:T(8,128)S(1)}, u32[]{:S(2)}, u32[]{:S(2)}) collective-permute-start(f32[2,8,512]{2,1,0:T(8,128)S(1)} %pad_maximum_fusion.3), channel_id=1, source_target_pairs={{8,0},{16,8},{24,16},{9,1},{17,9},{25,17},{10,2},{18,10},{26,18},{... | collective-permute-start | bytes 98312 | tf_op jit(solution)/shard_map/ppermute | solution.py:20
  8.3 1.1 fusion.66
  9.4 1.5 %collective-permute-start.3 = (f32[16,1,512]{2,1,0:T(1,128)S(1)}, f32[16,1,512]{2,1,0:T(1,128)S(1)}, u32[]{:S(2)}, u32[]{:S(2)}) collective-permute-start(f32[16,1,512]{2,1,0:T(1,128)S(1)} %get-tuple-element.61), channel_id=1, source_target_pairs={{0,1},{1,2},{2,3},{3,4},{4,5},{5,6},{6,7},{8,9},{9,10},{10,11},{11... | collective-permute-start | bytes 98312 | tf_op jit(solution)/shard_map/ppermute | solution.py:23
  10.8 1.0 slice.189
  11.8 0.1 pad_maximum_fusion.2
  11.9 1.4 %collective-permute-start.1 = (f32[16,2,512]{2,1,0:T(2,128)S(1)}, f32[16,2,512]{2,1,0:T(2,128)S(1)}, u32[]{:S(2)}, u32[]{:S(2)}) collective-permute-start(f32[16,2,512]{2,1,0:T(2,128)S(1)} %pad_maximum_fusion.2), channel_id=1, source_target_pairs={{1,0},{2,1},{3,2},{4,3},{5,4},{6,5},{7,6},{9,8},{10,9},{11,10},{12... | collective-permute-start | bytes 196616 | tf_op jit(solution)/shard_map/ppermute | solution.py:22
  13.3 1.1 fusion.67
  14.4 0.1 fusion.68
  14.7 0.7 copy-done.2
  15.4 0.1 slice.191
  15.6 1.2 %collective-permute-done.1 = f32[16,2,512]{2,1,0:T(2,128)S(1)} collective-permute-done((f32[16,2,512]{2,1,0:T(2,128)S(1)}, f32[16,2,512]{2,1,0:T(2,128)S(1)}, u32[]{:S(2)}, u32[]{:S(2)}) %collective-permute-start.1) | collective-permute-done | bytes 65568 | tf_op jit(solution)/shard_map/ppermute | solution.py:22
  16.9 1.1 %multiply_reduce_fusion = (f32[]{:T(128)}, f32[16,8,512]{2,1,0:T(8,128)S(1)}) fusion(f32[16,8,512]{2,1,0:T(8,128)S(1)} %copy-done.6, f32[16,8,511]{2,1,0:T(8,128)S(1)} %get-tuple-element.66, f32[16,8,512]{2,1,0:T(8,128)S(1)} %copy-done.3, f32[16,8,511]{2,1,0:T(8,128)S(1)} %get-tuple-element.65, f32[16,1,512]{2,1,0:T(1,128)S(1)} %get-tuple-element.68, ...), kind=kLoop, calls=%fused_computation.65 | loop fusion | flops 1835007 | bytes 4192772 | tf_op jit(solution)/shard_map/reduce_sum | solution.py:164
  18.1 0.1 fusion.62
  18.2 0.1 fusion.63
  18.3 4.5 %collective-permute-start.4 = (f32[1,8,512]{2,1,0:T(8,128)S(1)}, f32[1,8,512]{2,1,0:T(8,128)S(1)}, u32[]{:S(2)}, u32[]{:S(2)}) collective-permute-start(f32[1,8,512]{2,1,0:T(8,128)S(1)} %get-tuple-element.47), channel_id=1, source_target_pairs={{0,8},{8,16},{16,24},{1,9},{9,17},{17,25},{2,10},{10,18},{18,26},{... | collective-permute-start | bytes 49160 | tf_op jit(solution)/shard_map/ppermute | solution.py:21
  22.9 1.3 %collective-permute-start.5 = (f32[1,8,512]{2,1,0:T(8,128)S(1)}, f32[1,8,512]{2,1,0:T(8,128)S(1)}, u32[]{:S(2)}, u32[]{:S(2)}) collective-permute-start(f32[1,8,512]{2,1,0:T(8,128)S(1)} %get-tuple-element.48), channel_id=1, source_target_pairs={{8,0},{16,8},{24,16},{9,1},{17,9},{25,17},{10,2},{18,10},{26,18},{... | collective-permute-start | bytes 49160 | tf_op jit(solution)/shard_map/ppermute | solution.py:20
  24.2 4.6 %collective-permute-start.6 = (f32[16,1,512]{2,1,0:T(1,128)S(1)}, f32[16,1,512]{2,1,0:T(1,128)S(1)}, u32[]{:S(2)}, u32[]{:S(2)}) collective-permute-start(f32[16,1,512]{2,1,0:T(1,128)S(1)} %get-tuple-element.51), channel_id=1, source_target_pairs={{0,1},{1,2},{2,3},{3,4},{4,5},{5,6},{6,7},{8,9},{9,10},{10,11},{11... | collective-permute-start | bytes 98312 | tf_op jit(solution)/shard_map/ppermute | solution.py:23
  28.7 1.3 %collective-permute-start.7 = (f32[16,1,512]{2,1,0:T(1,128)S(1)}, f32[16,1,512]{2,1,0:T(1,128)S(1)}, u32[]{:S(2)}, u32[]{:S(2)}) collective-permute-start(f32[16,1,512]{2,1,0:T(1,128)S(1)} %get-tuple-element.52), channel_id=1, source_target_pairs={{1,0},{2,1},{3,2},{4,3},{5,4},{6,5},{7,6},{9,8},{10,9},{11,10},{12... | collective-permute-start | bytes 98312 | tf_op jit(solution)/shard_map/ppermute | solution.py:22
  30.1 1.9 %collective-permute-done.7 = f32[16,1,512]{2,1,0:T(1,128)S(1)} collective-permute-done((f32[16,1,512]{2,1,0:T(1,128)S(1)}, f32[16,1,512]{2,1,0:T(1,128)S(1)}, u32[]{:S(2)}, u32[]{:S(2)}) %collective-permute-start.7) | collective-permute-done | bytes 32800 | tf_op jit(solution)/shard_map/ppermute | solution.py:22
  32.0 0.4 bitcast_dynamic-update-slice_fusion.3
  32.5 0.1 fusion.57
  32.6 0.1 fusion.58
  32.7 4.9 %collective-permute-start.8 = (f32[1,8,512]{2,1,0:T(8,128)S(1)}, f32[1,8,512]{2,1,0:T(8,128)S(1)}, u32[]{:S(2)}, u32[]{:S(2)}) collective-permute-start(f32[1,8,512]{2,1,0:T(8,128)S(1)} %get-tuple-element.37), channel_id=1, source_target_pairs={{0,8},{8,16},{16,24},{1,9},{9,17},{17,25},{2,10},{10,18},{18,26},{... | collective-permute-start | bytes 49160 | tf_op jit(solution)/shard_map/ppermute | solution.py:21
  37.6 1.3 %collective-permute-start.9 = (f32[1,8,512]{2,1,0:T(8,128)S(1)}, f32[1,8,512]{2,1,0:T(8,128)S(1)}, u32[]{:S(2)}, u32[]{:S(2)}) collective-permute-start(f32[1,8,512]{2,1,0:T(8,128)S(1)} %get-tuple-element.38), channel_id=1, source_target_pairs={{8,0},{16,8},{24,16},{9,1},{17,9},{25,17},{10,2},{18,10},{26,18},{... | collective-permute-start | bytes 49160 | tf_op jit(solution)/shard_map/ppermute | solution.py:20
  38.9 4.3 %collective-permute-start.10 = (f32[16,1,512]{2,1,0:T(1,128)S(1)}, f32[16,1,512]{2,1,0:T(1,128)S(1)}, u32[]{:S(2)}, u32[]{:S(2)}) collective-permute-start(f32[16,1,512]{2,1,0:T(1,128)S(1)} %get-tuple-element.41), channel_id=1, source_target_pairs={{0,1},{1,2},{2,3},{3,4},{4,5},{5,6},{6,7},{8,9},{9,10},{10,11},{11... | collective-permute-start | bytes 98312 | tf_op jit(solution)/shard_map/ppermute | solution.py:23
  43.2 1.3 %collective-permute-start.11 = (f32[16,1,512]{2,1,0:T(1,128)S(1)}, f32[16,1,512]{2,1,0:T(1,128)S(1)}, u32[]{:S(2)}, u32[]{:S(2)}) collective-permute-start(f32[16,1,512]{2,1,0:T(1,128)S(1)} %get-tuple-element.42), channel_id=1, source_target_pairs={{1,0},{2,1},{3,2},{4,3},{5,4},{6,5},{7,6},{9,8},{10,9},{11,10},{12... | collective-permute-start | bytes 98312 | tf_op jit(solution)/shard_map/ppermute | solution.py:22
  44.6 1.7 %collective-permute-done.11 = f32[16,1,512]{2,1,0:T(1,128)S(1)} collective-permute-done((f32[16,1,512]{2,1,0:T(1,128)S(1)}, f32[16,1,512]{2,1,0:T(1,128)S(1)}, u32[]{:S(2)}, u32[]{:S(2)}) %collective-permute-start.11) | collective-permute-done | bytes 32800 | tf_op jit(solution)/shard_map/ppermute | solution.py:22
  46.3 0.4 bitcast_dynamic-update-slice_fusion.2
  46.8 0.1 fusion.52
  46.9 0.1 fusion.53
  47.0 5.4 %collective-permute-start.12 = (f32[1,8,512]{2,1,0:T(8,128)S(1)}, f32[1,8,512]{2,1,0:T(8,128)S(1)}, u32[]{:S(2)}, u32[]{:S(2)}) collective-permute-start(f32[1,8,512]{2,1,0:T(8,128)S(1)} %get-tuple-element.27), channel_id=1, source_target_pairs={{0,8},{8,16},{16,24},{1,9},{9,17},{17,25},{2,10},{10,18},{18,26},{... | collective-permute-start | bytes 49160 | tf_op jit(solution)/shard_map/ppermute | solution.py:21
  52.5 1.3 %collective-permute-start.13 = (f32[1,8,512]{2,1,0:T(8,128)S(1)}, f32[1,8,512]{2,1,0:T(8,128)S(1)}, u32[]{:S(2)}, u32[]{:S(2)}) collective-permute-start(f32[1,8,512]{2,1,0:T(8,128)S(1)} %get-tuple-element.28), channel_id=1, source_target_pairs={{8,0},{16,8},{24,16},{9,1},{17,9},{25,17},{10,2},{18,10},{26,18},{... | collective-permute-start | bytes 49160 | tf_op jit(solution)/shard_map/ppermute | solution.py:20
  53.8 4.0 %collective-permute-start.14 = (f32[16,1,512]{2,1,0:T(1,128)S(1)}, f32[16,1,512]{2,1,0:T(1,128)S(1)}, u32[]{:S(2)}, u32[]{:S(2)}) collective-permute-start(f32[16,1,512]{2,1,0:T(1,128)S(1)} %get-tuple-element.31), channel_id=1, source_target_pairs={{0,1},{1,2},{2,3},{3,4},{4,5},{5,6},{6,7},{8,9},{9,10},{10,11},{11... | collective-permute-start | bytes 98312 | tf_op jit(solution)/shard_map/ppermute | solution.py:23
  57.8 1.3 %collective-permute-start.15 = (f32[16,1,512]{2,1,0:T(1,128)S(1)}, f32[16,1,512]{2,1,0:T(1,128)S(1)}, u32[]{:S(2)}, u32[]{:S(2)}) collective-permute-start(f32[16,1,512]{2,1,0:T(1,128)S(1)} %get-tuple-element.32), channel_id=1, source_target_pairs={{1,0},{2,1},{3,2},{4,3},{5,4},{6,5},{7,6},{9,8},{10,9},{11,10},{12... | collective-permute-start | bytes 98312 | tf_op jit(solution)/shard_map/ppermute | solution.py:22
  59.2 1.7 %collective-permute-done.15 = f32[16,1,512]{2,1,0:T(1,128)S(1)} collective-permute-done((f32[16,1,512]{2,1,0:T(1,128)S(1)}, f32[16,1,512]{2,1,0:T(1,128)S(1)}, u32[]{:S(2)}, u32[]{:S(2)}) %collective-permute-start.15) | collective-permute-done | bytes 32800 | tf_op jit(solution)/shard_map/ppermute | solution.py:22
  60.9 0.4 bitcast_dynamic-update-slice_fusion.1
  61.4 0.1 fusion.48
  61.5 0.1 fusion.44
  61.6 5.4 %collective-permute-start.16 = (f32[1,8,512]{2,1,0:T(8,128)S(1)}, f32[1,8,512]{2,1,0:T(8,128)S(1)}, u32[]{:S(2)}, u32[]{:S(2)}) collective-permute-start(f32[1,8,512]{2,1,0:T(8,128)S(1)} %get-tuple-element.19), channel_id=1, source_target_pairs={{0,8},{8,16},{16,24},{1,9},{9,17},{17,25},{2,10},{10,18},{18,26},{... | collective-permute-start | bytes 49160 | tf_op jit(solution)/shard_map/ppermute | solution.py:21
  67.1 1.3 %collective-permute-start.17 = (f32[1,8,512]{2,1,0:T(8,128)S(1)}, f32[1,8,512]{2,1,0:T(8,128)S(1)}, u32[]{:S(2)}, u32[]{:S(2)}) collective-permute-start(f32[1,8,512]{2,1,0:T(8,128)S(1)} %get-tuple-element.20), channel_id=1, source_target_pairs={{8,0},{16,8},{24,16},{9,1},{17,9},{25,17},{10,2},{18,10},{26,18},{... | collective-permute-start | bytes 49160 | tf_op jit(solution)/shard_map/ppermute | solution.py:20
  68.4 4.0 %collective-permute-start.18 = (f32[16,1,512]{2,1,0:T(1,128)S(1)}, f32[16,1,512]{2,1,0:T(1,128)S(1)}, u32[]{:S(2)}, u32[]{:S(2)}) collective-permute-start(f32[16,1,512]{2,1,0:T(1,128)S(1)} %get-tuple-element.23), channel_id=1, source_target_pairs={{0,1},{1,2},{2,3},{3,4},{4,5},{5,6},{6,7},{8,9},{9,10},{10,11},{11... | collective-permute-start | bytes 98312 | tf_op jit(solution)/shard_map/ppermute | solution.py:23
  72.4 1.3 %collective-permute-start.19 = (f32[16,1,512]{2,1,0:T(1,128)S(1)}, f32[16,1,512]{2,1,0:T(1,128)S(1)}, u32[]{:S(2)}, u32[]{:S(2)}) collective-permute-start(f32[16,1,512]{2,1,0:T(1,128)S(1)} %get-tuple-element.24), channel_id=1, source_target_pairs={{1,0},{2,1},{3,2},{4,3},{5,4},{6,5},{7,6},{9,8},{10,9},{11,10},{12... | collective-permute-start | bytes 98312 | tf_op jit(solution)/shard_map/ppermute | solution.py:22
  73.8 1.7 %collective-permute-done.19 = f32[16,1,512]{2,1,0:T(1,128)S(1)} collective-permute-done((f32[16,1,512]{2,1,0:T(1,128)S(1)}, f32[16,1,512]{2,1,0:T(1,128)S(1)}, u32[]{:S(2)}, u32[]{:S(2)}) %collective-permute-start.19) | collective-permute-done | bytes 32800 | tf_op jit(solution)/shard_map/ppermute | solution.py:22
  75.5 0.4 bitcast_dynamic-update-slice_fusion.refs_1_
  76.0 4.8 %fusion.2 = f32[5,5]{1,0:T(8,128)S(1)} fusion(f32[5,16,8,512]{3,2,1,0:T(8,128)S(1)} %bitcast_dynamic-update-slice_fusion.refs_1_), kind=kOutput, calls=%fused_computation.2 | convolution fusion | flops 19660800 | bytes 1310820 | tf_op jit(solution)/shard_map/axyz,bxyz->ab/dot_general | solution.py:163
  80.8 0.1 reshape.9
  80.9 0.7 pad_maximum_fusion.4
  81.6 2.4 %collective-permute-start.20 = (f32[26]{0:T(128)S(1)}, f32[26]{0:T(128)S(1)}, u32[]{:S(2)}, u32[]{:S(2)}) collective-permute-start(f32[26]{0:T(128)S(1)} %pad_maximum_fusion.4), channel_id=1, source_target_pairs={{0,1},{1,0},{2,3},{3,2},{4,5},{5,4},{6,7},{7,6},{8,9},{9,8},{10,11... | collective-permute-start | bytes 320 | tf_op jit(solution)/shard_map/ppermute | solution.py:55
  84.1 0.8 collective-permute-done.20
  84.9 0.7 fusion.71
  85.6 1.6 %collective-permute-start.21 = (f32[26]{0:T(128)S(1)}, f32[26]{0:T(128)S(1)}, u32[]{:S(2)}, u32[]{:S(2)}) collective-permute-start(f32[26]{0:T(128)S(1)} %fusion.71), channel_id=1, source_target_pairs={{0,2},{1,3},{2,0},{3,1},{4,6},{5,7},{6,4},{7,5},{8,10},{9,11},{10,... | collective-permute-start | bytes 320 | tf_op jit(solution)/shard_map/ppermute | solution.py:55
  87.2 2.0 %collective-permute-done.21 = f32[26]{0:T(128)S(1)} collective-permute-done((f32[26]{0:T(128)S(1)}, f32[26]{0:T(128)S(1)}, u32[]{:S(2)}, u32[]{:S(2)}) %collective-permute-start.21) | collective-permute-done | bytes 136 | tf_op jit(solution)/shard_map/ppermute | solution.py:55
  89.1 2.6 %collective-permute-start.22 = (f32[26]{0:T(128)S(1)}, f32[26]{0:T(128)S(1)}, u32[]{:S(2)}, u32[]{:S(2)}) collective-permute-start(f32[26]{0:T(128)S(1)} %add.162), channel_id=1, source_target_pairs={{0,4},{1,5},{2,6},{3,7},{4,0},{5,1},{6,2},{7,3},{8,12},{9,13},{10,... | collective-permute-start | bytes 320 | tf_op jit(solution)/shard_map/ppermute | solution.py:55
  91.7 1.9 %collective-permute-done.22 = f32[26]{0:T(128)S(1)} collective-permute-done((f32[26]{0:T(128)S(1)}, f32[26]{0:T(128)S(1)}, u32[]{:S(2)}, u32[]{:S(2)}) %collective-permute-start.22) | collective-permute-done | bytes 136 | tf_op jit(solution)/shard_map/ppermute | solution.py:55
  93.6 3.5 %collective-permute-start.23 = (f32[26]{0:T(128)S(1)}, f32[26]{0:T(128)S(1)}, u32[]{:S(2)}, u32[]{:S(2)}) collective-permute-start(f32[26]{0:T(128)S(1)} %add.163), channel_id=1, source_target_pairs={{0,8},{8,0},{16,24},{24,16},{1,9},{9,1},{17,25},{25,17},{2,10},{10... | collective-permute-start | bytes 320 | tf_op jit(solution)/shard_map/ppermute | solution.py:55
  97.1 1.5 %collective-permute-done.23 = f32[26]{0:T(128)S(1)} collective-permute-done((f32[26]{0:T(128)S(1)}, f32[26]{0:T(128)S(1)}, u32[]{:S(2)}, u32[]{:S(2)}) %collective-permute-start.23) | collective-permute-done | bytes 136 | tf_op jit(solution)/shard_map/ppermute | solution.py:55
  98.7 3.5 %collective-permute-start.24 = (f32[26]{0:T(128)S(1)}, f32[26]{0:T(128)S(1)}, u32[]{:S(2)}, u32[]{:S(2)}) collective-permute-start(f32[26]{0:T(128)S(1)} %add.164), channel_id=1, source_target_pairs={{0,16},{8,24},{16,0},{24,8},{1,17},{9,25},{17,1},{25,9},{2,18},{10... | collective-permute-start | bytes 320 | tf_op jit(solution)/shard_map/ppermute | solution.py:55
  102.1 1.5 %collective-permute-done.24 = f32[26]{0:T(128)S(1)} collective-permute-done((f32[26]{0:T(128)S(1)}, f32[26]{0:T(128)S(1)}, u32[]{:S(2)}, u32[]{:S(2)}) %collective-permute-start.24) | collective-permute-done | bytes 136 | tf_op jit(solution)/shard_map/ppermute | solution.py:55
  103.6 0.5 add.165.refs_0_
  104.2 2.8 %shard_map.85 = (f32[5,16,8,512]{3,2,1,0:T(8,128)}, f32[8,128]{1,0:T(8,128)}, f32[8,128]{1,0:T(8,128)}) custom-call(f32[26]{0:T(128)} %add.165.refs_0_, f32[5,16,8,512]{3,2,1,0:T(8,128)} %copy-done.1), custom_call_target="tpu_custom_call" | custom-call | tf_op jit(solution)/shard_map/pallas_call | solution.py:117
  107.0 1.2 %slice.243 = f32[1,1]{1,0:T(1,128)} slice(f32[8,128]{1,0:T(8,128)} %get-tuple-element.8), slice={[0:1], [0:1]} | slice | bytes 8 | tf_op jit(solution)/shard_map/slice | solution.py:127
  (50 shorter events, 0.7 us)
Async XLA Ops:
  0.6 13.8 %copy-start = (f32[16,8,512]{2,1,0:T(8,128)S(1)}, f32[16,8,512]{2,1,0:T(8,128)}, u32[]{:S(2)}) copy-start(f32[16,8,512]{2,1,0:T(8,128)} %param.6) | copy-start | bytes 786436
  1.4 15.4 %collective-permute-start.2 = (f32[1,8,512]{2,1,0:T(8,128)S(1)}, f32[1,8,512]{2,1,0:T(8,128)S(1)}, u32[]{:S(2)}, u32[]{:S(2)}) collective-permute-start(f32[1,8,512]{2,1,0:T(8,128)S(1)} %get-tuple-element.57), channel_id=1, source_target_pairs={{0,8},{8,16},{16,24},{1,9},{9,17},{17,25},{2,10},{10,18},{18,26},{... | collective-permute-start | bytes 49160 | tf_op jit(solution)/shard_map/ppermute | solution.py:21
  7.0 8.6 %collective-permute-start = (f32[2,8,512]{2,1,0:T(8,128)S(1)}, f32[2,8,512]{2,1,0:T(8,128)S(1)}, u32[]{:S(2)}, u32[]{:S(2)}) collective-permute-start(f32[2,8,512]{2,1,0:T(8,128)S(1)} %pad_maximum_fusion.3), channel_id=1, source_target_pairs={{8,0},{16,8},{24,16},{9,1},{17,9},{25,17},{10,2},{18,10},{26,18},{... | collective-permute-start | bytes 98312 | tf_op jit(solution)/shard_map/ppermute | solution.py:20
  9.4 7.5 %collective-permute-start.3 = (f32[16,1,512]{2,1,0:T(1,128)S(1)}, f32[16,1,512]{2,1,0:T(1,128)S(1)}, u32[]{:S(2)}, u32[]{:S(2)}) collective-permute-start(f32[16,1,512]{2,1,0:T(1,128)S(1)} %get-tuple-element.61), channel_id=1, source_target_pairs={{0,1},{1,2},{2,3},{3,4},{4,5},{5,6},{6,7},{8,9},{9,10},{10,11},{11... | collective-permute-start | bytes 98312 | tf_op jit(solution)/shard_map/ppermute | solution.py:23
  11.9 2.8 %copy-start.4 = (f32[16,8,512]{2,1,0:T(8,128)S(1)}, f32[16,8,512]{2,1,0:T(8,128)}, u32[]{:S(2)}) copy-start(f32[16,8,512]{2,1,0:T(8,128)} %param.9) | copy-start | bytes 786436
  11.9 4.9 %collective-permute-start.1 = (f32[16,2,512]{2,1,0:T(2,128)S(1)}, f32[16,2,512]{2,1,0:T(2,128)S(1)}, u32[]{:S(2)}, u32[]{:S(2)}) collective-permute-start(f32[16,2,512]{2,1,0:T(2,128)S(1)} %pad_maximum_fusion.2), channel_id=1, source_target_pairs={{1,0},{2,1},{3,2},{4,3},{5,4},{6,5},{7,6},{9,8},{10,9},{11,10},{12... | collective-permute-start | bytes 196616 | tf_op jit(solution)/shard_map/ppermute | solution.py:22
  14.4 1.0 copy-start.2
  14.4 1.0 copy-start.3
  14.6 2.3 %copy-start.5 = (f32[16,8,512]{2,1,0:T(8,128)S(1)}, f32[16,8,512]{2,1,0:T(8,128)}, u32[]{:S(2)}) copy-start(f32[16,8,512]{2,1,0:T(8,128)} %param.8) | copy-start | bytes 786436
  14.6 2.3 %copy-start.6 = (f32[16,8,512]{2,1,0:T(8,128)S(1)}, f32[16,8,512]{2,1,0:T(8,128)}, u32[]{:S(2)}) copy-start(f32[16,8,512]{2,1,0:T(8,128)} %param.7) | copy-start | bytes 786436
  18.3 11.8 %collective-permute-start.4 = (f32[1,8,512]{2,1,0:T(8,128)S(1)}, f32[1,8,512]{2,1,0:T(8,128)S(1)}, u32[]{:S(2)}, u32[]{:S(2)}) collective-permute-start(f32[1,8,512]{2,1,0:T(8,128)S(1)} %get-tuple-element.47), channel_id=1, source_target_pairs={{0,8},{8,16},{16,24},{1,9},{9,17},{17,25},{2,10},{10,18},{18,26},{... | collective-permute-start | bytes 49160 | tf_op jit(solution)/shard_map/ppermute | solution.py:21
  22.9 7.2 %collective-permute-start.5 = (f32[1,8,512]{2,1,0:T(8,128)S(1)}, f32[1,8,512]{2,1,0:T(8,128)S(1)}, u32[]{:S(2)}, u32[]{:S(2)}) collective-permute-start(f32[1,8,512]{2,1,0:T(8,128)S(1)} %get-tuple-element.48), channel_id=1, source_target_pairs={{8,0},{16,8},{24,16},{9,1},{17,9},{25,17},{10,2},{18,10},{26,18},{... | collective-permute-start | bytes 49160 | tf_op jit(solution)/shard_map/ppermute | solution.py:20
  24.2 5.9 %collective-permute-start.6 = (f32[16,1,512]{2,1,0:T(1,128)S(1)}, f32[16,1,512]{2,1,0:T(1,128)S(1)}, u32[]{:S(2)}, u32[]{:S(2)}) collective-permute-start(f32[16,1,512]{2,1,0:T(1,128)S(1)} %get-tuple-element.51), channel_id=1, source_target_pairs={{0,1},{1,2},{2,3},{3,4},{4,5},{5,6},{6,7},{8,9},{9,10},{10,11},{11... | collective-permute-start | bytes 98312 | tf_op jit(solution)/shard_map/ppermute | solution.py:23
  28.7 3.3 %collective-permute-start.7 = (f32[16,1,512]{2,1,0:T(1,128)S(1)}, f32[16,1,512]{2,1,0:T(1,128)S(1)}, u32[]{:S(2)}, u32[]{:S(2)}) collective-permute-start(f32[16,1,512]{2,1,0:T(1,128)S(1)} %get-tuple-element.52), channel_id=1, source_target_pairs={{1,0},{2,1},{3,2},{4,3},{5,4},{6,5},{7,6},{9,8},{10,9},{11,10},{12... | collective-permute-start | bytes 98312 | tf_op jit(solution)/shard_map/ppermute | solution.py:22
  32.7 11.9 %collective-permute-start.8 = (f32[1,8,512]{2,1,0:T(8,128)S(1)}, f32[1,8,512]{2,1,0:T(8,128)S(1)}, u32[]{:S(2)}, u32[]{:S(2)}) collective-permute-start(f32[1,8,512]{2,1,0:T(8,128)S(1)} %get-tuple-element.37), channel_id=1, source_target_pairs={{0,8},{8,16},{16,24},{1,9},{9,17},{17,25},{2,10},{10,18},{18,26},{... | collective-permute-start | bytes 49160 | tf_op jit(solution)/shard_map/ppermute | solution.py:21
  37.6 6.9 %collective-permute-start.9 = (f32[1,8,512]{2,1,0:T(8,128)S(1)}, f32[1,8,512]{2,1,0:T(8,128)S(1)}, u32[]{:S(2)}, u32[]{:S(2)}) collective-permute-start(f32[1,8,512]{2,1,0:T(8,128)S(1)} %get-tuple-element.38), channel_id=1, source_target_pairs={{8,0},{16,8},{24,16},{9,1},{17,9},{25,17},{10,2},{18,10},{26,18},{... | collective-permute-start | bytes 49160 | tf_op jit(solution)/shard_map/ppermute | solution.py:20
  38.9 5.6 %collective-permute-start.10 = (f32[16,1,512]{2,1,0:T(1,128)S(1)}, f32[16,1,512]{2,1,0:T(1,128)S(1)}, u32[]{:S(2)}, u32[]{:S(2)}) collective-permute-start(f32[16,1,512]{2,1,0:T(1,128)S(1)} %get-tuple-element.41), channel_id=1, source_target_pairs={{0,1},{1,2},{2,3},{3,4},{4,5},{5,6},{6,7},{8,9},{9,10},{10,11},{11... | collective-permute-start | bytes 98312 | tf_op jit(solution)/shard_map/ppermute | solution.py:23
  43.2 3.1 %collective-permute-start.11 = (f32[16,1,512]{2,1,0:T(1,128)S(1)}, f32[16,1,512]{2,1,0:T(1,128)S(1)}, u32[]{:S(2)}, u32[]{:S(2)}) collective-permute-start(f32[16,1,512]{2,1,0:T(1,128)S(1)} %get-tuple-element.42), channel_id=1, source_target_pairs={{1,0},{2,1},{3,2},{4,3},{5,4},{6,5},{7,6},{9,8},{10,9},{11,10},{12... | collective-permute-start | bytes 98312 | tf_op jit(solution)/shard_map/ppermute | solution.py:22
  47.0 12.2 %collective-permute-start.12 = (f32[1,8,512]{2,1,0:T(8,128)S(1)}, f32[1,8,512]{2,1,0:T(8,128)S(1)}, u32[]{:S(2)}, u32[]{:S(2)}) collective-permute-start(f32[1,8,512]{2,1,0:T(8,128)S(1)} %get-tuple-element.27), channel_id=1, source_target_pairs={{0,8},{8,16},{16,24},{1,9},{9,17},{17,25},{2,10},{10,18},{18,26},{... | collective-permute-start | bytes 49160 | tf_op jit(solution)/shard_map/ppermute | solution.py:21
  52.5 6.7 %collective-permute-start.13 = (f32[1,8,512]{2,1,0:T(8,128)S(1)}, f32[1,8,512]{2,1,0:T(8,128)S(1)}, u32[]{:S(2)}, u32[]{:S(2)}) collective-permute-start(f32[1,8,512]{2,1,0:T(8,128)S(1)} %get-tuple-element.28), channel_id=1, source_target_pairs={{8,0},{16,8},{24,16},{9,1},{17,9},{25,17},{10,2},{18,10},{26,18},{... | collective-permute-start | bytes 49160 | tf_op jit(solution)/shard_map/ppermute | solution.py:20
  53.8 5.4 %collective-permute-start.14 = (f32[16,1,512]{2,1,0:T(1,128)S(1)}, f32[16,1,512]{2,1,0:T(1,128)S(1)}, u32[]{:S(2)}, u32[]{:S(2)}) collective-permute-start(f32[16,1,512]{2,1,0:T(1,128)S(1)} %get-tuple-element.31), channel_id=1, source_target_pairs={{0,1},{1,2},{2,3},{3,4},{4,5},{5,6},{6,7},{8,9},{9,10},{10,11},{11... | collective-permute-start | bytes 98312 | tf_op jit(solution)/shard_map/ppermute | solution.py:23
  57.8 3.1 %collective-permute-start.15 = (f32[16,1,512]{2,1,0:T(1,128)S(1)}, f32[16,1,512]{2,1,0:T(1,128)S(1)}, u32[]{:S(2)}, u32[]{:S(2)}) collective-permute-start(f32[16,1,512]{2,1,0:T(1,128)S(1)} %get-tuple-element.32), channel_id=1, source_target_pairs={{1,0},{2,1},{3,2},{4,3},{5,4},{6,5},{7,6},{9,8},{10,9},{11,10},{12... | collective-permute-start | bytes 98312 | tf_op jit(solution)/shard_map/ppermute | solution.py:22
  61.6 12.2 %collective-permute-start.16 = (f32[1,8,512]{2,1,0:T(8,128)S(1)}, f32[1,8,512]{2,1,0:T(8,128)S(1)}, u32[]{:S(2)}, u32[]{:S(2)}) collective-permute-start(f32[1,8,512]{2,1,0:T(8,128)S(1)} %get-tuple-element.19), channel_id=1, source_target_pairs={{0,8},{8,16},{16,24},{1,9},{9,17},{17,25},{2,10},{10,18},{18,26},{... | collective-permute-start | bytes 49160 | tf_op jit(solution)/shard_map/ppermute | solution.py:21
  67.1 6.7 %collective-permute-start.17 = (f32[1,8,512]{2,1,0:T(8,128)S(1)}, f32[1,8,512]{2,1,0:T(8,128)S(1)}, u32[]{:S(2)}, u32[]{:S(2)}) collective-permute-start(f32[1,8,512]{2,1,0:T(8,128)S(1)} %get-tuple-element.20), channel_id=1, source_target_pairs={{8,0},{16,8},{24,16},{9,1},{17,9},{25,17},{10,2},{18,10},{26,18},{... | collective-permute-start | bytes 49160 | tf_op jit(solution)/shard_map/ppermute | solution.py:20
  68.4 5.4 %collective-permute-start.18 = (f32[16,1,512]{2,1,0:T(1,128)S(1)}, f32[16,1,512]{2,1,0:T(1,128)S(1)}, u32[]{:S(2)}, u32[]{:S(2)}) collective-permute-start(f32[16,1,512]{2,1,0:T(1,128)S(1)} %get-tuple-element.23), channel_id=1, source_target_pairs={{0,1},{1,2},{2,3},{3,4},{4,5},{5,6},{6,7},{8,9},{9,10},{10,11},{11... | collective-permute-start | bytes 98312 | tf_op jit(solution)/shard_map/ppermute | solution.py:23
  72.4 3.1 %collective-permute-start.19 = (f32[16,1,512]{2,1,0:T(1,128)S(1)}, f32[16,1,512]{2,1,0:T(1,128)S(1)}, u32[]{:S(2)}, u32[]{:S(2)}) collective-permute-start(f32[16,1,512]{2,1,0:T(1,128)S(1)} %get-tuple-element.24), channel_id=1, source_target_pairs={{1,0},{2,1},{3,2},{4,3},{5,4},{6,5},{7,6},{9,8},{10,9},{11,10},{12... | collective-permute-start | bytes 98312 | tf_op jit(solution)/shard_map/ppermute | solution.py:22
  76.0 28.2 %copy-start.1 = (f32[5,16,8,512]{3,2,1,0:T(8,128)}, f32[5,16,8,512]{3,2,1,0:T(8,128)S(1)}, u32[]{:S(2)}) copy-start(f32[5,16,8,512]{3,2,1,0:T(8,128)S(1)} %bitcast_dynamic-update-slice_fusion.refs_1_) | copy-start | bytes 3932164
  81.6 3.2 %collective-permute-start.20 = (f32[26]{0:T(128)S(1)}, f32[26]{0:T(128)S(1)}, u32[]{:S(2)}, u32[]{:S(2)}) collective-permute-start(f32[26]{0:T(128)S(1)} %pad_maximum_fusion.4), channel_id=1, source_target_pairs={{0,1},{1,0},{2,3},{3,2},{4,5},{5,4},{6,7},{7,6},{8,9},{9,8},{10,11... | collective-permute-start | bytes 320 | tf_op jit(solution)/shard_map/ppermute | solution.py:55
  85.6 3.5 %collective-permute-start.21 = (f32[26]{0:T(128)S(1)}, f32[26]{0:T(128)S(1)}, u32[]{:S(2)}, u32[]{:S(2)}) collective-permute-start(f32[26]{0:T(128)S(1)} %fusion.71), channel_id=1, source_target_pairs={{0,2},{1,3},{2,0},{3,1},{4,6},{5,7},{6,4},{7,5},{8,10},{9,11},{10,... | collective-permute-start | bytes 320 | tf_op jit(solution)/shard_map/ppermute | solution.py:55
  89.1 4.4 %collective-permute-start.22 = (f32[26]{0:T(128)S(1)}, f32[26]{0:T(128)S(1)}, u32[]{:S(2)}, u32[]{:S(2)}) collective-permute-start(f32[26]{0:T(128)S(1)} %add.162), channel_id=1, source_target_pairs={{0,4},{1,5},{2,6},{3,7},{4,0},{5,1},{6,2},{7,3},{8,12},{9,13},{10,... | collective-permute-start | bytes 320 | tf_op jit(solution)/shard_map/ppermute | solution.py:55
  93.6 5.1 %collective-permute-start.23 = (f32[26]{0:T(128)S(1)}, f32[26]{0:T(128)S(1)}, u32[]{:S(2)}, u32[]{:S(2)}) collective-permute-start(f32[26]{0:T(128)S(1)} %add.163), channel_id=1, source_target_pairs={{0,8},{8,0},{16,24},{24,16},{1,9},{9,1},{17,25},{25,17},{2,10},{10... | collective-permute-start | bytes 320 | tf_op jit(solution)/shard_map/ppermute | solution.py:55
  98.7 5.0 %collective-permute-start.24 = (f32[26]{0:T(128)S(1)}, f32[26]{0:T(128)S(1)}, u32[]{:S(2)}, u32[]{:S(2)}) collective-permute-start(f32[26]{0:T(128)S(1)} %add.164), channel_id=1, source_target_pairs={{0,16},{8,24},{16,0},{24,8},{1,17},{9,25},{17,1},{25,9},{2,18},{10... | collective-permute-start | bytes 320 | tf_op jit(solution)/shard_map/ppermute | solution.py:55

commit v3 on v2

--- a/solution.py
+++ b/solution.py
@@ -16,32 +16,17 @@
     return [(i, i + by) for i in range(peers) if 0 <= i + by < peers]
 
 
-def exchange(to_low_x, to_high_x, to_low_y, to_high_y):
-    from_high_x = lax.ppermute(to_low_x, "gx", shift_pairs("gx", -1))
-    from_low_x = lax.ppermute(to_high_x, "gx", shift_pairs("gx", 1))
-    from_high_y = lax.ppermute(to_low_y, "gy", shift_pairs("gy", -1))
-    from_low_y = lax.ppermute(to_high_y, "gy", shift_pairs("gy", 1))
-    return from_low_x, from_high_x, from_low_y, from_high_y
+def deep_halo(packed, depth):
+    from_low = lax.ppermute(packed[-depth:], "gx", shift_pairs("gx", 1))
+    from_high = lax.ppermute(packed[:depth], "gx", shift_pairs("gx", -1))
+    wide = jnp.concatenate([from_low, packed, from_high], axis=0)
+    from_low = lax.ppermute(wide[:, -depth:], "gy", shift_pairs("gy", 1))
+    from_high = lax.ppermute(wide[:, :depth], "gy", shift_pairs("gy", -1))
+    return jnp.concatenate([from_low, wide, from_high], axis=1)
 
 
-def neighbour_sum(u, halo, coef):
-    lo_x, hi_x, lo_y, hi_y = halo
-    tx_lo, tx_hi, ty_lo, ty_hi, tz_lo, tz_hi = coef
-    zero_plane = jnp.zeros_like(u[..., :1])
-    u_xm = jnp.concatenate([lo_x, u[:-1]], axis=0)
-    u_xp = jnp.concatenate([u[1:], hi_x], axis=0)
-    u_ym = jnp.concatenate([lo_y, u[:, :-1]], axis=1)
-    u_yp = jnp.concatenate([u[:, 1:], hi_y], axis=1)
-    u_zm = jnp.concatenate([zero_plane, u[..., :-1]], axis=-1)
-    u_zp = jnp.concatenate([u[..., 1:], zero_plane], axis=-1)
-    total = tx_lo * u_xm + tx_hi * u_xp
-    total = total + ty_lo * u_ym + ty_hi * u_yp
-    total = total + tz_lo * u_zm + tz_hi * u_zp
-    return total
-
-
-def field_halo(u):
-    return exchange(u[:1], u[-1:], u[:, :1], u[:, -1:])
+def shift_z(a):
+    return jnp.concatenate([a[..., 1:], jnp.zeros_like(a[..., :1])], axis=-1)
 
 
 def all_sum(x):
@@ -130,38 +115,61 @@
 def local(start_field, right_side, accumulation, trans_x, trans_y, trans_z):
     size_x, size_y, size_z = start_field.shape
     cells = size_x * size_y * size_z * lax.axis_size("gx") * lax.axis_size("gy")
+    depth = STEPS + 1
 
-    lo_x, hi_both_x, lo_y, hi_both_y = exchange(
-        jnp.concatenate([start_field[:1], trans_x[:1]], axis=0),
-        start_field[-1:],
-        jnp.concatenate([start_field[:, :1], trans_y[:, :1]], axis=1),
-        start_field[:, -1:],
-    )
-    hi_x, plane_x = hi_both_x[:1], hi_both_x[1:]
-    hi_y, plane_y = hi_both_y[:, :1], hi_both_y[:, 1:]
+    inputs = (start_field, right_side, accumulation, trans_x, trans_y, trans_z)
+    wide = deep_halo(jnp.concatenate(inputs, axis=-1), depth)
+    field, rhs, acc, t_x, t_y, t_z = (wide[..., k * size_z : (k + 1) * size_z] for k in range(len(inputs)))
 
-    zero_plane = jnp.zeros_like(trans_z[..., :1])
-    tx_lo = trans_x
-    tx_hi = jnp.concatenate([trans_x[1:], plane_x], axis=0)
-    ty_lo = trans_y
-    ty_hi = jnp.concatenate([trans_y[:, 1:], plane_y], axis=1)
-    tz_lo = trans_z
-    tz_hi = jnp.concatenate([trans_z[..., 1:], zero_plane], axis=-1)
-    coef = (tx_lo, tx_hi, ty_lo, ty_hi, tz_lo, tz_hi)
-    diagonal = accumulation + tx_lo + tx_hi + ty_lo + ty_hi + tz_lo + tz_hi
+    first_x = lax.axis_index("gx") * size_x - depth
+    first_y = lax.axis_index("gy") * size_y - depth
+    grid_x = size_x * lax.axis_size("gx")
+    grid_y = size_y * lax.axis_size("gy")
 
-    total = neighbour_sum(start_field, (lo_x, hi_x, lo_y, hi_y), coef)
-    residual0 = right_side - (diagonal * start_field - total)
+    def region(a, m, dx=0, dy=0):
+        o = depth - m
+        return a[o + dx : o + dx + size_x + 2 * m, o + dy : o + dy + size_y + 2 * m]
 
-    vector = residual0
-    basis = [vector]
+    def inside(m):
+        o = depth - m
+        gi = first_x + o + lax.broadcasted_iota(jnp.int32, (size_x + 2 * m, 1, 1), 0)
+        gj = first_y + o + lax.broadcasted_iota(jnp.int32, (1, size_y + 2 * m, 1), 1)
+        return (gi >= 0) & (gi < grid_x) & (gj >= 0) & (gj < grid_y)
+
+    def coefficients(m):
+        tz_lo = region(t_z, m)
+        return (region(t_x, m), region(t_x, m, 1), region(t_y, m), region(t_y, m, 0, 1), tz_lo, shift_z(tz_lo))
+
+    def neighbour_sum(u, coef):
+        tx_lo, tx_hi, ty_lo, ty_hi, tz_lo, tz_hi = coef
+        centre = u[1:-1, 1:-1]
+        zero_plane = jnp.zeros_like(centre[..., :1])
+        z_low = jnp.concatenate([zero_plane, centre[..., :-1]], axis=-1)
+        z_high = jnp.concatenate([centre[..., 1:], zero_plane], axis=-1)
+        total = tx_lo * u[:-2, 1:-1] + tx_hi * u[2:, 1:-1]
+        total = total + ty_lo * u[1:-1, :-2] + ty_hi * u[1:-1, 2:]
+        total = total + tz_lo * z_low + tz_hi * z_high
+        return total
+
+    coef = coefficients(STEPS)
+    tx_lo, tx_hi, ty_lo, ty_hi, tz_lo, tz_hi = coef
+    diagonal = region(acc, STEPS) + tx_lo + tx_hi + ty_lo + ty_hi + tz_lo + tz_hi
+    total = neighbour_sum(field, coef)
+    residual0 = region(rhs, STEPS) - (diagonal * region(field, STEPS) - total)
+    vector = jnp.where(inside(STEPS), residual0, 0.0)
+
+    basis = [vector[STEPS : STEPS + size_x, STEPS : STEPS + size_y]]
     for step in range(STEPS):
-        total = neighbour_sum(vector, field_halo(vector), coef)
-        vector = 2.0 * total / diagonal
-        basis.append(vector)
+        m = STEPS - 1 - step
+        cut = STEPS - m
+        total = neighbour_sum(vector, coefficients(m))
+        vector = 2.0 * total / diagonal[cut : cut + size_x + 2 * m, cut : cut + size_y + 2 * m]
+        if m:
+            vector = jnp.where(inside(m), vector, 0.0)
+        basis.append(vector[m : m + size_x, m : m + size_y])
     block = jnp.stack(basis)
     local_gram = jnp.einsum("axyz,bxyz->ab", block, block, precision=lax.Precision.HIGHEST)
-    squares = jnp.sum(residual0 * residual0)
+    squares = jnp.sum(basis[0] * basis[0])
     stats = jnp.concatenate([squares[None], local_gram.reshape(-1)])
     stats = all_sum(stats)
     ortho, upper, scale = finish(stats, block, cells)

time: 109 us -> 108 us (level)
  starting transfers between devices: 70.2 us -> 36.9 us
  waiting for transfers between devices: 16 us -> 31.2 us
  local copies, waits for them, and re-layouts: 8.21 us -> 20.5 us
  other arithmetic: 4.88 us -> 10.3 us
    ppermute x20 -> x4, starting transfers between devices: 56.6 us -> 11.8 us  [the longest x1 4.86 us: deep_halo(): from_low = lax.ppermute(packed[-depth:], 'gx', shift_pairs('gx', 1))]
    ppermute x20 -> x4, waiting for transfers between devices: 8.3 us -> 21.8 us  [the longest x1 12.4 us: deep_halo(): from_high = lax.ppermute(packed[:depth], 'gx', shift_pairs('gx', -1))]
    ppermute x5, starting transfers between devices: 13.6 us -> 25.2 us  [all_sum(): x = x + lax.ppermute(x, axis, [(i, i ^ step) for i in range(n)])]
    ppermute x0 -> x2, local copies, waits for them, and re-layouts: none -> 5.07 us  [the longest x1 2.54 us: deep_halo(): from_high = lax.ppermute(wide[:, :depth], 'gy', shift_pairs('gy', -1))]
    select_n x0 -> x4, other arithmetic: none -> 4.87 us  [the longest x3 3.33 us: local(): vector = jnp.where(inside(m), vector, 0.0)]
    unnamed x15 -> x29, local copies, waits for them, and re-layouts: 0.78 us -> 4.81 us
    slice x32 -> x13, local copies, waits for them, and re-layouts: 6.16 us -> 9.32 us  [the longest x2 2.81 us: deep_halo(): from_low = lax.ppermute(wide[:, -depth:], 'gy', shift_pairs('gy', 1))]
    concatenate x2, other arithmetic: 0.07 us -> 2.04 us  [the longest x1 1.8 us: deep_halo(): return jnp.concatenate([from_low, wide, from_high], axis=1)]
  transfers between devices with their start and end apart: 25 -> 9, of which waited for: 10 -> 7; matrix products, arithmetic and copies ran while one was open for 4% -> 6% of each run, Pallas kernels for 0% -> 0%
where the time goes in v3:
time: 108 us
  starting transfers between devices  36.9 us (34%)
  waiting for transfers between devices  31.2 us (29%)
  local copies, waits for them, and re-layouts  20.5 us (19%)
  other arithmetic  10.3 us (10%)
  matrix products  4.84 us (4%)
  Pallas kernels  2.8 us (3%)
    ppermute x5, starting transfers between devices, all_sum(): x = x + lax.ppermute(x, axis, [(i, i ^ step) for i in range(n)])  25.2 us
    ppermute x1, waiting for transfers between devices, deep_halo(): from_high = lax.ppermute(packed[:depth], 'gx', shift_pairs('gx', -1))  12.4 us
    ppermute x5, waiting for transfers between devices, all_sum(): x = x + lax.ppermute(x, axis, [(i, i ^ step) for i in range(n)])  9.44 us
    ppermute x1, waiting for transfers between devices, deep_halo(): from_low = lax.ppermute(packed[-depth:], 'gx', shift_pairs('gx', 1))  9.43 us
    ppermute x1, starting transfers between devices, deep_halo(): from_low = lax.ppermute(packed[-depth:], 'gx', shift_pairs('gx', 1))  4.86 us
    dot_general x1, matrix products, local(): jnp.einsum('axyz,bxyz->ab', block, block, precision=lax.Precision.HIGHEST)  4.84 us
    unnamed x29, local copies, waits for them, and re-layouts  4.81 us
    ppermute x1, starting transfers between devices, deep_halo(): from_low = lax.ppermute(wide[:, -depth:], 'gy', shift_pairs('gy', 1))  4.33 us
  transfers between devices with their start and end apart: 9, of which 7 were waited for; matrix products, arithmetic and copies ran while one was open for 6% of the time, Pallas kernels for 0%

profile of v3, /device:TPU:0, one launch (start us, length us, event | category | flops | bytes accessed | tf_op | source)
XLA Modules:
  0.0 107.6 jit_solution(17911572218949685541)
XLA Ops:
  0.6 0.0 copy-start.5
  0.6 0.0 copy-start.7
  0.7 0.0 copy-start.3
  0.7 1.0 constant_dynamic-update-slice_fusion.5
  1.7 1.0 constant_dynamic-update-slice_fusion.4
  2.7 1.0 constant_dynamic-update-slice_fusion.3
  3.8 0.8 fusion.61
  4.6 4.9 %collective-permute-start = (f32[5,8,3072]{2,1,0:T(8,128)}, f32[5,8,3072]{2,1,0:T(8,128)S(1)}, u32[]{:S(2)}, u32[]{:S(2)}) collective-permute-start(f32[5,8,3072]{2,1,0:T(8,128)} %get-tuple-element.16), channel_id=1, source_target_pairs={{0,8},{8,16},{16,24},{1,9},{9,17},{17,25},{2,10},{10,18},{18,26},{... | collective-permute-start | bytes 1474568 | tf_op jit(solution)/shard_map/ppermute | solution.py:20
  9.5 1.3 %collective-permute-start.1 = (f32[5,8,3072]{2,1,0:T(8,128)S(1)}, f32[5,8,3072]{2,1,0:T(8,128)S(1)}, u32[]{:S(2)}, u32[]{:S(2)}) collective-permute-start(f32[5,8,3072]{2,1,0:T(8,128)S(1)} %get-tuple-element.17), channel_id=1, source_target_pairs={{8,0},{16,8},{24,16},{9,1},{17,9},{25,17},{10,2},{18,10},{26,18},{... | collective-permute-start | bytes 1474568 | tf_op jit(solution)/shard_map/ppermute | solution.py:21
  10.8 9.4 %collective-permute-done = f32[5,8,3072]{2,1,0:T(8,128)S(1)} collective-permute-done((f32[5,8,3072]{2,1,0:T(8,128)}, f32[5,8,3072]{2,1,0:T(8,128)S(1)}, u32[]{:S(2)}, u32[]{:S(2)}) %collective-permute-start) | collective-permute-done | bytes 491552 | tf_op jit(solution)/shard_map/ppermute | solution.py:20
  20.2 12.4 %collective-permute-done.1 = f32[5,8,3072]{2,1,0:T(8,128)S(1)} collective-permute-done((f32[5,8,3072]{2,1,0:T(8,128)S(1)}, f32[5,8,3072]{2,1,0:T(8,128)S(1)}, u32[]{:S(2)}, u32[]{:S(2)}) %collective-permute-start.1) | collective-permute-done | bytes 491552 | tf_op jit(solution)/shard_map/ppermute | solution.py:21
  32.6 0.2 pad_maximum_fusion.1
  32.9 0.6 fusion.60
  33.5 2.2 %copy.12 = f32[26,5,3072]{2,0,1:T(8,128)} copy(f32[26,5,3072]{2,1,0:T(8,128)S(1)} %get-tuple-element.15) | data formatting | bytes 3194880 | tf_op jit(solution)/shard_map/slice | solution.py:24
  35.7 1.3 %collective-permute-start.3 = (f32[26,5,3072]{2,0,1:T(8,128)}, f32[26,5,3072]{2,0,1:T(8,128)}, u32[]{:S(2)}, u32[]{:S(2)}) collective-permute-start(f32[26,5,3072]{2,0,1:T(8,128)} %copy.12), channel_id=1, source_target_pairs={{1,0},{2,1},{3,2},{4,3},{5,4},{6,5},{7,6},{9,8},{10,9},{11,10},{12... | collective-permute-start | bytes 4792328 | tf_op jit(solution)/shard_map/ppermute | solution.py:24
  37.0 2.2 %copy.11 = f32[26,5,3072]{2,0,1:T(8,128)} copy(f32[26,5,3072]{2,1,0:T(8,128)S(1)} %get-tuple-element.14) | data formatting | bytes 3194880 | tf_op jit(solution)/shard_map/slice | solution.py:23
  39.2 4.3 %collective-permute-start.2 = (f32[26,5,3072]{2,0,1:T(8,128)}, f32[26,5,3072]{2,0,1:T(8,128)}, u32[]{:S(2)}, u32[]{:S(2)}) collective-permute-start(f32[26,5,3072]{2,0,1:T(8,128)} %copy.11), channel_id=1, source_target_pairs={{0,1},{1,2},{2,3},{3,4},{4,5},{5,6},{6,7},{8,9},{9,10},{10,11},{11... | collective-permute-start | bytes 4792328 | tf_op jit(solution)/shard_map/ppermute | solution.py:23
  43.5 0.8 slice.364
  44.4 0.1 and_and_fusion.3
  44.5 0.1 and_and_fusion.2
  44.6 0.1 and_and_fusion.1
  44.7 0.1 and_and_fusion
  44.8 2.5 %copy.14 = f32[26,5,3072]{2,1,0:T(8,128)S(1)} copy(f32[26,5,3072]{2,0,1:T(8,128)} %collective-permute-done.3) | data formatting | bytes 3194880 | tf_op jit(solution)/shard_map/ppermute | solution.py:24
  47.3 2.5 %copy.13 = f32[26,5,3072]{2,1,0:T(8,128)S(1)} copy(f32[26,5,3072]{2,0,1:T(8,128)} %collective-permute-done.2) | data formatting | bytes 3194880 | tf_op jit(solution)/shard_map/ppermute | solution.py:23
  49.9 1.8 %pad_maximum_fusion = f32[26,18,3072]{2,1,0:T(8,128)S(1)} fusion(f32[26,5,3072]{2,1,0:T(8,128)S(1)} %copy.14, f32[5,8,3072]{2,1,0:T(8,128)S(1)} %collective-permute-done.1, f32[16,8,3072]{2,1,0:T(8,128)S(1)} %constant_dynamic-update-slice_fusion, f32[5,8,3072]{2,1,0:T(8,128)S(1)} %collective-permute-done, f32[26,5,3072]{2,1,0:T(8,128)S(1)} %copy.13), kind=kLoop, calls=%fused_computation | loop fusion | flops 5750784 | bytes 11501568 | tf_op jit(solution)/shard_map/concatenate | solution.py:25
  51.7 0.7 fusion.59
  52.4 0.3 slice.399
  52.7 0.3 slice.413
  53.0 0.3 slice.426
  53.2 1.5 %fusion.10 = (f32[24,16,512]{2,1,0:T(8,128)S(1)}, f32[24,16,512]{2,1,0:T(8,128)S(1)}) fusion(f32[26,18,3072]{2,1,0:T(8,128)S(1)} %pad_maximum_fusion, f32[24,16,511]{2,1,0:T(8,128)S(1)} %get-tuple-element.13, f32[24,16,511]{2,1,0:T(8,128)S(1)} %get-tuple-element.12, f32[24,16,511]{2,1,0:T(8,128)S(1)} %get-tuple-element.11, pred[24,16]{1,0:T(8,128)(4,1)S(1)} %and_and_fusion.3), kind=kLoop, calls=%fused_computation.11 | loop fusion | flops 4128768 | bytes 13365120 | tf_op jit(solution)/shard_map/jit(_where)/select_n | solution.py:159
  54.8 0.3 fusion.62
  55.1 0.7 multiply_reduce_fusion
  55.8 1.2 %fusion.18 = f32[22,14,512]{2,1,0:T(8,128)S(1)} fusion(f32[24,16,512]{2,1,0:T(8,128)S(1)} %get-tuple-element.10, f32[26,18,3072]{2,1,0:T(8,128)S(1)} %pad_maximum_fusion, f32[24,16,512]{2,1,0:T(8,128)S(1)} %get-tuple-element.9, f32[22,14,511]{2,1,0:T(8,128)S(1)} %get-tuple-element.19, f32[22,14,511]{2,1,0:T(8,128)S(1)} %slice.399, ...), kind=kLoop, calls=%fused_computation.25 | loop fusion | flops 2207744 | bytes 8827588 | tf_op jit(solution)/shard_map/jit(_where)/select_n | solution.py:168
  57.0 0.3 fusion.63
  57.3 1.1 %fusion.25 = f32[20,12,512]{2,1,0:T(8,128)S(1)} fusion(f32[24,16,512]{2,1,0:T(8,128)S(1)} %get-tuple-element.10, f32[26,18,3072]{2,1,0:T(8,128)S(1)} %pad_maximum_fusion, f32[22,14,512]{2,1,0:T(8,128)S(1)} %fusion.18, f32[20,12,511]{2,1,0:T(8,128)S(1)} %get-tuple-element.21, f32[20,12,511]{2,1,0:T(8,128)S(1)} %slice.413, ...), kind=kLoop, calls=%fused_computation.38 | loop fusion | flops 1720320 | bytes 6878640 | tf_op jit(solution)/shard_map/jit(_where)/select_n | solution.py:168
  58.4 0.0 copy-start.2
  58.4 0.3 fusion.64
  58.8 0.6 copy-done.2
  59.4 1.1 fusion.32
  60.5 0.0 copy-start.4
  60.5 0.0 copy-start.6
  60.5 0.0 copy-start.8
  60.5 0.1 fusion.65
  60.7 0.7 copy-done.4
  61.5 0.1 copy-done.6
  61.5 0.1 copy-done.8
  61.6 0.1 copy-done.9
  61.7 0.4 fusion.40.refs_1_
  62.1 4.8 %fusion.2 = f32[5,5]{1,0:T(8,128)S(1)} fusion(f32[5,16,8,512]{3,2,1,0:T(8,128)S(1)} %fusion.40.refs_1_), kind=kOutput, calls=%fused_computation.4 | convolution fusion | flops 19660800 | bytes 1310820 | tf_op jit(solution)/shard_map/axyz,bxyz->ab/dot_general | solution.py:171
  67.0 0.1 reshape.285
  67.0 0.7 pad_maximum_fusion.6
  67.8 18.0 %collective-permute-start.4 = (f32[26]{0:T(128)S(1)}, f32[26]{0:T(128)S(1)}, u32[]{:S(2)}, u32[]{:S(2)}) collective-permute-start(f32[26]{0:T(128)S(1)} %pad_maximum_fusion.6), channel_id=1, source_target_pairs={{0,1},{1,0},{2,3},{3,2},{4,5},{5,4},{6,7},{7,6},{8,9},{9,8},{10,11... | collective-permute-start | bytes 320 | tf_op jit(solution)/shard_map/ppermute | solution.py:40
  85.8 0.8 collective-permute-done.4
  86.6 0.7 fusion.66
  87.3 2.7 %collective-permute-start.5 = (f32[26]{0:T(128)S(1)}, f32[26]{0:T(128)S(1)}, u32[]{:S(2)}, u32[]{:S(2)}) collective-permute-start(f32[26]{0:T(128)S(1)} %fusion.66), channel_id=1, source_target_pairs={{0,2},{1,3},{2,0},{3,1},{4,6},{5,7},{6,4},{7,5},{8,10},{9,11},{10,... | collective-permute-start | bytes 320 | tf_op jit(solution)/shard_map/ppermute | solution.py:40
  90.0 1.5 %collective-permute-done.5 = f32[26]{0:T(128)S(1)} collective-permute-done((f32[26]{0:T(128)S(1)}, f32[26]{0:T(128)S(1)}, u32[]{:S(2)}, u32[]{:S(2)}) %collective-permute-start.5) | collective-permute-done | bytes 136 | tf_op jit(solution)/shard_map/ppermute | solution.py:40
  91.5 3.0 %collective-permute-start.6 = (f32[26]{0:T(128)S(1)}, f32[26]{0:T(128)S(1)}, u32[]{:S(2)}, u32[]{:S(2)}) collective-permute-start(f32[26]{0:T(128)S(1)} %add.336), channel_id=1, source_target_pairs={{0,4},{1,5},{2,6},{3,7},{4,0},{5,1},{6,2},{7,3},{8,12},{9,13},{10,... | collective-permute-start | bytes 320 | tf_op jit(solution)/shard_map/ppermute | solution.py:40
  94.5 1.5 %collective-permute-done.6 = f32[26]{0:T(128)S(1)} collective-permute-done((f32[26]{0:T(128)S(1)}, f32[26]{0:T(128)S(1)}, u32[]{:S(2)}, u32[]{:S(2)}) %collective-permute-start.6) | collective-permute-done | bytes 136 | tf_op jit(solution)/shard_map/ppermute | solution.py:40
  96.0 1.5 %collective-permute-start.7 = (f32[26]{0:T(128)S(1)}, f32[26]{0:T(128)S(1)}, u32[]{:S(2)}, u32[]{:S(2)}) collective-permute-start(f32[26]{0:T(128)S(1)} %add.337), channel_id=1, source_target_pairs={{0,8},{8,0},{16,24},{24,16},{1,9},{9,1},{17,25},{25,17},{2,10},{10... | collective-permute-start | bytes 320 | tf_op jit(solution)/shard_map/ppermute | solution.py:40
  97.5 2.0 %collective-permute-done.7 = f32[26]{0:T(128)S(1)} collective-permute-done((f32[26]{0:T(128)S(1)}, f32[26]{0:T(128)S(1)}, u32[]{:S(2)}, u32[]{:S(2)}) %collective-permute-start.7) | collective-permute-done | bytes 136 | tf_op jit(solution)/shard_map/ppermute | solution.py:40
  99.6 3.5 %collective-permute-done.8 = f32[26]{0:T(128)S(1)} collective-permute-done((f32[26]{0:T(128)S(1)}, f32[26]{0:T(128)S(1)}, u32[]{:S(2)}, u32[]{:S(2)}) %collective-permute-start.8) | collective-permute-done | bytes 136 | tf_op jit(solution)/shard_map/ppermute | solution.py:40
  103.1 0.5 add.339.refs_0_
  103.6 2.8 %shard_map.85 = (f32[5,16,8,512]{3,2,1,0:T(8,128)}, f32[8,128]{1,0:T(8,128)}, f32[8,128]{1,0:T(8,128)}) custom-call(f32[26]{0:T(128)} %add.339.refs_0_, f32[5,16,8,512]{3,2,1,0:T(8,128)} %copy-done), custom_call_target="tpu_custom_call" | custom-call | tf_op jit(solution)/shard_map/pallas_call | solution.py:102
  106.5 1.2 %slice.368 = f32[1,1]{1,0:T(1,128)} slice(f32[8,128]{1,0:T(8,128)} %get-tuple-element.8), slice={[0:1], [0:1]} | slice | bytes 8 | tf_op jit(solution)/shard_map/slice | solution.py:112
  (29 shorter events, 0.3 us)
Async XLA Ops:
  0.6 3.0 %copy-start.5 = (f32[16,8,512]{2,1,0:T(8,128)S(1)}, f32[16,8,512]{2,1,0:T(8,128)}, u32[]{:S(2)}) copy-start(f32[16,8,512]{2,1,0:T(8,128)} %param.9) | copy-start | bytes 786436
  0.6 3.1 %copy-start.7 = (f32[16,8,512]{2,1,0:T(8,128)S(1)}, f32[16,8,512]{2,1,0:T(8,128)}, u32[]{:S(2)}) copy-start(f32[16,8,512]{2,1,0:T(8,128)} %param.10) | copy-start | bytes 786436
  0.7 3.1 %copy-start.3 = (f32[16,8,512]{2,1,0:T(8,128)S(1)}, f32[16,8,512]{2,1,0:T(8,128)}, u32[]{:S(2)}) copy-start(f32[16,8,512]{2,1,0:T(8,128)} %param.11) | copy-start | bytes 786436
  4.6 15.6 %collective-permute-start = (f32[5,8,3072]{2,1,0:T(8,128)}, f32[5,8,3072]{2,1,0:T(8,128)S(1)}, u32[]{:S(2)}, u32[]{:S(2)}) collective-permute-start(f32[5,8,3072]{2,1,0:T(8,128)} %get-tuple-element.16), channel_id=1, source_target_pairs={{0,8},{8,16},{16,24},{1,9},{9,17},{17,25},{2,10},{10,18},{18,26},{... | collective-permute-start | bytes 1474568 | tf_op jit(solution)/shard_map/ppermute | solution.py:20
  9.5 23.1 %collective-permute-start.1 = (f32[5,8,3072]{2,1,0:T(8,128)S(1)}, f32[5,8,3072]{2,1,0:T(8,128)S(1)}, u32[]{:S(2)}, u32[]{:S(2)}) collective-permute-start(f32[5,8,3072]{2,1,0:T(8,128)S(1)} %get-tuple-element.17), channel_id=1, source_target_pairs={{8,0},{16,8},{24,16},{9,1},{17,9},{25,17},{10,2},{18,10},{26,18},{... | collective-permute-start | bytes 1474568 | tf_op jit(solution)/shard_map/ppermute | solution.py:21
  32.6 17.2 %copy-start.1 = (f32[5,8,3072]{2,1,0:T(8,128)}, f32[5,8,3072]{2,1,0:T(8,128)S(1)}, u32[]{:S(2)}) copy-start(f32[5,8,3072]{2,1,0:T(8,128)S(1)} %collective-permute-done.1) | copy-start | bytes 1474564
  35.7 9.1 %collective-permute-start.3 = (f32[26,5,3072]{2,0,1:T(8,128)}, f32[26,5,3072]{2,0,1:T(8,128)}, u32[]{:S(2)}, u32[]{:S(2)}) collective-permute-start(f32[26,5,3072]{2,0,1:T(8,128)} %copy.12), channel_id=1, source_target_pairs={{1,0},{2,1},{3,2},{4,3},{5,4},{6,5},{7,6},{9,8},{10,9},{11,10},{12... | collective-permute-start | bytes 4792328 | tf_op jit(solution)/shard_map/ppermute | solution.py:24
  39.2 8.1 %collective-permute-start.2 = (f32[26,5,3072]{2,0,1:T(8,128)}, f32[26,5,3072]{2,0,1:T(8,128)}, u32[]{:S(2)}, u32[]{:S(2)}) collective-permute-start(f32[26,5,3072]{2,0,1:T(8,128)} %copy.11), channel_id=1, source_target_pairs={{0,1},{1,2},{2,3},{3,4},{4,5},{5,6},{6,7},{8,9},{9,10},{10,11},{11... | collective-permute-start | bytes 4792328 | tf_op jit(solution)/shard_map/ppermute | solution.py:23
  58.4 1.0 copy-start.2
  60.5 1.0 copy-start.4
  60.5 1.0 copy-start.6
  60.5 1.1 %copy-start.8 = (f32[16,8,512]{2,1,0:T(8,128)S(1)}, f32[16,8,512]{2,1,0:T(8,128)}, u32[]{:S(2)}) copy-start(f32[16,8,512]{2,1,0:T(8,128)} %param.10) | copy-start | bytes 786436
  60.5 1.2 %copy-start.9 = (f32[16,8,511]{2,1,0:T(8,128)S(1)}, f32[16,8,511]{2,1,0:T(8,128)}, u32[]{:S(2)}) copy-start(f32[16,8,511]{2,1,0:T(8,128)} %slice.364) | copy-start | bytes 784900
  62.1 41.5 %copy-start = (f32[5,16,8,512]{3,2,1,0:T(8,128)}, f32[5,16,8,512]{3,2,1,0:T(8,128)S(1)}, u32[]{:S(2)}) copy-start(f32[5,16,8,512]{3,2,1,0:T(8,128)S(1)} %fusion.40.refs_1_) | copy-start | bytes 3932164
  67.8 18.8 %collective-permute-start.4 = (f32[26]{0:T(128)S(1)}, f32[26]{0:T(128)S(1)}, u32[]{:S(2)}, u32[]{:S(2)}) collective-permute-start(f32[26]{0:T(128)S(1)} %pad_maximum_fusion.6), channel_id=1, source_target_pairs={{0,1},{1,0},{2,3},{3,2},{4,5},{5,4},{6,7},{7,6},{8,9},{9,8},{10,11... | collective-permute-start | bytes 320 | tf_op jit(solution)/shard_map/ppermute | solution.py:40
  87.3 4.2 %collective-permute-start.5 = (f32[26]{0:T(128)S(1)}, f32[26]{0:T(128)S(1)}, u32[]{:S(2)}, u32[]{:S(2)}) collective-permute-start(f32[26]{0:T(128)S(1)} %fusion.66), channel_id=1, source_target_pairs={{0,2},{1,3},{2,0},{3,1},{4,6},{5,7},{6,4},{7,5},{8,10},{9,11},{10,... | collective-permute-start | bytes 320 | tf_op jit(solution)/shard_map/ppermute | solution.py:40
  91.5 4.6 %collective-permute-start.6 = (f32[26]{0:T(128)S(1)}, f32[26]{0:T(128)S(1)}, u32[]{:S(2)}, u32[]{:S(2)}) collective-permute-start(f32[26]{0:T(128)S(1)} %add.336), channel_id=1, source_target_pairs={{0,4},{1,5},{2,6},{3,7},{4,0},{5,1},{6,2},{7,3},{8,12},{9,13},{10,... | collective-permute-start | bytes 320 | tf_op jit(solution)/shard_map/ppermute | solution.py:40
  96.0 3.5 %collective-permute-start.7 = (f32[26]{0:T(128)S(1)}, f32[26]{0:T(128)S(1)}, u32[]{:S(2)}, u32[]{:S(2)}) collective-permute-start(f32[26]{0:T(128)S(1)} %add.337), channel_id=1, source_target_pairs={{0,8},{8,0},{16,24},{24,16},{1,9},{9,1},{17,25},{25,17},{2,10},{10... | collective-permute-start | bytes 320 | tf_op jit(solution)/shard_map/ppermute | solution.py:40
  99.6 3.5 %collective-permute-start.8 = (f32[26]{0:T(128)S(1)}, f32[26]{0:T(128)S(1)}, u32[]{:S(2)}, u32[]{:S(2)}) collective-permute-start(f32[26]{0:T(128)S(1)} %add.338), channel_id=1, source_target_pairs={{0,16},{8,24},{16,0},{24,8},{1,17},{9,25},{17,1},{25,9},{2,18},{10... | collective-permute-start | bytes 320 | tf_op jit(solution)/shard_map/ppermute | solution.py:40

commit v4 on v2

--- a/solution.py
+++ b/solution.py
@@ -16,11 +16,26 @@
     return [(i, i + by) for i in range(peers) if 0 <= i + by < peers]
 
 
+def swap_pairs(axis, parity):
+    peers = lax.axis_size(axis)
+    pairs = []
+    for i in range(parity, peers - 1, 2):
+        pairs += [(i, i + 1), (i + 1, i)]
+    return pairs
+
+
+def axis_exchange(to_low, to_high, axis):
+    odd = lax.axis_index(axis) % 2 == 1
+    even_swap = lax.ppermute(jnp.where(odd, to_low, to_high), axis, swap_pairs(axis, 0))
+    odd_swap = lax.ppermute(jnp.where(odd, to_high, to_low), axis, swap_pairs(axis, 1))
+    from_low = jnp.where(odd, even_swap, odd_swap)
+    from_high = jnp.where(odd, odd_swap, even_swap)
+    return from_low, from_high
+
+
 def exchange(to_low_x, to_high_x, to_low_y, to_high_y):
-    from_high_x = lax.ppermute(to_low_x, "gx", shift_pairs("gx", -1))
-    from_low_x = lax.ppermute(to_high_x, "gx", shift_pairs("gx", 1))
-    from_high_y = lax.ppermute(to_low_y, "gy", shift_pairs("gy", -1))
-    from_low_y = lax.ppermute(to_high_y, "gy", shift_pairs("gy", 1))
+    from_low_x, from_high_x = axis_exchange(to_low_x, to_high_x, "gx")
+    from_low_y, from_high_y = axis_exchange(to_low_y, to_high_y, "gy")
     return from_low_x, from_high_x, from_low_y, from_high_y
 
 
@@ -131,14 +146,14 @@
     size_x, size_y, size_z = start_field.shape
     cells = size_x * size_y * size_z * lax.axis_size("gx") * lax.axis_size("gy")
 
-    lo_x, hi_both_x, lo_y, hi_both_y = exchange(
+    lo_both_x, hi_both_x, lo_both_y, hi_both_y = exchange(
         jnp.concatenate([start_field[:1], trans_x[:1]], axis=0),
-        start_field[-1:],
+        jnp.concatenate([start_field[-1:], trans_x[-1:]], axis=0),
         jnp.concatenate([start_field[:, :1], trans_y[:, :1]], axis=1),
-        start_field[:, -1:],
+        jnp.concatenate([start_field[:, -1:], trans_y[:, -1:]], axis=1),
     )
-    hi_x, plane_x = hi_both_x[:1], hi_both_x[1:]
-    hi_y, plane_y = hi_both_y[:, :1], hi_both_y[:, 1:]
+    lo_x, hi_x, plane_x = lo_both_x[:1], hi_both_x[:1], hi_both_x[1:]
+    lo_y, hi_y, plane_y = lo_both_y[:, :1], hi_both_y[:, :1], hi_both_y[:, 1:]
 
     zero_plane = jnp.zeros_like(trans_z[..., :1])
     tx_lo = trans_x

time: 109 us -> 81.9 us (0.75)
  starting transfers between devices: 70.2 us -> 52.3 us
  waiting for transfers between devices: 16 us -> 8.33 us
  local copies, waits for them, and re-layouts: 8.21 us -> 6.59 us
    ppermute x20, starting transfers between devices: 56.6 us -> 37.7 us  [the longest x10 31 us: axis_exchange(): lax.ppermute(jnp.where(odd, to_low, to_high), axis, swap_pairs(axis, 0))]
    ppermute x20, waiting for transfers between devices: 8.3 us -> 0.7 us  [the longest x10 0.67 us: axis_exchange(): lax.ppermute(jnp.where(odd, to_low, to_high), axis, swap_pairs(axis, 0))]
    slice x12 -> x2, local copies, waits for them, and re-layouts: 1.93 us -> 0.06 us  [the longest x1 0.05 us: local(): lo_y, hi_y, plane_y = (lo_both_y[:, :1], hi_both_y[:, :1], hi_both_y[:, 1:])]
  transfers between devices with their start and end apart: 25 -> 25, of which waited for: 10 -> 9; matrix products, arithmetic and copies ran while one was open for 4% -> 4% of each run, Pallas kernels for 0% -> 0%
where the time goes in v4:
time: 81.9 us; the launch traced here: 81.4 us
  starting transfers between devices  52.3 us (64%)
  waiting for transfers between devices  8.33 us (10%)
  local copies, waits for them, and re-layouts  6.59 us (8%)
  other arithmetic  5.3 us (6%)
  matrix products  4.84 us (6%)
  Pallas kernels  2.8 us (3%)
  between operations  1.26 us (2%)
    ppermute x10, starting transfers between devices, axis_exchange(): lax.ppermute(jnp.where(odd, to_low, to_high), axis, swap_pairs(axis, 0))  31 us
    ppermute x5, starting transfers between devices, all_sum(): x = x + lax.ppermute(x, axis, [(i, i ^ step) for i in range(n)])  14.6 us
    ppermute x5, waiting for transfers between devices, all_sum(): x = x + lax.ppermute(x, axis, [(i, i ^ step) for i in range(n)])  7.62 us
    ppermute x10, starting transfers between devices, axis_exchange(): lax.ppermute(jnp.where(odd, to_high, to_low), axis, swap_pairs(axis, 1))  6.65 us
    dot_general x1, matrix products, local(): jnp.einsum('axyz,bxyz->ab', block, block, precision=lax.Precision.HIGHEST)  4.84 us
    pallas_call x1, Pallas kernels, finish(): pl.pallas_call(lambda *refs: finish_kernel(float(cells), size, *refs), ou...  2.8 us
  transfers between devices with their start and end apart: 25, of which 9 were waited for; matrix products, arithmetic and copies ran while one was open for 4% of the time, Pallas kernels for 0%

profile of v4, /device:TPU:0, one launch (start us, length us, event | category | flops | bytes accessed | tf_op | source)
XLA Modules:
  0.0 81.4 jit_solution(6998645083153417593)
XLA Ops:
  0.7 0.8 fusion.59
  1.5 3.0 %collective-permute-start.1 = (f32[2,8,512]{2,1,0:T(8,128)S(1)}, f32[2,8,512]{2,1,0:T(8,128)S(1)}, u32[]{:S(2)}, u32[]{:S(2)}) collective-permute-start(f32[2,8,512]{2,1,0:T(8,128)S(1)} %get-tuple-element.83), channel_id=1, source_target_pairs={{0,8},{8,0},{16,24},{24,16},{1,9},{9,1},{17,25},{25,17},{2,10},{10... | collective-permute-start | bytes 98312 | tf_op jit(solution)/shard_map/ppermute | solution.py:29
  4.5 0.7 collective-permute-start
  5.2 1.3 %fusion.62 = (f32[16,1,512]{2,1,0:T(1,128)S(1)}, f32[16,1,512]{2,1,0:T(1,128)S(1)}, f32[16,1,512]{2,1,0:T(1,128)S(1)}, f32[16,1,512]{2,1,0:T(1,128)S(1)}) fusion(f32[16,8,512]{2,1,0:T(8,128)} %param.6, f32[16,8,512]{2,1,0:T(8,128)} %param.10), kind=kLoop, calls=%fused_computation.128 | loop fusion | bytes 262144 | tf_op jit(solution)/shard_map/slice | solution.py:153
  6.5 0.1 broadcast_select_fusion.18
  6.6 0.1 collective-permute-start.3
  6.7 0.8 collective-permute-start.2
  7.5 1.1 %fusion.61 = (f32[16,7,512]{2,1,0:T(8,128)S(1)}, f32[16,7,512]{2,1,0:T(8,128)S(1)}) fusion(f32[16,8,512]{2,1,0:T(8,128)} %param.6), kind=kLoop, calls=%fused_computation.127 | loop fusion | bytes 917504 | tf_op jit(solution)/shard_map/slice | solution.py:48
  8.6 0.1 fusion.64
  8.7 0.1 fusion.58
  8.9 0.7 copy-done.2
  9.6 0.1 copy-done.4
  9.6 0.1 slice.207
  9.8 0.1 fusion.65
  10.0 1.1 %multiply_reduce_fusion = (f32[]{:T(128)}, f32[16,8,512]{2,1,0:T(8,128)S(1)}) fusion(f32[16,8,512]{2,1,0:T(8,128)S(1)} %copy-done.6, f32[16,8,511]{2,1,0:T(8,128)S(1)} %get-tuple-element.70, f32[16,8,512]{2,1,0:T(8,128)S(1)} %copy-done.4, f32[16,8,511]{2,1,0:T(8,128)S(1)} %get-tuple-element.69, f32[16,1,512]{2,1,0:T(1,128)S(1)} %get-tuple-element.82, ...), kind=kLoop, calls=%fused_computation.65 | loop fusion | flops 1835007 | bytes 4192772 | tf_op jit(solution)/shard_map/reduce_sum | solution.py:179
  11.1 0.1 fusion.57
  11.3 0.1 fusion.56
  11.4 4.3 %collective-permute-start.4 = (f32[1,8,512]{2,1,0:T(8,128)S(1)}, f32[1,8,512]{2,1,0:T(8,128)S(1)}, u32[]{:S(2)}, u32[]{:S(2)}) collective-permute-start(f32[1,8,512]{2,1,0:T(8,128)S(1)} %get-tuple-element.49), channel_id=1, source_target_pairs={{0,8},{8,0},{16,24},{24,16},{1,9},{9,1},{17,25},{25,17},{2,10},{10... | collective-permute-start | bytes 49160 | tf_op jit(solution)/shard_map/ppermute | solution.py:29
  15.7 0.7 collective-permute-start.5
  16.4 2.8 %collective-permute-start.6 = (f32[16,1,512]{2,1,0:T(1,128)S(1)}, f32[16,1,512]{2,1,0:T(1,128)S(1)}, u32[]{:S(2)}, u32[]{:S(2)}) collective-permute-start(f32[16,1,512]{2,1,0:T(1,128)S(1)} %get-tuple-element.53), channel_id=1, source_target_pairs={{0,1},{1,0},{2,3},{3,2},{4,5},{5,4},{6,7},{7,6},{8,9},{9,8},{10,11... | collective-permute-start | bytes 98312 | tf_op jit(solution)/shard_map/ppermute | solution.py:29
  19.2 0.7 collective-permute-start.7
  19.9 0.2 collective-permute-done.6
  20.1 0.4 bitcast_dynamic-update-slice_fusion.3
  20.6 0.1 fusion.54
  20.7 0.1 fusion.53
  20.8 2.2 %collective-permute-start.8 = (f32[1,8,512]{2,1,0:T(8,128)S(1)}, f32[1,8,512]{2,1,0:T(8,128)S(1)}, u32[]{:S(2)}, u32[]{:S(2)}) collective-permute-start(f32[1,8,512]{2,1,0:T(8,128)S(1)} %get-tuple-element.39), channel_id=1, source_target_pairs={{0,8},{8,0},{16,24},{24,16},{1,9},{9,1},{17,25},{25,17},{2,10},{10... | collective-permute-start | bytes 49160 | tf_op jit(solution)/shard_map/ppermute | solution.py:29
  23.0 0.7 collective-permute-start.9
  23.7 3.7 %collective-permute-start.10 = (f32[16,1,512]{2,1,0:T(1,128)S(1)}, f32[16,1,512]{2,1,0:T(1,128)S(1)}, u32[]{:S(2)}, u32[]{:S(2)}) collective-permute-start(f32[16,1,512]{2,1,0:T(1,128)S(1)} %get-tuple-element.43), channel_id=1, source_target_pairs={{0,1},{1,0},{2,3},{3,2},{4,5},{5,4},{6,7},{7,6},{8,9},{9,8},{10,11... | collective-permute-start | bytes 98312 | tf_op jit(solution)/shard_map/ppermute | solution.py:29
  27.4 0.7 collective-permute-start.11
  28.1 0.2 collective-permute-done.10
  28.3 0.4 bitcast_dynamic-update-slice_fusion.2
  28.8 0.1 fusion.51
  28.9 0.1 fusion.50
  29.0 4.1 %collective-permute-start.12 = (f32[1,8,512]{2,1,0:T(8,128)S(1)}, f32[1,8,512]{2,1,0:T(8,128)S(1)}, u32[]{:S(2)}, u32[]{:S(2)}) collective-permute-start(f32[1,8,512]{2,1,0:T(8,128)S(1)} %get-tuple-element.29), channel_id=1, source_target_pairs={{0,8},{8,0},{16,24},{24,16},{1,9},{9,1},{17,25},{25,17},{2,10},{10... | collective-permute-start | bytes 49160 | tf_op jit(solution)/shard_map/ppermute | solution.py:29
  33.1 0.7 collective-permute-start.13
  33.8 4.4 %collective-permute-start.14 = (f32[16,1,512]{2,1,0:T(1,128)S(1)}, f32[16,1,512]{2,1,0:T(1,128)S(1)}, u32[]{:S(2)}, u32[]{:S(2)}) collective-permute-start(f32[16,1,512]{2,1,0:T(1,128)S(1)} %get-tuple-element.33), channel_id=1, source_target_pairs={{0,1},{1,0},{2,3},{3,2},{4,5},{5,4},{6,7},{7,6},{8,9},{9,8},{10,11... | collective-permute-start | bytes 98312 | tf_op jit(solution)/shard_map/ppermute | solution.py:29
  38.3 0.7 collective-permute-start.15
  39.0 0.2 collective-permute-done.14
  39.1 0.4 bitcast_dynamic-update-slice_fusion.1
  39.7 0.1 fusion.46
  39.8 0.1 fusion.48
  39.9 1.8 %collective-permute-start.16 = (f32[1,8,512]{2,1,0:T(8,128)S(1)}, f32[1,8,512]{2,1,0:T(8,128)S(1)}, u32[]{:S(2)}, u32[]{:S(2)}) collective-permute-start(f32[1,8,512]{2,1,0:T(8,128)S(1)} %get-tuple-element.21), channel_id=1, source_target_pairs={{0,8},{8,0},{16,24},{24,16},{1,9},{9,1},{17,25},{25,17},{2,10},{10... | collective-permute-start | bytes 49160 | tf_op jit(solution)/shard_map/ppermute | solution.py:29
  41.7 0.7 collective-permute-start.17
  42.4 4.6 %collective-permute-start.18 = (f32[16,1,512]{2,1,0:T(1,128)S(1)}, f32[16,1,512]{2,1,0:T(1,128)S(1)}, u32[]{:S(2)}, u32[]{:S(2)}) collective-permute-start(f32[16,1,512]{2,1,0:T(1,128)S(1)} %get-tuple-element.25), channel_id=1, source_target_pairs={{0,1},{1,0},{2,3},{3,2},{4,5},{5,4},{6,7},{7,6},{8,9},{9,8},{10,11... | collective-permute-start | bytes 98312 | tf_op jit(solution)/shard_map/ppermute | solution.py:29
  46.9 0.7 collective-permute-start.19
  47.6 0.2 collective-permute-done.18
  47.8 0.4 bitcast_dynamic-update-slice_fusion.refs_1_
  48.3 4.8 %fusion.2 = f32[5,5]{1,0:T(8,128)S(1)} fusion(f32[5,16,8,512]{3,2,1,0:T(8,128)S(1)} %bitcast_dynamic-update-slice_fusion.refs_1_), kind=kOutput, calls=%fused_computation.2 | convolution fusion | flops 19660800 | bytes 1310820 | tf_op jit(solution)/shard_map/axyz,bxyz->ab/dot_general | solution.py:178
  53.1 0.1 reshape.9
  53.2 0.7 pad_maximum_fusion.6
  53.9 4.7 %collective-permute-start.20 = (f32[26]{0:T(128)S(1)}, f32[26]{0:T(128)S(1)}, u32[]{:S(2)}, u32[]{:S(2)}) collective-permute-start(f32[26]{0:T(128)S(1)} %pad_maximum_fusion.6), channel_id=1, source_target_pairs={{0,1},{1,0},{2,3},{3,2},{4,5},{5,4},{6,7},{7,6},{8,9},{9,8},{10,11... | collective-permute-start | bytes 320 | tf_op jit(solution)/shard_map/ppermute | solution.py:70
  58.6 0.8 %collective-permute-done.20 = f32[26]{0:T(128)S(1)} collective-permute-done((f32[26]{0:T(128)S(1)}, f32[26]{0:T(128)S(1)}, u32[]{:S(2)}, u32[]{:S(2)}) %collective-permute-start.20) | collective-permute-done | bytes 136 | tf_op jit(solution)/shard_map/ppermute | solution.py:70
  59.4 0.7 fusion.67
  60.2 2.1 %collective-permute-start.21 = (f32[26]{0:T(128)S(1)}, f32[26]{0:T(128)S(1)}, u32[]{:S(2)}, u32[]{:S(2)}) collective-permute-start(f32[26]{0:T(128)S(1)} %fusion.67), channel_id=1, source_target_pairs={{0,2},{1,3},{2,0},{3,1},{4,6},{5,7},{6,4},{7,5},{8,10},{9,11},{10,... | collective-permute-start | bytes 320 | tf_op jit(solution)/shard_map/ppermute | solution.py:70
  62.3 1.5 %collective-permute-done.21 = f32[26]{0:T(128)S(1)} collective-permute-done((f32[26]{0:T(128)S(1)}, f32[26]{0:T(128)S(1)}, u32[]{:S(2)}, u32[]{:S(2)}) %collective-permute-start.21) | collective-permute-done | bytes 136 | tf_op jit(solution)/shard_map/ppermute | solution.py:70
  63.8 3.0 %collective-permute-start.22 = (f32[26]{0:T(128)S(1)}, f32[26]{0:T(128)S(1)}, u32[]{:S(2)}, u32[]{:S(2)}) collective-permute-start(f32[26]{0:T(128)S(1)} %add.179), channel_id=1, source_target_pairs={{0,4},{1,5},{2,6},{3,7},{4,0},{5,1},{6,2},{7,3},{8,12},{9,13},{10,... | collective-permute-start | bytes 320 | tf_op jit(solution)/shard_map/ppermute | solution.py:70
  66.8 1.5 %collective-permute-done.22 = f32[26]{0:T(128)S(1)} collective-permute-done((f32[26]{0:T(128)S(1)}, f32[26]{0:T(128)S(1)}, u32[]{:S(2)}, u32[]{:S(2)}) %collective-permute-start.22) | collective-permute-done | bytes 136 | tf_op jit(solution)/shard_map/ppermute | solution.py:70
  68.3 3.5 %collective-permute-start.23 = (f32[26]{0:T(128)S(1)}, f32[26]{0:T(128)S(1)}, u32[]{:S(2)}, u32[]{:S(2)}) collective-permute-start(f32[26]{0:T(128)S(1)} %add.180), channel_id=1, source_target_pairs={{0,8},{8,0},{16,24},{24,16},{1,9},{9,1},{17,25},{25,17},{2,10},{10... | collective-permute-start | bytes 320 | tf_op jit(solution)/shard_map/ppermute | solution.py:70
  71.8 1.5 %collective-permute-done.23 = f32[26]{0:T(128)S(1)} collective-permute-done((f32[26]{0:T(128)S(1)}, f32[26]{0:T(128)S(1)}, u32[]{:S(2)}, u32[]{:S(2)}) %collective-permute-start.23) | collective-permute-done | bytes 136 | tf_op jit(solution)/shard_map/ppermute | solution.py:70
  73.3 1.3 %collective-permute-start.24 = (f32[26]{0:T(128)S(1)}, f32[26]{0:T(128)S(1)}, u32[]{:S(2)}, u32[]{:S(2)}) collective-permute-start(f32[26]{0:T(128)S(1)} %add.181), channel_id=1, source_target_pairs={{0,16},{8,24},{16,0},{24,8},{1,17},{9,25},{17,1},{25,9},{2,18},{10... | collective-permute-start | bytes 320 | tf_op jit(solution)/shard_map/ppermute | solution.py:70
  74.6 2.3 %collective-permute-done.24 = f32[26]{0:T(128)S(1)} collective-permute-done((f32[26]{0:T(128)S(1)}, f32[26]{0:T(128)S(1)}, u32[]{:S(2)}, u32[]{:S(2)}) %collective-permute-start.24) | collective-permute-done | bytes 136 | tf_op jit(solution)/shard_map/ppermute | solution.py:70
  76.9 0.5 add.182.refs_0_
  77.4 2.8 %shard_map.85 = (f32[5,16,8,512]{3,2,1,0:T(8,128)}, f32[8,128]{1,0:T(8,128)}, f32[8,128]{1,0:T(8,128)}) custom-call(f32[26]{0:T(128)} %add.182.refs_0_, f32[5,16,8,512]{3,2,1,0:T(8,128)} %copy-done.1), custom_call_target="tpu_custom_call" | custom-call | tf_op jit(solution)/shard_map/pallas_call | solution.py:132
  80.2 1.2 %slice.259 = f32[1,1]{1,0:T(1,128)} slice(f32[8,128]{1,0:T(8,128)} %get-tuple-element.8), slice={[0:1], [0:1]} | slice | bytes 8 | tf_op jit(solution)/shard_map/slice | solution.py:142
  (60 shorter events, 0.7 us)
Async XLA Ops:
  0.6 7.9 %copy-start = (f32[16,8,512]{2,1,0:T(8,128)S(1)}, f32[16,8,512]{2,1,0:T(8,128)}, u32[]{:S(2)}) copy-start(f32[16,8,512]{2,1,0:T(8,128)} %param.6) | copy-start | bytes 786436
  1.5 8.3 %collective-permute-start.1 = (f32[2,8,512]{2,1,0:T(8,128)S(1)}, f32[2,8,512]{2,1,0:T(8,128)S(1)}, u32[]{:S(2)}, u32[]{:S(2)}) collective-permute-start(f32[2,8,512]{2,1,0:T(8,128)S(1)} %get-tuple-element.83), channel_id=1, source_target_pairs={{0,8},{8,0},{16,24},{24,16},{1,9},{9,1},{17,25},{25,17},{2,10},{10... | collective-permute-start | bytes 98312 | tf_op jit(solution)/shard_map/ppermute | solution.py:29
  4.5 5.3 %collective-permute-start = (f32[2,8,512]{2,1,0:T(8,128)S(1)}, f32[2,8,512]{2,1,0:T(8,128)S(1)}, u32[]{:S(2)}, u32[]{:S(2)}) collective-permute-start(f32[2,8,512]{2,1,0:T(8,128)S(1)} %get-tuple-element.84), channel_id=1, source_target_pairs={{8,16},{16,8},{9,17},{17,9},{10,18},{18,10},{11,19},{19,11},{12,20... | collective-permute-start | bytes 98312 | tf_op jit(solution)/shard_map/ppermute | solution.py:30
  6.6 3.2 %collective-permute-start.3 = (f32[16,2,512]{2,1,0:T(2,128)S(1)}, f32[16,2,512]{2,1,0:T(2,128)S(1)}, u32[]{:S(2)}, u32[]{:S(2)}) collective-permute-start(f32[16,2,512]{2,1,0:T(2,128)S(1)} %get-tuple-element.71), channel_id=1, source_target_pairs={{0,1},{1,0},{2,3},{3,2},{4,5},{5,4},{6,7},{7,6},{8,9},{9,8},{10,11... | collective-permute-start | bytes 196616 | tf_op jit(solution)/shard_map/ppermute | solution.py:29
  6.7 2.1 %copy-start.3 = (f32[16,8,512]{2,1,0:T(8,128)S(1)}, f32[16,8,512]{2,1,0:T(8,128)}, u32[]{:S(2)}) copy-start(f32[16,8,512]{2,1,0:T(8,128)} %param.9) | copy-start | bytes 786436
  6.7 3.1 %collective-permute-start.2 = (f32[16,2,512]{2,1,0:T(2,128)S(1)}, f32[16,2,512]{2,1,0:T(2,128)S(1)}, u32[]{:S(2)}, u32[]{:S(2)}) collective-permute-start(f32[16,2,512]{2,1,0:T(2,128)S(1)} %get-tuple-element.72), channel_id=1, source_target_pairs={{1,2},{2,1},{3,4},{4,3},{5,6},{6,5},{9,10},{10,9},{11,12},{12,11},... | collective-permute-start | bytes 196616 | tf_op jit(solution)/shard_map/ppermute | solution.py:30
  8.6 1.0 %copy-start.2 = (f32[16,8,512]{2,1,0:T(8,128)S(1)}, f32[16,8,512]{2,1,0:T(8,128)}, u32[]{:S(2)}) copy-start(f32[16,8,512]{2,1,0:T(8,128)} %param.10) | copy-start | bytes 786436
  8.6 1.0 %copy-start.4 = (f32[16,8,512]{2,1,0:T(8,128)S(1)}, f32[16,8,512]{2,1,0:T(8,128)}, u32[]{:S(2)}) copy-start(f32[16,8,512]{2,1,0:T(8,128)} %param.11) | copy-start | bytes 786436
  8.8 1.1 %copy-start.5 = (f32[16,8,512]{2,1,0:T(8,128)S(1)}, f32[16,8,512]{2,1,0:T(8,128)}, u32[]{:S(2)}) copy-start(f32[16,8,512]{2,1,0:T(8,128)} %param.8) | copy-start | bytes 786436
  8.8 1.1 %copy-start.6 = (f32[16,8,512]{2,1,0:T(8,128)S(1)}, f32[16,8,512]{2,1,0:T(8,128)}, u32[]{:S(2)}) copy-start(f32[16,8,512]{2,1,0:T(8,128)} %param.7) | copy-start | bytes 786436
  11.4 8.5 %collective-permute-start.4 = (f32[1,8,512]{2,1,0:T(8,128)S(1)}, f32[1,8,512]{2,1,0:T(8,128)S(1)}, u32[]{:S(2)}, u32[]{:S(2)}) collective-permute-start(f32[1,8,512]{2,1,0:T(8,128)S(1)} %get-tuple-element.49), channel_id=1, source_target_pairs={{0,8},{8,0},{16,24},{24,16},{1,9},{9,1},{17,25},{25,17},{2,10},{10... | collective-permute-start | bytes 49160 | tf_op jit(solution)/shard_map/ppermute | solution.py:29
  15.7 4.2 %collective-permute-start.5 = (f32[1,8,512]{2,1,0:T(8,128)S(1)}, f32[1,8,512]{2,1,0:T(8,128)S(1)}, u32[]{:S(2)}, u32[]{:S(2)}) collective-permute-start(f32[1,8,512]{2,1,0:T(8,128)S(1)} %get-tuple-element.50), channel_id=1, source_target_pairs={{8,16},{16,8},{9,17},{17,9},{10,18},{18,10},{11,19},{19,11},{12,20... | collective-permute-start | bytes 49160 | tf_op jit(solution)/shard_map/ppermute | solution.py:30
  16.4 3.7 %collective-permute-start.6 = (f32[16,1,512]{2,1,0:T(1,128)S(1)}, f32[16,1,512]{2,1,0:T(1,128)S(1)}, u32[]{:S(2)}, u32[]{:S(2)}) collective-permute-start(f32[16,1,512]{2,1,0:T(1,128)S(1)} %get-tuple-element.53), channel_id=1, source_target_pairs={{0,1},{1,0},{2,3},{3,2},{4,5},{5,4},{6,7},{7,6},{8,9},{9,8},{10,11... | collective-permute-start | bytes 98312 | tf_op jit(solution)/shard_map/ppermute | solution.py:29
  19.2 0.9 %collective-permute-start.7 = (f32[16,1,512]{2,1,0:T(1,128)S(1)}, f32[16,1,512]{2,1,0:T(1,128)S(1)}, u32[]{:S(2)}, u32[]{:S(2)}) collective-permute-start(f32[16,1,512]{2,1,0:T(1,128)S(1)} %get-tuple-element.54), channel_id=1, source_target_pairs={{1,2},{2,1},{3,4},{4,3},{5,6},{6,5},{9,10},{10,9},{11,12},{12,11},... | collective-permute-start | bytes 98312 | tf_op jit(solution)/shard_map/ppermute | solution.py:30
  20.8 7.3 %collective-permute-start.8 = (f32[1,8,512]{2,1,0:T(8,128)S(1)}, f32[1,8,512]{2,1,0:T(8,128)S(1)}, u32[]{:S(2)}, u32[]{:S(2)}) collective-permute-start(f32[1,8,512]{2,1,0:T(8,128)S(1)} %get-tuple-element.39), channel_id=1, source_target_pairs={{0,8},{8,0},{16,24},{24,16},{1,9},{9,1},{17,25},{25,17},{2,10},{10... | collective-permute-start | bytes 49160 | tf_op jit(solution)/shard_map/ppermute | solution.py:29
  23.0 5.1 %collective-permute-start.9 = (f32[1,8,512]{2,1,0:T(8,128)S(1)}, f32[1,8,512]{2,1,0:T(8,128)S(1)}, u32[]{:S(2)}, u32[]{:S(2)}) collective-permute-start(f32[1,8,512]{2,1,0:T(8,128)S(1)} %get-tuple-element.40), channel_id=1, source_target_pairs={{8,16},{16,8},{9,17},{17,9},{10,18},{18,10},{11,19},{19,11},{12,20... | collective-permute-start | bytes 49160 | tf_op jit(solution)/shard_map/ppermute | solution.py:30
  23.7 4.5 %collective-permute-start.10 = (f32[16,1,512]{2,1,0:T(1,128)S(1)}, f32[16,1,512]{2,1,0:T(1,128)S(1)}, u32[]{:S(2)}, u32[]{:S(2)}) collective-permute-start(f32[16,1,512]{2,1,0:T(1,128)S(1)} %get-tuple-element.43), channel_id=1, source_target_pairs={{0,1},{1,0},{2,3},{3,2},{4,5},{5,4},{6,7},{7,6},{8,9},{9,8},{10,11... | collective-permute-start | bytes 98312 | tf_op jit(solution)/shard_map/ppermute | solution.py:29
  27.4 0.9 %collective-permute-start.11 = (f32[16,1,512]{2,1,0:T(1,128)S(1)}, f32[16,1,512]{2,1,0:T(1,128)S(1)}, u32[]{:S(2)}, u32[]{:S(2)}) collective-permute-start(f32[16,1,512]{2,1,0:T(1,128)S(1)} %get-tuple-element.44), channel_id=1, source_target_pairs={{1,2},{2,1},{3,4},{4,3},{5,6},{6,5},{9,10},{10,9},{11,12},{12,11},... | collective-permute-start | bytes 98312 | tf_op jit(solution)/shard_map/ppermute | solution.py:30
  29.0 9.9 %collective-permute-start.12 = (f32[1,8,512]{2,1,0:T(8,128)S(1)}, f32[1,8,512]{2,1,0:T(8,128)S(1)}, u32[]{:S(2)}, u32[]{:S(2)}) collective-permute-start(f32[1,8,512]{2,1,0:T(8,128)S(1)} %get-tuple-element.29), channel_id=1, source_target_pairs={{0,8},{8,0},{16,24},{24,16},{1,9},{9,1},{17,25},{25,17},{2,10},{10... | collective-permute-start | bytes 49160 | tf_op jit(solution)/shard_map/ppermute | solution.py:29
  33.1 5.8 %collective-permute-start.13 = (f32[1,8,512]{2,1,0:T(8,128)S(1)}, f32[1,8,512]{2,1,0:T(8,128)S(1)}, u32[]{:S(2)}, u32[]{:S(2)}) collective-permute-start(f32[1,8,512]{2,1,0:T(8,128)S(1)} %get-tuple-element.30), channel_id=1, source_target_pairs={{8,16},{16,8},{9,17},{17,9},{10,18},{18,10},{11,19},{19,11},{12,20... | collective-permute-start | bytes 49160 | tf_op jit(solution)/shard_map/ppermute | solution.py:30
  33.8 5.3 %collective-permute-start.14 = (f32[16,1,512]{2,1,0:T(1,128)S(1)}, f32[16,1,512]{2,1,0:T(1,128)S(1)}, u32[]{:S(2)}, u32[]{:S(2)}) collective-permute-start(f32[16,1,512]{2,1,0:T(1,128)S(1)} %get-tuple-element.33), channel_id=1, source_target_pairs={{0,1},{1,0},{2,3},{3,2},{4,5},{5,4},{6,7},{7,6},{8,9},{9,8},{10,11... | collective-permute-start | bytes 98312 | tf_op jit(solution)/shard_map/ppermute | solution.py:29
  38.3 0.9 %collective-permute-start.15 = (f32[16,1,512]{2,1,0:T(1,128)S(1)}, f32[16,1,512]{2,1,0:T(1,128)S(1)}, u32[]{:S(2)}, u32[]{:S(2)}) collective-permute-start(f32[16,1,512]{2,1,0:T(1,128)S(1)} %get-tuple-element.34), channel_id=1, source_target_pairs={{1,2},{2,1},{3,4},{4,3},{5,6},{6,5},{9,10},{10,9},{11,12},{12,11},... | collective-permute-start | bytes 98312 | tf_op jit(solution)/shard_map/ppermute | solution.py:30
  39.9 7.7 %collective-permute-start.16 = (f32[1,8,512]{2,1,0:T(8,128)S(1)}, f32[1,8,512]{2,1,0:T(8,128)S(1)}, u32[]{:S(2)}, u32[]{:S(2)}) collective-permute-start(f32[1,8,512]{2,1,0:T(8,128)S(1)} %get-tuple-element.21), channel_id=1, source_target_pairs={{0,8},{8,0},{16,24},{24,16},{1,9},{9,1},{17,25},{25,17},{2,10},{10... | collective-permute-start | bytes 49160 | tf_op jit(solution)/shard_map/ppermute | solution.py:29
  41.7 5.9 %collective-permute-start.17 = (f32[1,8,512]{2,1,0:T(8,128)S(1)}, f32[1,8,512]{2,1,0:T(8,128)S(1)}, u32[]{:S(2)}, u32[]{:S(2)}) collective-permute-start(f32[1,8,512]{2,1,0:T(8,128)S(1)} %get-tuple-element.22), channel_id=1, source_target_pairs={{8,16},{16,8},{9,17},{17,9},{10,18},{18,10},{11,19},{19,11},{12,20... | collective-permute-start | bytes 49160 | tf_op jit(solution)/shard_map/ppermute | solution.py:30
  42.4 5.4 %collective-permute-start.18 = (f32[16,1,512]{2,1,0:T(1,128)S(1)}, f32[16,1,512]{2,1,0:T(1,128)S(1)}, u32[]{:S(2)}, u32[]{:S(2)}) collective-permute-start(f32[16,1,512]{2,1,0:T(1,128)S(1)} %get-tuple-element.25), channel_id=1, source_target_pairs={{0,1},{1,0},{2,3},{3,2},{4,5},{5,4},{6,7},{7,6},{8,9},{9,8},{10,11... | collective-permute-start | bytes 98312 | tf_op jit(solution)/shard_map/ppermute | solution.py:29
  46.9 0.9 %collective-permute-start.19 = (f32[16,1,512]{2,1,0:T(1,128)S(1)}, f32[16,1,512]{2,1,0:T(1,128)S(1)}, u32[]{:S(2)}, u32[]{:S(2)}) collective-permute-start(f32[16,1,512]{2,1,0:T(1,128)S(1)} %get-tuple-element.26), channel_id=1, source_target_pairs={{1,2},{2,1},{3,4},{4,3},{5,6},{6,5},{9,10},{10,9},{11,12},{12,11},... | collective-permute-start | bytes 98312 | tf_op jit(solution)/shard_map/ppermute | solution.py:30
  48.3 29.1 %copy-start.1 = (f32[5,16,8,512]{3,2,1,0:T(8,128)}, f32[5,16,8,512]{3,2,1,0:T(8,128)S(1)}, u32[]{:S(2)}) copy-start(f32[5,16,8,512]{3,2,1,0:T(8,128)S(1)} %bitcast_dynamic-update-slice_fusion.refs_1_) | copy-start | bytes 3932164
  53.9 5.5 %collective-permute-start.20 = (f32[26]{0:T(128)S(1)}, f32[26]{0:T(128)S(1)}, u32[]{:S(2)}, u32[]{:S(2)}) collective-permute-start(f32[26]{0:T(128)S(1)} %pad_maximum_fusion.6), channel_id=1, source_target_pairs={{0,1},{1,0},{2,3},{3,2},{4,5},{5,4},{6,7},{7,6},{8,9},{9,8},{10,11... | collective-permute-start | bytes 320 | tf_op jit(solution)/shard_map/ppermute | solution.py:70
  60.2 3.6 %collective-permute-start.21 = (f32[26]{0:T(128)S(1)}, f32[26]{0:T(128)S(1)}, u32[]{:S(2)}, u32[]{:S(2)}) collective-permute-start(f32[26]{0:T(128)S(1)} %fusion.67), channel_id=1, source_target_pairs={{0,2},{1,3},{2,0},{3,1},{4,6},{5,7},{6,4},{7,5},{8,10},{9,11},{10,... | collective-permute-start | bytes 320 | tf_op jit(solution)/shard_map/ppermute | solution.py:70
  63.8 4.6 %collective-permute-start.22 = (f32[26]{0:T(128)S(1)}, f32[26]{0:T(128)S(1)}, u32[]{:S(2)}, u32[]{:S(2)}) collective-permute-start(f32[26]{0:T(128)S(1)} %add.179), channel_id=1, source_target_pairs={{0,4},{1,5},{2,6},{3,7},{4,0},{5,1},{6,2},{7,3},{8,12},{9,13},{10,... | collective-permute-start | bytes 320 | tf_op jit(solution)/shard_map/ppermute | solution.py:70
  68.3 5.0 %collective-permute-start.23 = (f32[26]{0:T(128)S(1)}, f32[26]{0:T(128)S(1)}, u32[]{:S(2)}, u32[]{:S(2)}) collective-permute-start(f32[26]{0:T(128)S(1)} %add.180), channel_id=1, source_target_pairs={{0,8},{8,0},{16,24},{24,16},{1,9},{9,1},{17,25},{25,17},{2,10},{10... | collective-permute-start | bytes 320 | tf_op jit(solution)/shard_map/ppermute | solution.py:70
  73.3 3.5 %collective-permute-start.24 = (f32[26]{0:T(128)S(1)}, f32[26]{0:T(128)S(1)}, u32[]{:S(2)}, u32[]{:S(2)}) collective-permute-start(f32[26]{0:T(128)S(1)} %add.181), channel_id=1, source_target_pairs={{0,16},{8,24},{16,0},{24,8},{1,17},{9,25},{17,1},{25,9},{2,18},{10... | collective-permute-start | bytes 320 | tf_op jit(solution)/shard_map/ppermute | solution.py:70

commit v5 on v4

--- a/solution.py
+++ b/solution.py
@@ -106,8 +106,8 @@
     for row in range(size):
         for col in range(row, size):
             packed = jnp.where((rows == row) & (cols == col), upper[row][col], packed)
-    upper_ref[...] = packed
-    scale_ref[...] = scale
+    upper_ref[...] = packed[: upper_ref.shape[0], : upper_ref.shape[1]]
+    scale_ref[...] = scale[:1, :1]
     lanes = basis_ref.shape[-1] // tile[1]
     weight = [
         [jnp.tile(inverse[j][k] / scale, (1, lanes)) if j <= k else None for k in range(size)]
@@ -133,13 +133,13 @@
         lambda *refs: finish_kernel(float(cells), size, *refs),
         out_shape=(
             jax.ShapeDtypeStruct(block.shape, jnp.float32),
-            jax.ShapeDtypeStruct((8, 128), jnp.float32),
-            jax.ShapeDtypeStruct((8, 128), jnp.float32),
+            jax.ShapeDtypeStruct((size, size), jnp.float32),
+            jax.ShapeDtypeStruct((1, 1), jnp.float32),
         ),
         in_specs=[pl.BlockSpec(memory_space=pltpu.SMEM), vmem],
         out_specs=(vmem, vmem, vmem),
     )(stats, block)
-    return ortho, upper[:size, :size], scale[0, 0]
+    return ortho, upper, scale.reshape(())
 
 
 def local(start_field, right_side, accumulation, trans_x, trans_y, trans_z):
@@ -170,14 +170,17 @@
 
     vector = residual0
     basis = [vector]
+    gram_rows = [[jnp.sum(vector * vector)]]
     for step in range(STEPS):
         total = neighbour_sum(vector, field_halo(vector), coef)
         vector = 2.0 * total / diagonal
+        gram_rows.append([jnp.sum(vector * earlier) for earlier in basis] + [jnp.sum(vector * vector)])
         basis.append(vector)
     block = jnp.stack(basis)
-    local_gram = jnp.einsum("axyz,bxyz->ab", block, block, precision=lax.Precision.HIGHEST)
-    squares = jnp.sum(residual0 * residual0)
-    stats = jnp.concatenate([squares[None], local_gram.reshape(-1)])
+    size = len(basis)
+    local_gram = [[gram_rows[max(a, b)][min(a, b)] for b in range(size)] for a in range(size)]
+    squares = gram_rows[0][0]
+    stats = jnp.stack([squares] + [entry for row in local_gram for entry in row])
     stats = all_sum(stats)
     ortho, upper, scale = finish(stats, block, cells)
     return (ortho, upper, scale)

time: 81.9 us -> 91.5 us (1.12)
  local copies, waits for them, and re-layouts: 6.59 us -> 21.7 us
  matrix products: 4.84 us -> 0 us
  other arithmetic: 5.3 us -> 4.31 us
    another operation x0 -> x1, local copies, waits for them, and re-layouts: none -> 16.5 us  [local(): jnp.stack([squares] + [entry for row in local_gram for entry in row])]
    dot_general x1 -> x0, matrix products: 4.84 us -> none  [local(): jnp.einsum('axyz,bxyz->ab', block, block, precision=lax.Precision.HIGHEST)]
    slice x1 -> x0, local copies, waits for them, and re-layouts: 1.19 us -> none  [finish(): return (ortho, upper[:size, :size], scale[0, 0])]
  transfers between devices with their start and end apart: 25 -> 25, of which waited for: 9 -> 9; matrix products, arithmetic and copies ran while one was open for 4% -> 3% of each run, Pallas kernels for 0% -> 0%
where the time goes in v5:
time: 91.5 us; the launch traced here: 90.8 us
  starting transfers between devices  52.3 us (57%)
  local copies, waits for them, and re-layouts  21.7 us (24%)
  waiting for transfers between devices  8.32 us (9%)
  other arithmetic  4.31 us (5%)
  Pallas kernels  2.8 us (3%)
  between operations  1.27 us (1%)
    ppermute x10, starting transfers between devices, axis_exchange(): lax.ppermute(jnp.where(odd, to_low, to_high), axis, swap_pairs(axis, 0))  31 us
    another operation x1, local copies, waits for them, and re-layouts, local(): jnp.stack([squares] + [entry for row in local_gram for entry in row])  16.5 us
    ppermute x5, starting transfers between devices, all_sum(): x = x + lax.ppermute(x, axis, [(i, i ^ step) for i in range(n)])  14.6 us
    ppermute x5, waiting for transfers between devices, all_sum(): x = x + lax.ppermute(x, axis, [(i, i ^ step) for i in range(n)])  7.62 us
    ppermute x10, starting transfers between devices, axis_exchange(): lax.ppermute(jnp.where(odd, to_high, to_low), axis, swap_pairs(axis, 1))  6.65 us
    pallas_call x1, Pallas kernels, finish(): pl.pallas_call(lambda *refs: finish_kernel(float(cells), size, *refs), ou...  2.8 us
  transfers between devices with their start and end apart: 25, of which 9 were waited for; matrix products, arithmetic and copies ran while one was open for 3% of the time, Pallas kernels for 0%

profile of v5, /device:TPU:0, one launch (start us, length us, event | category | flops | bytes accessed | tf_op | source)
XLA Modules:
  0.0 90.8 jit_solution(979624779040938953)
XLA Ops:
  0.6 0.0 copy-start
  0.7 0.8 fusion.55
  1.5 3.0 %collective-permute-start.1 = (f32[2,8,512]{2,1,0:T(8,128)S(1)}, f32[2,8,512]{2,1,0:T(8,128)S(1)}, u32[]{:S(2)}, u32[]{:S(2)}) collective-permute-start(f32[2,8,512]{2,1,0:T(8,128)S(1)} %get-tuple-element.100), channel_id=1, source_target_pairs={{0,8},{8,0},{16,24},{24,16},{1,9},{9,1},{17,25},{25,17},{2,10},{10... | collective-permute-start | bytes 98312 | tf_op jit(solution)/shard_map/ppermute | solution.py:29
  4.5 0.7 collective-permute-start
  5.2 1.3 %fusion.58 = (f32[16,1,512]{2,1,0:T(1,128)S(1)}, f32[16,1,512]{2,1,0:T(1,128)S(1)}, f32[16,1,512]{2,1,0:T(1,128)S(1)}, f32[16,1,512]{2,1,0:T(1,128)S(1)}) fusion(f32[16,8,512]{2,1,0:T(8,128)} %param.6, f32[16,8,512]{2,1,0:T(8,128)} %param.10), kind=kLoop, calls=%fused_computation.138 | loop fusion | bytes 262144 | tf_op jit(solution)/shard_map/slice | solution.py:153
  6.5 0.1 broadcast_select_fusion.18
  6.6 0.1 collective-permute-start.3
  6.7 0.0 copy-start.2
  6.7 0.8 collective-permute-start.2
  7.5 1.1 %fusion.57 = (f32[16,7,512]{2,1,0:T(8,128)S(1)}, f32[16,7,512]{2,1,0:T(8,128)S(1)}) fusion(f32[16,8,512]{2,1,0:T(8,128)} %param.6), kind=kLoop, calls=%fused_computation.137 | loop fusion | bytes 917504 | tf_op jit(solution)/shard_map/slice | solution.py:48
  8.6 0.1 fusion.60
  8.7 0.1 fusion.54
  8.8 0.0 copy-start.6
  8.9 0.7 copy-done.1
  9.6 0.1 copy-done.3
  9.6 0.1 slice.201
  9.8 0.1 fusion.61
  10.0 0.5 bitcast_dynamic-update-slice_fusion.4
  10.5 0.1 fusion.53
  10.7 0.1 fusion.52
  10.8 4.3 %collective-permute-start.4 = (f32[1,8,512]{2,1,0:T(8,128)S(1)}, f32[1,8,512]{2,1,0:T(8,128)S(1)}, u32[]{:S(2)}, u32[]{:S(2)}) collective-permute-start(f32[1,8,512]{2,1,0:T(8,128)S(1)} %get-tuple-element.66), channel_id=1, source_target_pairs={{0,8},{8,0},{16,24},{24,16},{1,9},{9,1},{17,25},{25,17},{2,10},{10... | collective-permute-start | bytes 49160 | tf_op jit(solution)/shard_map/ppermute | solution.py:29
  15.0 0.7 collective-permute-start.5
  15.8 2.8 %collective-permute-start.6 = (f32[16,1,512]{2,1,0:T(1,128)S(1)}, f32[16,1,512]{2,1,0:T(1,128)S(1)}, u32[]{:S(2)}, u32[]{:S(2)}) collective-permute-start(f32[16,1,512]{2,1,0:T(1,128)S(1)} %get-tuple-element.70), channel_id=1, source_target_pairs={{0,1},{1,0},{2,3},{3,2},{4,5},{5,4},{6,7},{7,6},{8,9},{9,8},{10,11... | collective-permute-start | bytes 98312 | tf_op jit(solution)/shard_map/ppermute | solution.py:29
  18.6 0.7 collective-permute-start.7
  19.3 0.2 collective-permute-done.6
  19.5 0.4 bitcast_dynamic-update-slice_fusion.3
  20.0 0.1 fusion.50
  20.1 0.1 fusion.49
  20.2 2.2 %collective-permute-start.8 = (f32[1,8,512]{2,1,0:T(8,128)S(1)}, f32[1,8,512]{2,1,0:T(8,128)S(1)}, u32[]{:S(2)}, u32[]{:S(2)}) collective-permute-start(f32[1,8,512]{2,1,0:T(8,128)S(1)} %get-tuple-element.56), channel_id=1, source_target_pairs={{0,8},{8,0},{16,24},{24,16},{1,9},{9,1},{17,25},{25,17},{2,10},{10... | collective-permute-start | bytes 49160 | tf_op jit(solution)/shard_map/ppermute | solution.py:29
  22.4 0.7 collective-permute-start.9
  23.1 3.7 %collective-permute-start.10 = (f32[16,1,512]{2,1,0:T(1,128)S(1)}, f32[16,1,512]{2,1,0:T(1,128)S(1)}, u32[]{:S(2)}, u32[]{:S(2)}) collective-permute-start(f32[16,1,512]{2,1,0:T(1,128)S(1)} %get-tuple-element.60), channel_id=1, source_target_pairs={{0,1},{1,0},{2,3},{3,2},{4,5},{5,4},{6,7},{7,6},{8,9},{9,8},{10,11... | collective-permute-start | bytes 98312 | tf_op jit(solution)/shard_map/ppermute | solution.py:29
  26.8 0.7 collective-permute-start.11
  27.5 0.2 collective-permute-done.10
  27.7 0.4 bitcast_dynamic-update-slice_fusion.2
  28.2 0.1 fusion.47
  28.3 0.1 fusion.46
  28.4 4.1 %collective-permute-start.12 = (f32[1,8,512]{2,1,0:T(8,128)S(1)}, f32[1,8,512]{2,1,0:T(8,128)S(1)}, u32[]{:S(2)}, u32[]{:S(2)}) collective-permute-start(f32[1,8,512]{2,1,0:T(8,128)S(1)} %get-tuple-element.46), channel_id=1, source_target_pairs={{0,8},{8,0},{16,24},{24,16},{1,9},{9,1},{17,25},{25,17},{2,10},{10... | collective-permute-start | bytes 49160 | tf_op jit(solution)/shard_map/ppermute | solution.py:29
  32.5 0.7 collective-permute-start.13
  33.2 4.4 %collective-permute-start.14 = (f32[16,1,512]{2,1,0:T(1,128)S(1)}, f32[16,1,512]{2,1,0:T(1,128)S(1)}, u32[]{:S(2)}, u32[]{:S(2)}) collective-permute-start(f32[16,1,512]{2,1,0:T(1,128)S(1)} %get-tuple-element.50), channel_id=1, source_target_pairs={{0,1},{1,0},{2,3},{3,2},{4,5},{5,4},{6,7},{7,6},{8,9},{9,8},{10,11... | collective-permute-start | bytes 98312 | tf_op jit(solution)/shard_map/ppermute | solution.py:29
  37.7 0.7 collective-permute-start.15
  38.4 0.2 collective-permute-done.14
  38.5 0.4 bitcast_dynamic-update-slice_fusion.1
  39.0 0.1 fusion.44
  39.2 0.1 fusion.43
  39.2 1.8 %collective-permute-start.16 = (f32[1,8,512]{2,1,0:T(8,128)S(1)}, f32[1,8,512]{2,1,0:T(8,128)S(1)}, u32[]{:S(2)}, u32[]{:S(2)}) collective-permute-start(f32[1,8,512]{2,1,0:T(8,128)S(1)} %get-tuple-element.36), channel_id=1, source_target_pairs={{0,8},{8,0},{16,24},{24,16},{1,9},{9,1},{17,25},{25,17},{2,10},{10... | collective-permute-start | bytes 49160 | tf_op jit(solution)/shard_map/ppermute | solution.py:29
  41.1 0.7 collective-permute-start.17
  41.8 4.6 %collective-permute-start.18 = (f32[16,1,512]{2,1,0:T(1,128)S(1)}, f32[16,1,512]{2,1,0:T(1,128)S(1)}, u32[]{:S(2)}, u32[]{:S(2)}) collective-permute-start(f32[16,1,512]{2,1,0:T(1,128)S(1)} %get-tuple-element.40), channel_id=1, source_target_pairs={{0,1},{1,0},{2,3},{3,2},{4,5},{5,4},{6,7},{7,6},{8,9},{9,8},{10,11... | collective-permute-start | bytes 98312 | tf_op jit(solution)/shard_map/ppermute | solution.py:29
  46.3 0.7 collective-permute-start.19
  47.0 0.2 collective-permute-done.18
  47.2 0.4 bitcast_dynamic-update-slice_fusion
  47.7 1.1 %multiply_reduce_fusion = (f32[]{:T(128)}, f32[]{:T(128)}, f32[]{:T(128)}, f32[]{:T(128)}, f32[]{:T(128)}, /*index=5*/f32[]{:T(128)}, f32[]{:T(128)}, f32[]{:T(1...) fusion(f32[16,8,512]{2,1,0:T(8,128)S(1)} %get-tuple-element.25, ...), kind=kLoop, calls=%fused_computation.62 | loop fusion | flops 1966065 | bytes 1310780 | tf_op jit(solution)/shard_map/reduce_sum | solution.py:177
  48.7 16.5 %stack.92 = f32[26]{0:T(128)S(1)} concatenate(f32[1]{0:T(128)} %bitcast, f32[1]{0:T(128)} %bitcast, f32[1]{0:T(128)} %bitcast.1, f32[1]{0:T(128)} %bitcast.2, f32[1]{0:T(128)} %bitcast.3, f32[1]{0:T(128)} %bitcast.4, f32[1]{0:T(128)} %bitcast.1, f32[1]{0:T(128)} %bitcast.5, f32[1]{0:T(128)} %bitcast.6, f32[1]{0:T(128)} %bitcast.7, f32[1]{0:T(128)} %bitcast.8, f32[1]{0:T(128)} %bitcast.2, ...), dimensions={0} | concatenate | bytes 208 | tf_op jit(solution)/shard_map/stack | solution.py:183
  65.2 4.7 %collective-permute-start.20 = (f32[26]{0:T(128)S(1)}, f32[26]{0:T(128)S(1)}, u32[]{:S(2)}, u32[]{:S(2)}) collective-permute-start(f32[26]{0:T(128)S(1)} %stack.92), channel_id=1, source_target_pairs={{0,1},{1,0},{2,3},{3,2},{4,5},{5,4},{6,7},{7,6},{8,9},{9,8},{10,11... | collective-permute-start | bytes 320 | tf_op jit(solution)/shard_map/ppermute | solution.py:70
  69.9 0.8 collective-permute-done.20
  70.7 2.1 %collective-permute-start.21 = (f32[26]{0:T(128)S(1)}, f32[26]{0:T(128)S(1)}, u32[]{:S(2)}, u32[]{:S(2)}) collective-permute-start(f32[26]{0:T(128)S(1)} %add.178), channel_id=1, source_target_pairs={{0,2},{1,3},{2,0},{3,1},{4,6},{5,7},{6,4},{7,5},{8,10},{9,11},{10,... | collective-permute-start | bytes 320 | tf_op jit(solution)/shard_map/ppermute | solution.py:70
  72.8 1.5 %collective-permute-done.21 = f32[26]{0:T(128)S(1)} collective-permute-done((f32[26]{0:T(128)S(1)}, f32[26]{0:T(128)S(1)}, u32[]{:S(2)}, u32[]{:S(2)}) %collective-permute-start.21) | collective-permute-done | bytes 136 | tf_op jit(solution)/shard_map/ppermute | solution.py:70
  74.3 3.0 %collective-permute-start.22 = (f32[26]{0:T(128)S(1)}, f32[26]{0:T(128)S(1)}, u32[]{:S(2)}, u32[]{:S(2)}) collective-permute-start(f32[26]{0:T(128)S(1)} %add.179), channel_id=1, source_target_pairs={{0,4},{1,5},{2,6},{3,7},{4,0},{5,1},{6,2},{7,3},{8,12},{9,13},{10,... | collective-permute-start | bytes 320 | tf_op jit(solution)/shard_map/ppermute | solution.py:70
  77.4 1.5 %collective-permute-done.22 = f32[26]{0:T(128)S(1)} collective-permute-done((f32[26]{0:T(128)S(1)}, f32[26]{0:T(128)S(1)}, u32[]{:S(2)}, u32[]{:S(2)}) %collective-permute-start.22) | collective-permute-done | bytes 136 | tf_op jit(solution)/shard_map/ppermute | solution.py:70
  78.9 3.5 %collective-permute-start.23 = (f32[26]{0:T(128)S(1)}, f32[26]{0:T(128)S(1)}, u32[]{:S(2)}, u32[]{:S(2)}) collective-permute-start(f32[26]{0:T(128)S(1)} %add.180), channel_id=1, source_target_pairs={{0,8},{8,0},{16,24},{24,16},{1,9},{9,1},{17,25},{25,17},{2,10},{10... | collective-permute-start | bytes 320 | tf_op jit(solution)/shard_map/ppermute | solution.py:70
  82.4 1.5 %collective-permute-done.23 = f32[26]{0:T(128)S(1)} collective-permute-done((f32[26]{0:T(128)S(1)}, f32[26]{0:T(128)S(1)}, u32[]{:S(2)}, u32[]{:S(2)}) %collective-permute-start.23) | collective-permute-done | bytes 136 | tf_op jit(solution)/shard_map/ppermute | solution.py:70
  83.9 1.3 %collective-permute-start.24 = (f32[26]{0:T(128)S(1)}, f32[26]{0:T(128)S(1)}, u32[]{:S(2)}, u32[]{:S(2)}) collective-permute-start(f32[26]{0:T(128)S(1)} %add.181), channel_id=1, source_target_pairs={{0,16},{8,24},{16,0},{24,8},{1,17},{9,25},{17,1},{25,9},{2,18},{10... | collective-permute-start | bytes 320 | tf_op jit(solution)/shard_map/ppermute | solution.py:70
  85.2 2.3 %collective-permute-done.24 = f32[26]{0:T(128)S(1)} collective-permute-done((f32[26]{0:T(128)S(1)}, f32[26]{0:T(128)S(1)}, u32[]{:S(2)}, u32[]{:S(2)}) %collective-permute-start.24) | collective-permute-done | bytes 136 | tf_op jit(solution)/shard_map/ppermute | solution.py:70
  87.4 0.5 add.182.refs_0_
  88.0 2.8 %shard_map.85 = (f32[5,16,8,512]{3,2,1,0:T(8,128)}, f32[5,5]{1,0:T(8,128)}, f32[1,1]{1,0:T(1,128)}) custom-call(f32[26]{0:T(128)} %add.182.refs_0_, f32[5,16,8,512]{3,2,1,0:T(8,128)} %copy-done.5), custom_call_target="tpu_custom_call" | custom-call | tf_op jit(solution)/shard_map/pallas_call | solution.py:132
  (57 shorter events, 0.6 us)
Async XLA Ops:
  0.6 7.9 %copy-start = (f32[16,8,512]{2,1,0:T(8,128)S(1)}, f32[16,8,512]{2,1,0:T(8,128)}, u32[]{:S(2)}) copy-start(f32[16,8,512]{2,1,0:T(8,128)} %param.6) | copy-start | bytes 786436
  1.5 8.3 %collective-permute-start.1 = (f32[2,8,512]{2,1,0:T(8,128)S(1)}, f32[2,8,512]{2,1,0:T(8,128)S(1)}, u32[]{:S(2)}, u32[]{:S(2)}) collective-permute-start(f32[2,8,512]{2,1,0:T(8,128)S(1)} %get-tuple-element.100), channel_id=1, source_target_pairs={{0,8},{8,0},{16,24},{24,16},{1,9},{9,1},{17,25},{25,17},{2,10},{10... | collective-permute-start | bytes 98312 | tf_op jit(solution)/shard_map/ppermute | solution.py:29
  4.5 5.3 %collective-permute-start = (f32[2,8,512]{2,1,0:T(8,128)S(1)}, f32[2,8,512]{2,1,0:T(8,128)S(1)}, u32[]{:S(2)}, u32[]{:S(2)}) collective-permute-start(f32[2,8,512]{2,1,0:T(8,128)S(1)} %get-tuple-element.101), channel_id=1, source_target_pairs={{8,16},{16,8},{9,17},{17,9},{10,18},{18,10},{11,19},{19,11},{12,20... | collective-permute-start | bytes 98312 | tf_op jit(solution)/shard_map/ppermute | solution.py:30
  6.6 3.2 %collective-permute-start.3 = (f32[16,2,512]{2,1,0:T(2,128)S(1)}, f32[16,2,512]{2,1,0:T(2,128)S(1)}, u32[]{:S(2)}, u32[]{:S(2)}) collective-permute-start(f32[16,2,512]{2,1,0:T(2,128)S(1)} %get-tuple-element.88), channel_id=1, source_target_pairs={{0,1},{1,0},{2,3},{3,2},{4,5},{5,4},{6,7},{7,6},{8,9},{9,8},{10,11... | collective-permute-start | bytes 196616 | tf_op jit(solution)/shard_map/ppermute | solution.py:29
  6.7 2.1 %copy-start.2 = (f32[16,8,512]{2,1,0:T(8,128)S(1)}, f32[16,8,512]{2,1,0:T(8,128)}, u32[]{:S(2)}) copy-start(f32[16,8,512]{2,1,0:T(8,128)} %param.9) | copy-start | bytes 786436
  6.7 3.1 %collective-permute-start.2 = (f32[16,2,512]{2,1,0:T(2,128)S(1)}, f32[16,2,512]{2,1,0:T(2,128)S(1)}, u32[]{:S(2)}, u32[]{:S(2)}) collective-permute-start(f32[16,2,512]{2,1,0:T(2,128)S(1)} %get-tuple-element.89), channel_id=1, source_target_pairs={{1,2},{2,1},{3,4},{4,3},{5,6},{6,5},{9,10},{10,9},{11,12},{12,11},... | collective-permute-start | bytes 196616 | tf_op jit(solution)/shard_map/ppermute | solution.py:30
  8.6 1.0 %copy-start.1 = (f32[16,8,512]{2,1,0:T(8,128)S(1)}, f32[16,8,512]{2,1,0:T(8,128)}, u32[]{:S(2)}) copy-start(f32[16,8,512]{2,1,0:T(8,128)} %param.10) | copy-start | bytes 786436
  8.6 1.0 %copy-start.3 = (f32[16,8,512]{2,1,0:T(8,128)S(1)}, f32[16,8,512]{2,1,0:T(8,128)}, u32[]{:S(2)}) copy-start(f32[16,8,512]{2,1,0:T(8,128)} %param.11) | copy-start | bytes 786436
  8.8 1.1 %copy-start.4 = (f32[16,8,512]{2,1,0:T(8,128)S(1)}, f32[16,8,512]{2,1,0:T(8,128)}, u32[]{:S(2)}) copy-start(f32[16,8,512]{2,1,0:T(8,128)} %param.8) | copy-start | bytes 786436
  8.8 1.1 %copy-start.6 = (f32[16,8,512]{2,1,0:T(8,128)S(1)}, f32[16,8,512]{2,1,0:T(8,128)}, u32[]{:S(2)}) copy-start(f32[16,8,512]{2,1,0:T(8,128)} %param.7) | copy-start | bytes 786436
  10.8 8.5 %collective-permute-start.4 = (f32[1,8,512]{2,1,0:T(8,128)S(1)}, f32[1,8,512]{2,1,0:T(8,128)S(1)}, u32[]{:S(2)}, u32[]{:S(2)}) collective-permute-start(f32[1,8,512]{2,1,0:T(8,128)S(1)} %get-tuple-element.66), channel_id=1, source_target_pairs={{0,8},{8,0},{16,24},{24,16},{1,9},{9,1},{17,25},{25,17},{2,10},{10... | collective-permute-start | bytes 49160 | tf_op jit(solution)/shard_map/ppermute | solution.py:29
  15.0 4.2 %collective-permute-start.5 = (f32[1,8,512]{2,1,0:T(8,128)S(1)}, f32[1,8,512]{2,1,0:T(8,128)S(1)}, u32[]{:S(2)}, u32[]{:S(2)}) collective-permute-start(f32[1,8,512]{2,1,0:T(8,128)S(1)} %get-tuple-element.67), channel_id=1, source_target_pairs={{8,16},{16,8},{9,17},{17,9},{10,18},{18,10},{11,19},{19,11},{12,20... | collective-permute-start | bytes 49160 | tf_op jit(solution)/shard_map/ppermute | solution.py:30
  15.8 3.7 %collective-permute-start.6 = (f32[16,1,512]{2,1,0:T(1,128)S(1)}, f32[16,1,512]{2,1,0:T(1,128)S(1)}, u32[]{:S(2)}, u32[]{:S(2)}) collective-permute-start(f32[16,1,512]{2,1,0:T(1,128)S(1)} %get-tuple-element.70), channel_id=1, source_target_pairs={{0,1},{1,0},{2,3},{3,2},{4,5},{5,4},{6,7},{7,6},{8,9},{9,8},{10,11... | collective-permute-start | bytes 98312 | tf_op jit(solution)/shard_map/ppermute | solution.py:29
  18.6 0.9 collective-permute-start.7
  20.2 7.3 %collective-permute-start.8 = (f32[1,8,512]{2,1,0:T(8,128)S(1)}, f32[1,8,512]{2,1,0:T(8,128)S(1)}, u32[]{:S(2)}, u32[]{:S(2)}) collective-permute-start(f32[1,8,512]{2,1,0:T(8,128)S(1)} %get-tuple-element.56), channel_id=1, source_target_pairs={{0,8},{8,0},{16,24},{24,16},{1,9},{9,1},{17,25},{25,17},{2,10},{10... | collective-permute-start | bytes 49160 | tf_op jit(solution)/shard_map/ppermute | solution.py:29
  22.4 5.1 %collective-permute-start.9 = (f32[1,8,512]{2,1,0:T(8,128)S(1)}, f32[1,8,512]{2,1,0:T(8,128)S(1)}, u32[]{:S(2)}, u32[]{:S(2)}) collective-permute-start(f32[1,8,512]{2,1,0:T(8,128)S(1)} %get-tuple-element.57), channel_id=1, source_target_pairs={{8,16},{16,8},{9,17},{17,9},{10,18},{18,10},{11,19},{19,11},{12,20... | collective-permute-start | bytes 49160 | tf_op jit(solution)/shard_map/ppermute | solution.py:30
  23.1 4.5 %collective-permute-start.10 = (f32[16,1,512]{2,1,0:T(1,128)S(1)}, f32[16,1,512]{2,1,0:T(1,128)S(1)}, u32[]{:S(2)}, u32[]{:S(2)}) collective-permute-start(f32[16,1,512]{2,1,0:T(1,128)S(1)} %get-tuple-element.60), channel_id=1, source_target_pairs={{0,1},{1,0},{2,3},{3,2},{4,5},{5,4},{6,7},{7,6},{8,9},{9,8},{10,11... | collective-permute-start | bytes 98312 | tf_op jit(solution)/shard_map/ppermute | solution.py:29
  26.8 0.9 collective-permute-start.11
  28.4 9.9 %collective-permute-start.12 = (f32[1,8,512]{2,1,0:T(8,128)S(1)}, f32[1,8,512]{2,1,0:T(8,128)S(1)}, u32[]{:S(2)}, u32[]{:S(2)}) collective-permute-start(f32[1,8,512]{2,1,0:T(8,128)S(1)} %get-tuple-element.46), channel_id=1, source_target_pairs={{0,8},{8,0},{16,24},{24,16},{1,9},{9,1},{17,25},{25,17},{2,10},{10... | collective-permute-start | bytes 49160 | tf_op jit(solution)/shard_map/ppermute | solution.py:29
  32.5 5.8 %collective-permute-start.13 = (f32[1,8,512]{2,1,0:T(8,128)S(1)}, f32[1,8,512]{2,1,0:T(8,128)S(1)}, u32[]{:S(2)}, u32[]{:S(2)}) collective-permute-start(f32[1,8,512]{2,1,0:T(8,128)S(1)} %get-tuple-element.47), channel_id=1, source_target_pairs={{8,16},{16,8},{9,17},{17,9},{10,18},{18,10},{11,19},{19,11},{12,20... | collective-permute-start | bytes 49160 | tf_op jit(solution)/shard_map/ppermute | solution.py:30
  33.2 5.3 %collective-permute-start.14 = (f32[16,1,512]{2,1,0:T(1,128)S(1)}, f32[16,1,512]{2,1,0:T(1,128)S(1)}, u32[]{:S(2)}, u32[]{:S(2)}) collective-permute-start(f32[16,1,512]{2,1,0:T(1,128)S(1)} %get-tuple-element.50), channel_id=1, source_target_pairs={{0,1},{1,0},{2,3},{3,2},{4,5},{5,4},{6,7},{7,6},{8,9},{9,8},{10,11... | collective-permute-start | bytes 98312 | tf_op jit(solution)/shard_map/ppermute | solution.py:29
  37.7 0.9 collective-permute-start.15
  39.2 7.7 %collective-permute-start.16 = (f32[1,8,512]{2,1,0:T(8,128)S(1)}, f32[1,8,512]{2,1,0:T(8,128)S(1)}, u32[]{:S(2)}, u32[]{:S(2)}) collective-permute-start(f32[1,8,512]{2,1,0:T(8,128)S(1)} %get-tuple-element.36), channel_id=1, source_target_pairs={{0,8},{8,0},{16,24},{24,16},{1,9},{9,1},{17,25},{25,17},{2,10},{10... | collective-permute-start | bytes 49160 | tf_op jit(solution)/shard_map/ppermute | solution.py:29
  41.1 5.9 %collective-permute-start.17 = (f32[1,8,512]{2,1,0:T(8,128)S(1)}, f32[1,8,512]{2,1,0:T(8,128)S(1)}, u32[]{:S(2)}, u32[]{:S(2)}) collective-permute-start(f32[1,8,512]{2,1,0:T(8,128)S(1)} %get-tuple-element.37), channel_id=1, source_target_pairs={{8,16},{16,8},{9,17},{17,9},{10,18},{18,10},{11,19},{19,11},{12,20... | collective-permute-start | bytes 49160 | tf_op jit(solution)/shard_map/ppermute | solution.py:30
  41.8 5.4 %collective-permute-start.18 = (f32[16,1,512]{2,1,0:T(1,128)S(1)}, f32[16,1,512]{2,1,0:T(1,128)S(1)}, u32[]{:S(2)}, u32[]{:S(2)}) collective-permute-start(f32[16,1,512]{2,1,0:T(1,128)S(1)} %get-tuple-element.40), channel_id=1, source_target_pairs={{0,1},{1,0},{2,3},{3,2},{4,5},{5,4},{6,7},{7,6},{8,9},{9,8},{10,11... | collective-permute-start | bytes 98312 | tf_op jit(solution)/shard_map/ppermute | solution.py:29
  46.3 0.9 collective-permute-start.19
  47.7 40.3 %copy-start.5 = (f32[5,16,8,512]{3,2,1,0:T(8,128)}, f32[5,16,8,512]{3,2,1,0:T(8,128)S(1)}, u32[]{:S(2)}) copy-start(f32[5,16,8,512]{3,2,1,0:T(8,128)S(1)} %get-tuple-element.24.refs_1_) | copy-start | bytes 3932164
  65.2 5.6 %collective-permute-start.20 = (f32[26]{0:T(128)S(1)}, f32[26]{0:T(128)S(1)}, u32[]{:S(2)}, u32[]{:S(2)}) collective-permute-start(f32[26]{0:T(128)S(1)} %stack.92), channel_id=1, source_target_pairs={{0,1},{1,0},{2,3},{3,2},{4,5},{5,4},{6,7},{7,6},{8,9},{9,8},{10,11... | collective-permute-start | bytes 320 | tf_op jit(solution)/shard_map/ppermute | solution.py:70
  70.7 3.6 %collective-permute-start.21 = (f32[26]{0:T(128)S(1)}, f32[26]{0:T(128)S(1)}, u32[]{:S(2)}, u32[]{:S(2)}) collective-permute-start(f32[26]{0:T(128)S(1)} %add.178), channel_id=1, source_target_pairs={{0,2},{1,3},{2,0},{3,1},{4,6},{5,7},{6,4},{7,5},{8,10},{9,11},{10,... | collective-permute-start | bytes 320 | tf_op jit(solution)/shard_map/ppermute | solution.py:70
  74.3 4.6 %collective-permute-start.22 = (f32[26]{0:T(128)S(1)}, f32[26]{0:T(128)S(1)}, u32[]{:S(2)}, u32[]{:S(2)}) collective-permute-start(f32[26]{0:T(128)S(1)} %add.179), channel_id=1, source_target_pairs={{0,4},{1,5},{2,6},{3,7},{4,0},{5,1},{6,2},{7,3},{8,12},{9,13},{10,... | collective-permute-start | bytes 320 | tf_op jit(solution)/shard_map/ppermute | solution.py:70
  78.9 5.0 %collective-permute-start.23 = (f32[26]{0:T(128)S(1)}, f32[26]{0:T(128)S(1)}, u32[]{:S(2)}, u32[]{:S(2)}) collective-permute-start(f32[26]{0:T(128)S(1)} %add.180), channel_id=1, source_target_pairs={{0,8},{8,0},{16,24},{24,16},{1,9},{9,1},{17,25},{25,17},{2,10},{10... | collective-permute-start | bytes 320 | tf_op jit(solution)/shard_map/ppermute | solution.py:70
  83.9 3.5 %collective-permute-start.24 = (f32[26]{0:T(128)S(1)}, f32[26]{0:T(128)S(1)}, u32[]{:S(2)}, u32[]{:S(2)}) collective-permute-start(f32[26]{0:T(128)S(1)} %add.181), channel_id=1, source_target_pairs={{0,16},{8,24},{16,0},{24,8},{1,17},{9,25},{17,1},{25,9},{2,18},{10... | collective-permute-start | bytes 320 | tf_op jit(solution)/shard_map/ppermute | solution.py:70

commit v6 on v5

--- a/solution.py
+++ b/solution.py
@@ -72,11 +72,52 @@
     return x
 
 
-def finish_kernel(cells, size, stats_ref, basis_ref, ortho_ref, upper_ref, scale_ref):
+def gram_kernel(size, *refs):
+    basis_refs, out_ref = refs[:size], refs[size]
+    tile = out_ref.shape
+    pairs = [(a, b) for a in range(size) for b in range(a, size)]
+    planes, rows, lanes = basis_refs[0].shape
+    chunks = lanes // tile[1]
+
+    def plane(i, accs):
+        accs = list(accs)
+        for c in range(chunks):
+            parts = [r[i, :, c * tile[1] : (c + 1) * tile[1]] for r in basis_refs]
+            for n, (a, b) in enumerate(pairs):
+                accs[n] = accs[n] + parts[a] * parts[b]
+        return tuple(accs)
+
+    zero = jnp.zeros((rows, tile[1]), jnp.float32)
+    accs = lax.fori_loop(0, planes, plane, tuple(zero for _ in pairs))
+    row_ids = lax.broadcasted_iota(jnp.int32, tile, 0)
+    lane_ids = lax.broadcasted_iota(jnp.int32, tile, 1)
+    packed = jnp.zeros(tile, jnp.float32)
+    for n, (a, b) in enumerate(pairs):
+        total = jnp.sum(accs[n])
+        hit = (lane_ids == 1 + a * size + b) | (lane_ids == 1 + b * size + a)
+        if a == 0 and b == 0:
+            hit = hit | (lane_ids == 0)
+        packed = jnp.where((row_ids == 0) & hit, total, packed)
+    out_ref[...] = packed
+
+
+def gram(basis):
+    size = len(basis)
+    vmem = pl.BlockSpec(memory_space=pltpu.VMEM)
+    return pl.pallas_call(
+        lambda *refs: gram_kernel(size, *refs),
+        out_shape=jax.ShapeDtypeStruct((8, 128), jnp.float32),
+        in_specs=[vmem] * size,
+        out_specs=vmem,
+    )(*basis)
+
+
+def finish_kernel(cells, size, stats_ref, *refs):
+    basis_refs, (ortho_ref, upper_ref, scale_ref) = refs[:size], refs[size:]
     tile = (8, 128)
 
     def held(i):
-        return jnp.full(tile, stats_ref[i], jnp.float32)
+        return jnp.full(tile, stats_ref[0, i], jnp.float32)
 
     scale = jnp.sqrt(held(0) / cells + EPS)
     square = scale * scale
@@ -108,14 +149,14 @@
             packed = jnp.where((rows == row) & (cols == col), upper[row][col], packed)
     upper_ref[...] = packed[: upper_ref.shape[0], : upper_ref.shape[1]]
     scale_ref[...] = scale[:1, :1]
-    lanes = basis_ref.shape[-1] // tile[1]
+    lanes = basis_refs[0].shape[-1] // tile[1]
     weight = [
         [jnp.tile(inverse[j][k] / scale, (1, lanes)) if j <= k else None for k in range(size)]
         for j in range(size)
     ]
 
     def plane(i, carry):
-        parts = [basis_ref[j, i] for j in range(size)]
+        parts = [basis_refs[j][i] for j in range(size)]
         for k in range(size):
             acc = parts[0] * weight[0][k]
             for j in range(1, k + 1):
@@ -123,22 +164,22 @@
             ortho_ref[k, i] = acc
         return carry
 
-    lax.fori_loop(0, basis_ref.shape[1], plane, 0)
-
-
-def finish(stats, block, cells):
-    size = block.shape[0]
+    lax.fori_loop(0, basis_refs[0].shape[0], plane, 0)
+
+
+def finish(stats, basis, cells):
+    size = len(basis)
     vmem = pl.BlockSpec(memory_space=pltpu.VMEM)
     ortho, upper, scale = pl.pallas_call(
         lambda *refs: finish_kernel(float(cells), size, *refs),
         out_shape=(
-            jax.ShapeDtypeStruct(block.shape, jnp.float32),
+            jax.ShapeDtypeStruct((size,) + basis[0].shape, jnp.float32),
             jax.ShapeDtypeStruct((size, size), jnp.float32),
             jax.ShapeDtypeStruct((1, 1), jnp.float32),
         ),
-        in_specs=[pl.BlockSpec(memory_space=pltpu.SMEM), vmem],
+        in_specs=[pl.BlockSpec(memory_space=pltpu.SMEM)] + [vmem] * size,
         out_specs=(vmem, vmem, vmem),
-    )(stats, block)
+    )(stats, *basis)
     return ortho, upper, scale.reshape(())
 
 
@@ -170,19 +211,13 @@
 
     vector = residual0
     basis = [vector]
-    gram_rows = [[jnp.sum(vector * vector)]]
     for step in range(STEPS):
         total = neighbour_sum(vector, field_halo(vector), coef)
         vector = 2.0 * total / diagonal
-        gram_rows.append([jnp.sum(vector * earlier) for earlier in basis] + [jnp.sum(vector * vector)])
         basis.append(vector)
-    block = jnp.stack(basis)
-    size = len(basis)
-    local_gram = [[gram_rows[max(a, b)][min(a, b)] for b in range(size)] for a in range(size)]
-    squares = gram_rows[0][0]
-    stats = jnp.stack([squares] + [entry for row in local_gram for entry in row])
+    stats = gram(basis)
     stats = all_sum(stats)
-    ortho, upper, scale = finish(stats, block, cells)
+    ortho, upper, scale = finish(stats, basis, cells)
     return (ortho, upper, scale)
 
 

time: 91.5 us -> 79.3 us (0.87)
  local copies, waits for them, and re-layouts: 21.7 us -> 5.32 us
  waiting for transfers between devices: 8.32 us -> 14.8 us
  starting transfers between devices: 52.3 us -> 47.6 us
  Pallas kernels: 2.8 us -> 5.06 us
    another operation x1 -> x0, local copies, waits for them, and re-layouts: 16.5 us -> none  [local(): jnp.stack([squares] + [entry for row in local_gram for entry in row])]
    ppermute x5, starting transfers between devices: 14.6 us -> 5.63 us  [all_sum(): x = x + lax.ppermute(x, axis, [(i, i ^ step) for i in range(n)])]
    ppermute x10, starting transfers between devices: 31 us -> 35.2 us  [axis_exchange(): lax.ppermute(jnp.where(odd, to_low, to_high), axis, swap_pairs(axis, 0))]
    ppermute x5, waiting for transfers between devices: 7.62 us -> 11.4 us  [all_sum(): x = x + lax.ppermute(x, axis, [(i, i ^ step) for i in range(n)])]
    ppermute x10, waiting for transfers between devices: 0.67 us -> 3.35 us  [axis_exchange(): lax.ppermute(jnp.where(odd, to_low, to_high), axis, swap_pairs(axis, 0))]
    div x0 -> x4, other arithmetic: none -> 2.52 us  [local(): vector = 2.0 * total / diagonal]
    pallas_call x0 -> x1, Pallas kernels: none -> 2.31 us  [gram(): pl.pallas_call(lambda *refs: gram_kernel(size, *refs), out_shape=jax.Shap...]
    unnamed x4 -> x0, other arithmetic: 1.83 us -> none
  transfers between devices with their start and end apart: 25 -> 25, of which waited for: 9 -> 9; matrix products, arithmetic and copies ran while one was open for 3% -> 4% of each run, Pallas kernels for 0% -> 0%
where the time goes in v6:
time: 79.3 us; the launch traced here: 78.7 us
  starting transfers between devices  47.6 us (60%)
  waiting for transfers between devices  14.8 us (19%)
  local copies, waits for them, and re-layouts  5.32 us (7%)
  Pallas kernels  5.06 us (6%)
  other arithmetic  4.77 us (6%)
  between operations  1.2 us (2%)
    ppermute x10, starting transfers between devices, axis_exchange(): lax.ppermute(jnp.where(odd, to_low, to_high), axis, swap_pairs(axis, 0))  35.2 us
    ppermute x5, waiting for transfers between devices, all_sum(): x = x + lax.ppermute(x, axis, [(i, i ^ step) for i in range(n)])  11.4 us
    ppermute x10, starting transfers between devices, axis_exchange(): lax.ppermute(jnp.where(odd, to_high, to_low), axis, swap_pairs(axis, 1))  6.75 us
    ppermute x5, starting transfers between devices, all_sum(): x = x + lax.ppermute(x, axis, [(i, i ^ step) for i in range(n)])  5.63 us
    ppermute x10, waiting for transfers between devices, axis_exchange(): lax.ppermute(jnp.where(odd, to_low, to_high), axis, swap_pairs(axis, 0))  3.35 us
    pallas_call x1, Pallas kernels, finish(): pl.pallas_call(lambda *refs: finish_kernel(float(cells), size, *refs), ou...  2.75 us
    div x4, other arithmetic, local(): vector = 2.0 * total / diagonal  2.52 us
    pallas_call x1, Pallas kernels, gram(): pl.pallas_call(lambda *refs: gram_kernel(size, *refs), out_shape=jax.Shap...  2.31 us
  transfers between devices with their start and end apart: 25, of which 9 were waited for; matrix products, arithmetic and copies ran while one was open for 4% of the time, Pallas kernels for 0%

profile of v6, /device:TPU:0, one launch (start us, length us, event | category | flops | bytes accessed | tf_op | source)
XLA Modules:
  0.0 78.7 jit_solution(9731523813114877225)
XLA Ops:
  0.6 0.0 copy-start.4
  0.7 0.8 %fusion.54 = (f32[1,8,512]{2,1,0:T(8,128)S(1)}, f32[1,8,512]{2,1,0:T(8,128)S(1)}, f32[1,8,512]{2,1,0:T(8,128)S(1)}, f32[1,8,512]{2,1,0:T(8,128)S(1)}) fusion(f32[16,8,512]{2,1,0:T(8,128)} %param.6, f32[16,8,512]{2,1,0:T(8,128)} %param.9), kind=kLoop, calls=%fused_computation.119 | loop fusion | bytes 131072 | tf_op jit(solution)/shard_map/slice | solution.py:192
  1.5 3.0 %collective-permute-start.1 = (f32[2,8,512]{2,1,0:T(8,128)S(1)}, f32[2,8,512]{2,1,0:T(8,128)S(1)}, u32[]{:S(2)}, u32[]{:S(2)}) collective-permute-start(f32[2,8,512]{2,1,0:T(8,128)S(1)} %get-tuple-element.75), channel_id=1, source_target_pairs={{0,8},{8,0},{16,24},{24,16},{1,9},{9,1},{17,25},{25,17},{2,10},{10... | collective-permute-start | bytes 98312 | tf_op jit(solution)/shard_map/ppermute | solution.py:29
  4.5 0.7 collective-permute-start
  5.2 1.3 %fusion.51 = (f32[16,1,512]{2,1,0:T(1,128)S(1)}, f32[16,1,512]{2,1,0:T(1,128)S(1)}, f32[16,1,512]{2,1,0:T(1,128)S(1)}, f32[16,1,512]{2,1,0:T(1,128)S(1)}) fusion(f32[16,8,512]{2,1,0:T(8,128)} %param.6, f32[16,8,512]{2,1,0:T(8,128)} %param.10), kind=kLoop, calls=%fused_computation.116 | loop fusion | bytes 262144 | tf_op jit(solution)/shard_map/slice | solution.py:194
  6.5 0.1 broadcast_select_fusion.18
  6.6 0.1 collective-permute-start.3
  6.7 0.8 %collective-permute-start.2 = (f32[16,2,512]{2,1,0:T(2,128)S(1)}, f32[16,2,512]{2,1,0:T(2,128)S(1)}, u32[]{:S(2)}, u32[]{:S(2)}) collective-permute-start(f32[16,2,512]{2,1,0:T(2,128)S(1)} %get-tuple-element.64), channel_id=1, source_target_pairs={{1,2},{2,1},{3,4},{4,3},{5,6},{6,5},{9,10},{10,9},{11,12},{12,11},... | collective-permute-start | bytes 196616 | tf_op jit(solution)/shard_map/ppermute | solution.py:30
  7.5 1.1 %fusion.50 = (f32[16,7,512]{2,1,0:T(8,128)S(1)}, f32[16,7,512]{2,1,0:T(8,128)S(1)}) fusion(f32[16,8,512]{2,1,0:T(8,128)} %param.6), kind=kLoop, calls=%fused_computation.115 | loop fusion | bytes 917504 | tf_op jit(solution)/shard_map/slice | solution.py:49
  8.6 0.0 copy-start.5
  8.6 0.0 copy-start.7
  8.6 0.1 fusion.49
  8.7 0.1 fusion.53
  8.9 0.7 copy-done.5
  9.6 0.1 copy-done.7
  9.6 0.1 slice.201
  9.8 0.1 fusion.56
  10.0 0.5 fusion.6.refs_0_.refs_1_
  10.5 0.1 fusion.48
  10.6 0.1 fusion.46
  10.7 0.1 fusion.47
  10.8 0.7 collective-permute-start.5
  11.4 5.7 %collective-permute-start.4 = (f32[1,8,512]{2,1,0:T(8,128)S(1)}, f32[1,8,512]{2,1,0:T(8,128)S(1)}, u32[]{:S(2)}, u32[]{:S(2)}) collective-permute-start(f32[1,8,512]{2,1,0:T(8,128)S(1)} %get-tuple-element.48), channel_id=1, source_target_pairs={{0,8},{8,0},{16,24},{24,16},{1,9},{9,1},{17,25},{25,17},{2,10},{10... | collective-permute-start | bytes 49160 | tf_op jit(solution)/shard_map/ppermute | solution.py:29
  17.2 0.7 collective-permute-start.7
  17.9 5.9 %collective-permute-start.6 = (f32[16,1,512]{2,1,0:T(1,128)S(1)}, f32[16,1,512]{2,1,0:T(1,128)S(1)}, u32[]{:S(2)}, u32[]{:S(2)}) collective-permute-start(f32[16,1,512]{2,1,0:T(1,128)S(1)} %get-tuple-element.44), channel_id=1, source_target_pairs={{0,1},{1,0},{2,3},{3,2},{4,5},{5,4},{6,7},{7,6},{8,9},{9,8},{10,11... | collective-permute-start | bytes 98312 | tf_op jit(solution)/shard_map/ppermute | solution.py:29
  23.8 0.8 %collective-permute-done.6 = f32[16,1,512]{2,1,0:T(1,128)S(1)} collective-permute-done((f32[16,1,512]{2,1,0:T(1,128)S(1)}, f32[16,1,512]{2,1,0:T(1,128)S(1)}, u32[]{:S(2)}, u32[]{:S(2)}) %collective-permute-start.6) | collective-permute-done | bytes 32800 | tf_op jit(solution)/shard_map/ppermute | solution.py:29
  24.6 0.5 fusion.13.refs_1_.refs_2_
  25.1 0.1 fusion.43
  25.3 0.1 fusion.44
  25.4 0.7 collective-permute-start.9
  26.0 3.8 %collective-permute-start.8 = (f32[1,8,512]{2,1,0:T(8,128)S(1)}, f32[1,8,512]{2,1,0:T(8,128)S(1)}, u32[]{:S(2)}, u32[]{:S(2)}) collective-permute-start(f32[1,8,512]{2,1,0:T(8,128)S(1)} %get-tuple-element.38), channel_id=1, source_target_pairs={{0,8},{8,0},{16,24},{24,16},{1,9},{9,1},{17,25},{25,17},{2,10},{10... | collective-permute-start | bytes 49160 | tf_op jit(solution)/shard_map/ppermute | solution.py:29
  29.9 0.7 collective-permute-start.11
  30.5 3.7 %collective-permute-start.10 = (f32[16,1,512]{2,1,0:T(1,128)S(1)}, f32[16,1,512]{2,1,0:T(1,128)S(1)}, u32[]{:S(2)}, u32[]{:S(2)}) collective-permute-start(f32[16,1,512]{2,1,0:T(1,128)S(1)} %get-tuple-element.34), channel_id=1, source_target_pairs={{0,1},{1,0},{2,3},{3,2},{4,5},{5,4},{6,7},{7,6},{8,9},{9,8},{10,11... | collective-permute-start | bytes 98312 | tf_op jit(solution)/shard_map/ppermute | solution.py:29
  34.3 0.8 %collective-permute-done.10 = f32[16,1,512]{2,1,0:T(1,128)S(1)} collective-permute-done((f32[16,1,512]{2,1,0:T(1,128)S(1)}, f32[16,1,512]{2,1,0:T(1,128)S(1)}, u32[]{:S(2)}, u32[]{:S(2)}) %collective-permute-start.10) | collective-permute-done | bytes 32800 | tf_op jit(solution)/shard_map/ppermute | solution.py:29
  35.1 0.5 fusion.20.refs_2_.refs_3_
  35.6 0.1 fusion.40
  35.8 0.1 fusion.41
  35.9 0.7 collective-permute-start.13
  36.5 2.1 %collective-permute-start.12 = (f32[1,8,512]{2,1,0:T(8,128)S(1)}, f32[1,8,512]{2,1,0:T(8,128)S(1)}, u32[]{:S(2)}, u32[]{:S(2)}) collective-permute-start(f32[1,8,512]{2,1,0:T(8,128)S(1)} %get-tuple-element.28), channel_id=1, source_target_pairs={{0,8},{8,0},{16,24},{24,16},{1,9},{9,1},{17,25},{25,17},{2,10},{10... | collective-permute-start | bytes 49160 | tf_op jit(solution)/shard_map/ppermute | solution.py:29
  38.7 0.7 collective-permute-start.15
  39.3 3.7 %collective-permute-start.14 = (f32[16,1,512]{2,1,0:T(1,128)S(1)}, f32[16,1,512]{2,1,0:T(1,128)S(1)}, u32[]{:S(2)}, u32[]{:S(2)}) collective-permute-start(f32[16,1,512]{2,1,0:T(1,128)S(1)} %get-tuple-element.24), channel_id=1, source_target_pairs={{0,1},{1,0},{2,3},{3,2},{4,5},{5,4},{6,7},{7,6},{8,9},{9,8},{10,11... | collective-permute-start | bytes 98312 | tf_op jit(solution)/shard_map/ppermute | solution.py:29
  43.1 0.8 %collective-permute-done.14 = f32[16,1,512]{2,1,0:T(1,128)S(1)} collective-permute-done((f32[16,1,512]{2,1,0:T(1,128)S(1)}, f32[16,1,512]{2,1,0:T(1,128)S(1)}, u32[]{:S(2)}, u32[]{:S(2)}) %collective-permute-start.14) | collective-permute-done | bytes 32800 | tf_op jit(solution)/shard_map/ppermute | solution.py:29
  43.9 0.5 fusion.27.refs_3_.refs_4_
  44.4 0.1 fusion.37
  44.6 0.1 fusion.38
  44.6 0.7 collective-permute-start.17
  45.3 3.6 %collective-permute-start.16 = (f32[1,8,512]{2,1,0:T(8,128)S(1)}, f32[1,8,512]{2,1,0:T(8,128)S(1)}, u32[]{:S(2)}, u32[]{:S(2)}) collective-permute-start(f32[1,8,512]{2,1,0:T(8,128)S(1)} %get-tuple-element.18), channel_id=1, source_target_pairs={{0,8},{8,0},{16,24},{24,16},{1,9},{9,1},{17,25},{25,17},{2,10},{10... | collective-permute-start | bytes 49160 | tf_op jit(solution)/shard_map/ppermute | solution.py:29
  48.9 0.7 collective-permute-start.19
  49.6 3.7 %collective-permute-start.18 = (f32[16,1,512]{2,1,0:T(1,128)S(1)}, f32[16,1,512]{2,1,0:T(1,128)S(1)}, u32[]{:S(2)}, u32[]{:S(2)}) collective-permute-start(f32[16,1,512]{2,1,0:T(1,128)S(1)} %get-tuple-element.14), channel_id=1, source_target_pairs={{0,1},{1,0},{2,3},{3,2},{4,5},{5,4},{6,7},{7,6},{8,9},{9,8},{10,11... | collective-permute-start | bytes 98312 | tf_op jit(solution)/shard_map/ppermute | solution.py:29
  53.3 0.8 %collective-permute-done.18 = f32[16,1,512]{2,1,0:T(1,128)S(1)} collective-permute-done((f32[16,1,512]{2,1,0:T(1,128)S(1)}, f32[16,1,512]{2,1,0:T(1,128)S(1)}, u32[]{:S(2)}, u32[]{:S(2)}) %collective-permute-start.18) | collective-permute-done | bytes 32800 | tf_op jit(solution)/shard_map/ppermute | solution.py:29
  54.1 1.2 %fusion.34.refs_4_.refs_5_ = f32[16,8,512]{2,1,0:T(8,128)} fusion(f32[16,8,512]{2,1,0:T(8,128)S(1)} %copy-done.6, f32[15,8,512]{2,1,0:T(8,128)S(1)} %get-tuple-element.16, f32[1,8,512]{2,1,0:T(8,128)S(1)} %get-tuple-element.78, f32[1,8,512]{2,1,0:T(8,128)S(1)} %get-tuple-element.77, f32[15,8,512]{2,1,0:T(8,128)S(1)} %get-tuple-element.15, ...), kind=kLoop, calls=%fused_computation.53 | loop fusion | flops 1638400 | bytes 3668480 | tf_op jit(solution)/shard_map/div | solution.py:216
  55.3 2.3 %shard_map.85 = f32[8,128]{1,0:T(8,128)} custom-call(f32[16,8,512]{2,1,0:T(8,128)} %copy-done.3, f32[16,8,512]{2,1,0:T(8,128)} %copy-done, f32[16,8,512]{2,1,0:T(8,128)} %copy-done.1, f32[16,8,512]{2,1,0:T(8,128)} %copy-done.2, f32[16,8,512]{2,1,0:T(8,128)} %fusion.34.refs_4_.refs_5_), custom_call_target="tpu_custom_call" | custom-call | tf_op jit(solution)/shard_map/pallas_call | solution.py:107
  57.6 0.7 collective-permute-start.20
  58.3 1.0 %collective-permute-done.20 = f32[8,128]{1,0:T(8,128)S(1)} collective-permute-done((f32[8,128]{1,0:T(8,128)}, f32[8,128]{1,0:T(8,128)S(1)}, u32[]{:S(2)}, u32[]{:S(2)}) %collective-permute-start.20) | collective-permute-done | bytes 4128 | tf_op jit(solution)/shard_map/ppermute | solution.py:70
  59.3 0.7 add.178
  60.0 2.0 %collective-permute-start.21 = (f32[8,128]{1,0:T(8,128)S(1)}, f32[8,128]{1,0:T(8,128)S(1)}, u32[]{:S(2)}, u32[]{:S(2)}) collective-permute-start(f32[8,128]{1,0:T(8,128)S(1)} %add.178), channel_id=1, source_target_pairs={{0,2},{1,3},{2,0},{3,1},{4,6},{5,7},{6,4},{7,5},{8,10},{9,11},{10,... | collective-permute-start | bytes 12296 | tf_op jit(solution)/shard_map/ppermute | solution.py:70
  62.0 1.6 %collective-permute-done.21 = f32[8,128]{1,0:T(8,128)S(1)} collective-permute-done((f32[8,128]{1,0:T(8,128)S(1)}, f32[8,128]{1,0:T(8,128)S(1)}, u32[]{:S(2)}, u32[]{:S(2)}) %collective-permute-start.21) | collective-permute-done | bytes 4128 | tf_op jit(solution)/shard_map/ppermute | solution.py:70
  63.6 3.0 %collective-permute-start.22 = (f32[8,128]{1,0:T(8,128)S(1)}, f32[8,128]{1,0:T(8,128)S(1)}, u32[]{:S(2)}, u32[]{:S(2)}) collective-permute-start(f32[8,128]{1,0:T(8,128)S(1)} %add.179), channel_id=1, source_target_pairs={{0,4},{1,5},{2,6},{3,7},{4,0},{5,1},{6,2},{7,3},{8,12},{9,13},{10,... | collective-permute-start | bytes 12296 | tf_op jit(solution)/shard_map/ppermute | solution.py:70
  66.6 1.6 %collective-permute-done.22 = f32[8,128]{1,0:T(8,128)S(1)} collective-permute-done((f32[8,128]{1,0:T(8,128)S(1)}, f32[8,128]{1,0:T(8,128)S(1)}, u32[]{:S(2)}, u32[]{:S(2)}) %collective-permute-start.22) | collective-permute-done | bytes 4128 | tf_op jit(solution)/shard_map/ppermute | solution.py:70
  68.2 0.0 collective-permute-start.23
  68.2 3.6 %collective-permute-done.23 = f32[8,128]{1,0:T(8,128)S(1)} collective-permute-done((f32[8,128]{1,0:T(8,128)S(1)}, f32[8,128]{1,0:T(8,128)S(1)}, u32[]{:S(2)}, u32[]{:S(2)}) %collective-permute-start.23) | collective-permute-done | bytes 4128 | tf_op jit(solution)/shard_map/ppermute | solution.py:70
  71.8 3.6 %collective-permute-done.24 = f32[8,128]{1,0:T(8,128)S(1)} collective-permute-done((f32[8,128]{1,0:T(8,128)S(1)}, f32[8,128]{1,0:T(8,128)S(1)}, u32[]{:S(2)}, u32[]{:S(2)}) %collective-permute-start.24) | collective-permute-done | bytes 4128 | tf_op jit(solution)/shard_map/ppermute | solution.py:70
  75.4 0.6 add.182.refs_0_
  76.0 2.8 %shard_map.86 = (f32[5,16,8,512]{3,2,1,0:T(8,128)}, f32[5,5]{1,0:T(8,128)}, f32[1,1]{1,0:T(1,128)}) custom-call(f32[8,128]{1,0:T(8,128)} %add.182.refs_0_, f32[16,8,512]{2,1,0:T(8,128)} %copy-done.3, f32[16,8,512]{2,1,0:T(8,128)} %copy-done, f32[16,8,512]{2,1,0:T(8,128)} %copy-done.1, f32[16,8,512]{2,1,0:T(8,128)} %copy-done.2, ...), custom_call_target="tpu_custom_call" | custom-call | tf_op jit(solution)/shard_map/pallas_call | solution.py:173
  (62 shorter events, 0.6 us)
Async XLA Ops:
  0.6 7.9 %copy-start.4 = (f32[16,8,512]{2,1,0:T(8,128)S(1)}, f32[16,8,512]{2,1,0:T(8,128)}, u32[]{:S(2)}) copy-start(f32[16,8,512]{2,1,0:T(8,128)} %param.6) | copy-start | bytes 786436
  1.5 8.3 %collective-permute-start.1 = (f32[2,8,512]{2,1,0:T(8,128)S(1)}, f32[2,8,512]{2,1,0:T(8,128)S(1)}, u32[]{:S(2)}, u32[]{:S(2)}) collective-permute-start(f32[2,8,512]{2,1,0:T(8,128)S(1)} %get-tuple-element.75), channel_id=1, source_target_pairs={{0,8},{8,0},{16,24},{24,16},{1,9},{9,1},{17,25},{25,17},{2,10},{10... | collective-permute-start | bytes 98312 | tf_op jit(solution)/shard_map/ppermute | solution.py:29
  4.5 5.3 %collective-permute-start = (f32[2,8,512]{2,1,0:T(8,128)S(1)}, f32[2,8,512]{2,1,0:T(8,128)S(1)}, u32[]{:S(2)}, u32[]{:S(2)}) collective-permute-start(f32[2,8,512]{2,1,0:T(8,128)S(1)} %get-tuple-element.76), channel_id=1, source_target_pairs={{8,16},{16,8},{9,17},{17,9},{10,18},{18,10},{11,19},{19,11},{12,20... | collective-permute-start | bytes 98312 | tf_op jit(solution)/shard_map/ppermute | solution.py:30
  6.6 3.2 %collective-permute-start.3 = (f32[16,2,512]{2,1,0:T(2,128)S(1)}, f32[16,2,512]{2,1,0:T(2,128)S(1)}, u32[]{:S(2)}, u32[]{:S(2)}) collective-permute-start(f32[16,2,512]{2,1,0:T(2,128)S(1)} %get-tuple-element.63), channel_id=1, source_target_pairs={{0,1},{1,0},{2,3},{3,2},{4,5},{5,4},{6,7},{7,6},{8,9},{9,8},{10,11... | collective-permute-start | bytes 196616 | tf_op jit(solution)/shard_map/ppermute | solution.py:29
  6.7 2.1 %copy-start.6 = (f32[16,8,512]{2,1,0:T(8,128)S(1)}, f32[16,8,512]{2,1,0:T(8,128)}, u32[]{:S(2)}) copy-start(f32[16,8,512]{2,1,0:T(8,128)} %param.9) | copy-start | bytes 786436
  6.7 3.1 %collective-permute-start.2 = (f32[16,2,512]{2,1,0:T(2,128)S(1)}, f32[16,2,512]{2,1,0:T(2,128)S(1)}, u32[]{:S(2)}, u32[]{:S(2)}) collective-permute-start(f32[16,2,512]{2,1,0:T(2,128)S(1)} %get-tuple-element.64), channel_id=1, source_target_pairs={{1,2},{2,1},{3,4},{4,3},{5,6},{6,5},{9,10},{10,9},{11,12},{12,11},... | collective-permute-start | bytes 196616 | tf_op jit(solution)/shard_map/ppermute | solution.py:30
  8.6 1.0 %copy-start.5 = (f32[16,8,512]{2,1,0:T(8,128)S(1)}, f32[16,8,512]{2,1,0:T(8,128)}, u32[]{:S(2)}) copy-start(f32[16,8,512]{2,1,0:T(8,128)} %param.10) | copy-start | bytes 786436
  8.6 1.0 %copy-start.7 = (f32[16,8,512]{2,1,0:T(8,128)S(1)}, f32[16,8,512]{2,1,0:T(8,128)}, u32[]{:S(2)}) copy-start(f32[16,8,512]{2,1,0:T(8,128)} %param.11) | copy-start | bytes 786436
  8.8 1.1 %copy-start.8 = (f32[16,8,512]{2,1,0:T(8,128)S(1)}, f32[16,8,512]{2,1,0:T(8,128)}, u32[]{:S(2)}) copy-start(f32[16,8,512]{2,1,0:T(8,128)} %param.8) | copy-start | bytes 786436
  8.8 1.1 %copy-start.9 = (f32[16,8,512]{2,1,0:T(8,128)S(1)}, f32[16,8,512]{2,1,0:T(8,128)}, u32[]{:S(2)}) copy-start(f32[16,8,512]{2,1,0:T(8,128)} %param.7) | copy-start | bytes 786436
  10.5 6.7 %copy-start.3 = (f32[16,8,512]{2,1,0:T(8,128)}, f32[16,8,512]{2,1,0:T(8,128)S(1)}, u32[]{:S(2)}) copy-start(f32[16,8,512]{2,1,0:T(8,128)S(1)} %fusion.6.refs_0_.refs_1_) | copy-start | bytes 786436
  10.8 13.0 %collective-permute-start.5 = (f32[1,8,512]{2,1,0:T(8,128)S(1)}, f32[1,8,512]{2,1,0:T(8,128)S(1)}, u32[]{:S(2)}, u32[]{:S(2)}) collective-permute-start(f32[1,8,512]{2,1,0:T(8,128)S(1)} %get-tuple-element.47), channel_id=1, source_target_pairs={{8,16},{16,8},{9,17},{17,9},{10,18},{18,10},{11,19},{19,11},{12,20... | collective-permute-start | bytes 49160 | tf_op jit(solution)/shard_map/ppermute | solution.py:30
  11.4 12.3 %collective-permute-start.4 = (f32[1,8,512]{2,1,0:T(8,128)S(1)}, f32[1,8,512]{2,1,0:T(8,128)S(1)}, u32[]{:S(2)}, u32[]{:S(2)}) collective-permute-start(f32[1,8,512]{2,1,0:T(8,128)S(1)} %get-tuple-element.48), channel_id=1, source_target_pairs={{0,8},{8,0},{16,24},{24,16},{1,9},{9,1},{17,25},{25,17},{2,10},{10... | collective-permute-start | bytes 49160 | tf_op jit(solution)/shard_map/ppermute | solution.py:29
  17.2 6.6 %collective-permute-start.7 = (f32[16,1,512]{2,1,0:T(1,128)S(1)}, f32[16,1,512]{2,1,0:T(1,128)S(1)}, u32[]{:S(2)}, u32[]{:S(2)}) collective-permute-start(f32[16,1,512]{2,1,0:T(1,128)S(1)} %get-tuple-element.43), channel_id=1, source_target_pairs={{1,2},{2,1},{3,4},{4,3},{5,6},{6,5},{9,10},{10,9},{11,12},{12,11},... | collective-permute-start | bytes 98312 | tf_op jit(solution)/shard_map/ppermute | solution.py:30
  17.9 6.8 %collective-permute-start.6 = (f32[16,1,512]{2,1,0:T(1,128)S(1)}, f32[16,1,512]{2,1,0:T(1,128)S(1)}, u32[]{:S(2)}, u32[]{:S(2)}) collective-permute-start(f32[16,1,512]{2,1,0:T(1,128)S(1)} %get-tuple-element.44), channel_id=1, source_target_pairs={{0,1},{1,0},{2,3},{3,2},{4,5},{5,4},{6,7},{7,6},{8,9},{9,8},{10,11... | collective-permute-start | bytes 98312 | tf_op jit(solution)/shard_map/ppermute | solution.py:29
  25.1 4.7 %copy-start = (f32[16,8,512]{2,1,0:T(8,128)}, f32[16,8,512]{2,1,0:T(8,128)S(1)}, u32[]{:S(2)}) copy-start(f32[16,8,512]{2,1,0:T(8,128)S(1)} %fusion.13.refs_1_.refs_2_) | copy-start | bytes 786436
  25.4 8.9 %collective-permute-start.9 = (f32[1,8,512]{2,1,0:T(8,128)S(1)}, f32[1,8,512]{2,1,0:T(8,128)S(1)}, u32[]{:S(2)}, u32[]{:S(2)}) collective-permute-start(f32[1,8,512]{2,1,0:T(8,128)S(1)} %get-tuple-element.37), channel_id=1, source_target_pairs={{8,16},{16,8},{9,17},{17,9},{10,18},{18,10},{11,19},{19,11},{12,20... | collective-permute-start | bytes 49160 | tf_op jit(solution)/shard_map/ppermute | solution.py:30
  26.0 8.2 %collective-permute-start.8 = (f32[1,8,512]{2,1,0:T(8,128)S(1)}, f32[1,8,512]{2,1,0:T(8,128)S(1)}, u32[]{:S(2)}, u32[]{:S(2)}) collective-permute-start(f32[1,8,512]{2,1,0:T(8,128)S(1)} %get-tuple-element.38), channel_id=1, source_target_pairs={{0,8},{8,0},{16,24},{24,16},{1,9},{9,1},{17,25},{25,17},{2,10},{10... | collective-permute-start | bytes 49160 | tf_op jit(solution)/shard_map/ppermute | solution.py:29
  29.9 4.4 %collective-permute-start.11 = (f32[16,1,512]{2,1,0:T(1,128)S(1)}, f32[16,1,512]{2,1,0:T(1,128)S(1)}, u32[]{:S(2)}, u32[]{:S(2)}) collective-permute-start(f32[16,1,512]{2,1,0:T(1,128)S(1)} %get-tuple-element.33), channel_id=1, source_target_pairs={{1,2},{2,1},{3,4},{4,3},{5,6},{6,5},{9,10},{10,9},{11,12},{12,11},... | collective-permute-start | bytes 98312 | tf_op jit(solution)/shard_map/ppermute | solution.py:30
  30.5 4.6 %collective-permute-start.10 = (f32[16,1,512]{2,1,0:T(1,128)S(1)}, f32[16,1,512]{2,1,0:T(1,128)S(1)}, u32[]{:S(2)}, u32[]{:S(2)}) collective-permute-start(f32[16,1,512]{2,1,0:T(1,128)S(1)} %get-tuple-element.34), channel_id=1, source_target_pairs={{0,1},{1,0},{2,3},{3,2},{4,5},{5,4},{6,7},{7,6},{8,9},{9,8},{10,11... | collective-permute-start | bytes 98312 | tf_op jit(solution)/shard_map/ppermute | solution.py:29
  35.6 3.1 %copy-start.1 = (f32[16,8,512]{2,1,0:T(8,128)}, f32[16,8,512]{2,1,0:T(8,128)S(1)}, u32[]{:S(2)}) copy-start(f32[16,8,512]{2,1,0:T(8,128)S(1)} %fusion.20.refs_2_.refs_3_) | copy-start | bytes 786436
  35.9 7.2 %collective-permute-start.13 = (f32[1,8,512]{2,1,0:T(8,128)S(1)}, f32[1,8,512]{2,1,0:T(8,128)S(1)}, u32[]{:S(2)}, u32[]{:S(2)}) collective-permute-start(f32[1,8,512]{2,1,0:T(8,128)S(1)} %get-tuple-element.27), channel_id=1, source_target_pairs={{8,16},{16,8},{9,17},{17,9},{10,18},{18,10},{11,19},{19,11},{12,20... | collective-permute-start | bytes 49160 | tf_op jit(solution)/shard_map/ppermute | solution.py:30
  36.5 6.5 %collective-permute-start.12 = (f32[1,8,512]{2,1,0:T(8,128)S(1)}, f32[1,8,512]{2,1,0:T(8,128)S(1)}, u32[]{:S(2)}, u32[]{:S(2)}) collective-permute-start(f32[1,8,512]{2,1,0:T(8,128)S(1)} %get-tuple-element.28), channel_id=1, source_target_pairs={{0,8},{8,0},{16,24},{24,16},{1,9},{9,1},{17,25},{25,17},{2,10},{10... | collective-permute-start | bytes 49160 | tf_op jit(solution)/shard_map/ppermute | solution.py:29
  38.7 4.4 %collective-permute-start.15 = (f32[16,1,512]{2,1,0:T(1,128)S(1)}, f32[16,1,512]{2,1,0:T(1,128)S(1)}, u32[]{:S(2)}, u32[]{:S(2)}) collective-permute-start(f32[16,1,512]{2,1,0:T(1,128)S(1)} %get-tuple-element.23), channel_id=1, source_target_pairs={{1,2},{2,1},{3,4},{4,3},{5,6},{6,5},{9,10},{10,9},{11,12},{12,11},... | collective-permute-start | bytes 98312 | tf_op jit(solution)/shard_map/ppermute | solution.py:30
  39.3 4.5 %collective-permute-start.14 = (f32[16,1,512]{2,1,0:T(1,128)S(1)}, f32[16,1,512]{2,1,0:T(1,128)S(1)}, u32[]{:S(2)}, u32[]{:S(2)}) collective-permute-start(f32[16,1,512]{2,1,0:T(1,128)S(1)} %get-tuple-element.24), channel_id=1, source_target_pairs={{0,1},{1,0},{2,3},{3,2},{4,5},{5,4},{6,7},{7,6},{8,9},{9,8},{10,11... | collective-permute-start | bytes 98312 | tf_op jit(solution)/shard_map/ppermute | solution.py:29
  44.3 4.5 %copy-start.2 = (f32[16,8,512]{2,1,0:T(8,128)}, f32[16,8,512]{2,1,0:T(8,128)S(1)}, u32[]{:S(2)}) copy-start(f32[16,8,512]{2,1,0:T(8,128)S(1)} %fusion.27.refs_3_.refs_4_) | copy-start | bytes 786436
  44.6 8.6 %collective-permute-start.17 = (f32[1,8,512]{2,1,0:T(8,128)S(1)}, f32[1,8,512]{2,1,0:T(8,128)S(1)}, u32[]{:S(2)}, u32[]{:S(2)}) collective-permute-start(f32[1,8,512]{2,1,0:T(8,128)S(1)} %get-tuple-element.17), channel_id=1, source_target_pairs={{8,16},{16,8},{9,17},{17,9},{10,18},{18,10},{11,19},{19,11},{12,20... | collective-permute-start | bytes 49160 | tf_op jit(solution)/shard_map/ppermute | solution.py:30
  45.3 8.0 %collective-permute-start.16 = (f32[1,8,512]{2,1,0:T(8,128)S(1)}, f32[1,8,512]{2,1,0:T(8,128)S(1)}, u32[]{:S(2)}, u32[]{:S(2)}) collective-permute-start(f32[1,8,512]{2,1,0:T(8,128)S(1)} %get-tuple-element.18), channel_id=1, source_target_pairs={{0,8},{8,0},{16,24},{24,16},{1,9},{9,1},{17,25},{25,17},{2,10},{10... | collective-permute-start | bytes 49160 | tf_op jit(solution)/shard_map/ppermute | solution.py:29
  48.9 4.4 %collective-permute-start.19 = (f32[16,1,512]{2,1,0:T(1,128)S(1)}, f32[16,1,512]{2,1,0:T(1,128)S(1)}, u32[]{:S(2)}, u32[]{:S(2)}) collective-permute-start(f32[16,1,512]{2,1,0:T(1,128)S(1)} %get-tuple-element.13), channel_id=1, source_target_pairs={{1,2},{2,1},{3,4},{4,3},{5,6},{6,5},{9,10},{10,9},{11,12},{12,11},... | collective-permute-start | bytes 98312 | tf_op jit(solution)/shard_map/ppermute | solution.py:30
  49.6 4.5 %collective-permute-start.18 = (f32[16,1,512]{2,1,0:T(1,128)S(1)}, f32[16,1,512]{2,1,0:T(1,128)S(1)}, u32[]{:S(2)}, u32[]{:S(2)}) collective-permute-start(f32[16,1,512]{2,1,0:T(1,128)S(1)} %get-tuple-element.14), channel_id=1, source_target_pairs={{0,1},{1,0},{2,3},{3,2},{4,5},{5,4},{6,7},{7,6},{8,9},{9,8},{10,11... | collective-permute-start | bytes 98312 | tf_op jit(solution)/shard_map/ppermute | solution.py:29
  57.6 1.7 %collective-permute-start.20 = (f32[8,128]{1,0:T(8,128)}, f32[8,128]{1,0:T(8,128)S(1)}, u32[]{:S(2)}, u32[]{:S(2)}) collective-permute-start(f32[8,128]{1,0:T(8,128)} %shard_map.85), channel_id=1, source_target_pairs={{0,1},{1,0},{2,3},{3,2},{4,5},{5,4},{6,7},{7,6},{8,9},{9,8},{10,11... | collective-permute-start | bytes 12296 | tf_op jit(solution)/shard_map/ppermute | solution.py:70
  60.0 3.6 %collective-permute-start.21 = (f32[8,128]{1,0:T(8,128)S(1)}, f32[8,128]{1,0:T(8,128)S(1)}, u32[]{:S(2)}, u32[]{:S(2)}) collective-permute-start(f32[8,128]{1,0:T(8,128)S(1)} %add.178), channel_id=1, source_target_pairs={{0,2},{1,3},{2,0},{3,1},{4,6},{5,7},{6,4},{7,5},{8,10},{9,11},{10,... | collective-permute-start | bytes 12296 | tf_op jit(solution)/shard_map/ppermute | solution.py:70
  63.6 4.6 %collective-permute-start.22 = (f32[8,128]{1,0:T(8,128)S(1)}, f32[8,128]{1,0:T(8,128)S(1)}, u32[]{:S(2)}, u32[]{:S(2)}) collective-permute-start(f32[8,128]{1,0:T(8,128)S(1)} %add.179), channel_id=1, source_target_pairs={{0,4},{1,5},{2,6},{3,7},{4,0},{5,1},{6,2},{7,3},{8,12},{9,13},{10,... | collective-permute-start | bytes 12296 | tf_op jit(solution)/shard_map/ppermute | solution.py:70
  68.2 3.6 %collective-permute-start.23 = (f32[8,128]{1,0:T(8,128)S(1)}, f32[8,128]{1,0:T(8,128)S(1)}, u32[]{:S(2)}, u32[]{:S(2)}) collective-permute-start(f32[8,128]{1,0:T(8,128)S(1)} %add.180), channel_id=1, source_target_pairs={{0,8},{8,0},{16,24},{24,16},{1,9},{9,1},{17,25},{25,17},{2,10},{10... | collective-permute-start | bytes 12296 | tf_op jit(solution)/shard_map/ppermute | solution.py:70
  71.8 3.6 %collective-permute-start.24 = (f32[8,128]{1,0:T(8,128)S(1)}, f32[8,128]{1,0:T(8,128)S(1)}, u32[]{:S(2)}, u32[]{:S(2)}) collective-permute-start(f32[8,128]{1,0:T(8,128)S(1)} %add.181), channel_id=1, source_target_pairs={{0,16},{8,24},{16,0},{24,8},{1,17},{9,25},{17,1},{25,9},{2,18},{10... | collective-permute-start | bytes 12296 | tf_op jit(solution)/shard_map/ppermute | solution.py:70

commit v7 on v6

--- a/solution.py
+++ b/solution.py
@@ -57,6 +57,10 @@
 
 def field_halo(u):
     return exchange(u[:1], u[-1:], u[:, :1], u[:, -1:])
+
+
+def shift_z(a):
+    return jnp.concatenate([a[..., 1:], jnp.zeros_like(a[..., :1])], axis=-1)
 
 
 def all_sum(x):
@@ -183,38 +187,68 @@
     return ortho, upper, scale.reshape(())
 
 
+def wide_exchange(block, depth):
+    from_low, from_high = axis_exchange(block[:depth], block[-depth:], "gx")
+    block = jnp.concatenate([from_low, block, from_high], axis=0)
+    from_low, from_high = axis_exchange(block[:, :depth], block[:, -depth:], "gy")
+    return jnp.concatenate([from_low, block, from_high], axis=1)
+
+
+def shrink_sum(u, coef):
+    tx_lo, tx_hi, ty_lo, ty_hi, tz_lo, tz_hi = coef
+    centre = u[1:-1, 1:-1]
+    zero_plane = jnp.zeros_like(centre[..., :1])
+    z_low = jnp.concatenate([zero_plane, centre[..., :-1]], axis=-1)
+    z_high = jnp.concatenate([centre[..., 1:], zero_plane], axis=-1)
+    total = tx_lo * u[:-2, 1:-1] + tx_hi * u[2:, 1:-1]
+    total = total + ty_lo * u[1:-1, :-2] + ty_hi * u[1:-1, 2:]
+    total = total + tz_lo * z_low + tz_hi * z_high
+    return total
+
+
 def local(start_field, right_side, accumulation, trans_x, trans_y, trans_z):
     size_x, size_y, size_z = start_field.shape
     cells = size_x * size_y * size_z * lax.axis_size("gx") * lax.axis_size("gy")
-
-    lo_both_x, hi_both_x, lo_both_y, hi_both_y = exchange(
-        jnp.concatenate([start_field[:1], trans_x[:1]], axis=0),
-        jnp.concatenate([start_field[-1:], trans_x[-1:]], axis=0),
-        jnp.concatenate([start_field[:, :1], trans_y[:, :1]], axis=1),
-        jnp.concatenate([start_field[:, -1:], trans_y[:, -1:]], axis=1),
-    )
-    lo_x, hi_x, plane_x = lo_both_x[:1], hi_both_x[:1], hi_both_x[1:]
-    lo_y, hi_y, plane_y = lo_both_y[:, :1], hi_both_y[:, :1], hi_both_y[:, 1:]
-
-    zero_plane = jnp.zeros_like(trans_z[..., :1])
-    tx_lo = trans_x
-    tx_hi = jnp.concatenate([trans_x[1:], plane_x], axis=0)
-    ty_lo = trans_y
-    ty_hi = jnp.concatenate([trans_y[:, 1:], plane_y], axis=1)
-    tz_lo = trans_z
-    tz_hi = jnp.concatenate([trans_z[..., 1:], zero_plane], axis=-1)
-    coef = (tx_lo, tx_hi, ty_lo, ty_hi, tz_lo, tz_hi)
-    diagonal = accumulation + tx_lo + tx_hi + ty_lo + ty_hi + tz_lo + tz_hi
-
-    total = neighbour_sum(start_field, (lo_x, hi_x, lo_y, hi_y), coef)
-    residual0 = right_side - (diagonal * start_field - total)
-
-    vector = residual0
-    basis = [vector]
-    for step in range(STEPS):
-        total = neighbour_sum(vector, field_halo(vector), coef)
-        vector = 2.0 * total / diagonal
-        basis.append(vector)
+    depth = 2
+
+    inputs = (start_field, right_side, accumulation, trans_x, trans_y, trans_z)
+    wide = wide_exchange(jnp.concatenate(inputs, axis=-1), depth)
+    field, rhs, acc, t_x, t_y, t_z = (wide[..., k * size_z : (k + 1) * size_z] for k in range(len(inputs)))
+
+    first_x = lax.axis_index("gx") * size_x - depth
+    first_y = lax.axis_index("gy") * size_y - depth
+    grid_x = size_x * lax.axis_size("gx")
+    grid_y = size_y * lax.axis_size("gy")
+
+    def region(a, m, dx=0, dy=0):
+        o = depth - m
+        return a[o + dx : o + dx + size_x + 2 * m, o + dy : o + dy + size_y + 2 * m]
+
+    def inside(m):
+        o = depth - m
+        gi = first_x + o + lax.broadcasted_iota(jnp.int32, (size_x + 2 * m, 1, 1), 0)
+        gj = first_y + o + lax.broadcasted_iota(jnp.int32, (1, size_y + 2 * m, 1), 1)
+        return (gi >= 0) & (gi < grid_x) & (gj >= 0) & (gj < grid_y)
+
+    def coefficients(m):
+        tz_lo = region(t_z, m)
+        return (region(t_x, m), region(t_x, m, 1), region(t_y, m), region(t_y, m, 0, 1), tz_lo, shift_z(tz_lo))
+
+    ring, centre = coefficients(1), coefficients(0)
+    tx_lo, tx_hi, ty_lo, ty_hi, tz_lo, tz_hi = ring
+    diag_ring = region(acc, 1) + tx_lo + tx_hi + ty_lo + ty_hi + tz_lo + tz_hi
+    diag = diag_ring[1:-1, 1:-1]
+
+    residual0 = region(rhs, 1) - (diag_ring * region(field, 1) - shrink_sum(field, ring))
+    residual0 = jnp.where(inside(1), residual0, 0.0)
+
+    basis = [residual0[1:-1, 1:-1]]
+    basis.append(2.0 * shrink_sum(residual0, centre) / diag)
+    vector = jnp.where(inside(1), 2.0 * shrink_sum(wide_exchange(basis[1], depth), ring) / diag_ring, 0.0)
+    basis.append(vector[1:-1, 1:-1])
+    basis.append(2.0 * shrink_sum(vector, centre) / diag)
+    basis.append(2.0 * neighbour_sum(basis[3], field_halo(basis[3]), centre) / diag)
+    assert len(basis) == STEPS + 1
     stats = gram(basis)
     stats = all_sum(stats)
     ortho, upper, scale = finish(stats, basis, cells)

time: 79.3 us -> 82.7 us (1.043)
  other arithmetic: 4.77 us -> 11.2 us
  starting transfers between devices: 47.6 us -> 44 us
  waiting for transfers between devices: 14.8 us -> 16.5 us
  local copies, waits for them, and re-layouts: 5.32 us -> 4.45 us
    ppermute x10 -> x6, starting transfers between devices: 35.2 us -> 29.2 us  [axis_exchange(): lax.ppermute(jnp.where(odd, to_low, to_high), axis, swap_pairs(axis, 0))]
    ppermute x10 -> x6, waiting for transfers between devices: 3.35 us -> 8.79 us  [axis_exchange(): lax.ppermute(jnp.where(odd, to_low, to_high), axis, swap_pairs(axis, 0))]
    ppermute x5, starting transfers between devices: 5.63 us -> 10.1 us  [all_sum(): x = x + lax.ppermute(x, axis, [(i, i ^ step) for i in range(n)])]
    ppermute x5, waiting for transfers between devices: 11.4 us -> 7.71 us  [all_sum(): x = x + lax.ppermute(x, axis, [(i, i ^ step) for i in range(n)])]
    unnamed x20 -> x15, local copies, waits for them, and re-layouts: 0.77 us -> 3.04 us
    select_n x0 -> x2, other arithmetic: none -> 2.06 us  [the longest x1 1.09 us: local(): residual0 = jnp.where(inside(1), residual0, 0.0)]
    ppermute x10 -> x6, starting transfers between devices: 6.75 us -> 4.73 us  [axis_exchange(): lax.ppermute(jnp.where(odd, to_high, to_low), axis, swap_pairs(axis, 1))]
    select_n x2 -> x4, other arithmetic: 0.04 us -> 1.31 us  [axis_exchange(): from_low = jnp.where(odd, even_swap, odd_swap)]
  transfers between devices with their start and end apart: 25 -> 17, of which waited for: 9 -> 10; matrix products, arithmetic and copies ran while one was open for 4% -> 0% of each run, Pallas kernels for 0% -> 0%
where the time goes in v7:
time: 82.7 us; the launch traced here: 82.2 us
  starting transfers between devices  44 us (53%)
  waiting for transfers between devices  16.5 us (20%)
  other arithmetic  11.2 us (14%)
  Pallas kernels  5.06 us (6%)
  local copies, waits for them, and re-layouts  4.45 us (5%)
  between operations  0.99 us (1%)
    ppermute x6, starting transfers between devices, axis_exchange(): lax.ppermute(jnp.where(odd, to_low, to_high), axis, swap_pairs(axis, 0))  29.2 us
    ppermute x5, starting transfers between devices, all_sum(): x = x + lax.ppermute(x, axis, [(i, i ^ step) for i in range(n)])  10.1 us
    ppermute x6, waiting for transfers between devices, axis_exchange(): lax.ppermute(jnp.where(odd, to_low, to_high), axis, swap_pairs(axis, 0))  8.79 us
    ppermute x5, waiting for transfers between devices, all_sum(): x = x + lax.ppermute(x, axis, [(i, i ^ step) for i in range(n)])  7.71 us
    ppermute x6, starting transfers between devices, axis_exchange(): lax.ppermute(jnp.where(odd, to_high, to_low), axis, swap_pairs(axis, 1))  4.73 us
    unnamed x15, local copies, waits for them, and re-layouts  3.04 us
    pallas_call x1, Pallas kernels, finish(): pl.pallas_call(lambda *refs: finish_kernel(float(cells), size, *refs), ou...  2.75 us
    pallas_call x1, Pallas kernels, gram(): pl.pallas_call(lambda *refs: gram_kernel(size, *refs), out_shape=jax.Shap...  2.31 us
  transfers between devices with their start and end apart: 17, of which 10 were waited for; matrix products, arithmetic and copies ran while one was open for 0% of the time, Pallas kernels for 0%

profile of v7, /device:TPU:0, one launch (start us, length us, event | category | flops | bytes accessed | tf_op | source)
XLA Modules:
  0.0 82.2 jit_solution(16749227951154671024)
XLA Ops:
  0.6 0.0 copy-start.3
  0.6 0.0 copy-start.4
  0.7 1.0 %constant_dynamic-update-slice_fusion.5 = f32[16,8,3072]{2,1,0:T(8,128)S(1)} fusion(f32[16,8,512]{2,1,0:T(8,128)} %param.6), kind=kLoop, calls=%fused_computation.113 | loop fusion | bytes 524288
  1.7 1.0 %constant_dynamic-update-slice_fusion.4 = f32[16,8,3072]{2,1,0:T(8,128)S(1)} fusion(f32[16,8,3072]{2,1,0:T(8,128)S(1)} %constant_dynamic-update-slice_fusion.5, f32[16,8,512]{2,1,0:T(8,128)} %param.7), kind=kLoop, calls=%fused_computation.112 | loop fusion | bytes 524288
  2.7 1.0 %constant_dynamic-update-slice_fusion.3 = f32[16,8,3072]{2,1,0:T(8,128)S(1)} fusion(f32[16,8,3072]{2,1,0:T(8,128)S(1)} %constant_dynamic-update-slice_fusion.4, f32[16,8,512]{2,1,0:T(8,128)} %param.8), kind=kLoop, calls=%fused_computation.111 | loop fusion | bytes 524288
  3.7 0.0 copy-done.3
  3.8 3.0 %collective-permute-start = (f32[2,8,3072]{2,1,0:T(8,128)S(1)}, f32[2,8,3072]{2,1,0:T(8,128)S(1)}, u32[]{:S(2)}, u32[]{:S(2)}) collective-permute-start(f32[2,8,3072]{2,1,0:T(8,128)S(1)} %get-tuple-element.24), channel_id=1, source_target_pairs={{0,8},{8,0},{16,24},{24,16},{1,9},{9,1},{17,25},{25,17},{2,10},{10... | collective-permute-start | bytes 589832 | tf_op jit(solution)/shard_map/ppermute | solution.py:29
  6.8 0.7 collective-permute-start.1
  7.5 4.2 %collective-permute-done = f32[2,8,3072]{2,1,0:T(8,128)S(1)} collective-permute-done((f32[2,8,3072]{2,1,0:T(8,128)S(1)}, f32[2,8,3072]{2,1,0:T(8,128)S(1)}, u32[]{:S(2)}, u32[]{:S(2)}) %collective-permute-start) | collective-permute-done | bytes 196640 | tf_op jit(solution)/shard_map/ppermute | solution.py:29
  11.7 0.0 collective-permute-done.1
  11.8 1.2 %broadcast_select_fusion.3 = (f32[20,2,3072]{2,1,0:T(2,128)}, f32[20,2,3072]{2,1,0:T(2,128)S(1)}, f32[20,2,3072]{2,1,0:T(2,128)S(1)}) fusion(pred[]{:T(512)S(6)} %eq.17, f32[2,8,3072]{2,1,0:T(8,128)S(1)} %get-tuple-element.38, f32[16,8,3072]{2,1,0:T(8,128)S(1)} %constant_dynamic-update-slice_fusion, f32[2,8,3072]{2,1,0:T(8,128)S(1)} %get-tuple-element.37), kind=kLoop, calls=%fused_computation.49 | loop fusion | flops 614400 | bytes 3440641 | tf_op jit(solution)/shard_map/jit(_where)/select_n | solution.py:29
  13.0 0.9 %broadcast_select_fusion.2 = f32[5,8,3072]{2,1,0:T(8,128)} fusion(f32[5,8,3072]{2,1,0:T(8,128)S(1)} %bitcast.25, f32[5,8,3072]{2,1,0:T(8,128)S(1)} %bitcast.24, pred[]{:T(512)S(6)} %eq.17), kind=kLoop, calls=%fused_computation.48 | loop fusion | flops 122880 | bytes 1474561 | tf_op jit(solution)/shard_map/jit(_where)/select_n | solution.py:30
  13.9 1.4 %collective-permute-start.3 = (f32[20,2,3072]{2,1,0:T(2,128)}, f32[20,2,3072]{2,1,0:T(2,128)}, u32[]{:S(2)}, u32[]{:S(2)}) collective-permute-start(f32[20,2,3072]{2,1,0:T(2,128)} %bitcast.3), channel_id=1, source_target_pairs={{1,2},{2,1},{3,4},{4,3},{5,6},{6,5},{9,10},{10,9},{11,12},{12,11},... | collective-permute-start | bytes 1474568 | tf_op jit(solution)/shard_map/ppermute | solution.py:30
  15.3 2.6 %collective-permute-start.2 = (f32[20,2,3072]{2,1,0:T(2,128)}, f32[20,2,3072]{2,1,0:T(2,128)}, u32[]{:S(2)}, u32[]{:S(2)}) collective-permute-start(f32[20,2,3072]{2,1,0:T(2,128)} %get-tuple-element.18), channel_id=1, source_target_pairs={{0,1},{1,0},{2,3},{3,2},{4,5},{5,4},{6,7},{7,6},{8,9},{9,8},{10,11... | collective-permute-start | bytes 1474568 | tf_op jit(solution)/shard_map/ppermute | solution.py:29
  17.9 0.1 slice.254
  18.0 0.1 and_and_fusion
  18.1 0.0 collective-permute-done.3
  18.1 1.6 %collective-permute-done.2 = f32[20,2,3072]{2,1,0:T(2,128)} collective-permute-done((f32[20,2,3072]{2,1,0:T(2,128)}, f32[20,2,3072]{2,1,0:T(2,128)}, u32[]{:S(2)}, u32[]{:S(2)}) %collective-permute-start.2) | collective-permute-done | bytes 491552 | tf_op jit(solution)/shard_map/ppermute | solution.py:29
  19.7 1.3 %broadcast_select_fusion.1 = (f32[5,8,3072]{2,1,0:T(8,128)S(1)}, f32[5,8,3072]{2,1,0:T(8,128)S(1)}) fusion(f32[5,8,3072]{2,1,0:T(8,128)} %bitcast.4, f32[5,8,3072]{2,1,0:T(8,128)} %bitcast.5, pred[]{:T(512)S(6)} %eq.17), kind=kLoop, calls=%fused_computation.47 | loop fusion | flops 245760 | bytes 1966081 | tf_op jit(solution)/shard_map/jit(_where)/select_n | solution.py:31
  21.0 0.7 pad_maximum_fusion
  21.6 0.5 fusion.48
  22.1 1.1 %fusion.14 = (f32[18,10,512]{2,1,0:T(8,128)S(1)}, f32[18,10,512]{2,1,0:T(8,128)S(1)}, f32[18,10,512]{2,1,0:T(8,128)S(1)}) fusion(f32[20,2,3072]{2,1,0:T(2,128)S(1)} %bitcast.20, f32[2,8,3072]{2,1,0:T(8,128)S(1)} %get-tuple-element.38, f32[16,8,3072]{2,1,0:T(8,128)S(1)} %constant_dynamic-update-slice_fusion, f32[2,8,3072]{2,1,0:T(8,128)S(1)} %get-tuple-element.37, ...), kind=kLoop, calls=%fused_computation.25 | loop fusion | flops 2764800 | bytes 8476740 | tf_op jit(solution)/shard_map/jit(_where)/select_n | solution.py:243
  23.2 0.1 fusion.51
  23.4 1.1 %fusion.35 = (f32[16,8,512]{2,1,0:T(8,128)S(1)}, f32[16,8,512]{2,1,0:T(8,128)S(1)}, f32[16,8,512]{2,1,0:T(8,128)S(1)}, f32[16,8,512]{2,1,0:T(8,128)}) fusion(f32[18,10,512]{2,1,0:T(8,128)S(1)} %get-tuple-element.15, f32[16,8,512]{2,1,0:T(8,128)S(1)} %copy-done.4, f32[16,8,512]{2,1,0:T(8,128)S(1)} %copy-done.3, f32[16,8,511]{2,1,0:T(8,128)S(1)} %get-tuple-element.36, ...), kind=kLoop, calls=%fused_computation.66 | loop fusion | flops 1114112 | bytes 6650368 | tf_op jit(solution)/shard_map/div | solution.py:246
  24.5 6.6 %collective-permute-start.4 = (f32[2,8,512]{2,1,0:T(8,128)S(1)}, f32[2,8,512]{2,1,0:T(8,128)S(1)}, u32[]{:S(2)}, u32[]{:S(2)}) collective-permute-start(f32[2,8,512]{2,1,0:T(8,128)S(1)} %get-tuple-element.49), channel_id=1, source_target_pairs={{0,8},{8,0},{16,24},{24,16},{1,9},{9,1},{17,25},{25,17},{2,10},{10... | collective-permute-start | bytes 98312 | tf_op jit(solution)/shard_map/ppermute | solution.py:29
  31.1 0.7 collective-permute-start.5
  31.8 1.2 %collective-permute-done.4 = f32[2,8,512]{2,1,0:T(8,128)S(1)} collective-permute-done((f32[2,8,512]{2,1,0:T(8,128)S(1)}, f32[2,8,512]{2,1,0:T(8,128)S(1)}, u32[]{:S(2)}, u32[]{:S(2)}) %collective-permute-start.4) | collective-permute-done | bytes 32800 | tf_op jit(solution)/shard_map/ppermute | solution.py:29
  33.0 0.0 collective-permute-done.5
  33.0 0.1 broadcast_select_fusion.9
  33.1 0.7 collective-permute-start.7
  33.8 8.0 %collective-permute-start.6 = (f32[20,2,512]{2,1,0:T(2,128)S(1)}, f32[20,2,512]{2,1,0:T(2,128)S(1)}, u32[]{:S(2)}, u32[]{:S(2)}) collective-permute-start(f32[20,2,512]{2,1,0:T(2,128)S(1)} %get-tuple-element.9), channel_id=1, source_target_pairs={{0,1},{1,0},{2,3},{3,2},{4,5},{5,4},{6,7},{7,6},{8,9},{9,8},{10,11... | collective-permute-start | bytes 245768 | tf_op jit(solution)/shard_map/ppermute | solution.py:29
  41.8 0.0 collective-permute-done.7
  41.8 0.9 %collective-permute-done.6 = f32[20,2,512]{2,1,0:T(2,128)S(1)} collective-permute-done((f32[20,2,512]{2,1,0:T(2,128)S(1)}, f32[20,2,512]{2,1,0:T(2,128)S(1)}, u32[]{:S(2)}, u32[]{:S(2)}) %collective-permute-start.6) | collective-permute-done | bytes 81952 | tf_op jit(solution)/shard_map/ppermute | solution.py:29
  42.7 0.1 pad_maximum_fusion.1
  42.8 0.3 fusion.49
  43.1 0.0 copy-done.1
  43.1 1.0 %fusion.23 = f32[18,10,512]{2,1,0:T(8,128)S(1)} fusion(f32[18,10,512]{2,1,0:T(8,128)S(1)} %get-tuple-element.16, f32[18,10,511]{2,1,0:T(8,128)S(1)} %get-tuple-element.29, f32[18,10,511]{2,1,0:T(8,128)S(1)} %get-tuple-element.28, f32[18,10,512]{2,1,0:T(8,128)S(1)} %get-tuple-element.17, f32[20,2,512]{2,1,0:T(2,128)S(1)} %bitcast.29, ...), kind=kLoop, calls=%fused_computation.42 | loop fusion | flops 1843200 | bytes 4913220 | tf_op jit(solution)/shard_map/jit(_where)/select_n | solution.py:247
  44.1 0.1 fusion.50
  44.2 1.1 %fusion.28 = (f32[16,8,512]{2,1,0:T(8,128)S(1)}, f32[16,8,512]{2,1,0:T(8,128)}) fusion(f32[16,8,512]{2,1,0:T(8,128)S(1)} %get-tuple-element.14, f32[18,10,512]{2,1,0:T(8,128)S(1)} %fusion.23, f32[16,8,512]{2,1,0:T(8,128)S(1)} %copy-done.4, f32[16,8,512]{2,1,0:T(8,128)S(1)} %get-tuple-element.13, f32[16,8,512]{2,1,0:T(8,128)S(1)} %copy-done.3, ...), kind=kLoop, calls=%fused_computation.55 | loop fusion | flops 851968 | bytes 4192768 | tf_op jit(solution)/shard_map/div | solution.py:249
  45.4 0.1 fusion.52
  45.5 0.1 fusion.53
  45.6 4.9 %collective-permute-start.8 = (f32[1,8,512]{2,1,0:T(8,128)S(1)}, f32[1,8,512]{2,1,0:T(8,128)S(1)}, u32[]{:S(2)}, u32[]{:S(2)}) collective-permute-start(f32[1,8,512]{2,1,0:T(8,128)S(1)} %get-tuple-element.48), channel_id=1, source_target_pairs={{0,8},{8,0},{16,24},{24,16},{1,9},{9,1},{17,25},{25,17},{2,10},{10... | collective-permute-start | bytes 49160 | tf_op jit(solution)/shard_map/ppermute | solution.py:29
  50.5 0.7 collective-permute-start.9
  51.2 0.7 collective-permute-start.11
  51.9 4.2 %collective-permute-start.10 = (f32[16,1,512]{2,1,0:T(1,128)S(1)}, f32[16,1,512]{2,1,0:T(1,128)S(1)}, u32[]{:S(2)}, u32[]{:S(2)}) collective-permute-start(f32[16,1,512]{2,1,0:T(1,128)S(1)} %get-tuple-element.44), channel_id=1, source_target_pairs={{0,1},{1,0},{2,3},{3,2},{4,5},{5,4},{6,7},{7,6},{8,9},{9,8},{10,11... | collective-permute-start | bytes 98312 | tf_op jit(solution)/shard_map/ppermute | solution.py:29
  56.1 0.0 collective-permute-done.8
  56.1 0.0 collective-permute-done.9
  56.1 0.0 collective-permute-done.11
  56.1 0.8 %collective-permute-done.10 = f32[16,1,512]{2,1,0:T(1,128)S(1)} collective-permute-done((f32[16,1,512]{2,1,0:T(1,128)S(1)}, f32[16,1,512]{2,1,0:T(1,128)S(1)}, u32[]{:S(2)}, u32[]{:S(2)}) %collective-permute-start.10) | collective-permute-done | bytes 32800 | tf_op jit(solution)/shard_map/ppermute | solution.py:29
  56.9 1.2 %fusion.44.refs_4_.refs_5_ = f32[16,8,512]{2,1,0:T(8,128)} fusion(f32[16,8,512]{2,1,0:T(8,128)S(1)} %copy-done.3, f32[15,8,512]{2,1,0:T(8,128)S(1)} %get-tuple-element.46, f32[1,8,512]{2,1,0:T(8,128)S(1)} %get-tuple-element.58, f32[16,8,512]{2,1,0:T(8,128)S(1)} %get-tuple-element.13, f32[1,8,512]{2,1,0:T(8,128)S(1)} %get-tuple-element.57, ...), kind=kLoop, calls=%fused_computation.83 | loop fusion | flops 1114112 | bytes 3668480 | tf_op jit(solution)/shard_map/div | solution.py:250
  58.1 2.3 %shard_map.85 = f32[8,128]{1,0:T(8,128)} custom-call(f32[16,8,512]{2,1,0:T(8,128)} %get-tuple-element.34.refs_0_.refs_1_, f32[16,8,512]{2,1,0:T(8,128)} %copy-done.1, f32[16,8,512]{2,1,0:T(8,128)} %get-tuple-element.31.refs_2_.refs_3_, f32[16,8,512]{2,1,0:T(8,128)} %copy-done, f32[16,8,512]{2,1,0:T(8,128)} %fusion.44.refs_4_.refs_5_), custom_call_target="tpu_custom_call" | custom-call | tf_op jit(solution)/shard_map/pallas_call | solution.py:111
  60.4 0.7 collective-permute-start.12
  61.1 1.0 %collective-permute-done.12 = f32[8,128]{1,0:T(8,128)S(1)} collective-permute-done((f32[8,128]{1,0:T(8,128)}, f32[8,128]{1,0:T(8,128)S(1)}, u32[]{:S(2)}, u32[]{:S(2)}) %collective-permute-start.12) | collective-permute-done | bytes 4128 | tf_op jit(solution)/shard_map/ppermute | solution.py:74
  62.1 0.7 add.225
  62.8 2.0 %collective-permute-start.13 = (f32[8,128]{1,0:T(8,128)S(1)}, f32[8,128]{1,0:T(8,128)S(1)}, u32[]{:S(2)}, u32[]{:S(2)}) collective-permute-start(f32[8,128]{1,0:T(8,128)S(1)} %add.225), channel_id=1, source_target_pairs={{0,2},{1,3},{2,0},{3,1},{4,6},{5,7},{6,4},{7,5},{8,10},{9,11},{10,... | collective-permute-start | bytes 12296 | tf_op jit(solution)/shard_map/ppermute | solution.py:74
  64.8 1.6 %collective-permute-done.13 = f32[8,128]{1,0:T(8,128)S(1)} collective-permute-done((f32[8,128]{1,0:T(8,128)S(1)}, f32[8,128]{1,0:T(8,128)S(1)}, u32[]{:S(2)}, u32[]{:S(2)}) %collective-permute-start.13) | collective-permute-done | bytes 4128 | tf_op jit(solution)/shard_map/ppermute | solution.py:74
  66.4 3.0 %collective-permute-start.14 = (f32[8,128]{1,0:T(8,128)S(1)}, f32[8,128]{1,0:T(8,128)S(1)}, u32[]{:S(2)}, u32[]{:S(2)}) collective-permute-start(f32[8,128]{1,0:T(8,128)S(1)} %add.226), channel_id=1, source_target_pairs={{0,4},{1,5},{2,6},{3,7},{4,0},{5,1},{6,2},{7,3},{8,12},{9,13},{10,... | collective-permute-start | bytes 12296 | tf_op jit(solution)/shard_map/ppermute | solution.py:74
  69.4 1.6 %collective-permute-done.14 = f32[8,128]{1,0:T(8,128)S(1)} collective-permute-done((f32[8,128]{1,0:T(8,128)S(1)}, f32[8,128]{1,0:T(8,128)S(1)}, u32[]{:S(2)}, u32[]{:S(2)}) %collective-permute-start.14) | collective-permute-done | bytes 4128 | tf_op jit(solution)/shard_map/ppermute | solution.py:74
  71.0 1.7 %collective-permute-start.15 = (f32[8,128]{1,0:T(8,128)S(1)}, f32[8,128]{1,0:T(8,128)S(1)}, u32[]{:S(2)}, u32[]{:S(2)}) collective-permute-start(f32[8,128]{1,0:T(8,128)S(1)} %add.227), channel_id=1, source_target_pairs={{0,8},{8,0},{16,24},{24,16},{1,9},{9,1},{17,25},{25,17},{2,10},{10... | collective-permute-start | bytes 12296 | tf_op jit(solution)/shard_map/ppermute | solution.py:74
  72.7 1.9 %collective-permute-done.15 = f32[8,128]{1,0:T(8,128)S(1)} collective-permute-done((f32[8,128]{1,0:T(8,128)S(1)}, f32[8,128]{1,0:T(8,128)S(1)}, u32[]{:S(2)}, u32[]{:S(2)}) %collective-permute-start.15) | collective-permute-done | bytes 4128 | tf_op jit(solution)/shard_map/ppermute | solution.py:74
  74.6 2.7 %collective-permute-start.16 = (f32[8,128]{1,0:T(8,128)S(1)}, f32[8,128]{1,0:T(8,128)S(1)}, u32[]{:S(2)}, u32[]{:S(2)}) collective-permute-start(f32[8,128]{1,0:T(8,128)S(1)} %add.228), channel_id=1, source_target_pairs={{0,16},{8,24},{16,0},{24,8},{1,17},{9,25},{17,1},{25,9},{2,18},{10... | collective-permute-start | bytes 12296 | tf_op jit(solution)/shard_map/ppermute | solution.py:74
  77.3 1.6 %collective-permute-done.16 = f32[8,128]{1,0:T(8,128)S(1)} collective-permute-done((f32[8,128]{1,0:T(8,128)S(1)}, f32[8,128]{1,0:T(8,128)S(1)}, u32[]{:S(2)}, u32[]{:S(2)}) %collective-permute-start.16) | collective-permute-done | bytes 4128 | tf_op jit(solution)/shard_map/ppermute | solution.py:74
  78.9 0.6 add.229.refs_0_
  79.5 2.8 %shard_map.86 = (f32[5,16,8,512]{3,2,1,0:T(8,128)}, f32[5,5]{1,0:T(8,128)}, f32[1,1]{1,0:T(1,128)}) custom-call(f32[8,128]{1,0:T(8,128)} %add.229.refs_0_, f32[16,8,512]{2,1,0:T(8,128)} %get-tuple-element.34.refs_0_.refs_1_, f32[16,8,512]{2,1,0:T(8,128)} %copy-done.1, f32[16,8,512]{2,1,0:T(8,128)} %get-tuple-element.31.refs_2_.refs_3_, ...), custom_call_target="tpu_custom_call" | custom-call | tf_op jit(solution)/shard_map/pallas_call | solution.py:177
  (25 shorter events, 0.3 us)
Async XLA Ops:
  0.6 3.0 %copy-start.3 = (f32[16,8,512]{2,1,0:T(8,128)S(1)}, f32[16,8,512]{2,1,0:T(8,128)}, u32[]{:S(2)}) copy-start(f32[16,8,512]{2,1,0:T(8,128)} %param.9) | copy-start | bytes 786436
  0.6 3.1 %copy-start.4 = (f32[16,8,512]{2,1,0:T(8,128)S(1)}, f32[16,8,512]{2,1,0:T(8,128)}, u32[]{:S(2)}) copy-start(f32[16,8,512]{2,1,0:T(8,128)} %param.10) | copy-start | bytes 786436
  0.7 3.1 %copy-start.2 = (f32[16,8,512]{2,1,0:T(8,128)S(1)}, f32[16,8,512]{2,1,0:T(8,128)}, u32[]{:S(2)}) copy-start(f32[16,8,512]{2,1,0:T(8,128)} %param.11) | copy-start | bytes 786436
  3.8 7.9 %collective-permute-start = (f32[2,8,3072]{2,1,0:T(8,128)S(1)}, f32[2,8,3072]{2,1,0:T(8,128)S(1)}, u32[]{:S(2)}, u32[]{:S(2)}) collective-permute-start(f32[2,8,3072]{2,1,0:T(8,128)S(1)} %get-tuple-element.24), channel_id=1, source_target_pairs={{0,8},{8,0},{16,24},{24,16},{1,9},{9,1},{17,25},{25,17},{2,10},{10... | collective-permute-start | bytes 589832 | tf_op jit(solution)/shard_map/ppermute | solution.py:29
  6.8 4.9 %collective-permute-start.1 = (f32[2,8,3072]{2,1,0:T(8,128)S(1)}, f32[2,8,3072]{2,1,0:T(8,128)S(1)}, u32[]{:S(2)}, u32[]{:S(2)}) collective-permute-start(f32[2,8,3072]{2,1,0:T(8,128)S(1)} %get-tuple-element.25), channel_id=1, source_target_pairs={{8,16},{16,8},{9,17},{17,9},{10,18},{18,10},{11,19},{19,11},{12,20... | collective-permute-start | bytes 589832 | tf_op jit(solution)/shard_map/ppermute | solution.py:30
  13.9 4.3 %collective-permute-start.3 = (f32[20,2,3072]{2,1,0:T(2,128)}, f32[20,2,3072]{2,1,0:T(2,128)}, u32[]{:S(2)}, u32[]{:S(2)}) collective-permute-start(f32[20,2,3072]{2,1,0:T(2,128)} %bitcast.3), channel_id=1, source_target_pairs={{1,2},{2,1},{3,4},{4,3},{5,6},{6,5},{9,10},{10,9},{11,12},{12,11},... | collective-permute-start | bytes 1474568 | tf_op jit(solution)/shard_map/ppermute | solution.py:30
  15.3 4.4 %collective-permute-start.2 = (f32[20,2,3072]{2,1,0:T(2,128)}, f32[20,2,3072]{2,1,0:T(2,128)}, u32[]{:S(2)}, u32[]{:S(2)}) collective-permute-start(f32[20,2,3072]{2,1,0:T(2,128)} %get-tuple-element.18), channel_id=1, source_target_pairs={{0,1},{1,0},{2,3},{3,2},{4,5},{5,4},{6,7},{7,6},{8,9},{9,8},{10,11... | collective-permute-start | bytes 1474568 | tf_op jit(solution)/shard_map/ppermute | solution.py:29
  24.5 18.6 %copy-start.1 = (f32[16,8,512]{2,1,0:T(8,128)}, f32[16,8,512]{2,1,0:T(8,128)S(1)}, u32[]{:S(2)}) copy-start(f32[16,8,512]{2,1,0:T(8,128)S(1)} %get-tuple-element.12.refs_1_.refs_2_) | copy-start | bytes 786436
  24.5 8.5 %collective-permute-start.4 = (f32[2,8,512]{2,1,0:T(8,128)S(1)}, f32[2,8,512]{2,1,0:T(8,128)S(1)}, u32[]{:S(2)}, u32[]{:S(2)}) collective-permute-start(f32[2,8,512]{2,1,0:T(8,128)S(1)} %get-tuple-element.49), channel_id=1, source_target_pairs={{0,8},{8,0},{16,24},{24,16},{1,9},{9,1},{17,25},{25,17},{2,10},{10... | collective-permute-start | bytes 98312 | tf_op jit(solution)/shard_map/ppermute | solution.py:29
  31.1 1.9 %collective-permute-start.5 = (f32[2,8,512]{2,1,0:T(8,128)S(1)}, f32[2,8,512]{2,1,0:T(8,128)S(1)}, u32[]{:S(2)}, u32[]{:S(2)}) collective-permute-start(f32[2,8,512]{2,1,0:T(8,128)S(1)} %get-tuple-element.50), channel_id=1, source_target_pairs={{8,16},{16,8},{9,17},{17,9},{10,18},{18,10},{11,19},{19,11},{12,20... | collective-permute-start | bytes 98312 | tf_op jit(solution)/shard_map/ppermute | solution.py:30
  33.1 8.6 %collective-permute-start.7 = (f32[20,2,512]{2,1,0:T(2,128)S(1)}, f32[20,2,512]{2,1,0:T(2,128)S(1)}, u32[]{:S(2)}, u32[]{:S(2)}) collective-permute-start(f32[20,2,512]{2,1,0:T(2,128)S(1)} %bitcast.36), channel_id=1, source_target_pairs={{1,2},{2,1},{3,4},{4,3},{5,6},{6,5},{9,10},{10,9},{11,12},{12,11},... | collective-permute-start | bytes 245768 | tf_op jit(solution)/shard_map/ppermute | solution.py:30
  33.8 8.9 %collective-permute-start.6 = (f32[20,2,512]{2,1,0:T(2,128)S(1)}, f32[20,2,512]{2,1,0:T(2,128)S(1)}, u32[]{:S(2)}, u32[]{:S(2)}) collective-permute-start(f32[20,2,512]{2,1,0:T(2,128)S(1)} %get-tuple-element.9), channel_id=1, source_target_pairs={{0,1},{1,0},{2,3},{3,2},{4,5},{5,4},{6,7},{7,6},{8,9},{9,8},{10,11... | collective-permute-start | bytes 245768 | tf_op jit(solution)/shard_map/ppermute | solution.py:29
  45.4 5.8 %copy-start = (f32[16,8,512]{2,1,0:T(8,128)}, f32[16,8,512]{2,1,0:T(8,128)S(1)}, u32[]{:S(2)}) copy-start(f32[16,8,512]{2,1,0:T(8,128)S(1)} %get-tuple-element.30.refs_3_.refs_4_) | copy-start | bytes 786436
  45.6 10.5 %collective-permute-start.8 = (f32[1,8,512]{2,1,0:T(8,128)S(1)}, f32[1,8,512]{2,1,0:T(8,128)S(1)}, u32[]{:S(2)}, u32[]{:S(2)}) collective-permute-start(f32[1,8,512]{2,1,0:T(8,128)S(1)} %get-tuple-element.48), channel_id=1, source_target_pairs={{0,8},{8,0},{16,24},{24,16},{1,9},{9,1},{17,25},{25,17},{2,10},{10... | collective-permute-start | bytes 49160 | tf_op jit(solution)/shard_map/ppermute | solution.py:29
  50.5 5.6 %collective-permute-start.9 = (f32[1,8,512]{2,1,0:T(8,128)S(1)}, f32[1,8,512]{2,1,0:T(8,128)S(1)}, u32[]{:S(2)}, u32[]{:S(2)}) collective-permute-start(f32[1,8,512]{2,1,0:T(8,128)S(1)} %get-tuple-element.47), channel_id=1, source_target_pairs={{8,16},{16,8},{9,17},{17,9},{10,18},{18,10},{11,19},{19,11},{12,20... | collective-permute-start | bytes 49160 | tf_op jit(solution)/shard_map/ppermute | solution.py:30
  51.2 4.9 %collective-permute-start.11 = (f32[16,1,512]{2,1,0:T(1,128)S(1)}, f32[16,1,512]{2,1,0:T(1,128)S(1)}, u32[]{:S(2)}, u32[]{:S(2)}) collective-permute-start(f32[16,1,512]{2,1,0:T(1,128)S(1)} %get-tuple-element.43), channel_id=1, source_target_pairs={{1,2},{2,1},{3,4},{4,3},{5,6},{6,5},{9,10},{10,9},{11,12},{12,11},... | collective-permute-start | bytes 98312 | tf_op jit(solution)/shard_map/ppermute | solution.py:30
  51.9 5.0 %collective-permute-start.10 = (f32[16,1,512]{2,1,0:T(1,128)S(1)}, f32[16,1,512]{2,1,0:T(1,128)S(1)}, u32[]{:S(2)}, u32[]{:S(2)}) collective-permute-start(f32[16,1,512]{2,1,0:T(1,128)S(1)} %get-tuple-element.44), channel_id=1, source_target_pairs={{0,1},{1,0},{2,3},{3,2},{4,5},{5,4},{6,7},{7,6},{8,9},{9,8},{10,11... | collective-permute-start | bytes 98312 | tf_op jit(solution)/shard_map/ppermute | solution.py:29
  60.4 1.7 %collective-permute-start.12 = (f32[8,128]{1,0:T(8,128)}, f32[8,128]{1,0:T(8,128)S(1)}, u32[]{:S(2)}, u32[]{:S(2)}) collective-permute-start(f32[8,128]{1,0:T(8,128)} %shard_map.85), channel_id=1, source_target_pairs={{0,1},{1,0},{2,3},{3,2},{4,5},{5,4},{6,7},{7,6},{8,9},{9,8},{10,11... | collective-permute-start | bytes 12296 | tf_op jit(solution)/shard_map/ppermute | solution.py:74
  62.8 3.6 %collective-permute-start.13 = (f32[8,128]{1,0:T(8,128)S(1)}, f32[8,128]{1,0:T(8,128)S(1)}, u32[]{:S(2)}, u32[]{:S(2)}) collective-permute-start(f32[8,128]{1,0:T(8,128)S(1)} %add.225), channel_id=1, source_target_pairs={{0,2},{1,3},{2,0},{3,1},{4,6},{5,7},{6,4},{7,5},{8,10},{9,11},{10,... | collective-permute-start | bytes 12296 | tf_op jit(solution)/shard_map/ppermute | solution.py:74
  66.4 4.6 %collective-permute-start.14 = (f32[8,128]{1,0:T(8,128)S(1)}, f32[8,128]{1,0:T(8,128)S(1)}, u32[]{:S(2)}, u32[]{:S(2)}) collective-permute-start(f32[8,128]{1,0:T(8,128)S(1)} %add.226), channel_id=1, source_target_pairs={{0,4},{1,5},{2,6},{3,7},{4,0},{5,1},{6,2},{7,3},{8,12},{9,13},{10,... | collective-permute-start | bytes 12296 | tf_op jit(solution)/shard_map/ppermute | solution.py:74
  71.0 3.6 %collective-permute-start.15 = (f32[8,128]{1,0:T(8,128)S(1)}, f32[8,128]{1,0:T(8,128)S(1)}, u32[]{:S(2)}, u32[]{:S(2)}) collective-permute-start(f32[8,128]{1,0:T(8,128)S(1)} %add.227), channel_id=1, source_target_pairs={{0,8},{8,0},{16,24},{24,16},{1,9},{9,1},{17,25},{25,17},{2,10},{10... | collective-permute-start | bytes 12296 | tf_op jit(solution)/shard_map/ppermute | solution.py:74
  74.6 4.3 %collective-permute-start.16 = (f32[8,128]{1,0:T(8,128)S(1)}, f32[8,128]{1,0:T(8,128)S(1)}, u32[]{:S(2)}, u32[]{:S(2)}) collective-permute-start(f32[8,128]{1,0:T(8,128)S(1)} %add.228), channel_id=1, source_target_pairs={{0,16},{8,24},{16,0},{24,8},{1,17},{9,25},{17,1},{25,9},{2,18},{10... | collective-permute-start | bytes 12296 | tf_op jit(solution)/shard_map/ppermute | solution.py:74

commit v8 on v7

--- a/solution.py
+++ b/solution.py
@@ -187,11 +187,21 @@
     return ortho, upper, scale.reshape(())
 
 
-def wide_exchange(block, depth):
-    from_low, from_high = axis_exchange(block[:depth], block[-depth:], "gx")
-    block = jnp.concatenate([from_low, block, from_high], axis=0)
-    from_low, from_high = axis_exchange(block[:, :depth], block[:, -depth:], "gy")
-    return jnp.concatenate([from_low, block, from_high], axis=1)
+def wide_exchange(blocks, depth):
+    lanes = blocks[0].shape[-1]
+
+    def edges(parts, dim):
+        low = jnp.concatenate([lax.slice_in_dim(p, 0, depth, axis=dim) for p in parts], axis=-1)
+        high = jnp.concatenate([lax.slice_in_dim(p, p.shape[dim] - depth, None, axis=dim) for p in parts], axis=-1)
+        return low, high
+
+    for axis, dim in (("gx", 0), ("gy", 1)):
+        from_low, from_high = axis_exchange(*edges(blocks, dim), axis)
+        blocks = [
+            jnp.concatenate([from_low[..., k * lanes : (k + 1) * lanes], b, from_high[..., k * lanes : (k + 1) * lanes]], axis=dim)
+            for k, b in enumerate(blocks)
+        ]
+    return blocks
 
 
 def shrink_sum(u, coef):
@@ -212,8 +222,7 @@
     depth = 2
 
     inputs = (start_field, right_side, accumulation, trans_x, trans_y, trans_z)
-    wide = wide_exchange(jnp.concatenate(inputs, axis=-1), depth)
-    field, rhs, acc, t_x, t_y, t_z = (wide[..., k * size_z : (k + 1) * size_z] for k in range(len(inputs)))
+    field, rhs, acc, t_x, t_y, t_z = wide_exchange(inputs, depth)
 
     first_x = lax.axis_index("gx") * size_x - depth
     first_y = lax.axis_index("gy") * size_y - depth
@@ -244,7 +253,7 @@
 
     basis = [residual0[1:-1, 1:-1]]
     basis.append(2.0 * shrink_sum(residual0, centre) / diag)
-    vector = jnp.where(inside(1), 2.0 * shrink_sum(wide_exchange(basis[1], depth), ring) / diag_ring, 0.0)
+    vector = jnp.where(inside(1), 2.0 * shrink_sum(wide_exchange([basis[1]], depth)[0], ring) / diag_ring, 0.0)
     basis.append(vector[1:-1, 1:-1])
     basis.append(2.0 * shrink_sum(vector, centre) / diag)
     basis.append(2.0 * neighbour_sum(basis[3], field_halo(basis[3]), centre) / diag)

time: 82.7 us -> 86.9 us (1.051)
  local copies, waits for them, and re-layouts: 4.45 us -> 8.15 us
  waiting for transfers between devices: 16.5 us -> 17.8 us
  other arithmetic: 11.2 us -> 10.2 us
    ppermute x5, starting transfers between devices: 10.1 us -> 6.64 us  [all_sum(): x = x + lax.ppermute(x, axis, [(i, i ^ step) for i in range(n)])]
    ppermute x6, starting transfers between devices: 29.2 us -> 32.2 us  [axis_exchange(): lax.ppermute(jnp.where(odd, to_low, to_high), axis, swap_pairs(axis, 0))]
    unnamed x15 -> x41, local copies, waits for them, and re-layouts: 3.04 us -> 5.82 us
    ppermute x5, waiting for transfers between devices: 7.71 us -> 10.4 us  [all_sum(): x = x + lax.ppermute(x, axis, [(i, i ^ step) for i in range(n)])]
    ppermute x6, waiting for transfers between devices: 8.79 us -> 7.34 us  [axis_exchange(): lax.ppermute(jnp.where(odd, to_low, to_high), axis, swap_pairs(axis, 0))]
    select_n x4, other arithmetic: 1.35 us -> 0.18 us  [axis_exchange(): jnp.where(odd, to_low, to_high)]
    select_n x1, other arithmetic: 1.09 us -> 2.25 us  [local(): residual0 = jnp.where(inside(1), residual0, 0.0)]
where the time goes in v8:
time: 86.9 us; the launch traced here: 86 us
  starting transfers between devices  43.6 us (50%)
  waiting for transfers between devices  17.8 us (20%)
  other arithmetic  10.2 us (12%)
  local copies, waits for them, and re-layouts  8.15 us (9%)
  Pallas kernels  5.06 us (6%)
  between operations  1.18 us (1%)
    ppermute x6, starting transfers between devices, axis_exchange(): lax.ppermute(jnp.where(odd, to_low, to_high), axis, swap_pairs(axis, 0))  32.2 us
    ppermute x5, waiting for transfers between devices, all_sum(): x = x + lax.ppermute(x, axis, [(i, i ^ step) for i in range(n)])  10.4 us
    ppermute x6, waiting for transfers between devices, axis_exchange(): lax.ppermute(jnp.where(odd, to_low, to_high), axis, swap_pairs(axis, 0))  7.34 us
    ppermute x5, starting transfers between devices, all_sum(): x = x + lax.ppermute(x, axis, [(i, i ^ step) for i in range(n)])  6.64 us
    unnamed x41, local copies, waits for them, and re-layouts  5.82 us
    ppermute x6, starting transfers between devices, axis_exchange(): lax.ppermute(jnp.where(odd, to_high, to_low), axis, swap_pairs(axis, 1))  4.78 us
    pallas_call x1, Pallas kernels, finish(): pl.pallas_call(lambda *refs: finish_kernel(float(cells), size, *refs), ou...  2.75 us
    pallas_call x1, Pallas kernels, gram(): pl.pallas_call(lambda *refs: gram_kernel(size, *refs), out_shape=jax.Shap...  2.31 us
  transfers between devices with their start and end apart: 17, of which 10 were waited for; matrix products, arithmetic and copies ran while one was open for 0% of the time, Pallas kernels for 0%

profile of v8, /device:TPU:0, one launch (start us, length us, event | category | flops | bytes accessed | tf_op | source)
XLA Modules:
  0.0 86.0 jit_solution(11266692711773780055)
XLA Ops:
  0.6 0.8 constant_dynamic-update-slice_fusion.5
  1.4 0.8 constant_dynamic-update-slice_fusion.4
  2.2 0.8 constant_dynamic-update-slice_fusion.3
  3.0 0.8 constant_dynamic-update-slice_fusion.2
  3.8 0.8 constant_dynamic-update-slice_fusion.1
  4.6 0.8 constant_dynamic-update-slice_fusion
  5.4 3.0 %collective-permute-start = (f32[2,8,3072]{2,1,0:T(8,128)S(1)}, f32[2,8,3072]{2,1,0:T(8,128)S(1)}, u32[]{:S(2)}, u32[]{:S(2)}) collective-permute-start(f32[2,8,3072]{2,1,0:T(8,128)S(1)} %get-tuple-element.44), channel_id=1, source_target_pairs={{0,8},{8,0},{16,24},{24,16},{1,9},{9,1},{17,25},{25,17},{2,10},{10... | collective-permute-start | bytes 589832 | tf_op jit(solution)/shard_map/ppermute | solution.py:29
  8.4 0.7 collective-permute-start.1
  9.1 4.2 %collective-permute-done = f32[2,8,3072]{2,1,0:T(8,128)S(1)} collective-permute-done((f32[2,8,3072]{2,1,0:T(8,128)S(1)}, f32[2,8,3072]{2,1,0:T(8,128)S(1)}, u32[]{:S(2)}, u32[]{:S(2)}) %collective-permute-start) | collective-permute-done | bytes 196640 | tf_op jit(solution)/shard_map/ppermute | solution.py:29
  13.6 0.1 maximum_dynamic-update-slice_fusion.4
  13.6 0.1 maximum_dynamic-update-slice_fusion.3
  13.7 0.6 copy-done.4
  14.3 0.1 maximum_dynamic-update-slice_fusion.2
  14.4 0.1 copy-done.1
  14.7 0.1 broadcast_select_fusion.3
  14.7 0.1 collective-permute-start.2
  14.8 1.5 %collective-permute-start.3 = (f32[20,2,3072]{2,1,0:T(2,128)S(1)}, f32[20,2,3072]{2,1,0:T(2,128)}, u32[]{:S(2)}, u32[]{:S(2)}) collective-permute-start(f32[20,2,3072]{2,1,0:T(2,128)S(1)} %bitcast.29), channel_id=1, source_target_pairs={{1,2},{2,1},{3,4},{4,3},{5,6},{6,5},{9,10},{10,9},{11,12},{12,11},... | collective-permute-start | bytes 1474568 | tf_op jit(solution)/shard_map/ppermute | solution.py:30
  16.3 0.1 slice.394
  16.5 0.1 and_and_fusion
  16.5 0.1 collective-permute-done.2
  16.7 1.1 %broadcast_select_fusion.1 = (f32[5,8,3072]{2,1,0:T(8,128)S(1)}, f32[5,8,3072]{2,1,0:T(8,128)S(1)}) fusion(f32[5,8,3072]{2,1,0:T(8,128)S(1)} %bitcast.28, f32[5,8,3072]{2,1,0:T(8,128)} %bitcast.6, pred[]{:T(512)S(6)} %eq.17), kind=kLoop, calls=%fused_computation.61 | loop fusion | flops 245760 | bytes 1966081 | tf_op jit(solution)/shard_map/jit(_where)/select_n | solution.py:31
  17.9 0.7 copy-done.15
  18.6 0.1 pad_maximum_fusion.2
  18.7 0.2 slice.450
  18.9 0.1 pad_maximum_fusion.1
  19.0 0.1 pad_maximum_fusion.3
  19.2 0.3 fusion.58
  19.5 0.4 copy-done.13
  19.9 0.1 pad_maximum_fusion
  20.1 2.2 %fusion.15 = (f32[18,10,512]{2,1,0:T(8,128)S(1)}, f32[18,10,512]{2,1,0:T(8,128)S(1)}) fusion(f32[20,2,512]{2,1,0:T(2,128)S(1)} %get-tuple-element.37, f32[2,8,512]{2,1,0:T(8,128)S(1)} %get-tuple-element.102, f32[16,8,512]{2,1,0:T(8,128)S(1)} %copy-done.5, f32[2,8,512]{2,1,0:T(8,128)S(1)} %get-tuple-element.87, f32[20,2,512]{2,1,0:T(2,128)S(1)} %get-tuple-element.31, ...), kind=kLoop, calls=%fused_computation.29 | loop fusion | flops 3594240 | bytes 6387780 | tf_op jit(solution)/shard_map/jit(_where)/select_n | solution.py:252
  22.3 0.1 fusion.60
  22.5 1.1 %fusion.37 = (f32[16,8,512]{2,1,0:T(8,128)S(1)}, f32[16,8,512]{2,1,0:T(8,128)}) fusion(f32[18,10,512]{2,1,0:T(8,128)S(1)} %get-tuple-element.12, f32[16,8,512]{2,1,0:T(8,128)S(1)} %copy-done.1, f32[2,8,512]{2,1,0:T(8,128)S(1)} %get-tuple-element.105, f32[16,8,512]{2,1,0:T(8,128)S(1)} %copy-done.4, f32[16,8,511]{2,1,0:T(8,128)S(1)} %get-tuple-element.29, ...), kind=kLoop, calls=%fused_computation.80 | loop fusion | flops 1114112 | bytes 3848704 | tf_op jit(solution)/shard_map/div | solution.py:255
  23.5 7.0 %collective-permute-start.4 = (f32[2,8,512]{2,1,0:T(8,128)S(1)}, f32[2,8,512]{2,1,0:T(8,128)S(1)}, u32[]{:S(2)}, u32[]{:S(2)}) collective-permute-start(f32[2,8,512]{2,1,0:T(8,128)S(1)} %get-tuple-element.68), channel_id=1, source_target_pairs={{0,8},{8,0},{16,24},{24,16},{1,9},{9,1},{17,25},{25,17},{2,10},{10... | collective-permute-start | bytes 98312 | tf_op jit(solution)/shard_map/ppermute | solution.py:29
  30.5 0.7 collective-permute-start.5
  31.2 1.2 %collective-permute-done.4 = f32[2,8,512]{2,1,0:T(8,128)S(1)} collective-permute-done((f32[2,8,512]{2,1,0:T(8,128)S(1)}, f32[2,8,512]{2,1,0:T(8,128)S(1)}, u32[]{:S(2)}, u32[]{:S(2)}) %collective-permute-start.4) | collective-permute-done | bytes 32800 | tf_op jit(solution)/shard_map/ppermute | solution.py:29
  32.4 0.1 broadcast_select_fusion.11
  32.5 0.7 collective-permute-start.7
  33.2 11.5 %collective-permute-start.6 = (f32[20,2,512]{2,1,0:T(2,128)S(1)}, f32[20,2,512]{2,1,0:T(2,128)S(1)}, u32[]{:S(2)}, u32[]{:S(2)}) collective-permute-start(f32[20,2,512]{2,1,0:T(2,128)S(1)} %get-tuple-element.9), channel_id=1, source_target_pairs={{0,1},{1,0},{2,3},{3,2},{4,5},{5,4},{6,7},{7,6},{8,9},{9,8},{10,11... | collective-permute-start | bytes 245768 | tf_op jit(solution)/shard_map/ppermute | solution.py:29
  44.7 0.9 %collective-permute-done.6 = f32[20,2,512]{2,1,0:T(2,128)S(1)} collective-permute-done((f32[20,2,512]{2,1,0:T(2,128)S(1)}, f32[20,2,512]{2,1,0:T(2,128)S(1)}, u32[]{:S(2)}, u32[]{:S(2)}) %collective-permute-start.6) | collective-permute-done | bytes 81952 | tf_op jit(solution)/shard_map/ppermute | solution.py:29
  45.7 0.1 pad_maximum_fusion.4
  45.8 0.3 fusion.57
  46.1 1.0 %fusion.25 = f32[18,10,512]{2,1,0:T(8,128)S(1)} fusion(f32[18,10,512]{2,1,0:T(8,128)S(1)} %get-tuple-element.13, f32[18,10,511]{2,1,0:T(8,128)S(1)} %get-tuple-element.19, f32[18,10,511]{2,1,0:T(8,128)S(1)} %get-tuple-element.18, f32[20,2,512]{2,1,0:T(2,128)S(1)} %bitcast.25, f32[2,8,512]{2,1,0:T(8,128)S(1)} %get-tuple-element.99, ...), kind=kLoop, calls=%fused_computation.59 | loop fusion | flops 2211840 | bytes 5036100 | tf_op jit(solution)/shard_map/jit(_where)/select_n | solution.py:256
  47.1 0.1 fusion.59
  47.2 1.0 %fusion.30 = (f32[16,8,512]{2,1,0:T(8,128)S(1)}, f32[16,8,512]{2,1,0:T(8,128)}) fusion(f32[18,10,512]{2,1,0:T(8,128)S(1)} %fusion.25, f32[16,8,512]{2,1,0:T(8,128)S(1)} %copy-done.1, f32[16,8,512]{2,1,0:T(8,128)S(1)} %copy-done.4, f32[2,8,512]{2,1,0:T(8,128)S(1)} %get-tuple-element.105, f32[16,8,511]{2,1,0:T(8,128)S(1)} %get-tuple-element.25, ...), kind=kLoop, calls=%fused_computation.69 | loop fusion | flops 1114112 | bytes 3848704 | tf_op jit(solution)/shard_map/div | solution.py:258
  48.3 0.1 fusion.63
  48.5 0.7 collective-permute-start.9
  49.2 6.5 %collective-permute-start.8 = (f32[1,8,512]{2,1,0:T(8,128)S(1)}, f32[1,8,512]{2,1,0:T(8,128)S(1)}, u32[]{:S(2)}, u32[]{:S(2)}) collective-permute-start(f32[1,8,512]{2,1,0:T(8,128)S(1)} %get-tuple-element.67), channel_id=1, source_target_pairs={{0,8},{8,0},{16,24},{24,16},{1,9},{9,1},{17,25},{25,17},{2,10},{10... | collective-permute-start | bytes 49160 | tf_op jit(solution)/shard_map/ppermute | solution.py:29
  55.7 0.7 collective-permute-start.11
  56.4 4.2 %collective-permute-start.10 = (f32[16,1,512]{2,1,0:T(1,128)S(1)}, f32[16,1,512]{2,1,0:T(1,128)S(1)}, u32[]{:S(2)}, u32[]{:S(2)}) collective-permute-start(f32[16,1,512]{2,1,0:T(1,128)S(1)} %get-tuple-element.63), channel_id=1, source_target_pairs={{0,1},{1,0},{2,3},{3,2},{4,5},{5,4},{6,7},{7,6},{8,9},{9,8},{10,11... | collective-permute-start | bytes 98312 | tf_op jit(solution)/shard_map/ppermute | solution.py:29
  60.6 0.8 collective-permute-done.10
  61.4 1.1 %fusion.47.refs_4_.refs_5_ = f32[16,8,512]{2,1,0:T(8,128)} fusion(f32[2,8,512]{2,1,0:T(8,128)S(1)} %get-tuple-element.105, f32[16,8,512]{2,1,0:T(8,128)S(1)} %copy-done.4, f32[15,8,512]{2,1,0:T(8,128)S(1)} %get-tuple-element.65, f32[1,8,512]{2,1,0:T(8,128)S(1)} %get-tuple-element.101, f32[1,8,512]{2,1,0:T(8,128)S(1)} %get-tuple-element.100, ...), kind=kLoop, calls=%fused_computation.94 | loop fusion | flops 1376256 | bytes 3324416 | tf_op jit(solution)/shard_map/div | solution.py:259
  62.6 2.3 %shard_map.85 = f32[8,128]{1,0:T(8,128)} custom-call(f32[16,8,512]{2,1,0:T(8,128)} %get-tuple-element.27.refs_0_.refs_1_, f32[16,8,512]{2,1,0:T(8,128)} %copy-done.2, f32[16,8,512]{2,1,0:T(8,128)} %get-tuple-element.23.refs_2_.refs_3_, f32[16,8,512]{2,1,0:T(8,128)} %copy-done, f32[16,8,512]{2,1,0:T(8,128)} %fusion.47.refs_4_.refs_5_), custom_call_target="tpu_custom_call" | custom-call | tf_op jit(solution)/shard_map/pallas_call | solution.py:111
  64.9 0.7 collective-permute-start.12
  65.5 1.0 %collective-permute-done.12 = f32[8,128]{1,0:T(8,128)S(1)} collective-permute-done((f32[8,128]{1,0:T(8,128)}, f32[8,128]{1,0:T(8,128)S(1)}, u32[]{:S(2)}, u32[]{:S(2)}) %collective-permute-start.12) | collective-permute-done | bytes 4128 | tf_op jit(solution)/shard_map/ppermute | solution.py:74
  66.6 0.7 add.225
  67.3 2.0 %collective-permute-start.13 = (f32[8,128]{1,0:T(8,128)S(1)}, f32[8,128]{1,0:T(8,128)S(1)}, u32[]{:S(2)}, u32[]{:S(2)}) collective-permute-start(f32[8,128]{1,0:T(8,128)S(1)} %add.225), channel_id=1, source_target_pairs={{0,2},{1,3},{2,0},{3,1},{4,6},{5,7},{6,4},{7,5},{8,10},{9,11},{10,... | collective-permute-start | bytes 12296 | tf_op jit(solution)/shard_map/ppermute | solution.py:74
  69.2 1.6 %collective-permute-done.13 = f32[8,128]{1,0:T(8,128)S(1)} collective-permute-done((f32[8,128]{1,0:T(8,128)S(1)}, f32[8,128]{1,0:T(8,128)S(1)}, u32[]{:S(2)}, u32[]{:S(2)}) %collective-permute-start.13) | collective-permute-done | bytes 4128 | tf_op jit(solution)/shard_map/ppermute | solution.py:74
  70.9 3.0 %collective-permute-start.14 = (f32[8,128]{1,0:T(8,128)S(1)}, f32[8,128]{1,0:T(8,128)S(1)}, u32[]{:S(2)}, u32[]{:S(2)}) collective-permute-start(f32[8,128]{1,0:T(8,128)S(1)} %add.226), channel_id=1, source_target_pairs={{0,4},{1,5},{2,6},{3,7},{4,0},{5,1},{6,2},{7,3},{8,12},{9,13},{10,... | collective-permute-start | bytes 12296 | tf_op jit(solution)/shard_map/ppermute | solution.py:74
  73.8 1.6 %collective-permute-done.14 = f32[8,128]{1,0:T(8,128)S(1)} collective-permute-done((f32[8,128]{1,0:T(8,128)S(1)}, f32[8,128]{1,0:T(8,128)S(1)}, u32[]{:S(2)}, u32[]{:S(2)}) %collective-permute-start.14) | collective-permute-done | bytes 4128 | tf_op jit(solution)/shard_map/ppermute | solution.py:74
  75.5 3.6 %collective-permute-done.15 = f32[8,128]{1,0:T(8,128)S(1)} collective-permute-done((f32[8,128]{1,0:T(8,128)S(1)}, f32[8,128]{1,0:T(8,128)S(1)}, u32[]{:S(2)}, u32[]{:S(2)}) %collective-permute-start.15) | collective-permute-done | bytes 4128 | tf_op jit(solution)/shard_map/ppermute | solution.py:74
  79.0 1.0 %collective-permute-start.16 = (f32[8,128]{1,0:T(8,128)S(1)}, f32[8,128]{1,0:T(8,128)S(1)}, u32[]{:S(2)}, u32[]{:S(2)}) collective-permute-start(f32[8,128]{1,0:T(8,128)S(1)} %add.228), channel_id=1, source_target_pairs={{0,16},{8,24},{16,0},{24,8},{1,17},{9,25},{17,1},{25,9},{2,18},{10... | collective-permute-start | bytes 12296 | tf_op jit(solution)/shard_map/ppermute | solution.py:74
  80.1 2.6 %collective-permute-done.16 = f32[8,128]{1,0:T(8,128)S(1)} collective-permute-done((f32[8,128]{1,0:T(8,128)S(1)}, f32[8,128]{1,0:T(8,128)S(1)}, u32[]{:S(2)}, u32[]{:S(2)}) %collective-permute-start.16) | collective-permute-done | bytes 4128 | tf_op jit(solution)/shard_map/ppermute | solution.py:74
  82.7 0.6 add.229.refs_0_
  83.2 2.8 %shard_map.86 = (f32[5,16,8,512]{3,2,1,0:T(8,128)}, f32[5,5]{1,0:T(8,128)}, f32[1,1]{1,0:T(1,128)}) custom-call(f32[8,128]{1,0:T(8,128)} %add.229.refs_0_, f32[16,8,512]{2,1,0:T(8,128)} %get-tuple-element.27.refs_0_.refs_1_, f32[16,8,512]{2,1,0:T(8,128)} %copy-done.2, f32[16,8,512]{2,1,0:T(8,128)} %get-tuple-element.23.refs_2_.refs_3_, ...), custom_call_target="tpu_custom_call" | custom-call | tf_op jit(solution)/shard_map/pallas_call | solution.py:177
  (63 shorter events, 0.7 us)
Async XLA Ops:
  3.8 9.7 %copy-start.5 = (f32[16,8,512]{2,1,0:T(8,128)S(1)}, f32[16,8,512]{2,1,0:T(8,128)}, u32[]{:S(2)}) copy-start(f32[16,8,512]{2,1,0:T(8,128)} %param.6) | copy-start | bytes 786436
  5.4 8.2 %copy-start.6 = (f32[16,8,512]{2,1,0:T(8,128)S(1)}, f32[16,8,512]{2,1,0:T(8,128)}, u32[]{:S(2)}) copy-start(f32[16,8,512]{2,1,0:T(8,128)} %param.7) | copy-start | bytes 786436
  5.4 8.2 %copy-start.7 = (f32[16,8,512]{2,1,0:T(8,128)S(1)}, f32[16,8,512]{2,1,0:T(8,128)}, u32[]{:S(2)}) copy-start(f32[16,8,512]{2,1,0:T(8,128)} %param.8) | copy-start | bytes 786436
  5.4 7.9 %collective-permute-start = (f32[2,8,3072]{2,1,0:T(8,128)S(1)}, f32[2,8,3072]{2,1,0:T(8,128)S(1)}, u32[]{:S(2)}, u32[]{:S(2)}) collective-permute-start(f32[2,8,3072]{2,1,0:T(8,128)S(1)} %get-tuple-element.44), channel_id=1, source_target_pairs={{0,8},{8,0},{16,24},{24,16},{1,9},{9,1},{17,25},{25,17},{2,10},{10... | collective-permute-start | bytes 589832 | tf_op jit(solution)/shard_map/ppermute | solution.py:29
  8.4 4.9 %collective-permute-start.1 = (f32[2,8,3072]{2,1,0:T(8,128)S(1)}, f32[2,8,3072]{2,1,0:T(8,128)S(1)}, u32[]{:S(2)}, u32[]{:S(2)}) collective-permute-start(f32[2,8,3072]{2,1,0:T(8,128)S(1)} %get-tuple-element.45), channel_id=1, source_target_pairs={{8,16},{16,8},{9,17},{17,9},{10,18},{18,10},{11,19},{19,11},{12,20... | collective-permute-start | bytes 589832 | tf_op jit(solution)/shard_map/ppermute | solution.py:30
  13.4 1.0 %copy-start.4 = (f32[16,8,512]{2,1,0:T(8,128)S(1)}, f32[16,8,512]{2,1,0:T(8,128)}, u32[]{:S(2)}) copy-start(f32[16,8,512]{2,1,0:T(8,128)} %param.9) | copy-start | bytes 786436
  13.4 1.1 %copy-start.1 = (f32[16,8,512]{2,1,0:T(8,128)S(1)}, f32[16,8,512]{2,1,0:T(8,128)}, u32[]{:S(2)}) copy-start(f32[16,8,512]{2,1,0:T(8,128)} %param.10) | copy-start | bytes 786436
  13.4 1.2 %copy-start.8 = (f32[2,8,512]{2,1,0:T(8,128)}, f32[2,8,512]{2,1,0:T(8,128)S(1)}, u32[]{:S(2)}) copy-start(f32[2,8,512]{2,1,0:T(8,128)S(1)} %get-tuple-element.103) | copy-start | bytes 98308
  13.4 1.2 %copy-start.10 = (f32[2,8,512]{2,1,0:T(8,128)}, f32[2,8,512]{2,1,0:T(8,128)S(1)}, u32[]{:S(2)}) copy-start(f32[2,8,512]{2,1,0:T(8,128)S(1)} %get-tuple-element.104) | copy-start | bytes 98308
  13.4 1.2 %copy-start.12 = (f32[2,8,512]{2,1,0:T(8,128)}, f32[2,8,512]{2,1,0:T(8,128)S(1)}, u32[]{:S(2)}) copy-start(f32[2,8,512]{2,1,0:T(8,128)S(1)} %get-tuple-element.84) | copy-start | bytes 98308
  13.5 1.2 %copy-start.14 = (f32[2,8,512]{2,1,0:T(8,128)}, f32[2,8,512]{2,1,0:T(8,128)S(1)}, u32[]{:S(2)}) copy-start(f32[2,8,512]{2,1,0:T(8,128)S(1)} %get-tuple-element.82) | copy-start | bytes 98308
  13.5 1.2 %copy-start.16 = (f32[2,8,512]{2,1,0:T(8,128)}, f32[2,8,512]{2,1,0:T(8,128)S(1)}, u32[]{:S(2)}) copy-start(f32[2,8,512]{2,1,0:T(8,128)S(1)} %get-tuple-element.107) | copy-start | bytes 98308
  13.5 1.1 %copy-start.3 = (f32[16,8,512]{2,1,0:T(8,128)S(1)}, f32[16,8,512]{2,1,0:T(8,128)}, u32[]{:S(2)}) copy-start(f32[16,8,512]{2,1,0:T(8,128)} %param.11) | copy-start | bytes 786436
  14.7 1.9 %collective-permute-start.2 = (f32[20,2,3072]{2,1,0:T(2,128)S(1)}, f32[20,2,3072]{2,1,0:T(2,128)S(1)}, u32[]{:S(2)}, u32[]{:S(2)}) collective-permute-start(f32[20,2,3072]{2,1,0:T(2,128)S(1)} %bitcast.30), channel_id=1, source_target_pairs={{0,1},{1,0},{2,3},{3,2},{4,5},{5,4},{6,7},{7,6},{8,9},{9,8},{10,11... | collective-permute-start | bytes 1474568 | tf_op jit(solution)/shard_map/ppermute | solution.py:29
  14.8 1.9 %collective-permute-start.3 = (f32[20,2,3072]{2,1,0:T(2,128)S(1)}, f32[20,2,3072]{2,1,0:T(2,128)}, u32[]{:S(2)}, u32[]{:S(2)}) collective-permute-start(f32[20,2,3072]{2,1,0:T(2,128)S(1)} %bitcast.29), channel_id=1, source_target_pairs={{1,2},{2,1},{3,4},{4,3},{5,6},{6,5},{9,10},{10,9},{11,12},{12,11},... | collective-permute-start | bytes 1474568 | tf_op jit(solution)/shard_map/ppermute | solution.py:30
  17.8 0.8 copy-start.15
  17.8 0.8 copy-start.17
  19.2 0.8 copy-start.13
  19.2 0.9 %copy-start.9 = (f32[2,8,512]{2,1,0:T(8,128)S(1)}, f32[2,8,512]{2,1,0:T(8,128)}, u32[]{:S(2)}) copy-start(f32[2,8,512]{2,1,0:T(8,128)} %copy-done.8) | copy-start | bytes 98308
  19.2 0.9 %copy-start.11 = (f32[2,8,512]{2,1,0:T(8,128)S(1)}, f32[2,8,512]{2,1,0:T(8,128)}, u32[]{:S(2)}) copy-start(f32[2,8,512]{2,1,0:T(8,128)} %copy-done.10) | copy-start | bytes 98308
  23.5 22.6 %copy-start.2 = (f32[16,8,512]{2,1,0:T(8,128)}, f32[16,8,512]{2,1,0:T(8,128)S(1)}, u32[]{:S(2)}) copy-start(f32[16,8,512]{2,1,0:T(8,128)S(1)} %get-tuple-element.26.refs_1_.refs_2_) | copy-start | bytes 786436
  23.5 8.9 %collective-permute-start.4 = (f32[2,8,512]{2,1,0:T(8,128)S(1)}, f32[2,8,512]{2,1,0:T(8,128)S(1)}, u32[]{:S(2)}, u32[]{:S(2)}) collective-permute-start(f32[2,8,512]{2,1,0:T(8,128)S(1)} %get-tuple-element.68), channel_id=1, source_target_pairs={{0,8},{8,0},{16,24},{24,16},{1,9},{9,1},{17,25},{25,17},{2,10},{10... | collective-permute-start | bytes 98312 | tf_op jit(solution)/shard_map/ppermute | solution.py:29
  30.5 1.9 %collective-permute-start.5 = (f32[2,8,512]{2,1,0:T(8,128)S(1)}, f32[2,8,512]{2,1,0:T(8,128)S(1)}, u32[]{:S(2)}, u32[]{:S(2)}) collective-permute-start(f32[2,8,512]{2,1,0:T(8,128)S(1)} %get-tuple-element.69), channel_id=1, source_target_pairs={{8,16},{16,8},{9,17},{17,9},{10,18},{18,10},{11,19},{19,11},{12,20... | collective-permute-start | bytes 98312 | tf_op jit(solution)/shard_map/ppermute | solution.py:30
  32.5 12.2 %collective-permute-start.7 = (f32[20,2,512]{2,1,0:T(2,128)S(1)}, f32[20,2,512]{2,1,0:T(2,128)S(1)}, u32[]{:S(2)}, u32[]{:S(2)}) collective-permute-start(f32[20,2,512]{2,1,0:T(2,128)S(1)} %bitcast.37), channel_id=1, source_target_pairs={{1,2},{2,1},{3,4},{4,3},{5,6},{6,5},{9,10},{10,9},{11,12},{12,11},... | collective-permute-start | bytes 245768 | tf_op jit(solution)/shard_map/ppermute | solution.py:30
  33.2 12.5 %collective-permute-start.6 = (f32[20,2,512]{2,1,0:T(2,128)S(1)}, f32[20,2,512]{2,1,0:T(2,128)S(1)}, u32[]{:S(2)}, u32[]{:S(2)}) collective-permute-start(f32[20,2,512]{2,1,0:T(2,128)S(1)} %get-tuple-element.9), channel_id=1, source_target_pairs={{0,1},{1,0},{2,3},{3,2},{4,5},{5,4},{6,7},{7,6},{8,9},{9,8},{10,11... | collective-permute-start | bytes 245768 | tf_op jit(solution)/shard_map/ppermute | solution.py:29
  48.3 7.4 %copy-start = (f32[16,8,512]{2,1,0:T(8,128)}, f32[16,8,512]{2,1,0:T(8,128)S(1)}, u32[]{:S(2)}) copy-start(f32[16,8,512]{2,1,0:T(8,128)S(1)} %get-tuple-element.22.refs_3_.refs_4_) | copy-start | bytes 786436
  48.5 12.0 %collective-permute-start.9 = (f32[1,8,512]{2,1,0:T(8,128)S(1)}, f32[1,8,512]{2,1,0:T(8,128)S(1)}, u32[]{:S(2)}, u32[]{:S(2)}) collective-permute-start(f32[1,8,512]{2,1,0:T(8,128)S(1)} %get-tuple-element.66), channel_id=1, source_target_pairs={{8,16},{16,8},{9,17},{17,9},{10,18},{18,10},{11,19},{19,11},{12,20... | collective-permute-start | bytes 49160 | tf_op jit(solution)/shard_map/ppermute | solution.py:30
  49.2 11.4 %collective-permute-start.8 = (f32[1,8,512]{2,1,0:T(8,128)S(1)}, f32[1,8,512]{2,1,0:T(8,128)S(1)}, u32[]{:S(2)}, u32[]{:S(2)}) collective-permute-start(f32[1,8,512]{2,1,0:T(8,128)S(1)} %get-tuple-element.67), channel_id=1, source_target_pairs={{0,8},{8,0},{16,24},{24,16},{1,9},{9,1},{17,25},{25,17},{2,10},{10... | collective-permute-start | bytes 49160 | tf_op jit(solution)/shard_map/ppermute | solution.py:29
  55.7 4.9 %collective-permute-start.11 = (f32[16,1,512]{2,1,0:T(1,128)S(1)}, f32[16,1,512]{2,1,0:T(1,128)S(1)}, u32[]{:S(2)}, u32[]{:S(2)}) collective-permute-start(f32[16,1,512]{2,1,0:T(1,128)S(1)} %get-tuple-element.62), channel_id=1, source_target_pairs={{1,2},{2,1},{3,4},{4,3},{5,6},{6,5},{9,10},{10,9},{11,12},{12,11},... | collective-permute-start | bytes 98312 | tf_op jit(solution)/shard_map/ppermute | solution.py:30
  56.4 5.0 %collective-permute-start.10 = (f32[16,1,512]{2,1,0:T(1,128)S(1)}, f32[16,1,512]{2,1,0:T(1,128)S(1)}, u32[]{:S(2)}, u32[]{:S(2)}) collective-permute-start(f32[16,1,512]{2,1,0:T(1,128)S(1)} %get-tuple-element.63), channel_id=1, source_target_pairs={{0,1},{1,0},{2,3},{3,2},{4,5},{5,4},{6,7},{7,6},{8,9},{9,8},{10,11... | collective-permute-start | bytes 98312 | tf_op jit(solution)/shard_map/ppermute | solution.py:29
  64.9 1.7 %collective-permute-start.12 = (f32[8,128]{1,0:T(8,128)}, f32[8,128]{1,0:T(8,128)S(1)}, u32[]{:S(2)}, u32[]{:S(2)}) collective-permute-start(f32[8,128]{1,0:T(8,128)} %shard_map.85), channel_id=1, source_target_pairs={{0,1},{1,0},{2,3},{3,2},{4,5},{5,4},{6,7},{7,6},{8,9},{9,8},{10,11... | collective-permute-start | bytes 12296 | tf_op jit(solution)/shard_map/ppermute | solution.py:74
  67.3 3.6 %collective-permute-start.13 = (f32[8,128]{1,0:T(8,128)S(1)}, f32[8,128]{1,0:T(8,128)S(1)}, u32[]{:S(2)}, u32[]{:S(2)}) collective-permute-start(f32[8,128]{1,0:T(8,128)S(1)} %add.225), channel_id=1, source_target_pairs={{0,2},{1,3},{2,0},{3,1},{4,6},{5,7},{6,4},{7,5},{8,10},{9,11},{10,... | collective-permute-start | bytes 12296 | tf_op jit(solution)/shard_map/ppermute | solution.py:74
  70.9 4.6 %collective-permute-start.14 = (f32[8,128]{1,0:T(8,128)S(1)}, f32[8,128]{1,0:T(8,128)S(1)}, u32[]{:S(2)}, u32[]{:S(2)}) collective-permute-start(f32[8,128]{1,0:T(8,128)S(1)} %add.226), channel_id=1, source_target_pairs={{0,4},{1,5},{2,6},{3,7},{4,0},{5,1},{6,2},{7,3},{8,12},{9,13},{10,... | collective-permute-start | bytes 12296 | tf_op jit(solution)/shard_map/ppermute | solution.py:74
  75.4 3.6 %collective-permute-start.15 = (f32[8,128]{1,0:T(8,128)S(1)}, f32[8,128]{1,0:T(8,128)S(1)}, u32[]{:S(2)}, u32[]{:S(2)}) collective-permute-start(f32[8,128]{1,0:T(8,128)S(1)} %add.227), channel_id=1, source_target_pairs={{0,8},{8,0},{16,24},{24,16},{1,9},{9,1},{17,25},{25,17},{2,10},{10... | collective-permute-start | bytes 12296 | tf_op jit(solution)/shard_map/ppermute | solution.py:74
  79.0 3.6 %collective-permute-start.16 = (f32[8,128]{1,0:T(8,128)S(1)}, f32[8,128]{1,0:T(8,128)S(1)}, u32[]{:S(2)}, u32[]{:S(2)}) collective-permute-start(f32[8,128]{1,0:T(8,128)S(1)} %add.228), channel_id=1, source_target_pairs={{0,16},{8,24},{16,0},{24,8},{1,17},{9,25},{17,1},{25,9},{2,18},{10... | collective-permute-start | bytes 12296 | tf_op jit(solution)/shard_map/ppermute | solution.py:74

commit v9 on v6

--- a/solution.py
+++ b/solution.py
@@ -39,24 +39,29 @@
     return from_low_x, from_high_x, from_low_y, from_high_y
 
 
-def neighbour_sum(u, halo, coef):
+def neighbour_sum(u, halo, coef, rows=None, cols=None):
     lo_x, hi_x, lo_y, hi_y = halo
-    tx_lo, tx_hi, ty_lo, ty_hi, tz_lo, tz_hi = coef
-    zero_plane = jnp.zeros_like(u[..., :1])
-    u_xm = jnp.concatenate([lo_x, u[:-1]], axis=0)
-    u_xp = jnp.concatenate([u[1:], hi_x], axis=0)
-    u_ym = jnp.concatenate([lo_y, u[:, :-1]], axis=1)
-    u_yp = jnp.concatenate([u[:, 1:], hi_y], axis=1)
-    u_zm = jnp.concatenate([zero_plane, u[..., :-1]], axis=-1)
-    u_zp = jnp.concatenate([u[..., 1:], zero_plane], axis=-1)
-    total = tx_lo * u_xm + tx_hi * u_xp
-    total = total + ty_lo * u_ym + ty_hi * u_yp
+    r0, r1 = rows or (0, u.shape[0])
+    c0, c1 = cols or (0, u.shape[1])
+    tx_lo, tx_hi, ty_lo, ty_hi, tz_lo, tz_hi = (c[r0:r1, c0:c1] for c in coef)
+    along_x = jnp.concatenate([lo_x, u, hi_x], axis=0)[:, c0:c1]
+    along_y = jnp.concatenate([lo_y, u, hi_y], axis=1)[r0:r1]
+    centre = u[r0:r1, c0:c1]
+    zero_plane = jnp.zeros_like(centre[..., :1])
+    u_zm = jnp.concatenate([zero_plane, centre[..., :-1]], axis=-1)
+    u_zp = jnp.concatenate([centre[..., 1:], zero_plane], axis=-1)
+    total = tx_lo * along_x[r0:r1] + tx_hi * along_x[r0 + 2 : r1 + 2]
+    total = total + ty_lo * along_y[:, c0:c1] + ty_hi * along_y[:, c0 + 2 : c1 + 2]
     total = total + tz_lo * u_zm + tz_hi * u_zp
     return total
 
 
+def faces(u):
+    return u[:1], u[-1:], u[:, :1], u[:, -1:]
+
+
 def field_halo(u):
-    return exchange(u[:1], u[-1:], u[:, :1], u[:, -1:])
+    return exchange(*faces(u))
 
 
 def all_sum(x):
@@ -206,14 +211,27 @@
     coef = (tx_lo, tx_hi, ty_lo, ty_hi, tz_lo, tz_hi)
     diagonal = accumulation + tx_lo + tx_hi + ty_lo + ty_hi + tz_lo + tz_hi
 
-    total = neighbour_sum(start_field, (lo_x, hi_x, lo_y, hi_y), coef)
-    residual0 = right_side - (diagonal * start_field - total)
-
-    vector = residual0
+    halo = (lo_x, hi_x, lo_y, hi_y)
+    size_x, size_y = start_field.shape[:2]
+    face_regions = (((0, 1), None), ((size_x - 1, size_x), None), (None, (0, 1)), (None, (size_y - 1, size_y)))
+
+    def residual(rows=None, cols=None):
+        part = lambda a: a[slice(*(rows or (0, size_x))), slice(*(cols or (0, size_y)))]
+        total = neighbour_sum(start_field, halo, coef, rows, cols)
+        return part(right_side) - (part(diagonal) * part(start_field) - total)
+
+    def step(u, u_halo, rows=None, cols=None):
+        part = diagonal[slice(*(rows or (0, size_x))), slice(*(cols or (0, size_y)))]
+        return 2.0 * neighbour_sum(u, u_halo, coef, rows, cols) / part
+
+    next_halo = exchange(*(residual(r, c) for r, c in face_regions))
+    vector = residual()
     basis = [vector]
-    for step in range(STEPS):
-        total = neighbour_sum(vector, field_halo(vector), coef)
-        vector = 2.0 * total / diagonal
+    for step_index in range(STEPS):
+        halo = next_halo
+        if step_index < STEPS - 1:
+            next_halo = exchange(*(step(vector, halo, r, c) for r, c in face_regions))
+        vector = step(vector, halo)
         basis.append(vector)
     stats = gram(basis)
     stats = all_sum(stats)

time: 79.3 us -> 83.2 us (1.049)
  other arithmetic: 4.77 us -> 6.83 us
    select_n x2 -> x10, other arithmetic: 0.13 us -> 2.61 us  [axis_exchange(): jnp.where(odd, to_low, to_high)]
    ppermute x10, starting transfers between devices: 35.2 us -> 36.1 us  [axis_exchange(): lax.ppermute(jnp.where(odd, to_low, to_high), axis, swap_pairs(axis, 0))]
    slice x15 -> x13, local copies, waits for them, and re-layouts: 2.2 us -> 3.03 us  [neighbour_sum(): u_zm = jnp.concatenate([zero_plane, centre[..., :-1]], axis=-1)]
  transfers between devices with their start and end apart: 25 -> 25, of which waited for: 9 -> 9; matrix products, arithmetic and copies ran while one was open for 4% -> 6% of each run, Pallas kernels for 0% -> 0%
where the time goes in v9:
time: 83.2 us; the launch traced here: 82.7 us
  starting transfers between devices  48.4 us (58%)
  waiting for transfers between devices  15.2 us (18%)
  other arithmetic  6.83 us (8%)
  local copies, waits for them, and re-layouts  6.06 us (7%)
  Pallas kernels  5.06 us (6%)
  between operations  1.16 us (1%)
    ppermute x10, starting transfers between devices, axis_exchange(): lax.ppermute(jnp.where(odd, to_low, to_high), axis, swap_pairs(axis, 0))  36.1 us
    ppermute x5, waiting for transfers between devices, all_sum(): x = x + lax.ppermute(x, axis, [(i, i ^ step) for i in range(n)])  11.5 us
    ppermute x10, starting transfers between devices, axis_exchange(): lax.ppermute(jnp.where(odd, to_high, to_low), axis, swap_pairs(axis, 1))  6.6 us
    ppermute x5, starting transfers between devices, all_sum(): x = x + lax.ppermute(x, axis, [(i, i ^ step) for i in range(n)])  5.63 us
    ppermute x10, waiting for transfers between devices, axis_exchange(): lax.ppermute(jnp.where(odd, to_low, to_high), axis, swap_pairs(axis, 0))  3.74 us
    slice x13, local copies, waits for them, and re-layouts, neighbour_sum(): u_zm = jnp.concatenate([zero_plane, centre[..., :-1]], axis=-1)  3.03 us
    pallas_call x1, Pallas kernels, finish(): pl.pallas_call(lambda *refs: finish_kernel(float(cells), size, *refs), ou...  2.75 us
    select_n x10, other arithmetic, axis_exchange(): jnp.where(odd, to_low, to_high)  2.61 us
  transfers between devices with their start and end apart: 25, of which 9 were waited for; matrix products, arithmetic and copies ran while one was open for 6% of the time, Pallas kernels for 0%

profile of v9, /device:TPU:0, one launch (start us, length us, event | category | flops | bytes accessed | tf_op | source)
XLA Modules:
  0.0 82.7 jit_solution(8609798324707305374)
XLA Ops:
  0.7 0.8 %fusion.211 = (f32[1,8,512]{2,1,0:T(8,128)S(1)}, f32[1,8,512]{2,1,0:T(8,128)S(1)}, f32[1,8,512]{2,1,0:T(8,128)S(1)}, f32[1,8,512]{2,1,0:T(8,128)S(1)}) fusion(f32[16,8,512]{2,1,0:T(8,128)} %param.6, f32[16,8,512]{2,1,0:T(8,128)} %param.9), kind=kLoop, calls=%fused_computation.367 | loop fusion | bytes 131072 | tf_op jit(solution)/shard_map/slice | solution.py:197
  1.5 3.0 %collective-permute-start.1 = (f32[2,8,512]{2,1,0:T(8,128)S(1)}, f32[2,8,512]{2,1,0:T(8,128)S(1)}, u32[]{:S(2)}, u32[]{:S(2)}) collective-permute-start(f32[2,8,512]{2,1,0:T(8,128)S(1)} %get-tuple-element.98), channel_id=1, source_target_pairs={{0,8},{8,0},{16,24},{24,16},{1,9},{9,1},{17,25},{25,17},{2,10},{10... | collective-permute-start | bytes 98312 | tf_op jit(solution)/shard_map/ppermute | solution.py:29
  4.5 0.7 collective-permute-start
  5.2 1.3 %fusion.209 = (f32[16,1,512]{2,1,0:T(1,128)S(1)}, f32[16,1,512]{2,1,0:T(1,128)S(1)}, f32[16,1,512]{2,1,0:T(1,128)S(1)}, f32[16,1,512]{2,1,0:T(1,128)S(1)}) fusion(f32[16,8,512]{2,1,0:T(8,128)} %param.6, f32[16,8,512]{2,1,0:T(8,128)} %param.10), kind=kLoop, calls=%fused_computation.365 | loop fusion | bytes 262144 | tf_op jit(solution)/shard_map/slice | solution.py:199
  6.5 0.1 broadcast_select_fusion.18
  6.7 0.7 collective-permute-start.2
  7.4 1.4 %fusion.208 = (f32[16,1,511]{2,1,0:T(1,128)S(1)}, f32[16,1,511]{2,1,0:T(1,128)S(1)}, f32[16,1,511]{2,1,0:T(1,128)S(1)}, f32[16,1,511]{2,1,0:T(1,128)S(1)}) fusion(f32[16,8,512]{2,1,0:T(8,128)} %param.6), kind=kLoop, calls=%fused_computation.364 | loop fusion | bytes 261632 | tf_op jit(solution)/shard_map/slice | solution.py:51
  8.8 0.1 fusion.207
  9.2 0.1 slice.707
  9.5 0.5 copy-done.8
  9.9 0.2 add_add_fusion
  10.2 0.1 copy-done.9
  10.3 0.5 broadcast_select_fusion.15
  10.8 0.4 fusion.41.refs_0_.refs_1_
  11.2 0.2 fusion.205
  11.5 0.1 fusion.204
  11.6 0.1 broadcast_select_fusion.36
  11.7 0.7 collective-permute-start.5
  12.4 6.2 %collective-permute-start.4 = (f32[1,8,512]{2,1,0:T(8,128)S(1)}, f32[1,8,512]{2,1,0:T(8,128)S(1)}, u32[]{:S(2)}, u32[]{:S(2)}) collective-permute-start(f32[1,8,512]{2,1,0:T(8,128)S(1)} %get-tuple-element.37), channel_id=1, source_target_pairs={{0,8},{8,0},{16,24},{24,16},{1,9},{9,1},{17,25},{25,17},{2,10},{10... | collective-permute-start | bytes 49160 | tf_op jit(solution)/shard_map/ppermute | solution.py:29
  18.6 0.7 collective-permute-start.7
  19.3 5.2 %collective-permute-start.6 = (f32[16,1,512]{2,1,0:T(1,128)S(1)}, f32[16,1,512]{2,1,0:T(1,128)S(1)}, u32[]{:S(2)}, u32[]{:S(2)}) collective-permute-start(f32[16,1,512]{2,1,0:T(1,128)S(1)} %get-tuple-element.33), channel_id=1, source_target_pairs={{0,1},{1,0},{2,3},{3,2},{4,5},{5,4},{6,7},{7,6},{8,9},{9,8},{10,11... | collective-permute-start | bytes 98312 | tf_op jit(solution)/shard_map/ppermute | solution.py:29
  24.5 0.8 %collective-permute-done.6 = f32[16,1,512]{2,1,0:T(1,128)S(1)} collective-permute-done((f32[16,1,512]{2,1,0:T(1,128)S(1)}, f32[16,1,512]{2,1,0:T(1,128)S(1)}, u32[]{:S(2)}, u32[]{:S(2)}) %collective-permute-start.6) | collective-permute-done | bytes 32800 | tf_op jit(solution)/shard_map/ppermute | solution.py:29
  25.3 0.5 broadcast_select_fusion.11
  25.9 0.4 fusion.30.refs_1_.refs_2_
  26.2 0.2 fusion.202
  26.5 0.1 fusion.201
  26.6 0.1 broadcast_select_fusion.32
  26.7 0.7 collective-permute-start.9
  27.4 3.8 %collective-permute-start.8 = (f32[1,8,512]{2,1,0:T(8,128)S(1)}, f32[1,8,512]{2,1,0:T(8,128)S(1)}, u32[]{:S(2)}, u32[]{:S(2)}) collective-permute-start(f32[1,8,512]{2,1,0:T(8,128)S(1)} %get-tuple-element.30), channel_id=1, source_target_pairs={{0,8},{8,0},{16,24},{24,16},{1,9},{9,1},{17,25},{25,17},{2,10},{10... | collective-permute-start | bytes 49160 | tf_op jit(solution)/shard_map/ppermute | solution.py:29
  31.2 0.7 collective-permute-start.11
  31.9 3.7 %collective-permute-start.10 = (f32[16,1,512]{2,1,0:T(1,128)S(1)}, f32[16,1,512]{2,1,0:T(1,128)S(1)}, u32[]{:S(2)}, u32[]{:S(2)}) collective-permute-start(f32[16,1,512]{2,1,0:T(1,128)S(1)} %get-tuple-element.25), channel_id=1, source_target_pairs={{0,1},{1,0},{2,3},{3,2},{4,5},{5,4},{6,7},{7,6},{8,9},{9,8},{10,11... | collective-permute-start | bytes 98312 | tf_op jit(solution)/shard_map/ppermute | solution.py:29
  35.6 0.8 %collective-permute-done.10 = f32[16,1,512]{2,1,0:T(1,128)S(1)} collective-permute-done((f32[16,1,512]{2,1,0:T(1,128)S(1)}, f32[16,1,512]{2,1,0:T(1,128)S(1)}, u32[]{:S(2)}, u32[]{:S(2)}) %collective-permute-start.10) | collective-permute-done | bytes 32800 | tf_op jit(solution)/shard_map/ppermute | solution.py:29
  36.5 0.5 broadcast_select_fusion.7
  37.0 0.4 fusion.19.refs_2_.refs_3_
  37.5 0.2 fusion.197
  37.7 0.1 fusion.198
  37.8 0.7 collective-permute-start.15
  38.5 3.7 %collective-permute-start.14 = (f32[16,1,512]{2,1,0:T(1,128)S(1)}, f32[16,1,512]{2,1,0:T(1,128)S(1)}, u32[]{:S(2)}, u32[]{:S(2)}) collective-permute-start(f32[16,1,512]{2,1,0:T(1,128)S(1)} %get-tuple-element.17), channel_id=1, source_target_pairs={{0,1},{1,0},{2,3},{3,2},{4,5},{5,4},{6,7},{7,6},{8,9},{9,8},{10,11... | collective-permute-start | bytes 98312 | tf_op jit(solution)/shard_map/ppermute | solution.py:29
  42.2 0.1 broadcast_select_fusion.28
  42.3 0.7 collective-permute-start.13
  43.0 2.1 %collective-permute-start.12 = (f32[1,8,512]{2,1,0:T(8,128)S(1)}, f32[1,8,512]{2,1,0:T(8,128)S(1)}, u32[]{:S(2)}, u32[]{:S(2)}) collective-permute-start(f32[1,8,512]{2,1,0:T(8,128)S(1)} %get-tuple-element.22), channel_id=1, source_target_pairs={{0,8},{8,0},{16,24},{24,16},{1,9},{9,1},{17,25},{25,17},{2,10},{10... | collective-permute-start | bytes 49160 | tf_op jit(solution)/shard_map/ppermute | solution.py:29
  45.1 1.8 %collective-permute-done.12 = f32[1,8,512]{2,1,0:T(8,128)S(1)} collective-permute-done((f32[1,8,512]{2,1,0:T(8,128)S(1)}, f32[1,8,512]{2,1,0:T(8,128)S(1)}, u32[]{:S(2)}, u32[]{:S(2)}) %collective-permute-start.12) | collective-permute-done | bytes 16416 | tf_op jit(solution)/shard_map/ppermute | solution.py:29
  46.9 0.1 broadcast_select_fusion.24
  47.0 0.7 collective-permute-start.17
  47.6 5.4 %collective-permute-start.16 = (f32[1,8,512]{2,1,0:T(8,128)S(1)}, f32[1,8,512]{2,1,0:T(8,128)S(1)}, u32[]{:S(2)}, u32[]{:S(2)}) collective-permute-start(f32[1,8,512]{2,1,0:T(8,128)S(1)} %get-tuple-element.9), channel_id=1, source_target_pairs={{0,8},{8,0},{16,24},{24,16},{1,9},{9,1},{17,25},{25,17},{2,10},{10... | collective-permute-start | bytes 49160 | tf_op jit(solution)/shard_map/ppermute | solution.py:29
  53.1 0.5 broadcast_select_fusion.3
  53.6 0.7 collective-permute-start.19
  54.3 3.0 %collective-permute-start.18 = (f32[16,1,512]{2,1,0:T(1,128)S(1)}, f32[16,1,512]{2,1,0:T(1,128)S(1)}, u32[]{:S(2)}, u32[]{:S(2)}) collective-permute-start(f32[16,1,512]{2,1,0:T(1,128)S(1)} %get-tuple-element.14), channel_id=1, source_target_pairs={{0,1},{1,0},{2,3},{3,2},{4,5},{5,4},{6,7},{7,6},{8,9},{9,8},{10,11... | collective-permute-start | bytes 98312 | tf_op jit(solution)/shard_map/ppermute | solution.py:29
  57.3 0.4 fusion.8.refs_3_.refs_4_
  57.7 0.1 fusion.196
  57.9 0.3 collective-permute-done.18
  58.1 1.1 %fusion.65.refs_4_.refs_5_ = f32[16,8,512]{2,1,0:T(8,128)} fusion(f32[16,1,512]{2,1,0:T(1,128)S(1)} %bitcast.38, f32[16,8,512]{2,1,0:T(8,128)S(1)} %fusion.8.refs_3_.refs_4_, f32[16,8,512]{2,1,0:T(8,128)S(1)} %copy-done, f32[16,1,512]{2,1,0:T(1,128)S(1)} %bitcast.37, f32[1,8,512]{2,1,0:T(8,128)S(1)} %get-tuple-element.101, f32[16,8,512]{2,1,0:T(8,128)S(1)} %copy-done.4, ...), kind=kLoop, calls=%fused_computation.136 | loop fusion | flops 1638400 | bytes 2980352 | tf_op jit(solution)/shard_map/div | solution.py:225
  59.2 2.3 %shard_map.85 = f32[8,128]{1,0:T(8,128)} custom-call(f32[16,8,512]{2,1,0:T(8,128)} %copy-done.1, f32[16,8,512]{2,1,0:T(8,128)} %copy-done.2, f32[16,8,512]{2,1,0:T(8,128)} %copy-done.3, f32[16,8,512]{2,1,0:T(8,128)} %copy-done.7, f32[16,8,512]{2,1,0:T(8,128)} %fusion.65.refs_4_.refs_5_), custom_call_target="tpu_custom_call" | custom-call | tf_op jit(solution)/shard_map/pallas_call | solution.py:112
  61.6 0.7 collective-permute-start.20
  62.2 1.0 %collective-permute-done.20 = f32[8,128]{1,0:T(8,128)S(1)} collective-permute-done((f32[8,128]{1,0:T(8,128)}, f32[8,128]{1,0:T(8,128)S(1)}, u32[]{:S(2)}, u32[]{:S(2)}) %collective-permute-start.20) | collective-permute-done | bytes 4128 | tf_op jit(solution)/shard_map/ppermute | solution.py:75
  63.3 0.7 add.562
  64.0 2.0 %collective-permute-start.21 = (f32[8,128]{1,0:T(8,128)S(1)}, f32[8,128]{1,0:T(8,128)S(1)}, u32[]{:S(2)}, u32[]{:S(2)}) collective-permute-start(f32[8,128]{1,0:T(8,128)S(1)} %add.562), channel_id=1, source_target_pairs={{0,2},{1,3},{2,0},{3,1},{4,6},{5,7},{6,4},{7,5},{8,10},{9,11},{10,... | collective-permute-start | bytes 12296 | tf_op jit(solution)/shard_map/ppermute | solution.py:75
  65.9 1.6 %collective-permute-done.21 = f32[8,128]{1,0:T(8,128)S(1)} collective-permute-done((f32[8,128]{1,0:T(8,128)S(1)}, f32[8,128]{1,0:T(8,128)S(1)}, u32[]{:S(2)}, u32[]{:S(2)}) %collective-permute-start.21) | collective-permute-done | bytes 4128 | tf_op jit(solution)/shard_map/ppermute | solution.py:75
  67.6 3.0 %collective-permute-start.22 = (f32[8,128]{1,0:T(8,128)S(1)}, f32[8,128]{1,0:T(8,128)S(1)}, u32[]{:S(2)}, u32[]{:S(2)}) collective-permute-start(f32[8,128]{1,0:T(8,128)S(1)} %add.563), channel_id=1, source_target_pairs={{0,4},{1,5},{2,6},{3,7},{4,0},{5,1},{6,2},{7,3},{8,12},{9,13},{10,... | collective-permute-start | bytes 12296 | tf_op jit(solution)/shard_map/ppermute | solution.py:75
  70.5 1.6 %collective-permute-done.22 = f32[8,128]{1,0:T(8,128)S(1)} collective-permute-done((f32[8,128]{1,0:T(8,128)S(1)}, f32[8,128]{1,0:T(8,128)S(1)}, u32[]{:S(2)}, u32[]{:S(2)}) %collective-permute-start.22) | collective-permute-done | bytes 4128 | tf_op jit(solution)/shard_map/ppermute | solution.py:75
  72.1 3.6 %collective-permute-done.23 = f32[8,128]{1,0:T(8,128)S(1)} collective-permute-done((f32[8,128]{1,0:T(8,128)S(1)}, f32[8,128]{1,0:T(8,128)S(1)}, u32[]{:S(2)}, u32[]{:S(2)}) %collective-permute-start.23) | collective-permute-done | bytes 4128 | tf_op jit(solution)/shard_map/ppermute | solution.py:75
  75.7 3.6 %collective-permute-done.24 = f32[8,128]{1,0:T(8,128)S(1)} collective-permute-done((f32[8,128]{1,0:T(8,128)S(1)}, f32[8,128]{1,0:T(8,128)S(1)}, u32[]{:S(2)}, u32[]{:S(2)}) %collective-permute-start.24) | collective-permute-done | bytes 4128 | tf_op jit(solution)/shard_map/ppermute | solution.py:75
  79.3 0.6 add.566.refs_0_
  79.9 2.8 %shard_map.86 = (f32[5,16,8,512]{3,2,1,0:T(8,128)}, f32[5,5]{1,0:T(8,128)}, f32[1,1]{1,0:T(1,128)}) custom-call(f32[8,128]{1,0:T(8,128)} %add.566.refs_0_, f32[16,8,512]{2,1,0:T(8,128)} %copy-done.1, f32[16,8,512]{2,1,0:T(8,128)} %copy-done.2, f32[16,8,512]{2,1,0:T(8,128)} %copy-done.3, f32[16,8,512]{2,1,0:T(8,128)} %copy-done.7, ...), custom_call_target="tpu_custom_call" | custom-call | tf_op jit(solution)/shard_map/pallas_call | solution.py:178
  (65 shorter events, 0.7 us)
Async XLA Ops:
  0.6 8.4 %copy-start.4 = (f32[16,8,512]{2,1,0:T(8,128)S(1)}, f32[16,8,512]{2,1,0:T(8,128)}, u32[]{:S(2)}) copy-start(f32[16,8,512]{2,1,0:T(8,128)} %param.9) | copy-start | bytes 786436
  0.6 8.2 %copy-start.6 = (f32[16,8,512]{2,1,0:T(8,128)S(1)}, f32[16,8,512]{2,1,0:T(8,128)}, u32[]{:S(2)}) copy-start(f32[16,8,512]{2,1,0:T(8,128)} %param.6) | copy-start | bytes 786436
  1.5 7.6 %copy-start = (f32[16,8,512]{2,1,0:T(8,128)S(1)}, f32[16,8,512]{2,1,0:T(8,128)}, u32[]{:S(2)}) copy-start(f32[16,8,512]{2,1,0:T(8,128)} %param.10) | copy-start | bytes 786436
  1.5 7.8 %collective-permute-start.1 = (f32[2,8,512]{2,1,0:T(8,128)S(1)}, f32[2,8,512]{2,1,0:T(8,128)S(1)}, u32[]{:S(2)}, u32[]{:S(2)}) collective-permute-start(f32[2,8,512]{2,1,0:T(8,128)S(1)} %get-tuple-element.98), channel_id=1, source_target_pairs={{0,8},{8,0},{16,24},{24,16},{1,9},{9,1},{17,25},{25,17},{2,10},{10... | collective-permute-start | bytes 98312 | tf_op jit(solution)/shard_map/ppermute | solution.py:29
  4.5 4.8 %collective-permute-start = (f32[2,8,512]{2,1,0:T(8,128)S(1)}, f32[2,8,512]{2,1,0:T(8,128)S(1)}, u32[]{:S(2)}, u32[]{:S(2)}) collective-permute-start(f32[2,8,512]{2,1,0:T(8,128)S(1)} %get-tuple-element.99), channel_id=1, source_target_pairs={{8,16},{16,8},{9,17},{17,9},{10,18},{18,10},{11,19},{19,11},{12,20... | collective-permute-start | bytes 98312 | tf_op jit(solution)/shard_map/ppermute | solution.py:30
  6.5 2.7 %copy-start.5 = (f32[16,8,512]{2,1,0:T(8,128)S(1)}, f32[16,8,512]{2,1,0:T(8,128)}, u32[]{:S(2)}) copy-start(f32[16,8,512]{2,1,0:T(8,128)} %param.11) | copy-start | bytes 786436
  6.6 2.7 %collective-permute-start.3 = (f32[16,2,512]{2,1,0:T(2,128)S(1)}, f32[16,2,512]{2,1,0:T(2,128)S(1)}, u32[]{:S(2)}, u32[]{:S(2)}) collective-permute-start(f32[16,2,512]{2,1,0:T(2,128)S(1)} %get-tuple-element.90), channel_id=1, source_target_pairs={{0,1},{1,0},{2,3},{3,2},{4,5},{5,4},{6,7},{7,6},{8,9},{9,8},{10,11... | collective-permute-start | bytes 196616 | tf_op jit(solution)/shard_map/ppermute | solution.py:29
  6.7 2.7 %collective-permute-start.2 = (f32[16,2,512]{2,1,0:T(2,128)S(1)}, f32[16,2,512]{2,1,0:T(2,128)S(1)}, u32[]{:S(2)}, u32[]{:S(2)}) collective-permute-start(f32[16,2,512]{2,1,0:T(2,128)S(1)} %get-tuple-element.91), channel_id=1, source_target_pairs={{1,2},{2,1},{3,4},{4,3},{5,6},{6,5},{9,10},{10,9},{11,12},{12,11},... | collective-permute-start | bytes 196616 | tf_op jit(solution)/shard_map/ppermute | solution.py:30
  9.0 1.0 %copy-start.8 = (f32[16,8,512]{2,1,0:T(8,128)S(1)}, f32[16,8,512]{2,1,0:T(8,128)}, u32[]{:S(2)}) copy-start(f32[16,8,512]{2,1,0:T(8,128)} %param.8) | copy-start | bytes 786436
  9.3 1.0 %copy-start.9 = (f32[16,8,512]{2,1,0:T(8,128)S(1)}, f32[16,8,512]{2,1,0:T(8,128)}, u32[]{:S(2)}) copy-start(f32[16,8,512]{2,1,0:T(8,128)} %param.7) | copy-start | bytes 786436
  11.2 15.4 %copy-start.1 = (f32[16,8,512]{2,1,0:T(8,128)}, f32[16,8,512]{2,1,0:T(8,128)S(1)}, u32[]{:S(2)}) copy-start(f32[16,8,512]{2,1,0:T(8,128)S(1)} %fusion.41.refs_0_.refs_1_) | copy-start | bytes 786436
  11.7 12.8 %collective-permute-start.5 = (f32[1,8,512]{2,1,0:T(8,128)S(1)}, f32[1,8,512]{2,1,0:T(8,128)S(1)}, u32[]{:S(2)}, u32[]{:S(2)}) collective-permute-start(f32[1,8,512]{2,1,0:T(8,128)S(1)} %broadcast_select_fusion.35), channel_id=1, source_target_pairs={{8,16},{16,8},{9,17},{17,9},{10,18},{18,10},{11,19},{19,11},{12,20... | collective-permute-start | bytes 49160 | tf_op jit(solution)/shard_map/ppermute | solution.py:30
  12.4 12.1 %collective-permute-start.4 = (f32[1,8,512]{2,1,0:T(8,128)S(1)}, f32[1,8,512]{2,1,0:T(8,128)S(1)}, u32[]{:S(2)}, u32[]{:S(2)}) collective-permute-start(f32[1,8,512]{2,1,0:T(8,128)S(1)} %get-tuple-element.37), channel_id=1, source_target_pairs={{0,8},{8,0},{16,24},{24,16},{1,9},{9,1},{17,25},{25,17},{2,10},{10... | collective-permute-start | bytes 49160 | tf_op jit(solution)/shard_map/ppermute | solution.py:29
  18.6 5.9 %collective-permute-start.7 = (f32[16,1,512]{2,1,0:T(1,128)S(1)}, f32[16,1,512]{2,1,0:T(1,128)S(1)}, u32[]{:S(2)}, u32[]{:S(2)}) collective-permute-start(f32[16,1,512]{2,1,0:T(1,128)S(1)} %bitcast.49), channel_id=1, source_target_pairs={{1,2},{2,1},{3,4},{4,3},{5,6},{6,5},{9,10},{10,9},{11,12},{12,11},... | collective-permute-start | bytes 98312 | tf_op jit(solution)/shard_map/ppermute | solution.py:30
  19.3 6.0 %collective-permute-start.6 = (f32[16,1,512]{2,1,0:T(1,128)S(1)}, f32[16,1,512]{2,1,0:T(1,128)S(1)}, u32[]{:S(2)}, u32[]{:S(2)}) collective-permute-start(f32[16,1,512]{2,1,0:T(1,128)S(1)} %get-tuple-element.33), channel_id=1, source_target_pairs={{0,1},{1,0},{2,3},{3,2},{4,5},{5,4},{6,7},{7,6},{8,9},{9,8},{10,11... | collective-permute-start | bytes 98312 | tf_op jit(solution)/shard_map/ppermute | solution.py:29
  26.2 16.0 %copy-start.2 = (f32[16,8,512]{2,1,0:T(8,128)}, f32[16,8,512]{2,1,0:T(8,128)S(1)}, u32[]{:S(2)}) copy-start(f32[16,8,512]{2,1,0:T(8,128)S(1)} %fusion.30.refs_1_.refs_2_) | copy-start | bytes 786436
  26.7 8.9 %collective-permute-start.9 = (f32[1,8,512]{2,1,0:T(8,128)S(1)}, f32[1,8,512]{2,1,0:T(8,128)S(1)}, u32[]{:S(2)}, u32[]{:S(2)}) collective-permute-start(f32[1,8,512]{2,1,0:T(8,128)S(1)} %broadcast_select_fusion.31), channel_id=1, source_target_pairs={{8,16},{16,8},{9,17},{17,9},{10,18},{18,10},{11,19},{19,11},{12,20... | collective-permute-start | bytes 49160 | tf_op jit(solution)/shard_map/ppermute | solution.py:30
  27.4 8.2 %collective-permute-start.8 = (f32[1,8,512]{2,1,0:T(8,128)S(1)}, f32[1,8,512]{2,1,0:T(8,128)S(1)}, u32[]{:S(2)}, u32[]{:S(2)}) collective-permute-start(f32[1,8,512]{2,1,0:T(8,128)S(1)} %get-tuple-element.30), channel_id=1, source_target_pairs={{0,8},{8,0},{16,24},{24,16},{1,9},{9,1},{17,25},{25,17},{2,10},{10... | collective-permute-start | bytes 49160 | tf_op jit(solution)/shard_map/ppermute | solution.py:29
  31.2 4.4 %collective-permute-start.11 = (f32[16,1,512]{2,1,0:T(1,128)S(1)}, f32[16,1,512]{2,1,0:T(1,128)S(1)}, u32[]{:S(2)}, u32[]{:S(2)}) collective-permute-start(f32[16,1,512]{2,1,0:T(1,128)S(1)} %bitcast.50), channel_id=1, source_target_pairs={{1,2},{2,1},{3,4},{4,3},{5,6},{6,5},{9,10},{10,9},{11,12},{12,11},... | collective-permute-start | bytes 98312 | tf_op jit(solution)/shard_map/ppermute | solution.py:30
  31.9 4.6 %collective-permute-start.10 = (f32[16,1,512]{2,1,0:T(1,128)S(1)}, f32[16,1,512]{2,1,0:T(1,128)S(1)}, u32[]{:S(2)}, u32[]{:S(2)}) collective-permute-start(f32[16,1,512]{2,1,0:T(1,128)S(1)} %get-tuple-element.25), channel_id=1, source_target_pairs={{0,1},{1,0},{2,3},{3,2},{4,5},{5,4},{6,7},{7,6},{8,9},{9,8},{10,11... | collective-permute-start | bytes 98312 | tf_op jit(solution)/shard_map/ppermute | solution.py:29
  37.4 19.9 %copy-start.3 = (f32[16,8,512]{2,1,0:T(8,128)}, f32[16,8,512]{2,1,0:T(8,128)S(1)}, u32[]{:S(2)}) copy-start(f32[16,8,512]{2,1,0:T(8,128)S(1)} %fusion.19.refs_2_.refs_3_) | copy-start | bytes 786436
  37.8 7.2 %collective-permute-start.15 = (f32[16,1,512]{2,1,0:T(1,128)S(1)}, f32[16,1,512]{2,1,0:T(1,128)S(1)}, u32[]{:S(2)}, u32[]{:S(2)}) collective-permute-start(f32[16,1,512]{2,1,0:T(1,128)S(1)} %bitcast.47), channel_id=1, source_target_pairs={{1,2},{2,1},{3,4},{4,3},{5,6},{6,5},{9,10},{10,9},{11,12},{12,11},... | collective-permute-start | bytes 98312 | tf_op jit(solution)/shard_map/ppermute | solution.py:30
  38.5 6.6 %collective-permute-start.14 = (f32[16,1,512]{2,1,0:T(1,128)S(1)}, f32[16,1,512]{2,1,0:T(1,128)S(1)}, u32[]{:S(2)}, u32[]{:S(2)}) collective-permute-start(f32[16,1,512]{2,1,0:T(1,128)S(1)} %get-tuple-element.17), channel_id=1, source_target_pairs={{0,1},{1,0},{2,3},{3,2},{4,5},{5,4},{6,7},{7,6},{8,9},{9,8},{10,11... | collective-permute-start | bytes 98312 | tf_op jit(solution)/shard_map/ppermute | solution.py:29
  42.3 2.8 %collective-permute-start.13 = (f32[1,8,512]{2,1,0:T(8,128)S(1)}, f32[1,8,512]{2,1,0:T(8,128)S(1)}, u32[]{:S(2)}, u32[]{:S(2)}) collective-permute-start(f32[1,8,512]{2,1,0:T(8,128)S(1)} %broadcast_select_fusion.27), channel_id=1, source_target_pairs={{8,16},{16,8},{9,17},{17,9},{10,18},{18,10},{11,19},{19,11},{12,20... | collective-permute-start | bytes 49160 | tf_op jit(solution)/shard_map/ppermute | solution.py:30
  43.0 3.9 %collective-permute-start.12 = (f32[1,8,512]{2,1,0:T(8,128)S(1)}, f32[1,8,512]{2,1,0:T(8,128)S(1)}, u32[]{:S(2)}, u32[]{:S(2)}) collective-permute-start(f32[1,8,512]{2,1,0:T(8,128)S(1)} %get-tuple-element.22), channel_id=1, source_target_pairs={{0,8},{8,0},{16,24},{24,16},{1,9},{9,1},{17,25},{25,17},{2,10},{10... | collective-permute-start | bytes 49160 | tf_op jit(solution)/shard_map/ppermute | solution.py:29
  47.0 10.8 %collective-permute-start.17 = (f32[1,8,512]{2,1,0:T(8,128)S(1)}, f32[1,8,512]{2,1,0:T(8,128)S(1)}, u32[]{:S(2)}, u32[]{:S(2)}) collective-permute-start(f32[1,8,512]{2,1,0:T(8,128)S(1)} %broadcast_select_fusion.23), channel_id=1, source_target_pairs={{8,16},{16,8},{9,17},{17,9},{10,18},{18,10},{11,19},{19,11},{12,20... | collective-permute-start | bytes 49160 | tf_op jit(solution)/shard_map/ppermute | solution.py:30
  47.6 10.2 %collective-permute-start.16 = (f32[1,8,512]{2,1,0:T(8,128)S(1)}, f32[1,8,512]{2,1,0:T(8,128)S(1)}, u32[]{:S(2)}, u32[]{:S(2)}) collective-permute-start(f32[1,8,512]{2,1,0:T(8,128)S(1)} %get-tuple-element.9), channel_id=1, source_target_pairs={{0,8},{8,0},{16,24},{24,16},{1,9},{9,1},{17,25},{25,17},{2,10},{10... | collective-permute-start | bytes 49160 | tf_op jit(solution)/shard_map/ppermute | solution.py:29
  53.6 4.2 %collective-permute-start.19 = (f32[16,1,512]{2,1,0:T(1,128)S(1)}, f32[16,1,512]{2,1,0:T(1,128)S(1)}, u32[]{:S(2)}, u32[]{:S(2)}) collective-permute-start(f32[16,1,512]{2,1,0:T(1,128)S(1)} %bitcast.48), channel_id=1, source_target_pairs={{1,2},{2,1},{3,4},{4,3},{5,6},{6,5},{9,10},{10,9},{11,12},{12,11},... | collective-permute-start | bytes 98312 | tf_op jit(solution)/shard_map/ppermute | solution.py:30
  54.3 3.9 %collective-permute-start.18 = (f32[16,1,512]{2,1,0:T(1,128)S(1)}, f32[16,1,512]{2,1,0:T(1,128)S(1)}, u32[]{:S(2)}, u32[]{:S(2)}) collective-permute-start(f32[16,1,512]{2,1,0:T(1,128)S(1)} %get-tuple-element.14), channel_id=1, source_target_pairs={{0,1},{1,0},{2,3},{3,2},{4,5},{5,4},{6,7},{7,6},{8,9},{9,8},{10,11... | collective-permute-start | bytes 98312 | tf_op jit(solution)/shard_map/ppermute | solution.py:29
  57.7 1.6 %copy-start.7 = (f32[16,8,512]{2,1,0:T(8,128)}, f32[16,8,512]{2,1,0:T(8,128)S(1)}, u32[]{:S(2)}) copy-start(f32[16,8,512]{2,1,0:T(8,128)S(1)} %fusion.8.refs_3_.refs_4_) | copy-start | bytes 786436
  61.6 1.7 %collective-permute-start.20 = (f32[8,128]{1,0:T(8,128)}, f32[8,128]{1,0:T(8,128)S(1)}, u32[]{:S(2)}, u32[]{:S(2)}) collective-permute-start(f32[8,128]{1,0:T(8,128)} %shard_map.85), channel_id=1, source_target_pairs={{0,1},{1,0},{2,3},{3,2},{4,5},{5,4},{6,7},{7,6},{8,9},{9,8},{10,11... | collective-permute-start | bytes 12296 | tf_op jit(solution)/shard_map/ppermute | solution.py:75
  64.0 3.6 %collective-permute-start.21 = (f32[8,128]{1,0:T(8,128)S(1)}, f32[8,128]{1,0:T(8,128)S(1)}, u32[]{:S(2)}, u32[]{:S(2)}) collective-permute-start(f32[8,128]{1,0:T(8,128)S(1)} %add.562), channel_id=1, source_target_pairs={{0,2},{1,3},{2,0},{3,1},{4,6},{5,7},{6,4},{7,5},{8,10},{9,11},{10,... | collective-permute-start | bytes 12296 | tf_op jit(solution)/shard_map/ppermute | solution.py:75
  67.6 4.6 %collective-permute-start.22 = (f32[8,128]{1,0:T(8,128)S(1)}, f32[8,128]{1,0:T(8,128)S(1)}, u32[]{:S(2)}, u32[]{:S(2)}) collective-permute-start(f32[8,128]{1,0:T(8,128)S(1)} %add.563), channel_id=1, source_target_pairs={{0,4},{1,5},{2,6},{3,7},{4,0},{5,1},{6,2},{7,3},{8,12},{9,13},{10,... | collective-permute-start | bytes 12296 | tf_op jit(solution)/shard_map/ppermute | solution.py:75
  72.1 3.6 %collective-permute-start.23 = (f32[8,128]{1,0:T(8,128)S(1)}, f32[8,128]{1,0:T(8,128)S(1)}, u32[]{:S(2)}, u32[]{:S(2)}) collective-permute-start(f32[8,128]{1,0:T(8,128)S(1)} %add.564), channel_id=1, source_target_pairs={{0,8},{8,0},{16,24},{24,16},{1,9},{9,1},{17,25},{25,17},{2,10},{10... | collective-permute-start | bytes 12296 | tf_op jit(solution)/shard_map/ppermute | solution.py:75
  75.7 3.6 %collective-permute-start.24 = (f32[8,128]{1,0:T(8,128)S(1)}, f32[8,128]{1,0:T(8,128)S(1)}, u32[]{:S(2)}, u32[]{:S(2)}) collective-permute-start(f32[8,128]{1,0:T(8,128)S(1)} %add.565), channel_id=1, source_target_pairs={{0,16},{8,24},{16,0},{24,8},{1,17},{9,25},{17,1},{25,9},{2,18},{10... | collective-permute-start | bytes 12296 | tf_op jit(solution)/shard_map/ppermute | solution.py:75

commit v10 on v6

--- a/solution.py
+++ b/solution.py
@@ -72,10 +72,10 @@
     return x
 
 
-def gram_kernel(size, *refs):
-    basis_refs, out_ref = refs[:size], refs[size]
+def gram_kernel(size, pairs, count, *refs):
+    basis_refs, rest = refs[:count], refs[count:]
+    out_ref = rest[-1]
     tile = out_ref.shape
-    pairs = [(a, b) for a in range(size) for b in range(a, size)]
     planes, rows, lanes = basis_refs[0].shape
     chunks = lanes // tile[1]
 
@@ -91,7 +91,7 @@
     accs = lax.fori_loop(0, planes, plane, tuple(zero for _ in pairs))
     row_ids = lax.broadcasted_iota(jnp.int32, tile, 0)
     lane_ids = lax.broadcasted_iota(jnp.int32, tile, 1)
-    packed = jnp.zeros(tile, jnp.float32)
+    packed = rest[0][...] if len(rest) > 1 else jnp.zeros(tile, jnp.float32)
     for n, (a, b) in enumerate(pairs):
         total = jnp.sum(accs[n])
         hit = (lane_ids == 1 + a * size + b) | (lane_ids == 1 + b * size + a)
@@ -101,15 +101,15 @@
     out_ref[...] = packed
 
 
-def gram(basis):
-    size = len(basis)
+def gram(vectors, pairs, size, base=None):
     vmem = pl.BlockSpec(memory_space=pltpu.VMEM)
+    extra = [] if base is None else [base]
     return pl.pallas_call(
-        lambda *refs: gram_kernel(size, *refs),
+        lambda *refs: gram_kernel(size, pairs, len(vectors), *refs),
         out_shape=jax.ShapeDtypeStruct((8, 128), jnp.float32),
-        in_specs=[vmem] * size,
+        in_specs=[vmem] * (len(vectors) + len(extra)),
         out_specs=vmem,
-    )(*basis)
+    )(*vectors, *extra)
 
 
 def finish_kernel(cells, size, stats_ref, *refs):
@@ -212,10 +212,13 @@
     vector = residual0
     basis = [vector]
     for step in range(STEPS):
+        if step == STEPS - 1:
+            early = [(a, b) for a in range(STEPS) for b in range(a, STEPS)]
+            stats = gram(basis, early, STEPS + 1)
         total = neighbour_sum(vector, field_halo(vector), coef)
         vector = 2.0 * total / diagonal
         basis.append(vector)
-    stats = gram(basis)
+    stats = gram(basis, [(a, STEPS) for a in range(STEPS + 1)], STEPS + 1, stats)
     stats = all_sum(stats)
     ortho, upper, scale = finish(stats, basis, cells)
     return (ortho, upper, scale)

time: 79.3 us -> 80 us (level)
  Pallas kernels: 5.06 us -> 7.03 us
  starting transfers between devices: 47.6 us -> 46.3 us
    pallas_call x1 -> x2, Pallas kernels: 2.31 us -> 4.27 us  [gram(): pl.pallas_call(lambda *refs: gram_kernel(size, pairs, len(vectors), *refs...]
    ppermute x10, starting transfers between devices: 35.2 us -> 34.1 us  [axis_exchange(): lax.ppermute(jnp.where(odd, to_low, to_high), axis, swap_pairs(axis, 0))]
  transfers between devices with their start and end apart: 25 -> 25, of which waited for: 9 -> 9; matrix products, arithmetic and copies ran while one was open for 4% -> 4% of each run, Pallas kernels for 0% -> 3%
where the time goes in v10:
time: 80 us; the launch traced here: 79.4 us
  starting transfers between devices  46.3 us (58%)
  waiting for transfers between devices  14.8 us (18%)
  Pallas kernels  7.03 us (9%)
  local copies, waits for them, and re-layouts  5.3 us (7%)
  other arithmetic  4.76 us (6%)
  between operations  1.18 us (1%)
    ppermute x10, starting transfers between devices, axis_exchange(): lax.ppermute(jnp.where(odd, to_low, to_high), axis, swap_pairs(axis, 0))  34.1 us
    ppermute x5, waiting for transfers between devices, all_sum(): x = x + lax.ppermute(x, axis, [(i, i ^ step) for i in range(n)])  11.4 us
    ppermute x10, starting transfers between devices, axis_exchange(): lax.ppermute(jnp.where(odd, to_high, to_low), axis, swap_pairs(axis, 1))  6.62 us
    ppermute x5, starting transfers between devices, all_sum(): x = x + lax.ppermute(x, axis, [(i, i ^ step) for i in range(n)])  5.63 us
    pallas_call x2, Pallas kernels, gram(): pl.pallas_call(lambda *refs: gram_kernel(size, pairs, len(vectors), *refs...  4.27 us
    ppermute x10, waiting for transfers between devices, axis_exchange(): lax.ppermute(jnp.where(odd, to_low, to_high), axis, swap_pairs(axis, 0))  3.35 us
    pallas_call x1, Pallas kernels, finish(): pl.pallas_call(lambda *refs: finish_kernel(float(cells), size, *refs), ou...  2.75 us
    div x4, other arithmetic, local(): vector = 2.0 * total / diagonal  2.51 us
  transfers between devices with their start and end apart: 25, of which 9 were waited for; matrix products, arithmetic and copies ran while one was open for 4% of the time, Pallas kernels for 3%

profile of v10, /device:TPU:0, one launch (start us, length us, event | category | flops | bytes accessed | tf_op | source)
XLA Modules:
  0.0 79.4 jit_solution(9683219847648027738)
XLA Ops:
  0.6 0.0 copy-start.4
  0.7 0.8 %fusion.54 = (f32[1,8,512]{2,1,0:T(8,128)S(1)}, f32[1,8,512]{2,1,0:T(8,128)S(1)}, f32[1,8,512]{2,1,0:T(8,128)S(1)}, f32[1,8,512]{2,1,0:T(8,128)S(1)}) fusion(f32[16,8,512]{2,1,0:T(8,128)} %param.6, f32[16,8,512]{2,1,0:T(8,128)} %param.9), kind=kLoop, calls=%fused_computation.119 | loop fusion | bytes 131072 | tf_op jit(solution)/shard_map/slice | solution.py:192
  1.5 0.7 collective-permute-start
  2.1 5.7 %collective-permute-start.1 = (f32[2,8,512]{2,1,0:T(8,128)S(1)}, f32[2,8,512]{2,1,0:T(8,128)S(1)}, u32[]{:S(2)}, u32[]{:S(2)}) collective-permute-start(f32[2,8,512]{2,1,0:T(8,128)S(1)} %get-tuple-element.75), channel_id=1, source_target_pairs={{0,8},{8,0},{16,24},{24,16},{1,9},{9,1},{17,25},{25,17},{2,10},{10... | collective-permute-start | bytes 98312 | tf_op jit(solution)/shard_map/ppermute | solution.py:29
  7.9 1.3 %fusion.51 = (f32[16,1,512]{2,1,0:T(1,128)S(1)}, f32[16,1,512]{2,1,0:T(1,128)S(1)}, f32[16,1,512]{2,1,0:T(1,128)S(1)}, f32[16,1,512]{2,1,0:T(1,128)S(1)}) fusion(f32[16,8,512]{2,1,0:T(8,128)} %param.6, f32[16,8,512]{2,1,0:T(8,128)} %param.10), kind=kLoop, calls=%fused_computation.116 | loop fusion | bytes 262144 | tf_op jit(solution)/shard_map/slice | solution.py:194
  9.2 0.1 broadcast_select_fusion.18
  9.3 0.7 collective-permute-start.2
  10.0 3.0 %collective-permute-start.3 = (f32[16,2,512]{2,1,0:T(2,128)S(1)}, f32[16,2,512]{2,1,0:T(2,128)S(1)}, u32[]{:S(2)}, u32[]{:S(2)}) collective-permute-start(f32[16,2,512]{2,1,0:T(2,128)S(1)} %get-tuple-element.63), channel_id=1, source_target_pairs={{0,1},{1,0},{2,3},{3,2},{4,5},{5,4},{6,7},{7,6},{8,9},{9,8},{10,11... | collective-permute-start | bytes 196616 | tf_op jit(solution)/shard_map/ppermute | solution.py:29
  13.0 1.1 %fusion.50 = (f32[16,7,512]{2,1,0:T(8,128)S(1)}, f32[16,7,512]{2,1,0:T(8,128)S(1)}) fusion(f32[16,8,512]{2,1,0:T(8,128)} %param.6), kind=kLoop, calls=%fused_computation.115 | loop fusion | bytes 917504 | tf_op jit(solution)/shard_map/slice | solution.py:49
  14.1 0.0 copy-start.5
  14.1 0.1 fusion.49
  14.3 0.1 fusion.53
  14.4 0.7 copy-done.5
  15.1 0.1 copy-done.7
  15.1 0.1 slice.201
  15.4 0.1 fusion.56
  15.5 0.5 fusion.6.refs_0_.refs_1_
  16.0 0.1 fusion.48
  16.1 0.1 fusion.46
  16.3 0.7 collective-permute-start.5
  16.9 2.8 %collective-permute-start.4 = (f32[1,8,512]{2,1,0:T(8,128)S(1)}, f32[1,8,512]{2,1,0:T(8,128)S(1)}, u32[]{:S(2)}, u32[]{:S(2)}) collective-permute-start(f32[1,8,512]{2,1,0:T(8,128)S(1)} %get-tuple-element.48), channel_id=1, source_target_pairs={{0,8},{8,0},{16,24},{24,16},{1,9},{9,1},{17,25},{25,17},{2,10},{10... | collective-permute-start | bytes 49160 | tf_op jit(solution)/shard_map/ppermute | solution.py:29
  19.8 0.7 collective-permute-start.7
  20.4 3.0 %collective-permute-start.6 = (f32[16,1,512]{2,1,0:T(1,128)S(1)}, f32[16,1,512]{2,1,0:T(1,128)S(1)}, u32[]{:S(2)}, u32[]{:S(2)}) collective-permute-start(f32[16,1,512]{2,1,0:T(1,128)S(1)} %get-tuple-element.44), channel_id=1, source_target_pairs={{0,1},{1,0},{2,3},{3,2},{4,5},{5,4},{6,7},{7,6},{8,9},{9,8},{10,11... | collective-permute-start | bytes 98312 | tf_op jit(solution)/shard_map/ppermute | solution.py:29
  23.5 0.8 %collective-permute-done.6 = f32[16,1,512]{2,1,0:T(1,128)S(1)} collective-permute-done((f32[16,1,512]{2,1,0:T(1,128)S(1)}, f32[16,1,512]{2,1,0:T(1,128)S(1)}, u32[]{:S(2)}, u32[]{:S(2)}) %collective-permute-start.6) | collective-permute-done | bytes 32800 | tf_op jit(solution)/shard_map/ppermute | solution.py:29
  24.3 0.5 fusion.13.refs_1_.refs_2_
  24.9 0.1 fusion.44
  24.9 0.1 fusion.43
  25.1 0.7 collective-permute-start.9
  25.7 2.9 %collective-permute-start.8 = (f32[1,8,512]{2,1,0:T(8,128)S(1)}, f32[1,8,512]{2,1,0:T(8,128)S(1)}, u32[]{:S(2)}, u32[]{:S(2)}) collective-permute-start(f32[1,8,512]{2,1,0:T(8,128)S(1)} %get-tuple-element.38), channel_id=1, source_target_pairs={{0,8},{8,0},{16,24},{24,16},{1,9},{9,1},{17,25},{25,17},{2,10},{10... | collective-permute-start | bytes 49160 | tf_op jit(solution)/shard_map/ppermute | solution.py:29
  28.6 0.7 collective-permute-start.11
  29.3 3.7 %collective-permute-start.10 = (f32[16,1,512]{2,1,0:T(1,128)S(1)}, f32[16,1,512]{2,1,0:T(1,128)S(1)}, u32[]{:S(2)}, u32[]{:S(2)}) collective-permute-start(f32[16,1,512]{2,1,0:T(1,128)S(1)} %get-tuple-element.34), channel_id=1, source_target_pairs={{0,1},{1,0},{2,3},{3,2},{4,5},{5,4},{6,7},{7,6},{8,9},{9,8},{10,11... | collective-permute-start | bytes 98312 | tf_op jit(solution)/shard_map/ppermute | solution.py:29
  33.0 0.8 %collective-permute-done.10 = f32[16,1,512]{2,1,0:T(1,128)S(1)} collective-permute-done((f32[16,1,512]{2,1,0:T(1,128)S(1)}, f32[16,1,512]{2,1,0:T(1,128)S(1)}, u32[]{:S(2)}, u32[]{:S(2)}) %collective-permute-start.10) | collective-permute-done | bytes 32800 | tf_op jit(solution)/shard_map/ppermute | solution.py:29
  33.9 0.5 fusion.20.refs_2_.refs_3_
  34.4 0.1 fusion.41
  34.4 0.1 fusion.40
  34.6 0.7 collective-permute-start.13
  35.3 2.8 %collective-permute-start.12 = (f32[1,8,512]{2,1,0:T(8,128)S(1)}, f32[1,8,512]{2,1,0:T(8,128)S(1)}, u32[]{:S(2)}, u32[]{:S(2)}) collective-permute-start(f32[1,8,512]{2,1,0:T(8,128)S(1)} %get-tuple-element.28), channel_id=1, source_target_pairs={{0,8},{8,0},{16,24},{24,16},{1,9},{9,1},{17,25},{25,17},{2,10},{10... | collective-permute-start | bytes 49160 | tf_op jit(solution)/shard_map/ppermute | solution.py:29
  38.1 0.7 collective-permute-start.15
  38.8 3.7 %collective-permute-start.14 = (f32[16,1,512]{2,1,0:T(1,128)S(1)}, f32[16,1,512]{2,1,0:T(1,128)S(1)}, u32[]{:S(2)}, u32[]{:S(2)}) collective-permute-start(f32[16,1,512]{2,1,0:T(1,128)S(1)} %get-tuple-element.24), channel_id=1, source_target_pairs={{0,1},{1,0},{2,3},{3,2},{4,5},{5,4},{6,7},{7,6},{8,9},{9,8},{10,11... | collective-permute-start | bytes 98312 | tf_op jit(solution)/shard_map/ppermute | solution.py:29
  42.5 0.8 %collective-permute-done.14 = f32[16,1,512]{2,1,0:T(1,128)S(1)} collective-permute-done((f32[16,1,512]{2,1,0:T(1,128)S(1)}, f32[16,1,512]{2,1,0:T(1,128)S(1)}, u32[]{:S(2)}, u32[]{:S(2)}) %collective-permute-start.14) | collective-permute-done | bytes 32800 | tf_op jit(solution)/shard_map/ppermute | solution.py:29
  43.3 0.5 fusion.27.refs_3_.refs_4_
  43.8 0.1 fusion.39
  43.9 0.1 fusion.38
  43.9 0.1 fusion.37
  44.1 0.7 collective-permute-start.17
  44.7 2.9 %collective-permute-start.16 = (f32[1,8,512]{2,1,0:T(8,128)S(1)}, f32[1,8,512]{2,1,0:T(8,128)S(1)}, u32[]{:S(2)}, u32[]{:S(2)}) collective-permute-start(f32[1,8,512]{2,1,0:T(8,128)S(1)} %get-tuple-element.18), channel_id=1, source_target_pairs={{0,8},{8,0},{16,24},{24,16},{1,9},{9,1},{17,25},{25,17},{2,10},{10... | collective-permute-start | bytes 49160 | tf_op jit(solution)/shard_map/ppermute | solution.py:29
  47.7 2.1 %shard_map.85.refs_5_ = f32[8,128]{1,0:T(8,128)} custom-call(f32[16,8,512]{2,1,0:T(8,128)} %copy-done.3, f32[16,8,512]{2,1,0:T(8,128)} %copy-done, f32[16,8,512]{2,1,0:T(8,128)} %copy-done.1, f32[16,8,512]{2,1,0:T(8,128)} %copy-done.2), custom_call_target="tpu_custom_call" | custom-call | tf_op jit(solution)/shard_map/pallas_call | solution.py:107
  49.8 0.7 collective-permute-start.19
  50.4 3.7 %collective-permute-start.18 = (f32[16,1,512]{2,1,0:T(1,128)S(1)}, f32[16,1,512]{2,1,0:T(1,128)S(1)}, u32[]{:S(2)}, u32[]{:S(2)}) collective-permute-start(f32[16,1,512]{2,1,0:T(1,128)S(1)} %get-tuple-element.14), channel_id=1, source_target_pairs={{0,1},{1,0},{2,3},{3,2},{4,5},{5,4},{6,7},{7,6},{8,9},{9,8},{10,11... | collective-permute-start | bytes 98312 | tf_op jit(solution)/shard_map/ppermute | solution.py:29
  54.2 0.8 %collective-permute-done.18 = f32[16,1,512]{2,1,0:T(1,128)S(1)} collective-permute-done((f32[16,1,512]{2,1,0:T(1,128)S(1)}, f32[16,1,512]{2,1,0:T(1,128)S(1)}, u32[]{:S(2)}, u32[]{:S(2)}) %collective-permute-start.18) | collective-permute-done | bytes 32800 | tf_op jit(solution)/shard_map/ppermute | solution.py:29
  55.0 1.2 %fusion.34.refs_4_.refs_5_ = f32[16,8,512]{2,1,0:T(8,128)} fusion(f32[16,8,512]{2,1,0:T(8,128)S(1)} %copy-done.6, f32[15,8,512]{2,1,0:T(8,128)S(1)} %get-tuple-element.16, f32[1,8,512]{2,1,0:T(8,128)S(1)} %get-tuple-element.78, f32[1,8,512]{2,1,0:T(8,128)S(1)} %get-tuple-element.77, f32[15,8,512]{2,1,0:T(8,128)S(1)} %get-tuple-element.15, ...), kind=kLoop, calls=%fused_computation.53 | loop fusion | flops 1638400 | bytes 3668480 | tf_op jit(solution)/shard_map/div | solution.py:219
  56.1 2.1 %shard_map.86 = f32[8,128]{1,0:T(8,128)} custom-call(f32[16,8,512]{2,1,0:T(8,128)} %copy-done.3, f32[16,8,512]{2,1,0:T(8,128)} %copy-done, f32[16,8,512]{2,1,0:T(8,128)} %copy-done.1, f32[16,8,512]{2,1,0:T(8,128)} %copy-done.2, f32[16,8,512]{2,1,0:T(8,128)} %fusion.34.refs_4_.refs_5_, f32[8,128]{1,0:T(8,128)} %shard_map.85.refs_5_), custom_call_target="tpu_custom_call" | custom-call | tf_op jit(solution)/shard_map/pallas_call | solution.py:107
  58.3 0.7 collective-permute-start.20
  59.0 1.0 %collective-permute-done.20 = f32[8,128]{1,0:T(8,128)S(1)} collective-permute-done((f32[8,128]{1,0:T(8,128)}, f32[8,128]{1,0:T(8,128)S(1)}, u32[]{:S(2)}, u32[]{:S(2)}) %collective-permute-start.20) | collective-permute-done | bytes 4128 | tf_op jit(solution)/shard_map/ppermute | solution.py:70
  60.0 0.7 add.178
  60.7 2.0 %collective-permute-start.21 = (f32[8,128]{1,0:T(8,128)S(1)}, f32[8,128]{1,0:T(8,128)S(1)}, u32[]{:S(2)}, u32[]{:S(2)}) collective-permute-start(f32[8,128]{1,0:T(8,128)S(1)} %add.178), channel_id=1, source_target_pairs={{0,2},{1,3},{2,0},{3,1},{4,6},{5,7},{6,4},{7,5},{8,10},{9,11},{10,... | collective-permute-start | bytes 12296 | tf_op jit(solution)/shard_map/ppermute | solution.py:70
  62.7 1.6 %collective-permute-done.21 = f32[8,128]{1,0:T(8,128)S(1)} collective-permute-done((f32[8,128]{1,0:T(8,128)S(1)}, f32[8,128]{1,0:T(8,128)S(1)}, u32[]{:S(2)}, u32[]{:S(2)}) %collective-permute-start.21) | collective-permute-done | bytes 4128 | tf_op jit(solution)/shard_map/ppermute | solution.py:70
  64.3 3.0 %collective-permute-start.22 = (f32[8,128]{1,0:T(8,128)S(1)}, f32[8,128]{1,0:T(8,128)S(1)}, u32[]{:S(2)}, u32[]{:S(2)}) collective-permute-start(f32[8,128]{1,0:T(8,128)S(1)} %add.179), channel_id=1, source_target_pairs={{0,4},{1,5},{2,6},{3,7},{4,0},{5,1},{6,2},{7,3},{8,12},{9,13},{10,... | collective-permute-start | bytes 12296 | tf_op jit(solution)/shard_map/ppermute | solution.py:70
  67.3 1.6 %collective-permute-done.22 = f32[8,128]{1,0:T(8,128)S(1)} collective-permute-done((f32[8,128]{1,0:T(8,128)S(1)}, f32[8,128]{1,0:T(8,128)S(1)}, u32[]{:S(2)}, u32[]{:S(2)}) %collective-permute-start.22) | collective-permute-done | bytes 4128 | tf_op jit(solution)/shard_map/ppermute | solution.py:70
  68.9 0.0 collective-permute-start.23
  68.9 3.6 %collective-permute-done.23 = f32[8,128]{1,0:T(8,128)S(1)} collective-permute-done((f32[8,128]{1,0:T(8,128)S(1)}, f32[8,128]{1,0:T(8,128)S(1)}, u32[]{:S(2)}, u32[]{:S(2)}) %collective-permute-start.23) | collective-permute-done | bytes 4128 | tf_op jit(solution)/shard_map/ppermute | solution.py:70
  72.5 3.6 %collective-permute-done.24 = f32[8,128]{1,0:T(8,128)S(1)} collective-permute-done((f32[8,128]{1,0:T(8,128)S(1)}, f32[8,128]{1,0:T(8,128)S(1)}, u32[]{:S(2)}, u32[]{:S(2)}) %collective-permute-start.24) | collective-permute-done | bytes 4128 | tf_op jit(solution)/shard_map/ppermute | solution.py:70
  76.1 0.6 add.182.refs_0_
  76.7 2.8 %shard_map.87 = (f32[5,16,8,512]{3,2,1,0:T(8,128)}, f32[5,5]{1,0:T(8,128)}, f32[1,1]{1,0:T(1,128)}) custom-call(f32[8,128]{1,0:T(8,128)} %add.182.refs_0_, f32[16,8,512]{2,1,0:T(8,128)} %copy-done.3, f32[16,8,512]{2,1,0:T(8,128)} %copy-done, f32[16,8,512]{2,1,0:T(8,128)} %copy-done.1, f32[16,8,512]{2,1,0:T(8,128)} %copy-done.2, ...), custom_call_target="tpu_custom_call" | custom-call | tf_op jit(solution)/shard_map/pallas_call | solution.py:173
  (63 shorter events, 0.6 us)
Async XLA Ops:
  0.6 13.5 %copy-start.4 = (f32[16,8,512]{2,1,0:T(8,128)S(1)}, f32[16,8,512]{2,1,0:T(8,128)}, u32[]{:S(2)}) copy-start(f32[16,8,512]{2,1,0:T(8,128)} %param.6) | copy-start | bytes 786436
  1.5 13.8 %collective-permute-start = (f32[2,8,512]{2,1,0:T(8,128)S(1)}, f32[2,8,512]{2,1,0:T(8,128)S(1)}, u32[]{:S(2)}, u32[]{:S(2)}) collective-permute-start(f32[2,8,512]{2,1,0:T(8,128)S(1)} %get-tuple-element.76), channel_id=1, source_target_pairs={{8,16},{16,8},{9,17},{17,9},{10,18},{18,10},{11,19},{19,11},{12,20... | collective-permute-start | bytes 98312 | tf_op jit(solution)/shard_map/ppermute | solution.py:30
  2.1 13.1 %collective-permute-start.1 = (f32[2,8,512]{2,1,0:T(8,128)S(1)}, f32[2,8,512]{2,1,0:T(8,128)S(1)}, u32[]{:S(2)}, u32[]{:S(2)}) collective-permute-start(f32[2,8,512]{2,1,0:T(8,128)S(1)} %get-tuple-element.75), channel_id=1, source_target_pairs={{0,8},{8,0},{16,24},{24,16},{1,9},{9,1},{17,25},{25,17},{2,10},{10... | collective-permute-start | bytes 98312 | tf_op jit(solution)/shard_map/ppermute | solution.py:29
  9.3 6.0 %collective-permute-start.2 = (f32[16,2,512]{2,1,0:T(2,128)S(1)}, f32[16,2,512]{2,1,0:T(2,128)S(1)}, u32[]{:S(2)}, u32[]{:S(2)}) collective-permute-start(f32[16,2,512]{2,1,0:T(2,128)S(1)} %get-tuple-element.64), channel_id=1, source_target_pairs={{1,2},{2,1},{3,4},{4,3},{5,6},{6,5},{9,10},{10,9},{11,12},{12,11},... | collective-permute-start | bytes 196616 | tf_op jit(solution)/shard_map/ppermute | solution.py:30
  10.0 4.3 %copy-start.6 = (f32[16,8,512]{2,1,0:T(8,128)S(1)}, f32[16,8,512]{2,1,0:T(8,128)}, u32[]{:S(2)}) copy-start(f32[16,8,512]{2,1,0:T(8,128)} %param.9) | copy-start | bytes 786436
  10.0 5.3 %collective-permute-start.3 = (f32[16,2,512]{2,1,0:T(2,128)S(1)}, f32[16,2,512]{2,1,0:T(2,128)S(1)}, u32[]{:S(2)}, u32[]{:S(2)}) collective-permute-start(f32[16,2,512]{2,1,0:T(2,128)S(1)} %get-tuple-element.63), channel_id=1, source_target_pairs={{0,1},{1,0},{2,3},{3,2},{4,5},{5,4},{6,7},{7,6},{8,9},{9,8},{10,11... | collective-permute-start | bytes 196616 | tf_op jit(solution)/shard_map/ppermute | solution.py:29
  14.1 1.0 %copy-start.5 = (f32[16,8,512]{2,1,0:T(8,128)S(1)}, f32[16,8,512]{2,1,0:T(8,128)}, u32[]{:S(2)}) copy-start(f32[16,8,512]{2,1,0:T(8,128)} %param.10) | copy-start | bytes 786436
  14.1 1.0 %copy-start.7 = (f32[16,8,512]{2,1,0:T(8,128)S(1)}, f32[16,8,512]{2,1,0:T(8,128)}, u32[]{:S(2)}) copy-start(f32[16,8,512]{2,1,0:T(8,128)} %param.11) | copy-start | bytes 786436
  14.3 1.1 %copy-start.8 = (f32[16,8,512]{2,1,0:T(8,128)S(1)}, f32[16,8,512]{2,1,0:T(8,128)}, u32[]{:S(2)}) copy-start(f32[16,8,512]{2,1,0:T(8,128)} %param.8) | copy-start | bytes 786436
  14.3 1.1 %copy-start.9 = (f32[16,8,512]{2,1,0:T(8,128)S(1)}, f32[16,8,512]{2,1,0:T(8,128)}, u32[]{:S(2)}) copy-start(f32[16,8,512]{2,1,0:T(8,128)} %param.7) | copy-start | bytes 786436
  16.0 3.7 %copy-start.3 = (f32[16,8,512]{2,1,0:T(8,128)}, f32[16,8,512]{2,1,0:T(8,128)S(1)}, u32[]{:S(2)}) copy-start(f32[16,8,512]{2,1,0:T(8,128)S(1)} %fusion.6.refs_0_.refs_1_) | copy-start | bytes 786436
  16.3 7.2 %collective-permute-start.5 = (f32[1,8,512]{2,1,0:T(8,128)S(1)}, f32[1,8,512]{2,1,0:T(8,128)S(1)}, u32[]{:S(2)}, u32[]{:S(2)}) collective-permute-start(f32[1,8,512]{2,1,0:T(8,128)S(1)} %get-tuple-element.47), channel_id=1, source_target_pairs={{8,16},{16,8},{9,17},{17,9},{10,18},{18,10},{11,19},{19,11},{12,20... | collective-permute-start | bytes 49160 | tf_op jit(solution)/shard_map/ppermute | solution.py:30
  16.9 6.5 %collective-permute-start.4 = (f32[1,8,512]{2,1,0:T(8,128)S(1)}, f32[1,8,512]{2,1,0:T(8,128)S(1)}, u32[]{:S(2)}, u32[]{:S(2)}) collective-permute-start(f32[1,8,512]{2,1,0:T(8,128)S(1)} %get-tuple-element.48), channel_id=1, source_target_pairs={{0,8},{8,0},{16,24},{24,16},{1,9},{9,1},{17,25},{25,17},{2,10},{10... | collective-permute-start | bytes 49160 | tf_op jit(solution)/shard_map/ppermute | solution.py:29
  19.8 3.7 %collective-permute-start.7 = (f32[16,1,512]{2,1,0:T(1,128)S(1)}, f32[16,1,512]{2,1,0:T(1,128)S(1)}, u32[]{:S(2)}, u32[]{:S(2)}) collective-permute-start(f32[16,1,512]{2,1,0:T(1,128)S(1)} %get-tuple-element.43), channel_id=1, source_target_pairs={{1,2},{2,1},{3,4},{4,3},{5,6},{6,5},{9,10},{10,9},{11,12},{12,11},... | collective-permute-start | bytes 98312 | tf_op jit(solution)/shard_map/ppermute | solution.py:30
  20.4 3.9 %collective-permute-start.6 = (f32[16,1,512]{2,1,0:T(1,128)S(1)}, f32[16,1,512]{2,1,0:T(1,128)S(1)}, u32[]{:S(2)}, u32[]{:S(2)}) collective-permute-start(f32[16,1,512]{2,1,0:T(1,128)S(1)} %get-tuple-element.44), channel_id=1, source_target_pairs={{0,1},{1,0},{2,3},{3,2},{4,5},{5,4},{6,7},{7,6},{8,9},{9,8},{10,11... | collective-permute-start | bytes 98312 | tf_op jit(solution)/shard_map/ppermute | solution.py:29
  24.8 3.8 %copy-start = (f32[16,8,512]{2,1,0:T(8,128)}, f32[16,8,512]{2,1,0:T(8,128)S(1)}, u32[]{:S(2)}) copy-start(f32[16,8,512]{2,1,0:T(8,128)S(1)} %fusion.13.refs_1_.refs_2_) | copy-start | bytes 786436
  25.1 7.9 %collective-permute-start.9 = (f32[1,8,512]{2,1,0:T(8,128)S(1)}, f32[1,8,512]{2,1,0:T(8,128)S(1)}, u32[]{:S(2)}, u32[]{:S(2)}) collective-permute-start(f32[1,8,512]{2,1,0:T(8,128)S(1)} %get-tuple-element.37), channel_id=1, source_target_pairs={{8,16},{16,8},{9,17},{17,9},{10,18},{18,10},{11,19},{19,11},{12,20... | collective-permute-start | bytes 49160 | tf_op jit(solution)/shard_map/ppermute | solution.py:30
  25.7 7.3 %collective-permute-start.8 = (f32[1,8,512]{2,1,0:T(8,128)S(1)}, f32[1,8,512]{2,1,0:T(8,128)S(1)}, u32[]{:S(2)}, u32[]{:S(2)}) collective-permute-start(f32[1,8,512]{2,1,0:T(8,128)S(1)} %get-tuple-element.38), channel_id=1, source_target_pairs={{0,8},{8,0},{16,24},{24,16},{1,9},{9,1},{17,25},{25,17},{2,10},{10... | collective-permute-start | bytes 49160 | tf_op jit(solution)/shard_map/ppermute | solution.py:29
  28.6 4.4 %collective-permute-start.11 = (f32[16,1,512]{2,1,0:T(1,128)S(1)}, f32[16,1,512]{2,1,0:T(1,128)S(1)}, u32[]{:S(2)}, u32[]{:S(2)}) collective-permute-start(f32[16,1,512]{2,1,0:T(1,128)S(1)} %get-tuple-element.33), channel_id=1, source_target_pairs={{1,2},{2,1},{3,4},{4,3},{5,6},{6,5},{9,10},{10,9},{11,12},{12,11},... | collective-permute-start | bytes 98312 | tf_op jit(solution)/shard_map/ppermute | solution.py:30
  29.3 4.5 %collective-permute-start.10 = (f32[16,1,512]{2,1,0:T(1,128)S(1)}, f32[16,1,512]{2,1,0:T(1,128)S(1)}, u32[]{:S(2)}, u32[]{:S(2)}) collective-permute-start(f32[16,1,512]{2,1,0:T(1,128)S(1)} %get-tuple-element.34), channel_id=1, source_target_pairs={{0,1},{1,0},{2,3},{3,2},{4,5},{5,4},{6,7},{7,6},{8,9},{9,8},{10,11... | collective-permute-start | bytes 98312 | tf_op jit(solution)/shard_map/ppermute | solution.py:29
  34.3 3.8 %copy-start.1 = (f32[16,8,512]{2,1,0:T(8,128)}, f32[16,8,512]{2,1,0:T(8,128)S(1)}, u32[]{:S(2)}) copy-start(f32[16,8,512]{2,1,0:T(8,128)S(1)} %fusion.20.refs_2_.refs_3_) | copy-start | bytes 786436
  34.6 7.9 %collective-permute-start.13 = (f32[1,8,512]{2,1,0:T(8,128)S(1)}, f32[1,8,512]{2,1,0:T(8,128)S(1)}, u32[]{:S(2)}, u32[]{:S(2)}) collective-permute-start(f32[1,8,512]{2,1,0:T(8,128)S(1)} %get-tuple-element.27), channel_id=1, source_target_pairs={{8,16},{16,8},{9,17},{17,9},{10,18},{18,10},{11,19},{19,11},{12,20... | collective-permute-start | bytes 49160 | tf_op jit(solution)/shard_map/ppermute | solution.py:30
  35.3 7.2 %collective-permute-start.12 = (f32[1,8,512]{2,1,0:T(8,128)S(1)}, f32[1,8,512]{2,1,0:T(8,128)S(1)}, u32[]{:S(2)}, u32[]{:S(2)}) collective-permute-start(f32[1,8,512]{2,1,0:T(8,128)S(1)} %get-tuple-element.28), channel_id=1, source_target_pairs={{0,8},{8,0},{16,24},{24,16},{1,9},{9,1},{17,25},{25,17},{2,10},{10... | collective-permute-start | bytes 49160 | tf_op jit(solution)/shard_map/ppermute | solution.py:29
  38.1 4.4 %collective-permute-start.15 = (f32[16,1,512]{2,1,0:T(1,128)S(1)}, f32[16,1,512]{2,1,0:T(1,128)S(1)}, u32[]{:S(2)}, u32[]{:S(2)}) collective-permute-start(f32[16,1,512]{2,1,0:T(1,128)S(1)} %get-tuple-element.23), channel_id=1, source_target_pairs={{1,2},{2,1},{3,4},{4,3},{5,6},{6,5},{9,10},{10,9},{11,12},{12,11},... | collective-permute-start | bytes 98312 | tf_op jit(solution)/shard_map/ppermute | solution.py:30
  38.8 4.5 %collective-permute-start.14 = (f32[16,1,512]{2,1,0:T(1,128)S(1)}, f32[16,1,512]{2,1,0:T(1,128)S(1)}, u32[]{:S(2)}, u32[]{:S(2)}) collective-permute-start(f32[16,1,512]{2,1,0:T(1,128)S(1)} %get-tuple-element.24), channel_id=1, source_target_pairs={{0,1},{1,0},{2,3},{3,2},{4,5},{5,4},{6,7},{7,6},{8,9},{9,8},{10,11... | collective-permute-start | bytes 98312 | tf_op jit(solution)/shard_map/ppermute | solution.py:29
  43.8 3.8 %copy-start.2 = (f32[16,8,512]{2,1,0:T(8,128)}, f32[16,8,512]{2,1,0:T(8,128)S(1)}, u32[]{:S(2)}) copy-start(f32[16,8,512]{2,1,0:T(8,128)S(1)} %fusion.27.refs_3_.refs_4_) | copy-start | bytes 786436
  44.1 10.1 %collective-permute-start.17 = (f32[1,8,512]{2,1,0:T(8,128)S(1)}, f32[1,8,512]{2,1,0:T(8,128)S(1)}, u32[]{:S(2)}, u32[]{:S(2)}) collective-permute-start(f32[1,8,512]{2,1,0:T(8,128)S(1)} %get-tuple-element.17), channel_id=1, source_target_pairs={{8,16},{16,8},{9,17},{17,9},{10,18},{18,10},{11,19},{19,11},{12,20... | collective-permute-start | bytes 49160 | tf_op jit(solution)/shard_map/ppermute | solution.py:30
  44.7 9.4 %collective-permute-start.16 = (f32[1,8,512]{2,1,0:T(8,128)S(1)}, f32[1,8,512]{2,1,0:T(8,128)S(1)}, u32[]{:S(2)}, u32[]{:S(2)}) collective-permute-start(f32[1,8,512]{2,1,0:T(8,128)S(1)} %get-tuple-element.18), channel_id=1, source_target_pairs={{0,8},{8,0},{16,24},{24,16},{1,9},{9,1},{17,25},{25,17},{2,10},{10... | collective-permute-start | bytes 49160 | tf_op jit(solution)/shard_map/ppermute | solution.py:29
  49.8 4.4 %collective-permute-start.19 = (f32[16,1,512]{2,1,0:T(1,128)S(1)}, f32[16,1,512]{2,1,0:T(1,128)S(1)}, u32[]{:S(2)}, u32[]{:S(2)}) collective-permute-start(f32[16,1,512]{2,1,0:T(1,128)S(1)} %get-tuple-element.13), channel_id=1, source_target_pairs={{1,2},{2,1},{3,4},{4,3},{5,6},{6,5},{9,10},{10,9},{11,12},{12,11},... | collective-permute-start | bytes 98312 | tf_op jit(solution)/shard_map/ppermute | solution.py:30
  50.4 4.5 %collective-permute-start.18 = (f32[16,1,512]{2,1,0:T(1,128)S(1)}, f32[16,1,512]{2,1,0:T(1,128)S(1)}, u32[]{:S(2)}, u32[]{:S(2)}) collective-permute-start(f32[16,1,512]{2,1,0:T(1,128)S(1)} %get-tuple-element.14), channel_id=1, source_target_pairs={{0,1},{1,0},{2,3},{3,2},{4,5},{5,4},{6,7},{7,6},{8,9},{9,8},{10,11... | collective-permute-start | bytes 98312 | tf_op jit(solution)/shard_map/ppermute | solution.py:29
  58.3 1.7 %collective-permute-start.20 = (f32[8,128]{1,0:T(8,128)}, f32[8,128]{1,0:T(8,128)S(1)}, u32[]{:S(2)}, u32[]{:S(2)}) collective-permute-start(f32[8,128]{1,0:T(8,128)} %shard_map.86), channel_id=1, source_target_pairs={{0,1},{1,0},{2,3},{3,2},{4,5},{5,4},{6,7},{7,6},{8,9},{9,8},{10,11... | collective-permute-start | bytes 12296 | tf_op jit(solution)/shard_map/ppermute | solution.py:70
  60.7 3.6 %collective-permute-start.21 = (f32[8,128]{1,0:T(8,128)S(1)}, f32[8,128]{1,0:T(8,128)S(1)}, u32[]{:S(2)}, u32[]{:S(2)}) collective-permute-start(f32[8,128]{1,0:T(8,128)S(1)} %add.178), channel_id=1, source_target_pairs={{0,2},{1,3},{2,0},{3,1},{4,6},{5,7},{6,4},{7,5},{8,10},{9,11},{10,... | collective-permute-start | bytes 12296 | tf_op jit(solution)/shard_map/ppermute | solution.py:70
  64.3 4.6 %collective-permute-start.22 = (f32[8,128]{1,0:T(8,128)S(1)}, f32[8,128]{1,0:T(8,128)S(1)}, u32[]{:S(2)}, u32[]{:S(2)}) collective-permute-start(f32[8,128]{1,0:T(8,128)S(1)} %add.179), channel_id=1, source_target_pairs={{0,4},{1,5},{2,6},{3,7},{4,0},{5,1},{6,2},{7,3},{8,12},{9,13},{10,... | collective-permute-start | bytes 12296 | tf_op jit(solution)/shard_map/ppermute | solution.py:70
  68.9 3.6 %collective-permute-start.23 = (f32[8,128]{1,0:T(8,128)S(1)}, f32[8,128]{1,0:T(8,128)S(1)}, u32[]{:S(2)}, u32[]{:S(2)}) collective-permute-start(f32[8,128]{1,0:T(8,128)S(1)} %add.180), channel_id=1, source_target_pairs={{0,8},{8,0},{16,24},{24,16},{1,9},{9,1},{17,25},{25,17},{2,10},{10... | collective-permute-start | bytes 12296 | tf_op jit(solution)/shard_map/ppermute | solution.py:70
  72.5 3.6 %collective-permute-start.24 = (f32[8,128]{1,0:T(8,128)S(1)}, f32[8,128]{1,0:T(8,128)S(1)}, u32[]{:S(2)}, u32[]{:S(2)}) collective-permute-start(f32[8,128]{1,0:T(8,128)S(1)} %add.181), channel_id=1, source_target_pairs={{0,16},{8,24},{16,0},{24,8},{1,17},{9,25},{17,1},{25,9},{2,18},{10... | collective-permute-start | bytes 12296 | tf_op jit(solution)/shard_map/ppermute | solution.py:70

commit v11 on v6

--- a/solution.py
+++ b/solution.py
@@ -187,12 +187,13 @@
     size_x, size_y, size_z = start_field.shape
     cells = size_x * size_y * size_z * lax.axis_size("gx") * lax.axis_size("gy")
 
-    lo_both_x, hi_both_x, lo_both_y, hi_both_y = exchange(
+    messages = lax.optimization_barrier((
         jnp.concatenate([start_field[:1], trans_x[:1]], axis=0),
         jnp.concatenate([start_field[-1:], trans_x[-1:]], axis=0),
         jnp.concatenate([start_field[:, :1], trans_y[:, :1]], axis=1),
         jnp.concatenate([start_field[:, -1:], trans_y[:, -1:]], axis=1),
-    )
+    ))
+    lo_both_x, hi_both_x, lo_both_y, hi_both_y = exchange(*messages)
     lo_x, hi_x, plane_x = lo_both_x[:1], hi_both_x[:1], hi_both_x[1:]
     lo_y, hi_y, plane_y = lo_both_y[:, :1], hi_both_y[:, :1], hi_both_y[:, 1:]
 

time: 79.3 us -> 81 us (1.021)
  starting transfers between devices: 47.6 us -> 48.6 us
    slice x0 -> x2, local copies, waits for them, and re-layouts: none -> 1.85 us  [the longest x1 1.11 us: local(): trans_y[:, -1:]]
    slice x5, local copies, waits for them, and re-layouts: 1.29 us -> 0.27 us  [neighbour_sum(): u_yp = jnp.concatenate([u[:, 1:], hi_y], axis=1)]
    ppermute x10, starting transfers between devices: 35.2 us -> 36.2 us  [axis_exchange(): lax.ppermute(jnp.where(odd, to_low, to_high), axis, swap_pairs(axis, 0))]
  transfers between devices with their start and end apart: 25 -> 25, of which waited for: 9 -> 9; matrix products, arithmetic and copies ran while one was open for 4% -> 1% of each run, Pallas kernels for 0% -> 0%
where the time goes in v11:
time: 81 us; the launch traced here: 80.3 us
  starting transfers between devices  48.6 us (60%)
  waiting for transfers between devices  14.8 us (18%)
  local copies, waits for them, and re-layouts  5.91 us (7%)
  Pallas kernels  5.06 us (6%)
  other arithmetic  4.7 us (6%)
  between operations  1.23 us (2%)
    ppermute x10, starting transfers between devices, axis_exchange(): lax.ppermute(jnp.where(odd, to_low, to_high), axis, swap_pairs(axis, 0))  36.2 us
    ppermute x5, waiting for transfers between devices, all_sum(): x = x + lax.ppermute(x, axis, [(i, i ^ step) for i in range(n)])  11.4 us
    ppermute x10, starting transfers between devices, axis_exchange(): lax.ppermute(jnp.where(odd, to_high, to_low), axis, swap_pairs(axis, 1))  6.75 us
    ppermute x5, starting transfers between devices, all_sum(): x = x + lax.ppermute(x, axis, [(i, i ^ step) for i in range(n)])  5.63 us
    ppermute x10, waiting for transfers between devices, axis_exchange(): lax.ppermute(jnp.where(odd, to_low, to_high), axis, swap_pairs(axis, 0))  3.35 us
    pallas_call x1, Pallas kernels, finish(): pl.pallas_call(lambda *refs: finish_kernel(float(cells), size, *refs), ou...  2.75 us
    div x4, other arithmetic, local(): vector = 2.0 * total / diagonal  2.44 us
    pallas_call x1, Pallas kernels, gram(): pl.pallas_call(lambda *refs: gram_kernel(size, *refs), out_shape=jax.Shap...  2.31 us
  transfers between devices with their start and end apart: 25, of which 9 were waited for; matrix products, arithmetic and copies ran while one was open for 1% of the time, Pallas kernels for 0%

profile of v11, /device:TPU:0, one launch (start us, length us, event | category | flops | bytes accessed | tf_op | source)
XLA Modules:
  0.0 80.3 jit_solution(14418008407717696988)
XLA Ops:
  0.7 0.8 fusion.52
  1.4 1.1 %fusion.50 = (f32[16,1,512]{2,1,0:T(1,128)S(1)}, f32[16,1,512]{2,1,0:T(1,128)S(1)}) fusion(f32[16,8,512]{2,1,0:T(8,128)} %param.6), kind=kLoop, calls=%fused_computation.117 | loop fusion | bytes 131072 | tf_op jit(solution)/shard_map/slice | solution.py:194
  2.5 0.7 fusion.53
  3.3 1.1 %fusion.51 = (f32[16,1,512]{2,1,0:T(1,128)S(1)}, f32[16,1,512]{2,1,0:T(1,128)S(1)}) fusion(f32[16,8,512]{2,1,0:T(8,128)} %param.10), kind=kLoop, calls=%fused_computation.118 | loop fusion | bytes 131072 | tf_op jit(solution)/shard_map/slice | solution.py:194
  4.4 0.1 pad_maximum_fusion.2
  4.5 3.0 %collective-permute-start.1 = (f32[2,8,512]{2,1,0:T(8,128)S(1)}, f32[2,8,512]{2,1,0:T(8,128)S(1)}, u32[]{:S(2)}, u32[]{:S(2)}) collective-permute-start(f32[2,8,512]{2,1,0:T(8,128)S(1)} %get-tuple-element.83), channel_id=1, source_target_pairs={{0,8},{8,0},{16,24},{24,16},{1,9},{9,1},{17,25},{25,17},{2,10},{10... | collective-permute-start | bytes 98312 | tf_op jit(solution)/shard_map/ppermute | solution.py:29
  7.5 0.7 collective-permute-start
  8.2 0.1 collective-permute-start.3
  8.3 0.8 collective-permute-start.2
  9.2 0.1 fusion.47
  9.4 0.1 fusion.49
  9.5 0.7 copy-done.5
  10.2 0.0 copy-done.7
  10.2 0.1 slice.201
  10.5 0.1 fusion.54
  10.6 0.5 fusion.6.refs_0_.refs_1_
  11.1 0.1 fusion.46
  11.2 0.1 fusion.44
  11.3 0.1 fusion.45
  11.4 0.7 collective-permute-start.5
  12.1 8.1 %collective-permute-start.4 = (f32[1,8,512]{2,1,0:T(8,128)S(1)}, f32[1,8,512]{2,1,0:T(8,128)S(1)}, u32[]{:S(2)}, u32[]{:S(2)}) collective-permute-start(f32[1,8,512]{2,1,0:T(8,128)S(1)} %get-tuple-element.56), channel_id=1, source_target_pairs={{0,8},{8,0},{16,24},{24,16},{1,9},{9,1},{17,25},{25,17},{2,10},{10... | collective-permute-start | bytes 49160 | tf_op jit(solution)/shard_map/ppermute | solution.py:29
  20.2 0.7 collective-permute-start.7
  20.9 4.5 %collective-permute-start.6 = (f32[16,1,512]{2,1,0:T(1,128)S(1)}, f32[16,1,512]{2,1,0:T(1,128)S(1)}, u32[]{:S(2)}, u32[]{:S(2)}) collective-permute-start(f32[16,1,512]{2,1,0:T(1,128)S(1)} %get-tuple-element.52), channel_id=1, source_target_pairs={{0,1},{1,0},{2,3},{3,2},{4,5},{5,4},{6,7},{7,6},{8,9},{9,8},{10,11... | collective-permute-start | bytes 98312 | tf_op jit(solution)/shard_map/ppermute | solution.py:29
  25.4 0.8 %collective-permute-done.6 = f32[16,1,512]{2,1,0:T(1,128)S(1)} collective-permute-done((f32[16,1,512]{2,1,0:T(1,128)S(1)}, f32[16,1,512]{2,1,0:T(1,128)S(1)}, u32[]{:S(2)}, u32[]{:S(2)}) %collective-permute-start.6) | collective-permute-done | bytes 32800 | tf_op jit(solution)/shard_map/ppermute | solution.py:29
  26.3 0.4 fusion.13.refs_1_.refs_2_
  26.7 0.1 fusion.43
  26.8 0.1 fusion.41
  26.9 0.1 fusion.42
  27.0 0.7 collective-permute-start.9
  27.7 3.8 %collective-permute-start.8 = (f32[1,8,512]{2,1,0:T(8,128)S(1)}, f32[1,8,512]{2,1,0:T(8,128)S(1)}, u32[]{:S(2)}, u32[]{:S(2)}) collective-permute-start(f32[1,8,512]{2,1,0:T(8,128)S(1)} %get-tuple-element.46), channel_id=1, source_target_pairs={{0,8},{8,0},{16,24},{24,16},{1,9},{9,1},{17,25},{25,17},{2,10},{10... | collective-permute-start | bytes 49160 | tf_op jit(solution)/shard_map/ppermute | solution.py:29
  31.5 0.7 collective-permute-start.11
  32.2 3.7 %collective-permute-start.10 = (f32[16,1,512]{2,1,0:T(1,128)S(1)}, f32[16,1,512]{2,1,0:T(1,128)S(1)}, u32[]{:S(2)}, u32[]{:S(2)}) collective-permute-start(f32[16,1,512]{2,1,0:T(1,128)S(1)} %get-tuple-element.42), channel_id=1, source_target_pairs={{0,1},{1,0},{2,3},{3,2},{4,5},{5,4},{6,7},{7,6},{8,9},{9,8},{10,11... | collective-permute-start | bytes 98312 | tf_op jit(solution)/shard_map/ppermute | solution.py:29
  35.9 0.8 %collective-permute-done.10 = f32[16,1,512]{2,1,0:T(1,128)S(1)} collective-permute-done((f32[16,1,512]{2,1,0:T(1,128)S(1)}, f32[16,1,512]{2,1,0:T(1,128)S(1)}, u32[]{:S(2)}, u32[]{:S(2)}) %collective-permute-start.10) | collective-permute-done | bytes 32800 | tf_op jit(solution)/shard_map/ppermute | solution.py:29
  36.7 0.4 fusion.20.refs_2_.refs_3_
  37.2 0.1 fusion.40
  37.3 0.1 fusion.38
  37.4 0.1 fusion.39
  37.5 0.7 collective-permute-start.13
  38.1 2.1 %collective-permute-start.12 = (f32[1,8,512]{2,1,0:T(8,128)S(1)}, f32[1,8,512]{2,1,0:T(8,128)S(1)}, u32[]{:S(2)}, u32[]{:S(2)}) collective-permute-start(f32[1,8,512]{2,1,0:T(8,128)S(1)} %get-tuple-element.36), channel_id=1, source_target_pairs={{0,8},{8,0},{16,24},{24,16},{1,9},{9,1},{17,25},{25,17},{2,10},{10... | collective-permute-start | bytes 49160 | tf_op jit(solution)/shard_map/ppermute | solution.py:29
  40.3 0.7 collective-permute-start.15
  41.0 3.7 %collective-permute-start.14 = (f32[16,1,512]{2,1,0:T(1,128)S(1)}, f32[16,1,512]{2,1,0:T(1,128)S(1)}, u32[]{:S(2)}, u32[]{:S(2)}) collective-permute-start(f32[16,1,512]{2,1,0:T(1,128)S(1)} %get-tuple-element.32), channel_id=1, source_target_pairs={{0,1},{1,0},{2,3},{3,2},{4,5},{5,4},{6,7},{7,6},{8,9},{9,8},{10,11... | collective-permute-start | bytes 98312 | tf_op jit(solution)/shard_map/ppermute | solution.py:29
  44.7 0.8 %collective-permute-done.14 = f32[16,1,512]{2,1,0:T(1,128)S(1)} collective-permute-done((f32[16,1,512]{2,1,0:T(1,128)S(1)}, f32[16,1,512]{2,1,0:T(1,128)S(1)}, u32[]{:S(2)}, u32[]{:S(2)}) %collective-permute-start.14) | collective-permute-done | bytes 32800 | tf_op jit(solution)/shard_map/ppermute | solution.py:29
  45.5 0.4 fusion.27.refs_3_.refs_4_
  46.0 0.1 fusion.37
  46.0 0.1 fusion.35
  46.2 0.1 fusion.36
  46.2 0.7 collective-permute-start.17
  46.9 3.6 %collective-permute-start.16 = (f32[1,8,512]{2,1,0:T(8,128)S(1)}, f32[1,8,512]{2,1,0:T(8,128)S(1)}, u32[]{:S(2)}, u32[]{:S(2)}) collective-permute-start(f32[1,8,512]{2,1,0:T(8,128)S(1)} %get-tuple-element.26), channel_id=1, source_target_pairs={{0,8},{8,0},{16,24},{24,16},{1,9},{9,1},{17,25},{25,17},{2,10},{10... | collective-permute-start | bytes 49160 | tf_op jit(solution)/shard_map/ppermute | solution.py:29
  50.5 0.7 collective-permute-start.19
  51.2 3.7 %collective-permute-start.18 = (f32[16,1,512]{2,1,0:T(1,128)S(1)}, f32[16,1,512]{2,1,0:T(1,128)S(1)}, u32[]{:S(2)}, u32[]{:S(2)}) collective-permute-start(f32[16,1,512]{2,1,0:T(1,128)S(1)} %get-tuple-element.22), channel_id=1, source_target_pairs={{0,1},{1,0},{2,3},{3,2},{4,5},{5,4},{6,7},{7,6},{8,9},{9,8},{10,11... | collective-permute-start | bytes 98312 | tf_op jit(solution)/shard_map/ppermute | solution.py:29
  54.9 0.8 %collective-permute-done.18 = f32[16,1,512]{2,1,0:T(1,128)S(1)} collective-permute-done((f32[16,1,512]{2,1,0:T(1,128)S(1)}, f32[16,1,512]{2,1,0:T(1,128)S(1)}, u32[]{:S(2)}, u32[]{:S(2)}) %collective-permute-start.18) | collective-permute-done | bytes 32800 | tf_op jit(solution)/shard_map/ppermute | solution.py:29
  55.8 1.1 %fusion.34.refs_4_.refs_5_ = f32[16,8,512]{2,1,0:T(8,128)} fusion(f32[16,8,512]{2,1,0:T(8,128)S(1)} %copy-done.6, f32[15,8,512]{2,1,0:T(8,128)S(1)} %get-tuple-element.24, f32[1,8,512]{2,1,0:T(8,128)S(1)} %get-tuple-element.86, f32[1,8,512]{2,1,0:T(8,128)S(1)} %get-tuple-element.85, f32[15,8,512]{2,1,0:T(8,128)S(1)} %get-tuple-element.23, ...), kind=kLoop, calls=%fused_computation.53 | loop fusion | flops 1638400 | bytes 3668480 | tf_op jit(solution)/shard_map/div | solution.py:217
  56.9 2.3 %shard_map.85 = f32[8,128]{1,0:T(8,128)} custom-call(f32[16,8,512]{2,1,0:T(8,128)} %copy-done.3, f32[16,8,512]{2,1,0:T(8,128)} %copy-done, f32[16,8,512]{2,1,0:T(8,128)} %copy-done.1, f32[16,8,512]{2,1,0:T(8,128)} %copy-done.2, f32[16,8,512]{2,1,0:T(8,128)} %fusion.34.refs_4_.refs_5_), custom_call_target="tpu_custom_call" | custom-call | tf_op jit(solution)/shard_map/pallas_call | solution.py:107
  59.2 0.7 collective-permute-start.20
  59.9 1.0 %collective-permute-done.20 = f32[8,128]{1,0:T(8,128)S(1)} collective-permute-done((f32[8,128]{1,0:T(8,128)}, f32[8,128]{1,0:T(8,128)S(1)}, u32[]{:S(2)}, u32[]{:S(2)}) %collective-permute-start.20) | collective-permute-done | bytes 4128 | tf_op jit(solution)/shard_map/ppermute | solution.py:70
  60.9 0.7 add.178
  61.6 2.0 %collective-permute-start.21 = (f32[8,128]{1,0:T(8,128)S(1)}, f32[8,128]{1,0:T(8,128)S(1)}, u32[]{:S(2)}, u32[]{:S(2)}) collective-permute-start(f32[8,128]{1,0:T(8,128)S(1)} %add.178), channel_id=1, source_target_pairs={{0,2},{1,3},{2,0},{3,1},{4,6},{5,7},{6,4},{7,5},{8,10},{9,11},{10,... | collective-permute-start | bytes 12296 | tf_op jit(solution)/shard_map/ppermute | solution.py:70
  63.5 1.6 %collective-permute-done.21 = f32[8,128]{1,0:T(8,128)S(1)} collective-permute-done((f32[8,128]{1,0:T(8,128)S(1)}, f32[8,128]{1,0:T(8,128)S(1)}, u32[]{:S(2)}, u32[]{:S(2)}) %collective-permute-start.21) | collective-permute-done | bytes 4128 | tf_op jit(solution)/shard_map/ppermute | solution.py:70
  65.2 3.0 %collective-permute-start.22 = (f32[8,128]{1,0:T(8,128)S(1)}, f32[8,128]{1,0:T(8,128)S(1)}, u32[]{:S(2)}, u32[]{:S(2)}) collective-permute-start(f32[8,128]{1,0:T(8,128)S(1)} %add.179), channel_id=1, source_target_pairs={{0,4},{1,5},{2,6},{3,7},{4,0},{5,1},{6,2},{7,3},{8,12},{9,13},{10,... | collective-permute-start | bytes 12296 | tf_op jit(solution)/shard_map/ppermute | solution.py:70
  68.2 1.6 %collective-permute-done.22 = f32[8,128]{1,0:T(8,128)S(1)} collective-permute-done((f32[8,128]{1,0:T(8,128)S(1)}, f32[8,128]{1,0:T(8,128)S(1)}, u32[]{:S(2)}, u32[]{:S(2)}) %collective-permute-start.22) | collective-permute-done | bytes 4128 | tf_op jit(solution)/shard_map/ppermute | solution.py:70
  69.8 3.6 %collective-permute-done.23 = f32[8,128]{1,0:T(8,128)S(1)} collective-permute-done((f32[8,128]{1,0:T(8,128)S(1)}, f32[8,128]{1,0:T(8,128)S(1)}, u32[]{:S(2)}, u32[]{:S(2)}) %collective-permute-start.23) | collective-permute-done | bytes 4128 | tf_op jit(solution)/shard_map/ppermute | solution.py:70
  73.4 3.6 %collective-permute-done.24 = f32[8,128]{1,0:T(8,128)S(1)} collective-permute-done((f32[8,128]{1,0:T(8,128)S(1)}, f32[8,128]{1,0:T(8,128)S(1)}, u32[]{:S(2)}, u32[]{:S(2)}) %collective-permute-start.24) | collective-permute-done | bytes 4128 | tf_op jit(solution)/shard_map/ppermute | solution.py:70
  77.0 0.6 add.182.refs_0_
  77.6 2.8 %shard_map.86 = (f32[5,16,8,512]{3,2,1,0:T(8,128)}, f32[5,5]{1,0:T(8,128)}, f32[1,1]{1,0:T(1,128)}) custom-call(f32[8,128]{1,0:T(8,128)} %add.182.refs_0_, f32[16,8,512]{2,1,0:T(8,128)} %copy-done.3, f32[16,8,512]{2,1,0:T(8,128)} %copy-done, f32[16,8,512]{2,1,0:T(8,128)} %copy-done.1, f32[16,8,512]{2,1,0:T(8,128)} %copy-done.2, ...), custom_call_target="tpu_custom_call" | custom-call | tf_op jit(solution)/shard_map/pallas_call | solution.py:173
  (66 shorter events, 0.6 us)
Async XLA Ops:
  0.6 8.5 %copy-start.4 = (f32[16,8,512]{2,1,0:T(8,128)S(1)}, f32[16,8,512]{2,1,0:T(8,128)}, u32[]{:S(2)}) copy-start(f32[16,8,512]{2,1,0:T(8,128)} %param.6) | copy-start | bytes 786436
  4.5 5.8 %collective-permute-start.1 = (f32[2,8,512]{2,1,0:T(8,128)S(1)}, f32[2,8,512]{2,1,0:T(8,128)S(1)}, u32[]{:S(2)}, u32[]{:S(2)}) collective-permute-start(f32[2,8,512]{2,1,0:T(8,128)S(1)} %get-tuple-element.83), channel_id=1, source_target_pairs={{0,8},{8,0},{16,24},{24,16},{1,9},{9,1},{17,25},{25,17},{2,10},{10... | collective-permute-start | bytes 98312 | tf_op jit(solution)/shard_map/ppermute | solution.py:29
  7.5 2.8 %collective-permute-start = (f32[2,8,512]{2,1,0:T(8,128)S(1)}, f32[2,8,512]{2,1,0:T(8,128)S(1)}, u32[]{:S(2)}, u32[]{:S(2)}) collective-permute-start(f32[2,8,512]{2,1,0:T(8,128)S(1)} %get-tuple-element.84), channel_id=1, source_target_pairs={{8,16},{16,8},{9,17},{17,9},{10,18},{18,10},{11,19},{19,11},{12,20... | collective-permute-start | bytes 98312 | tf_op jit(solution)/shard_map/ppermute | solution.py:30
  8.2 2.2 %collective-permute-start.3 = (f32[16,2,512]{2,1,0:T(2,128)S(1)}, f32[16,2,512]{2,1,0:T(2,128)S(1)}, u32[]{:S(2)}, u32[]{:S(2)}) collective-permute-start(f32[16,2,512]{2,1,0:T(2,128)S(1)} %bitcast.38), channel_id=1, source_target_pairs={{0,1},{1,0},{2,3},{3,2},{4,5},{5,4},{6,7},{7,6},{8,9},{9,8},{10,11... | collective-permute-start | bytes 196616 | tf_op jit(solution)/shard_map/ppermute | solution.py:29
  8.3 1.1 %copy-start.6 = (f32[16,8,512]{2,1,0:T(8,128)S(1)}, f32[16,8,512]{2,1,0:T(8,128)}, u32[]{:S(2)}) copy-start(f32[16,8,512]{2,1,0:T(8,128)} %param.9) | copy-start | bytes 786436
  8.3 2.1 %collective-permute-start.2 = (f32[16,2,512]{2,1,0:T(2,128)S(1)}, f32[16,2,512]{2,1,0:T(2,128)S(1)}, u32[]{:S(2)}, u32[]{:S(2)}) collective-permute-start(f32[16,2,512]{2,1,0:T(2,128)S(1)} %bitcast.37), channel_id=1, source_target_pairs={{1,2},{2,1},{3,4},{4,3},{5,6},{6,5},{9,10},{10,9},{11,12},{12,11},... | collective-permute-start | bytes 196616 | tf_op jit(solution)/shard_map/ppermute | solution.py:30
  9.2 1.0 %copy-start.5 = (f32[16,8,512]{2,1,0:T(8,128)S(1)}, f32[16,8,512]{2,1,0:T(8,128)}, u32[]{:S(2)}) copy-start(f32[16,8,512]{2,1,0:T(8,128)} %param.10) | copy-start | bytes 786436
  9.2 1.0 %copy-start.7 = (f32[16,8,512]{2,1,0:T(8,128)S(1)}, f32[16,8,512]{2,1,0:T(8,128)}, u32[]{:S(2)}) copy-start(f32[16,8,512]{2,1,0:T(8,128)} %param.11) | copy-start | bytes 786436
  9.4 1.2 %copy-start.8 = (f32[16,8,512]{2,1,0:T(8,128)S(1)}, f32[16,8,512]{2,1,0:T(8,128)}, u32[]{:S(2)}) copy-start(f32[16,8,512]{2,1,0:T(8,128)} %param.8) | copy-start | bytes 786436
  9.4 1.2 %copy-start.9 = (f32[16,8,512]{2,1,0:T(8,128)S(1)}, f32[16,8,512]{2,1,0:T(8,128)}, u32[]{:S(2)}) copy-start(f32[16,8,512]{2,1,0:T(8,128)} %param.7) | copy-start | bytes 786436
  11.1 9.1 %copy-start.3 = (f32[16,8,512]{2,1,0:T(8,128)}, f32[16,8,512]{2,1,0:T(8,128)S(1)}, u32[]{:S(2)}) copy-start(f32[16,8,512]{2,1,0:T(8,128)S(1)} %fusion.6.refs_0_.refs_1_) | copy-start | bytes 786436
  11.4 14.0 %collective-permute-start.5 = (f32[1,8,512]{2,1,0:T(8,128)S(1)}, f32[1,8,512]{2,1,0:T(8,128)S(1)}, u32[]{:S(2)}, u32[]{:S(2)}) collective-permute-start(f32[1,8,512]{2,1,0:T(8,128)S(1)} %get-tuple-element.55), channel_id=1, source_target_pairs={{8,16},{16,8},{9,17},{17,9},{10,18},{18,10},{11,19},{19,11},{12,20... | collective-permute-start | bytes 49160 | tf_op jit(solution)/shard_map/ppermute | solution.py:30
  12.1 13.3 %collective-permute-start.4 = (f32[1,8,512]{2,1,0:T(8,128)S(1)}, f32[1,8,512]{2,1,0:T(8,128)S(1)}, u32[]{:S(2)}, u32[]{:S(2)}) collective-permute-start(f32[1,8,512]{2,1,0:T(8,128)S(1)} %get-tuple-element.56), channel_id=1, source_target_pairs={{0,8},{8,0},{16,24},{24,16},{1,9},{9,1},{17,25},{25,17},{2,10},{10... | collective-permute-start | bytes 49160 | tf_op jit(solution)/shard_map/ppermute | solution.py:29
  20.2 5.2 %collective-permute-start.7 = (f32[16,1,512]{2,1,0:T(1,128)S(1)}, f32[16,1,512]{2,1,0:T(1,128)S(1)}, u32[]{:S(2)}, u32[]{:S(2)}) collective-permute-start(f32[16,1,512]{2,1,0:T(1,128)S(1)} %get-tuple-element.51), channel_id=1, source_target_pairs={{1,2},{2,1},{3,4},{4,3},{5,6},{6,5},{9,10},{10,9},{11,12},{12,11},... | collective-permute-start | bytes 98312 | tf_op jit(solution)/shard_map/ppermute | solution.py:30
  20.9 5.3 %collective-permute-start.6 = (f32[16,1,512]{2,1,0:T(1,128)S(1)}, f32[16,1,512]{2,1,0:T(1,128)S(1)}, u32[]{:S(2)}, u32[]{:S(2)}) collective-permute-start(f32[16,1,512]{2,1,0:T(1,128)S(1)} %get-tuple-element.52), channel_id=1, source_target_pairs={{0,1},{1,0},{2,3},{3,2},{4,5},{5,4},{6,7},{7,6},{8,9},{9,8},{10,11... | collective-permute-start | bytes 98312 | tf_op jit(solution)/shard_map/ppermute | solution.py:29
  26.7 4.7 %copy-start = (f32[16,8,512]{2,1,0:T(8,128)}, f32[16,8,512]{2,1,0:T(8,128)S(1)}, u32[]{:S(2)}) copy-start(f32[16,8,512]{2,1,0:T(8,128)S(1)} %fusion.13.refs_1_.refs_2_) | copy-start | bytes 786436
  27.0 8.9 %collective-permute-start.9 = (f32[1,8,512]{2,1,0:T(8,128)S(1)}, f32[1,8,512]{2,1,0:T(8,128)S(1)}, u32[]{:S(2)}, u32[]{:S(2)}) collective-permute-start(f32[1,8,512]{2,1,0:T(8,128)S(1)} %get-tuple-element.45), channel_id=1, source_target_pairs={{8,16},{16,8},{9,17},{17,9},{10,18},{18,10},{11,19},{19,11},{12,20... | collective-permute-start | bytes 49160 | tf_op jit(solution)/shard_map/ppermute | solution.py:30
  27.7 8.2 %collective-permute-start.8 = (f32[1,8,512]{2,1,0:T(8,128)S(1)}, f32[1,8,512]{2,1,0:T(8,128)S(1)}, u32[]{:S(2)}, u32[]{:S(2)}) collective-permute-start(f32[1,8,512]{2,1,0:T(8,128)S(1)} %get-tuple-element.46), channel_id=1, source_target_pairs={{0,8},{8,0},{16,24},{24,16},{1,9},{9,1},{17,25},{25,17},{2,10},{10... | collective-permute-start | bytes 49160 | tf_op jit(solution)/shard_map/ppermute | solution.py:29
  31.5 4.4 %collective-permute-start.11 = (f32[16,1,512]{2,1,0:T(1,128)S(1)}, f32[16,1,512]{2,1,0:T(1,128)S(1)}, u32[]{:S(2)}, u32[]{:S(2)}) collective-permute-start(f32[16,1,512]{2,1,0:T(1,128)S(1)} %get-tuple-element.41), channel_id=1, source_target_pairs={{1,2},{2,1},{3,4},{4,3},{5,6},{6,5},{9,10},{10,9},{11,12},{12,11},... | collective-permute-start | bytes 98312 | tf_op jit(solution)/shard_map/ppermute | solution.py:30
  32.2 4.6 %collective-permute-start.10 = (f32[16,1,512]{2,1,0:T(1,128)S(1)}, f32[16,1,512]{2,1,0:T(1,128)S(1)}, u32[]{:S(2)}, u32[]{:S(2)}) collective-permute-start(f32[16,1,512]{2,1,0:T(1,128)S(1)} %get-tuple-element.42), channel_id=1, source_target_pairs={{0,1},{1,0},{2,3},{3,2},{4,5},{5,4},{6,7},{7,6},{8,9},{9,8},{10,11... | collective-permute-start | bytes 98312 | tf_op jit(solution)/shard_map/ppermute | solution.py:29
  37.2 3.1 %copy-start.1 = (f32[16,8,512]{2,1,0:T(8,128)}, f32[16,8,512]{2,1,0:T(8,128)S(1)}, u32[]{:S(2)}) copy-start(f32[16,8,512]{2,1,0:T(8,128)S(1)} %fusion.20.refs_2_.refs_3_) | copy-start | bytes 786436
  37.5 7.2 %collective-permute-start.13 = (f32[1,8,512]{2,1,0:T(8,128)S(1)}, f32[1,8,512]{2,1,0:T(8,128)S(1)}, u32[]{:S(2)}, u32[]{:S(2)}) collective-permute-start(f32[1,8,512]{2,1,0:T(8,128)S(1)} %get-tuple-element.35), channel_id=1, source_target_pairs={{8,16},{16,8},{9,17},{17,9},{10,18},{18,10},{11,19},{19,11},{12,20... | collective-permute-start | bytes 49160 | tf_op jit(solution)/shard_map/ppermute | solution.py:30
  38.1 6.5 %collective-permute-start.12 = (f32[1,8,512]{2,1,0:T(8,128)S(1)}, f32[1,8,512]{2,1,0:T(8,128)S(1)}, u32[]{:S(2)}, u32[]{:S(2)}) collective-permute-start(f32[1,8,512]{2,1,0:T(8,128)S(1)} %get-tuple-element.36), channel_id=1, source_target_pairs={{0,8},{8,0},{16,24},{24,16},{1,9},{9,1},{17,25},{25,17},{2,10},{10... | collective-permute-start | bytes 49160 | tf_op jit(solution)/shard_map/ppermute | solution.py:29
  40.3 4.4 %collective-permute-start.15 = (f32[16,1,512]{2,1,0:T(1,128)S(1)}, f32[16,1,512]{2,1,0:T(1,128)S(1)}, u32[]{:S(2)}, u32[]{:S(2)}) collective-permute-start(f32[16,1,512]{2,1,0:T(1,128)S(1)} %get-tuple-element.31), channel_id=1, source_target_pairs={{1,2},{2,1},{3,4},{4,3},{5,6},{6,5},{9,10},{10,9},{11,12},{12,11},... | collective-permute-start | bytes 98312 | tf_op jit(solution)/shard_map/ppermute | solution.py:30
  41.0 4.5 %collective-permute-start.14 = (f32[16,1,512]{2,1,0:T(1,128)S(1)}, f32[16,1,512]{2,1,0:T(1,128)S(1)}, u32[]{:S(2)}, u32[]{:S(2)}) collective-permute-start(f32[16,1,512]{2,1,0:T(1,128)S(1)} %get-tuple-element.32), channel_id=1, source_target_pairs={{0,1},{1,0},{2,3},{3,2},{4,5},{5,4},{6,7},{7,6},{8,9},{9,8},{10,11... | collective-permute-start | bytes 98312 | tf_op jit(solution)/shard_map/ppermute | solution.py:29
  46.0 4.5 %copy-start.2 = (f32[16,8,512]{2,1,0:T(8,128)}, f32[16,8,512]{2,1,0:T(8,128)S(1)}, u32[]{:S(2)}) copy-start(f32[16,8,512]{2,1,0:T(8,128)S(1)} %fusion.27.refs_3_.refs_4_) | copy-start | bytes 786436
  46.2 8.6 %collective-permute-start.17 = (f32[1,8,512]{2,1,0:T(8,128)S(1)}, f32[1,8,512]{2,1,0:T(8,128)S(1)}, u32[]{:S(2)}, u32[]{:S(2)}) collective-permute-start(f32[1,8,512]{2,1,0:T(8,128)S(1)} %get-tuple-element.25), channel_id=1, source_target_pairs={{8,16},{16,8},{9,17},{17,9},{10,18},{18,10},{11,19},{19,11},{12,20... | collective-permute-start | bytes 49160 | tf_op jit(solution)/shard_map/ppermute | solution.py:30
  46.9 8.0 %collective-permute-start.16 = (f32[1,8,512]{2,1,0:T(8,128)S(1)}, f32[1,8,512]{2,1,0:T(8,128)S(1)}, u32[]{:S(2)}, u32[]{:S(2)}) collective-permute-start(f32[1,8,512]{2,1,0:T(8,128)S(1)} %get-tuple-element.26), channel_id=1, source_target_pairs={{0,8},{8,0},{16,24},{24,16},{1,9},{9,1},{17,25},{25,17},{2,10},{10... | collective-permute-start | bytes 49160 | tf_op jit(solution)/shard_map/ppermute | solution.py:29
  50.5 4.4 %collective-permute-start.19 = (f32[16,1,512]{2,1,0:T(1,128)S(1)}, f32[16,1,512]{2,1,0:T(1,128)S(1)}, u32[]{:S(2)}, u32[]{:S(2)}) collective-permute-start(f32[16,1,512]{2,1,0:T(1,128)S(1)} %get-tuple-element.21), channel_id=1, source_target_pairs={{1,2},{2,1},{3,4},{4,3},{5,6},{6,5},{9,10},{10,9},{11,12},{12,11},... | collective-permute-start | bytes 98312 | tf_op jit(solution)/shard_map/ppermute | solution.py:30
  51.2 4.5 %collective-permute-start.18 = (f32[16,1,512]{2,1,0:T(1,128)S(1)}, f32[16,1,512]{2,1,0:T(1,128)S(1)}, u32[]{:S(2)}, u32[]{:S(2)}) collective-permute-start(f32[16,1,512]{2,1,0:T(1,128)S(1)} %get-tuple-element.22), channel_id=1, source_target_pairs={{0,1},{1,0},{2,3},{3,2},{4,5},{5,4},{6,7},{7,6},{8,9},{9,8},{10,11... | collective-permute-start | bytes 98312 | tf_op jit(solution)/shard_map/ppermute | solution.py:29
  59.2 1.7 %collective-permute-start.20 = (f32[8,128]{1,0:T(8,128)}, f32[8,128]{1,0:T(8,128)S(1)}, u32[]{:S(2)}, u32[]{:S(2)}) collective-permute-start(f32[8,128]{1,0:T(8,128)} %shard_map.85), channel_id=1, source_target_pairs={{0,1},{1,0},{2,3},{3,2},{4,5},{5,4},{6,7},{7,6},{8,9},{9,8},{10,11... | collective-permute-start | bytes 12296 | tf_op jit(solution)/shard_map/ppermute | solution.py:70
  61.6 3.6 %collective-permute-start.21 = (f32[8,128]{1,0:T(8,128)S(1)}, f32[8,128]{1,0:T(8,128)S(1)}, u32[]{:S(2)}, u32[]{:S(2)}) collective-permute-start(f32[8,128]{1,0:T(8,128)S(1)} %add.178), channel_id=1, source_target_pairs={{0,2},{1,3},{2,0},{3,1},{4,6},{5,7},{6,4},{7,5},{8,10},{9,11},{10,... | collective-permute-start | bytes 12296 | tf_op jit(solution)/shard_map/ppermute | solution.py:70
  65.2 4.6 %collective-permute-start.22 = (f32[8,128]{1,0:T(8,128)S(1)}, f32[8,128]{1,0:T(8,128)S(1)}, u32[]{:S(2)}, u32[]{:S(2)}) collective-permute-start(f32[8,128]{1,0:T(8,128)S(1)} %add.179), channel_id=1, source_target_pairs={{0,4},{1,5},{2,6},{3,7},{4,0},{5,1},{6,2},{7,3},{8,12},{9,13},{10,... | collective-permute-start | bytes 12296 | tf_op jit(solution)/shard_map/ppermute | solution.py:70
  69.8 3.6 %collective-permute-start.23 = (f32[8,128]{1,0:T(8,128)S(1)}, f32[8,128]{1,0:T(8,128)S(1)}, u32[]{:S(2)}, u32[]{:S(2)}) collective-permute-start(f32[8,128]{1,0:T(8,128)S(1)} %add.180), channel_id=1, source_target_pairs={{0,8},{8,0},{16,24},{24,16},{1,9},{9,1},{17,25},{25,17},{2,10},{10... | collective-permute-start | bytes 12296 | tf_op jit(solution)/shard_map/ppermute | solution.py:70
  73.4 3.6 %collective-permute-start.24 = (f32[8,128]{1,0:T(8,128)S(1)}, f32[8,128]{1,0:T(8,128)S(1)}, u32[]{:S(2)}, u32[]{:S(2)}) collective-permute-start(f32[8,128]{1,0:T(8,128)S(1)} %add.181), channel_id=1, source_target_pairs={{0,16},{8,24},{16,0},{24,8},{1,17},{9,25},{17,1},{25,9},{2,18},{10... | collective-permute-start | bytes 12296 | tf_op jit(solution)/shard_map/ppermute | solution.py:70

commit v12 on v6

--- a/solution.py
+++ b/solution.py
@@ -113,7 +113,10 @@
 
 
 def finish_kernel(cells, size, stats_ref, *refs):
-    basis_refs, (ortho_ref, upper_ref, scale_ref) = refs[:size], refs[size:]
+    sources, (ortho_ref, upper_ref, scale_ref, held_basis, arrived) = refs[:size], refs[size:]
+    copies = [pltpu.make_async_copy(sources[j], held_basis.at[j], arrived.at[j]) for j in range(size)]
+    for copy in copies:
+        copy.start()
     tile = (8, 128)
 
     def held(i):
@@ -149,14 +152,17 @@
             packed = jnp.where((rows == row) & (cols == col), upper[row][col], packed)
     upper_ref[...] = packed[: upper_ref.shape[0], : upper_ref.shape[1]]
     scale_ref[...] = scale[:1, :1]
-    lanes = basis_refs[0].shape[-1] // tile[1]
+    lanes = held_basis.shape[-1] // tile[1]
     weight = [
         [jnp.tile(inverse[j][k] / scale, (1, lanes)) if j <= k else None for k in range(size)]
         for j in range(size)
     ]
 
+    for copy in copies:
+        copy.wait()
+
     def plane(i, carry):
-        parts = [basis_refs[j][i] for j in range(size)]
+        parts = [held_basis[j, i] for j in range(size)]
         for k in range(size):
             acc = parts[0] * weight[0][k]
             for j in range(1, k + 1):
@@ -164,7 +170,7 @@
             ortho_ref[k, i] = acc
         return carry
 
-    lax.fori_loop(0, basis_refs[0].shape[0], plane, 0)
+    lax.fori_loop(0, held_basis.shape[1], plane, 0)
 
 
 def finish(stats, basis, cells):
@@ -177,8 +183,9 @@
             jax.ShapeDtypeStruct((size, size), jnp.float32),
             jax.ShapeDtypeStruct((1, 1), jnp.float32),
         ),
-        in_specs=[pl.BlockSpec(memory_space=pltpu.SMEM)] + [vmem] * size,
+        in_specs=[pl.BlockSpec(memory_space=pltpu.SMEM)] + [pl.BlockSpec(memory_space=pl.ANY)] * size,
         out_specs=(vmem, vmem, vmem),
+        scratch_shapes=[pltpu.VMEM((size,) + basis[0].shape, jnp.float32), pltpu.SemaphoreType.DMA((size,))],
     )(stats, *basis)
     return ortho, upper, scale.reshape(())
 

time: 79.3 us -> 79.9 us (level)
  no operation moved by 1% of the time
where the time goes in v12:
time: 79.9 us; the launch traced here: 79.4 us
  starting transfers between devices  47.6 us (60%)
  waiting for transfers between devices  14.8 us (19%)
  Pallas kernels  5.69 us (7%)
  local copies, waits for them, and re-layouts  5.32 us (7%)
  other arithmetic  4.77 us (6%)
  between operations  1.2 us (2%)
    ppermute x10, starting transfers between devices, axis_exchange(): lax.ppermute(jnp.where(odd, to_low, to_high), axis, swap_pairs(axis, 0))  35.2 us
    ppermute x5, waiting for transfers between devices, all_sum(): x = x + lax.ppermute(x, axis, [(i, i ^ step) for i in range(n)])  11.4 us
    ppermute x10, starting transfers between devices, axis_exchange(): lax.ppermute(jnp.where(odd, to_high, to_low), axis, swap_pairs(axis, 1))  6.75 us
    ppermute x5, starting transfers between devices, all_sum(): x = x + lax.ppermute(x, axis, [(i, i ^ step) for i in range(n)])  5.63 us
    pallas_call x1, Pallas kernels, finish(): pl.pallas_call(lambda *refs: finish_kernel(float(cells), size, *refs), ou...  3.38 us
    ppermute x10, waiting for transfers between devices, axis_exchange(): lax.ppermute(jnp.where(odd, to_low, to_high), axis, swap_pairs(axis, 0))  3.35 us
    div x4, other arithmetic, local(): vector = 2.0 * total / diagonal  2.52 us
    pallas_call x1, Pallas kernels, gram(): pl.pallas_call(lambda *refs: gram_kernel(size, *refs), out_shape=jax.Shap...  2.31 us
  transfers between devices with their start and end apart: 25, of which 9 were waited for; matrix products, arithmetic and copies ran while one was open for 4% of the time, Pallas kernels for 0%

profile of v12, /device:TPU:0, one launch (start us, length us, event | category | flops | bytes accessed | tf_op | source)
XLA Modules:
  0.0 79.4 jit_solution(15792849928694192322)
XLA Ops:
  0.6 0.0 copy-start.4
  0.7 0.8 %fusion.54 = (f32[1,8,512]{2,1,0:T(8,128)S(1)}, f32[1,8,512]{2,1,0:T(8,128)S(1)}, f32[1,8,512]{2,1,0:T(8,128)S(1)}, f32[1,8,512]{2,1,0:T(8,128)S(1)}) fusion(f32[16,8,512]{2,1,0:T(8,128)} %param.6, f32[16,8,512]{2,1,0:T(8,128)} %param.9), kind=kLoop, calls=%fused_computation.119 | loop fusion | bytes 131072 | tf_op jit(solution)/shard_map/slice | solution.py:199
  1.5 3.0 %collective-permute-start.1 = (f32[2,8,512]{2,1,0:T(8,128)S(1)}, f32[2,8,512]{2,1,0:T(8,128)S(1)}, u32[]{:S(2)}, u32[]{:S(2)}) collective-permute-start(f32[2,8,512]{2,1,0:T(8,128)S(1)} %get-tuple-element.75), channel_id=1, source_target_pairs={{0,8},{8,0},{16,24},{24,16},{1,9},{9,1},{17,25},{25,17},{2,10},{10... | collective-permute-start | bytes 98312 | tf_op jit(solution)/shard_map/ppermute | solution.py:29
  4.5 0.7 collective-permute-start
  5.2 1.3 %fusion.51 = (f32[16,1,512]{2,1,0:T(1,128)S(1)}, f32[16,1,512]{2,1,0:T(1,128)S(1)}, f32[16,1,512]{2,1,0:T(1,128)S(1)}, f32[16,1,512]{2,1,0:T(1,128)S(1)}) fusion(f32[16,8,512]{2,1,0:T(8,128)} %param.6, f32[16,8,512]{2,1,0:T(8,128)} %param.10), kind=kLoop, calls=%fused_computation.116 | loop fusion | bytes 262144 | tf_op jit(solution)/shard_map/slice | solution.py:201
  6.5 0.1 broadcast_select_fusion.18
  6.6 0.1 collective-permute-start.3
  6.7 0.0 copy-start.6
  6.7 0.8 %collective-permute-start.2 = (f32[16,2,512]{2,1,0:T(2,128)S(1)}, f32[16,2,512]{2,1,0:T(2,128)S(1)}, u32[]{:S(2)}, u32[]{:S(2)}) collective-permute-start(f32[16,2,512]{2,1,0:T(2,128)S(1)} %get-tuple-element.64), channel_id=1, source_target_pairs={{1,2},{2,1},{3,4},{4,3},{5,6},{6,5},{9,10},{10,9},{11,12},{12,11},... | collective-permute-start | bytes 196616 | tf_op jit(solution)/shard_map/ppermute | solution.py:30
  7.5 1.1 %fusion.50 = (f32[16,7,512]{2,1,0:T(8,128)S(1)}, f32[16,7,512]{2,1,0:T(8,128)S(1)}) fusion(f32[16,8,512]{2,1,0:T(8,128)} %param.6), kind=kLoop, calls=%fused_computation.115 | loop fusion | bytes 917504 | tf_op jit(solution)/shard_map/slice | solution.py:49
  8.6 0.0 copy-start.5
  8.6 0.1 fusion.49
  8.7 0.1 fusion.53
  8.9 0.7 copy-done.5
  9.6 0.1 copy-done.7
  9.6 0.1 slice.201
  9.8 0.1 fusion.56
  10.0 0.5 fusion.6.refs_0_.refs_1_
  10.5 0.1 fusion.48
  10.6 0.1 fusion.46
  10.7 0.1 fusion.47
  10.8 0.7 collective-permute-start.5
  11.4 5.7 %collective-permute-start.4 = (f32[1,8,512]{2,1,0:T(8,128)S(1)}, f32[1,8,512]{2,1,0:T(8,128)S(1)}, u32[]{:S(2)}, u32[]{:S(2)}) collective-permute-start(f32[1,8,512]{2,1,0:T(8,128)S(1)} %get-tuple-element.48), channel_id=1, source_target_pairs={{0,8},{8,0},{16,24},{24,16},{1,9},{9,1},{17,25},{25,17},{2,10},{10... | collective-permute-start | bytes 49160 | tf_op jit(solution)/shard_map/ppermute | solution.py:29
  17.2 0.7 collective-permute-start.7
  17.9 5.9 %collective-permute-start.6 = (f32[16,1,512]{2,1,0:T(1,128)S(1)}, f32[16,1,512]{2,1,0:T(1,128)S(1)}, u32[]{:S(2)}, u32[]{:S(2)}) collective-permute-start(f32[16,1,512]{2,1,0:T(1,128)S(1)} %get-tuple-element.44), channel_id=1, source_target_pairs={{0,1},{1,0},{2,3},{3,2},{4,5},{5,4},{6,7},{7,6},{8,9},{9,8},{10,11... | collective-permute-start | bytes 98312 | tf_op jit(solution)/shard_map/ppermute | solution.py:29
  23.8 0.8 %collective-permute-done.6 = f32[16,1,512]{2,1,0:T(1,128)S(1)} collective-permute-done((f32[16,1,512]{2,1,0:T(1,128)S(1)}, f32[16,1,512]{2,1,0:T(1,128)S(1)}, u32[]{:S(2)}, u32[]{:S(2)}) %collective-permute-start.6) | collective-permute-done | bytes 32800 | tf_op jit(solution)/shard_map/ppermute | solution.py:29
  24.6 0.5 fusion.13.refs_1_.refs_2_
  25.1 0.1 fusion.43
  25.3 0.1 fusion.44
  25.4 0.7 collective-permute-start.9
  26.0 3.8 %collective-permute-start.8 = (f32[1,8,512]{2,1,0:T(8,128)S(1)}, f32[1,8,512]{2,1,0:T(8,128)S(1)}, u32[]{:S(2)}, u32[]{:S(2)}) collective-permute-start(f32[1,8,512]{2,1,0:T(8,128)S(1)} %get-tuple-element.38), channel_id=1, source_target_pairs={{0,8},{8,0},{16,24},{24,16},{1,9},{9,1},{17,25},{25,17},{2,10},{10... | collective-permute-start | bytes 49160 | tf_op jit(solution)/shard_map/ppermute | solution.py:29
  29.9 0.7 collective-permute-start.11
  30.5 3.7 %collective-permute-start.10 = (f32[16,1,512]{2,1,0:T(1,128)S(1)}, f32[16,1,512]{2,1,0:T(1,128)S(1)}, u32[]{:S(2)}, u32[]{:S(2)}) collective-permute-start(f32[16,1,512]{2,1,0:T(1,128)S(1)} %get-tuple-element.34), channel_id=1, source_target_pairs={{0,1},{1,0},{2,3},{3,2},{4,5},{5,4},{6,7},{7,6},{8,9},{9,8},{10,11... | collective-permute-start | bytes 98312 | tf_op jit(solution)/shard_map/ppermute | solution.py:29
  34.3 0.8 %collective-permute-done.10 = f32[16,1,512]{2,1,0:T(1,128)S(1)} collective-permute-done((f32[16,1,512]{2,1,0:T(1,128)S(1)}, f32[16,1,512]{2,1,0:T(1,128)S(1)}, u32[]{:S(2)}, u32[]{:S(2)}) %collective-permute-start.10) | collective-permute-done | bytes 32800 | tf_op jit(solution)/shard_map/ppermute | solution.py:29
  35.1 0.5 fusion.20.refs_2_.refs_3_
  35.6 0.1 fusion.40
  35.8 0.1 fusion.41
  35.9 0.7 collective-permute-start.13
  36.5 2.1 %collective-permute-start.12 = (f32[1,8,512]{2,1,0:T(8,128)S(1)}, f32[1,8,512]{2,1,0:T(8,128)S(1)}, u32[]{:S(2)}, u32[]{:S(2)}) collective-permute-start(f32[1,8,512]{2,1,0:T(8,128)S(1)} %get-tuple-element.28), channel_id=1, source_target_pairs={{0,8},{8,0},{16,24},{24,16},{1,9},{9,1},{17,25},{25,17},{2,10},{10... | collective-permute-start | bytes 49160 | tf_op jit(solution)/shard_map/ppermute | solution.py:29
  38.7 0.7 collective-permute-start.15
  39.3 3.7 %collective-permute-start.14 = (f32[16,1,512]{2,1,0:T(1,128)S(1)}, f32[16,1,512]{2,1,0:T(1,128)S(1)}, u32[]{:S(2)}, u32[]{:S(2)}) collective-permute-start(f32[16,1,512]{2,1,0:T(1,128)S(1)} %get-tuple-element.24), channel_id=1, source_target_pairs={{0,1},{1,0},{2,3},{3,2},{4,5},{5,4},{6,7},{7,6},{8,9},{9,8},{10,11... | collective-permute-start | bytes 98312 | tf_op jit(solution)/shard_map/ppermute | solution.py:29
  43.1 0.8 %collective-permute-done.14 = f32[16,1,512]{2,1,0:T(1,128)S(1)} collective-permute-done((f32[16,1,512]{2,1,0:T(1,128)S(1)}, f32[16,1,512]{2,1,0:T(1,128)S(1)}, u32[]{:S(2)}, u32[]{:S(2)}) %collective-permute-start.14) | collective-permute-done | bytes 32800 | tf_op jit(solution)/shard_map/ppermute | solution.py:29
  43.9 0.5 fusion.27.refs_3_.refs_4_
  44.4 0.1 fusion.37
  44.6 0.1 fusion.38
  44.6 0.7 collective-permute-start.17
  45.3 3.6 %collective-permute-start.16 = (f32[1,8,512]{2,1,0:T(8,128)S(1)}, f32[1,8,512]{2,1,0:T(8,128)S(1)}, u32[]{:S(2)}, u32[]{:S(2)}) collective-permute-start(f32[1,8,512]{2,1,0:T(8,128)S(1)} %get-tuple-element.18), channel_id=1, source_target_pairs={{0,8},{8,0},{16,24},{24,16},{1,9},{9,1},{17,25},{25,17},{2,10},{10... | collective-permute-start | bytes 49160 | tf_op jit(solution)/shard_map/ppermute | solution.py:29
  48.9 0.7 collective-permute-start.19
  49.6 3.7 %collective-permute-start.18 = (f32[16,1,512]{2,1,0:T(1,128)S(1)}, f32[16,1,512]{2,1,0:T(1,128)S(1)}, u32[]{:S(2)}, u32[]{:S(2)}) collective-permute-start(f32[16,1,512]{2,1,0:T(1,128)S(1)} %get-tuple-element.14), channel_id=1, source_target_pairs={{0,1},{1,0},{2,3},{3,2},{4,5},{5,4},{6,7},{7,6},{8,9},{9,8},{10,11... | collective-permute-start | bytes 98312 | tf_op jit(solution)/shard_map/ppermute | solution.py:29
  53.3 0.8 %collective-permute-done.18 = f32[16,1,512]{2,1,0:T(1,128)S(1)} collective-permute-done((f32[16,1,512]{2,1,0:T(1,128)S(1)}, f32[16,1,512]{2,1,0:T(1,128)S(1)}, u32[]{:S(2)}, u32[]{:S(2)}) %collective-permute-start.18) | collective-permute-done | bytes 32800 | tf_op jit(solution)/shard_map/ppermute | solution.py:29
  54.1 1.2 %fusion.34.refs_4_.refs_5_ = f32[16,8,512]{2,1,0:T(8,128)} fusion(f32[16,8,512]{2,1,0:T(8,128)S(1)} %copy-done.6, f32[15,8,512]{2,1,0:T(8,128)S(1)} %get-tuple-element.16, f32[1,8,512]{2,1,0:T(8,128)S(1)} %get-tuple-element.78, f32[1,8,512]{2,1,0:T(8,128)S(1)} %get-tuple-element.77, f32[15,8,512]{2,1,0:T(8,128)S(1)} %get-tuple-element.15, ...), kind=kLoop, calls=%fused_computation.53 | loop fusion | flops 1638400 | bytes 3668480 | tf_op jit(solution)/shard_map/div | solution.py:223
  55.3 2.3 %shard_map.85 = f32[8,128]{1,0:T(8,128)} custom-call(f32[16,8,512]{2,1,0:T(8,128)} %copy-done.3, f32[16,8,512]{2,1,0:T(8,128)} %copy-done, f32[16,8,512]{2,1,0:T(8,128)} %copy-done.1, f32[16,8,512]{2,1,0:T(8,128)} %copy-done.2, f32[16,8,512]{2,1,0:T(8,128)} %fusion.34.refs_4_.refs_5_), custom_call_target="tpu_custom_call" | custom-call | tf_op jit(solution)/shard_map/pallas_call | solution.py:107
  57.6 0.7 collective-permute-start.20
  58.3 1.0 %collective-permute-done.20 = f32[8,128]{1,0:T(8,128)S(1)} collective-permute-done((f32[8,128]{1,0:T(8,128)}, f32[8,128]{1,0:T(8,128)S(1)}, u32[]{:S(2)}, u32[]{:S(2)}) %collective-permute-start.20) | collective-permute-done | bytes 4128 | tf_op jit(solution)/shard_map/ppermute | solution.py:70
  59.3 0.7 add.178
  60.0 2.0 %collective-permute-start.21 = (f32[8,128]{1,0:T(8,128)S(1)}, f32[8,128]{1,0:T(8,128)S(1)}, u32[]{:S(2)}, u32[]{:S(2)}) collective-permute-start(f32[8,128]{1,0:T(8,128)S(1)} %add.178), channel_id=1, source_target_pairs={{0,2},{1,3},{2,0},{3,1},{4,6},{5,7},{6,4},{7,5},{8,10},{9,11},{10,... | collective-permute-start | bytes 12296 | tf_op jit(solution)/shard_map/ppermute | solution.py:70
  62.0 1.6 %collective-permute-done.21 = f32[8,128]{1,0:T(8,128)S(1)} collective-permute-done((f32[8,128]{1,0:T(8,128)S(1)}, f32[8,128]{1,0:T(8,128)S(1)}, u32[]{:S(2)}, u32[]{:S(2)}) %collective-permute-start.21) | collective-permute-done | bytes 4128 | tf_op jit(solution)/shard_map/ppermute | solution.py:70
  63.6 3.0 %collective-permute-start.22 = (f32[8,128]{1,0:T(8,128)S(1)}, f32[8,128]{1,0:T(8,128)S(1)}, u32[]{:S(2)}, u32[]{:S(2)}) collective-permute-start(f32[8,128]{1,0:T(8,128)S(1)} %add.179), channel_id=1, source_target_pairs={{0,4},{1,5},{2,6},{3,7},{4,0},{5,1},{6,2},{7,3},{8,12},{9,13},{10,... | collective-permute-start | bytes 12296 | tf_op jit(solution)/shard_map/ppermute | solution.py:70
  66.6 1.6 %collective-permute-done.22 = f32[8,128]{1,0:T(8,128)S(1)} collective-permute-done((f32[8,128]{1,0:T(8,128)S(1)}, f32[8,128]{1,0:T(8,128)S(1)}, u32[]{:S(2)}, u32[]{:S(2)}) %collective-permute-start.22) | collective-permute-done | bytes 4128 | tf_op jit(solution)/shard_map/ppermute | solution.py:70
  68.2 0.0 collective-permute-start.23
  68.2 3.6 %collective-permute-done.23 = f32[8,128]{1,0:T(8,128)S(1)} collective-permute-done((f32[8,128]{1,0:T(8,128)S(1)}, f32[8,128]{1,0:T(8,128)S(1)}, u32[]{:S(2)}, u32[]{:S(2)}) %collective-permute-start.23) | collective-permute-done | bytes 4128 | tf_op jit(solution)/shard_map/ppermute | solution.py:70
  71.8 3.6 %collective-permute-done.24 = f32[8,128]{1,0:T(8,128)S(1)} collective-permute-done((f32[8,128]{1,0:T(8,128)S(1)}, f32[8,128]{1,0:T(8,128)S(1)}, u32[]{:S(2)}, u32[]{:S(2)}) %collective-permute-start.24) | collective-permute-done | bytes 4128 | tf_op jit(solution)/shard_map/ppermute | solution.py:70
  75.4 0.6 add.182.refs_0_
  76.0 3.4 %shard_map.86 = (f32[5,16,8,512]{3,2,1,0:T(8,128)}, f32[5,5]{1,0:T(8,128)}, f32[1,1]{1,0:T(1,128)}) custom-call(f32[8,128]{1,0:T(8,128)} %add.182.refs_0_, f32[16,8,512]{2,1,0:T(8,128)} %copy-done.3, f32[16,8,512]{2,1,0:T(8,128)} %copy-done, f32[16,8,512]{2,1,0:T(8,128)} %copy-done.1, f32[16,8,512]{2,1,0:T(8,128)} %copy-done.2, ...), custom_call_target="tpu_custom_call" | custom-call | tf_op jit(solution)/shard_map/pallas_call | solution.py:179
  (62 shorter events, 0.6 us)
Async XLA Ops:
  0.6 7.9 %copy-start.4 = (f32[16,8,512]{2,1,0:T(8,128)S(1)}, f32[16,8,512]{2,1,0:T(8,128)}, u32[]{:S(2)}) copy-start(f32[16,8,512]{2,1,0:T(8,128)} %param.6) | copy-start | bytes 786436
  1.5 8.3 %collective-permute-start.1 = (f32[2,8,512]{2,1,0:T(8,128)S(1)}, f32[2,8,512]{2,1,0:T(8,128)S(1)}, u32[]{:S(2)}, u32[]{:S(2)}) collective-permute-start(f32[2,8,512]{2,1,0:T(8,128)S(1)} %get-tuple-element.75), channel_id=1, source_target_pairs={{0,8},{8,0},{16,24},{24,16},{1,9},{9,1},{17,25},{25,17},{2,10},{10... | collective-permute-start | bytes 98312 | tf_op jit(solution)/shard_map/ppermute | solution.py:29
  4.5 5.3 %collective-permute-start = (f32[2,8,512]{2,1,0:T(8,128)S(1)}, f32[2,8,512]{2,1,0:T(8,128)S(1)}, u32[]{:S(2)}, u32[]{:S(2)}) collective-permute-start(f32[2,8,512]{2,1,0:T(8,128)S(1)} %get-tuple-element.76), channel_id=1, source_target_pairs={{8,16},{16,8},{9,17},{17,9},{10,18},{18,10},{11,19},{19,11},{12,20... | collective-permute-start | bytes 98312 | tf_op jit(solution)/shard_map/ppermute | solution.py:30
  6.6 3.2 %collective-permute-start.3 = (f32[16,2,512]{2,1,0:T(2,128)S(1)}, f32[16,2,512]{2,1,0:T(2,128)S(1)}, u32[]{:S(2)}, u32[]{:S(2)}) collective-permute-start(f32[16,2,512]{2,1,0:T(2,128)S(1)} %get-tuple-element.63), channel_id=1, source_target_pairs={{0,1},{1,0},{2,3},{3,2},{4,5},{5,4},{6,7},{7,6},{8,9},{9,8},{10,11... | collective-permute-start | bytes 196616 | tf_op jit(solution)/shard_map/ppermute | solution.py:29
  6.7 2.1 %copy-start.6 = (f32[16,8,512]{2,1,0:T(8,128)S(1)}, f32[16,8,512]{2,1,0:T(8,128)}, u32[]{:S(2)}) copy-start(f32[16,8,512]{2,1,0:T(8,128)} %param.9) | copy-start | bytes 786436
  6.7 3.1 %collective-permute-start.2 = (f32[16,2,512]{2,1,0:T(2,128)S(1)}, f32[16,2,512]{2,1,0:T(2,128)S(1)}, u32[]{:S(2)}, u32[]{:S(2)}) collective-permute-start(f32[16,2,512]{2,1,0:T(2,128)S(1)} %get-tuple-element.64), channel_id=1, source_target_pairs={{1,2},{2,1},{3,4},{4,3},{5,6},{6,5},{9,10},{10,9},{11,12},{12,11},... | collective-permute-start | bytes 196616 | tf_op jit(solution)/shard_map/ppermute | solution.py:30
  8.6 1.0 %copy-start.5 = (f32[16,8,512]{2,1,0:T(8,128)S(1)}, f32[16,8,512]{2,1,0:T(8,128)}, u32[]{:S(2)}) copy-start(f32[16,8,512]{2,1,0:T(8,128)} %param.10) | copy-start | bytes 786436
  8.6 1.0 %copy-start.7 = (f32[16,8,512]{2,1,0:T(8,128)S(1)}, f32[16,8,512]{2,1,0:T(8,128)}, u32[]{:S(2)}) copy-start(f32[16,8,512]{2,1,0:T(8,128)} %param.11) | copy-start | bytes 786436
  8.8 1.1 %copy-start.8 = (f32[16,8,512]{2,1,0:T(8,128)S(1)}, f32[16,8,512]{2,1,0:T(8,128)}, u32[]{:S(2)}) copy-start(f32[16,8,512]{2,1,0:T(8,128)} %param.8) | copy-start | bytes 786436
  8.8 1.1 %copy-start.9 = (f32[16,8,512]{2,1,0:T(8,128)S(1)}, f32[16,8,512]{2,1,0:T(8,128)}, u32[]{:S(2)}) copy-start(f32[16,8,512]{2,1,0:T(8,128)} %param.7) | copy-start | bytes 786436
  10.5 6.7 %copy-start.3 = (f32[16,8,512]{2,1,0:T(8,128)}, f32[16,8,512]{2,1,0:T(8,128)S(1)}, u32[]{:S(2)}) copy-start(f32[16,8,512]{2,1,0:T(8,128)S(1)} %fusion.6.refs_0_.refs_1_) | copy-start | bytes 786436
  10.8 13.0 %collective-permute-start.5 = (f32[1,8,512]{2,1,0:T(8,128)S(1)}, f32[1,8,512]{2,1,0:T(8,128)S(1)}, u32[]{:S(2)}, u32[]{:S(2)}) collective-permute-start(f32[1,8,512]{2,1,0:T(8,128)S(1)} %get-tuple-element.47), channel_id=1, source_target_pairs={{8,16},{16,8},{9,17},{17,9},{10,18},{18,10},{11,19},{19,11},{12,20... | collective-permute-start | bytes 49160 | tf_op jit(solution)/shard_map/ppermute | solution.py:30
  11.4 12.3 %collective-permute-start.4 = (f32[1,8,512]{2,1,0:T(8,128)S(1)}, f32[1,8,512]{2,1,0:T(8,128)S(1)}, u32[]{:S(2)}, u32[]{:S(2)}) collective-permute-start(f32[1,8,512]{2,1,0:T(8,128)S(1)} %get-tuple-element.48), channel_id=1, source_target_pairs={{0,8},{8,0},{16,24},{24,16},{1,9},{9,1},{17,25},{25,17},{2,10},{10... | collective-permute-start | bytes 49160 | tf_op jit(solution)/shard_map/ppermute | solution.py:29
  17.2 6.6 %collective-permute-start.7 = (f32[16,1,512]{2,1,0:T(1,128)S(1)}, f32[16,1,512]{2,1,0:T(1,128)S(1)}, u32[]{:S(2)}, u32[]{:S(2)}) collective-permute-start(f32[16,1,512]{2,1,0:T(1,128)S(1)} %get-tuple-element.43), channel_id=1, source_target_pairs={{1,2},{2,1},{3,4},{4,3},{5,6},{6,5},{9,10},{10,9},{11,12},{12,11},... | collective-permute-start | bytes 98312 | tf_op jit(solution)/shard_map/ppermute | solution.py:30
  17.9 6.8 %collective-permute-start.6 = (f32[16,1,512]{2,1,0:T(1,128)S(1)}, f32[16,1,512]{2,1,0:T(1,128)S(1)}, u32[]{:S(2)}, u32[]{:S(2)}) collective-permute-start(f32[16,1,512]{2,1,0:T(1,128)S(1)} %get-tuple-element.44), channel_id=1, source_target_pairs={{0,1},{1,0},{2,3},{3,2},{4,5},{5,4},{6,7},{7,6},{8,9},{9,8},{10,11... | collective-permute-start | bytes 98312 | tf_op jit(solution)/shard_map/ppermute | solution.py:29
  25.1 4.7 %copy-start = (f32[16,8,512]{2,1,0:T(8,128)}, f32[16,8,512]{2,1,0:T(8,128)S(1)}, u32[]{:S(2)}) copy-start(f32[16,8,512]{2,1,0:T(8,128)S(1)} %fusion.13.refs_1_.refs_2_) | copy-start | bytes 786436
  25.4 8.9 %collective-permute-start.9 = (f32[1,8,512]{2,1,0:T(8,128)S(1)}, f32[1,8,512]{2,1,0:T(8,128)S(1)}, u32[]{:S(2)}, u32[]{:S(2)}) collective-permute-start(f32[1,8,512]{2,1,0:T(8,128)S(1)} %get-tuple-element.37), channel_id=1, source_target_pairs={{8,16},{16,8},{9,17},{17,9},{10,18},{18,10},{11,19},{19,11},{12,20... | collective-permute-start | bytes 49160 | tf_op jit(solution)/shard_map/ppermute | solution.py:30
  26.0 8.2 %collective-permute-start.8 = (f32[1,8,512]{2,1,0:T(8,128)S(1)}, f32[1,8,512]{2,1,0:T(8,128)S(1)}, u32[]{:S(2)}, u32[]{:S(2)}) collective-permute-start(f32[1,8,512]{2,1,0:T(8,128)S(1)} %get-tuple-element.38), channel_id=1, source_target_pairs={{0,8},{8,0},{16,24},{24,16},{1,9},{9,1},{17,25},{25,17},{2,10},{10... | collective-permute-start | bytes 49160 | tf_op jit(solution)/shard_map/ppermute | solution.py:29
  29.9 4.4 %collective-permute-start.11 = (f32[16,1,512]{2,1,0:T(1,128)S(1)}, f32[16,1,512]{2,1,0:T(1,128)S(1)}, u32[]{:S(2)}, u32[]{:S(2)}) collective-permute-start(f32[16,1,512]{2,1,0:T(1,128)S(1)} %get-tuple-element.33), channel_id=1, source_target_pairs={{1,2},{2,1},{3,4},{4,3},{5,6},{6,5},{9,10},{10,9},{11,12},{12,11},... | collective-permute-start | bytes 98312 | tf_op jit(solution)/shard_map/ppermute | solution.py:30
  30.5 4.6 %collective-permute-start.10 = (f32[16,1,512]{2,1,0:T(1,128)S(1)}, f32[16,1,512]{2,1,0:T(1,128)S(1)}, u32[]{:S(2)}, u32[]{:S(2)}) collective-permute-start(f32[16,1,512]{2,1,0:T(1,128)S(1)} %get-tuple-element.34), channel_id=1, source_target_pairs={{0,1},{1,0},{2,3},{3,2},{4,5},{5,4},{6,7},{7,6},{8,9},{9,8},{10,11... | collective-permute-start | bytes 98312 | tf_op jit(solution)/shard_map/ppermute | solution.py:29
  35.6 3.1 %copy-start.1 = (f32[16,8,512]{2,1,0:T(8,128)}, f32[16,8,512]{2,1,0:T(8,128)S(1)}, u32[]{:S(2)}) copy-start(f32[16,8,512]{2,1,0:T(8,128)S(1)} %fusion.20.refs_2_.refs_3_) | copy-start | bytes 786436
  35.9 7.2 %collective-permute-start.13 = (f32[1,8,512]{2,1,0:T(8,128)S(1)}, f32[1,8,512]{2,1,0:T(8,128)S(1)}, u32[]{:S(2)}, u32[]{:S(2)}) collective-permute-start(f32[1,8,512]{2,1,0:T(8,128)S(1)} %get-tuple-element.27), channel_id=1, source_target_pairs={{8,16},{16,8},{9,17},{17,9},{10,18},{18,10},{11,19},{19,11},{12,20... | collective-permute-start | bytes 49160 | tf_op jit(solution)/shard_map/ppermute | solution.py:30
  36.5 6.5 %collective-permute-start.12 = (f32[1,8,512]{2,1,0:T(8,128)S(1)}, f32[1,8,512]{2,1,0:T(8,128)S(1)}, u32[]{:S(2)}, u32[]{:S(2)}) collective-permute-start(f32[1,8,512]{2,1,0:T(8,128)S(1)} %get-tuple-element.28), channel_id=1, source_target_pairs={{0,8},{8,0},{16,24},{24,16},{1,9},{9,1},{17,25},{25,17},{2,10},{10... | collective-permute-start | bytes 49160 | tf_op jit(solution)/shard_map/ppermute | solution.py:29
  38.7 4.4 %collective-permute-start.15 = (f32[16,1,512]{2,1,0:T(1,128)S(1)}, f32[16,1,512]{2,1,0:T(1,128)S(1)}, u32[]{:S(2)}, u32[]{:S(2)}) collective-permute-start(f32[16,1,512]{2,1,0:T(1,128)S(1)} %get-tuple-element.23), channel_id=1, source_target_pairs={{1,2},{2,1},{3,4},{4,3},{5,6},{6,5},{9,10},{10,9},{11,12},{12,11},... | collective-permute-start | bytes 98312 | tf_op jit(solution)/shard_map/ppermute | solution.py:30
  39.3 4.5 %collective-permute-start.14 = (f32[16,1,512]{2,1,0:T(1,128)S(1)}, f32[16,1,512]{2,1,0:T(1,128)S(1)}, u32[]{:S(2)}, u32[]{:S(2)}) collective-permute-start(f32[16,1,512]{2,1,0:T(1,128)S(1)} %get-tuple-element.24), channel_id=1, source_target_pairs={{0,1},{1,0},{2,3},{3,2},{4,5},{5,4},{6,7},{7,6},{8,9},{9,8},{10,11... | collective-permute-start | bytes 98312 | tf_op jit(solution)/shard_map/ppermute | solution.py:29
  44.3 4.5 %copy-start.2 = (f32[16,8,512]{2,1,0:T(8,128)}, f32[16,8,512]{2,1,0:T(8,128)S(1)}, u32[]{:S(2)}) copy-start(f32[16,8,512]{2,1,0:T(8,128)S(1)} %fusion.27.refs_3_.refs_4_) | copy-start | bytes 786436
  44.6 8.6 %collective-permute-start.17 = (f32[1,8,512]{2,1,0:T(8,128)S(1)}, f32[1,8,512]{2,1,0:T(8,128)S(1)}, u32[]{:S(2)}, u32[]{:S(2)}) collective-permute-start(f32[1,8,512]{2,1,0:T(8,128)S(1)} %get-tuple-element.17), channel_id=1, source_target_pairs={{8,16},{16,8},{9,17},{17,9},{10,18},{18,10},{11,19},{19,11},{12,20... | collective-permute-start | bytes 49160 | tf_op jit(solution)/shard_map/ppermute | solution.py:30
  45.3 8.0 %collective-permute-start.16 = (f32[1,8,512]{2,1,0:T(8,128)S(1)}, f32[1,8,512]{2,1,0:T(8,128)S(1)}, u32[]{:S(2)}, u32[]{:S(2)}) collective-permute-start(f32[1,8,512]{2,1,0:T(8,128)S(1)} %get-tuple-element.18), channel_id=1, source_target_pairs={{0,8},{8,0},{16,24},{24,16},{1,9},{9,1},{17,25},{25,17},{2,10},{10... | collective-permute-start | bytes 49160 | tf_op jit(solution)/shard_map/ppermute | solution.py:29
  48.9 4.4 %collective-permute-start.19 = (f32[16,1,512]{2,1,0:T(1,128)S(1)}, f32[16,1,512]{2,1,0:T(1,128)S(1)}, u32[]{:S(2)}, u32[]{:S(2)}) collective-permute-start(f32[16,1,512]{2,1,0:T(1,128)S(1)} %get-tuple-element.13), channel_id=1, source_target_pairs={{1,2},{2,1},{3,4},{4,3},{5,6},{6,5},{9,10},{10,9},{11,12},{12,11},... | collective-permute-start | bytes 98312 | tf_op jit(solution)/shard_map/ppermute | solution.py:30
  49.6 4.5 %collective-permute-start.18 = (f32[16,1,512]{2,1,0:T(1,128)S(1)}, f32[16,1,512]{2,1,0:T(1,128)S(1)}, u32[]{:S(2)}, u32[]{:S(2)}) collective-permute-start(f32[16,1,512]{2,1,0:T(1,128)S(1)} %get-tuple-element.14), channel_id=1, source_target_pairs={{0,1},{1,0},{2,3},{3,2},{4,5},{5,4},{6,7},{7,6},{8,9},{9,8},{10,11... | collective-permute-start | bytes 98312 | tf_op jit(solution)/shard_map/ppermute | solution.py:29
  57.6 1.7 %collective-permute-start.20 = (f32[8,128]{1,0:T(8,128)}, f32[8,128]{1,0:T(8,128)S(1)}, u32[]{:S(2)}, u32[]{:S(2)}) collective-permute-start(f32[8,128]{1,0:T(8,128)} %shard_map.85), channel_id=1, source_target_pairs={{0,1},{1,0},{2,3},{3,2},{4,5},{5,4},{6,7},{7,6},{8,9},{9,8},{10,11... | collective-permute-start | bytes 12296 | tf_op jit(solution)/shard_map/ppermute | solution.py:70
  60.0 3.6 %collective-permute-start.21 = (f32[8,128]{1,0:T(8,128)S(1)}, f32[8,128]{1,0:T(8,128)S(1)}, u32[]{:S(2)}, u32[]{:S(2)}) collective-permute-start(f32[8,128]{1,0:T(8,128)S(1)} %add.178), channel_id=1, source_target_pairs={{0,2},{1,3},{2,0},{3,1},{4,6},{5,7},{6,4},{7,5},{8,10},{9,11},{10,... | collective-permute-start | bytes 12296 | tf_op jit(solution)/shard_map/ppermute | solution.py:70
  63.6 4.6 %collective-permute-start.22 = (f32[8,128]{1,0:T(8,128)S(1)}, f32[8,128]{1,0:T(8,128)S(1)}, u32[]{:S(2)}, u32[]{:S(2)}) collective-permute-start(f32[8,128]{1,0:T(8,128)S(1)} %add.179), channel_id=1, source_target_pairs={{0,4},{1,5},{2,6},{3,7},{4,0},{5,1},{6,2},{7,3},{8,12},{9,13},{10,... | collective-permute-start | bytes 12296 | tf_op jit(solution)/shard_map/ppermute | solution.py:70
  68.2 3.6 %collective-permute-start.23 = (f32[8,128]{1,0:T(8,128)S(1)}, f32[8,128]{1,0:T(8,128)S(1)}, u32[]{:S(2)}, u32[]{:S(2)}) collective-permute-start(f32[8,128]{1,0:T(8,128)S(1)} %add.180), channel_id=1, source_target_pairs={{0,8},{8,0},{16,24},{24,16},{1,9},{9,1},{17,25},{25,17},{2,10},{10... | collective-permute-start | bytes 12296 | tf_op jit(solution)/shard_map/ppermute | solution.py:70
  71.8 3.6 %collective-permute-start.24 = (f32[8,128]{1,0:T(8,128)S(1)}, f32[8,128]{1,0:T(8,128)S(1)}, u32[]{:S(2)}, u32[]{:S(2)}) collective-permute-start(f32[8,128]{1,0:T(8,128)S(1)} %add.181), channel_id=1, source_target_pairs={{0,16},{8,24},{16,0},{24,8},{1,17},{9,25},{17,1},{25,9},{2,18},{10... | collective-permute-start | bytes 12296 | tf_op jit(solution)/shard_map/ppermute | solution.py:70

commit v13 on v6

--- a/solution.py
+++ b/solution.py
@@ -56,7 +56,8 @@
 
 
 def field_halo(u):
-    return exchange(u[:1], u[-1:], u[:, :1], u[:, -1:])
+    lo_x, hi_x, lo_y, hi_y = exchange(u[:1], u[-1:], u[:, 0], u[:, -1])
+    return lo_x, hi_x, lo_y[:, None], hi_y[:, None]
 
 
 def all_sum(x):
@@ -190,11 +191,12 @@
     lo_both_x, hi_both_x, lo_both_y, hi_both_y = exchange(
         jnp.concatenate([start_field[:1], trans_x[:1]], axis=0),
         jnp.concatenate([start_field[-1:], trans_x[-1:]], axis=0),
-        jnp.concatenate([start_field[:, :1], trans_y[:, :1]], axis=1),
-        jnp.concatenate([start_field[:, -1:], trans_y[:, -1:]], axis=1),
+        jnp.concatenate([start_field[:, 0], trans_y[:, 0]], axis=0),
+        jnp.concatenate([start_field[:, -1], trans_y[:, -1]], axis=0),
     )
+    size_x = start_field.shape[0]
     lo_x, hi_x, plane_x = lo_both_x[:1], hi_both_x[:1], hi_both_x[1:]
-    lo_y, hi_y, plane_y = lo_both_y[:, :1], hi_both_y[:, :1], hi_both_y[:, 1:]
+    lo_y, hi_y, plane_y = (a[:, None] for a in (lo_both_y[:size_x], hi_both_y[:size_x], hi_both_y[size_x:]))
 
     zero_plane = jnp.zeros_like(trans_z[..., :1])
     tx_lo = trans_x

time: 79.3 us -> 86.7 us (1.093)
  local copies, waits for them, and re-layouts: 5.32 us -> 10.5 us
  other arithmetic: 4.77 us -> 8.81 us
  starting transfers between devices: 47.6 us -> 46.2 us
    unnamed x20 -> x28, local copies, waits for them, and re-layouts: 0.77 us -> 5.04 us
    add x0 -> x3, other arithmetic: none -> 1.47 us  [the longest x1 0.72 us: neighbour_sum(): total = total + tz_lo * u_zm + tz_hi * u_zp]
    ppermute x10, starting transfers between devices: 35.2 us -> 34 us  [axis_exchange(): lax.ppermute(jnp.where(odd, to_low, to_high), axis, swap_pairs(axis, 0))]
    slice x5 -> x4, local copies, waits for them, and re-layouts: 1.29 us -> 0.18 us  [neighbour_sum(): u_yp = jnp.concatenate([u[:, 1:], hi_y], axis=1)]
    sub x0 -> x1, local copies, waits for them, and re-layouts: none -> 0.88 us  [local(): residual0 = right_side - (diagonal * start_field - total)]
  transfers between devices with their start and end apart: 25 -> 25, of which waited for: 9 -> 9; matrix products, arithmetic and copies ran while one was open for 4% -> 7% of each run, Pallas kernels for 0% -> 0%
where the time goes in v13:
time: 86.7 us; the launch traced here: 86 us
  starting transfers between devices  46.2 us (53%)
  waiting for transfers between devices  14.2 us (16%)
  local copies, waits for them, and re-layouts  10.5 us (12%)
  other arithmetic  8.81 us (10%)
  Pallas kernels  5.06 us (6%)
  between operations  1.27 us (1%)
    ppermute x10, starting transfers between devices, axis_exchange(): lax.ppermute(jnp.where(odd, to_low, to_high), axis, swap_pairs(axis, 0))  34 us
    ppermute x5, waiting for transfers between devices, all_sum(): x = x + lax.ppermute(x, axis, [(i, i ^ step) for i in range(n)])  11.4 us
    ppermute x10, starting transfers between devices, axis_exchange(): lax.ppermute(jnp.where(odd, to_high, to_low), axis, swap_pairs(axis, 1))  6.59 us
    ppermute x5, starting transfers between devices, all_sum(): x = x + lax.ppermute(x, axis, [(i, i ^ step) for i in range(n)])  5.64 us
    unnamed x28, local copies, waits for them, and re-layouts  5.04 us
    div x4, other arithmetic, local(): vector = 2.0 * total / diagonal  2.87 us
    pallas_call x1, Pallas kernels, finish(): pl.pallas_call(lambda *refs: finish_kernel(float(cells), size, *refs), ou...  2.75 us
    ppermute x10, waiting for transfers between devices, axis_exchange(): lax.ppermute(jnp.where(odd, to_low, to_high), axis, swap_pairs(axis, 0))  2.75 us
  transfers between devices with their start and end apart: 25, of which 9 were waited for; matrix products, arithmetic and copies ran while one was open for 7% of the time, Pallas kernels for 0%

profile of v13, /device:TPU:0, one launch (start us, length us, event | category | flops | bytes accessed | tf_op | source)
XLA Modules:
  0.0 86.0 jit_solution(11774500925581424263)
XLA Ops:
  0.6 0.7 fusion.60
  1.4 0.7 fusion.59
  2.3 0.7 collective-permute-start
  3.0 5.7 %collective-permute-start.1 = (f32[2,8,512]{2,0,1:T(2,128)S(1)}, f32[2,8,512]{2,0,1:T(2,128)S(1)}, u32[]{:S(2)}, u32[]{:S(2)}) collective-permute-start(f32[2,8,512]{2,0,1:T(2,128)S(1)} %get-tuple-element.81), channel_id=1, source_target_pairs={{0,8},{8,0},{16,24},{24,16},{1,9},{9,1},{17,25},{25,17},{2,10},{10... | collective-permute-start | bytes 98312 | tf_op jit(solution)/shard_map/ppermute | solution.py:29
  8.7 1.1 %copy.18 = f32[16,8,512]{2,0,1:T(8,128)S(1)} copy(f32[16,8,512]{2,1,0:T(8,128)} %param.6) | data formatting | bytes 524288 | tf_op args[0]
  9.8 1.1 %copy.16 = f32[16,8,512]{2,0,1:T(8,128)S(1)} copy(f32[16,8,512]{2,1,0:T(8,128)} %param.10) | data formatting | bytes 524288 | tf_op args[4]
  11.0 0.7 collective-permute-start.2
  11.7 3.0 %collective-permute-start.3 = (f32[32,512]{1,0:T(8,128)S(1)}, f32[32,512]{1,0:T(8,128)S(1)}, u32[]{:S(2)}, u32[]{:S(2)}) collective-permute-start(f32[32,512]{1,0:T(8,128)S(1)} %get-tuple-element.65), channel_id=1, source_target_pairs={{0,1},{1,0},{2,3},{3,2},{4,5},{5,4},{6,7},{7,6},{8,9},{9,8},{10,11... | collective-permute-start | bytes 196616 | tf_op jit(solution)/shard_map/ppermute | solution.py:29
  14.9 0.7 slice-done
  15.7 0.1 copy.152
  16.0 0.2 copy.153
  16.3 0.3 copy-done.2
  16.8 0.7 pad_maximum_fusion.1
  17.4 0.3 copy_add_fusion.1
  17.8 1.4 %fusion.6 = f32[16,8,512]{2,0,1:T(8,128)S(1)} fusion(f32[15,8,512]{2,0,1:T(8,128)S(1)} %get-tuple-element.60, f32[1,8,512]{2,0,1:T(1,128)S(1)} %get-tuple-element.99, f32[1,8,512]{2,0,1:T(1,128)S(1)} %get-tuple-element.96, f32[15,8,512]{2,0,1:T(8,128)S(1)} %get-tuple-element.59, f32[16,7,512]{2,0,1:T(8,128)S(1)} %get-tuple-element.54, ...), kind=kLoop, calls=%fused_computation.9 | loop fusion | flops 1310720 | bytes 4192768 | tf_op jit(solution)/shard_map/sub | solution.py:212
  19.5 0.7 collective-permute-start.5
  20.1 2.8 %collective-permute-start.4 = (f32[1,8,512]{2,0,1:T(1,128)S(1)}, f32[1,8,512]{2,0,1:T(1,128)S(1)}, u32[]{:S(2)}, u32[]{:S(2)}) collective-permute-start(f32[1,8,512]{2,0,1:T(1,128)S(1)} %get-tuple-element.50), channel_id=1, source_target_pairs={{0,8},{8,0},{16,24},{24,16},{1,9},{9,1},{17,25},{25,17},{2,10},{10... | collective-permute-start | bytes 49160 | tf_op jit(solution)/shard_map/ppermute | solution.py:29
  22.9 0.9 %copy.74.refs_0_.refs_1_ = f32[16,8,512]{2,1,0:T(8,128)} copy(f32[16,8,512]{2,0,1:T(8,128)S(1)} %fusion.6) | data formatting | bytes 524288 | tf_op jit(solution)/shard_map/sub | solution.py:212
  23.8 0.7 collective-permute-start.7
  24.4 3.0 %collective-permute-start.6 = (f32[16,512]{1,0:T(8,128)S(1)}, f32[16,512]{1,0:T(8,128)S(1)}, u32[]{:S(2)}, u32[]{:S(2)}) collective-permute-start(f32[16,512]{1,0:T(8,128)S(1)} %get-tuple-element.46), channel_id=1, source_target_pairs={{0,1},{1,0},{2,3},{3,2},{4,5},{5,4},{6,7},{7,6},{8,9},{9,8},{10,11... | collective-permute-start | bytes 98312 | tf_op jit(solution)/shard_map/ppermute | solution.py:29
  27.5 0.8 collective-permute-done.6
  28.3 1.0 %fusion.13 = f32[16,8,512]{2,0,1:T(8,128)S(1)} fusion(f32[15,8,512]{2,0,1:T(8,128)S(1)} %get-tuple-element.48, f32[1,8,512]{2,0,1:T(1,128)S(1)} %bitcast.72, f32[1,8,512]{2,0,1:T(1,128)S(1)} %bitcast.71, f32[15,8,512]{2,0,1:T(8,128)S(1)} %get-tuple-element.47, f32[16,7,512]{2,0,1:T(8,128)S(1)} %get-tuple-element.44, f32[16,1,512]{2,0,1:T(8,128)S(1)} %get-tuple-element.78, ...), kind=kLoop, calls=%fused_computation.20 | loop fusion | flops 1245184 | bytes 3668480 | tf_op jit(solution)/shard_map/div | solution.py:218
  29.6 0.7 collective-permute-start.9
  30.2 2.9 %collective-permute-start.8 = (f32[1,8,512]{2,0,1:T(1,128)S(1)}, f32[1,8,512]{2,0,1:T(1,128)S(1)}, u32[]{:S(2)}, u32[]{:S(2)}) collective-permute-start(f32[1,8,512]{2,0,1:T(1,128)S(1)} %get-tuple-element.40), channel_id=1, source_target_pairs={{0,8},{8,0},{16,24},{24,16},{1,9},{9,1},{17,25},{25,17},{2,10},{10... | collective-permute-start | bytes 49160 | tf_op jit(solution)/shard_map/ppermute | solution.py:29
  33.1 0.9 %copy.75.refs_1_.refs_2_ = f32[16,8,512]{2,1,0:T(8,128)} copy(f32[16,8,512]{2,0,1:T(8,128)S(1)} %fusion.13) | data formatting | bytes 524288 | tf_op jit(solution)/shard_map/div | solution.py:218
  34.0 0.7 collective-permute-start.11
  34.6 3.7 %collective-permute-start.10 = (f32[16,512]{1,0:T(8,128)S(1)}, f32[16,512]{1,0:T(8,128)S(1)}, u32[]{:S(2)}, u32[]{:S(2)}) collective-permute-start(f32[16,512]{1,0:T(8,128)S(1)} %get-tuple-element.36), channel_id=1, source_target_pairs={{0,1},{1,0},{2,3},{3,2},{4,5},{5,4},{6,7},{7,6},{8,9},{9,8},{10,11... | collective-permute-start | bytes 98312 | tf_op jit(solution)/shard_map/ppermute | solution.py:29
  38.3 0.8 collective-permute-done.10
  39.2 0.8 fusion.19
  40.0 0.2 copy_divide_fusion.refs_2_.refs_3_
  40.5 0.4 copy-done
  40.9 0.7 collective-permute-start.13
  41.6 2.8 %collective-permute-start.12 = (f32[1,8,512]{2,0,1:T(1,128)S(1)}, f32[1,8,512]{2,0,1:T(1,128)S(1)}, u32[]{:S(2)}, u32[]{:S(2)}) collective-permute-start(f32[1,8,512]{2,0,1:T(1,128)S(1)} %get-tuple-element.90), channel_id=1, source_target_pairs={{0,8},{8,0},{16,24},{24,16},{1,9},{9,1},{17,25},{25,17},{2,10},{10... | collective-permute-start | bytes 49160 | tf_op jit(solution)/shard_map/ppermute | solution.py:29
  44.4 0.1 collective-permute-start.14
  44.5 0.7 collective-permute-start.15
  45.2 0.1 copy.80
  45.4 0.1 copy.81
  45.5 0.1 copy.84
  45.7 0.6 collective-permute-done.12
  46.3 0.5 fusion.21
  46.7 0.6 fusion.26.refs_3_.refs_4_
  47.7 0.4 copy-done.1
  48.1 0.7 collective-permute-start.17
  48.8 4.7 %collective-permute-start.16 = (f32[1,8,512]{2,0,1:T(1,128)S(1)}, f32[1,8,512]{2,0,1:T(1,128)S(1)}, u32[]{:S(2)}, u32[]{:S(2)}) collective-permute-start(f32[1,8,512]{2,0,1:T(1,128)S(1)} %get-tuple-element.86), channel_id=1, source_target_pairs={{0,8},{8,0},{16,24},{24,16},{1,9},{9,1},{17,25},{25,17},{2,10},{10... | collective-permute-start | bytes 49160 | tf_op jit(solution)/shard_map/ppermute | solution.py:29
  53.5 0.1 copy.87
  53.7 0.1 copy.88
  54.0 0.7 collective-permute-start.19
  54.6 5.3 %collective-permute-start.18 = (f32[16,512]{1,0:T(8,128)S(1)}, f32[16,512]{1,0:T(8,128)S(1)}, u32[]{:S(2)}, u32[]{:S(2)}) collective-permute-start(f32[16,512]{1,0:T(8,128)S(1)} %get-tuple-element.70), channel_id=1, source_target_pairs={{0,1},{1,0},{2,3},{3,2},{4,5},{5,4},{6,7},{7,6},{8,9},{9,8},{10,11... | collective-permute-start | bytes 98312 | tf_op jit(solution)/shard_map/ppermute | solution.py:29
  60.0 0.2 copy.93
  60.3 0.5 collective-permute-done.18
  60.8 0.7 fusion.30
  61.5 1.1 %fusion.32.refs_4_.refs_5_ = f32[16,8,512]{2,1,0:T(8,128)} fusion(f32[16,8,512]{2,1,0:T(8,128)S(1)} %copy_add_fusion.1, f32[16,8,512]{2,0,1:T(8,128)S(1)} %fusion.30, f32[16,8,511]{2,1,0:T(8,128)S(1)} %get-tuple-element.9, f32[16,8,512]{2,0,1:T(8,128)S(1)} %concatenate.117), kind=kLoop, calls=%fused_computation.55 | loop fusion | flops 262144 | bytes 1310208 | tf_op jit(solution)/shard_map/div | solution.py:218
  62.6 2.3 %shard_map.85 = f32[8,128]{1,0:T(8,128)} custom-call(f32[16,8,512]{2,1,0:T(8,128)} %copy.74.refs_0_.refs_1_, f32[16,8,512]{2,1,0:T(8,128)} %copy.75.refs_1_.refs_2_, f32[16,8,512]{2,1,0:T(8,128)} %copy-done, f32[16,8,512]{2,1,0:T(8,128)} %copy-done.1, f32[16,8,512]{2,1,0:T(8,128)} %fusion.32.refs_4_.refs_5_), custom_call_target="tpu_custom_call" | custom-call | tf_op jit(solution)/shard_map/pallas_call | solution.py:108
  64.9 0.7 collective-permute-start.20
  65.5 1.0 %collective-permute-done.20 = f32[8,128]{1,0:T(8,128)S(1)} collective-permute-done((f32[8,128]{1,0:T(8,128)}, f32[8,128]{1,0:T(8,128)S(1)}, u32[]{:S(2)}, u32[]{:S(2)}) %collective-permute-start.20) | collective-permute-done | bytes 4128 | tf_op jit(solution)/shard_map/ppermute | solution.py:71
  66.6 0.7 add.178
  67.3 2.0 %collective-permute-start.21 = (f32[8,128]{1,0:T(8,128)S(1)}, f32[8,128]{1,0:T(8,128)S(1)}, u32[]{:S(2)}, u32[]{:S(2)}) collective-permute-start(f32[8,128]{1,0:T(8,128)S(1)} %add.178), channel_id=1, source_target_pairs={{0,2},{1,3},{2,0},{3,1},{4,6},{5,7},{6,4},{7,5},{8,10},{9,11},{10,... | collective-permute-start | bytes 12296 | tf_op jit(solution)/shard_map/ppermute | solution.py:71
  69.2 1.6 %collective-permute-done.21 = f32[8,128]{1,0:T(8,128)S(1)} collective-permute-done((f32[8,128]{1,0:T(8,128)S(1)}, f32[8,128]{1,0:T(8,128)S(1)}, u32[]{:S(2)}, u32[]{:S(2)}) %collective-permute-start.21) | collective-permute-done | bytes 4128 | tf_op jit(solution)/shard_map/ppermute | solution.py:71
  70.9 3.0 %collective-permute-start.22 = (f32[8,128]{1,0:T(8,128)S(1)}, f32[8,128]{1,0:T(8,128)S(1)}, u32[]{:S(2)}, u32[]{:S(2)}) collective-permute-start(f32[8,128]{1,0:T(8,128)S(1)} %add.179), channel_id=1, source_target_pairs={{0,4},{1,5},{2,6},{3,7},{4,0},{5,1},{6,2},{7,3},{8,12},{9,13},{10,... | collective-permute-start | bytes 12296 | tf_op jit(solution)/shard_map/ppermute | solution.py:71
  73.9 1.6 %collective-permute-done.22 = f32[8,128]{1,0:T(8,128)S(1)} collective-permute-done((f32[8,128]{1,0:T(8,128)S(1)}, f32[8,128]{1,0:T(8,128)S(1)}, u32[]{:S(2)}, u32[]{:S(2)}) %collective-permute-start.22) | collective-permute-done | bytes 4128 | tf_op jit(solution)/shard_map/ppermute | solution.py:71
  75.5 3.6 %collective-permute-done.23 = f32[8,128]{1,0:T(8,128)S(1)} collective-permute-done((f32[8,128]{1,0:T(8,128)S(1)}, f32[8,128]{1,0:T(8,128)S(1)}, u32[]{:S(2)}, u32[]{:S(2)}) %collective-permute-start.23) | collective-permute-done | bytes 4128 | tf_op jit(solution)/shard_map/ppermute | solution.py:71
  79.1 3.6 %collective-permute-done.24 = f32[8,128]{1,0:T(8,128)S(1)} collective-permute-done((f32[8,128]{1,0:T(8,128)S(1)}, f32[8,128]{1,0:T(8,128)S(1)}, u32[]{:S(2)}, u32[]{:S(2)}) %collective-permute-start.24) | collective-permute-done | bytes 4128 | tf_op jit(solution)/shard_map/ppermute | solution.py:71
  82.7 0.6 add.182.refs_0_
  83.3 2.8 %shard_map.86 = (f32[5,16,8,512]{3,2,1,0:T(8,128)}, f32[5,5]{1,0:T(8,128)}, f32[1,1]{1,0:T(1,128)}) custom-call(f32[8,128]{1,0:T(8,128)} %add.182.refs_0_, f32[16,8,512]{2,1,0:T(8,128)} %copy.74.refs_0_.refs_1_, f32[16,8,512]{2,1,0:T(8,128)} %copy.75.refs_1_.refs_2_, f32[16,8,512]{2,1,0:T(8,128)} %copy-done, f32[16,8,512]{2,1,0:T(8,128)} %copy-done.1, ...), custom_call_target="tpu_custom_call" | custom-call | tf_op jit(solution)/shard_map/pallas_call | solution.py:174
  (88 shorter events, 2.5 us)
Async XLA Ops:
  2.3 13.9 %collective-permute-start = (f32[2,8,512]{2,0,1:T(2,128)S(1)}, f32[2,8,512]{2,0,1:T(2,128)S(1)}, u32[]{:S(2)}, u32[]{:S(2)}) collective-permute-start(f32[2,8,512]{2,0,1:T(2,128)S(1)} %get-tuple-element.82), channel_id=1, source_target_pairs={{8,16},{16,8},{9,17},{17,9},{10,18},{18,10},{11,19},{19,11},{12,20... | collective-permute-start | bytes 98312 | tf_op jit(solution)/shard_map/ppermute | solution.py:30
  3.0 13.2 %collective-permute-start.1 = (f32[2,8,512]{2,0,1:T(2,128)S(1)}, f32[2,8,512]{2,0,1:T(2,128)S(1)}, u32[]{:S(2)}, u32[]{:S(2)}) collective-permute-start(f32[2,8,512]{2,0,1:T(2,128)S(1)} %get-tuple-element.81), channel_id=1, source_target_pairs={{0,8},{8,0},{16,24},{24,16},{1,9},{9,1},{17,25},{25,17},{2,10},{10... | collective-permute-start | bytes 98312 | tf_op jit(solution)/shard_map/ppermute | solution.py:29
  11.0 5.3 %collective-permute-start.2 = (f32[32,512]{1,0:T(8,128)S(1)}, f32[32,512]{1,0:T(8,128)S(1)}, u32[]{:S(2)}, u32[]{:S(2)}) collective-permute-start(f32[32,512]{1,0:T(8,128)S(1)} %get-tuple-element.66), channel_id=1, source_target_pairs={{1,2},{2,1},{3,4},{4,3},{5,6},{6,5},{9,10},{10,9},{11,12},{12,11},... | collective-permute-start | bytes 196616 | tf_op jit(solution)/shard_map/ppermute | solution.py:30
  11.7 4.6 %collective-permute-start.3 = (f32[32,512]{1,0:T(8,128)S(1)}, f32[32,512]{1,0:T(8,128)S(1)}, u32[]{:S(2)}, u32[]{:S(2)}) collective-permute-start(f32[32,512]{1,0:T(8,128)S(1)} %get-tuple-element.65), channel_id=1, source_target_pairs={{0,1},{1,0},{2,3},{3,2},{4,5},{5,4},{6,7},{7,6},{8,9},{9,8},{10,11... | collective-permute-start | bytes 196616 | tf_op jit(solution)/shard_map/ppermute | solution.py:29
  14.7 0.9 %slice-start = ((f32[16,8,512]{2,1,0:T(8,128)}), f32[15,8,512]{2,1,0:T(8,128)S(1)}, s32[]{:S(2)}) async-start(f32[16,8,512]{2,1,0:T(8,128)} %param.9), calls=%async_computation | async-start | bytes 491520 | tf_op jit(solution)/shard_map/slice | solution.py:203
  14.9 1.0 %copy-start.4 = (f32[16,8,512]{2,1,0:T(8,128)S(1)}, f32[16,8,512]{2,1,0:T(8,128)}, u32[]{:S(2)}) copy-start(f32[16,8,512]{2,1,0:T(8,128)} %param.11) | copy-start | bytes 786436
  15.7 1.0 %copy-start.2 = (f32[16,8,512]{2,1,0:T(8,128)S(1)}, f32[16,8,512]{2,1,0:T(8,128)}, u32[]{:S(2)}) copy-start(f32[16,8,512]{2,1,0:T(8,128)} %param.9) | copy-start | bytes 786436
  15.7 1.0 %copy-start.3 = (f32[16,8,512]{2,1,0:T(8,128)S(1)}, f32[16,8,512]{2,1,0:T(8,128)}, u32[]{:S(2)}) copy-start(f32[16,8,512]{2,1,0:T(8,128)} %param.10) | copy-start | bytes 786436
  15.7 1.1 %copy-start.7 = (f32[16,8,512]{2,1,0:T(8,128)S(1)}, f32[16,8,512]{2,1,0:T(8,128)}, u32[]{:S(2)}) copy-start(f32[16,8,512]{2,1,0:T(8,128)} %param.8) | copy-start | bytes 786436
  16.8 1.0 %copy-start.5 = (f32[16,8,512]{2,1,0:T(8,128)S(1)}, f32[16,8,512]{2,1,0:T(8,128)}, u32[]{:S(2)}) copy-start(f32[16,8,512]{2,1,0:T(8,128)} %param.6) | copy-start | bytes 786436
  16.8 1.0 %copy-start.6 = (f32[16,8,512]{2,1,0:T(8,128)S(1)}, f32[16,8,512]{2,1,0:T(8,128)}, u32[]{:S(2)}) copy-start(f32[16,8,512]{2,1,0:T(8,128)} %param.7) | copy-start | bytes 786436
  19.5 8.0 %collective-permute-start.5 = (f32[1,8,512]{2,0,1:T(1,128)S(1)}, f32[1,8,512]{2,0,1:T(1,128)S(1)}, u32[]{:S(2)}, u32[]{:S(2)}) collective-permute-start(f32[1,8,512]{2,0,1:T(1,128)S(1)} %get-tuple-element.49), channel_id=1, source_target_pairs={{8,16},{16,8},{9,17},{17,9},{10,18},{18,10},{11,19},{19,11},{12,20... | collective-permute-start | bytes 49160 | tf_op jit(solution)/shard_map/ppermute | solution.py:30
  20.1 7.3 %collective-permute-start.4 = (f32[1,8,512]{2,0,1:T(1,128)S(1)}, f32[1,8,512]{2,0,1:T(1,128)S(1)}, u32[]{:S(2)}, u32[]{:S(2)}) collective-permute-start(f32[1,8,512]{2,0,1:T(1,128)S(1)} %get-tuple-element.50), channel_id=1, source_target_pairs={{0,8},{8,0},{16,24},{24,16},{1,9},{9,1},{17,25},{25,17},{2,10},{10... | collective-permute-start | bytes 49160 | tf_op jit(solution)/shard_map/ppermute | solution.py:29
  23.8 3.7 %collective-permute-start.7 = (f32[16,512]{1,0:T(8,128)S(1)}, f32[16,512]{1,0:T(8,128)S(1)}, u32[]{:S(2)}, u32[]{:S(2)}) collective-permute-start(f32[16,512]{1,0:T(8,128)S(1)} %get-tuple-element.45), channel_id=1, source_target_pairs={{1,2},{2,1},{3,4},{4,3},{5,6},{6,5},{9,10},{10,9},{11,12},{12,11},... | collective-permute-start | bytes 98312 | tf_op jit(solution)/shard_map/ppermute | solution.py:30
  24.4 3.9 %collective-permute-start.6 = (f32[16,512]{1,0:T(8,128)S(1)}, f32[16,512]{1,0:T(8,128)S(1)}, u32[]{:S(2)}, u32[]{:S(2)}) collective-permute-start(f32[16,512]{1,0:T(8,128)S(1)} %get-tuple-element.46), channel_id=1, source_target_pairs={{0,1},{1,0},{2,3},{3,2},{4,5},{5,4},{6,7},{7,6},{8,9},{9,8},{10,11... | collective-permute-start | bytes 98312 | tf_op jit(solution)/shard_map/ppermute | solution.py:29
  29.6 8.7 %collective-permute-start.9 = (f32[1,8,512]{2,0,1:T(1,128)S(1)}, f32[1,8,512]{2,0,1:T(1,128)S(1)}, u32[]{:S(2)}, u32[]{:S(2)}) collective-permute-start(f32[1,8,512]{2,0,1:T(1,128)S(1)} %get-tuple-element.39), channel_id=1, source_target_pairs={{8,16},{16,8},{9,17},{17,9},{10,18},{18,10},{11,19},{19,11},{12,20... | collective-permute-start | bytes 49160 | tf_op jit(solution)/shard_map/ppermute | solution.py:30
  30.2 8.1 %collective-permute-start.8 = (f32[1,8,512]{2,0,1:T(1,128)S(1)}, f32[1,8,512]{2,0,1:T(1,128)S(1)}, u32[]{:S(2)}, u32[]{:S(2)}) collective-permute-start(f32[1,8,512]{2,0,1:T(1,128)S(1)} %get-tuple-element.40), channel_id=1, source_target_pairs={{0,8},{8,0},{16,24},{24,16},{1,9},{9,1},{17,25},{25,17},{2,10},{10... | collective-permute-start | bytes 49160 | tf_op jit(solution)/shard_map/ppermute | solution.py:29
  34.0 4.4 %collective-permute-start.11 = (f32[16,512]{1,0:T(8,128)S(1)}, f32[16,512]{1,0:T(8,128)S(1)}, u32[]{:S(2)}, u32[]{:S(2)}) collective-permute-start(f32[16,512]{1,0:T(8,128)S(1)} %get-tuple-element.35), channel_id=1, source_target_pairs={{1,2},{2,1},{3,4},{4,3},{5,6},{6,5},{9,10},{10,9},{11,12},{12,11},... | collective-permute-start | bytes 98312 | tf_op jit(solution)/shard_map/ppermute | solution.py:30
  34.6 4.5 %collective-permute-start.10 = (f32[16,512]{1,0:T(8,128)S(1)}, f32[16,512]{1,0:T(8,128)S(1)}, u32[]{:S(2)}, u32[]{:S(2)}) collective-permute-start(f32[16,512]{1,0:T(8,128)S(1)} %get-tuple-element.36), channel_id=1, source_target_pairs={{0,1},{1,0},{2,3},{3,2},{4,5},{5,4},{6,7},{7,6},{8,9},{9,8},{10,11... | collective-permute-start | bytes 98312 | tf_op jit(solution)/shard_map/ppermute | solution.py:29
  40.2 0.7 copy-start
  40.9 4.7 %collective-permute-start.13 = (f32[1,8,512]{2,0,1:T(1,128)S(1)}, f32[1,8,512]{2,0,1:T(1,128)S(1)}, u32[]{:S(2)}, u32[]{:S(2)}) collective-permute-start(f32[1,8,512]{2,0,1:T(1,128)S(1)} %get-tuple-element.89), channel_id=1, source_target_pairs={{8,16},{16,8},{9,17},{17,9},{10,18},{18,10},{11,19},{19,11},{12,20... | collective-permute-start | bytes 49160 | tf_op jit(solution)/shard_map/ppermute | solution.py:30
  41.6 4.6 %collective-permute-start.12 = (f32[1,8,512]{2,0,1:T(1,128)S(1)}, f32[1,8,512]{2,0,1:T(1,128)S(1)}, u32[]{:S(2)}, u32[]{:S(2)}) collective-permute-start(f32[1,8,512]{2,0,1:T(1,128)S(1)} %get-tuple-element.90), channel_id=1, source_target_pairs={{0,8},{8,0},{16,24},{24,16},{1,9},{9,1},{17,25},{25,17},{2,10},{10... | collective-permute-start | bytes 49160 | tf_op jit(solution)/shard_map/ppermute | solution.py:29
  44.4 1.8 %collective-permute-start.14 = (f32[16,512]{1,0:T(8,128)S(1)}, f32[16,512]{1,0:T(8,128)S(1)}, u32[]{:S(2)}, u32[]{:S(2)}) collective-permute-start(f32[16,512]{1,0:T(8,128)S(1)} %get-tuple-element.73), channel_id=1, source_target_pairs={{0,1},{1,0},{2,3},{3,2},{4,5},{5,4},{6,7},{7,6},{8,9},{9,8},{10,11... | collective-permute-start | bytes 98312 | tf_op jit(solution)/shard_map/ppermute | solution.py:29
  44.5 1.7 %collective-permute-start.15 = (f32[16,512]{1,0:T(8,128)S(1)}, f32[16,512]{1,0:T(8,128)S(1)}, u32[]{:S(2)}, u32[]{:S(2)}) collective-permute-start(f32[16,512]{1,0:T(8,128)S(1)} %get-tuple-element.74), channel_id=1, source_target_pairs={{1,2},{2,1},{3,4},{4,3},{5,6},{6,5},{9,10},{10,9},{11,12},{12,11},... | collective-permute-start | bytes 98312 | tf_op jit(solution)/shard_map/ppermute | solution.py:30
  47.4 0.7 copy-start.1
  48.1 12.1 %collective-permute-start.17 = (f32[1,8,512]{2,0,1:T(1,128)S(1)}, f32[1,8,512]{2,0,1:T(1,128)S(1)}, u32[]{:S(2)}, u32[]{:S(2)}) collective-permute-start(f32[1,8,512]{2,0,1:T(1,128)S(1)} %get-tuple-element.85), channel_id=1, source_target_pairs={{8,16},{16,8},{9,17},{17,9},{10,18},{18,10},{11,19},{19,11},{12,20... | collective-permute-start | bytes 49160 | tf_op jit(solution)/shard_map/ppermute | solution.py:30
  48.8 11.4 %collective-permute-start.16 = (f32[1,8,512]{2,0,1:T(1,128)S(1)}, f32[1,8,512]{2,0,1:T(1,128)S(1)}, u32[]{:S(2)}, u32[]{:S(2)}) collective-permute-start(f32[1,8,512]{2,0,1:T(1,128)S(1)} %get-tuple-element.86), channel_id=1, source_target_pairs={{0,8},{8,0},{16,24},{24,16},{1,9},{9,1},{17,25},{25,17},{2,10},{10... | collective-permute-start | bytes 49160 | tf_op jit(solution)/shard_map/ppermute | solution.py:29
  54.0 6.3 %collective-permute-start.19 = (f32[16,512]{1,0:T(8,128)S(1)}, f32[16,512]{1,0:T(8,128)S(1)}, u32[]{:S(2)}, u32[]{:S(2)}) collective-permute-start(f32[16,512]{1,0:T(8,128)S(1)} %get-tuple-element.69), channel_id=1, source_target_pairs={{1,2},{2,1},{3,4},{4,3},{5,6},{6,5},{9,10},{10,9},{11,12},{12,11},... | collective-permute-start | bytes 98312 | tf_op jit(solution)/shard_map/ppermute | solution.py:30
  54.6 6.1 %collective-permute-start.18 = (f32[16,512]{1,0:T(8,128)S(1)}, f32[16,512]{1,0:T(8,128)S(1)}, u32[]{:S(2)}, u32[]{:S(2)}) collective-permute-start(f32[16,512]{1,0:T(8,128)S(1)} %get-tuple-element.70), channel_id=1, source_target_pairs={{0,1},{1,0},{2,3},{3,2},{4,5},{5,4},{6,7},{7,6},{8,9},{9,8},{10,11... | collective-permute-start | bytes 98312 | tf_op jit(solution)/shard_map/ppermute | solution.py:29
  64.9 1.7 %collective-permute-start.20 = (f32[8,128]{1,0:T(8,128)}, f32[8,128]{1,0:T(8,128)S(1)}, u32[]{:S(2)}, u32[]{:S(2)}) collective-permute-start(f32[8,128]{1,0:T(8,128)} %shard_map.85), channel_id=1, source_target_pairs={{0,1},{1,0},{2,3},{3,2},{4,5},{5,4},{6,7},{7,6},{8,9},{9,8},{10,11... | collective-permute-start | bytes 12296 | tf_op jit(solution)/shard_map/ppermute | solution.py:71
  67.3 3.6 %collective-permute-start.21 = (f32[8,128]{1,0:T(8,128)S(1)}, f32[8,128]{1,0:T(8,128)S(1)}, u32[]{:S(2)}, u32[]{:S(2)}) collective-permute-start(f32[8,128]{1,0:T(8,128)S(1)} %add.178), channel_id=1, source_target_pairs={{0,2},{1,3},{2,0},{3,1},{4,6},{5,7},{6,4},{7,5},{8,10},{9,11},{10,... | collective-permute-start | bytes 12296 | tf_op jit(solution)/shard_map/ppermute | solution.py:71
  70.9 4.6 %collective-permute-start.22 = (f32[8,128]{1,0:T(8,128)S(1)}, f32[8,128]{1,0:T(8,128)S(1)}, u32[]{:S(2)}, u32[]{:S(2)}) collective-permute-start(f32[8,128]{1,0:T(8,128)S(1)} %add.179), channel_id=1, source_target_pairs={{0,4},{1,5},{2,6},{3,7},{4,0},{5,1},{6,2},{7,3},{8,12},{9,13},{10,... | collective-permute-start | bytes 12296 | tf_op jit(solution)/shard_map/ppermute | solution.py:71
  75.4 3.6 %collective-permute-start.23 = (f32[8,128]{1,0:T(8,128)S(1)}, f32[8,128]{1,0:T(8,128)S(1)}, u32[]{:S(2)}, u32[]{:S(2)}) collective-permute-start(f32[8,128]{1,0:T(8,128)S(1)} %add.180), channel_id=1, source_target_pairs={{0,8},{8,0},{16,24},{24,16},{1,9},{9,1},{17,25},{25,17},{2,10},{10... | collective-permute-start | bytes 12296 | tf_op jit(solution)/shard_map/ppermute | solution.py:71
  79.1 3.6 %collective-permute-start.24 = (f32[8,128]{1,0:T(8,128)S(1)}, f32[8,128]{1,0:T(8,128)S(1)}, u32[]{:S(2)}, u32[]{:S(2)}) collective-permute-start(f32[8,128]{1,0:T(8,128)S(1)} %add.181), channel_id=1, source_target_pairs={{0,16},{8,24},{16,0},{24,8},{1,17},{9,25},{17,1},{25,9},{2,18},{10... | collective-permute-start | bytes 12296 | tf_op jit(solution)/shard_map/ppermute | solution.py:71

commit v14 on v6

--- a/solution.py
+++ b/solution.py
@@ -119,28 +119,35 @@
     def held(i):
         return jnp.full(tile, stats_ref[0, i], jnp.float32)
 
-    scale = jnp.sqrt(held(0) / cells + EPS)
-    square = scale * scale
-    gram = [[held(1 + a * size + b) / cells / square for b in range(size)] for a in range(size)]
+    per_cell = 1.0 / cells
+    scale = jnp.sqrt(held(0) * per_cell + EPS)
+    unscale = 1.0 / scale
+    weight_g = per_cell * (unscale * unscale)
+    gram = [[held(1 + a * size + b) * weight_g for b in range(size)] for a in range(size)]
     upper = [[None] * size for _ in range(size)]
+    recip = [None] * size
     for row in range(size):
         value = gram[row][row]
         for prev in range(row):
             value = value - upper[prev][row] * upper[prev][row]
         pivot = jnp.sqrt(value)
         upper[row][row] = pivot
+        recip[row] = 1.0 / pivot
         for col in range(row + 1, size):
             value = gram[row][col]
             for prev in range(row):
                 value = value - upper[prev][row] * upper[prev][col]
-            upper[row][col] = value / pivot
+            upper[row][col] = value * recip[row]
     inverse = [[None] * size for _ in range(size)]
     for col in range(size):
         for row in reversed(range(col + 1)):
-            value = jnp.full(tile, 1.0 if row == col else 0.0, jnp.float32)
+            if row == col:
+                inverse[row][col] = recip[row]
+                continue
+            value = jnp.zeros(tile, jnp.float32)
             for inner in range(row + 1, col + 1):
                 value = value - upper[row][inner] * inverse[inner][col]
-            inverse[row][col] = value / upper[row][row]
+            inverse[row][col] = value * recip[row]
     rows = lax.broadcasted_iota(jnp.int32, tile, 0)
     cols = lax.broadcasted_iota(jnp.int32, tile, 1)
     packed = jnp.zeros(tile, jnp.float32)
@@ -151,7 +158,7 @@
     scale_ref[...] = scale[:1, :1]
     lanes = basis_refs[0].shape[-1] // tile[1]
     weight = [
-        [jnp.tile(inverse[j][k] / scale, (1, lanes)) if j <= k else None for k in range(size)]
+        [jnp.tile(inverse[j][k] * unscale, (1, lanes)) if j <= k else None for k in range(size)]
         for j in range(size)
     ]
 

time: 79.3 us -> 79.3 us (level)
  no operation moved by 1% of the time
where the time goes in v14:
time: 79.3 us; the launch traced here: 78.7 us
  starting transfers between devices  47.6 us (60%)
  waiting for transfers between devices  14.8 us (19%)
  local copies, waits for them, and re-layouts  5.32 us (7%)
  Pallas kernels  5.06 us (6%)
  other arithmetic  4.77 us (6%)
  between operations  1.2 us (2%)
    ppermute x10, starting transfers between devices, axis_exchange(): lax.ppermute(jnp.where(odd, to_low, to_high), axis, swap_pairs(axis, 0))  35.2 us
    ppermute x5, waiting for transfers between devices, all_sum(): x = x + lax.ppermute(x, axis, [(i, i ^ step) for i in range(n)])  11.4 us
    ppermute x10, starting transfers between devices, axis_exchange(): lax.ppermute(jnp.where(odd, to_high, to_low), axis, swap_pairs(axis, 1))  6.75 us
    ppermute x5, starting transfers between devices, all_sum(): x = x + lax.ppermute(x, axis, [(i, i ^ step) for i in range(n)])  5.63 us
    ppermute x10, waiting for transfers between devices, axis_exchange(): lax.ppermute(jnp.where(odd, to_low, to_high), axis, swap_pairs(axis, 0))  3.35 us
    pallas_call x1, Pallas kernels, finish(): pl.pallas_call(lambda *refs: finish_kernel(float(cells), size, *refs), ou...  2.75 us
    div x4, other arithmetic, local(): vector = 2.0 * total / diagonal  2.52 us
    pallas_call x1, Pallas kernels, gram(): pl.pallas_call(lambda *refs: gram_kernel(size, *refs), out_shape=jax.Shap...  2.31 us
  transfers between devices with their start and end apart: 25, of which 9 were waited for; matrix products, arithmetic and copies ran while one was open for 4% of the time, Pallas kernels for 0%

profile of v14, /device:TPU:0, one launch (start us, length us, event | category | flops | bytes accessed | tf_op | source)
XLA Modules:
  0.0 78.7 jit_solution(16472996989212995064)
XLA Ops:
  0.6 0.0 copy-start.4
  0.7 0.8 %fusion.54 = (f32[1,8,512]{2,1,0:T(8,128)S(1)}, f32[1,8,512]{2,1,0:T(8,128)S(1)}, f32[1,8,512]{2,1,0:T(8,128)S(1)}, f32[1,8,512]{2,1,0:T(8,128)S(1)}) fusion(f32[16,8,512]{2,1,0:T(8,128)} %param.6, f32[16,8,512]{2,1,0:T(8,128)} %param.9), kind=kLoop, calls=%fused_computation.119 | loop fusion | bytes 131072 | tf_op jit(solution)/shard_map/slice | solution.py:199
  1.5 3.0 %collective-permute-start.1 = (f32[2,8,512]{2,1,0:T(8,128)S(1)}, f32[2,8,512]{2,1,0:T(8,128)S(1)}, u32[]{:S(2)}, u32[]{:S(2)}) collective-permute-start(f32[2,8,512]{2,1,0:T(8,128)S(1)} %get-tuple-element.75), channel_id=1, source_target_pairs={{0,8},{8,0},{16,24},{24,16},{1,9},{9,1},{17,25},{25,17},{2,10},{10... | collective-permute-start | bytes 98312 | tf_op jit(solution)/shard_map/ppermute | solution.py:29
  4.5 0.7 collective-permute-start
  5.2 1.3 %fusion.51 = (f32[16,1,512]{2,1,0:T(1,128)S(1)}, f32[16,1,512]{2,1,0:T(1,128)S(1)}, f32[16,1,512]{2,1,0:T(1,128)S(1)}, f32[16,1,512]{2,1,0:T(1,128)S(1)}) fusion(f32[16,8,512]{2,1,0:T(8,128)} %param.6, f32[16,8,512]{2,1,0:T(8,128)} %param.10), kind=kLoop, calls=%fused_computation.116 | loop fusion | bytes 262144 | tf_op jit(solution)/shard_map/slice | solution.py:201
  6.5 0.1 broadcast_select_fusion.18
  6.6 0.1 collective-permute-start.3
  6.7 0.8 %collective-permute-start.2 = (f32[16,2,512]{2,1,0:T(2,128)S(1)}, f32[16,2,512]{2,1,0:T(2,128)S(1)}, u32[]{:S(2)}, u32[]{:S(2)}) collective-permute-start(f32[16,2,512]{2,1,0:T(2,128)S(1)} %get-tuple-element.64), channel_id=1, source_target_pairs={{1,2},{2,1},{3,4},{4,3},{5,6},{6,5},{9,10},{10,9},{11,12},{12,11},... | collective-permute-start | bytes 196616 | tf_op jit(solution)/shard_map/ppermute | solution.py:30
  7.5 1.1 %fusion.50 = (f32[16,7,512]{2,1,0:T(8,128)S(1)}, f32[16,7,512]{2,1,0:T(8,128)S(1)}) fusion(f32[16,8,512]{2,1,0:T(8,128)} %param.6), kind=kLoop, calls=%fused_computation.115 | loop fusion | bytes 917504 | tf_op jit(solution)/shard_map/slice | solution.py:49
  8.6 0.0 copy-start.5
  8.6 0.0 copy-start.7
  8.6 0.1 fusion.49
  8.7 0.1 fusion.53
  8.9 0.7 copy-done.5
  9.6 0.1 copy-done.7
  9.6 0.1 slice.201
  9.8 0.1 fusion.56
  10.0 0.5 fusion.6.refs_0_.refs_1_
  10.5 0.1 fusion.48
  10.6 0.1 fusion.46
  10.7 0.1 fusion.47
  10.8 0.7 collective-permute-start.5
  11.4 5.7 %collective-permute-start.4 = (f32[1,8,512]{2,1,0:T(8,128)S(1)}, f32[1,8,512]{2,1,0:T(8,128)S(1)}, u32[]{:S(2)}, u32[]{:S(2)}) collective-permute-start(f32[1,8,512]{2,1,0:T(8,128)S(1)} %get-tuple-element.48), channel_id=1, source_target_pairs={{0,8},{8,0},{16,24},{24,16},{1,9},{9,1},{17,25},{25,17},{2,10},{10... | collective-permute-start | bytes 49160 | tf_op jit(solution)/shard_map/ppermute | solution.py:29
  17.2 0.7 collective-permute-start.7
  17.9 5.9 %collective-permute-start.6 = (f32[16,1,512]{2,1,0:T(1,128)S(1)}, f32[16,1,512]{2,1,0:T(1,128)S(1)}, u32[]{:S(2)}, u32[]{:S(2)}) collective-permute-start(f32[16,1,512]{2,1,0:T(1,128)S(1)} %get-tuple-element.44), channel_id=1, source_target_pairs={{0,1},{1,0},{2,3},{3,2},{4,5},{5,4},{6,7},{7,6},{8,9},{9,8},{10,11... | collective-permute-start | bytes 98312 | tf_op jit(solution)/shard_map/ppermute | solution.py:29
  23.8 0.8 %collective-permute-done.6 = f32[16,1,512]{2,1,0:T(1,128)S(1)} collective-permute-done((f32[16,1,512]{2,1,0:T(1,128)S(1)}, f32[16,1,512]{2,1,0:T(1,128)S(1)}, u32[]{:S(2)}, u32[]{:S(2)}) %collective-permute-start.6) | collective-permute-done | bytes 32800 | tf_op jit(solution)/shard_map/ppermute | solution.py:29
  24.6 0.5 fusion.13.refs_1_.refs_2_
  25.1 0.1 fusion.43
  25.3 0.1 fusion.44
  25.4 0.7 collective-permute-start.9
  26.0 3.8 %collective-permute-start.8 = (f32[1,8,512]{2,1,0:T(8,128)S(1)}, f32[1,8,512]{2,1,0:T(8,128)S(1)}, u32[]{:S(2)}, u32[]{:S(2)}) collective-permute-start(f32[1,8,512]{2,1,0:T(8,128)S(1)} %get-tuple-element.38), channel_id=1, source_target_pairs={{0,8},{8,0},{16,24},{24,16},{1,9},{9,1},{17,25},{25,17},{2,10},{10... | collective-permute-start | bytes 49160 | tf_op jit(solution)/shard_map/ppermute | solution.py:29
  29.9 0.7 collective-permute-start.11
  30.5 3.7 %collective-permute-start.10 = (f32[16,1,512]{2,1,0:T(1,128)S(1)}, f32[16,1,512]{2,1,0:T(1,128)S(1)}, u32[]{:S(2)}, u32[]{:S(2)}) collective-permute-start(f32[16,1,512]{2,1,0:T(1,128)S(1)} %get-tuple-element.34), channel_id=1, source_target_pairs={{0,1},{1,0},{2,3},{3,2},{4,5},{5,4},{6,7},{7,6},{8,9},{9,8},{10,11... | collective-permute-start | bytes 98312 | tf_op jit(solution)/shard_map/ppermute | solution.py:29
  34.3 0.8 %collective-permute-done.10 = f32[16,1,512]{2,1,0:T(1,128)S(1)} collective-permute-done((f32[16,1,512]{2,1,0:T(1,128)S(1)}, f32[16,1,512]{2,1,0:T(1,128)S(1)}, u32[]{:S(2)}, u32[]{:S(2)}) %collective-permute-start.10) | collective-permute-done | bytes 32800 | tf_op jit(solution)/shard_map/ppermute | solution.py:29
  35.1 0.5 fusion.20.refs_2_.refs_3_
  35.6 0.1 fusion.40
  35.8 0.1 fusion.41
  35.9 0.7 collective-permute-start.13
  36.5 2.1 %collective-permute-start.12 = (f32[1,8,512]{2,1,0:T(8,128)S(1)}, f32[1,8,512]{2,1,0:T(8,128)S(1)}, u32[]{:S(2)}, u32[]{:S(2)}) collective-permute-start(f32[1,8,512]{2,1,0:T(8,128)S(1)} %get-tuple-element.28), channel_id=1, source_target_pairs={{0,8},{8,0},{16,24},{24,16},{1,9},{9,1},{17,25},{25,17},{2,10},{10... | collective-permute-start | bytes 49160 | tf_op jit(solution)/shard_map/ppermute | solution.py:29
  38.7 0.7 collective-permute-start.15
  39.3 3.7 %collective-permute-start.14 = (f32[16,1,512]{2,1,0:T(1,128)S(1)}, f32[16,1,512]{2,1,0:T(1,128)S(1)}, u32[]{:S(2)}, u32[]{:S(2)}) collective-permute-start(f32[16,1,512]{2,1,0:T(1,128)S(1)} %get-tuple-element.24), channel_id=1, source_target_pairs={{0,1},{1,0},{2,3},{3,2},{4,5},{5,4},{6,7},{7,6},{8,9},{9,8},{10,11... | collective-permute-start | bytes 98312 | tf_op jit(solution)/shard_map/ppermute | solution.py:29
  43.1 0.8 %collective-permute-done.14 = f32[16,1,512]{2,1,0:T(1,128)S(1)} collective-permute-done((f32[16,1,512]{2,1,0:T(1,128)S(1)}, f32[16,1,512]{2,1,0:T(1,128)S(1)}, u32[]{:S(2)}, u32[]{:S(2)}) %collective-permute-start.14) | collective-permute-done | bytes 32800 | tf_op jit(solution)/shard_map/ppermute | solution.py:29
  43.9 0.5 fusion.27.refs_3_.refs_4_
  44.4 0.1 fusion.37
  44.6 0.1 fusion.38
  44.6 0.7 collective-permute-start.17
  45.3 3.6 %collective-permute-start.16 = (f32[1,8,512]{2,1,0:T(8,128)S(1)}, f32[1,8,512]{2,1,0:T(8,128)S(1)}, u32[]{:S(2)}, u32[]{:S(2)}) collective-permute-start(f32[1,8,512]{2,1,0:T(8,128)S(1)} %get-tuple-element.18), channel_id=1, source_target_pairs={{0,8},{8,0},{16,24},{24,16},{1,9},{9,1},{17,25},{25,17},{2,10},{10... | collective-permute-start | bytes 49160 | tf_op jit(solution)/shard_map/ppermute | solution.py:29
  48.9 0.7 collective-permute-start.19
  49.6 3.7 %collective-permute-start.18 = (f32[16,1,512]{2,1,0:T(1,128)S(1)}, f32[16,1,512]{2,1,0:T(1,128)S(1)}, u32[]{:S(2)}, u32[]{:S(2)}) collective-permute-start(f32[16,1,512]{2,1,0:T(1,128)S(1)} %get-tuple-element.14), channel_id=1, source_target_pairs={{0,1},{1,0},{2,3},{3,2},{4,5},{5,4},{6,7},{7,6},{8,9},{9,8},{10,11... | collective-permute-start | bytes 98312 | tf_op jit(solution)/shard_map/ppermute | solution.py:29
  53.3 0.8 %collective-permute-done.18 = f32[16,1,512]{2,1,0:T(1,128)S(1)} collective-permute-done((f32[16,1,512]{2,1,0:T(1,128)S(1)}, f32[16,1,512]{2,1,0:T(1,128)S(1)}, u32[]{:S(2)}, u32[]{:S(2)}) %collective-permute-start.18) | collective-permute-done | bytes 32800 | tf_op jit(solution)/shard_map/ppermute | solution.py:29
  54.1 1.2 %fusion.34.refs_4_.refs_5_ = f32[16,8,512]{2,1,0:T(8,128)} fusion(f32[16,8,512]{2,1,0:T(8,128)S(1)} %copy-done.6, f32[15,8,512]{2,1,0:T(8,128)S(1)} %get-tuple-element.16, f32[1,8,512]{2,1,0:T(8,128)S(1)} %get-tuple-element.78, f32[1,8,512]{2,1,0:T(8,128)S(1)} %get-tuple-element.77, f32[15,8,512]{2,1,0:T(8,128)S(1)} %get-tuple-element.15, ...), kind=kLoop, calls=%fused_computation.53 | loop fusion | flops 1638400 | bytes 3668480 | tf_op jit(solution)/shard_map/div | solution.py:223
  55.3 2.3 %shard_map.85 = f32[8,128]{1,0:T(8,128)} custom-call(f32[16,8,512]{2,1,0:T(8,128)} %copy-done.3, f32[16,8,512]{2,1,0:T(8,128)} %copy-done, f32[16,8,512]{2,1,0:T(8,128)} %copy-done.1, f32[16,8,512]{2,1,0:T(8,128)} %copy-done.2, f32[16,8,512]{2,1,0:T(8,128)} %fusion.34.refs_4_.refs_5_), custom_call_target="tpu_custom_call" | custom-call | tf_op jit(solution)/shard_map/pallas_call | solution.py:107
  57.6 0.7 collective-permute-start.20
  58.3 1.0 %collective-permute-done.20 = f32[8,128]{1,0:T(8,128)S(1)} collective-permute-done((f32[8,128]{1,0:T(8,128)}, f32[8,128]{1,0:T(8,128)S(1)}, u32[]{:S(2)}, u32[]{:S(2)}) %collective-permute-start.20) | collective-permute-done | bytes 4128 | tf_op jit(solution)/shard_map/ppermute | solution.py:70
  59.3 0.7 add.178
  60.0 2.0 %collective-permute-start.21 = (f32[8,128]{1,0:T(8,128)S(1)}, f32[8,128]{1,0:T(8,128)S(1)}, u32[]{:S(2)}, u32[]{:S(2)}) collective-permute-start(f32[8,128]{1,0:T(8,128)S(1)} %add.178), channel_id=1, source_target_pairs={{0,2},{1,3},{2,0},{3,1},{4,6},{5,7},{6,4},{7,5},{8,10},{9,11},{10,... | collective-permute-start | bytes 12296 | tf_op jit(solution)/shard_map/ppermute | solution.py:70
  62.0 1.6 %collective-permute-done.21 = f32[8,128]{1,0:T(8,128)S(1)} collective-permute-done((f32[8,128]{1,0:T(8,128)S(1)}, f32[8,128]{1,0:T(8,128)S(1)}, u32[]{:S(2)}, u32[]{:S(2)}) %collective-permute-start.21) | collective-permute-done | bytes 4128 | tf_op jit(solution)/shard_map/ppermute | solution.py:70
  63.6 3.0 %collective-permute-start.22 = (f32[8,128]{1,0:T(8,128)S(1)}, f32[8,128]{1,0:T(8,128)S(1)}, u32[]{:S(2)}, u32[]{:S(2)}) collective-permute-start(f32[8,128]{1,0:T(8,128)S(1)} %add.179), channel_id=1, source_target_pairs={{0,4},{1,5},{2,6},{3,7},{4,0},{5,1},{6,2},{7,3},{8,12},{9,13},{10,... | collective-permute-start | bytes 12296 | tf_op jit(solution)/shard_map/ppermute | solution.py:70
  66.6 1.6 %collective-permute-done.22 = f32[8,128]{1,0:T(8,128)S(1)} collective-permute-done((f32[8,128]{1,0:T(8,128)S(1)}, f32[8,128]{1,0:T(8,128)S(1)}, u32[]{:S(2)}, u32[]{:S(2)}) %collective-permute-start.22) | collective-permute-done | bytes 4128 | tf_op jit(solution)/shard_map/ppermute | solution.py:70
  68.2 0.0 collective-permute-start.23
  68.2 3.6 %collective-permute-done.23 = f32[8,128]{1,0:T(8,128)S(1)} collective-permute-done((f32[8,128]{1,0:T(8,128)S(1)}, f32[8,128]{1,0:T(8,128)S(1)}, u32[]{:S(2)}, u32[]{:S(2)}) %collective-permute-start.23) | collective-permute-done | bytes 4128 | tf_op jit(solution)/shard_map/ppermute | solution.py:70
  71.8 3.6 %collective-permute-done.24 = f32[8,128]{1,0:T(8,128)S(1)} collective-permute-done((f32[8,128]{1,0:T(8,128)S(1)}, f32[8,128]{1,0:T(8,128)S(1)}, u32[]{:S(2)}, u32[]{:S(2)}) %collective-permute-start.24) | collective-permute-done | bytes 4128 | tf_op jit(solution)/shard_map/ppermute | solution.py:70
  75.4 0.6 add.182.refs_0_
  76.0 2.8 %shard_map.86 = (f32[5,16,8,512]{3,2,1,0:T(8,128)}, f32[5,5]{1,0:T(8,128)}, f32[1,1]{1,0:T(1,128)}) custom-call(f32[8,128]{1,0:T(8,128)} %add.182.refs_0_, f32[16,8,512]{2,1,0:T(8,128)} %copy-done.3, f32[16,8,512]{2,1,0:T(8,128)} %copy-done, f32[16,8,512]{2,1,0:T(8,128)} %copy-done.1, f32[16,8,512]{2,1,0:T(8,128)} %copy-done.2, ...), custom_call_target="tpu_custom_call" | custom-call | tf_op jit(solution)/shard_map/pallas_call | solution.py:180
  (62 shorter events, 0.6 us)
Async XLA Ops:
  0.6 7.9 %copy-start.4 = (f32[16,8,512]{2,1,0:T(8,128)S(1)}, f32[16,8,512]{2,1,0:T(8,128)}, u32[]{:S(2)}) copy-start(f32[16,8,512]{2,1,0:T(8,128)} %param.6) | copy-start | bytes 786436
  1.5 8.3 %collective-permute-start.1 = (f32[2,8,512]{2,1,0:T(8,128)S(1)}, f32[2,8,512]{2,1,0:T(8,128)S(1)}, u32[]{:S(2)}, u32[]{:S(2)}) collective-permute-start(f32[2,8,512]{2,1,0:T(8,128)S(1)} %get-tuple-element.75), channel_id=1, source_target_pairs={{0,8},{8,0},{16,24},{24,16},{1,9},{9,1},{17,25},{25,17},{2,10},{10... | collective-permute-start | bytes 98312 | tf_op jit(solution)/shard_map/ppermute | solution.py:29
  4.5 5.3 %collective-permute-start = (f32[2,8,512]{2,1,0:T(8,128)S(1)}, f32[2,8,512]{2,1,0:T(8,128)S(1)}, u32[]{:S(2)}, u32[]{:S(2)}) collective-permute-start(f32[2,8,512]{2,1,0:T(8,128)S(1)} %get-tuple-element.76), channel_id=1, source_target_pairs={{8,16},{16,8},{9,17},{17,9},{10,18},{18,10},{11,19},{19,11},{12,20... | collective-permute-start | bytes 98312 | tf_op jit(solution)/shard_map/ppermute | solution.py:30
  6.6 3.2 %collective-permute-start.3 = (f32[16,2,512]{2,1,0:T(2,128)S(1)}, f32[16,2,512]{2,1,0:T(2,128)S(1)}, u32[]{:S(2)}, u32[]{:S(2)}) collective-permute-start(f32[16,2,512]{2,1,0:T(2,128)S(1)} %get-tuple-element.63), channel_id=1, source_target_pairs={{0,1},{1,0},{2,3},{3,2},{4,5},{5,4},{6,7},{7,6},{8,9},{9,8},{10,11... | collective-permute-start | bytes 196616 | tf_op jit(solution)/shard_map/ppermute | solution.py:29
  6.7 2.1 %copy-start.6 = (f32[16,8,512]{2,1,0:T(8,128)S(1)}, f32[16,8,512]{2,1,0:T(8,128)}, u32[]{:S(2)}) copy-start(f32[16,8,512]{2,1,0:T(8,128)} %param.9) | copy-start | bytes 786436
  6.7 3.1 %collective-permute-start.2 = (f32[16,2,512]{2,1,0:T(2,128)S(1)}, f32[16,2,512]{2,1,0:T(2,128)S(1)}, u32[]{:S(2)}, u32[]{:S(2)}) collective-permute-start(f32[16,2,512]{2,1,0:T(2,128)S(1)} %get-tuple-element.64), channel_id=1, source_target_pairs={{1,2},{2,1},{3,4},{4,3},{5,6},{6,5},{9,10},{10,9},{11,12},{12,11},... | collective-permute-start | bytes 196616 | tf_op jit(solution)/shard_map/ppermute | solution.py:30
  8.6 1.0 %copy-start.5 = (f32[16,8,512]{2,1,0:T(8,128)S(1)}, f32[16,8,512]{2,1,0:T(8,128)}, u32[]{:S(2)}) copy-start(f32[16,8,512]{2,1,0:T(8,128)} %param.10) | copy-start | bytes 786436
  8.6 1.0 %copy-start.7 = (f32[16,8,512]{2,1,0:T(8,128)S(1)}, f32[16,8,512]{2,1,0:T(8,128)}, u32[]{:S(2)}) copy-start(f32[16,8,512]{2,1,0:T(8,128)} %param.11) | copy-start | bytes 786436
  8.8 1.1 %copy-start.8 = (f32[16,8,512]{2,1,0:T(8,128)S(1)}, f32[16,8,512]{2,1,0:T(8,128)}, u32[]{:S(2)}) copy-start(f32[16,8,512]{2,1,0:T(8,128)} %param.8) | copy-start | bytes 786436
  8.8 1.1 %copy-start.9 = (f32[16,8,512]{2,1,0:T(8,128)S(1)}, f32[16,8,512]{2,1,0:T(8,128)}, u32[]{:S(2)}) copy-start(f32[16,8,512]{2,1,0:T(8,128)} %param.7) | copy-start | bytes 786436
  10.5 6.7 %copy-start.3 = (f32[16,8,512]{2,1,0:T(8,128)}, f32[16,8,512]{2,1,0:T(8,128)S(1)}, u32[]{:S(2)}) copy-start(f32[16,8,512]{2,1,0:T(8,128)S(1)} %fusion.6.refs_0_.refs_1_) | copy-start | bytes 786436
  10.8 13.0 %collective-permute-start.5 = (f32[1,8,512]{2,1,0:T(8,128)S(1)}, f32[1,8,512]{2,1,0:T(8,128)S(1)}, u32[]{:S(2)}, u32[]{:S(2)}) collective-permute-start(f32[1,8,512]{2,1,0:T(8,128)S(1)} %get-tuple-element.47), channel_id=1, source_target_pairs={{8,16},{16,8},{9,17},{17,9},{10,18},{18,10},{11,19},{19,11},{12,20... | collective-permute-start | bytes 49160 | tf_op jit(solution)/shard_map/ppermute | solution.py:30
  11.4 12.3 %collective-permute-start.4 = (f32[1,8,512]{2,1,0:T(8,128)S(1)}, f32[1,8,512]{2,1,0:T(8,128)S(1)}, u32[]{:S(2)}, u32[]{:S(2)}) collective-permute-start(f32[1,8,512]{2,1,0:T(8,128)S(1)} %get-tuple-element.48), channel_id=1, source_target_pairs={{0,8},{8,0},{16,24},{24,16},{1,9},{9,1},{17,25},{25,17},{2,10},{10... | collective-permute-start | bytes 49160 | tf_op jit(solution)/shard_map/ppermute | solution.py:29
  17.2 6.6 %collective-permute-start.7 = (f32[16,1,512]{2,1,0:T(1,128)S(1)}, f32[16,1,512]{2,1,0:T(1,128)S(1)}, u32[]{:S(2)}, u32[]{:S(2)}) collective-permute-start(f32[16,1,512]{2,1,0:T(1,128)S(1)} %get-tuple-element.43), channel_id=1, source_target_pairs={{1,2},{2,1},{3,4},{4,3},{5,6},{6,5},{9,10},{10,9},{11,12},{12,11},... | collective-permute-start | bytes 98312 | tf_op jit(solution)/shard_map/ppermute | solution.py:30
  17.9 6.8 %collective-permute-start.6 = (f32[16,1,512]{2,1,0:T(1,128)S(1)}, f32[16,1,512]{2,1,0:T(1,128)S(1)}, u32[]{:S(2)}, u32[]{:S(2)}) collective-permute-start(f32[16,1,512]{2,1,0:T(1,128)S(1)} %get-tuple-element.44), channel_id=1, source_target_pairs={{0,1},{1,0},{2,3},{3,2},{4,5},{5,4},{6,7},{7,6},{8,9},{9,8},{10,11... | collective-permute-start | bytes 98312 | tf_op jit(solution)/shard_map/ppermute | solution.py:29
  25.1 4.7 %copy-start = (f32[16,8,512]{2,1,0:T(8,128)}, f32[16,8,512]{2,1,0:T(8,128)S(1)}, u32[]{:S(2)}) copy-start(f32[16,8,512]{2,1,0:T(8,128)S(1)} %fusion.13.refs_1_.refs_2_) | copy-start | bytes 786436
  25.4 8.9 %collective-permute-start.9 = (f32[1,8,512]{2,1,0:T(8,128)S(1)}, f32[1,8,512]{2,1,0:T(8,128)S(1)}, u32[]{:S(2)}, u32[]{:S(2)}) collective-permute-start(f32[1,8,512]{2,1,0:T(8,128)S(1)} %get-tuple-element.37), channel_id=1, source_target_pairs={{8,16},{16,8},{9,17},{17,9},{10,18},{18,10},{11,19},{19,11},{12,20... | collective-permute-start | bytes 49160 | tf_op jit(solution)/shard_map/ppermute | solution.py:30
  26.0 8.2 %collective-permute-start.8 = (f32[1,8,512]{2,1,0:T(8,128)S(1)}, f32[1,8,512]{2,1,0:T(8,128)S(1)}, u32[]{:S(2)}, u32[]{:S(2)}) collective-permute-start(f32[1,8,512]{2,1,0:T(8,128)S(1)} %get-tuple-element.38), channel_id=1, source_target_pairs={{0,8},{8,0},{16,24},{24,16},{1,9},{9,1},{17,25},{25,17},{2,10},{10... | collective-permute-start | bytes 49160 | tf_op jit(solution)/shard_map/ppermute | solution.py:29
  29.9 4.4 %collective-permute-start.11 = (f32[16,1,512]{2,1,0:T(1,128)S(1)}, f32[16,1,512]{2,1,0:T(1,128)S(1)}, u32[]{:S(2)}, u32[]{:S(2)}) collective-permute-start(f32[16,1,512]{2,1,0:T(1,128)S(1)} %get-tuple-element.33), channel_id=1, source_target_pairs={{1,2},{2,1},{3,4},{4,3},{5,6},{6,5},{9,10},{10,9},{11,12},{12,11},... | collective-permute-start | bytes 98312 | tf_op jit(solution)/shard_map/ppermute | solution.py:30
  30.5 4.6 %collective-permute-start.10 = (f32[16,1,512]{2,1,0:T(1,128)S(1)}, f32[16,1,512]{2,1,0:T(1,128)S(1)}, u32[]{:S(2)}, u32[]{:S(2)}) collective-permute-start(f32[16,1,512]{2,1,0:T(1,128)S(1)} %get-tuple-element.34), channel_id=1, source_target_pairs={{0,1},{1,0},{2,3},{3,2},{4,5},{5,4},{6,7},{7,6},{8,9},{9,8},{10,11... | collective-permute-start | bytes 98312 | tf_op jit(solution)/shard_map/ppermute | solution.py:29
  35.6 3.1 %copy-start.1 = (f32[16,8,512]{2,1,0:T(8,128)}, f32[16,8,512]{2,1,0:T(8,128)S(1)}, u32[]{:S(2)}) copy-start(f32[16,8,512]{2,1,0:T(8,128)S(1)} %fusion.20.refs_2_.refs_3_) | copy-start | bytes 786436
  35.9 7.2 %collective-permute-start.13 = (f32[1,8,512]{2,1,0:T(8,128)S(1)}, f32[1,8,512]{2,1,0:T(8,128)S(1)}, u32[]{:S(2)}, u32[]{:S(2)}) collective-permute-start(f32[1,8,512]{2,1,0:T(8,128)S(1)} %get-tuple-element.27), channel_id=1, source_target_pairs={{8,16},{16,8},{9,17},{17,9},{10,18},{18,10},{11,19},{19,11},{12,20... | collective-permute-start | bytes 49160 | tf_op jit(solution)/shard_map/ppermute | solution.py:30
  36.5 6.5 %collective-permute-start.12 = (f32[1,8,512]{2,1,0:T(8,128)S(1)}, f32[1,8,512]{2,1,0:T(8,128)S(1)}, u32[]{:S(2)}, u32[]{:S(2)}) collective-permute-start(f32[1,8,512]{2,1,0:T(8,128)S(1)} %get-tuple-element.28), channel_id=1, source_target_pairs={{0,8},{8,0},{16,24},{24,16},{1,9},{9,1},{17,25},{25,17},{2,10},{10... | collective-permute-start | bytes 49160 | tf_op jit(solution)/shard_map/ppermute | solution.py:29
  38.7 4.4 %collective-permute-start.15 = (f32[16,1,512]{2,1,0:T(1,128)S(1)}, f32[16,1,512]{2,1,0:T(1,128)S(1)}, u32[]{:S(2)}, u32[]{:S(2)}) collective-permute-start(f32[16,1,512]{2,1,0:T(1,128)S(1)} %get-tuple-element.23), channel_id=1, source_target_pairs={{1,2},{2,1},{3,4},{4,3},{5,6},{6,5},{9,10},{10,9},{11,12},{12,11},... | collective-permute-start | bytes 98312 | tf_op jit(solution)/shard_map/ppermute | solution.py:30
  39.3 4.5 %collective-permute-start.14 = (f32[16,1,512]{2,1,0:T(1,128)S(1)}, f32[16,1,512]{2,1,0:T(1,128)S(1)}, u32[]{:S(2)}, u32[]{:S(2)}) collective-permute-start(f32[16,1,512]{2,1,0:T(1,128)S(1)} %get-tuple-element.24), channel_id=1, source_target_pairs={{0,1},{1,0},{2,3},{3,2},{4,5},{5,4},{6,7},{7,6},{8,9},{9,8},{10,11... | collective-permute-start | bytes 98312 | tf_op jit(solution)/shard_map/ppermute | solution.py:29
  44.3 4.5 %copy-start.2 = (f32[16,8,512]{2,1,0:T(8,128)}, f32[16,8,512]{2,1,0:T(8,128)S(1)}, u32[]{:S(2)}) copy-start(f32[16,8,512]{2,1,0:T(8,128)S(1)} %fusion.27.refs_3_.refs_4_) | copy-start | bytes 786436
  44.6 8.6 %collective-permute-start.17 = (f32[1,8,512]{2,1,0:T(8,128)S(1)}, f32[1,8,512]{2,1,0:T(8,128)S(1)}, u32[]{:S(2)}, u32[]{:S(2)}) collective-permute-start(f32[1,8,512]{2,1,0:T(8,128)S(1)} %get-tuple-element.17), channel_id=1, source_target_pairs={{8,16},{16,8},{9,17},{17,9},{10,18},{18,10},{11,19},{19,11},{12,20... | collective-permute-start | bytes 49160 | tf_op jit(solution)/shard_map/ppermute | solution.py:30
  45.3 8.0 %collective-permute-start.16 = (f32[1,8,512]{2,1,0:T(8,128)S(1)}, f32[1,8,512]{2,1,0:T(8,128)S(1)}, u32[]{:S(2)}, u32[]{:S(2)}) collective-permute-start(f32[1,8,512]{2,1,0:T(8,128)S(1)} %get-tuple-element.18), channel_id=1, source_target_pairs={{0,8},{8,0},{16,24},{24,16},{1,9},{9,1},{17,25},{25,17},{2,10},{10... | collective-permute-start | bytes 49160 | tf_op jit(solution)/shard_map/ppermute | solution.py:29
  48.9 4.4 %collective-permute-start.19 = (f32[16,1,512]{2,1,0:T(1,128)S(1)}, f32[16,1,512]{2,1,0:T(1,128)S(1)}, u32[]{:S(2)}, u32[]{:S(2)}) collective-permute-start(f32[16,1,512]{2,1,0:T(1,128)S(1)} %get-tuple-element.13), channel_id=1, source_target_pairs={{1,2},{2,1},{3,4},{4,3},{5,6},{6,5},{9,10},{10,9},{11,12},{12,11},... | collective-permute-start | bytes 98312 | tf_op jit(solution)/shard_map/ppermute | solution.py:30
  49.6 4.5 %collective-permute-start.18 = (f32[16,1,512]{2,1,0:T(1,128)S(1)}, f32[16,1,512]{2,1,0:T(1,128)S(1)}, u32[]{:S(2)}, u32[]{:S(2)}) collective-permute-start(f32[16,1,512]{2,1,0:T(1,128)S(1)} %get-tuple-element.14), channel_id=1, source_target_pairs={{0,1},{1,0},{2,3},{3,2},{4,5},{5,4},{6,7},{7,6},{8,9},{9,8},{10,11... | collective-permute-start | bytes 98312 | tf_op jit(solution)/shard_map/ppermute | solution.py:29
  57.6 1.7 %collective-permute-start.20 = (f32[8,128]{1,0:T(8,128)}, f32[8,128]{1,0:T(8,128)S(1)}, u32[]{:S(2)}, u32[]{:S(2)}) collective-permute-start(f32[8,128]{1,0:T(8,128)} %shard_map.85), channel_id=1, source_target_pairs={{0,1},{1,0},{2,3},{3,2},{4,5},{5,4},{6,7},{7,6},{8,9},{9,8},{10,11... | collective-permute-start | bytes 12296 | tf_op jit(solution)/shard_map/ppermute | solution.py:70
  60.0 3.6 %collective-permute-start.21 = (f32[8,128]{1,0:T(8,128)S(1)}, f32[8,128]{1,0:T(8,128)S(1)}, u32[]{:S(2)}, u32[]{:S(2)}) collective-permute-start(f32[8,128]{1,0:T(8,128)S(1)} %add.178), channel_id=1, source_target_pairs={{0,2},{1,3},{2,0},{3,1},{4,6},{5,7},{6,4},{7,5},{8,10},{9,11},{10,... | collective-permute-start | bytes 12296 | tf_op jit(solution)/shard_map/ppermute | solution.py:70
  63.6 4.6 %collective-permute-start.22 = (f32[8,128]{1,0:T(8,128)S(1)}, f32[8,128]{1,0:T(8,128)S(1)}, u32[]{:S(2)}, u32[]{:S(2)}) collective-permute-start(f32[8,128]{1,0:T(8,128)S(1)} %add.179), channel_id=1, source_target_pairs={{0,4},{1,5},{2,6},{3,7},{4,0},{5,1},{6,2},{7,3},{8,12},{9,13},{10,... | collective-permute-start | bytes 12296 | tf_op jit(solution)/shard_map/ppermute | solution.py:70
  68.2 3.6 %collective-permute-start.23 = (f32[8,128]{1,0:T(8,128)S(1)}, f32[8,128]{1,0:T(8,128)S(1)}, u32[]{:S(2)}, u32[]{:S(2)}) collective-permute-start(f32[8,128]{1,0:T(8,128)S(1)} %add.180), channel_id=1, source_target_pairs={{0,8},{8,0},{16,24},{24,16},{1,9},{9,1},{17,25},{25,17},{2,10},{10... | collective-permute-start | bytes 12296 | tf_op jit(solution)/shard_map/ppermute | solution.py:70
  71.8 3.6 %collective-permute-start.24 = (f32[8,128]{1,0:T(8,128)S(1)}, f32[8,128]{1,0:T(8,128)S(1)}, u32[]{:S(2)}, u32[]{:S(2)}) collective-permute-start(f32[8,128]{1,0:T(8,128)S(1)} %add.181), channel_id=1, source_target_pairs={{0,16},{8,24},{16,0},{24,8},{1,17},{9,25},{17,1},{25,9},{2,18},{10... | collective-permute-start | bytes 12296 | tf_op jit(solution)/shard_map/ppermute | solution.py:70

commit v15 on v14

--- a/solution.py
+++ b/solution.py
@@ -176,16 +176,23 @@
 
 def finish(stats, basis, cells):
     size = len(basis)
-    vmem = pl.BlockSpec(memory_space=pltpu.VMEM)
+    planes, rows, lanes = basis[0].shape
+    chunk = 4 if planes % 4 == 0 else planes
+    part = pl.BlockSpec((chunk, rows, lanes), lambda i: (i, 0, 0))
     ortho, upper, scale = pl.pallas_call(
         lambda *refs: finish_kernel(float(cells), size, *refs),
+        grid=(planes // chunk,),
         out_shape=(
             jax.ShapeDtypeStruct((size,) + basis[0].shape, jnp.float32),
             jax.ShapeDtypeStruct((size, size), jnp.float32),
             jax.ShapeDtypeStruct((1, 1), jnp.float32),
         ),
-        in_specs=[pl.BlockSpec(memory_space=pltpu.SMEM)] + [vmem] * size,
-        out_specs=(vmem, vmem, vmem),
+        in_specs=[pl.BlockSpec(memory_space=pltpu.SMEM)] + [part] * size,
+        out_specs=(
+            pl.BlockSpec((size, chunk, rows, lanes), lambda i: (0, i, 0, 0)),
+            pl.BlockSpec((size, size), lambda i: (0, 0)),
+            pl.BlockSpec((1, 1), lambda i: (0, 0)),
+        ),
     )(stats, *basis)
     return ortho, upper, scale.reshape(())
 

time: 79.3 us -> 80.5 us (1.015)
  Pallas kernels: 5.06 us -> 6.13 us
    pallas_call x1, Pallas kernels: 2.75 us -> 3.82 us  [finish(): pl.pallas_call(lambda *refs: finish_kernel(float(cells), size, *refs), gr...]
where the time goes in v15:
time: 80.5 us; the launch traced here: 79.8 us
  starting transfers between devices  47.6 us (59%)
  waiting for transfers between devices  14.8 us (18%)
  Pallas kernels  6.13 us (8%)
  local copies, waits for them, and re-layouts  5.32 us (7%)
  other arithmetic  4.77 us (6%)
  between operations  1.2 us (1%)
    ppermute x10, starting transfers between devices, axis_exchange(): lax.ppermute(jnp.where(odd, to_low, to_high), axis, swap_pairs(axis, 0))  35.2 us
    ppermute x5, waiting for transfers between devices, all_sum(): x = x + lax.ppermute(x, axis, [(i, i ^ step) for i in range(n)])  11.4 us
    ppermute x10, starting transfers between devices, axis_exchange(): lax.ppermute(jnp.where(odd, to_high, to_low), axis, swap_pairs(axis, 1))  6.75 us
    ppermute x5, starting transfers between devices, all_sum(): x = x + lax.ppermute(x, axis, [(i, i ^ step) for i in range(n)])  5.63 us
    pallas_call x1, Pallas kernels, finish(): pl.pallas_call(lambda *refs: finish_kernel(float(cells), size, *refs), gr...  3.82 us
    ppermute x10, waiting for transfers between devices, axis_exchange(): lax.ppermute(jnp.where(odd, to_low, to_high), axis, swap_pairs(axis, 0))  3.35 us
    div x4, other arithmetic, local(): vector = 2.0 * total / diagonal  2.52 us
    pallas_call x1, Pallas kernels, gram(): pl.pallas_call(lambda *refs: gram_kernel(size, *refs), out_shape=jax.Shap...  2.31 us
  transfers between devices with their start and end apart: 25, of which 9 were waited for; matrix products, arithmetic and copies ran while one was open for 4% of the time, Pallas kernels for 0%

profile of v15, /device:TPU:0, one launch (start us, length us, event | category | flops | bytes accessed | tf_op | source)
XLA Modules:
  0.0 79.8 jit_solution(2984533513392513105)
XLA Ops:
  0.7 0.8 %fusion.54 = (f32[1,8,512]{2,1,0:T(8,128)S(1)}, f32[1,8,512]{2,1,0:T(8,128)S(1)}, f32[1,8,512]{2,1,0:T(8,128)S(1)}, f32[1,8,512]{2,1,0:T(8,128)S(1)}) fusion(f32[16,8,512]{2,1,0:T(8,128)} %param.6, f32[16,8,512]{2,1,0:T(8,128)} %param.9), kind=kLoop, calls=%fused_computation.119 | loop fusion | bytes 131072 | tf_op jit(solution)/shard_map/slice | solution.py:206
  1.5 3.0 %collective-permute-start.1 = (f32[2,8,512]{2,1,0:T(8,128)S(1)}, f32[2,8,512]{2,1,0:T(8,128)S(1)}, u32[]{:S(2)}, u32[]{:S(2)}) collective-permute-start(f32[2,8,512]{2,1,0:T(8,128)S(1)} %get-tuple-element.75), channel_id=1, source_target_pairs={{0,8},{8,0},{16,24},{24,16},{1,9},{9,1},{17,25},{25,17},{2,10},{10... | collective-permute-start | bytes 98312 | tf_op jit(solution)/shard_map/ppermute | solution.py:29
  4.5 0.7 collective-permute-start
  5.2 1.3 %fusion.51 = (f32[16,1,512]{2,1,0:T(1,128)S(1)}, f32[16,1,512]{2,1,0:T(1,128)S(1)}, f32[16,1,512]{2,1,0:T(1,128)S(1)}, f32[16,1,512]{2,1,0:T(1,128)S(1)}) fusion(f32[16,8,512]{2,1,0:T(8,128)} %param.6, f32[16,8,512]{2,1,0:T(8,128)} %param.10), kind=kLoop, calls=%fused_computation.116 | loop fusion | bytes 262144 | tf_op jit(solution)/shard_map/slice | solution.py:208
  6.5 0.1 broadcast_select_fusion.18
  6.6 0.1 collective-permute-start.3
  6.7 0.0 copy-start.6
  6.7 0.8 collective-permute-start.2
  7.5 1.1 %fusion.50 = (f32[16,7,512]{2,1,0:T(8,128)S(1)}, f32[16,7,512]{2,1,0:T(8,128)S(1)}) fusion(f32[16,8,512]{2,1,0:T(8,128)} %param.6), kind=kLoop, calls=%fused_computation.115 | loop fusion | bytes 917504 | tf_op jit(solution)/shard_map/slice | solution.py:49
  8.6 0.0 copy-start.7
  8.6 0.1 fusion.49
  8.7 0.1 fusion.53
  8.8 0.0 copy-start.8
  8.9 0.7 copy-done.5
  9.6 0.1 copy-done.7
  9.6 0.1 slice.201
  9.8 0.1 fusion.56
  10.0 0.5 fusion.6.refs_0_.refs_1_
  10.5 0.1 fusion.48
  10.6 0.1 fusion.46
  10.7 0.1 fusion.47
  10.8 0.7 collective-permute-start.5
  11.4 5.7 %collective-permute-start.4 = (f32[1,8,512]{2,1,0:T(8,128)S(1)}, f32[1,8,512]{2,1,0:T(8,128)S(1)}, u32[]{:S(2)}, u32[]{:S(2)}) collective-permute-start(f32[1,8,512]{2,1,0:T(8,128)S(1)} %get-tuple-element.48), channel_id=1, source_target_pairs={{0,8},{8,0},{16,24},{24,16},{1,9},{9,1},{17,25},{25,17},{2,10},{10... | collective-permute-start | bytes 49160 | tf_op jit(solution)/shard_map/ppermute | solution.py:29
  17.2 0.7 collective-permute-start.7
  17.9 5.9 %collective-permute-start.6 = (f32[16,1,512]{2,1,0:T(1,128)S(1)}, f32[16,1,512]{2,1,0:T(1,128)S(1)}, u32[]{:S(2)}, u32[]{:S(2)}) collective-permute-start(f32[16,1,512]{2,1,0:T(1,128)S(1)} %get-tuple-element.44), channel_id=1, source_target_pairs={{0,1},{1,0},{2,3},{3,2},{4,5},{5,4},{6,7},{7,6},{8,9},{9,8},{10,11... | collective-permute-start | bytes 98312 | tf_op jit(solution)/shard_map/ppermute | solution.py:29
  23.8 0.8 %collective-permute-done.6 = f32[16,1,512]{2,1,0:T(1,128)S(1)} collective-permute-done((f32[16,1,512]{2,1,0:T(1,128)S(1)}, f32[16,1,512]{2,1,0:T(1,128)S(1)}, u32[]{:S(2)}, u32[]{:S(2)}) %collective-permute-start.6) | collective-permute-done | bytes 32800 | tf_op jit(solution)/shard_map/ppermute | solution.py:29
  24.6 0.5 fusion.13.refs_1_.refs_2_
  25.1 0.1 fusion.43
  25.3 0.1 fusion.44
  25.4 0.7 collective-permute-start.9
  26.0 3.8 %collective-permute-start.8 = (f32[1,8,512]{2,1,0:T(8,128)S(1)}, f32[1,8,512]{2,1,0:T(8,128)S(1)}, u32[]{:S(2)}, u32[]{:S(2)}) collective-permute-start(f32[1,8,512]{2,1,0:T(8,128)S(1)} %get-tuple-element.38), channel_id=1, source_target_pairs={{0,8},{8,0},{16,24},{24,16},{1,9},{9,1},{17,25},{25,17},{2,10},{10... | collective-permute-start | bytes 49160 | tf_op jit(solution)/shard_map/ppermute | solution.py:29
  29.9 0.7 collective-permute-start.11
  30.5 3.7 %collective-permute-start.10 = (f32[16,1,512]{2,1,0:T(1,128)S(1)}, f32[16,1,512]{2,1,0:T(1,128)S(1)}, u32[]{:S(2)}, u32[]{:S(2)}) collective-permute-start(f32[16,1,512]{2,1,0:T(1,128)S(1)} %get-tuple-element.34), channel_id=1, source_target_pairs={{0,1},{1,0},{2,3},{3,2},{4,5},{5,4},{6,7},{7,6},{8,9},{9,8},{10,11... | collective-permute-start | bytes 98312 | tf_op jit(solution)/shard_map/ppermute | solution.py:29
  34.3 0.8 %collective-permute-done.10 = f32[16,1,512]{2,1,0:T(1,128)S(1)} collective-permute-done((f32[16,1,512]{2,1,0:T(1,128)S(1)}, f32[16,1,512]{2,1,0:T(1,128)S(1)}, u32[]{:S(2)}, u32[]{:S(2)}) %collective-permute-start.10) | collective-permute-done | bytes 32800 | tf_op jit(solution)/shard_map/ppermute | solution.py:29
  35.1 0.5 fusion.20.refs_2_.refs_3_
  35.6 0.1 fusion.40
  35.8 0.1 fusion.41
  35.9 0.7 collective-permute-start.13
  36.5 2.1 %collective-permute-start.12 = (f32[1,8,512]{2,1,0:T(8,128)S(1)}, f32[1,8,512]{2,1,0:T(8,128)S(1)}, u32[]{:S(2)}, u32[]{:S(2)}) collective-permute-start(f32[1,8,512]{2,1,0:T(8,128)S(1)} %get-tuple-element.28), channel_id=1, source_target_pairs={{0,8},{8,0},{16,24},{24,16},{1,9},{9,1},{17,25},{25,17},{2,10},{10... | collective-permute-start | bytes 49160 | tf_op jit(solution)/shard_map/ppermute | solution.py:29
  38.7 0.7 collective-permute-start.15
  39.3 3.7 %collective-permute-start.14 = (f32[16,1,512]{2,1,0:T(1,128)S(1)}, f32[16,1,512]{2,1,0:T(1,128)S(1)}, u32[]{:S(2)}, u32[]{:S(2)}) collective-permute-start(f32[16,1,512]{2,1,0:T(1,128)S(1)} %get-tuple-element.24), channel_id=1, source_target_pairs={{0,1},{1,0},{2,3},{3,2},{4,5},{5,4},{6,7},{7,6},{8,9},{9,8},{10,11... | collective-permute-start | bytes 98312 | tf_op jit(solution)/shard_map/ppermute | solution.py:29
  43.1 0.8 %collective-permute-done.14 = f32[16,1,512]{2,1,0:T(1,128)S(1)} collective-permute-done((f32[16,1,512]{2,1,0:T(1,128)S(1)}, f32[16,1,512]{2,1,0:T(1,128)S(1)}, u32[]{:S(2)}, u32[]{:S(2)}) %collective-permute-start.14) | collective-permute-done | bytes 32800 | tf_op jit(solution)/shard_map/ppermute | solution.py:29
  43.9 0.5 fusion.27.refs_3_.refs_4_
  44.4 0.1 fusion.37
  44.6 0.1 fusion.38
  44.6 0.7 collective-permute-start.17
  45.3 3.6 %collective-permute-start.16 = (f32[1,8,512]{2,1,0:T(8,128)S(1)}, f32[1,8,512]{2,1,0:T(8,128)S(1)}, u32[]{:S(2)}, u32[]{:S(2)}) collective-permute-start(f32[1,8,512]{2,1,0:T(8,128)S(1)} %get-tuple-element.18), channel_id=1, source_target_pairs={{0,8},{8,0},{16,24},{24,16},{1,9},{9,1},{17,25},{25,17},{2,10},{10... | collective-permute-start | bytes 49160 | tf_op jit(solution)/shard_map/ppermute | solution.py:29
  48.9 0.7 collective-permute-start.19
  49.6 3.7 %collective-permute-start.18 = (f32[16,1,512]{2,1,0:T(1,128)S(1)}, f32[16,1,512]{2,1,0:T(1,128)S(1)}, u32[]{:S(2)}, u32[]{:S(2)}) collective-permute-start(f32[16,1,512]{2,1,0:T(1,128)S(1)} %get-tuple-element.14), channel_id=1, source_target_pairs={{0,1},{1,0},{2,3},{3,2},{4,5},{5,4},{6,7},{7,6},{8,9},{9,8},{10,11... | collective-permute-start | bytes 98312 | tf_op jit(solution)/shard_map/ppermute | solution.py:29
  53.3 0.8 %collective-permute-done.18 = f32[16,1,512]{2,1,0:T(1,128)S(1)} collective-permute-done((f32[16,1,512]{2,1,0:T(1,128)S(1)}, f32[16,1,512]{2,1,0:T(1,128)S(1)}, u32[]{:S(2)}, u32[]{:S(2)}) %collective-permute-start.18) | collective-permute-done | bytes 32800 | tf_op jit(solution)/shard_map/ppermute | solution.py:29
  54.1 1.2 %fusion.34.refs_4_.refs_5_ = f32[16,8,512]{2,1,0:T(8,128)} fusion(f32[16,8,512]{2,1,0:T(8,128)S(1)} %copy-done.6, f32[15,8,512]{2,1,0:T(8,128)S(1)} %get-tuple-element.16, f32[1,8,512]{2,1,0:T(8,128)S(1)} %get-tuple-element.78, f32[1,8,512]{2,1,0:T(8,128)S(1)} %get-tuple-element.77, f32[15,8,512]{2,1,0:T(8,128)S(1)} %get-tuple-element.15, ...), kind=kLoop, calls=%fused_computation.53 | loop fusion | flops 1638400 | bytes 3668480 | tf_op jit(solution)/shard_map/div | solution.py:230
  55.3 2.3 %shard_map.85 = f32[8,128]{1,0:T(8,128)} custom-call(f32[16,8,512]{2,1,0:T(8,128)} %copy-done.3, f32[16,8,512]{2,1,0:T(8,128)} %copy-done, f32[16,8,512]{2,1,0:T(8,128)} %copy-done.1, f32[16,8,512]{2,1,0:T(8,128)} %copy-done.2, f32[16,8,512]{2,1,0:T(8,128)} %fusion.34.refs_4_.refs_5_), custom_call_target="tpu_custom_call" | custom-call | tf_op jit(solution)/shard_map/pallas_call | solution.py:107
  57.6 0.7 collective-permute-start.20
  58.3 1.0 %collective-permute-done.20 = f32[8,128]{1,0:T(8,128)S(1)} collective-permute-done((f32[8,128]{1,0:T(8,128)}, f32[8,128]{1,0:T(8,128)S(1)}, u32[]{:S(2)}, u32[]{:S(2)}) %collective-permute-start.20) | collective-permute-done | bytes 4128 | tf_op jit(solution)/shard_map/ppermute | solution.py:70
  59.3 0.7 add.178
  60.0 2.0 %collective-permute-start.21 = (f32[8,128]{1,0:T(8,128)S(1)}, f32[8,128]{1,0:T(8,128)S(1)}, u32[]{:S(2)}, u32[]{:S(2)}) collective-permute-start(f32[8,128]{1,0:T(8,128)S(1)} %add.178), channel_id=1, source_target_pairs={{0,2},{1,3},{2,0},{3,1},{4,6},{5,7},{6,4},{7,5},{8,10},{9,11},{10,... | collective-permute-start | bytes 12296 | tf_op jit(solution)/shard_map/ppermute | solution.py:70
  62.0 1.6 %collective-permute-done.21 = f32[8,128]{1,0:T(8,128)S(1)} collective-permute-done((f32[8,128]{1,0:T(8,128)S(1)}, f32[8,128]{1,0:T(8,128)S(1)}, u32[]{:S(2)}, u32[]{:S(2)}) %collective-permute-start.21) | collective-permute-done | bytes 4128 | tf_op jit(solution)/shard_map/ppermute | solution.py:70
  63.6 3.0 %collective-permute-start.22 = (f32[8,128]{1,0:T(8,128)S(1)}, f32[8,128]{1,0:T(8,128)S(1)}, u32[]{:S(2)}, u32[]{:S(2)}) collective-permute-start(f32[8,128]{1,0:T(8,128)S(1)} %add.179), channel_id=1, source_target_pairs={{0,4},{1,5},{2,6},{3,7},{4,0},{5,1},{6,2},{7,3},{8,12},{9,13},{10,... | collective-permute-start | bytes 12296 | tf_op jit(solution)/shard_map/ppermute | solution.py:70
  66.6 1.6 %collective-permute-done.22 = f32[8,128]{1,0:T(8,128)S(1)} collective-permute-done((f32[8,128]{1,0:T(8,128)S(1)}, f32[8,128]{1,0:T(8,128)S(1)}, u32[]{:S(2)}, u32[]{:S(2)}) %collective-permute-start.22) | collective-permute-done | bytes 4128 | tf_op jit(solution)/shard_map/ppermute | solution.py:70
  68.2 0.0 collective-permute-start.23
  68.2 3.6 %collective-permute-done.23 = f32[8,128]{1,0:T(8,128)S(1)} collective-permute-done((f32[8,128]{1,0:T(8,128)S(1)}, f32[8,128]{1,0:T(8,128)S(1)}, u32[]{:S(2)}, u32[]{:S(2)}) %collective-permute-start.23) | collective-permute-done | bytes 4128 | tf_op jit(solution)/shard_map/ppermute | solution.py:70
  71.8 3.6 %collective-permute-done.24 = f32[8,128]{1,0:T(8,128)S(1)} collective-permute-done((f32[8,128]{1,0:T(8,128)S(1)}, f32[8,128]{1,0:T(8,128)S(1)}, u32[]{:S(2)}, u32[]{:S(2)}) %collective-permute-start.24) | collective-permute-done | bytes 4128 | tf_op jit(solution)/shard_map/ppermute | solution.py:70
  75.4 0.6 add.182.refs_0_
  76.0 3.8 %shard_map.86 = (f32[5,16,8,512]{3,2,1,0:T(8,128)}, f32[5,5]{1,0:T(8,128)}, f32[1,1]{1,0:T(1,128)}) custom-call(f32[8,128]{1,0:T(8,128)} %add.182.refs_0_, f32[16,8,512]{2,1,0:T(8,128)} %copy-done.3, f32[16,8,512]{2,1,0:T(8,128)} %copy-done, f32[16,8,512]{2,1,0:T(8,128)} %copy-done.1, f32[16,8,512]{2,1,0:T(8,128)} %copy-done.2, ...), custom_call_target="tpu_custom_call" | custom-call | tf_op jit(solution)/shard_map/pallas_call | solution.py:182
  (62 shorter events, 0.6 us)
Async XLA Ops:
  0.6 7.9 %copy-start.4 = (f32[16,8,512]{2,1,0:T(8,128)S(1)}, f32[16,8,512]{2,1,0:T(8,128)}, u32[]{:S(2)}) copy-start(f32[16,8,512]{2,1,0:T(8,128)} %param.6) | copy-start | bytes 786436
  1.5 8.3 %collective-permute-start.1 = (f32[2,8,512]{2,1,0:T(8,128)S(1)}, f32[2,8,512]{2,1,0:T(8,128)S(1)}, u32[]{:S(2)}, u32[]{:S(2)}) collective-permute-start(f32[2,8,512]{2,1,0:T(8,128)S(1)} %get-tuple-element.75), channel_id=1, source_target_pairs={{0,8},{8,0},{16,24},{24,16},{1,9},{9,1},{17,25},{25,17},{2,10},{10... | collective-permute-start | bytes 98312 | tf_op jit(solution)/shard_map/ppermute | solution.py:29
  4.5 5.3 %collective-permute-start = (f32[2,8,512]{2,1,0:T(8,128)S(1)}, f32[2,8,512]{2,1,0:T(8,128)S(1)}, u32[]{:S(2)}, u32[]{:S(2)}) collective-permute-start(f32[2,8,512]{2,1,0:T(8,128)S(1)} %get-tuple-element.76), channel_id=1, source_target_pairs={{8,16},{16,8},{9,17},{17,9},{10,18},{18,10},{11,19},{19,11},{12,20... | collective-permute-start | bytes 98312 | tf_op jit(solution)/shard_map/ppermute | solution.py:30
  6.6 3.2 %collective-permute-start.3 = (f32[16,2,512]{2,1,0:T(2,128)S(1)}, f32[16,2,512]{2,1,0:T(2,128)S(1)}, u32[]{:S(2)}, u32[]{:S(2)}) collective-permute-start(f32[16,2,512]{2,1,0:T(2,128)S(1)} %get-tuple-element.63), channel_id=1, source_target_pairs={{0,1},{1,0},{2,3},{3,2},{4,5},{5,4},{6,7},{7,6},{8,9},{9,8},{10,11... | collective-permute-start | bytes 196616 | tf_op jit(solution)/shard_map/ppermute | solution.py:29
  6.7 2.1 %copy-start.6 = (f32[16,8,512]{2,1,0:T(8,128)S(1)}, f32[16,8,512]{2,1,0:T(8,128)}, u32[]{:S(2)}) copy-start(f32[16,8,512]{2,1,0:T(8,128)} %param.9) | copy-start | bytes 786436
  6.7 3.1 %collective-permute-start.2 = (f32[16,2,512]{2,1,0:T(2,128)S(1)}, f32[16,2,512]{2,1,0:T(2,128)S(1)}, u32[]{:S(2)}, u32[]{:S(2)}) collective-permute-start(f32[16,2,512]{2,1,0:T(2,128)S(1)} %get-tuple-element.64), channel_id=1, source_target_pairs={{1,2},{2,1},{3,4},{4,3},{5,6},{6,5},{9,10},{10,9},{11,12},{12,11},... | collective-permute-start | bytes 196616 | tf_op jit(solution)/shard_map/ppermute | solution.py:30
  8.6 1.0 %copy-start.5 = (f32[16,8,512]{2,1,0:T(8,128)S(1)}, f32[16,8,512]{2,1,0:T(8,128)}, u32[]{:S(2)}) copy-start(f32[16,8,512]{2,1,0:T(8,128)} %param.10) | copy-start | bytes 786436
  8.6 1.0 %copy-start.7 = (f32[16,8,512]{2,1,0:T(8,128)S(1)}, f32[16,8,512]{2,1,0:T(8,128)}, u32[]{:S(2)}) copy-start(f32[16,8,512]{2,1,0:T(8,128)} %param.11) | copy-start | bytes 786436
  8.8 1.1 %copy-start.8 = (f32[16,8,512]{2,1,0:T(8,128)S(1)}, f32[16,8,512]{2,1,0:T(8,128)}, u32[]{:S(2)}) copy-start(f32[16,8,512]{2,1,0:T(8,128)} %param.8) | copy-start | bytes 786436
  8.8 1.1 %copy-start.9 = (f32[16,8,512]{2,1,0:T(8,128)S(1)}, f32[16,8,512]{2,1,0:T(8,128)}, u32[]{:S(2)}) copy-start(f32[16,8,512]{2,1,0:T(8,128)} %param.7) | copy-start | bytes 786436
  10.5 6.7 %copy-start.3 = (f32[16,8,512]{2,1,0:T(8,128)}, f32[16,8,512]{2,1,0:T(8,128)S(1)}, u32[]{:S(2)}) copy-start(f32[16,8,512]{2,1,0:T(8,128)S(1)} %fusion.6.refs_0_.refs_1_) | copy-start | bytes 786436
  10.8 13.0 %collective-permute-start.5 = (f32[1,8,512]{2,1,0:T(8,128)S(1)}, f32[1,8,512]{2,1,0:T(8,128)S(1)}, u32[]{:S(2)}, u32[]{:S(2)}) collective-permute-start(f32[1,8,512]{2,1,0:T(8,128)S(1)} %get-tuple-element.47), channel_id=1, source_target_pairs={{8,16},{16,8},{9,17},{17,9},{10,18},{18,10},{11,19},{19,11},{12,20... | collective-permute-start | bytes 49160 | tf_op jit(solution)/shard_map/ppermute | solution.py:30
  11.4 12.3 %collective-permute-start.4 = (f32[1,8,512]{2,1,0:T(8,128)S(1)}, f32[1,8,512]{2,1,0:T(8,128)S(1)}, u32[]{:S(2)}, u32[]{:S(2)}) collective-permute-start(f32[1,8,512]{2,1,0:T(8,128)S(1)} %get-tuple-element.48), channel_id=1, source_target_pairs={{0,8},{8,0},{16,24},{24,16},{1,9},{9,1},{17,25},{25,17},{2,10},{10... | collective-permute-start | bytes 49160 | tf_op jit(solution)/shard_map/ppermute | solution.py:29
  17.2 6.6 %collective-permute-start.7 = (f32[16,1,512]{2,1,0:T(1,128)S(1)}, f32[16,1,512]{2,1,0:T(1,128)S(1)}, u32[]{:S(2)}, u32[]{:S(2)}) collective-permute-start(f32[16,1,512]{2,1,0:T(1,128)S(1)} %get-tuple-element.43), channel_id=1, source_target_pairs={{1,2},{2,1},{3,4},{4,3},{5,6},{6,5},{9,10},{10,9},{11,12},{12,11},... | collective-permute-start | bytes 98312 | tf_op jit(solution)/shard_map/ppermute | solution.py:30
  17.9 6.8 %collective-permute-start.6 = (f32[16,1,512]{2,1,0:T(1,128)S(1)}, f32[16,1,512]{2,1,0:T(1,128)S(1)}, u32[]{:S(2)}, u32[]{:S(2)}) collective-permute-start(f32[16,1,512]{2,1,0:T(1,128)S(1)} %get-tuple-element.44), channel_id=1, source_target_pairs={{0,1},{1,0},{2,3},{3,2},{4,5},{5,4},{6,7},{7,6},{8,9},{9,8},{10,11... | collective-permute-start | bytes 98312 | tf_op jit(solution)/shard_map/ppermute | solution.py:29
  25.1 4.7 %copy-start = (f32[16,8,512]{2,1,0:T(8,128)}, f32[16,8,512]{2,1,0:T(8,128)S(1)}, u32[]{:S(2)}) copy-start(f32[16,8,512]{2,1,0:T(8,128)S(1)} %fusion.13.refs_1_.refs_2_) | copy-start | bytes 786436
  25.4 8.9 %collective-permute-start.9 = (f32[1,8,512]{2,1,0:T(8,128)S(1)}, f32[1,8,512]{2,1,0:T(8,128)S(1)}, u32[]{:S(2)}, u32[]{:S(2)}) collective-permute-start(f32[1,8,512]{2,1,0:T(8,128)S(1)} %get-tuple-element.37), channel_id=1, source_target_pairs={{8,16},{16,8},{9,17},{17,9},{10,18},{18,10},{11,19},{19,11},{12,20... | collective-permute-start | bytes 49160 | tf_op jit(solution)/shard_map/ppermute | solution.py:30
  26.0 8.2 %collective-permute-start.8 = (f32[1,8,512]{2,1,0:T(8,128)S(1)}, f32[1,8,512]{2,1,0:T(8,128)S(1)}, u32[]{:S(2)}, u32[]{:S(2)}) collective-permute-start(f32[1,8,512]{2,1,0:T(8,128)S(1)} %get-tuple-element.38), channel_id=1, source_target_pairs={{0,8},{8,0},{16,24},{24,16},{1,9},{9,1},{17,25},{25,17},{2,10},{10... | collective-permute-start | bytes 49160 | tf_op jit(solution)/shard_map/ppermute | solution.py:29
  29.9 4.4 %collective-permute-start.11 = (f32[16,1,512]{2,1,0:T(1,128)S(1)}, f32[16,1,512]{2,1,0:T(1,128)S(1)}, u32[]{:S(2)}, u32[]{:S(2)}) collective-permute-start(f32[16,1,512]{2,1,0:T(1,128)S(1)} %get-tuple-element.33), channel_id=1, source_target_pairs={{1,2},{2,1},{3,4},{4,3},{5,6},{6,5},{9,10},{10,9},{11,12},{12,11},... | collective-permute-start | bytes 98312 | tf_op jit(solution)/shard_map/ppermute | solution.py:30
  30.5 4.6 %collective-permute-start.10 = (f32[16,1,512]{2,1,0:T(1,128)S(1)}, f32[16,1,512]{2,1,0:T(1,128)S(1)}, u32[]{:S(2)}, u32[]{:S(2)}) collective-permute-start(f32[16,1,512]{2,1,0:T(1,128)S(1)} %get-tuple-element.34), channel_id=1, source_target_pairs={{0,1},{1,0},{2,3},{3,2},{4,5},{5,4},{6,7},{7,6},{8,9},{9,8},{10,11... | collective-permute-start | bytes 98312 | tf_op jit(solution)/shard_map/ppermute | solution.py:29
  35.6 3.1 %copy-start.1 = (f32[16,8,512]{2,1,0:T(8,128)}, f32[16,8,512]{2,1,0:T(8,128)S(1)}, u32[]{:S(2)}) copy-start(f32[16,8,512]{2,1,0:T(8,128)S(1)} %fusion.20.refs_2_.refs_3_) | copy-start | bytes 786436
  35.9 7.2 %collective-permute-start.13 = (f32[1,8,512]{2,1,0:T(8,128)S(1)}, f32[1,8,512]{2,1,0:T(8,128)S(1)}, u32[]{:S(2)}, u32[]{:S(2)}) collective-permute-start(f32[1,8,512]{2,1,0:T(8,128)S(1)} %get-tuple-element.27), channel_id=1, source_target_pairs={{8,16},{16,8},{9,17},{17,9},{10,18},{18,10},{11,19},{19,11},{12,20... | collective-permute-start | bytes 49160 | tf_op jit(solution)/shard_map/ppermute | solution.py:30
  36.5 6.5 %collective-permute-start.12 = (f32[1,8,512]{2,1,0:T(8,128)S(1)}, f32[1,8,512]{2,1,0:T(8,128)S(1)}, u32[]{:S(2)}, u32[]{:S(2)}) collective-permute-start(f32[1,8,512]{2,1,0:T(8,128)S(1)} %get-tuple-element.28), channel_id=1, source_target_pairs={{0,8},{8,0},{16,24},{24,16},{1,9},{9,1},{17,25},{25,17},{2,10},{10... | collective-permute-start | bytes 49160 | tf_op jit(solution)/shard_map/ppermute | solution.py:29
  38.7 4.4 %collective-permute-start.15 = (f32[16,1,512]{2,1,0:T(1,128)S(1)}, f32[16,1,512]{2,1,0:T(1,128)S(1)}, u32[]{:S(2)}, u32[]{:S(2)}) collective-permute-start(f32[16,1,512]{2,1,0:T(1,128)S(1)} %get-tuple-element.23), channel_id=1, source_target_pairs={{1,2},{2,1},{3,4},{4,3},{5,6},{6,5},{9,10},{10,9},{11,12},{12,11},... | collective-permute-start | bytes 98312 | tf_op jit(solution)/shard_map/ppermute | solution.py:30
  39.3 4.5 %collective-permute-start.14 = (f32[16,1,512]{2,1,0:T(1,128)S(1)}, f32[16,1,512]{2,1,0:T(1,128)S(1)}, u32[]{:S(2)}, u32[]{:S(2)}) collective-permute-start(f32[16,1,512]{2,1,0:T(1,128)S(1)} %get-tuple-element.24), channel_id=1, source_target_pairs={{0,1},{1,0},{2,3},{3,2},{4,5},{5,4},{6,7},{7,6},{8,9},{9,8},{10,11... | collective-permute-start | bytes 98312 | tf_op jit(solution)/shard_map/ppermute | solution.py:29
  44.3 4.5 %copy-start.2 = (f32[16,8,512]{2,1,0:T(8,128)}, f32[16,8,512]{2,1,0:T(8,128)S(1)}, u32[]{:S(2)}) copy-start(f32[16,8,512]{2,1,0:T(8,128)S(1)} %fusion.27.refs_3_.refs_4_) | copy-start | bytes 786436
  44.6 8.6 %collective-permute-start.17 = (f32[1,8,512]{2,1,0:T(8,128)S(1)}, f32[1,8,512]{2,1,0:T(8,128)S(1)}, u32[]{:S(2)}, u32[]{:S(2)}) collective-permute-start(f32[1,8,512]{2,1,0:T(8,128)S(1)} %get-tuple-element.17), channel_id=1, source_target_pairs={{8,16},{16,8},{9,17},{17,9},{10,18},{18,10},{11,19},{19,11},{12,20... | collective-permute-start | bytes 49160 | tf_op jit(solution)/shard_map/ppermute | solution.py:30
  45.3 8.0 %collective-permute-start.16 = (f32[1,8,512]{2,1,0:T(8,128)S(1)}, f32[1,8,512]{2,1,0:T(8,128)S(1)}, u32[]{:S(2)}, u32[]{:S(2)}) collective-permute-start(f32[1,8,512]{2,1,0:T(8,128)S(1)} %get-tuple-element.18), channel_id=1, source_target_pairs={{0,8},{8,0},{16,24},{24,16},{1,9},{9,1},{17,25},{25,17},{2,10},{10... | collective-permute-start | bytes 49160 | tf_op jit(solution)/shard_map/ppermute | solution.py:29
  48.9 4.4 %collective-permute-start.19 = (f32[16,1,512]{2,1,0:T(1,128)S(1)}, f32[16,1,512]{2,1,0:T(1,128)S(1)}, u32[]{:S(2)}, u32[]{:S(2)}) collective-permute-start(f32[16,1,512]{2,1,0:T(1,128)S(1)} %get-tuple-element.13), channel_id=1, source_target_pairs={{1,2},{2,1},{3,4},{4,3},{5,6},{6,5},{9,10},{10,9},{11,12},{12,11},... | collective-permute-start | bytes 98312 | tf_op jit(solution)/shard_map/ppermute | solution.py:30
  49.6 4.5 %collective-permute-start.18 = (f32[16,1,512]{2,1,0:T(1,128)S(1)}, f32[16,1,512]{2,1,0:T(1,128)S(1)}, u32[]{:S(2)}, u32[]{:S(2)}) collective-permute-start(f32[16,1,512]{2,1,0:T(1,128)S(1)} %get-tuple-element.14), channel_id=1, source_target_pairs={{0,1},{1,0},{2,3},{3,2},{4,5},{5,4},{6,7},{7,6},{8,9},{9,8},{10,11... | collective-permute-start | bytes 98312 | tf_op jit(solution)/shard_map/ppermute | solution.py:29
  57.6 1.7 %collective-permute-start.20 = (f32[8,128]{1,0:T(8,128)}, f32[8,128]{1,0:T(8,128)S(1)}, u32[]{:S(2)}, u32[]{:S(2)}) collective-permute-start(f32[8,128]{1,0:T(8,128)} %shard_map.85), channel_id=1, source_target_pairs={{0,1},{1,0},{2,3},{3,2},{4,5},{5,4},{6,7},{7,6},{8,9},{9,8},{10,11... | collective-permute-start | bytes 12296 | tf_op jit(solution)/shard_map/ppermute | solution.py:70
  60.0 3.6 %collective-permute-start.21 = (f32[8,128]{1,0:T(8,128)S(1)}, f32[8,128]{1,0:T(8,128)S(1)}, u32[]{:S(2)}, u32[]{:S(2)}) collective-permute-start(f32[8,128]{1,0:T(8,128)S(1)} %add.178), channel_id=1, source_target_pairs={{0,2},{1,3},{2,0},{3,1},{4,6},{5,7},{6,4},{7,5},{8,10},{9,11},{10,... | collective-permute-start | bytes 12296 | tf_op jit(solution)/shard_map/ppermute | solution.py:70
  63.6 4.6 %collective-permute-start.22 = (f32[8,128]{1,0:T(8,128)S(1)}, f32[8,128]{1,0:T(8,128)S(1)}, u32[]{:S(2)}, u32[]{:S(2)}) collective-permute-start(f32[8,128]{1,0:T(8,128)S(1)} %add.179), channel_id=1, source_target_pairs={{0,4},{1,5},{2,6},{3,7},{4,0},{5,1},{6,2},{7,3},{8,12},{9,13},{10,... | collective-permute-start | bytes 12296 | tf_op jit(solution)/shard_map/ppermute | solution.py:70
  68.2 3.6 %collective-permute-start.23 = (f32[8,128]{1,0:T(8,128)S(1)}, f32[8,128]{1,0:T(8,128)S(1)}, u32[]{:S(2)}, u32[]{:S(2)}) collective-permute-start(f32[8,128]{1,0:T(8,128)S(1)} %add.180), channel_id=1, source_target_pairs={{0,8},{8,0},{16,24},{24,16},{1,9},{9,1},{17,25},{25,17},{2,10},{10... | collective-permute-start | bytes 12296 | tf_op jit(solution)/shard_map/ppermute | solution.py:70
  71.8 3.6 %collective-permute-start.24 = (f32[8,128]{1,0:T(8,128)S(1)}, f32[8,128]{1,0:T(8,128)S(1)}, u32[]{:S(2)}, u32[]{:S(2)}) collective-permute-start(f32[8,128]{1,0:T(8,128)S(1)} %add.181), channel_id=1, source_target_pairs={{0,16},{8,24},{16,0},{24,8},{1,17},{9,25},{17,1},{25,9},{2,18},{10... | collective-permute-start | bytes 12296 | tf_op jit(solution)/shard_map/ppermute | solution.py:70

commit v16 on v14

--- a/solution.py
+++ b/solution.py
@@ -106,7 +106,7 @@
     vmem = pl.BlockSpec(memory_space=pltpu.VMEM)
     return pl.pallas_call(
         lambda *refs: gram_kernel(size, *refs),
-        out_shape=jax.ShapeDtypeStruct((8, 128), jnp.float32),
+        out_shape=jax.ShapeDtypeStruct((1, 128), jnp.float32),
         in_specs=[vmem] * size,
         out_specs=vmem,
     )(*basis)

time: 79.3 us -> 78.7 us (level)
  no operation moved by 1% of the time
where the time goes in v16:
time: 78.7 us; the launch traced here: 78.2 us
  starting transfers between devices  47.5 us (60%)
  waiting for transfers between devices  14.5 us (18%)
  local copies, waits for them, and re-layouts  5.32 us (7%)
  Pallas kernels  4.98 us (6%)
  other arithmetic  4.73 us (6%)
  between operations  1.2 us (2%)
    ppermute x10, starting transfers between devices, axis_exchange(): lax.ppermute(jnp.where(odd, to_low, to_high), axis, swap_pairs(axis, 0))  35.2 us
    ppermute x5, waiting for transfers between devices, all_sum(): x = x + lax.ppermute(x, axis, [(i, i ^ step) for i in range(n)])  11.1 us
    ppermute x10, starting transfers between devices, axis_exchange(): lax.ppermute(jnp.where(odd, to_high, to_low), axis, swap_pairs(axis, 1))  6.75 us
    ppermute x5, starting transfers between devices, all_sum(): x = x + lax.ppermute(x, axis, [(i, i ^ step) for i in range(n)])  5.55 us
    ppermute x10, waiting for transfers between devices, axis_exchange(): lax.ppermute(jnp.where(odd, to_low, to_high), axis, swap_pairs(axis, 0))  3.35 us
    pallas_call x1, Pallas kernels, finish(): pl.pallas_call(lambda *refs: finish_kernel(float(cells), size, *refs), ou...  2.75 us
    div x4, other arithmetic, local(): vector = 2.0 * total / diagonal  2.52 us
    pallas_call x1, Pallas kernels, gram(): pl.pallas_call(lambda *refs: gram_kernel(size, *refs), out_shape=jax.Shap...  2.23 us
  transfers between devices with their start and end apart: 25, of which 9 were waited for; matrix products, arithmetic and copies ran while one was open for 4% of the time, Pallas kernels for 0%

profile of v16, /device:TPU:0, one launch (start us, length us, event | category | flops | bytes accessed | tf_op | source)
XLA Modules:
  0.0 78.2 jit_solution(5244498800728176944)
XLA Ops:
  0.6 0.0 copy-start.4
  0.7 0.8 %fusion.54 = (f32[1,8,512]{2,1,0:T(8,128)S(1)}, f32[1,8,512]{2,1,0:T(8,128)S(1)}, f32[1,8,512]{2,1,0:T(8,128)S(1)}, f32[1,8,512]{2,1,0:T(8,128)S(1)}) fusion(f32[16,8,512]{2,1,0:T(8,128)} %param.6, f32[16,8,512]{2,1,0:T(8,128)} %param.9), kind=kLoop, calls=%fused_computation.119 | loop fusion | bytes 131072 | tf_op jit(solution)/shard_map/slice | solution.py:199
  1.5 3.0 %collective-permute-start.1 = (f32[2,8,512]{2,1,0:T(8,128)S(1)}, f32[2,8,512]{2,1,0:T(8,128)S(1)}, u32[]{:S(2)}, u32[]{:S(2)}) collective-permute-start(f32[2,8,512]{2,1,0:T(8,128)S(1)} %get-tuple-element.75), channel_id=1, source_target_pairs={{0,8},{8,0},{16,24},{24,16},{1,9},{9,1},{17,25},{25,17},{2,10},{10... | collective-permute-start | bytes 98312 | tf_op jit(solution)/shard_map/ppermute | solution.py:29
  4.5 0.7 collective-permute-start
  5.2 1.3 %fusion.51 = (f32[16,1,512]{2,1,0:T(1,128)S(1)}, f32[16,1,512]{2,1,0:T(1,128)S(1)}, f32[16,1,512]{2,1,0:T(1,128)S(1)}, f32[16,1,512]{2,1,0:T(1,128)S(1)}) fusion(f32[16,8,512]{2,1,0:T(8,128)} %param.6, f32[16,8,512]{2,1,0:T(8,128)} %param.10), kind=kLoop, calls=%fused_computation.116 | loop fusion | bytes 262144 | tf_op jit(solution)/shard_map/slice | solution.py:201
  6.5 0.1 broadcast_select_fusion.18
  6.6 0.1 collective-permute-start.3
  6.7 0.8 %collective-permute-start.2 = (f32[16,2,512]{2,1,0:T(2,128)S(1)}, f32[16,2,512]{2,1,0:T(2,128)S(1)}, u32[]{:S(2)}, u32[]{:S(2)}) collective-permute-start(f32[16,2,512]{2,1,0:T(2,128)S(1)} %get-tuple-element.64), channel_id=1, source_target_pairs={{1,2},{2,1},{3,4},{4,3},{5,6},{6,5},{9,10},{10,9},{11,12},{12,11},... | collective-permute-start | bytes 196616 | tf_op jit(solution)/shard_map/ppermute | solution.py:30
  7.5 1.1 %fusion.50 = (f32[16,7,512]{2,1,0:T(8,128)S(1)}, f32[16,7,512]{2,1,0:T(8,128)S(1)}) fusion(f32[16,8,512]{2,1,0:T(8,128)} %param.6), kind=kLoop, calls=%fused_computation.115 | loop fusion | bytes 917504 | tf_op jit(solution)/shard_map/slice | solution.py:49
  8.6 0.0 copy-start.5
  8.6 0.0 copy-start.7
  8.6 0.1 fusion.49
  8.7 0.1 fusion.53
  8.9 0.7 copy-done.5
  9.6 0.1 copy-done.7
  9.6 0.1 slice.201
  9.8 0.1 fusion.56
  10.0 0.5 fusion.6.refs_0_.refs_1_
  10.5 0.1 fusion.48
  10.6 0.1 fusion.46
  10.7 0.1 fusion.47
  10.8 0.7 collective-permute-start.5
  11.4 5.7 %collective-permute-start.4 = (f32[1,8,512]{2,1,0:T(8,128)S(1)}, f32[1,8,512]{2,1,0:T(8,128)S(1)}, u32[]{:S(2)}, u32[]{:S(2)}) collective-permute-start(f32[1,8,512]{2,1,0:T(8,128)S(1)} %get-tuple-element.48), channel_id=1, source_target_pairs={{0,8},{8,0},{16,24},{24,16},{1,9},{9,1},{17,25},{25,17},{2,10},{10... | collective-permute-start | bytes 49160 | tf_op jit(solution)/shard_map/ppermute | solution.py:29
  17.2 0.7 collective-permute-start.7
  17.9 5.9 %collective-permute-start.6 = (f32[16,1,512]{2,1,0:T(1,128)S(1)}, f32[16,1,512]{2,1,0:T(1,128)S(1)}, u32[]{:S(2)}, u32[]{:S(2)}) collective-permute-start(f32[16,1,512]{2,1,0:T(1,128)S(1)} %get-tuple-element.44), channel_id=1, source_target_pairs={{0,1},{1,0},{2,3},{3,2},{4,5},{5,4},{6,7},{7,6},{8,9},{9,8},{10,11... | collective-permute-start | bytes 98312 | tf_op jit(solution)/shard_map/ppermute | solution.py:29
  23.8 0.8 %collective-permute-done.6 = f32[16,1,512]{2,1,0:T(1,128)S(1)} collective-permute-done((f32[16,1,512]{2,1,0:T(1,128)S(1)}, f32[16,1,512]{2,1,0:T(1,128)S(1)}, u32[]{:S(2)}, u32[]{:S(2)}) %collective-permute-start.6) | collective-permute-done | bytes 32800 | tf_op jit(solution)/shard_map/ppermute | solution.py:29
  24.6 0.5 fusion.13.refs_1_.refs_2_
  25.1 0.1 fusion.43
  25.3 0.1 fusion.44
  25.4 0.7 collective-permute-start.9
  26.0 3.8 %collective-permute-start.8 = (f32[1,8,512]{2,1,0:T(8,128)S(1)}, f32[1,8,512]{2,1,0:T(8,128)S(1)}, u32[]{:S(2)}, u32[]{:S(2)}) collective-permute-start(f32[1,8,512]{2,1,0:T(8,128)S(1)} %get-tuple-element.38), channel_id=1, source_target_pairs={{0,8},{8,0},{16,24},{24,16},{1,9},{9,1},{17,25},{25,17},{2,10},{10... | collective-permute-start | bytes 49160 | tf_op jit(solution)/shard_map/ppermute | solution.py:29
  29.9 0.7 collective-permute-start.11
  30.5 3.7 %collective-permute-start.10 = (f32[16,1,512]{2,1,0:T(1,128)S(1)}, f32[16,1,512]{2,1,0:T(1,128)S(1)}, u32[]{:S(2)}, u32[]{:S(2)}) collective-permute-start(f32[16,1,512]{2,1,0:T(1,128)S(1)} %get-tuple-element.34), channel_id=1, source_target_pairs={{0,1},{1,0},{2,3},{3,2},{4,5},{5,4},{6,7},{7,6},{8,9},{9,8},{10,11... | collective-permute-start | bytes 98312 | tf_op jit(solution)/shard_map/ppermute | solution.py:29
  34.3 0.8 %collective-permute-done.10 = f32[16,1,512]{2,1,0:T(1,128)S(1)} collective-permute-done((f32[16,1,512]{2,1,0:T(1,128)S(1)}, f32[16,1,512]{2,1,0:T(1,128)S(1)}, u32[]{:S(2)}, u32[]{:S(2)}) %collective-permute-start.10) | collective-permute-done | bytes 32800 | tf_op jit(solution)/shard_map/ppermute | solution.py:29
  35.1 0.5 fusion.20.refs_2_.refs_3_
  35.6 0.1 fusion.40
  35.8 0.1 fusion.41
  35.9 0.7 collective-permute-start.13
  36.5 2.1 %collective-permute-start.12 = (f32[1,8,512]{2,1,0:T(8,128)S(1)}, f32[1,8,512]{2,1,0:T(8,128)S(1)}, u32[]{:S(2)}, u32[]{:S(2)}) collective-permute-start(f32[1,8,512]{2,1,0:T(8,128)S(1)} %get-tuple-element.28), channel_id=1, source_target_pairs={{0,8},{8,0},{16,24},{24,16},{1,9},{9,1},{17,25},{25,17},{2,10},{10... | collective-permute-start | bytes 49160 | tf_op jit(solution)/shard_map/ppermute | solution.py:29
  38.7 0.7 collective-permute-start.15
  39.3 3.7 %collective-permute-start.14 = (f32[16,1,512]{2,1,0:T(1,128)S(1)}, f32[16,1,512]{2,1,0:T(1,128)S(1)}, u32[]{:S(2)}, u32[]{:S(2)}) collective-permute-start(f32[16,1,512]{2,1,0:T(1,128)S(1)} %get-tuple-element.24), channel_id=1, source_target_pairs={{0,1},{1,0},{2,3},{3,2},{4,5},{5,4},{6,7},{7,6},{8,9},{9,8},{10,11... | collective-permute-start | bytes 98312 | tf_op jit(solution)/shard_map/ppermute | solution.py:29
  43.1 0.8 %collective-permute-done.14 = f32[16,1,512]{2,1,0:T(1,128)S(1)} collective-permute-done((f32[16,1,512]{2,1,0:T(1,128)S(1)}, f32[16,1,512]{2,1,0:T(1,128)S(1)}, u32[]{:S(2)}, u32[]{:S(2)}) %collective-permute-start.14) | collective-permute-done | bytes 32800 | tf_op jit(solution)/shard_map/ppermute | solution.py:29
  43.9 0.5 fusion.27.refs_3_.refs_4_
  44.4 0.1 fusion.37
  44.6 0.1 fusion.38
  44.6 0.7 collective-permute-start.17
  45.3 3.6 %collective-permute-start.16 = (f32[1,8,512]{2,1,0:T(8,128)S(1)}, f32[1,8,512]{2,1,0:T(8,128)S(1)}, u32[]{:S(2)}, u32[]{:S(2)}) collective-permute-start(f32[1,8,512]{2,1,0:T(8,128)S(1)} %get-tuple-element.18), channel_id=1, source_target_pairs={{0,8},{8,0},{16,24},{24,16},{1,9},{9,1},{17,25},{25,17},{2,10},{10... | collective-permute-start | bytes 49160 | tf_op jit(solution)/shard_map/ppermute | solution.py:29
  48.9 0.7 collective-permute-start.19
  49.6 3.7 %collective-permute-start.18 = (f32[16,1,512]{2,1,0:T(1,128)S(1)}, f32[16,1,512]{2,1,0:T(1,128)S(1)}, u32[]{:S(2)}, u32[]{:S(2)}) collective-permute-start(f32[16,1,512]{2,1,0:T(1,128)S(1)} %get-tuple-element.14), channel_id=1, source_target_pairs={{0,1},{1,0},{2,3},{3,2},{4,5},{5,4},{6,7},{7,6},{8,9},{9,8},{10,11... | collective-permute-start | bytes 98312 | tf_op jit(solution)/shard_map/ppermute | solution.py:29
  53.3 0.8 %collective-permute-done.18 = f32[16,1,512]{2,1,0:T(1,128)S(1)} collective-permute-done((f32[16,1,512]{2,1,0:T(1,128)S(1)}, f32[16,1,512]{2,1,0:T(1,128)S(1)}, u32[]{:S(2)}, u32[]{:S(2)}) %collective-permute-start.18) | collective-permute-done | bytes 32800 | tf_op jit(solution)/shard_map/ppermute | solution.py:29
  54.1 1.2 %fusion.34.refs_4_.refs_5_ = f32[16,8,512]{2,1,0:T(8,128)} fusion(f32[16,8,512]{2,1,0:T(8,128)S(1)} %copy-done.6, f32[15,8,512]{2,1,0:T(8,128)S(1)} %get-tuple-element.16, f32[1,8,512]{2,1,0:T(8,128)S(1)} %get-tuple-element.78, f32[1,8,512]{2,1,0:T(8,128)S(1)} %get-tuple-element.77, f32[15,8,512]{2,1,0:T(8,128)S(1)} %get-tuple-element.15, ...), kind=kLoop, calls=%fused_computation.53 | loop fusion | flops 1638400 | bytes 3668480 | tf_op jit(solution)/shard_map/div | solution.py:223
  55.3 2.2 %shard_map.85 = f32[1,128]{1,0:T(1,128)} custom-call(f32[16,8,512]{2,1,0:T(8,128)} %copy-done.3, f32[16,8,512]{2,1,0:T(8,128)} %copy-done, f32[16,8,512]{2,1,0:T(8,128)} %copy-done.1, f32[16,8,512]{2,1,0:T(8,128)} %copy-done.2, f32[16,8,512]{2,1,0:T(8,128)} %fusion.34.refs_4_.refs_5_), custom_call_target="tpu_custom_call" | custom-call | tf_op jit(solution)/shard_map/pallas_call | solution.py:107
  57.5 0.7 collective-permute-start.20
  58.2 1.0 %collective-permute-done.20 = f32[1,128]{1,0:T(1,128)S(1)} collective-permute-done((f32[1,128]{1,0:T(1,128)}, f32[1,128]{1,0:T(1,128)S(1)}, u32[]{:S(2)}, u32[]{:S(2)}) %collective-permute-start.20) | collective-permute-done | bytes 544 | tf_op jit(solution)/shard_map/ppermute | solution.py:70
  59.1 0.7 add.178
  59.8 1.9 %collective-permute-start.21 = (f32[1,128]{1,0:T(1,128)S(1)}, f32[1,128]{1,0:T(1,128)S(1)}, u32[]{:S(2)}, u32[]{:S(2)}) collective-permute-start(f32[1,128]{1,0:T(1,128)S(1)} %add.178), channel_id=1, source_target_pairs={{0,2},{1,3},{2,0},{3,1},{4,6},{5,7},{6,4},{7,5},{8,10},{9,11},{10,... | collective-permute-start | bytes 1544 | tf_op jit(solution)/shard_map/ppermute | solution.py:70
  61.7 1.6 %collective-permute-done.21 = f32[1,128]{1,0:T(1,128)S(1)} collective-permute-done((f32[1,128]{1,0:T(1,128)S(1)}, f32[1,128]{1,0:T(1,128)S(1)}, u32[]{:S(2)}, u32[]{:S(2)}) %collective-permute-start.21) | collective-permute-done | bytes 544 | tf_op jit(solution)/shard_map/ppermute | solution.py:70
  63.4 2.9 %collective-permute-start.22 = (f32[1,128]{1,0:T(1,128)S(1)}, f32[1,128]{1,0:T(1,128)S(1)}, u32[]{:S(2)}, u32[]{:S(2)}) collective-permute-start(f32[1,128]{1,0:T(1,128)S(1)} %add.179), channel_id=1, source_target_pairs={{0,4},{1,5},{2,6},{3,7},{4,0},{5,1},{6,2},{7,3},{8,12},{9,13},{10,... | collective-permute-start | bytes 1544 | tf_op jit(solution)/shard_map/ppermute | solution.py:70
  66.3 1.5 %collective-permute-done.22 = f32[1,128]{1,0:T(1,128)S(1)} collective-permute-done((f32[1,128]{1,0:T(1,128)S(1)}, f32[1,128]{1,0:T(1,128)S(1)}, u32[]{:S(2)}, u32[]{:S(2)}) %collective-permute-start.22) | collective-permute-done | bytes 544 | tf_op jit(solution)/shard_map/ppermute | solution.py:70
  67.8 0.0 collective-permute-start.23
  67.8 3.5 %collective-permute-done.23 = f32[1,128]{1,0:T(1,128)S(1)} collective-permute-done((f32[1,128]{1,0:T(1,128)S(1)}, f32[1,128]{1,0:T(1,128)S(1)}, u32[]{:S(2)}, u32[]{:S(2)}) %collective-permute-start.23) | collective-permute-done | bytes 544 | tf_op jit(solution)/shard_map/ppermute | solution.py:70
  71.4 3.5 %collective-permute-done.24 = f32[1,128]{1,0:T(1,128)S(1)} collective-permute-done((f32[1,128]{1,0:T(1,128)S(1)}, f32[1,128]{1,0:T(1,128)S(1)}, u32[]{:S(2)}, u32[]{:S(2)}) %collective-permute-start.24) | collective-permute-done | bytes 544 | tf_op jit(solution)/shard_map/ppermute | solution.py:70
  74.9 0.6 add.182.refs_0_
  75.5 2.8 %shard_map.86 = (f32[5,16,8,512]{3,2,1,0:T(8,128)}, f32[5,5]{1,0:T(8,128)}, f32[1,1]{1,0:T(1,128)}) custom-call(f32[1,128]{1,0:T(1,128)} %add.182.refs_0_, f32[16,8,512]{2,1,0:T(8,128)} %copy-done.3, f32[16,8,512]{2,1,0:T(8,128)} %copy-done, f32[16,8,512]{2,1,0:T(8,128)} %copy-done.1, f32[16,8,512]{2,1,0:T(8,128)} %copy-done.2, ...), custom_call_target="tpu_custom_call" | custom-call | tf_op jit(solution)/shard_map/pallas_call | solution.py:180
  (62 shorter events, 0.6 us)
Async XLA Ops:
  0.6 7.9 %copy-start.4 = (f32[16,8,512]{2,1,0:T(8,128)S(1)}, f32[16,8,512]{2,1,0:T(8,128)}, u32[]{:S(2)}) copy-start(f32[16,8,512]{2,1,0:T(8,128)} %param.6) | copy-start | bytes 786436
  1.5 8.3 %collective-permute-start.1 = (f32[2,8,512]{2,1,0:T(8,128)S(1)}, f32[2,8,512]{2,1,0:T(8,128)S(1)}, u32[]{:S(2)}, u32[]{:S(2)}) collective-permute-start(f32[2,8,512]{2,1,0:T(8,128)S(1)} %get-tuple-element.75), channel_id=1, source_target_pairs={{0,8},{8,0},{16,24},{24,16},{1,9},{9,1},{17,25},{25,17},{2,10},{10... | collective-permute-start | bytes 98312 | tf_op jit(solution)/shard_map/ppermute | solution.py:29
  4.5 5.3 %collective-permute-start = (f32[2,8,512]{2,1,0:T(8,128)S(1)}, f32[2,8,512]{2,1,0:T(8,128)S(1)}, u32[]{:S(2)}, u32[]{:S(2)}) collective-permute-start(f32[2,8,512]{2,1,0:T(8,128)S(1)} %get-tuple-element.76), channel_id=1, source_target_pairs={{8,16},{16,8},{9,17},{17,9},{10,18},{18,10},{11,19},{19,11},{12,20... | collective-permute-start | bytes 98312 | tf_op jit(solution)/shard_map/ppermute | solution.py:30
  6.6 3.2 %collective-permute-start.3 = (f32[16,2,512]{2,1,0:T(2,128)S(1)}, f32[16,2,512]{2,1,0:T(2,128)S(1)}, u32[]{:S(2)}, u32[]{:S(2)}) collective-permute-start(f32[16,2,512]{2,1,0:T(2,128)S(1)} %get-tuple-element.63), channel_id=1, source_target_pairs={{0,1},{1,0},{2,3},{3,2},{4,5},{5,4},{6,7},{7,6},{8,9},{9,8},{10,11... | collective-permute-start | bytes 196616 | tf_op jit(solution)/shard_map/ppermute | solution.py:29
  6.7 2.1 %copy-start.6 = (f32[16,8,512]{2,1,0:T(8,128)S(1)}, f32[16,8,512]{2,1,0:T(8,128)}, u32[]{:S(2)}) copy-start(f32[16,8,512]{2,1,0:T(8,128)} %param.9) | copy-start | bytes 786436
  6.7 3.1 %collective-permute-start.2 = (f32[16,2,512]{2,1,0:T(2,128)S(1)}, f32[16,2,512]{2,1,0:T(2,128)S(1)}, u32[]{:S(2)}, u32[]{:S(2)}) collective-permute-start(f32[16,2,512]{2,1,0:T(2,128)S(1)} %get-tuple-element.64), channel_id=1, source_target_pairs={{1,2},{2,1},{3,4},{4,3},{5,6},{6,5},{9,10},{10,9},{11,12},{12,11},... | collective-permute-start | bytes 196616 | tf_op jit(solution)/shard_map/ppermute | solution.py:30
  8.6 1.0 %copy-start.5 = (f32[16,8,512]{2,1,0:T(8,128)S(1)}, f32[16,8,512]{2,1,0:T(8,128)}, u32[]{:S(2)}) copy-start(f32[16,8,512]{2,1,0:T(8,128)} %param.10) | copy-start | bytes 786436
  8.6 1.0 %copy-start.7 = (f32[16,8,512]{2,1,0:T(8,128)S(1)}, f32[16,8,512]{2,1,0:T(8,128)}, u32[]{:S(2)}) copy-start(f32[16,8,512]{2,1,0:T(8,128)} %param.11) | copy-start | bytes 786436
  8.8 1.1 %copy-start.8 = (f32[16,8,512]{2,1,0:T(8,128)S(1)}, f32[16,8,512]{2,1,0:T(8,128)}, u32[]{:S(2)}) copy-start(f32[16,8,512]{2,1,0:T(8,128)} %param.8) | copy-start | bytes 786436
  8.8 1.1 %copy-start.9 = (f32[16,8,512]{2,1,0:T(8,128)S(1)}, f32[16,8,512]{2,1,0:T(8,128)}, u32[]{:S(2)}) copy-start(f32[16,8,512]{2,1,0:T(8,128)} %param.7) | copy-start | bytes 786436
  10.5 6.7 %copy-start.3 = (f32[16,8,512]{2,1,0:T(8,128)}, f32[16,8,512]{2,1,0:T(8,128)S(1)}, u32[]{:S(2)}) copy-start(f32[16,8,512]{2,1,0:T(8,128)S(1)} %fusion.6.refs_0_.refs_1_) | copy-start | bytes 786436
  10.8 13.0 %collective-permute-start.5 = (f32[1,8,512]{2,1,0:T(8,128)S(1)}, f32[1,8,512]{2,1,0:T(8,128)S(1)}, u32[]{:S(2)}, u32[]{:S(2)}) collective-permute-start(f32[1,8,512]{2,1,0:T(8,128)S(1)} %get-tuple-element.47), channel_id=1, source_target_pairs={{8,16},{16,8},{9,17},{17,9},{10,18},{18,10},{11,19},{19,11},{12,20... | collective-permute-start | bytes 49160 | tf_op jit(solution)/shard_map/ppermute | solution.py:30
  11.4 12.3 %collective-permute-start.4 = (f32[1,8,512]{2,1,0:T(8,128)S(1)}, f32[1,8,512]{2,1,0:T(8,128)S(1)}, u32[]{:S(2)}, u32[]{:S(2)}) collective-permute-start(f32[1,8,512]{2,1,0:T(8,128)S(1)} %get-tuple-element.48), channel_id=1, source_target_pairs={{0,8},{8,0},{16,24},{24,16},{1,9},{9,1},{17,25},{25,17},{2,10},{10... | collective-permute-start | bytes 49160 | tf_op jit(solution)/shard_map/ppermute | solution.py:29
  17.2 6.6 %collective-permute-start.7 = (f32[16,1,512]{2,1,0:T(1,128)S(1)}, f32[16,1,512]{2,1,0:T(1,128)S(1)}, u32[]{:S(2)}, u32[]{:S(2)}) collective-permute-start(f32[16,1,512]{2,1,0:T(1,128)S(1)} %get-tuple-element.43), channel_id=1, source_target_pairs={{1,2},{2,1},{3,4},{4,3},{5,6},{6,5},{9,10},{10,9},{11,12},{12,11},... | collective-permute-start | bytes 98312 | tf_op jit(solution)/shard_map/ppermute | solution.py:30
  17.9 6.8 %collective-permute-start.6 = (f32[16,1,512]{2,1,0:T(1,128)S(1)}, f32[16,1,512]{2,1,0:T(1,128)S(1)}, u32[]{:S(2)}, u32[]{:S(2)}) collective-permute-start(f32[16,1,512]{2,1,0:T(1,128)S(1)} %get-tuple-element.44), channel_id=1, source_target_pairs={{0,1},{1,0},{2,3},{3,2},{4,5},{5,4},{6,7},{7,6},{8,9},{9,8},{10,11... | collective-permute-start | bytes 98312 | tf_op jit(solution)/shard_map/ppermute | solution.py:29
  25.1 4.7 %copy-start = (f32[16,8,512]{2,1,0:T(8,128)}, f32[16,8,512]{2,1,0:T(8,128)S(1)}, u32[]{:S(2)}) copy-start(f32[16,8,512]{2,1,0:T(8,128)S(1)} %fusion.13.refs_1_.refs_2_) | copy-start | bytes 786436
  25.4 8.9 %collective-permute-start.9 = (f32[1,8,512]{2,1,0:T(8,128)S(1)}, f32[1,8,512]{2,1,0:T(8,128)S(1)}, u32[]{:S(2)}, u32[]{:S(2)}) collective-permute-start(f32[1,8,512]{2,1,0:T(8,128)S(1)} %get-tuple-element.37), channel_id=1, source_target_pairs={{8,16},{16,8},{9,17},{17,9},{10,18},{18,10},{11,19},{19,11},{12,20... | collective-permute-start | bytes 49160 | tf_op jit(solution)/shard_map/ppermute | solution.py:30
  26.0 8.2 %collective-permute-start.8 = (f32[1,8,512]{2,1,0:T(8,128)S(1)}, f32[1,8,512]{2,1,0:T(8,128)S(1)}, u32[]{:S(2)}, u32[]{:S(2)}) collective-permute-start(f32[1,8,512]{2,1,0:T(8,128)S(1)} %get-tuple-element.38), channel_id=1, source_target_pairs={{0,8},{8,0},{16,24},{24,16},{1,9},{9,1},{17,25},{25,17},{2,10},{10... | collective-permute-start | bytes 49160 | tf_op jit(solution)/shard_map/ppermute | solution.py:29
  29.9 4.4 %collective-permute-start.11 = (f32[16,1,512]{2,1,0:T(1,128)S(1)}, f32[16,1,512]{2,1,0:T(1,128)S(1)}, u32[]{:S(2)}, u32[]{:S(2)}) collective-permute-start(f32[16,1,512]{2,1,0:T(1,128)S(1)} %get-tuple-element.33), channel_id=1, source_target_pairs={{1,2},{2,1},{3,4},{4,3},{5,6},{6,5},{9,10},{10,9},{11,12},{12,11},... | collective-permute-start | bytes 98312 | tf_op jit(solution)/shard_map/ppermute | solution.py:30
  30.5 4.6 %collective-permute-start.10 = (f32[16,1,512]{2,1,0:T(1,128)S(1)}, f32[16,1,512]{2,1,0:T(1,128)S(1)}, u32[]{:S(2)}, u32[]{:S(2)}) collective-permute-start(f32[16,1,512]{2,1,0:T(1,128)S(1)} %get-tuple-element.34), channel_id=1, source_target_pairs={{0,1},{1,0},{2,3},{3,2},{4,5},{5,4},{6,7},{7,6},{8,9},{9,8},{10,11... | collective-permute-start | bytes 98312 | tf_op jit(solution)/shard_map/ppermute | solution.py:29
  35.6 3.1 %copy-start.1 = (f32[16,8,512]{2,1,0:T(8,128)}, f32[16,8,512]{2,1,0:T(8,128)S(1)}, u32[]{:S(2)}) copy-start(f32[16,8,512]{2,1,0:T(8,128)S(1)} %fusion.20.refs_2_.refs_3_) | copy-start | bytes 786436
  35.9 7.2 %collective-permute-start.13 = (f32[1,8,512]{2,1,0:T(8,128)S(1)}, f32[1,8,512]{2,1,0:T(8,128)S(1)}, u32[]{:S(2)}, u32[]{:S(2)}) collective-permute-start(f32[1,8,512]{2,1,0:T(8,128)S(1)} %get-tuple-element.27), channel_id=1, source_target_pairs={{8,16},{16,8},{9,17},{17,9},{10,18},{18,10},{11,19},{19,11},{12,20... | collective-permute-start | bytes 49160 | tf_op jit(solution)/shard_map/ppermute | solution.py:30
  36.5 6.5 %collective-permute-start.12 = (f32[1,8,512]{2,1,0:T(8,128)S(1)}, f32[1,8,512]{2,1,0:T(8,128)S(1)}, u32[]{:S(2)}, u32[]{:S(2)}) collective-permute-start(f32[1,8,512]{2,1,0:T(8,128)S(1)} %get-tuple-element.28), channel_id=1, source_target_pairs={{0,8},{8,0},{16,24},{24,16},{1,9},{9,1},{17,25},{25,17},{2,10},{10... | collective-permute-start | bytes 49160 | tf_op jit(solution)/shard_map/ppermute | solution.py:29
  38.7 4.4 %collective-permute-start.15 = (f32[16,1,512]{2,1,0:T(1,128)S(1)}, f32[16,1,512]{2,1,0:T(1,128)S(1)}, u32[]{:S(2)}, u32[]{:S(2)}) collective-permute-start(f32[16,1,512]{2,1,0:T(1,128)S(1)} %get-tuple-element.23), channel_id=1, source_target_pairs={{1,2},{2,1},{3,4},{4,3},{5,6},{6,5},{9,10},{10,9},{11,12},{12,11},... | collective-permute-start | bytes 98312 | tf_op jit(solution)/shard_map/ppermute | solution.py:30
  39.3 4.5 %collective-permute-start.14 = (f32[16,1,512]{2,1,0:T(1,128)S(1)}, f32[16,1,512]{2,1,0:T(1,128)S(1)}, u32[]{:S(2)}, u32[]{:S(2)}) collective-permute-start(f32[16,1,512]{2,1,0:T(1,128)S(1)} %get-tuple-element.24), channel_id=1, source_target_pairs={{0,1},{1,0},{2,3},{3,2},{4,5},{5,4},{6,7},{7,6},{8,9},{9,8},{10,11... | collective-permute-start | bytes 98312 | tf_op jit(solution)/shard_map/ppermute | solution.py:29
  44.3 4.5 %copy-start.2 = (f32[16,8,512]{2,1,0:T(8,128)}, f32[16,8,512]{2,1,0:T(8,128)S(1)}, u32[]{:S(2)}) copy-start(f32[16,8,512]{2,1,0:T(8,128)S(1)} %fusion.27.refs_3_.refs_4_) | copy-start | bytes 786436
  44.6 8.6 %collective-permute-start.17 = (f32[1,8,512]{2,1,0:T(8,128)S(1)}, f32[1,8,512]{2,1,0:T(8,128)S(1)}, u32[]{:S(2)}, u32[]{:S(2)}) collective-permute-start(f32[1,8,512]{2,1,0:T(8,128)S(1)} %get-tuple-element.17), channel_id=1, source_target_pairs={{8,16},{16,8},{9,17},{17,9},{10,18},{18,10},{11,19},{19,11},{12,20... | collective-permute-start | bytes 49160 | tf_op jit(solution)/shard_map/ppermute | solution.py:30
  45.3 8.0 %collective-permute-start.16 = (f32[1,8,512]{2,1,0:T(8,128)S(1)}, f32[1,8,512]{2,1,0:T(8,128)S(1)}, u32[]{:S(2)}, u32[]{:S(2)}) collective-permute-start(f32[1,8,512]{2,1,0:T(8,128)S(1)} %get-tuple-element.18), channel_id=1, source_target_pairs={{0,8},{8,0},{16,24},{24,16},{1,9},{9,1},{17,25},{25,17},{2,10},{10... | collective-permute-start | bytes 49160 | tf_op jit(solution)/shard_map/ppermute | solution.py:29
  48.9 4.4 %collective-permute-start.19 = (f32[16,1,512]{2,1,0:T(1,128)S(1)}, f32[16,1,512]{2,1,0:T(1,128)S(1)}, u32[]{:S(2)}, u32[]{:S(2)}) collective-permute-start(f32[16,1,512]{2,1,0:T(1,128)S(1)} %get-tuple-element.13), channel_id=1, source_target_pairs={{1,2},{2,1},{3,4},{4,3},{5,6},{6,5},{9,10},{10,9},{11,12},{12,11},... | collective-permute-start | bytes 98312 | tf_op jit(solution)/shard_map/ppermute | solution.py:30
  49.6 4.5 %collective-permute-start.18 = (f32[16,1,512]{2,1,0:T(1,128)S(1)}, f32[16,1,512]{2,1,0:T(1,128)S(1)}, u32[]{:S(2)}, u32[]{:S(2)}) collective-permute-start(f32[16,1,512]{2,1,0:T(1,128)S(1)} %get-tuple-element.14), channel_id=1, source_target_pairs={{0,1},{1,0},{2,3},{3,2},{4,5},{5,4},{6,7},{7,6},{8,9},{9,8},{10,11... | collective-permute-start | bytes 98312 | tf_op jit(solution)/shard_map/ppermute | solution.py:29
  57.5 1.6 %collective-permute-start.20 = (f32[1,128]{1,0:T(1,128)}, f32[1,128]{1,0:T(1,128)S(1)}, u32[]{:S(2)}, u32[]{:S(2)}) collective-permute-start(f32[1,128]{1,0:T(1,128)} %shard_map.85), channel_id=1, source_target_pairs={{0,1},{1,0},{2,3},{3,2},{4,5},{5,4},{6,7},{7,6},{8,9},{9,8},{10,11... | collective-permute-start | bytes 1544 | tf_op jit(solution)/shard_map/ppermute | solution.py:70
  59.8 3.5 %collective-permute-start.21 = (f32[1,128]{1,0:T(1,128)S(1)}, f32[1,128]{1,0:T(1,128)S(1)}, u32[]{:S(2)}, u32[]{:S(2)}) collective-permute-start(f32[1,128]{1,0:T(1,128)S(1)} %add.178), channel_id=1, source_target_pairs={{0,2},{1,3},{2,0},{3,1},{4,6},{5,7},{6,4},{7,5},{8,10},{9,11},{10,... | collective-permute-start | bytes 1544 | tf_op jit(solution)/shard_map/ppermute | solution.py:70
  63.4 4.5 %collective-permute-start.22 = (f32[1,128]{1,0:T(1,128)S(1)}, f32[1,128]{1,0:T(1,128)S(1)}, u32[]{:S(2)}, u32[]{:S(2)}) collective-permute-start(f32[1,128]{1,0:T(1,128)S(1)} %add.179), channel_id=1, source_target_pairs={{0,4},{1,5},{2,6},{3,7},{4,0},{5,1},{6,2},{7,3},{8,12},{9,13},{10,... | collective-permute-start | bytes 1544 | tf_op jit(solution)/shard_map/ppermute | solution.py:70
  67.8 3.5 %collective-permute-start.23 = (f32[1,128]{1,0:T(1,128)S(1)}, f32[1,128]{1,0:T(1,128)S(1)}, u32[]{:S(2)}, u32[]{:S(2)}) collective-permute-start(f32[1,128]{1,0:T(1,128)S(1)} %add.180), channel_id=1, source_target_pairs={{0,8},{8,0},{16,24},{24,16},{1,9},{9,1},{17,25},{25,17},{2,10},{10... | collective-permute-start | bytes 1544 | tf_op jit(solution)/shard_map/ppermute | solution.py:70
  71.4 3.5 %collective-permute-start.24 = (f32[1,128]{1,0:T(1,128)S(1)}, f32[1,128]{1,0:T(1,128)S(1)}, u32[]{:S(2)}, u32[]{:S(2)}) collective-permute-start(f32[1,128]{1,0:T(1,128)S(1)} %add.181), channel_id=1, source_target_pairs={{0,16},{8,24},{16,0},{24,8},{1,17},{9,25},{17,1},{25,9},{2,18},{10... | collective-permute-start | bytes 1544 | tf_op jit(solution)/shard_map/ppermute | solution.py:70

commit v17 on v16

--- a/solution.py
+++ b/solution.py
@@ -60,16 +60,25 @@
 
 
 def all_sum(x):
+    rounds = []
     for axis in ("gy", "gx"):
         n = lax.axis_size(axis)
         if n & (n - 1):
-            x = lax.psum(x, axis)
+            rounds.append((axis, None))
             continue
         step = 1
         while step < n:
-            x = x + lax.ppermute(x, axis, [(i, i ^ step) for i in range(n)])
+            rounds.append((axis, step))
             step *= 2
-    return x
+    for k, (axis, step) in enumerate(rounds):
+        if step is None:
+            x = lax.psum(x, axis)
+            continue
+        other = lax.ppermute(x, axis, [(i, i ^ step) for i in range(lax.axis_size(axis))])
+        if k == len(rounds) - 1:
+            return x, other
+        x = x + other
+    return x, jnp.zeros_like(x)
 
 
 def gram_kernel(size, *refs):
@@ -112,12 +121,12 @@
     )(*basis)
 
 
-def finish_kernel(cells, size, stats_ref, *refs):
+def finish_kernel(cells, size, stats_ref, other_ref, *refs):
     basis_refs, (ortho_ref, upper_ref, scale_ref) = refs[:size], refs[size:]
     tile = (8, 128)
 
     def held(i):
-        return jnp.full(tile, stats_ref[0, i], jnp.float32)
+        return jnp.full(tile, stats_ref[0, i], jnp.float32) + jnp.full(tile, other_ref[0, i], jnp.float32)
 
     per_cell = 1.0 / cells
     scale = jnp.sqrt(held(0) * per_cell + EPS)
@@ -184,9 +193,9 @@
             jax.ShapeDtypeStruct((size, size), jnp.float32),
             jax.ShapeDtypeStruct((1, 1), jnp.float32),
         ),
-        in_specs=[pl.BlockSpec(memory_space=pltpu.SMEM)] + [vmem] * size,
+        in_specs=[pl.BlockSpec(memory_space=pltpu.SMEM)] * 2 + [vmem] * size,
         out_specs=(vmem, vmem, vmem),
-    )(stats, *basis)
+    )(*stats, *basis)
     return ortho, upper, scale.reshape(())
 
 

time: 78.7 us -> 78.7 us (level)
  no operation moved by 1% of the time
where the time goes in v17:
time: 78.7 us; the launch traced here: 78.2 us
  starting transfers between devices  47.5 us (60%)
  waiting for transfers between devices  14.5 us (18%)
  local copies, waits for them, and re-layouts  5.86 us (7%)
  Pallas kernels  4.98 us (6%)
  other arithmetic  4.13 us (5%)
  between operations  1.2 us (2%)
    ppermute x10, starting transfers between devices, axis_exchange(): lax.ppermute(jnp.where(odd, to_low, to_high), axis, swap_pairs(axis, 0))  35.2 us
    ppermute x5, waiting for transfers between devices, all_sum(): lax.ppermute(x, axis, [(i, i ^ step) for i in range(lax.axis_size(axis))])  11.1 us
    ppermute x10, starting transfers between devices, axis_exchange(): lax.ppermute(jnp.where(odd, to_high, to_low), axis, swap_pairs(axis, 1))  6.75 us
    ppermute x5, starting transfers between devices, all_sum(): lax.ppermute(x, axis, [(i, i ^ step) for i in range(lax.axis_size(axis))])  5.55 us
    ppermute x10, waiting for transfers between devices, axis_exchange(): lax.ppermute(jnp.where(odd, to_low, to_high), axis, swap_pairs(axis, 0))  3.35 us
    pallas_call x1, Pallas kernels, finish(): pl.pallas_call(lambda *refs: finish_kernel(float(cells), size, *refs), ou...  2.75 us
    div x4, other arithmetic, local(): vector = 2.0 * total / diagonal  2.51 us
    pallas_call x1, Pallas kernels, gram(): pl.pallas_call(lambda *refs: gram_kernel(size, *refs), out_shape=jax.Shap...  2.23 us
  transfers between devices with their start and end apart: 25, of which 9 were waited for; matrix products, arithmetic and copies ran while one was open for 4% of the time, Pallas kernels for 0%

profile of v17, /device:TPU:0, one launch (start us, length us, event | category | flops | bytes accessed | tf_op | source)
XLA Modules:
  0.0 78.2 jit_solution(16658926691200082268)
XLA Ops:
  0.6 0.0 copy-start.4
  0.7 0.8 %fusion.54 = (f32[1,8,512]{2,1,0:T(8,128)S(1)}, f32[1,8,512]{2,1,0:T(8,128)S(1)}, f32[1,8,512]{2,1,0:T(8,128)S(1)}, f32[1,8,512]{2,1,0:T(8,128)S(1)}) fusion(f32[16,8,512]{2,1,0:T(8,128)} %param.6, f32[16,8,512]{2,1,0:T(8,128)} %param.9), kind=kLoop, calls=%fused_computation.119 | loop fusion | bytes 131072 | tf_op jit(solution)/shard_map/slice | solution.py:208
  1.5 3.0 %collective-permute-start.1 = (f32[2,8,512]{2,1,0:T(8,128)S(1)}, f32[2,8,512]{2,1,0:T(8,128)S(1)}, u32[]{:S(2)}, u32[]{:S(2)}) collective-permute-start(f32[2,8,512]{2,1,0:T(8,128)S(1)} %get-tuple-element.75), channel_id=1, source_target_pairs={{0,8},{8,0},{16,24},{24,16},{1,9},{9,1},{17,25},{25,17},{2,10},{10... | collective-permute-start | bytes 98312 | tf_op jit(solution)/shard_map/ppermute | solution.py:29
  4.5 0.7 collective-permute-start
  5.2 1.3 %fusion.51 = (f32[16,1,512]{2,1,0:T(1,128)S(1)}, f32[16,1,512]{2,1,0:T(1,128)S(1)}, f32[16,1,512]{2,1,0:T(1,128)S(1)}, f32[16,1,512]{2,1,0:T(1,128)S(1)}) fusion(f32[16,8,512]{2,1,0:T(8,128)} %param.6, f32[16,8,512]{2,1,0:T(8,128)} %param.10), kind=kLoop, calls=%fused_computation.116 | loop fusion | bytes 262144 | tf_op jit(solution)/shard_map/slice | solution.py:210
  6.5 0.1 broadcast_select_fusion.18
  6.6 0.1 collective-permute-start.3
  6.7 0.8 %collective-permute-start.2 = (f32[16,2,512]{2,1,0:T(2,128)S(1)}, f32[16,2,512]{2,1,0:T(2,128)S(1)}, u32[]{:S(2)}, u32[]{:S(2)}) collective-permute-start(f32[16,2,512]{2,1,0:T(2,128)S(1)} %get-tuple-element.64), channel_id=1, source_target_pairs={{1,2},{2,1},{3,4},{4,3},{5,6},{6,5},{9,10},{10,9},{11,12},{12,11},... | collective-permute-start | bytes 196616 | tf_op jit(solution)/shard_map/ppermute | solution.py:30
  7.5 1.1 %fusion.50 = (f32[16,7,512]{2,1,0:T(8,128)S(1)}, f32[16,7,512]{2,1,0:T(8,128)S(1)}) fusion(f32[16,8,512]{2,1,0:T(8,128)} %param.6), kind=kLoop, calls=%fused_computation.115 | loop fusion | bytes 917504 | tf_op jit(solution)/shard_map/slice | solution.py:49
  8.6 0.0 copy-start.5
  8.6 0.0 copy-start.7
  8.6 0.1 fusion.49
  8.7 0.1 fusion.53
  8.9 0.7 copy-done.5
  9.6 0.1 copy-done.7
  9.6 0.1 slice.201
  9.8 0.1 fusion.56
  10.0 0.5 fusion.6.refs_0_.refs_2_
  10.5 0.1 fusion.48
  10.6 0.1 fusion.46
  10.7 0.1 fusion.47
  10.8 0.7 collective-permute-start.5
  11.4 5.7 %collective-permute-start.4 = (f32[1,8,512]{2,1,0:T(8,128)S(1)}, f32[1,8,512]{2,1,0:T(8,128)S(1)}, u32[]{:S(2)}, u32[]{:S(2)}) collective-permute-start(f32[1,8,512]{2,1,0:T(8,128)S(1)} %get-tuple-element.48), channel_id=1, source_target_pairs={{0,8},{8,0},{16,24},{24,16},{1,9},{9,1},{17,25},{25,17},{2,10},{10... | collective-permute-start | bytes 49160 | tf_op jit(solution)/shard_map/ppermute | solution.py:29
  17.2 0.7 collective-permute-start.7
  17.9 5.9 %collective-permute-start.6 = (f32[16,1,512]{2,1,0:T(1,128)S(1)}, f32[16,1,512]{2,1,0:T(1,128)S(1)}, u32[]{:S(2)}, u32[]{:S(2)}) collective-permute-start(f32[16,1,512]{2,1,0:T(1,128)S(1)} %get-tuple-element.44), channel_id=1, source_target_pairs={{0,1},{1,0},{2,3},{3,2},{4,5},{5,4},{6,7},{7,6},{8,9},{9,8},{10,11... | collective-permute-start | bytes 98312 | tf_op jit(solution)/shard_map/ppermute | solution.py:29
  23.8 0.8 %collective-permute-done.6 = f32[16,1,512]{2,1,0:T(1,128)S(1)} collective-permute-done((f32[16,1,512]{2,1,0:T(1,128)S(1)}, f32[16,1,512]{2,1,0:T(1,128)S(1)}, u32[]{:S(2)}, u32[]{:S(2)}) %collective-permute-start.6) | collective-permute-done | bytes 32800 | tf_op jit(solution)/shard_map/ppermute | solution.py:29
  24.6 0.5 fusion.13.refs_1_.refs_3_
  25.1 0.1 fusion.43
  25.3 0.1 fusion.44
  25.4 0.7 collective-permute-start.9
  26.0 3.8 %collective-permute-start.8 = (f32[1,8,512]{2,1,0:T(8,128)S(1)}, f32[1,8,512]{2,1,0:T(8,128)S(1)}, u32[]{:S(2)}, u32[]{:S(2)}) collective-permute-start(f32[1,8,512]{2,1,0:T(8,128)S(1)} %get-tuple-element.38), channel_id=1, source_target_pairs={{0,8},{8,0},{16,24},{24,16},{1,9},{9,1},{17,25},{25,17},{2,10},{10... | collective-permute-start | bytes 49160 | tf_op jit(solution)/shard_map/ppermute | solution.py:29
  29.9 0.7 collective-permute-start.11
  30.5 3.7 %collective-permute-start.10 = (f32[16,1,512]{2,1,0:T(1,128)S(1)}, f32[16,1,512]{2,1,0:T(1,128)S(1)}, u32[]{:S(2)}, u32[]{:S(2)}) collective-permute-start(f32[16,1,512]{2,1,0:T(1,128)S(1)} %get-tuple-element.34), channel_id=1, source_target_pairs={{0,1},{1,0},{2,3},{3,2},{4,5},{5,4},{6,7},{7,6},{8,9},{9,8},{10,11... | collective-permute-start | bytes 98312 | tf_op jit(solution)/shard_map/ppermute | solution.py:29
  34.3 0.8 %collective-permute-done.10 = f32[16,1,512]{2,1,0:T(1,128)S(1)} collective-permute-done((f32[16,1,512]{2,1,0:T(1,128)S(1)}, f32[16,1,512]{2,1,0:T(1,128)S(1)}, u32[]{:S(2)}, u32[]{:S(2)}) %collective-permute-start.10) | collective-permute-done | bytes 32800 | tf_op jit(solution)/shard_map/ppermute | solution.py:29
  35.1 0.5 fusion.20.refs_2_.refs_4_
  35.6 0.1 fusion.40
  35.8 0.1 fusion.41
  35.9 0.7 collective-permute-start.13
  36.5 2.1 %collective-permute-start.12 = (f32[1,8,512]{2,1,0:T(8,128)S(1)}, f32[1,8,512]{2,1,0:T(8,128)S(1)}, u32[]{:S(2)}, u32[]{:S(2)}) collective-permute-start(f32[1,8,512]{2,1,0:T(8,128)S(1)} %get-tuple-element.28), channel_id=1, source_target_pairs={{0,8},{8,0},{16,24},{24,16},{1,9},{9,1},{17,25},{25,17},{2,10},{10... | collective-permute-start | bytes 49160 | tf_op jit(solution)/shard_map/ppermute | solution.py:29
  38.7 0.7 collective-permute-start.15
  39.3 3.7 %collective-permute-start.14 = (f32[16,1,512]{2,1,0:T(1,128)S(1)}, f32[16,1,512]{2,1,0:T(1,128)S(1)}, u32[]{:S(2)}, u32[]{:S(2)}) collective-permute-start(f32[16,1,512]{2,1,0:T(1,128)S(1)} %get-tuple-element.24), channel_id=1, source_target_pairs={{0,1},{1,0},{2,3},{3,2},{4,5},{5,4},{6,7},{7,6},{8,9},{9,8},{10,11... | collective-permute-start | bytes 98312 | tf_op jit(solution)/shard_map/ppermute | solution.py:29
  43.1 0.8 %collective-permute-done.14 = f32[16,1,512]{2,1,0:T(1,128)S(1)} collective-permute-done((f32[16,1,512]{2,1,0:T(1,128)S(1)}, f32[16,1,512]{2,1,0:T(1,128)S(1)}, u32[]{:S(2)}, u32[]{:S(2)}) %collective-permute-start.14) | collective-permute-done | bytes 32800 | tf_op jit(solution)/shard_map/ppermute | solution.py:29
  43.9 0.5 fusion.27.refs_3_.refs_5_
  44.4 0.1 fusion.37
  44.6 0.1 fusion.38
  44.6 0.7 collective-permute-start.17
  45.3 3.6 %collective-permute-start.16 = (f32[1,8,512]{2,1,0:T(8,128)S(1)}, f32[1,8,512]{2,1,0:T(8,128)S(1)}, u32[]{:S(2)}, u32[]{:S(2)}) collective-permute-start(f32[1,8,512]{2,1,0:T(8,128)S(1)} %get-tuple-element.18), channel_id=1, source_target_pairs={{0,8},{8,0},{16,24},{24,16},{1,9},{9,1},{17,25},{25,17},{2,10},{10... | collective-permute-start | bytes 49160 | tf_op jit(solution)/shard_map/ppermute | solution.py:29
  48.9 0.7 collective-permute-start.19
  49.6 3.7 %collective-permute-start.18 = (f32[16,1,512]{2,1,0:T(1,128)S(1)}, f32[16,1,512]{2,1,0:T(1,128)S(1)}, u32[]{:S(2)}, u32[]{:S(2)}) collective-permute-start(f32[16,1,512]{2,1,0:T(1,128)S(1)} %get-tuple-element.14), channel_id=1, source_target_pairs={{0,1},{1,0},{2,3},{3,2},{4,5},{5,4},{6,7},{7,6},{8,9},{9,8},{10,11... | collective-permute-start | bytes 98312 | tf_op jit(solution)/shard_map/ppermute | solution.py:29
  53.3 0.8 %collective-permute-done.18 = f32[16,1,512]{2,1,0:T(1,128)S(1)} collective-permute-done((f32[16,1,512]{2,1,0:T(1,128)S(1)}, f32[16,1,512]{2,1,0:T(1,128)S(1)}, u32[]{:S(2)}, u32[]{:S(2)}) %collective-permute-start.18) | collective-permute-done | bytes 32800 | tf_op jit(solution)/shard_map/ppermute | solution.py:29
  54.1 1.2 %fusion.34.refs_4_.refs_6_ = f32[16,8,512]{2,1,0:T(8,128)} fusion(f32[16,8,512]{2,1,0:T(8,128)S(1)} %copy-done.6, f32[15,8,512]{2,1,0:T(8,128)S(1)} %get-tuple-element.16, f32[1,8,512]{2,1,0:T(8,128)S(1)} %get-tuple-element.78, f32[1,8,512]{2,1,0:T(8,128)S(1)} %get-tuple-element.77, f32[15,8,512]{2,1,0:T(8,128)S(1)} %get-tuple-element.15, ...), kind=kLoop, calls=%fused_computation.53 | loop fusion | flops 1638400 | bytes 3668480 | tf_op jit(solution)/shard_map/div | solution.py:232
  55.3 2.2 %shard_map.85 = f32[1,128]{1,0:T(1,128)} custom-call(f32[16,8,512]{2,1,0:T(8,128)} %copy-done.3, f32[16,8,512]{2,1,0:T(8,128)} %copy-done, f32[16,8,512]{2,1,0:T(8,128)} %copy-done.1, f32[16,8,512]{2,1,0:T(8,128)} %copy-done.2, f32[16,8,512]{2,1,0:T(8,128)} %fusion.34.refs_4_.refs_6_), custom_call_target="tpu_custom_call" | custom-call | tf_op jit(solution)/shard_map/pallas_call | solution.py:116
  57.5 0.7 collective-permute-start.20
  58.2 1.0 %collective-permute-done.20 = f32[1,128]{1,0:T(1,128)S(1)} collective-permute-done((f32[1,128]{1,0:T(1,128)}, f32[1,128]{1,0:T(1,128)S(1)}, u32[]{:S(2)}, u32[]{:S(2)}) %collective-permute-start.20) | collective-permute-done | bytes 544 | tf_op jit(solution)/shard_map/ppermute | solution.py:77
  59.1 0.7 add.175
  59.8 1.9 %collective-permute-start.21 = (f32[1,128]{1,0:T(1,128)S(1)}, f32[1,128]{1,0:T(1,128)S(1)}, u32[]{:S(2)}, u32[]{:S(2)}) collective-permute-start(f32[1,128]{1,0:T(1,128)S(1)} %add.175), channel_id=1, source_target_pairs={{0,2},{1,3},{2,0},{3,1},{4,6},{5,7},{6,4},{7,5},{8,10},{9,11},{10,... | collective-permute-start | bytes 1544 | tf_op jit(solution)/shard_map/ppermute | solution.py:77
  61.7 1.6 %collective-permute-done.21 = f32[1,128]{1,0:T(1,128)S(1)} collective-permute-done((f32[1,128]{1,0:T(1,128)S(1)}, f32[1,128]{1,0:T(1,128)S(1)}, u32[]{:S(2)}, u32[]{:S(2)}) %collective-permute-start.21) | collective-permute-done | bytes 544 | tf_op jit(solution)/shard_map/ppermute | solution.py:77
  63.3 2.9 %collective-permute-start.22 = (f32[1,128]{1,0:T(1,128)S(1)}, f32[1,128]{1,0:T(1,128)S(1)}, u32[]{:S(2)}, u32[]{:S(2)}) collective-permute-start(f32[1,128]{1,0:T(1,128)S(1)} %add.176), channel_id=1, source_target_pairs={{0,4},{1,5},{2,6},{3,7},{4,0},{5,1},{6,2},{7,3},{8,12},{9,13},{10,... | collective-permute-start | bytes 1544 | tf_op jit(solution)/shard_map/ppermute | solution.py:77
  66.3 1.5 %collective-permute-done.22 = f32[1,128]{1,0:T(1,128)S(1)} collective-permute-done((f32[1,128]{1,0:T(1,128)S(1)}, f32[1,128]{1,0:T(1,128)S(1)}, u32[]{:S(2)}, u32[]{:S(2)}) %collective-permute-start.22) | collective-permute-done | bytes 544 | tf_op jit(solution)/shard_map/ppermute | solution.py:77
  67.8 0.0 collective-permute-start.23
  67.8 3.5 %collective-permute-done.23 = f32[1,128]{1,0:T(1,128)S(1)} collective-permute-done((f32[1,128]{1,0:T(1,128)S(1)}, f32[1,128]{1,0:T(1,128)S(1)}, u32[]{:S(2)}, u32[]{:S(2)}) %collective-permute-start.23) | collective-permute-done | bytes 544 | tf_op jit(solution)/shard_map/ppermute | solution.py:77
  71.4 3.5 %collective-permute-done.24.refs_1_ = f32[1,128]{1,0:T(1,128)S(1)} collective-permute-done((f32[1,128]{1,0:T(1,128)S(1)}, f32[1,128]{1,0:T(1,128)S(1)}, u32[]{:S(2)}, u32[]{:S(2)}) %collective-permute-start.24) | collective-permute-done | bytes 544 | tf_op jit(solution)/shard_map/ppermute | solution.py:77
  74.9 0.5 copy-done.11
  75.4 2.8 %shard_map.86 = (f32[5,16,8,512]{3,2,1,0:T(8,128)}, f32[5,5]{1,0:T(8,128)}, f32[1,1]{1,0:T(1,128)}) custom-call(f32[1,128]{1,0:T(1,128)} %copy-done.10, f32[1,128]{1,0:T(1,128)} %copy-done.11, f32[16,8,512]{2,1,0:T(8,128)} %copy-done.3, f32[16,8,512]{2,1,0:T(8,128)} %copy-done, f32[16,8,512]{2,1,0:T(8,128)} %copy-done.1, f32[16,8,512]{2,1,0:T(8,128)} %copy-done.2, ...), custom_call_target="tpu_custom_call" | custom-call | tf_op jit(solution)/shard_map/pallas_call | solution.py:189
  (65 shorter events, 0.6 us)
Async XLA Ops:
  0.6 7.9 %copy-start.4 = (f32[16,8,512]{2,1,0:T(8,128)S(1)}, f32[16,8,512]{2,1,0:T(8,128)}, u32[]{:S(2)}) copy-start(f32[16,8,512]{2,1,0:T(8,128)} %param.6) | copy-start | bytes 786436
  1.5 8.3 %collective-permute-start.1 = (f32[2,8,512]{2,1,0:T(8,128)S(1)}, f32[2,8,512]{2,1,0:T(8,128)S(1)}, u32[]{:S(2)}, u32[]{:S(2)}) collective-permute-start(f32[2,8,512]{2,1,0:T(8,128)S(1)} %get-tuple-element.75), channel_id=1, source_target_pairs={{0,8},{8,0},{16,24},{24,16},{1,9},{9,1},{17,25},{25,17},{2,10},{10... | collective-permute-start | bytes 98312 | tf_op jit(solution)/shard_map/ppermute | solution.py:29
  4.5 5.3 %collective-permute-start = (f32[2,8,512]{2,1,0:T(8,128)S(1)}, f32[2,8,512]{2,1,0:T(8,128)S(1)}, u32[]{:S(2)}, u32[]{:S(2)}) collective-permute-start(f32[2,8,512]{2,1,0:T(8,128)S(1)} %get-tuple-element.76), channel_id=1, source_target_pairs={{8,16},{16,8},{9,17},{17,9},{10,18},{18,10},{11,19},{19,11},{12,20... | collective-permute-start | bytes 98312 | tf_op jit(solution)/shard_map/ppermute | solution.py:30
  6.6 3.2 %collective-permute-start.3 = (f32[16,2,512]{2,1,0:T(2,128)S(1)}, f32[16,2,512]{2,1,0:T(2,128)S(1)}, u32[]{:S(2)}, u32[]{:S(2)}) collective-permute-start(f32[16,2,512]{2,1,0:T(2,128)S(1)} %get-tuple-element.63), channel_id=1, source_target_pairs={{0,1},{1,0},{2,3},{3,2},{4,5},{5,4},{6,7},{7,6},{8,9},{9,8},{10,11... | collective-permute-start | bytes 196616 | tf_op jit(solution)/shard_map/ppermute | solution.py:29
  6.7 2.1 %copy-start.6 = (f32[16,8,512]{2,1,0:T(8,128)S(1)}, f32[16,8,512]{2,1,0:T(8,128)}, u32[]{:S(2)}) copy-start(f32[16,8,512]{2,1,0:T(8,128)} %param.9) | copy-start | bytes 786436
  6.7 3.1 %collective-permute-start.2 = (f32[16,2,512]{2,1,0:T(2,128)S(1)}, f32[16,2,512]{2,1,0:T(2,128)S(1)}, u32[]{:S(2)}, u32[]{:S(2)}) collective-permute-start(f32[16,2,512]{2,1,0:T(2,128)S(1)} %get-tuple-element.64), channel_id=1, source_target_pairs={{1,2},{2,1},{3,4},{4,3},{5,6},{6,5},{9,10},{10,9},{11,12},{12,11},... | collective-permute-start | bytes 196616 | tf_op jit(solution)/shard_map/ppermute | solution.py:30
  8.6 1.0 %copy-start.5 = (f32[16,8,512]{2,1,0:T(8,128)S(1)}, f32[16,8,512]{2,1,0:T(8,128)}, u32[]{:S(2)}) copy-start(f32[16,8,512]{2,1,0:T(8,128)} %param.10) | copy-start | bytes 786436
  8.6 1.0 %copy-start.7 = (f32[16,8,512]{2,1,0:T(8,128)S(1)}, f32[16,8,512]{2,1,0:T(8,128)}, u32[]{:S(2)}) copy-start(f32[16,8,512]{2,1,0:T(8,128)} %param.11) | copy-start | bytes 786436
  8.8 1.1 %copy-start.8 = (f32[16,8,512]{2,1,0:T(8,128)S(1)}, f32[16,8,512]{2,1,0:T(8,128)}, u32[]{:S(2)}) copy-start(f32[16,8,512]{2,1,0:T(8,128)} %param.8) | copy-start | bytes 786436
  8.8 1.1 %copy-start.9 = (f32[16,8,512]{2,1,0:T(8,128)S(1)}, f32[16,8,512]{2,1,0:T(8,128)}, u32[]{:S(2)}) copy-start(f32[16,8,512]{2,1,0:T(8,128)} %param.7) | copy-start | bytes 786436
  10.5 6.7 %copy-start.3 = (f32[16,8,512]{2,1,0:T(8,128)}, f32[16,8,512]{2,1,0:T(8,128)S(1)}, u32[]{:S(2)}) copy-start(f32[16,8,512]{2,1,0:T(8,128)S(1)} %fusion.6.refs_0_.refs_2_) | copy-start | bytes 786436
  10.8 13.0 %collective-permute-start.5 = (f32[1,8,512]{2,1,0:T(8,128)S(1)}, f32[1,8,512]{2,1,0:T(8,128)S(1)}, u32[]{:S(2)}, u32[]{:S(2)}) collective-permute-start(f32[1,8,512]{2,1,0:T(8,128)S(1)} %get-tuple-element.47), channel_id=1, source_target_pairs={{8,16},{16,8},{9,17},{17,9},{10,18},{18,10},{11,19},{19,11},{12,20... | collective-permute-start | bytes 49160 | tf_op jit(solution)/shard_map/ppermute | solution.py:30
  11.4 12.3 %collective-permute-start.4 = (f32[1,8,512]{2,1,0:T(8,128)S(1)}, f32[1,8,512]{2,1,0:T(8,128)S(1)}, u32[]{:S(2)}, u32[]{:S(2)}) collective-permute-start(f32[1,8,512]{2,1,0:T(8,128)S(1)} %get-tuple-element.48), channel_id=1, source_target_pairs={{0,8},{8,0},{16,24},{24,16},{1,9},{9,1},{17,25},{25,17},{2,10},{10... | collective-permute-start | bytes 49160 | tf_op jit(solution)/shard_map/ppermute | solution.py:29
  17.2 6.6 %collective-permute-start.7 = (f32[16,1,512]{2,1,0:T(1,128)S(1)}, f32[16,1,512]{2,1,0:T(1,128)S(1)}, u32[]{:S(2)}, u32[]{:S(2)}) collective-permute-start(f32[16,1,512]{2,1,0:T(1,128)S(1)} %get-tuple-element.43), channel_id=1, source_target_pairs={{1,2},{2,1},{3,4},{4,3},{5,6},{6,5},{9,10},{10,9},{11,12},{12,11},... | collective-permute-start | bytes 98312 | tf_op jit(solution)/shard_map/ppermute | solution.py:30
  17.9 6.8 %collective-permute-start.6 = (f32[16,1,512]{2,1,0:T(1,128)S(1)}, f32[16,1,512]{2,1,0:T(1,128)S(1)}, u32[]{:S(2)}, u32[]{:S(2)}) collective-permute-start(f32[16,1,512]{2,1,0:T(1,128)S(1)} %get-tuple-element.44), channel_id=1, source_target_pairs={{0,1},{1,0},{2,3},{3,2},{4,5},{5,4},{6,7},{7,6},{8,9},{9,8},{10,11... | collective-permute-start | bytes 98312 | tf_op jit(solution)/shard_map/ppermute | solution.py:29
  25.1 4.7 %copy-start = (f32[16,8,512]{2,1,0:T(8,128)}, f32[16,8,512]{2,1,0:T(8,128)S(1)}, u32[]{:S(2)}) copy-start(f32[16,8,512]{2,1,0:T(8,128)S(1)} %fusion.13.refs_1_.refs_3_) | copy-start | bytes 786436
  25.4 8.9 %collective-permute-start.9 = (f32[1,8,512]{2,1,0:T(8,128)S(1)}, f32[1,8,512]{2,1,0:T(8,128)S(1)}, u32[]{:S(2)}, u32[]{:S(2)}) collective-permute-start(f32[1,8,512]{2,1,0:T(8,128)S(1)} %get-tuple-element.37), channel_id=1, source_target_pairs={{8,16},{16,8},{9,17},{17,9},{10,18},{18,10},{11,19},{19,11},{12,20... | collective-permute-start | bytes 49160 | tf_op jit(solution)/shard_map/ppermute | solution.py:30
  26.0 8.2 %collective-permute-start.8 = (f32[1,8,512]{2,1,0:T(8,128)S(1)}, f32[1,8,512]{2,1,0:T(8,128)S(1)}, u32[]{:S(2)}, u32[]{:S(2)}) collective-permute-start(f32[1,8,512]{2,1,0:T(8,128)S(1)} %get-tuple-element.38), channel_id=1, source_target_pairs={{0,8},{8,0},{16,24},{24,16},{1,9},{9,1},{17,25},{25,17},{2,10},{10... | collective-permute-start | bytes 49160 | tf_op jit(solution)/shard_map/ppermute | solution.py:29
  29.9 4.4 %collective-permute-start.11 = (f32[16,1,512]{2,1,0:T(1,128)S(1)}, f32[16,1,512]{2,1,0:T(1,128)S(1)}, u32[]{:S(2)}, u32[]{:S(2)}) collective-permute-start(f32[16,1,512]{2,1,0:T(1,128)S(1)} %get-tuple-element.33), channel_id=1, source_target_pairs={{1,2},{2,1},{3,4},{4,3},{5,6},{6,5},{9,10},{10,9},{11,12},{12,11},... | collective-permute-start | bytes 98312 | tf_op jit(solution)/shard_map/ppermute | solution.py:30
  30.5 4.6 %collective-permute-start.10 = (f32[16,1,512]{2,1,0:T(1,128)S(1)}, f32[16,1,512]{2,1,0:T(1,128)S(1)}, u32[]{:S(2)}, u32[]{:S(2)}) collective-permute-start(f32[16,1,512]{2,1,0:T(1,128)S(1)} %get-tuple-element.34), channel_id=1, source_target_pairs={{0,1},{1,0},{2,3},{3,2},{4,5},{5,4},{6,7},{7,6},{8,9},{9,8},{10,11... | collective-permute-start | bytes 98312 | tf_op jit(solution)/shard_map/ppermute | solution.py:29
  35.6 3.1 %copy-start.1 = (f32[16,8,512]{2,1,0:T(8,128)}, f32[16,8,512]{2,1,0:T(8,128)S(1)}, u32[]{:S(2)}) copy-start(f32[16,8,512]{2,1,0:T(8,128)S(1)} %fusion.20.refs_2_.refs_4_) | copy-start | bytes 786436
  35.9 7.2 %collective-permute-start.13 = (f32[1,8,512]{2,1,0:T(8,128)S(1)}, f32[1,8,512]{2,1,0:T(8,128)S(1)}, u32[]{:S(2)}, u32[]{:S(2)}) collective-permute-start(f32[1,8,512]{2,1,0:T(8,128)S(1)} %get-tuple-element.27), channel_id=1, source_target_pairs={{8,16},{16,8},{9,17},{17,9},{10,18},{18,10},{11,19},{19,11},{12,20... | collective-permute-start | bytes 49160 | tf_op jit(solution)/shard_map/ppermute | solution.py:30
  36.5 6.5 %collective-permute-start.12 = (f32[1,8,512]{2,1,0:T(8,128)S(1)}, f32[1,8,512]{2,1,0:T(8,128)S(1)}, u32[]{:S(2)}, u32[]{:S(2)}) collective-permute-start(f32[1,8,512]{2,1,0:T(8,128)S(1)} %get-tuple-element.28), channel_id=1, source_target_pairs={{0,8},{8,0},{16,24},{24,16},{1,9},{9,1},{17,25},{25,17},{2,10},{10... | collective-permute-start | bytes 49160 | tf_op jit(solution)/shard_map/ppermute | solution.py:29
  38.7 4.4 %collective-permute-start.15 = (f32[16,1,512]{2,1,0:T(1,128)S(1)}, f32[16,1,512]{2,1,0:T(1,128)S(1)}, u32[]{:S(2)}, u32[]{:S(2)}) collective-permute-start(f32[16,1,512]{2,1,0:T(1,128)S(1)} %get-tuple-element.23), channel_id=1, source_target_pairs={{1,2},{2,1},{3,4},{4,3},{5,6},{6,5},{9,10},{10,9},{11,12},{12,11},... | collective-permute-start | bytes 98312 | tf_op jit(solution)/shard_map/ppermute | solution.py:30
  39.3 4.5 %collective-permute-start.14 = (f32[16,1,512]{2,1,0:T(1,128)S(1)}, f32[16,1,512]{2,1,0:T(1,128)S(1)}, u32[]{:S(2)}, u32[]{:S(2)}) collective-permute-start(f32[16,1,512]{2,1,0:T(1,128)S(1)} %get-tuple-element.24), channel_id=1, source_target_pairs={{0,1},{1,0},{2,3},{3,2},{4,5},{5,4},{6,7},{7,6},{8,9},{9,8},{10,11... | collective-permute-start | bytes 98312 | tf_op jit(solution)/shard_map/ppermute | solution.py:29
  44.3 4.5 %copy-start.2 = (f32[16,8,512]{2,1,0:T(8,128)}, f32[16,8,512]{2,1,0:T(8,128)S(1)}, u32[]{:S(2)}) copy-start(f32[16,8,512]{2,1,0:T(8,128)S(1)} %fusion.27.refs_3_.refs_5_) | copy-start | bytes 786436
  44.6 8.6 %collective-permute-start.17 = (f32[1,8,512]{2,1,0:T(8,128)S(1)}, f32[1,8,512]{2,1,0:T(8,128)S(1)}, u32[]{:S(2)}, u32[]{:S(2)}) collective-permute-start(f32[1,8,512]{2,1,0:T(8,128)S(1)} %get-tuple-element.17), channel_id=1, source_target_pairs={{8,16},{16,8},{9,17},{17,9},{10,18},{18,10},{11,19},{19,11},{12,20... | collective-permute-start | bytes 49160 | tf_op jit(solution)/shard_map/ppermute | solution.py:30
  45.3 8.0 %collective-permute-start.16 = (f32[1,8,512]{2,1,0:T(8,128)S(1)}, f32[1,8,512]{2,1,0:T(8,128)S(1)}, u32[]{:S(2)}, u32[]{:S(2)}) collective-permute-start(f32[1,8,512]{2,1,0:T(8,128)S(1)} %get-tuple-element.18), channel_id=1, source_target_pairs={{0,8},{8,0},{16,24},{24,16},{1,9},{9,1},{17,25},{25,17},{2,10},{10... | collective-permute-start | bytes 49160 | tf_op jit(solution)/shard_map/ppermute | solution.py:29
  48.9 4.4 %collective-permute-start.19 = (f32[16,1,512]{2,1,0:T(1,128)S(1)}, f32[16,1,512]{2,1,0:T(1,128)S(1)}, u32[]{:S(2)}, u32[]{:S(2)}) collective-permute-start(f32[16,1,512]{2,1,0:T(1,128)S(1)} %get-tuple-element.13), channel_id=1, source_target_pairs={{1,2},{2,1},{3,4},{4,3},{5,6},{6,5},{9,10},{10,9},{11,12},{12,11},... | collective-permute-start | bytes 98312 | tf_op jit(solution)/shard_map/ppermute | solution.py:30
  49.6 4.5 %collective-permute-start.18 = (f32[16,1,512]{2,1,0:T(1,128)S(1)}, f32[16,1,512]{2,1,0:T(1,128)S(1)}, u32[]{:S(2)}, u32[]{:S(2)}) collective-permute-start(f32[16,1,512]{2,1,0:T(1,128)S(1)} %get-tuple-element.14), channel_id=1, source_target_pairs={{0,1},{1,0},{2,3},{3,2},{4,5},{5,4},{6,7},{7,6},{8,9},{9,8},{10,11... | collective-permute-start | bytes 98312 | tf_op jit(solution)/shard_map/ppermute | solution.py:29
  57.5 1.6 %collective-permute-start.20 = (f32[1,128]{1,0:T(1,128)}, f32[1,128]{1,0:T(1,128)S(1)}, u32[]{:S(2)}, u32[]{:S(2)}) collective-permute-start(f32[1,128]{1,0:T(1,128)} %shard_map.85), channel_id=1, source_target_pairs={{0,1},{1,0},{2,3},{3,2},{4,5},{5,4},{6,7},{7,6},{8,9},{9,8},{10,11... | collective-permute-start | bytes 1544 | tf_op jit(solution)/shard_map/ppermute | solution.py:77
  59.8 3.5 %collective-permute-start.21 = (f32[1,128]{1,0:T(1,128)S(1)}, f32[1,128]{1,0:T(1,128)S(1)}, u32[]{:S(2)}, u32[]{:S(2)}) collective-permute-start(f32[1,128]{1,0:T(1,128)S(1)} %add.175), channel_id=1, source_target_pairs={{0,2},{1,3},{2,0},{3,1},{4,6},{5,7},{6,4},{7,5},{8,10},{9,11},{10,... | collective-permute-start | bytes 1544 | tf_op jit(solution)/shard_map/ppermute | solution.py:77
  63.3 4.5 %collective-permute-start.22 = (f32[1,128]{1,0:T(1,128)S(1)}, f32[1,128]{1,0:T(1,128)S(1)}, u32[]{:S(2)}, u32[]{:S(2)}) collective-permute-start(f32[1,128]{1,0:T(1,128)S(1)} %add.176), channel_id=1, source_target_pairs={{0,4},{1,5},{2,6},{3,7},{4,0},{5,1},{6,2},{7,3},{8,12},{9,13},{10,... | collective-permute-start | bytes 1544 | tf_op jit(solution)/shard_map/ppermute | solution.py:77
  67.8 3.5 %collective-permute-start.23 = (f32[1,128]{1,0:T(1,128)S(1)}, f32[1,128]{1,0:T(1,128)S(1)}, u32[]{:S(2)}, u32[]{:S(2)}) collective-permute-start(f32[1,128]{1,0:T(1,128)S(1)} %add.177), channel_id=1, source_target_pairs={{0,8},{8,0},{16,24},{24,16},{1,9},{9,1},{17,25},{25,17},{2,10},{10... | collective-permute-start | bytes 1544 | tf_op jit(solution)/shard_map/ppermute | solution.py:77
  71.3 3.5 %copy-start.10 = (f32[1,128]{1,0:T(1,128)}, f32[1,128]{1,0:T(1,128)S(1)}, u32[]{:S(2)}) copy-start(f32[1,128]{1,0:T(1,128)S(1)} %add.178.refs_0_) | copy-start | bytes 1540
  71.3 3.5 %collective-permute-start.24 = (f32[1,128]{1,0:T(1,128)S(1)}, f32[1,128]{1,0:T(1,128)S(1)}, u32[]{:S(2)}, u32[]{:S(2)}) collective-permute-start(f32[1,128]{1,0:T(1,128)S(1)} %add.178.refs_0_), channel_id=1, source_target_pairs={{0,16},{8,24},{16,0},{24,8},{1,17},{9,25},{17,1},{25,9},{2,18},{10... | collective-permute-start | bytes 1544 | tf_op jit(solution)/shard_map/ppermute | solution.py:77
  74.9 0.5 copy-start.11

commit v18 on v16

--- a/solution.py
+++ b/solution.py
@@ -117,7 +117,7 @@
     tile = (8, 128)
 
     def held(i):
-        return jnp.full(tile, stats_ref[0, i], jnp.float32)
+        return jnp.broadcast_to(stats_ref[:, i : i + 1], tile)
 
     per_cell = 1.0 / cells
     scale = jnp.sqrt(held(0) * per_cell + EPS)
@@ -184,7 +184,7 @@
             jax.ShapeDtypeStruct((size, size), jnp.float32),
             jax.ShapeDtypeStruct((1, 1), jnp.float32),
         ),
-        in_specs=[pl.BlockSpec(memory_space=pltpu.SMEM)] + [vmem] * size,
+        in_specs=[vmem] * (size + 1),
         out_specs=(vmem, vmem, vmem),
     )(stats, *basis)
     return ortho, upper, scale.reshape(())

time: 78.7 us -> 78.8 us (level)
  no operation moved by 1% of the time
where the time goes in v18:
time: 78.8 us; the launch traced here: 78.3 us
  starting transfers between devices  47.5 us (60%)
  waiting for transfers between devices  14.5 us (18%)
  local copies, waits for them, and re-layouts  5.32 us (7%)
  Pallas kernels  5.04 us (6%)
  other arithmetic  4.73 us (6%)
  between operations  1.2 us (2%)
    ppermute x10, starting transfers between devices, axis_exchange(): lax.ppermute(jnp.where(odd, to_low, to_high), axis, swap_pairs(axis, 0))  35.2 us
    ppermute x5, waiting for transfers between devices, all_sum(): x = x + lax.ppermute(x, axis, [(i, i ^ step) for i in range(n)])  11.1 us
    ppermute x10, starting transfers between devices, axis_exchange(): lax.ppermute(jnp.where(odd, to_high, to_low), axis, swap_pairs(axis, 1))  6.75 us
    ppermute x5, starting transfers between devices, all_sum(): x = x + lax.ppermute(x, axis, [(i, i ^ step) for i in range(n)])  5.55 us
    ppermute x10, waiting for transfers between devices, axis_exchange(): lax.ppermute(jnp.where(odd, to_low, to_high), axis, swap_pairs(axis, 0))  3.35 us
    pallas_call x1, Pallas kernels, finish(): pl.pallas_call(lambda *refs: finish_kernel(float(cells), size, *refs), ou...  2.81 us
    div x4, other arithmetic, local(): vector = 2.0 * total / diagonal  2.52 us
    pallas_call x1, Pallas kernels, gram(): pl.pallas_call(lambda *refs: gram_kernel(size, *refs), out_shape=jax.Shap...  2.23 us
  transfers between devices with their start and end apart: 25, of which 9 were waited for; matrix products, arithmetic and copies ran while one was open for 4% of the time, Pallas kernels for 0%

profile of v18, /device:TPU:0, one launch (start us, length us, event | category | flops | bytes accessed | tf_op | source)
XLA Modules:
  0.0 78.3 jit_solution(5677693519217444541)
XLA Ops:
  0.6 0.0 copy-start.4
  0.7 0.8 %fusion.54 = (f32[1,8,512]{2,1,0:T(8,128)S(1)}, f32[1,8,512]{2,1,0:T(8,128)S(1)}, f32[1,8,512]{2,1,0:T(8,128)S(1)}, f32[1,8,512]{2,1,0:T(8,128)S(1)}) fusion(f32[16,8,512]{2,1,0:T(8,128)} %param.6, f32[16,8,512]{2,1,0:T(8,128)} %param.9), kind=kLoop, calls=%fused_computation.119 | loop fusion | bytes 131072 | tf_op jit(solution)/shard_map/slice | solution.py:199
  1.5 3.0 %collective-permute-start.1 = (f32[2,8,512]{2,1,0:T(8,128)S(1)}, f32[2,8,512]{2,1,0:T(8,128)S(1)}, u32[]{:S(2)}, u32[]{:S(2)}) collective-permute-start(f32[2,8,512]{2,1,0:T(8,128)S(1)} %get-tuple-element.75), channel_id=1, source_target_pairs={{0,8},{8,0},{16,24},{24,16},{1,9},{9,1},{17,25},{25,17},{2,10},{10... | collective-permute-start | bytes 98312 | tf_op jit(solution)/shard_map/ppermute | solution.py:29
  4.5 0.7 collective-permute-start
  5.2 1.3 %fusion.51 = (f32[16,1,512]{2,1,0:T(1,128)S(1)}, f32[16,1,512]{2,1,0:T(1,128)S(1)}, f32[16,1,512]{2,1,0:T(1,128)S(1)}, f32[16,1,512]{2,1,0:T(1,128)S(1)}) fusion(f32[16,8,512]{2,1,0:T(8,128)} %param.6, f32[16,8,512]{2,1,0:T(8,128)} %param.10), kind=kLoop, calls=%fused_computation.116 | loop fusion | bytes 262144 | tf_op jit(solution)/shard_map/slice | solution.py:201
  6.5 0.1 broadcast_select_fusion.18
  6.6 0.1 collective-permute-start.3
  6.7 0.8 %collective-permute-start.2 = (f32[16,2,512]{2,1,0:T(2,128)S(1)}, f32[16,2,512]{2,1,0:T(2,128)S(1)}, u32[]{:S(2)}, u32[]{:S(2)}) collective-permute-start(f32[16,2,512]{2,1,0:T(2,128)S(1)} %get-tuple-element.64), channel_id=1, source_target_pairs={{1,2},{2,1},{3,4},{4,3},{5,6},{6,5},{9,10},{10,9},{11,12},{12,11},... | collective-permute-start | bytes 196616 | tf_op jit(solution)/shard_map/ppermute | solution.py:30
  7.5 1.1 %fusion.50 = (f32[16,7,512]{2,1,0:T(8,128)S(1)}, f32[16,7,512]{2,1,0:T(8,128)S(1)}) fusion(f32[16,8,512]{2,1,0:T(8,128)} %param.6), kind=kLoop, calls=%fused_computation.115 | loop fusion | bytes 917504 | tf_op jit(solution)/shard_map/slice | solution.py:49
  8.6 0.0 copy-start.5
  8.6 0.0 copy-start.7
  8.6 0.1 fusion.49
  8.7 0.1 fusion.53
  8.9 0.7 copy-done.5
  9.6 0.1 copy-done.7
  9.6 0.1 slice.201
  9.8 0.1 fusion.56
  10.0 0.5 fusion.6.refs_0_.refs_1_
  10.5 0.1 fusion.48
  10.6 0.1 fusion.46
  10.7 0.1 fusion.47
  10.8 0.7 collective-permute-start.5
  11.4 5.7 %collective-permute-start.4 = (f32[1,8,512]{2,1,0:T(8,128)S(1)}, f32[1,8,512]{2,1,0:T(8,128)S(1)}, u32[]{:S(2)}, u32[]{:S(2)}) collective-permute-start(f32[1,8,512]{2,1,0:T(8,128)S(1)} %get-tuple-element.48), channel_id=1, source_target_pairs={{0,8},{8,0},{16,24},{24,16},{1,9},{9,1},{17,25},{25,17},{2,10},{10... | collective-permute-start | bytes 49160 | tf_op jit(solution)/shard_map/ppermute | solution.py:29
  17.2 0.7 collective-permute-start.7
  17.9 5.9 %collective-permute-start.6 = (f32[16,1,512]{2,1,0:T(1,128)S(1)}, f32[16,1,512]{2,1,0:T(1,128)S(1)}, u32[]{:S(2)}, u32[]{:S(2)}) collective-permute-start(f32[16,1,512]{2,1,0:T(1,128)S(1)} %get-tuple-element.44), channel_id=1, source_target_pairs={{0,1},{1,0},{2,3},{3,2},{4,5},{5,4},{6,7},{7,6},{8,9},{9,8},{10,11... | collective-permute-start | bytes 98312 | tf_op jit(solution)/shard_map/ppermute | solution.py:29
  23.8 0.8 %collective-permute-done.6 = f32[16,1,512]{2,1,0:T(1,128)S(1)} collective-permute-done((f32[16,1,512]{2,1,0:T(1,128)S(1)}, f32[16,1,512]{2,1,0:T(1,128)S(1)}, u32[]{:S(2)}, u32[]{:S(2)}) %collective-permute-start.6) | collective-permute-done | bytes 32800 | tf_op jit(solution)/shard_map/ppermute | solution.py:29
  24.6 0.5 fusion.13.refs_1_.refs_2_
  25.1 0.1 fusion.43
  25.3 0.1 fusion.44
  25.4 0.7 collective-permute-start.9
  26.0 3.8 %collective-permute-start.8 = (f32[1,8,512]{2,1,0:T(8,128)S(1)}, f32[1,8,512]{2,1,0:T(8,128)S(1)}, u32[]{:S(2)}, u32[]{:S(2)}) collective-permute-start(f32[1,8,512]{2,1,0:T(8,128)S(1)} %get-tuple-element.38), channel_id=1, source_target_pairs={{0,8},{8,0},{16,24},{24,16},{1,9},{9,1},{17,25},{25,17},{2,10},{10... | collective-permute-start | bytes 49160 | tf_op jit(solution)/shard_map/ppermute | solution.py:29
  29.9 0.7 collective-permute-start.11
  30.5 3.7 %collective-permute-start.10 = (f32[16,1,512]{2,1,0:T(1,128)S(1)}, f32[16,1,512]{2,1,0:T(1,128)S(1)}, u32[]{:S(2)}, u32[]{:S(2)}) collective-permute-start(f32[16,1,512]{2,1,0:T(1,128)S(1)} %get-tuple-element.34), channel_id=1, source_target_pairs={{0,1},{1,0},{2,3},{3,2},{4,5},{5,4},{6,7},{7,6},{8,9},{9,8},{10,11... | collective-permute-start | bytes 98312 | tf_op jit(solution)/shard_map/ppermute | solution.py:29
  34.3 0.8 %collective-permute-done.10 = f32[16,1,512]{2,1,0:T(1,128)S(1)} collective-permute-done((f32[16,1,512]{2,1,0:T(1,128)S(1)}, f32[16,1,512]{2,1,0:T(1,128)S(1)}, u32[]{:S(2)}, u32[]{:S(2)}) %collective-permute-start.10) | collective-permute-done | bytes 32800 | tf_op jit(solution)/shard_map/ppermute | solution.py:29
  35.1 0.5 fusion.20.refs_2_.refs_3_
  35.6 0.1 fusion.40
  35.8 0.1 fusion.41
  35.9 0.7 collective-permute-start.13
  36.5 2.1 %collective-permute-start.12 = (f32[1,8,512]{2,1,0:T(8,128)S(1)}, f32[1,8,512]{2,1,0:T(8,128)S(1)}, u32[]{:S(2)}, u32[]{:S(2)}) collective-permute-start(f32[1,8,512]{2,1,0:T(8,128)S(1)} %get-tuple-element.28), channel_id=1, source_target_pairs={{0,8},{8,0},{16,24},{24,16},{1,9},{9,1},{17,25},{25,17},{2,10},{10... | collective-permute-start | bytes 49160 | tf_op jit(solution)/shard_map/ppermute | solution.py:29
  38.7 0.7 collective-permute-start.15
  39.3 3.7 %collective-permute-start.14 = (f32[16,1,512]{2,1,0:T(1,128)S(1)}, f32[16,1,512]{2,1,0:T(1,128)S(1)}, u32[]{:S(2)}, u32[]{:S(2)}) collective-permute-start(f32[16,1,512]{2,1,0:T(1,128)S(1)} %get-tuple-element.24), channel_id=1, source_target_pairs={{0,1},{1,0},{2,3},{3,2},{4,5},{5,4},{6,7},{7,6},{8,9},{9,8},{10,11... | collective-permute-start | bytes 98312 | tf_op jit(solution)/shard_map/ppermute | solution.py:29
  43.1 0.8 %collective-permute-done.14 = f32[16,1,512]{2,1,0:T(1,128)S(1)} collective-permute-done((f32[16,1,512]{2,1,0:T(1,128)S(1)}, f32[16,1,512]{2,1,0:T(1,128)S(1)}, u32[]{:S(2)}, u32[]{:S(2)}) %collective-permute-start.14) | collective-permute-done | bytes 32800 | tf_op jit(solution)/shard_map/ppermute | solution.py:29
  43.9 0.5 fusion.27.refs_3_.refs_4_
  44.4 0.1 fusion.37
  44.6 0.1 fusion.38
  44.6 0.7 collective-permute-start.17
  45.3 3.6 %collective-permute-start.16 = (f32[1,8,512]{2,1,0:T(8,128)S(1)}, f32[1,8,512]{2,1,0:T(8,128)S(1)}, u32[]{:S(2)}, u32[]{:S(2)}) collective-permute-start(f32[1,8,512]{2,1,0:T(8,128)S(1)} %get-tuple-element.18), channel_id=1, source_target_pairs={{0,8},{8,0},{16,24},{24,16},{1,9},{9,1},{17,25},{25,17},{2,10},{10... | collective-permute-start | bytes 49160 | tf_op jit(solution)/shard_map/ppermute | solution.py:29
  48.9 0.7 collective-permute-start.19
  49.6 3.7 %collective-permute-start.18 = (f32[16,1,512]{2,1,0:T(1,128)S(1)}, f32[16,1,512]{2,1,0:T(1,128)S(1)}, u32[]{:S(2)}, u32[]{:S(2)}) collective-permute-start(f32[16,1,512]{2,1,0:T(1,128)S(1)} %get-tuple-element.14), channel_id=1, source_target_pairs={{0,1},{1,0},{2,3},{3,2},{4,5},{5,4},{6,7},{7,6},{8,9},{9,8},{10,11... | collective-permute-start | bytes 98312 | tf_op jit(solution)/shard_map/ppermute | solution.py:29
  53.3 0.8 %collective-permute-done.18 = f32[16,1,512]{2,1,0:T(1,128)S(1)} collective-permute-done((f32[16,1,512]{2,1,0:T(1,128)S(1)}, f32[16,1,512]{2,1,0:T(1,128)S(1)}, u32[]{:S(2)}, u32[]{:S(2)}) %collective-permute-start.18) | collective-permute-done | bytes 32800 | tf_op jit(solution)/shard_map/ppermute | solution.py:29
  54.1 1.2 %fusion.34.refs_4_.refs_5_ = f32[16,8,512]{2,1,0:T(8,128)} fusion(f32[16,8,512]{2,1,0:T(8,128)S(1)} %copy-done.6, f32[15,8,512]{2,1,0:T(8,128)S(1)} %get-tuple-element.16, f32[1,8,512]{2,1,0:T(8,128)S(1)} %get-tuple-element.78, f32[1,8,512]{2,1,0:T(8,128)S(1)} %get-tuple-element.77, f32[15,8,512]{2,1,0:T(8,128)S(1)} %get-tuple-element.15, ...), kind=kLoop, calls=%fused_computation.53 | loop fusion | flops 1638400 | bytes 3668480 | tf_op jit(solution)/shard_map/div | solution.py:223
  55.3 2.2 %shard_map.85 = f32[1,128]{1,0:T(1,128)} custom-call(f32[16,8,512]{2,1,0:T(8,128)} %copy-done.3, f32[16,8,512]{2,1,0:T(8,128)} %copy-done, f32[16,8,512]{2,1,0:T(8,128)} %copy-done.1, f32[16,8,512]{2,1,0:T(8,128)} %copy-done.2, f32[16,8,512]{2,1,0:T(8,128)} %fusion.34.refs_4_.refs_5_), custom_call_target="tpu_custom_call" | custom-call | tf_op jit(solution)/shard_map/pallas_call | solution.py:107
  57.5 0.7 collective-permute-start.20
  58.2 1.0 %collective-permute-done.20 = f32[1,128]{1,0:T(1,128)S(1)} collective-permute-done((f32[1,128]{1,0:T(1,128)}, f32[1,128]{1,0:T(1,128)S(1)}, u32[]{:S(2)}, u32[]{:S(2)}) %collective-permute-start.20) | collective-permute-done | bytes 544 | tf_op jit(solution)/shard_map/ppermute | solution.py:70
  59.1 0.7 add.178
  59.8 1.9 %collective-permute-start.21 = (f32[1,128]{1,0:T(1,128)S(1)}, f32[1,128]{1,0:T(1,128)S(1)}, u32[]{:S(2)}, u32[]{:S(2)}) collective-permute-start(f32[1,128]{1,0:T(1,128)S(1)} %add.178), channel_id=1, source_target_pairs={{0,2},{1,3},{2,0},{3,1},{4,6},{5,7},{6,4},{7,5},{8,10},{9,11},{10,... | collective-permute-start | bytes 1544 | tf_op jit(solution)/shard_map/ppermute | solution.py:70
  61.7 1.6 %collective-permute-done.21 = f32[1,128]{1,0:T(1,128)S(1)} collective-permute-done((f32[1,128]{1,0:T(1,128)S(1)}, f32[1,128]{1,0:T(1,128)S(1)}, u32[]{:S(2)}, u32[]{:S(2)}) %collective-permute-start.21) | collective-permute-done | bytes 544 | tf_op jit(solution)/shard_map/ppermute | solution.py:70
  63.4 2.9 %collective-permute-start.22 = (f32[1,128]{1,0:T(1,128)S(1)}, f32[1,128]{1,0:T(1,128)S(1)}, u32[]{:S(2)}, u32[]{:S(2)}) collective-permute-start(f32[1,128]{1,0:T(1,128)S(1)} %add.179), channel_id=1, source_target_pairs={{0,4},{1,5},{2,6},{3,7},{4,0},{5,1},{6,2},{7,3},{8,12},{9,13},{10,... | collective-permute-start | bytes 1544 | tf_op jit(solution)/shard_map/ppermute | solution.py:70
  66.3 1.5 %collective-permute-done.22 = f32[1,128]{1,0:T(1,128)S(1)} collective-permute-done((f32[1,128]{1,0:T(1,128)S(1)}, f32[1,128]{1,0:T(1,128)S(1)}, u32[]{:S(2)}, u32[]{:S(2)}) %collective-permute-start.22) | collective-permute-done | bytes 544 | tf_op jit(solution)/shard_map/ppermute | solution.py:70
  67.8 0.0 collective-permute-start.23
  67.8 3.5 %collective-permute-done.23 = f32[1,128]{1,0:T(1,128)S(1)} collective-permute-done((f32[1,128]{1,0:T(1,128)S(1)}, f32[1,128]{1,0:T(1,128)S(1)}, u32[]{:S(2)}, u32[]{:S(2)}) %collective-permute-start.23) | collective-permute-done | bytes 544 | tf_op jit(solution)/shard_map/ppermute | solution.py:70
  71.4 3.5 %collective-permute-done.24 = f32[1,128]{1,0:T(1,128)S(1)} collective-permute-done((f32[1,128]{1,0:T(1,128)S(1)}, f32[1,128]{1,0:T(1,128)S(1)}, u32[]{:S(2)}, u32[]{:S(2)}) %collective-permute-start.24) | collective-permute-done | bytes 544 | tf_op jit(solution)/shard_map/ppermute | solution.py:70
  74.9 0.6 add.182.refs_0_
  75.5 2.8 %shard_map.86 = (f32[5,16,8,512]{3,2,1,0:T(8,128)}, f32[5,5]{1,0:T(8,128)}, f32[1,1]{1,0:T(1,128)}) custom-call(f32[1,128]{1,0:T(1,128)} %add.182.refs_0_, f32[16,8,512]{2,1,0:T(8,128)} %copy-done.3, f32[16,8,512]{2,1,0:T(8,128)} %copy-done, f32[16,8,512]{2,1,0:T(8,128)} %copy-done.1, f32[16,8,512]{2,1,0:T(8,128)} %copy-done.2, ...), custom_call_target="tpu_custom_call" | custom-call | tf_op jit(solution)/shard_map/pallas_call | solution.py:180
  (62 shorter events, 0.6 us)
Async XLA Ops:
  0.6 7.9 %copy-start.4 = (f32[16,8,512]{2,1,0:T(8,128)S(1)}, f32[16,8,512]{2,1,0:T(8,128)}, u32[]{:S(2)}) copy-start(f32[16,8,512]{2,1,0:T(8,128)} %param.6) | copy-start | bytes 786436
  1.5 8.3 %collective-permute-start.1 = (f32[2,8,512]{2,1,0:T(8,128)S(1)}, f32[2,8,512]{2,1,0:T(8,128)S(1)}, u32[]{:S(2)}, u32[]{:S(2)}) collective-permute-start(f32[2,8,512]{2,1,0:T(8,128)S(1)} %get-tuple-element.75), channel_id=1, source_target_pairs={{0,8},{8,0},{16,24},{24,16},{1,9},{9,1},{17,25},{25,17},{2,10},{10... | collective-permute-start | bytes 98312 | tf_op jit(solution)/shard_map/ppermute | solution.py:29
  4.5 5.3 %collective-permute-start = (f32[2,8,512]{2,1,0:T(8,128)S(1)}, f32[2,8,512]{2,1,0:T(8,128)S(1)}, u32[]{:S(2)}, u32[]{:S(2)}) collective-permute-start(f32[2,8,512]{2,1,0:T(8,128)S(1)} %get-tuple-element.76), channel_id=1, source_target_pairs={{8,16},{16,8},{9,17},{17,9},{10,18},{18,10},{11,19},{19,11},{12,20... | collective-permute-start | bytes 98312 | tf_op jit(solution)/shard_map/ppermute | solution.py:30
  6.6 3.2 %collective-permute-start.3 = (f32[16,2,512]{2,1,0:T(2,128)S(1)}, f32[16,2,512]{2,1,0:T(2,128)S(1)}, u32[]{:S(2)}, u32[]{:S(2)}) collective-permute-start(f32[16,2,512]{2,1,0:T(2,128)S(1)} %get-tuple-element.63), channel_id=1, source_target_pairs={{0,1},{1,0},{2,3},{3,2},{4,5},{5,4},{6,7},{7,6},{8,9},{9,8},{10,11... | collective-permute-start | bytes 196616 | tf_op jit(solution)/shard_map/ppermute | solution.py:29
  6.7 2.1 %copy-start.6 = (f32[16,8,512]{2,1,0:T(8,128)S(1)}, f32[16,8,512]{2,1,0:T(8,128)}, u32[]{:S(2)}) copy-start(f32[16,8,512]{2,1,0:T(8,128)} %param.9) | copy-start | bytes 786436
  6.7 3.1 %collective-permute-start.2 = (f32[16,2,512]{2,1,0:T(2,128)S(1)}, f32[16,2,512]{2,1,0:T(2,128)S(1)}, u32[]{:S(2)}, u32[]{:S(2)}) collective-permute-start(f32[16,2,512]{2,1,0:T(2,128)S(1)} %get-tuple-element.64), channel_id=1, source_target_pairs={{1,2},{2,1},{3,4},{4,3},{5,6},{6,5},{9,10},{10,9},{11,12},{12,11},... | collective-permute-start | bytes 196616 | tf_op jit(solution)/shard_map/ppermute | solution.py:30
  8.6 1.0 %copy-start.5 = (f32[16,8,512]{2,1,0:T(8,128)S(1)}, f32[16,8,512]{2,1,0:T(8,128)}, u32[]{:S(2)}) copy-start(f32[16,8,512]{2,1,0:T(8,128)} %param.10) | copy-start | bytes 786436
  8.6 1.0 %copy-start.7 = (f32[16,8,512]{2,1,0:T(8,128)S(1)}, f32[16,8,512]{2,1,0:T(8,128)}, u32[]{:S(2)}) copy-start(f32[16,8,512]{2,1,0:T(8,128)} %param.11) | copy-start | bytes 786436
  8.8 1.1 %copy-start.8 = (f32[16,8,512]{2,1,0:T(8,128)S(1)}, f32[16,8,512]{2,1,0:T(8,128)}, u32[]{:S(2)}) copy-start(f32[16,8,512]{2,1,0:T(8,128)} %param.8) | copy-start | bytes 786436
  8.8 1.1 %copy-start.9 = (f32[16,8,512]{2,1,0:T(8,128)S(1)}, f32[16,8,512]{2,1,0:T(8,128)}, u32[]{:S(2)}) copy-start(f32[16,8,512]{2,1,0:T(8,128)} %param.7) | copy-start | bytes 786436
  10.5 6.7 %copy-start.3 = (f32[16,8,512]{2,1,0:T(8,128)}, f32[16,8,512]{2,1,0:T(8,128)S(1)}, u32[]{:S(2)}) copy-start(f32[16,8,512]{2,1,0:T(8,128)S(1)} %fusion.6.refs_0_.refs_1_) | copy-start | bytes 786436
  10.8 13.0 %collective-permute-start.5 = (f32[1,8,512]{2,1,0:T(8,128)S(1)}, f32[1,8,512]{2,1,0:T(8,128)S(1)}, u32[]{:S(2)}, u32[]{:S(2)}) collective-permute-start(f32[1,8,512]{2,1,0:T(8,128)S(1)} %get-tuple-element.47), channel_id=1, source_target_pairs={{8,16},{16,8},{9,17},{17,9},{10,18},{18,10},{11,19},{19,11},{12,20... | collective-permute-start | bytes 49160 | tf_op jit(solution)/shard_map/ppermute | solution.py:30
  11.4 12.3 %collective-permute-start.4 = (f32[1,8,512]{2,1,0:T(8,128)S(1)}, f32[1,8,512]{2,1,0:T(8,128)S(1)}, u32[]{:S(2)}, u32[]{:S(2)}) collective-permute-start(f32[1,8,512]{2,1,0:T(8,128)S(1)} %get-tuple-element.48), channel_id=1, source_target_pairs={{0,8},{8,0},{16,24},{24,16},{1,9},{9,1},{17,25},{25,17},{2,10},{10... | collective-permute-start | bytes 49160 | tf_op jit(solution)/shard_map/ppermute | solution.py:29
  17.2 6.6 %collective-permute-start.7 = (f32[16,1,512]{2,1,0:T(1,128)S(1)}, f32[16,1,512]{2,1,0:T(1,128)S(1)}, u32[]{:S(2)}, u32[]{:S(2)}) collective-permute-start(f32[16,1,512]{2,1,0:T(1,128)S(1)} %get-tuple-element.43), channel_id=1, source_target_pairs={{1,2},{2,1},{3,4},{4,3},{5,6},{6,5},{9,10},{10,9},{11,12},{12,11},... | collective-permute-start | bytes 98312 | tf_op jit(solution)/shard_map/ppermute | solution.py:30
  17.9 6.8 %collective-permute-start.6 = (f32[16,1,512]{2,1,0:T(1,128)S(1)}, f32[16,1,512]{2,1,0:T(1,128)S(1)}, u32[]{:S(2)}, u32[]{:S(2)}) collective-permute-start(f32[16,1,512]{2,1,0:T(1,128)S(1)} %get-tuple-element.44), channel_id=1, source_target_pairs={{0,1},{1,0},{2,3},{3,2},{4,5},{5,4},{6,7},{7,6},{8,9},{9,8},{10,11... | collective-permute-start | bytes 98312 | tf_op jit(solution)/shard_map/ppermute | solution.py:29
  25.1 4.7 %copy-start = (f32[16,8,512]{2,1,0:T(8,128)}, f32[16,8,512]{2,1,0:T(8,128)S(1)}, u32[]{:S(2)}) copy-start(f32[16,8,512]{2,1,0:T(8,128)S(1)} %fusion.13.refs_1_.refs_2_) | copy-start | bytes 786436
  25.4 8.9 %collective-permute-start.9 = (f32[1,8,512]{2,1,0:T(8,128)S(1)}, f32[1,8,512]{2,1,0:T(8,128)S(1)}, u32[]{:S(2)}, u32[]{:S(2)}) collective-permute-start(f32[1,8,512]{2,1,0:T(8,128)S(1)} %get-tuple-element.37), channel_id=1, source_target_pairs={{8,16},{16,8},{9,17},{17,9},{10,18},{18,10},{11,19},{19,11},{12,20... | collective-permute-start | bytes 49160 | tf_op jit(solution)/shard_map/ppermute | solution.py:30
  26.0 8.2 %collective-permute-start.8 = (f32[1,8,512]{2,1,0:T(8,128)S(1)}, f32[1,8,512]{2,1,0:T(8,128)S(1)}, u32[]{:S(2)}, u32[]{:S(2)}) collective-permute-start(f32[1,8,512]{2,1,0:T(8,128)S(1)} %get-tuple-element.38), channel_id=1, source_target_pairs={{0,8},{8,0},{16,24},{24,16},{1,9},{9,1},{17,25},{25,17},{2,10},{10... | collective-permute-start | bytes 49160 | tf_op jit(solution)/shard_map/ppermute | solution.py:29
  29.9 4.4 %collective-permute-start.11 = (f32[16,1,512]{2,1,0:T(1,128)S(1)}, f32[16,1,512]{2,1,0:T(1,128)S(1)}, u32[]{:S(2)}, u32[]{:S(2)}) collective-permute-start(f32[16,1,512]{2,1,0:T(1,128)S(1)} %get-tuple-element.33), channel_id=1, source_target_pairs={{1,2},{2,1},{3,4},{4,3},{5,6},{6,5},{9,10},{10,9},{11,12},{12,11},... | collective-permute-start | bytes 98312 | tf_op jit(solution)/shard_map/ppermute | solution.py:30
  30.5 4.6 %collective-permute-start.10 = (f32[16,1,512]{2,1,0:T(1,128)S(1)}, f32[16,1,512]{2,1,0:T(1,128)S(1)}, u32[]{:S(2)}, u32[]{:S(2)}) collective-permute-start(f32[16,1,512]{2,1,0:T(1,128)S(1)} %get-tuple-element.34), channel_id=1, source_target_pairs={{0,1},{1,0},{2,3},{3,2},{4,5},{5,4},{6,7},{7,6},{8,9},{9,8},{10,11... | collective-permute-start | bytes 98312 | tf_op jit(solution)/shard_map/ppermute | solution.py:29
  35.6 3.1 %copy-start.1 = (f32[16,8,512]{2,1,0:T(8,128)}, f32[16,8,512]{2,1,0:T(8,128)S(1)}, u32[]{:S(2)}) copy-start(f32[16,8,512]{2,1,0:T(8,128)S(1)} %fusion.20.refs_2_.refs_3_) | copy-start | bytes 786436
  35.9 7.2 %collective-permute-start.13 = (f32[1,8,512]{2,1,0:T(8,128)S(1)}, f32[1,8,512]{2,1,0:T(8,128)S(1)}, u32[]{:S(2)}, u32[]{:S(2)}) collective-permute-start(f32[1,8,512]{2,1,0:T(8,128)S(1)} %get-tuple-element.27), channel_id=1, source_target_pairs={{8,16},{16,8},{9,17},{17,9},{10,18},{18,10},{11,19},{19,11},{12,20... | collective-permute-start | bytes 49160 | tf_op jit(solution)/shard_map/ppermute | solution.py:30
  36.5 6.5 %collective-permute-start.12 = (f32[1,8,512]{2,1,0:T(8,128)S(1)}, f32[1,8,512]{2,1,0:T(8,128)S(1)}, u32[]{:S(2)}, u32[]{:S(2)}) collective-permute-start(f32[1,8,512]{2,1,0:T(8,128)S(1)} %get-tuple-element.28), channel_id=1, source_target_pairs={{0,8},{8,0},{16,24},{24,16},{1,9},{9,1},{17,25},{25,17},{2,10},{10... | collective-permute-start | bytes 49160 | tf_op jit(solution)/shard_map/ppermute | solution.py:29
  38.7 4.4 %collective-permute-start.15 = (f32[16,1,512]{2,1,0:T(1,128)S(1)}, f32[16,1,512]{2,1,0:T(1,128)S(1)}, u32[]{:S(2)}, u32[]{:S(2)}) collective-permute-start(f32[16,1,512]{2,1,0:T(1,128)S(1)} %get-tuple-element.23), channel_id=1, source_target_pairs={{1,2},{2,1},{3,4},{4,3},{5,6},{6,5},{9,10},{10,9},{11,12},{12,11},... | collective-permute-start | bytes 98312 | tf_op jit(solution)/shard_map/ppermute | solution.py:30
  39.3 4.5 %collective-permute-start.14 = (f32[16,1,512]{2,1,0:T(1,128)S(1)}, f32[16,1,512]{2,1,0:T(1,128)S(1)}, u32[]{:S(2)}, u32[]{:S(2)}) collective-permute-start(f32[16,1,512]{2,1,0:T(1,128)S(1)} %get-tuple-element.24), channel_id=1, source_target_pairs={{0,1},{1,0},{2,3},{3,2},{4,5},{5,4},{6,7},{7,6},{8,9},{9,8},{10,11... | collective-permute-start | bytes 98312 | tf_op jit(solution)/shard_map/ppermute | solution.py:29
  44.3 4.5 %copy-start.2 = (f32[16,8,512]{2,1,0:T(8,128)}, f32[16,8,512]{2,1,0:T(8,128)S(1)}, u32[]{:S(2)}) copy-start(f32[16,8,512]{2,1,0:T(8,128)S(1)} %fusion.27.refs_3_.refs_4_) | copy-start | bytes 786436
  44.6 8.6 %collective-permute-start.17 = (f32[1,8,512]{2,1,0:T(8,128)S(1)}, f32[1,8,512]{2,1,0:T(8,128)S(1)}, u32[]{:S(2)}, u32[]{:S(2)}) collective-permute-start(f32[1,8,512]{2,1,0:T(8,128)S(1)} %get-tuple-element.17), channel_id=1, source_target_pairs={{8,16},{16,8},{9,17},{17,9},{10,18},{18,10},{11,19},{19,11},{12,20... | collective-permute-start | bytes 49160 | tf_op jit(solution)/shard_map/ppermute | solution.py:30
  45.3 8.0 %collective-permute-start.16 = (f32[1,8,512]{2,1,0:T(8,128)S(1)}, f32[1,8,512]{2,1,0:T(8,128)S(1)}, u32[]{:S(2)}, u32[]{:S(2)}) collective-permute-start(f32[1,8,512]{2,1,0:T(8,128)S(1)} %get-tuple-element.18), channel_id=1, source_target_pairs={{0,8},{8,0},{16,24},{24,16},{1,9},{9,1},{17,25},{25,17},{2,10},{10... | collective-permute-start | bytes 49160 | tf_op jit(solution)/shard_map/ppermute | solution.py:29
  48.9 4.4 %collective-permute-start.19 = (f32[16,1,512]{2,1,0:T(1,128)S(1)}, f32[16,1,512]{2,1,0:T(1,128)S(1)}, u32[]{:S(2)}, u32[]{:S(2)}) collective-permute-start(f32[16,1,512]{2,1,0:T(1,128)S(1)} %get-tuple-element.13), channel_id=1, source_target_pairs={{1,2},{2,1},{3,4},{4,3},{5,6},{6,5},{9,10},{10,9},{11,12},{12,11},... | collective-permute-start | bytes 98312 | tf_op jit(solution)/shard_map/ppermute | solution.py:30
  49.6 4.5 %collective-permute-start.18 = (f32[16,1,512]{2,1,0:T(1,128)S(1)}, f32[16,1,512]{2,1,0:T(1,128)S(1)}, u32[]{:S(2)}, u32[]{:S(2)}) collective-permute-start(f32[16,1,512]{2,1,0:T(1,128)S(1)} %get-tuple-element.14), channel_id=1, source_target_pairs={{0,1},{1,0},{2,3},{3,2},{4,5},{5,4},{6,7},{7,6},{8,9},{9,8},{10,11... | collective-permute-start | bytes 98312 | tf_op jit(solution)/shard_map/ppermute | solution.py:29
  57.5 1.6 %collective-permute-start.20 = (f32[1,128]{1,0:T(1,128)}, f32[1,128]{1,0:T(1,128)S(1)}, u32[]{:S(2)}, u32[]{:S(2)}) collective-permute-start(f32[1,128]{1,0:T(1,128)} %shard_map.85), channel_id=1, source_target_pairs={{0,1},{1,0},{2,3},{3,2},{4,5},{5,4},{6,7},{7,6},{8,9},{9,8},{10,11... | collective-permute-start | bytes 1544 | tf_op jit(solution)/shard_map/ppermute | solution.py:70
  59.8 3.5 %collective-permute-start.21 = (f32[1,128]{1,0:T(1,128)S(1)}, f32[1,128]{1,0:T(1,128)S(1)}, u32[]{:S(2)}, u32[]{:S(2)}) collective-permute-start(f32[1,128]{1,0:T(1,128)S(1)} %add.178), channel_id=1, source_target_pairs={{0,2},{1,3},{2,0},{3,1},{4,6},{5,7},{6,4},{7,5},{8,10},{9,11},{10,... | collective-permute-start | bytes 1544 | tf_op jit(solution)/shard_map/ppermute | solution.py:70
  63.4 4.5 %collective-permute-start.22 = (f32[1,128]{1,0:T(1,128)S(1)}, f32[1,128]{1,0:T(1,128)S(1)}, u32[]{:S(2)}, u32[]{:S(2)}) collective-permute-start(f32[1,128]{1,0:T(1,128)S(1)} %add.179), channel_id=1, source_target_pairs={{0,4},{1,5},{2,6},{3,7},{4,0},{5,1},{6,2},{7,3},{8,12},{9,13},{10,... | collective-permute-start | bytes 1544 | tf_op jit(solution)/shard_map/ppermute | solution.py:70
  67.8 3.5 %collective-permute-start.23 = (f32[1,128]{1,0:T(1,128)S(1)}, f32[1,128]{1,0:T(1,128)S(1)}, u32[]{:S(2)}, u32[]{:S(2)}) collective-permute-start(f32[1,128]{1,0:T(1,128)S(1)} %add.180), channel_id=1, source_target_pairs={{0,8},{8,0},{16,24},{24,16},{1,9},{9,1},{17,25},{25,17},{2,10},{10... | collective-permute-start | bytes 1544 | tf_op jit(solution)/shard_map/ppermute | solution.py:70
  71.4 3.5 %collective-permute-start.24 = (f32[1,128]{1,0:T(1,128)S(1)}, f32[1,128]{1,0:T(1,128)S(1)}, u32[]{:S(2)}, u32[]{:S(2)}) collective-permute-start(f32[1,128]{1,0:T(1,128)S(1)} %add.181), channel_id=1, source_target_pairs={{0,16},{8,24},{16,0},{24,8},{1,17},{9,25},{17,1},{25,9},{2,18},{10... | collective-permute-start | bytes 1544 | tf_op jit(solution)/shard_map/ppermute | solution.py:70

commit v19 on v17

--- a/solution.py
+++ b/solution.py
@@ -126,7 +126,7 @@
     tile = (8, 128)
 
     def held(i):
-        return jnp.full(tile, stats_ref[0, i], jnp.float32) + jnp.full(tile, other_ref[0, i], jnp.float32)
+        return jnp.broadcast_to(stats_ref[:, i : i + 1] + other_ref[:, i : i + 1], tile)
 
     per_cell = 1.0 / cells
     scale = jnp.sqrt(held(0) * per_cell + EPS)
@@ -193,7 +193,7 @@
             jax.ShapeDtypeStruct((size, size), jnp.float32),
             jax.ShapeDtypeStruct((1, 1), jnp.float32),
         ),
-        in_specs=[pl.BlockSpec(memory_space=pltpu.SMEM)] * 2 + [vmem] * size,
+        in_specs=[vmem] * (size + 2),
         out_specs=(vmem, vmem, vmem),
     )(*stats, *basis)
     return ortho, upper, scale.reshape(())

time: 78.7 us -> 78.8 us (level)
  no operation moved by 1% of the time
where the time goes in v19:
time: 78.8 us; the launch traced here: 78.3 us
  starting transfers between devices  47.5 us (60%)
  waiting for transfers between devices  14.5 us (18%)
  local copies, waits for them, and re-layouts  5.86 us (7%)
  Pallas kernels  5.05 us (6%)
  other arithmetic  4.13 us (5%)
  between operations  1.2 us (2%)
    ppermute x10, starting transfers between devices, axis_exchange(): lax.ppermute(jnp.where(odd, to_low, to_high), axis, swap_pairs(axis, 0))  35.2 us
    ppermute x5, waiting for transfers between devices, all_sum(): lax.ppermute(x, axis, [(i, i ^ step) for i in range(lax.axis_size(axis))])  11.1 us
    ppermute x10, starting transfers between devices, axis_exchange(): lax.ppermute(jnp.where(odd, to_high, to_low), axis, swap_pairs(axis, 1))  6.75 us
    ppermute x5, starting transfers between devices, all_sum(): lax.ppermute(x, axis, [(i, i ^ step) for i in range(lax.axis_size(axis))])  5.55 us
    ppermute x10, waiting for transfers between devices, axis_exchange(): lax.ppermute(jnp.where(odd, to_low, to_high), axis, swap_pairs(axis, 0))  3.35 us
    pallas_call x1, Pallas kernels, finish(): pl.pallas_call(lambda *refs: finish_kernel(float(cells), size, *refs), ou...  2.82 us
    div x4, other arithmetic, local(): vector = 2.0 * total / diagonal  2.51 us
    pallas_call x1, Pallas kernels, gram(): pl.pallas_call(lambda *refs: gram_kernel(size, *refs), out_shape=jax.Shap...  2.23 us
  transfers between devices with their start and end apart: 25, of which 9 were waited for; matrix products, arithmetic and copies ran while one was open for 4% of the time, Pallas kernels for 0%

profile of v19, /device:TPU:0, one launch (start us, length us, event | category | flops | bytes accessed | tf_op | source)
XLA Modules:
  0.0 78.3 jit_solution(16231620583678651220)
XLA Ops:
  0.6 0.0 copy-start.4
  0.7 0.8 %fusion.54 = (f32[1,8,512]{2,1,0:T(8,128)S(1)}, f32[1,8,512]{2,1,0:T(8,128)S(1)}, f32[1,8,512]{2,1,0:T(8,128)S(1)}, f32[1,8,512]{2,1,0:T(8,128)S(1)}) fusion(f32[16,8,512]{2,1,0:T(8,128)} %param.6, f32[16,8,512]{2,1,0:T(8,128)} %param.9), kind=kLoop, calls=%fused_computation.119 | loop fusion | bytes 131072 | tf_op jit(solution)/shard_map/slice | solution.py:208
  1.5 3.0 %collective-permute-start.1 = (f32[2,8,512]{2,1,0:T(8,128)S(1)}, f32[2,8,512]{2,1,0:T(8,128)S(1)}, u32[]{:S(2)}, u32[]{:S(2)}) collective-permute-start(f32[2,8,512]{2,1,0:T(8,128)S(1)} %get-tuple-element.75), channel_id=1, source_target_pairs={{0,8},{8,0},{16,24},{24,16},{1,9},{9,1},{17,25},{25,17},{2,10},{10... | collective-permute-start | bytes 98312 | tf_op jit(solution)/shard_map/ppermute | solution.py:29
  4.5 0.7 collective-permute-start
  5.2 1.3 %fusion.51 = (f32[16,1,512]{2,1,0:T(1,128)S(1)}, f32[16,1,512]{2,1,0:T(1,128)S(1)}, f32[16,1,512]{2,1,0:T(1,128)S(1)}, f32[16,1,512]{2,1,0:T(1,128)S(1)}) fusion(f32[16,8,512]{2,1,0:T(8,128)} %param.6, f32[16,8,512]{2,1,0:T(8,128)} %param.10), kind=kLoop, calls=%fused_computation.116 | loop fusion | bytes 262144 | tf_op jit(solution)/shard_map/slice | solution.py:210
  6.5 0.1 broadcast_select_fusion.18
  6.6 0.1 collective-permute-start.3
  6.7 0.8 %collective-permute-start.2 = (f32[16,2,512]{2,1,0:T(2,128)S(1)}, f32[16,2,512]{2,1,0:T(2,128)S(1)}, u32[]{:S(2)}, u32[]{:S(2)}) collective-permute-start(f32[16,2,512]{2,1,0:T(2,128)S(1)} %get-tuple-element.64), channel_id=1, source_target_pairs={{1,2},{2,1},{3,4},{4,3},{5,6},{6,5},{9,10},{10,9},{11,12},{12,11},... | collective-permute-start | bytes 196616 | tf_op jit(solution)/shard_map/ppermute | solution.py:30
  7.5 1.1 %fusion.50 = (f32[16,7,512]{2,1,0:T(8,128)S(1)}, f32[16,7,512]{2,1,0:T(8,128)S(1)}) fusion(f32[16,8,512]{2,1,0:T(8,128)} %param.6), kind=kLoop, calls=%fused_computation.115 | loop fusion | bytes 917504 | tf_op jit(solution)/shard_map/slice | solution.py:49
  8.6 0.0 copy-start.5
  8.6 0.0 copy-start.7
  8.6 0.1 fusion.49
  8.7 0.1 fusion.53
  8.9 0.7 copy-done.5
  9.6 0.1 copy-done.7
  9.6 0.1 slice.201
  9.8 0.1 fusion.56
  10.0 0.5 fusion.6.refs_0_.refs_2_
  10.5 0.1 fusion.48
  10.6 0.1 fusion.46
  10.7 0.1 fusion.47
  10.8 0.7 collective-permute-start.5
  11.4 5.7 %collective-permute-start.4 = (f32[1,8,512]{2,1,0:T(8,128)S(1)}, f32[1,8,512]{2,1,0:T(8,128)S(1)}, u32[]{:S(2)}, u32[]{:S(2)}) collective-permute-start(f32[1,8,512]{2,1,0:T(8,128)S(1)} %get-tuple-element.48), channel_id=1, source_target_pairs={{0,8},{8,0},{16,24},{24,16},{1,9},{9,1},{17,25},{25,17},{2,10},{10... | collective-permute-start | bytes 49160 | tf_op jit(solution)/shard_map/ppermute | solution.py:29
  17.2 0.7 collective-permute-start.7
  17.9 5.9 %collective-permute-start.6 = (f32[16,1,512]{2,1,0:T(1,128)S(1)}, f32[16,1,512]{2,1,0:T(1,128)S(1)}, u32[]{:S(2)}, u32[]{:S(2)}) collective-permute-start(f32[16,1,512]{2,1,0:T(1,128)S(1)} %get-tuple-element.44), channel_id=1, source_target_pairs={{0,1},{1,0},{2,3},{3,2},{4,5},{5,4},{6,7},{7,6},{8,9},{9,8},{10,11... | collective-permute-start | bytes 98312 | tf_op jit(solution)/shard_map/ppermute | solution.py:29
  23.8 0.8 %collective-permute-done.6 = f32[16,1,512]{2,1,0:T(1,128)S(1)} collective-permute-done((f32[16,1,512]{2,1,0:T(1,128)S(1)}, f32[16,1,512]{2,1,0:T(1,128)S(1)}, u32[]{:S(2)}, u32[]{:S(2)}) %collective-permute-start.6) | collective-permute-done | bytes 32800 | tf_op jit(solution)/shard_map/ppermute | solution.py:29
  24.6 0.5 fusion.13.refs_1_.refs_3_
  25.1 0.1 fusion.43
  25.3 0.1 fusion.44
  25.4 0.7 collective-permute-start.9
  26.0 3.8 %collective-permute-start.8 = (f32[1,8,512]{2,1,0:T(8,128)S(1)}, f32[1,8,512]{2,1,0:T(8,128)S(1)}, u32[]{:S(2)}, u32[]{:S(2)}) collective-permute-start(f32[1,8,512]{2,1,0:T(8,128)S(1)} %get-tuple-element.38), channel_id=1, source_target_pairs={{0,8},{8,0},{16,24},{24,16},{1,9},{9,1},{17,25},{25,17},{2,10},{10... | collective-permute-start | bytes 49160 | tf_op jit(solution)/shard_map/ppermute | solution.py:29
  29.9 0.7 collective-permute-start.11
  30.5 3.7 %collective-permute-start.10 = (f32[16,1,512]{2,1,0:T(1,128)S(1)}, f32[16,1,512]{2,1,0:T(1,128)S(1)}, u32[]{:S(2)}, u32[]{:S(2)}) collective-permute-start(f32[16,1,512]{2,1,0:T(1,128)S(1)} %get-tuple-element.34), channel_id=1, source_target_pairs={{0,1},{1,0},{2,3},{3,2},{4,5},{5,4},{6,7},{7,6},{8,9},{9,8},{10,11... | collective-permute-start | bytes 98312 | tf_op jit(solution)/shard_map/ppermute | solution.py:29
  34.3 0.8 %collective-permute-done.10 = f32[16,1,512]{2,1,0:T(1,128)S(1)} collective-permute-done((f32[16,1,512]{2,1,0:T(1,128)S(1)}, f32[16,1,512]{2,1,0:T(1,128)S(1)}, u32[]{:S(2)}, u32[]{:S(2)}) %collective-permute-start.10) | collective-permute-done | bytes 32800 | tf_op jit(solution)/shard_map/ppermute | solution.py:29
  35.1 0.5 fusion.20.refs_2_.refs_4_
  35.6 0.1 fusion.40
  35.8 0.1 fusion.41
  35.9 0.7 collective-permute-start.13
  36.5 2.1 %collective-permute-start.12 = (f32[1,8,512]{2,1,0:T(8,128)S(1)}, f32[1,8,512]{2,1,0:T(8,128)S(1)}, u32[]{:S(2)}, u32[]{:S(2)}) collective-permute-start(f32[1,8,512]{2,1,0:T(8,128)S(1)} %get-tuple-element.28), channel_id=1, source_target_pairs={{0,8},{8,0},{16,24},{24,16},{1,9},{9,1},{17,25},{25,17},{2,10},{10... | collective-permute-start | bytes 49160 | tf_op jit(solution)/shard_map/ppermute | solution.py:29
  38.7 0.7 collective-permute-start.15
  39.3 3.7 %collective-permute-start.14 = (f32[16,1,512]{2,1,0:T(1,128)S(1)}, f32[16,1,512]{2,1,0:T(1,128)S(1)}, u32[]{:S(2)}, u32[]{:S(2)}) collective-permute-start(f32[16,1,512]{2,1,0:T(1,128)S(1)} %get-tuple-element.24), channel_id=1, source_target_pairs={{0,1},{1,0},{2,3},{3,2},{4,5},{5,4},{6,7},{7,6},{8,9},{9,8},{10,11... | collective-permute-start | bytes 98312 | tf_op jit(solution)/shard_map/ppermute | solution.py:29
  43.1 0.8 %collective-permute-done.14 = f32[16,1,512]{2,1,0:T(1,128)S(1)} collective-permute-done((f32[16,1,512]{2,1,0:T(1,128)S(1)}, f32[16,1,512]{2,1,0:T(1,128)S(1)}, u32[]{:S(2)}, u32[]{:S(2)}) %collective-permute-start.14) | collective-permute-done | bytes 32800 | tf_op jit(solution)/shard_map/ppermute | solution.py:29
  43.9 0.5 fusion.27.refs_3_.refs_5_
  44.4 0.1 fusion.37
  44.6 0.1 fusion.38
  44.6 0.7 collective-permute-start.17
  45.3 3.6 %collective-permute-start.16 = (f32[1,8,512]{2,1,0:T(8,128)S(1)}, f32[1,8,512]{2,1,0:T(8,128)S(1)}, u32[]{:S(2)}, u32[]{:S(2)}) collective-permute-start(f32[1,8,512]{2,1,0:T(8,128)S(1)} %get-tuple-element.18), channel_id=1, source_target_pairs={{0,8},{8,0},{16,24},{24,16},{1,9},{9,1},{17,25},{25,17},{2,10},{10... | collective-permute-start | bytes 49160 | tf_op jit(solution)/shard_map/ppermute | solution.py:29
  48.9 0.7 collective-permute-start.19
  49.6 3.7 %collective-permute-start.18 = (f32[16,1,512]{2,1,0:T(1,128)S(1)}, f32[16,1,512]{2,1,0:T(1,128)S(1)}, u32[]{:S(2)}, u32[]{:S(2)}) collective-permute-start(f32[16,1,512]{2,1,0:T(1,128)S(1)} %get-tuple-element.14), channel_id=1, source_target_pairs={{0,1},{1,0},{2,3},{3,2},{4,5},{5,4},{6,7},{7,6},{8,9},{9,8},{10,11... | collective-permute-start | bytes 98312 | tf_op jit(solution)/shard_map/ppermute | solution.py:29
  53.3 0.8 %collective-permute-done.18 = f32[16,1,512]{2,1,0:T(1,128)S(1)} collective-permute-done((f32[16,1,512]{2,1,0:T(1,128)S(1)}, f32[16,1,512]{2,1,0:T(1,128)S(1)}, u32[]{:S(2)}, u32[]{:S(2)}) %collective-permute-start.18) | collective-permute-done | bytes 32800 | tf_op jit(solution)/shard_map/ppermute | solution.py:29
  54.1 1.2 %fusion.34.refs_4_.refs_6_ = f32[16,8,512]{2,1,0:T(8,128)} fusion(f32[16,8,512]{2,1,0:T(8,128)S(1)} %copy-done.6, f32[15,8,512]{2,1,0:T(8,128)S(1)} %get-tuple-element.16, f32[1,8,512]{2,1,0:T(8,128)S(1)} %get-tuple-element.78, f32[1,8,512]{2,1,0:T(8,128)S(1)} %get-tuple-element.77, f32[15,8,512]{2,1,0:T(8,128)S(1)} %get-tuple-element.15, ...), kind=kLoop, calls=%fused_computation.53 | loop fusion | flops 1638400 | bytes 3668480 | tf_op jit(solution)/shard_map/div | solution.py:232
  55.3 2.2 %shard_map.85 = f32[1,128]{1,0:T(1,128)} custom-call(f32[16,8,512]{2,1,0:T(8,128)} %copy-done.3, f32[16,8,512]{2,1,0:T(8,128)} %copy-done, f32[16,8,512]{2,1,0:T(8,128)} %copy-done.1, f32[16,8,512]{2,1,0:T(8,128)} %copy-done.2, f32[16,8,512]{2,1,0:T(8,128)} %fusion.34.refs_4_.refs_6_), custom_call_target="tpu_custom_call" | custom-call | tf_op jit(solution)/shard_map/pallas_call | solution.py:116
  57.5 0.7 collective-permute-start.20
  58.2 1.0 %collective-permute-done.20 = f32[1,128]{1,0:T(1,128)S(1)} collective-permute-done((f32[1,128]{1,0:T(1,128)}, f32[1,128]{1,0:T(1,128)S(1)}, u32[]{:S(2)}, u32[]{:S(2)}) %collective-permute-start.20) | collective-permute-done | bytes 544 | tf_op jit(solution)/shard_map/ppermute | solution.py:77
  59.1 0.7 add.175
  59.8 1.9 %collective-permute-start.21 = (f32[1,128]{1,0:T(1,128)S(1)}, f32[1,128]{1,0:T(1,128)S(1)}, u32[]{:S(2)}, u32[]{:S(2)}) collective-permute-start(f32[1,128]{1,0:T(1,128)S(1)} %add.175), channel_id=1, source_target_pairs={{0,2},{1,3},{2,0},{3,1},{4,6},{5,7},{6,4},{7,5},{8,10},{9,11},{10,... | collective-permute-start | bytes 1544 | tf_op jit(solution)/shard_map/ppermute | solution.py:77
  61.7 1.6 %collective-permute-done.21 = f32[1,128]{1,0:T(1,128)S(1)} collective-permute-done((f32[1,128]{1,0:T(1,128)S(1)}, f32[1,128]{1,0:T(1,128)S(1)}, u32[]{:S(2)}, u32[]{:S(2)}) %collective-permute-start.21) | collective-permute-done | bytes 544 | tf_op jit(solution)/shard_map/ppermute | solution.py:77
  63.3 2.9 %collective-permute-start.22 = (f32[1,128]{1,0:T(1,128)S(1)}, f32[1,128]{1,0:T(1,128)S(1)}, u32[]{:S(2)}, u32[]{:S(2)}) collective-permute-start(f32[1,128]{1,0:T(1,128)S(1)} %add.176), channel_id=1, source_target_pairs={{0,4},{1,5},{2,6},{3,7},{4,0},{5,1},{6,2},{7,3},{8,12},{9,13},{10,... | collective-permute-start | bytes 1544 | tf_op jit(solution)/shard_map/ppermute | solution.py:77
  66.3 1.5 %collective-permute-done.22 = f32[1,128]{1,0:T(1,128)S(1)} collective-permute-done((f32[1,128]{1,0:T(1,128)S(1)}, f32[1,128]{1,0:T(1,128)S(1)}, u32[]{:S(2)}, u32[]{:S(2)}) %collective-permute-start.22) | collective-permute-done | bytes 544 | tf_op jit(solution)/shard_map/ppermute | solution.py:77
  67.8 0.0 collective-permute-start.23
  67.8 3.5 %collective-permute-done.23 = f32[1,128]{1,0:T(1,128)S(1)} collective-permute-done((f32[1,128]{1,0:T(1,128)S(1)}, f32[1,128]{1,0:T(1,128)S(1)}, u32[]{:S(2)}, u32[]{:S(2)}) %collective-permute-start.23) | collective-permute-done | bytes 544 | tf_op jit(solution)/shard_map/ppermute | solution.py:77
  71.4 3.5 %collective-permute-done.24.refs_1_ = f32[1,128]{1,0:T(1,128)S(1)} collective-permute-done((f32[1,128]{1,0:T(1,128)S(1)}, f32[1,128]{1,0:T(1,128)S(1)}, u32[]{:S(2)}, u32[]{:S(2)}) %collective-permute-start.24) | collective-permute-done | bytes 544 | tf_op jit(solution)/shard_map/ppermute | solution.py:77
  74.9 0.5 copy-done.11
  75.4 2.8 %shard_map.86 = (f32[5,16,8,512]{3,2,1,0:T(8,128)}, f32[5,5]{1,0:T(8,128)}, f32[1,1]{1,0:T(1,128)}) custom-call(f32[1,128]{1,0:T(1,128)} %copy-done.10, f32[1,128]{1,0:T(1,128)} %copy-done.11, f32[16,8,512]{2,1,0:T(8,128)} %copy-done.3, f32[16,8,512]{2,1,0:T(8,128)} %copy-done, f32[16,8,512]{2,1,0:T(8,128)} %copy-done.1, f32[16,8,512]{2,1,0:T(8,128)} %copy-done.2, ...), custom_call_target="tpu_custom_call" | custom-call | tf_op jit(solution)/shard_map/pallas_call | solution.py:189
  (65 shorter events, 0.6 us)
Async XLA Ops:
  0.6 7.9 %copy-start.4 = (f32[16,8,512]{2,1,0:T(8,128)S(1)}, f32[16,8,512]{2,1,0:T(8,128)}, u32[]{:S(2)}) copy-start(f32[16,8,512]{2,1,0:T(8,128)} %param.6) | copy-start | bytes 786436
  1.5 8.3 %collective-permute-start.1 = (f32[2,8,512]{2,1,0:T(8,128)S(1)}, f32[2,8,512]{2,1,0:T(8,128)S(1)}, u32[]{:S(2)}, u32[]{:S(2)}) collective-permute-start(f32[2,8,512]{2,1,0:T(8,128)S(1)} %get-tuple-element.75), channel_id=1, source_target_pairs={{0,8},{8,0},{16,24},{24,16},{1,9},{9,1},{17,25},{25,17},{2,10},{10... | collective-permute-start | bytes 98312 | tf_op jit(solution)/shard_map/ppermute | solution.py:29
  4.5 5.3 %collective-permute-start = (f32[2,8,512]{2,1,0:T(8,128)S(1)}, f32[2,8,512]{2,1,0:T(8,128)S(1)}, u32[]{:S(2)}, u32[]{:S(2)}) collective-permute-start(f32[2,8,512]{2,1,0:T(8,128)S(1)} %get-tuple-element.76), channel_id=1, source_target_pairs={{8,16},{16,8},{9,17},{17,9},{10,18},{18,10},{11,19},{19,11},{12,20... | collective-permute-start | bytes 98312 | tf_op jit(solution)/shard_map/ppermute | solution.py:30
  6.6 3.2 %collective-permute-start.3 = (f32[16,2,512]{2,1,0:T(2,128)S(1)}, f32[16,2,512]{2,1,0:T(2,128)S(1)}, u32[]{:S(2)}, u32[]{:S(2)}) collective-permute-start(f32[16,2,512]{2,1,0:T(2,128)S(1)} %get-tuple-element.63), channel_id=1, source_target_pairs={{0,1},{1,0},{2,3},{3,2},{4,5},{5,4},{6,7},{7,6},{8,9},{9,8},{10,11... | collective-permute-start | bytes 196616 | tf_op jit(solution)/shard_map/ppermute | solution.py:29
  6.7 2.1 %copy-start.6 = (f32[16,8,512]{2,1,0:T(8,128)S(1)}, f32[16,8,512]{2,1,0:T(8,128)}, u32[]{:S(2)}) copy-start(f32[16,8,512]{2,1,0:T(8,128)} %param.9) | copy-start | bytes 786436
  6.7 3.1 %collective-permute-start.2 = (f32[16,2,512]{2,1,0:T(2,128)S(1)}, f32[16,2,512]{2,1,0:T(2,128)S(1)}, u32[]{:S(2)}, u32[]{:S(2)}) collective-permute-start(f32[16,2,512]{2,1,0:T(2,128)S(1)} %get-tuple-element.64), channel_id=1, source_target_pairs={{1,2},{2,1},{3,4},{4,3},{5,6},{6,5},{9,10},{10,9},{11,12},{12,11},... | collective-permute-start | bytes 196616 | tf_op jit(solution)/shard_map/ppermute | solution.py:30
  8.6 1.0 %copy-start.5 = (f32[16,8,512]{2,1,0:T(8,128)S(1)}, f32[16,8,512]{2,1,0:T(8,128)}, u32[]{:S(2)}) copy-start(f32[16,8,512]{2,1,0:T(8,128)} %param.10) | copy-start | bytes 786436
  8.6 1.0 %copy-start.7 = (f32[16,8,512]{2,1,0:T(8,128)S(1)}, f32[16,8,512]{2,1,0:T(8,128)}, u32[]{:S(2)}) copy-start(f32[16,8,512]{2,1,0:T(8,128)} %param.11) | copy-start | bytes 786436
  8.8 1.1 %copy-start.8 = (f32[16,8,512]{2,1,0:T(8,128)S(1)}, f32[16,8,512]{2,1,0:T(8,128)}, u32[]{:S(2)}) copy-start(f32[16,8,512]{2,1,0:T(8,128)} %param.8) | copy-start | bytes 786436
  8.8 1.1 %copy-start.9 = (f32[16,8,512]{2,1,0:T(8,128)S(1)}, f32[16,8,512]{2,1,0:T(8,128)}, u32[]{:S(2)}) copy-start(f32[16,8,512]{2,1,0:T(8,128)} %param.7) | copy-start | bytes 786436
  10.5 6.7 %copy-start.3 = (f32[16,8,512]{2,1,0:T(8,128)}, f32[16,8,512]{2,1,0:T(8,128)S(1)}, u32[]{:S(2)}) copy-start(f32[16,8,512]{2,1,0:T(8,128)S(1)} %fusion.6.refs_0_.refs_2_) | copy-start | bytes 786436
  10.8 13.0 %collective-permute-start.5 = (f32[1,8,512]{2,1,0:T(8,128)S(1)}, f32[1,8,512]{2,1,0:T(8,128)S(1)}, u32[]{:S(2)}, u32[]{:S(2)}) collective-permute-start(f32[1,8,512]{2,1,0:T(8,128)S(1)} %get-tuple-element.47), channel_id=1, source_target_pairs={{8,16},{16,8},{9,17},{17,9},{10,18},{18,10},{11,19},{19,11},{12,20... | collective-permute-start | bytes 49160 | tf_op jit(solution)/shard_map/ppermute | solution.py:30
  11.4 12.3 %collective-permute-start.4 = (f32[1,8,512]{2,1,0:T(8,128)S(1)}, f32[1,8,512]{2,1,0:T(8,128)S(1)}, u32[]{:S(2)}, u32[]{:S(2)}) collective-permute-start(f32[1,8,512]{2,1,0:T(8,128)S(1)} %get-tuple-element.48), channel_id=1, source_target_pairs={{0,8},{8,0},{16,24},{24,16},{1,9},{9,1},{17,25},{25,17},{2,10},{10... | collective-permute-start | bytes 49160 | tf_op jit(solution)/shard_map/ppermute | solution.py:29
  17.2 6.6 %collective-permute-start.7 = (f32[16,1,512]{2,1,0:T(1,128)S(1)}, f32[16,1,512]{2,1,0:T(1,128)S(1)}, u32[]{:S(2)}, u32[]{:S(2)}) collective-permute-start(f32[16,1,512]{2,1,0:T(1,128)S(1)} %get-tuple-element.43), channel_id=1, source_target_pairs={{1,2},{2,1},{3,4},{4,3},{5,6},{6,5},{9,10},{10,9},{11,12},{12,11},... | collective-permute-start | bytes 98312 | tf_op jit(solution)/shard_map/ppermute | solution.py:30
  17.9 6.8 %collective-permute-start.6 = (f32[16,1,512]{2,1,0:T(1,128)S(1)}, f32[16,1,512]{2,1,0:T(1,128)S(1)}, u32[]{:S(2)}, u32[]{:S(2)}) collective-permute-start(f32[16,1,512]{2,1,0:T(1,128)S(1)} %get-tuple-element.44), channel_id=1, source_target_pairs={{0,1},{1,0},{2,3},{3,2},{4,5},{5,4},{6,7},{7,6},{8,9},{9,8},{10,11... | collective-permute-start | bytes 98312 | tf_op jit(solution)/shard_map/ppermute | solution.py:29
  25.1 4.7 %copy-start = (f32[16,8,512]{2,1,0:T(8,128)}, f32[16,8,512]{2,1,0:T(8,128)S(1)}, u32[]{:S(2)}) copy-start(f32[16,8,512]{2,1,0:T(8,128)S(1)} %fusion.13.refs_1_.refs_3_) | copy-start | bytes 786436
  25.4 8.9 %collective-permute-start.9 = (f32[1,8,512]{2,1,0:T(8,128)S(1)}, f32[1,8,512]{2,1,0:T(8,128)S(1)}, u32[]{:S(2)}, u32[]{:S(2)}) collective-permute-start(f32[1,8,512]{2,1,0:T(8,128)S(1)} %get-tuple-element.37), channel_id=1, source_target_pairs={{8,16},{16,8},{9,17},{17,9},{10,18},{18,10},{11,19},{19,11},{12,20... | collective-permute-start | bytes 49160 | tf_op jit(solution)/shard_map/ppermute | solution.py:30
  26.0 8.2 %collective-permute-start.8 = (f32[1,8,512]{2,1,0:T(8,128)S(1)}, f32[1,8,512]{2,1,0:T(8,128)S(1)}, u32[]{:S(2)}, u32[]{:S(2)}) collective-permute-start(f32[1,8,512]{2,1,0:T(8,128)S(1)} %get-tuple-element.38), channel_id=1, source_target_pairs={{0,8},{8,0},{16,24},{24,16},{1,9},{9,1},{17,25},{25,17},{2,10},{10... | collective-permute-start | bytes 49160 | tf_op jit(solution)/shard_map/ppermute | solution.py:29
  29.9 4.4 %collective-permute-start.11 = (f32[16,1,512]{2,1,0:T(1,128)S(1)}, f32[16,1,512]{2,1,0:T(1,128)S(1)}, u32[]{:S(2)}, u32[]{:S(2)}) collective-permute-start(f32[16,1,512]{2,1,0:T(1,128)S(1)} %get-tuple-element.33), channel_id=1, source_target_pairs={{1,2},{2,1},{3,4},{4,3},{5,6},{6,5},{9,10},{10,9},{11,12},{12,11},... | collective-permute-start | bytes 98312 | tf_op jit(solution)/shard_map/ppermute | solution.py:30
  30.5 4.6 %collective-permute-start.10 = (f32[16,1,512]{2,1,0:T(1,128)S(1)}, f32[16,1,512]{2,1,0:T(1,128)S(1)}, u32[]{:S(2)}, u32[]{:S(2)}) collective-permute-start(f32[16,1,512]{2,1,0:T(1,128)S(1)} %get-tuple-element.34), channel_id=1, source_target_pairs={{0,1},{1,0},{2,3},{3,2},{4,5},{5,4},{6,7},{7,6},{8,9},{9,8},{10,11... | collective-permute-start | bytes 98312 | tf_op jit(solution)/shard_map/ppermute | solution.py:29
  35.6 3.1 %copy-start.1 = (f32[16,8,512]{2,1,0:T(8,128)}, f32[16,8,512]{2,1,0:T(8,128)S(1)}, u32[]{:S(2)}) copy-start(f32[16,8,512]{2,1,0:T(8,128)S(1)} %fusion.20.refs_2_.refs_4_) | copy-start | bytes 786436
  35.9 7.2 %collective-permute-start.13 = (f32[1,8,512]{2,1,0:T(8,128)S(1)}, f32[1,8,512]{2,1,0:T(8,128)S(1)}, u32[]{:S(2)}, u32[]{:S(2)}) collective-permute-start(f32[1,8,512]{2,1,0:T(8,128)S(1)} %get-tuple-element.27), channel_id=1, source_target_pairs={{8,16},{16,8},{9,17},{17,9},{10,18},{18,10},{11,19},{19,11},{12,20... | collective-permute-start | bytes 49160 | tf_op jit(solution)/shard_map/ppermute | solution.py:30
  36.5 6.5 %collective-permute-start.12 = (f32[1,8,512]{2,1,0:T(8,128)S(1)}, f32[1,8,512]{2,1,0:T(8,128)S(1)}, u32[]{:S(2)}, u32[]{:S(2)}) collective-permute-start(f32[1,8,512]{2,1,0:T(8,128)S(1)} %get-tuple-element.28), channel_id=1, source_target_pairs={{0,8},{8,0},{16,24},{24,16},{1,9},{9,1},{17,25},{25,17},{2,10},{10... | collective-permute-start | bytes 49160 | tf_op jit(solution)/shard_map/ppermute | solution.py:29
  38.7 4.4 %collective-permute-start.15 = (f32[16,1,512]{2,1,0:T(1,128)S(1)}, f32[16,1,512]{2,1,0:T(1,128)S(1)}, u32[]{:S(2)}, u32[]{:S(2)}) collective-permute-start(f32[16,1,512]{2,1,0:T(1,128)S(1)} %get-tuple-element.23), channel_id=1, source_target_pairs={{1,2},{2,1},{3,4},{4,3},{5,6},{6,5},{9,10},{10,9},{11,12},{12,11},... | collective-permute-start | bytes 98312 | tf_op jit(solution)/shard_map/ppermute | solution.py:30
  39.3 4.5 %collective-permute-start.14 = (f32[16,1,512]{2,1,0:T(1,128)S(1)}, f32[16,1,512]{2,1,0:T(1,128)S(1)}, u32[]{:S(2)}, u32[]{:S(2)}) collective-permute-start(f32[16,1,512]{2,1,0:T(1,128)S(1)} %get-tuple-element.24), channel_id=1, source_target_pairs={{0,1},{1,0},{2,3},{3,2},{4,5},{5,4},{6,7},{7,6},{8,9},{9,8},{10,11... | collective-permute-start | bytes 98312 | tf_op jit(solution)/shard_map/ppermute | solution.py:29
  44.3 4.5 %copy-start.2 = (f32[16,8,512]{2,1,0:T(8,128)}, f32[16,8,512]{2,1,0:T(8,128)S(1)}, u32[]{:S(2)}) copy-start(f32[16,8,512]{2,1,0:T(8,128)S(1)} %fusion.27.refs_3_.refs_5_) | copy-start | bytes 786436
  44.6 8.6 %collective-permute-start.17 = (f32[1,8,512]{2,1,0:T(8,128)S(1)}, f32[1,8,512]{2,1,0:T(8,128)S(1)}, u32[]{:S(2)}, u32[]{:S(2)}) collective-permute-start(f32[1,8,512]{2,1,0:T(8,128)S(1)} %get-tuple-element.17), channel_id=1, source_target_pairs={{8,16},{16,8},{9,17},{17,9},{10,18},{18,10},{11,19},{19,11},{12,20... | collective-permute-start | bytes 49160 | tf_op jit(solution)/shard_map/ppermute | solution.py:30
  45.3 8.0 %collective-permute-start.16 = (f32[1,8,512]{2,1,0:T(8,128)S(1)}, f32[1,8,512]{2,1,0:T(8,128)S(1)}, u32[]{:S(2)}, u32[]{:S(2)}) collective-permute-start(f32[1,8,512]{2,1,0:T(8,128)S(1)} %get-tuple-element.18), channel_id=1, source_target_pairs={{0,8},{8,0},{16,24},{24,16},{1,9},{9,1},{17,25},{25,17},{2,10},{10... | collective-permute-start | bytes 49160 | tf_op jit(solution)/shard_map/ppermute | solution.py:29
  48.9 4.4 %collective-permute-start.19 = (f32[16,1,512]{2,1,0:T(1,128)S(1)}, f32[16,1,512]{2,1,0:T(1,128)S(1)}, u32[]{:S(2)}, u32[]{:S(2)}) collective-permute-start(f32[16,1,512]{2,1,0:T(1,128)S(1)} %get-tuple-element.13), channel_id=1, source_target_pairs={{1,2},{2,1},{3,4},{4,3},{5,6},{6,5},{9,10},{10,9},{11,12},{12,11},... | collective-permute-start | bytes 98312 | tf_op jit(solution)/shard_map/ppermute | solution.py:30
  49.6 4.5 %collective-permute-start.18 = (f32[16,1,512]{2,1,0:T(1,128)S(1)}, f32[16,1,512]{2,1,0:T(1,128)S(1)}, u32[]{:S(2)}, u32[]{:S(2)}) collective-permute-start(f32[16,1,512]{2,1,0:T(1,128)S(1)} %get-tuple-element.14), channel_id=1, source_target_pairs={{0,1},{1,0},{2,3},{3,2},{4,5},{5,4},{6,7},{7,6},{8,9},{9,8},{10,11... | collective-permute-start | bytes 98312 | tf_op jit(solution)/shard_map/ppermute | solution.py:29
  57.5 1.6 %collective-permute-start.20 = (f32[1,128]{1,0:T(1,128)}, f32[1,128]{1,0:T(1,128)S(1)}, u32[]{:S(2)}, u32[]{:S(2)}) collective-permute-start(f32[1,128]{1,0:T(1,128)} %shard_map.85), channel_id=1, source_target_pairs={{0,1},{1,0},{2,3},{3,2},{4,5},{5,4},{6,7},{7,6},{8,9},{9,8},{10,11... | collective-permute-start | bytes 1544 | tf_op jit(solution)/shard_map/ppermute | solution.py:77
  59.8 3.5 %collective-permute-start.21 = (f32[1,128]{1,0:T(1,128)S(1)}, f32[1,128]{1,0:T(1,128)S(1)}, u32[]{:S(2)}, u32[]{:S(2)}) collective-permute-start(f32[1,128]{1,0:T(1,128)S(1)} %add.175), channel_id=1, source_target_pairs={{0,2},{1,3},{2,0},{3,1},{4,6},{5,7},{6,4},{7,5},{8,10},{9,11},{10,... | collective-permute-start | bytes 1544 | tf_op jit(solution)/shard_map/ppermute | solution.py:77
  63.3 4.5 %collective-permute-start.22 = (f32[1,128]{1,0:T(1,128)S(1)}, f32[1,128]{1,0:T(1,128)S(1)}, u32[]{:S(2)}, u32[]{:S(2)}) collective-permute-start(f32[1,128]{1,0:T(1,128)S(1)} %add.176), channel_id=1, source_target_pairs={{0,4},{1,5},{2,6},{3,7},{4,0},{5,1},{6,2},{7,3},{8,12},{9,13},{10,... | collective-permute-start | bytes 1544 | tf_op jit(solution)/shard_map/ppermute | solution.py:77
  67.8 3.5 %collective-permute-start.23 = (f32[1,128]{1,0:T(1,128)S(1)}, f32[1,128]{1,0:T(1,128)S(1)}, u32[]{:S(2)}, u32[]{:S(2)}) collective-permute-start(f32[1,128]{1,0:T(1,128)S(1)} %add.177), channel_id=1, source_target_pairs={{0,8},{8,0},{16,24},{24,16},{1,9},{9,1},{17,25},{25,17},{2,10},{10... | collective-permute-start | bytes 1544 | tf_op jit(solution)/shard_map/ppermute | solution.py:77
  71.3 3.5 %copy-start.10 = (f32[1,128]{1,0:T(1,128)}, f32[1,128]{1,0:T(1,128)S(1)}, u32[]{:S(2)}) copy-start(f32[1,128]{1,0:T(1,128)S(1)} %add.178.refs_0_) | copy-start | bytes 1540
  71.3 3.5 %collective-permute-start.24 = (f32[1,128]{1,0:T(1,128)S(1)}, f32[1,128]{1,0:T(1,128)S(1)}, u32[]{:S(2)}, u32[]{:S(2)}) collective-permute-start(f32[1,128]{1,0:T(1,128)S(1)} %add.178.refs_0_), channel_id=1, source_target_pairs={{0,16},{8,24},{16,0},{24,8},{1,17},{9,25},{17,1},{25,9},{2,18},{10... | collective-permute-start | bytes 1544 | tf_op jit(solution)/shard_map/ppermute | solution.py:77
  74.9 0.5 copy-start.11

commit v20 on v16

--- a/solution.py
+++ b/solution.py
@@ -55,8 +55,18 @@
     return total
 
 
+def face_exchange(u, axis, dim):
+    last = u.shape[dim] - 1
+    odd = lax.axis_index(axis) % 2 == 1
+    to_even = lax.dynamic_slice_in_dim(u, jnp.where(odd, 0, last), 1, axis=dim)
+    to_odd = lax.dynamic_slice_in_dim(u, jnp.where(odd, last, 0), 1, axis=dim)
+    even_swap = lax.ppermute(to_even, axis, swap_pairs(axis, 0))
+    odd_swap = lax.ppermute(to_odd, axis, swap_pairs(axis, 1))
+    return jnp.where(odd, even_swap, odd_swap), jnp.where(odd, odd_swap, even_swap)
+
+
 def field_halo(u):
-    return exchange(u[:1], u[-1:], u[:, :1], u[:, -1:])
+    return face_exchange(u, "gx", 0) + face_exchange(u, "gy", 1)
 
 
 def all_sum(x):

time: 78.7 us -> 78.8 us (level)
    ppermute x0 -> x16, starting transfers between devices: none -> 37.4 us  [the longest x8 32.1 us: face_exchange(): even_swap = lax.ppermute(to_even, axis, swap_pairs(axis, 0))]
    ppermute x10 -> x2, starting transfers between devices: 35.2 us -> 3.07 us  [axis_exchange(): lax.ppermute(jnp.where(odd, to_low, to_high), axis, swap_pairs(axis, 0))]
    ppermute x10 -> x2, starting transfers between devices: 6.75 us -> 1.45 us  [axis_exchange(): lax.ppermute(jnp.where(odd, to_high, to_low), axis, swap_pairs(axis, 1))]
    ppermute x0 -> x16, waiting for transfers between devices: none -> 3.37 us  [the longest x8 3.35 us: face_exchange(): even_swap = lax.ppermute(to_even, axis, swap_pairs(axis, 0))]
    ppermute x10 -> x2, waiting for transfers between devices: 3.35 us -> 0.01 us  [axis_exchange(): lax.ppermute(jnp.where(odd, to_low, to_high), axis, swap_pairs(axis, 0))]
where the time goes in v20:
time: 78.8 us; the launch traced here: 78.3 us
  starting transfers between devices  47.5 us (60%)
  waiting for transfers between devices  14.5 us (18%)
  local copies, waits for them, and re-layouts  5.56 us (7%)
  Pallas kernels  4.98 us (6%)
  other arithmetic  4.51 us (6%)
  between operations  1.22 us (2%)
    ppermute x8, starting transfers between devices, face_exchange(): even_swap = lax.ppermute(to_even, axis, swap_pairs(axis, 0))  32.1 us
    ppermute x5, waiting for transfers between devices, all_sum(): x = x + lax.ppermute(x, axis, [(i, i ^ step) for i in range(n)])  11.1 us
    ppermute x5, starting transfers between devices, all_sum(): x = x + lax.ppermute(x, axis, [(i, i ^ step) for i in range(n)])  5.56 us
    ppermute x8, starting transfers between devices, face_exchange(): odd_swap = lax.ppermute(to_odd, axis, swap_pairs(axis, 1))  5.3 us
    ppermute x8, waiting for transfers between devices, face_exchange(): even_swap = lax.ppermute(to_even, axis, swap_pairs(axis, 0))  3.35 us
    ppermute x2, starting transfers between devices, axis_exchange(): lax.ppermute(jnp.where(odd, to_low, to_high), axis, swap_pairs(axis, 0))  3.07 us
    pallas_call x1, Pallas kernels, finish(): pl.pallas_call(lambda *refs: finish_kernel(float(cells), size, *refs), ou...  2.75 us
    div x4, other arithmetic, local(): vector = 2.0 * total / diagonal  2.49 us
  transfers between devices with their start and end apart: 25, of which 9 were waited for; matrix products, arithmetic and copies ran while one was open for 4% of the time, Pallas kernels for 0%

profile of v20, /device:TPU:0, one launch (start us, length us, event | category | flops | bytes accessed | tf_op | source)
XLA Modules:
  0.0 78.3 jit_solution(12450777056453066028)
XLA Ops:
  0.7 0.8 %fusion.54 = (f32[1,8,512]{2,1,0:T(8,128)S(1)}, f32[1,8,512]{2,1,0:T(8,128)S(1)}, f32[1,8,512]{2,1,0:T(8,128)S(1)}, f32[1,8,512]{2,1,0:T(8,128)S(1)}) fusion(f32[16,8,512]{2,1,0:T(8,128)} %param.6, f32[16,8,512]{2,1,0:T(8,128)} %param.9), kind=kLoop, calls=%fused_computation.119 | loop fusion | bytes 131072 | tf_op jit(solution)/shard_map/slice | solution.py:209
  1.5 3.0 %collective-permute-start.1 = (f32[2,8,512]{2,1,0:T(8,128)S(1)}, f32[2,8,512]{2,1,0:T(8,128)S(1)}, u32[]{:S(2)}, u32[]{:S(2)}) collective-permute-start(f32[2,8,512]{2,1,0:T(8,128)S(1)} %get-tuple-element.75), channel_id=1, source_target_pairs={{0,8},{8,0},{16,24},{24,16},{1,9},{9,1},{17,25},{25,17},{2,10},{10... | collective-permute-start | bytes 98312 | tf_op jit(solution)/shard_map/ppermute | solution.py:29
  4.5 0.7 collective-permute-start
  5.2 1.3 %fusion.51 = (f32[16,1,512]{2,1,0:T(1,128)S(1)}, f32[16,1,512]{2,1,0:T(1,128)S(1)}, f32[16,1,512]{2,1,0:T(1,128)S(1)}, f32[16,1,512]{2,1,0:T(1,128)S(1)}) fusion(f32[16,8,512]{2,1,0:T(8,128)} %param.6, f32[16,8,512]{2,1,0:T(8,128)} %param.10), kind=kLoop, calls=%fused_computation.116 | loop fusion | bytes 262144 | tf_op jit(solution)/shard_map/slice | solution.py:211
  6.5 0.1 broadcast_select_fusion.10
  6.6 0.1 collective-permute-start.3
  6.7 0.8 %collective-permute-start.2 = (f32[16,2,512]{2,1,0:T(2,128)S(1)}, f32[16,2,512]{2,1,0:T(2,128)S(1)}, u32[]{:S(2)}, u32[]{:S(2)}) collective-permute-start(f32[16,2,512]{2,1,0:T(2,128)S(1)} %get-tuple-element.64), channel_id=1, source_target_pairs={{1,2},{2,1},{3,4},{4,3},{5,6},{6,5},{9,10},{10,9},{11,12},{12,11},... | collective-permute-start | bytes 196616 | tf_op jit(solution)/shard_map/ppermute | solution.py:30
  7.5 1.1 %fusion.50 = (f32[16,7,512]{2,1,0:T(8,128)S(1)}, f32[16,7,512]{2,1,0:T(8,128)S(1)}) fusion(f32[16,8,512]{2,1,0:T(8,128)} %param.6), kind=kLoop, calls=%fused_computation.115 | loop fusion | bytes 917504 | tf_op jit(solution)/shard_map/slice | solution.py:49
  8.6 0.1 fusion.49
  8.7 0.1 fusion.53
  8.9 0.7 copy-done.5
  9.6 0.1 copy-done.7
  9.6 0.1 slice.153
  9.8 0.1 fusion.56
  10.0 0.5 fusion.6.refs_0_.refs_1_
  10.5 0.1 fusion.48
  10.5 0.1 fusion.46
  10.7 0.1 fusion.47
  10.8 0.7 collective-permute-start.5
  11.4 5.7 %collective-permute-start.4 = (f32[1,8,512]{2,1,0:T(8,128)S(1)}, f32[1,8,512]{2,1,0:T(8,128)S(1)}, u32[]{:S(2)}, u32[]{:S(2)}) collective-permute-start(f32[1,8,512]{2,1,0:T(8,128)S(1)} %get-tuple-element.48), channel_id=1, source_target_pairs={{0,8},{8,0},{16,24},{24,16},{1,9},{9,1},{17,25},{25,17},{2,10},{10... | collective-permute-start | bytes 49160 | tf_op jit(solution)/shard_map/ppermute | solution.py:63
  17.1 0.1 constant_dynamic-slice_fusion.12
  17.2 0.7 collective-permute-start.7
  17.9 5.9 %collective-permute-start.6 = (f32[16,1,512]{2,1,0:T(1,128)S(1)}, f32[16,1,512]{2,1,0:T(1,128)S(1)}, u32[]{:S(2)}, u32[]{:S(2)}) collective-permute-start(f32[16,1,512]{2,1,0:T(1,128)S(1)} %get-tuple-element.44), channel_id=1, source_target_pairs={{0,1},{1,0},{2,3},{3,2},{4,5},{5,4},{6,7},{7,6},{8,9},{9,8},{10,11... | collective-permute-start | bytes 98312 | tf_op jit(solution)/shard_map/ppermute | solution.py:63
  23.8 0.8 %collective-permute-done.6 = f32[16,1,512]{2,1,0:T(1,128)S(1)} collective-permute-done((f32[16,1,512]{2,1,0:T(1,128)S(1)}, f32[16,1,512]{2,1,0:T(1,128)S(1)}, u32[]{:S(2)}, u32[]{:S(2)}) %collective-permute-start.6) | collective-permute-done | bytes 32800 | tf_op jit(solution)/shard_map/ppermute | solution.py:63
  24.6 0.4 fusion.13.refs_1_.refs_2_
  25.2 0.1 fusion.43
  25.3 0.1 fusion.44
  25.4 0.7 collective-permute-start.9
  26.0 3.8 %collective-permute-start.8 = (f32[1,8,512]{2,1,0:T(8,128)S(1)}, f32[1,8,512]{2,1,0:T(8,128)S(1)}, u32[]{:S(2)}, u32[]{:S(2)}) collective-permute-start(f32[1,8,512]{2,1,0:T(8,128)S(1)} %get-tuple-element.38), channel_id=1, source_target_pairs={{0,8},{8,0},{16,24},{24,16},{1,9},{9,1},{17,25},{25,17},{2,10},{10... | collective-permute-start | bytes 49160 | tf_op jit(solution)/shard_map/ppermute | solution.py:63
  29.8 0.1 constant_dynamic-slice_fusion.8
  29.9 0.7 collective-permute-start.11
  30.6 3.7 %collective-permute-start.10 = (f32[16,1,512]{2,1,0:T(1,128)S(1)}, f32[16,1,512]{2,1,0:T(1,128)S(1)}, u32[]{:S(2)}, u32[]{:S(2)}) collective-permute-start(f32[16,1,512]{2,1,0:T(1,128)S(1)} %get-tuple-element.34), channel_id=1, source_target_pairs={{0,1},{1,0},{2,3},{3,2},{4,5},{5,4},{6,7},{7,6},{8,9},{9,8},{10,11... | collective-permute-start | bytes 98312 | tf_op jit(solution)/shard_map/ppermute | solution.py:63
  34.3 0.8 %collective-permute-done.10 = f32[16,1,512]{2,1,0:T(1,128)S(1)} collective-permute-done((f32[16,1,512]{2,1,0:T(1,128)S(1)}, f32[16,1,512]{2,1,0:T(1,128)S(1)}, u32[]{:S(2)}, u32[]{:S(2)}) %collective-permute-start.10) | collective-permute-done | bytes 32800 | tf_op jit(solution)/shard_map/ppermute | solution.py:63
  35.1 0.4 fusion.20.refs_2_.refs_3_
  35.7 0.1 fusion.40
  35.8 0.1 fusion.41
  35.9 0.7 collective-permute-start.13
  36.6 2.1 %collective-permute-start.12 = (f32[1,8,512]{2,1,0:T(8,128)S(1)}, f32[1,8,512]{2,1,0:T(8,128)S(1)}, u32[]{:S(2)}, u32[]{:S(2)}) collective-permute-start(f32[1,8,512]{2,1,0:T(8,128)S(1)} %get-tuple-element.28), channel_id=1, source_target_pairs={{0,8},{8,0},{16,24},{24,16},{1,9},{9,1},{17,25},{25,17},{2,10},{10... | collective-permute-start | bytes 49160 | tf_op jit(solution)/shard_map/ppermute | solution.py:63
  38.6 0.1 constant_dynamic-slice_fusion.4
  38.7 0.7 collective-permute-start.15
  39.4 3.7 %collective-permute-start.14 = (f32[16,1,512]{2,1,0:T(1,128)S(1)}, f32[16,1,512]{2,1,0:T(1,128)S(1)}, u32[]{:S(2)}, u32[]{:S(2)}) collective-permute-start(f32[16,1,512]{2,1,0:T(1,128)S(1)} %get-tuple-element.24), channel_id=1, source_target_pairs={{0,1},{1,0},{2,3},{3,2},{4,5},{5,4},{6,7},{7,6},{8,9},{9,8},{10,11... | collective-permute-start | bytes 98312 | tf_op jit(solution)/shard_map/ppermute | solution.py:63
  43.1 0.8 %collective-permute-done.14 = f32[16,1,512]{2,1,0:T(1,128)S(1)} collective-permute-done((f32[16,1,512]{2,1,0:T(1,128)S(1)}, f32[16,1,512]{2,1,0:T(1,128)S(1)}, u32[]{:S(2)}, u32[]{:S(2)}) %collective-permute-start.14) | collective-permute-done | bytes 32800 | tf_op jit(solution)/shard_map/ppermute | solution.py:63
  43.9 0.4 fusion.27.refs_3_.refs_4_
  44.5 0.1 fusion.37
  44.6 0.1 fusion.38
  44.7 0.7 collective-permute-start.17
  45.3 3.6 %collective-permute-start.16 = (f32[1,8,512]{2,1,0:T(8,128)S(1)}, f32[1,8,512]{2,1,0:T(8,128)S(1)}, u32[]{:S(2)}, u32[]{:S(2)}) collective-permute-start(f32[1,8,512]{2,1,0:T(8,128)S(1)} %get-tuple-element.18), channel_id=1, source_target_pairs={{0,8},{8,0},{16,24},{24,16},{1,9},{9,1},{17,25},{25,17},{2,10},{10... | collective-permute-start | bytes 49160 | tf_op jit(solution)/shard_map/ppermute | solution.py:63
  48.9 0.1 constant_dynamic-slice_fusion
  49.0 0.7 collective-permute-start.19
  49.6 3.7 %collective-permute-start.18 = (f32[16,1,512]{2,1,0:T(1,128)S(1)}, f32[16,1,512]{2,1,0:T(1,128)S(1)}, u32[]{:S(2)}, u32[]{:S(2)}) collective-permute-start(f32[16,1,512]{2,1,0:T(1,128)S(1)} %get-tuple-element.14), channel_id=1, source_target_pairs={{0,1},{1,0},{2,3},{3,2},{4,5},{5,4},{6,7},{7,6},{8,9},{9,8},{10,11... | collective-permute-start | bytes 98312 | tf_op jit(solution)/shard_map/ppermute | solution.py:63
  53.4 0.8 %collective-permute-done.18 = f32[16,1,512]{2,1,0:T(1,128)S(1)} collective-permute-done((f32[16,1,512]{2,1,0:T(1,128)S(1)}, f32[16,1,512]{2,1,0:T(1,128)S(1)}, u32[]{:S(2)}, u32[]{:S(2)}) %collective-permute-start.18) | collective-permute-done | bytes 32800 | tf_op jit(solution)/shard_map/ppermute | solution.py:63
  54.2 1.1 %fusion.34.refs_4_.refs_5_ = f32[16,8,512]{2,1,0:T(8,128)} fusion(f32[16,8,512]{2,1,0:T(8,128)S(1)} %copy-done.6, f32[15,8,512]{2,1,0:T(8,128)S(1)} %get-tuple-element.16, f32[1,8,512]{2,1,0:T(8,128)S(1)} %get-tuple-element.78, f32[1,8,512]{2,1,0:T(8,128)S(1)} %get-tuple-element.77, f32[15,8,512]{2,1,0:T(8,128)S(1)} %get-tuple-element.15, ...), kind=kLoop, calls=%fused_computation.53 | loop fusion | flops 1638400 | bytes 3668480 | tf_op jit(solution)/shard_map/div | solution.py:233
  55.3 2.2 %shard_map.85 = f32[1,128]{1,0:T(1,128)} custom-call(f32[16,8,512]{2,1,0:T(8,128)} %copy-done.3, f32[16,8,512]{2,1,0:T(8,128)} %copy-done, f32[16,8,512]{2,1,0:T(8,128)} %copy-done.1, f32[16,8,512]{2,1,0:T(8,128)} %copy-done.2, f32[16,8,512]{2,1,0:T(8,128)} %fusion.34.refs_4_.refs_5_), custom_call_target="tpu_custom_call" | custom-call | tf_op jit(solution)/shard_map/pallas_call | solution.py:117
  57.6 0.7 collective-permute-start.20
  58.2 1.0 %collective-permute-done.20 = f32[1,128]{1,0:T(1,128)S(1)} collective-permute-done((f32[1,128]{1,0:T(1,128)}, f32[1,128]{1,0:T(1,128)S(1)}, u32[]{:S(2)}, u32[]{:S(2)}) %collective-permute-start.20) | collective-permute-done | bytes 544 | tf_op jit(solution)/shard_map/ppermute | solution.py:80
  59.2 0.7 add.194
  59.9 1.9 %collective-permute-start.21 = (f32[1,128]{1,0:T(1,128)S(1)}, f32[1,128]{1,0:T(1,128)S(1)}, u32[]{:S(2)}, u32[]{:S(2)}) collective-permute-start(f32[1,128]{1,0:T(1,128)S(1)} %add.194), channel_id=1, source_target_pairs={{0,2},{1,3},{2,0},{3,1},{4,6},{5,7},{6,4},{7,5},{8,10},{9,11},{10,... | collective-permute-start | bytes 1544 | tf_op jit(solution)/shard_map/ppermute | solution.py:80
  61.8 1.6 %collective-permute-done.21 = f32[1,128]{1,0:T(1,128)S(1)} collective-permute-done((f32[1,128]{1,0:T(1,128)S(1)}, f32[1,128]{1,0:T(1,128)S(1)}, u32[]{:S(2)}, u32[]{:S(2)}) %collective-permute-start.21) | collective-permute-done | bytes 544 | tf_op jit(solution)/shard_map/ppermute | solution.py:80
  63.4 2.9 %collective-permute-start.22 = (f32[1,128]{1,0:T(1,128)S(1)}, f32[1,128]{1,0:T(1,128)S(1)}, u32[]{:S(2)}, u32[]{:S(2)}) collective-permute-start(f32[1,128]{1,0:T(1,128)S(1)} %add.195), channel_id=1, source_target_pairs={{0,4},{1,5},{2,6},{3,7},{4,0},{5,1},{6,2},{7,3},{8,12},{9,13},{10,... | collective-permute-start | bytes 1544 | tf_op jit(solution)/shard_map/ppermute | solution.py:80
  66.3 1.5 %collective-permute-done.22 = f32[1,128]{1,0:T(1,128)S(1)} collective-permute-done((f32[1,128]{1,0:T(1,128)S(1)}, f32[1,128]{1,0:T(1,128)S(1)}, u32[]{:S(2)}, u32[]{:S(2)}) %collective-permute-start.22) | collective-permute-done | bytes 544 | tf_op jit(solution)/shard_map/ppermute | solution.py:80
  67.9 3.5 %collective-permute-done.23 = f32[1,128]{1,0:T(1,128)S(1)} collective-permute-done((f32[1,128]{1,0:T(1,128)S(1)}, f32[1,128]{1,0:T(1,128)S(1)}, u32[]{:S(2)}, u32[]{:S(2)}) %collective-permute-start.23) | collective-permute-done | bytes 544 | tf_op jit(solution)/shard_map/ppermute | solution.py:80
  71.4 3.5 %collective-permute-done.24 = f32[1,128]{1,0:T(1,128)S(1)} collective-permute-done((f32[1,128]{1,0:T(1,128)S(1)}, f32[1,128]{1,0:T(1,128)S(1)}, u32[]{:S(2)}, u32[]{:S(2)}) %collective-permute-start.24) | collective-permute-done | bytes 544 | tf_op jit(solution)/shard_map/ppermute | solution.py:80
  74.9 0.6 add.198.refs_0_
  75.5 2.8 %shard_map.86 = (f32[5,16,8,512]{3,2,1,0:T(8,128)}, f32[5,5]{1,0:T(8,128)}, f32[1,1]{1,0:T(1,128)}) custom-call(f32[1,128]{1,0:T(1,128)} %add.198.refs_0_, f32[16,8,512]{2,1,0:T(8,128)} %copy-done.3, f32[16,8,512]{2,1,0:T(8,128)} %copy-done, f32[16,8,512]{2,1,0:T(8,128)} %copy-done.1, f32[16,8,512]{2,1,0:T(8,128)} %copy-done.2, ...), custom_call_target="tpu_custom_call" | custom-call | tf_op jit(solution)/shard_map/pallas_call | solution.py:190
  (62 shorter events, 0.5 us)
Async XLA Ops:
  0.6 7.9 %copy-start.4 = (f32[16,8,512]{2,1,0:T(8,128)S(1)}, f32[16,8,512]{2,1,0:T(8,128)}, u32[]{:S(2)}) copy-start(f32[16,8,512]{2,1,0:T(8,128)} %param.6) | copy-start | bytes 786436
  1.5 8.3 %collective-permute-start.1 = (f32[2,8,512]{2,1,0:T(8,128)S(1)}, f32[2,8,512]{2,1,0:T(8,128)S(1)}, u32[]{:S(2)}, u32[]{:S(2)}) collective-permute-start(f32[2,8,512]{2,1,0:T(8,128)S(1)} %get-tuple-element.75), channel_id=1, source_target_pairs={{0,8},{8,0},{16,24},{24,16},{1,9},{9,1},{17,25},{25,17},{2,10},{10... | collective-permute-start | bytes 98312 | tf_op jit(solution)/shard_map/ppermute | solution.py:29
  4.5 5.3 %collective-permute-start = (f32[2,8,512]{2,1,0:T(8,128)S(1)}, f32[2,8,512]{2,1,0:T(8,128)S(1)}, u32[]{:S(2)}, u32[]{:S(2)}) collective-permute-start(f32[2,8,512]{2,1,0:T(8,128)S(1)} %get-tuple-element.76), channel_id=1, source_target_pairs={{8,16},{16,8},{9,17},{17,9},{10,18},{18,10},{11,19},{19,11},{12,20... | collective-permute-start | bytes 98312 | tf_op jit(solution)/shard_map/ppermute | solution.py:30
  6.6 3.2 %collective-permute-start.3 = (f32[16,2,512]{2,1,0:T(2,128)S(1)}, f32[16,2,512]{2,1,0:T(2,128)S(1)}, u32[]{:S(2)}, u32[]{:S(2)}) collective-permute-start(f32[16,2,512]{2,1,0:T(2,128)S(1)} %get-tuple-element.63), channel_id=1, source_target_pairs={{0,1},{1,0},{2,3},{3,2},{4,5},{5,4},{6,7},{7,6},{8,9},{9,8},{10,11... | collective-permute-start | bytes 196616 | tf_op jit(solution)/shard_map/ppermute | solution.py:29
  6.7 2.2 %copy-start.6 = (f32[16,8,512]{2,1,0:T(8,128)S(1)}, f32[16,8,512]{2,1,0:T(8,128)}, u32[]{:S(2)}) copy-start(f32[16,8,512]{2,1,0:T(8,128)} %param.9) | copy-start | bytes 786436
  6.7 3.1 %collective-permute-start.2 = (f32[16,2,512]{2,1,0:T(2,128)S(1)}, f32[16,2,512]{2,1,0:T(2,128)S(1)}, u32[]{:S(2)}, u32[]{:S(2)}) collective-permute-start(f32[16,2,512]{2,1,0:T(2,128)S(1)} %get-tuple-element.64), channel_id=1, source_target_pairs={{1,2},{2,1},{3,4},{4,3},{5,6},{6,5},{9,10},{10,9},{11,12},{12,11},... | collective-permute-start | bytes 196616 | tf_op jit(solution)/shard_map/ppermute | solution.py:30
  8.6 1.0 %copy-start.5 = (f32[16,8,512]{2,1,0:T(8,128)S(1)}, f32[16,8,512]{2,1,0:T(8,128)}, u32[]{:S(2)}) copy-start(f32[16,8,512]{2,1,0:T(8,128)} %param.10) | copy-start | bytes 786436
  8.6 1.0 %copy-start.7 = (f32[16,8,512]{2,1,0:T(8,128)S(1)}, f32[16,8,512]{2,1,0:T(8,128)}, u32[]{:S(2)}) copy-start(f32[16,8,512]{2,1,0:T(8,128)} %param.11) | copy-start | bytes 786436
  8.8 1.2 %copy-start.8 = (f32[16,8,512]{2,1,0:T(8,128)S(1)}, f32[16,8,512]{2,1,0:T(8,128)}, u32[]{:S(2)}) copy-start(f32[16,8,512]{2,1,0:T(8,128)} %param.8) | copy-start | bytes 786436
  8.8 1.2 %copy-start.9 = (f32[16,8,512]{2,1,0:T(8,128)S(1)}, f32[16,8,512]{2,1,0:T(8,128)}, u32[]{:S(2)}) copy-start(f32[16,8,512]{2,1,0:T(8,128)} %param.7) | copy-start | bytes 786436
  10.5 6.7 %copy-start.3 = (f32[16,8,512]{2,1,0:T(8,128)}, f32[16,8,512]{2,1,0:T(8,128)S(1)}, u32[]{:S(2)}) copy-start(f32[16,8,512]{2,1,0:T(8,128)S(1)} %fusion.6.refs_0_.refs_1_) | copy-start | bytes 786436
  10.8 13.0 %collective-permute-start.5 = (f32[1,8,512]{2,1,0:T(8,128)S(1)}, f32[1,8,512]{2,1,0:T(8,128)S(1)}, u32[]{:S(2)}, u32[]{:S(2)}) collective-permute-start(f32[1,8,512]{2,1,0:T(8,128)S(1)} %get-tuple-element.47), channel_id=1, source_target_pairs={{8,16},{16,8},{9,17},{17,9},{10,18},{18,10},{11,19},{19,11},{12,20... | collective-permute-start | bytes 49160 | tf_op jit(solution)/shard_map/ppermute | solution.py:64
  11.4 12.3 %collective-permute-start.4 = (f32[1,8,512]{2,1,0:T(8,128)S(1)}, f32[1,8,512]{2,1,0:T(8,128)S(1)}, u32[]{:S(2)}, u32[]{:S(2)}) collective-permute-start(f32[1,8,512]{2,1,0:T(8,128)S(1)} %get-tuple-element.48), channel_id=1, source_target_pairs={{0,8},{8,0},{16,24},{24,16},{1,9},{9,1},{17,25},{25,17},{2,10},{10... | collective-permute-start | bytes 49160 | tf_op jit(solution)/shard_map/ppermute | solution.py:63
  17.2 6.6 %collective-permute-start.7 = (f32[16,1,512]{2,1,0:T(1,128)S(1)}, f32[16,1,512]{2,1,0:T(1,128)S(1)}, u32[]{:S(2)}, u32[]{:S(2)}) collective-permute-start(f32[16,1,512]{2,1,0:T(1,128)S(1)} %get-tuple-element.43), channel_id=1, source_target_pairs={{1,2},{2,1},{3,4},{4,3},{5,6},{6,5},{9,10},{10,9},{11,12},{12,11},... | collective-permute-start | bytes 98312 | tf_op jit(solution)/shard_map/ppermute | solution.py:64
  17.9 6.8 %collective-permute-start.6 = (f32[16,1,512]{2,1,0:T(1,128)S(1)}, f32[16,1,512]{2,1,0:T(1,128)S(1)}, u32[]{:S(2)}, u32[]{:S(2)}) collective-permute-start(f32[16,1,512]{2,1,0:T(1,128)S(1)} %get-tuple-element.44), channel_id=1, source_target_pairs={{0,1},{1,0},{2,3},{3,2},{4,5},{5,4},{6,7},{7,6},{8,9},{9,8},{10,11... | collective-permute-start | bytes 98312 | tf_op jit(solution)/shard_map/ppermute | solution.py:63
  25.1 4.8 %copy-start = (f32[16,8,512]{2,1,0:T(8,128)}, f32[16,8,512]{2,1,0:T(8,128)S(1)}, u32[]{:S(2)}) copy-start(f32[16,8,512]{2,1,0:T(8,128)S(1)} %fusion.13.refs_1_.refs_2_) | copy-start | bytes 786436
  25.4 8.9 %collective-permute-start.9 = (f32[1,8,512]{2,1,0:T(8,128)S(1)}, f32[1,8,512]{2,1,0:T(8,128)S(1)}, u32[]{:S(2)}, u32[]{:S(2)}) collective-permute-start(f32[1,8,512]{2,1,0:T(8,128)S(1)} %get-tuple-element.37), channel_id=1, source_target_pairs={{8,16},{16,8},{9,17},{17,9},{10,18},{18,10},{11,19},{19,11},{12,20... | collective-permute-start | bytes 49160 | tf_op jit(solution)/shard_map/ppermute | solution.py:64
  26.0 8.2 %collective-permute-start.8 = (f32[1,8,512]{2,1,0:T(8,128)S(1)}, f32[1,8,512]{2,1,0:T(8,128)S(1)}, u32[]{:S(2)}, u32[]{:S(2)}) collective-permute-start(f32[1,8,512]{2,1,0:T(8,128)S(1)} %get-tuple-element.38), channel_id=1, source_target_pairs={{0,8},{8,0},{16,24},{24,16},{1,9},{9,1},{17,25},{25,17},{2,10},{10... | collective-permute-start | bytes 49160 | tf_op jit(solution)/shard_map/ppermute | solution.py:63
  29.9 4.4 %collective-permute-start.11 = (f32[16,1,512]{2,1,0:T(1,128)S(1)}, f32[16,1,512]{2,1,0:T(1,128)S(1)}, u32[]{:S(2)}, u32[]{:S(2)}) collective-permute-start(f32[16,1,512]{2,1,0:T(1,128)S(1)} %get-tuple-element.33), channel_id=1, source_target_pairs={{1,2},{2,1},{3,4},{4,3},{5,6},{6,5},{9,10},{10,9},{11,12},{12,11},... | collective-permute-start | bytes 98312 | tf_op jit(solution)/shard_map/ppermute | solution.py:64
  30.6 4.6 %collective-permute-start.10 = (f32[16,1,512]{2,1,0:T(1,128)S(1)}, f32[16,1,512]{2,1,0:T(1,128)S(1)}, u32[]{:S(2)}, u32[]{:S(2)}) collective-permute-start(f32[16,1,512]{2,1,0:T(1,128)S(1)} %get-tuple-element.34), channel_id=1, source_target_pairs={{0,1},{1,0},{2,3},{3,2},{4,5},{5,4},{6,7},{7,6},{8,9},{9,8},{10,11... | collective-permute-start | bytes 98312 | tf_op jit(solution)/shard_map/ppermute | solution.py:63
  35.6 3.1 %copy-start.1 = (f32[16,8,512]{2,1,0:T(8,128)}, f32[16,8,512]{2,1,0:T(8,128)S(1)}, u32[]{:S(2)}) copy-start(f32[16,8,512]{2,1,0:T(8,128)S(1)} %fusion.20.refs_2_.refs_3_) | copy-start | bytes 786436
  35.9 7.2 %collective-permute-start.13 = (f32[1,8,512]{2,1,0:T(8,128)S(1)}, f32[1,8,512]{2,1,0:T(8,128)S(1)}, u32[]{:S(2)}, u32[]{:S(2)}) collective-permute-start(f32[1,8,512]{2,1,0:T(8,128)S(1)} %get-tuple-element.27), channel_id=1, source_target_pairs={{8,16},{16,8},{9,17},{17,9},{10,18},{18,10},{11,19},{19,11},{12,20... | collective-permute-start | bytes 49160 | tf_op jit(solution)/shard_map/ppermute | solution.py:64
  36.6 6.5 %collective-permute-start.12 = (f32[1,8,512]{2,1,0:T(8,128)S(1)}, f32[1,8,512]{2,1,0:T(8,128)S(1)}, u32[]{:S(2)}, u32[]{:S(2)}) collective-permute-start(f32[1,8,512]{2,1,0:T(8,128)S(1)} %get-tuple-element.28), channel_id=1, source_target_pairs={{0,8},{8,0},{16,24},{24,16},{1,9},{9,1},{17,25},{25,17},{2,10},{10... | collective-permute-start | bytes 49160 | tf_op jit(solution)/shard_map/ppermute | solution.py:63
  38.7 4.4 %collective-permute-start.15 = (f32[16,1,512]{2,1,0:T(1,128)S(1)}, f32[16,1,512]{2,1,0:T(1,128)S(1)}, u32[]{:S(2)}, u32[]{:S(2)}) collective-permute-start(f32[16,1,512]{2,1,0:T(1,128)S(1)} %get-tuple-element.23), channel_id=1, source_target_pairs={{1,2},{2,1},{3,4},{4,3},{5,6},{6,5},{9,10},{10,9},{11,12},{12,11},... | collective-permute-start | bytes 98312 | tf_op jit(solution)/shard_map/ppermute | solution.py:64
  39.4 4.5 %collective-permute-start.14 = (f32[16,1,512]{2,1,0:T(1,128)S(1)}, f32[16,1,512]{2,1,0:T(1,128)S(1)}, u32[]{:S(2)}, u32[]{:S(2)}) collective-permute-start(f32[16,1,512]{2,1,0:T(1,128)S(1)} %get-tuple-element.24), channel_id=1, source_target_pairs={{0,1},{1,0},{2,3},{3,2},{4,5},{5,4},{6,7},{7,6},{8,9},{9,8},{10,11... | collective-permute-start | bytes 98312 | tf_op jit(solution)/shard_map/ppermute | solution.py:63
  44.4 4.5 %copy-start.2 = (f32[16,8,512]{2,1,0:T(8,128)}, f32[16,8,512]{2,1,0:T(8,128)S(1)}, u32[]{:S(2)}) copy-start(f32[16,8,512]{2,1,0:T(8,128)S(1)} %fusion.27.refs_3_.refs_4_) | copy-start | bytes 786436
  44.7 8.7 %collective-permute-start.17 = (f32[1,8,512]{2,1,0:T(8,128)S(1)}, f32[1,8,512]{2,1,0:T(8,128)S(1)}, u32[]{:S(2)}, u32[]{:S(2)}) collective-permute-start(f32[1,8,512]{2,1,0:T(8,128)S(1)} %get-tuple-element.17), channel_id=1, source_target_pairs={{8,16},{16,8},{9,17},{17,9},{10,18},{18,10},{11,19},{19,11},{12,20... | collective-permute-start | bytes 49160 | tf_op jit(solution)/shard_map/ppermute | solution.py:64
  45.3 8.0 %collective-permute-start.16 = (f32[1,8,512]{2,1,0:T(8,128)S(1)}, f32[1,8,512]{2,1,0:T(8,128)S(1)}, u32[]{:S(2)}, u32[]{:S(2)}) collective-permute-start(f32[1,8,512]{2,1,0:T(8,128)S(1)} %get-tuple-element.18), channel_id=1, source_target_pairs={{0,8},{8,0},{16,24},{24,16},{1,9},{9,1},{17,25},{25,17},{2,10},{10... | collective-permute-start | bytes 49160 | tf_op jit(solution)/shard_map/ppermute | solution.py:63
  49.0 4.4 %collective-permute-start.19 = (f32[16,1,512]{2,1,0:T(1,128)S(1)}, f32[16,1,512]{2,1,0:T(1,128)S(1)}, u32[]{:S(2)}, u32[]{:S(2)}) collective-permute-start(f32[16,1,512]{2,1,0:T(1,128)S(1)} %get-tuple-element.13), channel_id=1, source_target_pairs={{1,2},{2,1},{3,4},{4,3},{5,6},{6,5},{9,10},{10,9},{11,12},{12,11},... | collective-permute-start | bytes 98312 | tf_op jit(solution)/shard_map/ppermute | solution.py:64
  49.6 4.5 %collective-permute-start.18 = (f32[16,1,512]{2,1,0:T(1,128)S(1)}, f32[16,1,512]{2,1,0:T(1,128)S(1)}, u32[]{:S(2)}, u32[]{:S(2)}) collective-permute-start(f32[16,1,512]{2,1,0:T(1,128)S(1)} %get-tuple-element.14), channel_id=1, source_target_pairs={{0,1},{1,0},{2,3},{3,2},{4,5},{5,4},{6,7},{7,6},{8,9},{9,8},{10,11... | collective-permute-start | bytes 98312 | tf_op jit(solution)/shard_map/ppermute | solution.py:63
  57.6 1.6 %collective-permute-start.20 = (f32[1,128]{1,0:T(1,128)}, f32[1,128]{1,0:T(1,128)S(1)}, u32[]{:S(2)}, u32[]{:S(2)}) collective-permute-start(f32[1,128]{1,0:T(1,128)} %shard_map.85), channel_id=1, source_target_pairs={{0,1},{1,0},{2,3},{3,2},{4,5},{5,4},{6,7},{7,6},{8,9},{9,8},{10,11... | collective-permute-start | bytes 1544 | tf_op jit(solution)/shard_map/ppermute | solution.py:80
  59.9 3.5 %collective-permute-start.21 = (f32[1,128]{1,0:T(1,128)S(1)}, f32[1,128]{1,0:T(1,128)S(1)}, u32[]{:S(2)}, u32[]{:S(2)}) collective-permute-start(f32[1,128]{1,0:T(1,128)S(1)} %add.194), channel_id=1, source_target_pairs={{0,2},{1,3},{2,0},{3,1},{4,6},{5,7},{6,4},{7,5},{8,10},{9,11},{10,... | collective-permute-start | bytes 1544 | tf_op jit(solution)/shard_map/ppermute | solution.py:80
  63.4 4.5 %collective-permute-start.22 = (f32[1,128]{1,0:T(1,128)S(1)}, f32[1,128]{1,0:T(1,128)S(1)}, u32[]{:S(2)}, u32[]{:S(2)}) collective-permute-start(f32[1,128]{1,0:T(1,128)S(1)} %add.195), channel_id=1, source_target_pairs={{0,4},{1,5},{2,6},{3,7},{4,0},{5,1},{6,2},{7,3},{8,12},{9,13},{10,... | collective-permute-start | bytes 1544 | tf_op jit(solution)/shard_map/ppermute | solution.py:80
  67.9 3.5 %collective-permute-start.23 = (f32[1,128]{1,0:T(1,128)S(1)}, f32[1,128]{1,0:T(1,128)S(1)}, u32[]{:S(2)}, u32[]{:S(2)}) collective-permute-start(f32[1,128]{1,0:T(1,128)S(1)} %add.196), channel_id=1, source_target_pairs={{0,8},{8,0},{16,24},{24,16},{1,9},{9,1},{17,25},{25,17},{2,10},{10... | collective-permute-start | bytes 1544 | tf_op jit(solution)/shard_map/ppermute | solution.py:80
  71.4 3.5 %collective-permute-start.24 = (f32[1,128]{1,0:T(1,128)S(1)}, f32[1,128]{1,0:T(1,128)S(1)}, u32[]{:S(2)}, u32[]{:S(2)}) collective-permute-start(f32[1,128]{1,0:T(1,128)S(1)} %add.197), channel_id=1, source_target_pairs={{0,16},{8,24},{16,0},{24,8},{1,17},{9,25},{17,1},{25,9},{2,18},{10... | collective-permute-start | bytes 1544 | tf_op jit(solution)/shard_map/ppermute | solution.py:80
